TPU v7x, 32 devices: a whole 2x2x4 slice. The times are simulated.
32 devices in a mesh: groups: 2 (over y), tm: 4 (over z), face: 4 (over x, core).
Axes of the slice: x: 2, y: 2, z: 4, core: 2. Of those that a mesh axis runs over, the one named last changes fastest.
Arguments:
- latents: bfloat16 [8, 4, 896, 1152], P(('groups', 'tm'), 'face'), parts along dimension 0, may hold values from -6 to 6
- modulation: float32 [6, 1152], P('groups'), parts along dimension 0, may hold values from -3 to 3
- w_qkv: bfloat16 [1152, 1728], P('face'), as said below
- w_out: bfloat16 [576, 1152], P(None, 'face'), may hold values from -0.25 to 0.25
- edge_table: int32 [4, 4, 4], replicated, may hold values from 0 to 3, as said below
- space_ramp: int32 [2], replicated, may hold values from 1 to 8, as said below
- time_ramp: int32 [4], replicated, may hold values from 1 to 8, as said below
Outputs:
- blended: bfloat16 [8, 4, 896, 1152], P(('groups', 'tm'), 'face'), parts along dimension 0
There are 2 independent parts, one for each index of `groups`. A program takes and returns all parts, laid end to end along the dimension named above; an argument that names none is the same for every part. Nothing has to cross between parts.
Inputs may be any that keep to these rules, and one draw needn't show every extreme that they name: Row edge_table[g, e] = (p, e2, flip, route): route r in 0..3 names an offset o = 1, -1, 2, -2 with p = (g + o) mod 4; the four edges of a tile take the four routes; row edge_table[p, e2] points back to (g, e) with the same flip (0 or 1) and the route of the opposite offset. `space_ramp`: distinct positive integers, one of them 8. `time_ramp`: distinct positive integers, one of them 8. `w_qkv`: projection weights of order 1152 ** -0.5 in most heads.
All inputs are finite; a program needn't handle non-finite values.
Results may differ from a plain program's by a relative error of at most 0.0046.
Values may be sent and summed in bfloat16 or wider, within the bound.
No kernel may reach another device: no remote copies, remote signals or barrier semaphores. Data moves between devices by JAX's collectives and lax.ppermute only.
A program may use at most 64 MiB of HBM per device.

v0:
```python
import math

import jax
import jax.numpy as jnp
from jax import lax
from jax.sharding import PartitionSpec as P

D = 1152
HD = 72
HEADS = 8
S = 8
OVS = 2
OVT = 4
F = 14


NORM_EPS = 1e-06
OFFSETS = (1, -1, 2, -2)
PARTNER_ROUTE = (1, 0, 3, 2)


def passed_along(block, axis, distance):
    devices = range(lax.axis_size(axis))
    route = [((i - distance) % len(devices), i) for i in devices]
    return lax.ppermute(block, axis, route)


def extended(block, sides, width):
    for axis, dim in sides:
        count = lax.axis_size(axis)
        forward = [(i, i + 1) for i in range(count - 1)]
        backward = [(target, source) for source, target in forward]
        low = lax.ppermute(
            lax.slice_in_dim(block, block.shape[dim] - width, None, axis=dim), axis, forward
        )
        high = lax.ppermute(lax.slice_in_dim(block, 0, width, axis=dim), axis, backward)
        block = jnp.concatenate([low, block, high], axis=dim)
    return block


def modulate(block_in, modulation):
    values = block_in.astype(jnp.float32)
    center = jnp.mean(values, axis=-1, keepdims=True)
    spread = jnp.mean(jnp.square(values - center), axis=-1, keepdims=True)
    normed = (values - center) * lax.rsqrt(spread + NORM_EPS)
    return (normed * (1.0 + modulation[1]) + modulation[0]).astype(jnp.bfloat16)


def attend(qkv_all, head_count, head_size):
    tokens = qkv_all.shape[0]
    stacked = qkv_all.reshape(tokens, 3, head_count, head_size).transpose(1, 2, 0, 3)

    def one_head(operands):
        queries, keyset, valset = operands
        scores = jnp.dot(queries, keyset.T, preferred_element_type=jnp.float32) * (
            1.0 / math.sqrt(head_size)
        )
        row_max = jnp.max(scores, axis=-1, keepdims=True)
        weights = jnp.exp(scores - row_max)
        row_sum = jnp.sum(weights, axis=-1, keepdims=True)
        probabilities = (weights / row_sum).astype(jnp.bfloat16)
        return jnp.dot(probabilities, valset, preferred_element_type=jnp.float32).astype(
            jnp.bfloat16
        )

    outputs = lax.map(one_head, (stacked[0], stacked[1], stacked[2]))
    return outputs.transpose(1, 0, 2).reshape(tokens, head_count * head_size)


def take_strips(block):
    extent = block.shape[1]
    middle = slice(OVS, extent - OVS)
    upper_rim = block[:, :OVS, middle]
    lower_rim = block[:, extent - OVS :, middle][:, ::-1]
    left_rim = jnp.swapaxes(block[:, middle, :OVS], 1, 2)
    right_rim = jnp.swapaxes(block[:, middle, extent - OVS :][:, :, ::-1], 1, 2)
    return jnp.stack([upper_rim, lower_rim, left_rim, right_rim])


def put_strips(block, strips):
    extent = block.shape[1]
    middle = slice(OVS, extent - OVS)
    block = block.at[:, :OVS, middle].set(strips[0])
    block = block.at[:, extent - OVS :, middle].set(strips[1][:, ::-1])
    block = block.at[:, middle, :OVS].set(jnp.swapaxes(strips[2], 1, 2))
    block = block.at[:, middle, extent - OVS :].set(jnp.swapaxes(strips[3], 1, 2)[:, :, ::-1])
    return block


def blend_strips(own_strips, incoming, flip_bits, space_ramp):
    ramp = space_ramp.astype(jnp.float32)
    weight_own = (ramp / (ramp + ramp[::-1]))[None, None, :, None, None]
    weight_far = (ramp[::-1] / (ramp + ramp[::-1]))[None, None, :, None, None]
    mapped = incoming.astype(jnp.float32)[:, :, ::-1]
    mapped = jnp.where(flip_bits[:, None, None, None, None] > 0, mapped[:, :, :, ::-1], mapped)
    mixed = weight_own * own_strips.astype(jnp.float32) + weight_far * mapped
    return mixed.astype(jnp.bfloat16)


def blend_rims(spaced, lower, upper, has_lower, has_upper, time_ramp):
    ramp = time_ramp.astype(jnp.float32)
    shape_rim = (-1,) + (1,) * (spaced.ndim - 1)
    weight_own = (ramp / (ramp + ramp[::-1])).reshape(shape_rim)
    weight_far = (ramp[::-1] / (ramp + ramp[::-1])).reshape(shape_rim)
    frames = spaced.shape[0]
    own_low = spaced[:OVT].astype(jnp.float32)
    own_high = spaced[frames - OVT :].astype(jnp.float32)
    low_mix = jnp.where(
        has_lower, weight_own * own_low + weight_far * lower.astype(jnp.float32), own_low
    )
    high_mix = jnp.where(
        has_upper,
        weight_own[::-1] * own_high + weight_far[::-1] * upper.astype(jnp.float32),
        own_high,
    )
    updated = spaced.at[:OVT].set(low_mix.astype(jnp.bfloat16))
    return updated.at[frames - OVT :].set(high_mix.astype(jnp.bfloat16))


def pick_edge(strips, edge_ids, routes, route_id):
    sender = jnp.sum(edge_ids * (routes == route_id))
    return lax.dynamic_index_in_dim(strips, sender, 0, keepdims=False)


def place_edge(incoming, arrived, edge_ids, routes, route_id):
    target = jnp.sum(edge_ids * (routes == route_id))
    chosen = (edge_ids == target)[:, None, None, None, None]
    return jnp.where(chosen, arrived[None], incoming)


def per_device(latents, modulation, w_qkv, w_out, edge_table, space_ramp, time_ramp):
    block_in = latents[0, 0]
    moved = modulate(block_in, modulation)
    qkv_sums = jnp.dot(
        moved, lax.all_gather(w_qkv, "face", axis=0, tiled=True), preferred_element_type=jnp.float32
    )
    qkv_all = qkv_sums.astype(jnp.bfloat16)
    mixed = attend(qkv_all, HEADS, HD)
    projected = jnp.dot(
        mixed, lax.all_gather(w_out, "face", axis=1, tiled=True), preferred_element_type=jnp.float32
    )
    tile_out = (block_in.astype(jnp.float32) + modulation[2] * projected).astype(jnp.bfloat16)
    tile_grid = tile_out.reshape(F, S, S, D)
    my_rows = lax.dynamic_index_in_dim(edge_table, lax.axis_index("face"), 0, keepdims=False)
    flip_bits = my_rows[:, 2]
    routes = my_rows[:, 3]
    edge_ids = jnp.arange(4, dtype=jnp.int32)
    span_id = lax.axis_index("tm")
    has_lower = span_id > 0
    has_upper = span_id < lax.axis_size("tm") - 1
    strips = take_strips(tile_grid)
    incoming = jnp.zeros_like(strips)
    for route_id in range(4):
        outgoing = pick_edge(strips, edge_ids, routes, PARTNER_ROUTE[route_id])
        arrived = passed_along(outgoing, "face", -OFFSETS[route_id])
        incoming = place_edge(incoming, arrived, edge_ids, routes, route_id)
    spaced = put_strips(tile_grid, blend_strips(strips, incoming, flip_bits, space_ramp))
    rims = jnp.concatenate([spaced[:OVT], spaced[F - OVT :]], axis=0)
    widened = extended(rims, (("tm", 0),), OVT)
    lower = widened[:OVT]
    upper = widened[3 * OVT :]
    result = blend_rims(spaced, lower, upper, has_lower, has_upper, time_ramp)
    return result.reshape(1, 1, F * S * S, D)


def solution(mesh):
    return jax.shard_map(
        per_device,
        mesh=mesh,
        in_specs=(
            P(("groups", "tm"), "face", None, None),
            P("groups", None),
            P("face", None),
            P(None, "face"),
            P(),
            P(),
            P(),
        ),
        out_specs=P(("groups", "tm"), "face", None, None),
        check_vma=False,
    )
```

profile of v0, /device:TPU:0, one launch (start us, length us, event | category | flops | bytes accessed | tf_op | source)
XLA Modules:
  0.0 221.4 jit_solution(15109691575389352282)
XLA Ops:
  17.3 2.1 convert_reduce_fusion
  23.9 21.9 %all-gather.3.cloned.1.call-done = bf16[1152,1728]{1,0:T(8,128)(2,1)} async-done(((bf16[288,1728]{1,0:T(8,128)(2,1)}), bf16[1152,1728]{1,0:T(8,128)(2,1)}) %all-gather.3.cloned.1.call-update) | async-done | bytes 3981328 | tf_op jit(solution)/shard_map/all_gather | solution.py:135
  45.8 9.0 %convolution_convert_fusion = bf16[896,1728]{0,1:T(8,128)(2,1)} fusion(bf16[1152,1728]{1,0:T(8,128)(2,1)} %all-gather.3.cloned.1.call-done, bf16[1,1,896,1152]{3,2,1,0:T(8,128)(2,1)S(1)} %copy-done.3, f32[1152]{0:T(1024)S(1)} %get-tuple-element.106, f32[1152]{0:T(1024)S(1)} %get-tuple-element.107, f32[896]{0:T(1024)S(1)} %add_rsqrt_fusion, ...), kind=kOutput, calls=%fused_computation.30 | convolution fusion | flops 3574996992 | bytes 9158656 | tf_op jit(solution)/shard_map/dot_general | solution.py:134
  54.8 6.4 %copy.8 = bf16[896,3,8,72]{3,0,2,1:T(8,128)(2,1)} copy(bf16[896,3,8,72]{0,3,2,1:T(8,128)(2,1)} %bitcast.105) | data formatting | bytes 6193152 | tf_op jit(solution)/shard_map/reshape | solution.py:51
  61.1 5.3 %slice_bitcast_fusion = (bf16[8,896,72]{2,1,0:T(8,128)(2,1)}, bf16[8,896,72]{2,1,0:T(8,128)(2,1)}, bf16[8,896,72]{2,1,0:T(8,128)(2,1)}) fusion(bf16[3,8,896,72]{3,2,1,0:T(8,128)(2,1)} %bitcast.101), kind=kLoop, calls=%fused_computation.40 | loop fusion | bytes 6193152 | tf_op jit(solution)/shard_map/squeeze | solution.py:66
  66.4 31.6 %while.16 = (s32[]{:T(128)}, bf16[8,896,72]{1,2,0:T(8,128)(2,1)S(1)}, bf16[8,896,72]{2,1,0:T(8,128)(2,1)}, bf16[8,896,72]{2,1,0:T(8,128)(2,1)}, bf16[8,896,72]{2,1,0:T(8,128)(2,1)}, /*index=5*/s32[]{:T(128)}) while((s32[]{:T(128)}, bf16[8,896,72]{1,2,0:T(8,128)(2,1)S(1)}, bf16[8,896,72]{2,1,0:T(8,128)(2,1)}, bf16[8,896,72]{2,1,0:T(8,128)(2,1)}, ...), condition=%wide.region_5.6_spmd, body=%wide.region_2.5_spmd.sunk | while | flops 238499072 | bytes 10472005 | solution.py:66
  66.4 1.6 multiply_reduce_fusion.2
  68.6 1.7 fusion.49
  70.4 1.6 multiply_reduce_fusion.2
  72.6 1.7 fusion.49
  74.3 1.6 multiply_reduce_fusion.2
  76.5 1.7 fusion.49
  78.3 1.6 multiply_reduce_fusion.2
  80.5 1.7 fusion.49
  82.2 1.6 multiply_reduce_fusion.2
  84.4 1.7 fusion.49
  86.2 1.6 multiply_reduce_fusion.2
  88.4 1.7 fusion.49
  90.1 1.6 multiply_reduce_fusion.2
  92.3 1.7 fusion.49
  94.1 1.6 multiply_reduce_fusion.2
  96.3 1.7 fusion.49
  98.0 3.4 %fusion.23 = bf16[896,1152]{1,0:T(8,128)(2,1)S(1)} fusion(bf16[1,1,896,1152]{3,2,1,0:T(8,128)(2,1)S(1)} %copy-done.3, bf16[896,576]{0,1:T(8,128)(2,1)S(1)} %bitcast.112, bf16[576,1152]{0,1:T(8,128)(2,1)} %all-gather.5.cloned.1.call-done, f32[1152]{0:T(1024)S(1)} %get-tuple-element.105), kind=kOutput, calls=%fused_computation.29 | convolution fusion | flops 1193213952 | bytes 6492672 | tf_op jit(solution)/shard_map/dot_general | solution.py:139
  102.7 2.3 %constant_dynamic-slice_fusion = (bf16[14,2,4,1152]{3,2,1,0:T(4,128)(2,1)}, bf16[14,2,4,1152]{3,2,1,0:T(4,128)(2,1)S(1)}, bf16[14,2,4,1152]{3,2,1,0:T(4,128)(2,1)S(1)}) fusion(bf16[14,8,8,1152]{3,2,1,0:T(8,128)(2,1)S(1)} %bitcast.103, s32[]{:T(128)} %bitcast.25, s32[]{:T(128)} %bitcast.26), kind=kLoop, calls=%fused_computation.72 | loop fusion | bytes 1548296 | tf_op jit(solution)/shard_map/dynamic-slice.20
  105.2 1.5 rev.31
  106.9 1.5 rev.32
  108.4 2.0 pad_maximum_fusion
  111.5 1.7 collective-permute-start.1
  113.3 1.7 collective-permute-start.3
  115.8 4.5 %collective-permute-done = bf16[14,2,4,1152]{3,1,2,0:T(2,128)(2,1)S(1)} collective-permute-done((bf16[14,2,4,1152]{3,1,2,0:T(2,128)(2,1)S(1)}, bf16[14,2,4,1152]{3,1,2,0:T(2,128)(2,1)S(1)}, u32[]{:S(2)}, u32[]{:S(2)}) %collective-permute-start) | collective-permute-done | bytes 258080 | tf_op jit(solution)/shard_map/ppermute | solution.py:25
  120.3 5.5 %collective-permute-done.1 = bf16[14,2,4,1152]{3,1,2,0:T(2,128)(2,1)S(1)} collective-permute-done((bf16[14,2,4,1152]{3,1,2,0:T(2,128)(2,1)S(1)}, bf16[14,2,4,1152]{3,1,2,0:T(2,128)(2,1)S(1)}, u32[]{:S(2)}, u32[]{:S(2)}) %collective-permute-start.1) | collective-permute-done | bytes 258080 | tf_op jit(solution)/shard_map/ppermute | solution.py:25
  125.8 4.1 %collective-permute-done.2 = bf16[14,2,4,1152]{3,1,2,0:T(2,128)(2,1)S(1)} collective-permute-done((bf16[14,2,4,1152]{3,1,2,0:T(2,128)(2,1)S(1)}, bf16[14,2,4,1152]{3,1,2,0:T(2,128)(2,1)S(1)}, u32[]{:S(2)}, u32[]{:S(2)}) %collective-permute-start.2) | collective-permute-done | bytes 258080 | tf_op jit(solution)/shard_map/ppermute | solution.py:25
  130.6 2.7 %fusion.33 = f32[4,14,2,4,1152]{4,2,3,1,0:T(2,128)S(1)} fusion(pred[4]{0:T(512)(128)(4,1)S(1)} %iota_compare_fusion.3, pred[4]{0:T(512)(128)(4,1)S(1)} %iota_compare_fusion, pred[4]{0:T(512)(128)(4,1)S(1)} %iota_compare_fusion.1, pred[4]{0:T(512)(128)(4,1)S(1)} %iota_compare_fusion.2, bf16[14,2,4,1152]{3,1,2,0:T(2,128)(2,1)} %collective-permute-done.3, ...), kind=kLoop, calls=%fused_computation.51 | loop fusion | flops 2580480 | bytes 3096592 | tf_op jit(solution)/shard_map/convert_element_type | solution.py:94
  133.4 8.5 %rev.33 = f32[4,14,2,4,1152]{4,2,3,1,0:T(2,128)} reverse(f32[4,14,2,4,1152]{4,2,3,1,0:T(2,128)S(1)} %fusion.33), dimensions={2,3} | reverse | bytes 4128768 | tf_op jit(solution)/shard_map/rev | solution.py:95
  141.9 8.6 %rev.34 = f32[4,14,2,4,1152]{4,2,3,1,0:T(2,128)} reverse(f32[4,14,2,4,1152]{4,2,3,1,0:T(2,128)S(1)} %fusion.33), dimensions={2} | reverse | bytes 4128768 | tf_op jit(solution)/shard_map/rev | solution.py:94
  150.4 3.7 %add_convert_fusion = bf16[4,14,2,4,1152]{4,2,3,1,0:T(2,128)(2,1)S(1)} fusion(f32[4,14,2,4,1152]{4,2,3,1,0:T(2,128)} %rev.33, f32[4,14,2,4,1152]{4,2,3,1,0:T(2,128)} %rev.34, pred[4]{0:T(512)(128)(4,1)S(1)} %get-tuple-element.108, f32[2]{0:T(128)S(1)} %get-tuple-element.144, f32[2]{0:T(128)S(1)} %get-tuple-element.143, ...), kind=kLoop, calls=%fused_computation.31 | loop fusion | flops 4644864 | bytes 6193172 | tf_op jit(solution)/shard_map/convert_element_type | solution.py:97
  156.9 6.4 %scatter.20 = bf16[14,8,8,1152]{3,2,1,0:T(8,128)(2,1)S(1)} dynamic-update-slice(bf16[14,8,8,1152]{3,2,1,0:T(8,128)(2,1)S(1)} %bitcast.104, bf16[14,2,4,1152]{3,2,1,0:T(4,128)(2,1)} %copy.12, s32[]{:T(128)} %constant.224.clone.1, s32[]{:T(128)} %bitcast.25, s32[]{:T(128)} %bitcast.26, s32[]{:T(128)} %constant.224.clone.1) | dynamic-update-slice | bytes 516100 | tf_op jit(solution)/shard_map/scatter | solution.py:83
  163.3 5.3 %rev.35 = bf16[14,2,4,1152]{3,1,2,0:T(2,128)(2,1)} reverse(bf16[14,2,4,1152]{3,1,2,0:T(2,128)(2,1)} %get-tuple-element.136), dimensions={1} | reverse | bytes 516096 | tf_op jit(solution)/shard_map/rev | solution.py:84
  168.6 1.7 copy.13
  170.3 5.1 %scatter.21 = bf16[14,8,8,1152]{3,2,1,0:T(8,128)(2,1)S(1)} dynamic-update-slice(bf16[14,8,8,1152]{3,2,1,0:T(8,128)(2,1)S(1)} %scatter.20, bf16[14,2,4,1152]{3,2,1,0:T(4,128)(2,1)} %copy.13, s32[]{:T(128)} %constant.224.clone.1, s32[]{:T(128)} %constant.238.clone.1, s32[]{:T(128)} %constant.231.clone.1, s32[]{:T(128)} %constant.224.clone.1) | dynamic-update-slice | bytes 516100 | tf_op jit(solution)/shard_map/scatter | solution.py:84
  175.8 1.5 rev.36
  177.7 3.5 %collective-permute-start.4 = (bf16[4,8,8,1152]{3,2,1,0:T(8,128)(2,1)S(1)}, bf16[4,8,8,1152]{3,2,1,0:T(8,128)(2,1)S(1)}, u32[]{:S(2)}, u32[]{:S(2)}) collective-permute-start(bf16[4,8,8,1152]{3,2,1,0:T(8,128)(2,1)S(1)} %slice.277), channel_id=1, source_target_pairs={{0,4},{4,8},{8,12},{1,5},{5,9},{9,13},{2,6},{6,10},{10,14},{3,7},{... | collective-permute-start | bytes 1769480 | tf_op jit(solution)/shard_map/ppermute | solution.py:33
  181.4 1.3 copy.31
  182.7 11.2 %collective-permute-done.4 = bf16[4,8,8,1152]{3,2,1,0:T(8,128)(2,1)S(1)} collective-permute-done((bf16[4,8,8,1152]{3,2,1,0:T(8,128)(2,1)S(1)}, bf16[4,8,8,1152]{3,2,1,0:T(8,128)(2,1)S(1)}, u32[]{:S(2)}, u32[]{:S(2)}) %collective-permute-start.4) | collective-permute-done | bytes 589856 | tf_op jit(solution)/shard_map/ppermute | solution.py:33
  193.9 2.4 %fusion.39 = (bf16[4,8,8,1152]{3,2,1,0:T(8,128)(2,1)}, bf16[14,8,8,1152]{3,2,1,0:T(8,128)(2,1)}) fusion(bf16[14,8,8,1152]{3,2,1,0:T(8,128)(2,1)} %copy.31, bf16[4,8,8,1152]{3,2,1,0:T(8,128)(2,1)S(1)} %collective-permute-done.4, f32[4]{0:T(128)S(1)} %get-tuple-element.142, f32[4]{0:T(128)S(1)} %get-tuple-element.141, pred[]{:T(512)S(6)} %gt.16), kind=kLoop, calls=%fused_computation.96 | loop fusion | flops 2064384 | bytes 2359329 | tf_op jit(solution)/shard_map/slice | solution.py:106
  196.3 1.3 collective-permute-start.5
  197.8 15.7 %collective-permute-done.5 = bf16[4,8,8,1152]{3,2,1,0:T(8,128)(2,1)S(1)} collective-permute-done((bf16[4,8,8,1152]{3,2,1,0:T(8,128)(2,1)}, bf16[4,8,8,1152]{3,2,1,0:T(8,128)(2,1)S(1)}, u32[]{:S(2)}, u32[]{:S(2)}) %collective-permute-start.5) | collective-permute-done | bytes 589856 | tf_op jit(solution)/shard_map/ppermute | solution.py:36
  213.4 1.1 fusion.34
  (76 shorter events, 20.3 us)
Async XLA Ops:
  6.5 1.5 copy-start
  6.5 12.9 %copy-start.3 = (bf16[1,1,896,1152]{3,2,1,0:T(8,128)(2,1)S(1)}, bf16[1,1,896,1152]{3,2,1,0:T(8,128)(2,1)}, u32[]{:S(2)}) copy-start(bf16[1,1,896,1152]{3,2,1,0:T(8,128)(2,1)} %param.21) | copy-start | bytes 6193156
  6.5 39.2 %all-gather.3.cloned.1.call-start = ((), (), s32[]{:S(2)}) async-start(), calls=%async_computation | async-start | bytes 5160960 | tf_op jit(solution)/shard_map/all_gather | solution.py:135
  7.3 90.8 %all-gather.5.cloned.1.call-start = ((), (), s32[]{:S(2)}) async-start(), calls=%async_computation.1 | async-start | bytes 1843200 | tf_op jit(solution)/shard_map/all_gather | solution.py:140
  17.3 5.9 %copy-start.12 = (s32[4]{0:T(128)S(1)}, s32[4]{0:T(128)}, u32[]{:S(2)}) copy-start(s32[4]{0:T(128)} %constant.232.clone.1) | copy-start | bytes 52
  101.4 1.3 copy-start.1
  106.7 4.5 %copy-start.4 = (bf16[14,2,4,1152]{3,1,2,0:T(2,128)(2,1)}, bf16[14,2,4,1152]{3,1,2,0:T(2,128)(2,1)S(1)}, u32[]{:S(2)}) copy-start(bf16[14,2,4,1152]{3,1,2,0:T(2,128)(2,1)S(1)} %rev.31) | copy-start | bytes 774148
  106.9 4.3 %copy-start.5 = (bf16[14,2,4,1152]{3,1,2,0:T(2,128)(2,1)}, bf16[14,2,4,1152]{3,1,2,0:T(2,128)(2,1)S(1)}, u32[]{:S(2)}) copy-start(bf16[14,2,4,1152]{3,1,2,0:T(2,128)(2,1)S(1)} %copy.19) | copy-start | bytes 774148
  108.4 2.8 %copy-start.6 = (bf16[14,4,2,1152]{3,2,1,0:T(2,128)(2,1)}, bf16[14,4,2,1152]{3,2,1,0:T(2,128)(2,1)S(1)}, u32[]{:S(2)}) copy-start(bf16[14,4,2,1152]{3,2,1,0:T(2,128)(2,1)S(1)} %rev.32) | copy-start | bytes 774148
  108.4 7.3 %copy-start.10 = (s32[2]{0:T(128)S(1)}, s32[2]{0:T(128)}, u32[]{:S(2)}) copy-start(s32[2]{0:T(128)} %param.26) | copy-start | bytes 28
  111.2 9.1 %collective-permute-start = (bf16[14,2,4,1152]{3,1,2,0:T(2,128)(2,1)S(1)}, bf16[14,2,4,1152]{3,1,2,0:T(2,128)(2,1)S(1)}, u32[]{:S(2)}, u32[]{:S(2)}) collective-permute-start(bf16[14,2,4,1152]{3,1,2,0:T(2,128)(2,1)S(1)} %get-tuple-element.137), channel_id=1, source_target_pairs={{2,0},{3,1},{0,2},{1,3},{6,4},{7,5},{4,6},{5,7},{10,8},{11,9},{8,1... | collective-permute-start | bytes 774152 | tf_op jit(solution)/shard_map/ppermute | solution.py:25
  111.5 14.3 %collective-permute-start.1 = (bf16[14,2,4,1152]{3,1,2,0:T(2,128)(2,1)S(1)}, bf16[14,2,4,1152]{3,1,2,0:T(2,128)(2,1)S(1)}, u32[]{:S(2)}, u32[]{:S(2)}) collective-permute-start(bf16[14,2,4,1152]{3,1,2,0:T(2,128)(2,1)S(1)} %get-tuple-element.140), channel_id=1, source_target_pairs={{2,0},{3,1},{0,2},{1,3},{6,4},{7,5},{4,6},{5,7},{10,8},{11,9},{8,1... | collective-permute-start | bytes 774152 | tf_op jit(solution)/shard_map/ppermute | solution.py:25
  113.2 16.7 %collective-permute-start.2 = (bf16[14,2,4,1152]{3,1,2,0:T(2,128)(2,1)S(1)}, bf16[14,2,4,1152]{3,1,2,0:T(2,128)(2,1)S(1)}, u32[]{:S(2)}, u32[]{:S(2)}) collective-permute-start(bf16[14,2,4,1152]{3,1,2,0:T(2,128)(2,1)S(1)} %get-tuple-element.139), channel_id=1, source_target_pairs={{3,0},{0,1},{1,2},{2,3},{7,4},{4,5},{5,6},{6,7},{11,8},{8,9},{9,10... | collective-permute-start | bytes 774152 | tf_op jit(solution)/shard_map/ppermute | solution.py:25
  113.3 17.4 %collective-permute-start.3 = (bf16[14,2,4,1152]{3,1,2,0:T(2,128)(2,1)S(1)}, bf16[14,2,4,1152]{3,1,2,0:T(2,128)(2,1)}, u32[]{:S(2)}, u32[]{:S(2)}) collective-permute-start(bf16[14,2,4,1152]{3,1,2,0:T(2,128)(2,1)S(1)} %get-tuple-element.138), channel_id=1, source_target_pairs={{1,0},{2,1},{3,2},{0,3},{5,4},{6,5},{7,6},{4,7},{9,8},{10,9},{11,1... | collective-permute-start | bytes 774152 | tf_op jit(solution)/shard_map/ppermute | solution.py:25
  125.8 4.1 %copy-start.8 = (bf16[14,2,4,1152]{3,1,2,0:T(2,128)(2,1)}, bf16[14,2,4,1152]{3,1,2,0:T(2,128)(2,1)S(1)}, u32[]{:S(2)}) copy-start(bf16[14,2,4,1152]{3,1,2,0:T(2,128)(2,1)S(1)} %collective-permute-done.1) | copy-start | bytes 774148
  129.9 0.7 copy-start.9
  150.4 4.8 %copy-start.7 = (bf16[14,2,4,1152]{3,2,1,0:T(4,128)(2,1)S(1)}, bf16[14,2,4,1152]{3,2,1,0:T(4,128)(2,1)}, u32[]{:S(2)}) copy-start(bf16[14,2,4,1152]{3,2,1,0:T(4,128)(2,1)} %get-tuple-element.130) | copy-start | bytes 774148
  154.2 2.7 %copy-start.2 = (bf16[896,1152]{1,0:T(8,128)(2,1)S(1)}, bf16[896,1152]{1,0:T(8,128)(2,1)}, u32[]{:S(2)}) copy-start(bf16[896,1152]{1,0:T(8,128)(2,1)} %copy-done.1) | copy-start | bytes 6193156
  163.3 18.0 %copy-start.11 = (s32[4]{0:T(128)S(1)}, s32[4]{0:T(128)}, u32[]{:S(2)}) copy-start(s32[4]{0:T(128)} %param.27) | copy-start | bytes 52
  177.7 16.2 %collective-permute-start.4 = (bf16[4,8,8,1152]{3,2,1,0:T(8,128)(2,1)S(1)}, bf16[4,8,8,1152]{3,2,1,0:T(8,128)(2,1)S(1)}, u32[]{:S(2)}, u32[]{:S(2)}) collective-permute-start(bf16[4,8,8,1152]{3,2,1,0:T(8,128)(2,1)S(1)} %slice.277), channel_id=1, source_target_pairs={{0,4},{4,8},{8,12},{1,5},{5,9},{9,13},{2,6},{6,10},{10,14},{3,7},{... | collective-permute-start | bytes 1769480 | tf_op jit(solution)/shard_map/ppermute | solution.py:33
  196.3 17.1 %collective-permute-start.5 = (bf16[4,8,8,1152]{3,2,1,0:T(8,128)(2,1)}, bf16[4,8,8,1152]{3,2,1,0:T(8,128)(2,1)S(1)}, u32[]{:S(2)}, u32[]{:S(2)}) collective-permute-start(bf16[4,8,8,1152]{3,2,1,0:T(8,128)(2,1)} %get-tuple-element.128), channel_id=1, source_target_pairs={{4,0},{8,4},{12,8},{5,1},{9,5},{13,9},{6,2},{10,6},{14,10},{7,3},{... | collective-permute-start | bytes 1769480 | tf_op jit(solution)/shard_map/ppermute | solution.py:36
Sparse Core Ops, SparseCore 0:
  8.9 36.7 all-gather.2
  47.3 19.0 all-gather.4
where the time goes:
time: 223 us; the launch traced here: 221 us
  waiting for transfers between devices  64.3 us (29%)
  local copies, waits for them, and re-layouts  62 us (28%)
  matrix products  39.2 us (18%)
  other arithmetic  25.9 us (12%)
  between operations  21.2 us (10%)
  starting transfers between devices  8.71 us (4%)
    all_gather x1, waiting for transfers between devices, per_device(): lax.all_gather(w_qkv, 'face', axis=0, tiled=True)  21.9 us
    ppermute x1, waiting for transfers between devices, extended(): lax.ppermute(lax.slice_in_dim(block, 0, width, axis=dim), axis, backward)  15.7 us
    ppermute x4, waiting for transfers between devices, passed_along(): return lax.ppermute(block, axis, route)  14.2 us
    dot_general x8, matrix products, one_head(): jnp.dot(probabilities, valset, preferred_element_type=jnp.float32)  13.7 us
    dot_general x8, matrix products, one_head(): jnp.dot(queries, keyset.T, preferred_element_type=jnp.float32)  13.1 us
    ppermute x1, waiting for transfers between devices, extended(): lax.ppermute(lax.slice_in_dim(block, block.shape[dim] - width, None, axis...  11.2 us
    dot_general x1, matrix products, per_device(): jnp.dot(moved, lax.all_gather(w_qkv, 'face', axis=0, tiled=True), preferr...  8.99 us
    rev x1, local copies, waits for them, and re-layouts, blend_strips(): mapped = incoming.astype(jnp.float32)[:, :, ::-1]  8.57 us
  transfers between devices with their start and end apart: 8, of which 6 were waited for; matrix products, arithmetic and copies ran while one was open for 28% of the time, Pallas kernels for 0%

commit v1 on v0

v1 whole, which is shorter than its diff:
```python
import math

import jax
import jax.numpy as jnp
import numpy as np
from jax import lax
from jax.sharding import PartitionSpec as P

D = 1152
HD = 72
HEADS = 8
S = 8
OVS = 2
OVT = 4
MID = S - 2 * OVS


NORM_EPS = 1e-06
OFFSETS = (1, -1, 2, -2)
PARTNER_ROUTE = (1, 0, 3, 2)


def modulate(block_in, modulation):
    values = block_in.astype(jnp.float32)
    center = jnp.mean(values, axis=-1, keepdims=True)
    spread = jnp.mean(jnp.square(values - center), axis=-1, keepdims=True)
    normed = (values - center) * lax.rsqrt(spread + NORM_EPS)
    return (normed * (1.0 + modulation[1]) + modulation[0]).astype(jnp.bfloat16)


def attend(qkv_all, head_count, head_size):
    tokens = qkv_all.shape[0]
    stacked = qkv_all.reshape(tokens, 3, head_count, head_size).transpose(1, 2, 0, 3)

    def one_head(operands):
        queries, keyset, valset = operands
        scores = jnp.dot(queries, keyset.T, preferred_element_type=jnp.float32) * (
            1.0 / math.sqrt(head_size)
        )
        row_max = jnp.max(scores, axis=-1, keepdims=True)
        weights = jnp.exp(scores - row_max)
        row_sum = jnp.sum(weights, axis=-1, keepdims=True)
        probabilities = (weights / row_sum).astype(jnp.bfloat16)
        return jnp.dot(probabilities, valset, preferred_element_type=jnp.float32).astype(
            jnp.bfloat16
        )

    outputs = lax.map(one_head, (stacked[0], stacked[1], stacked[2]))
    return outputs.transpose(1, 0, 2).reshape(tokens, head_count * head_size)


def face_pieces(shard):
    n = lax.axis_size("face")
    me = lax.axis_index("face")

    def fetch(x, src_of):
        return lax.ppermute(x, "face", [(src_of(i), i) for i in range(n)])

    pieces = [(shard, me), (fetch(shard, lambda i: i ^ 1), me ^ 1)]
    for j in range(1, n // 2):
        far = fetch(shard, lambda i: (i + 2 * j) % n)
        pieces.append((far, (me + 2 * j) % n))
        pieces.append((fetch(far, lambda i: i ^ 1), ((me ^ 1) + 2 * j) % n))
    return pieces


def cell_token(edge, frame, depth, pos):
    row = jnp.where(edge == 0, depth, jnp.where(edge == 1, S - 1 - depth, OVS + pos))
    col = jnp.where(edge < 2, OVS + pos, jnp.where(edge == 2, depth, S - 1 - depth))
    return frame * (S * S) + row * S + col


def strip_depth(frames):
    grid = np.full((S, S), -1, np.int32)
    for d in range(OVS):
        grid[d, OVS : S - OVS] = d
        grid[S - 1 - d, OVS : S - OVS] = d
        grid[OVS : S - OVS, d] = d
        grid[OVS : S - OVS, S - 1 - d] = d
    return np.tile(grid.reshape(-1), frames)


def per_device(latents, modulation, w_qkv, w_out, edge_table, space_ramp, time_ramp):
    block_in = latents[0, 0]
    tokens = block_in.shape[0]
    frames = tokens // (S * S)
    n = lax.axis_size("face")
    rows = w_qkv.shape[0]
    moved = modulate(block_in, modulation)
    if n <= 4:
        moved_parts = moved.reshape(tokens, n, rows).transpose(1, 0, 2)
        qkv_sums = None
        for piece, index in face_pieces(w_qkv):
            part = jnp.dot(
                lax.dynamic_index_in_dim(moved_parts, index, 0, keepdims=False),
                piece,
                preferred_element_type=jnp.float32,
            )
            qkv_sums = part if qkv_sums is None else qkv_sums + part
    else:
        qkv_stack = jnp.zeros((n,) + w_qkv.shape, w_qkv.dtype)
        for piece, index in face_pieces(w_qkv):
            qkv_stack = lax.dynamic_update_index_in_dim(qkv_stack, piece, index, 0)
        w_qkv_full = qkv_stack.reshape(n * rows, w_qkv.shape[1])
        qkv_sums = jnp.dot(moved, w_qkv_full, preferred_element_type=jnp.float32)
    qkv_all = qkv_sums.astype(jnp.bfloat16)

    out_stack = jnp.zeros((n,) + w_out.shape, w_out.dtype)
    for piece, index in face_pieces(w_out):
        out_stack = lax.dynamic_update_index_in_dim(out_stack, piece, index, 0)
    w_out_full = out_stack.transpose(1, 0, 2).reshape(w_out.shape[0], n * w_out.shape[1])

    mixed = attend(qkv_all, HEADS, HD)
    projected = jnp.dot(mixed, w_out_full, preferred_element_type=jnp.float32)
    tile_out = (block_in.astype(jnp.float32) + modulation[2] * projected).astype(jnp.bfloat16)

    my_rows = lax.dynamic_index_in_dim(edge_table, lax.axis_index("face"), 0, keepdims=False)
    flips = my_rows[:, 2]
    routes = my_rows[:, 3]
    edge_ids = jnp.arange(4, dtype=jnp.int32)
    frame = jnp.arange(frames, dtype=jnp.int32)[:, None, None]
    depth = jnp.arange(OVS, dtype=jnp.int32)[None, :, None]
    pos = jnp.arange(MID, dtype=jnp.int32)[None, None, :]
    send_cells = []
    recv_cells = []
    for route_id in range(4):
        sender = jnp.sum(edge_ids * (routes == PARTNER_ROUTE[route_id]))
        flip = jnp.sum(flips * (edge_ids == sender))
        mapped_pos = jnp.where(flip > 0, MID - 1 - pos, pos)
        send_cells.append(cell_token(sender, frame, OVS - 1 - depth, mapped_pos).reshape(-1))
        target = jnp.sum(edge_ids * (routes == route_id))
        recv_cells.append(cell_token(target, frame, depth, pos).reshape(-1))
    token_ids = jnp.arange(tokens, dtype=jnp.int32)
    send_cells = jnp.concatenate(send_cells)
    recv_cells = jnp.concatenate(recv_cells)
    pick = (send_cells[:, None] == token_ids[None, :]).astype(jnp.bfloat16)
    outgoing = jnp.dot(pick, tile_out, preferred_element_type=jnp.float32).astype(jnp.bfloat16)
    strip_len = frames * OVS * MID
    arrived = []
    for route_id in range(4):
        sent = outgoing[route_id * strip_len : (route_id + 1) * strip_len]
        shift = -OFFSETS[route_id]
        arrived.append(
            lax.ppermute(sent, "face", [(i, (i + shift) % n) for i in range(n)])
        )
    arrived = jnp.concatenate(arrived, axis=0)
    place = (token_ids[:, None] == recv_cells[None, :]).astype(jnp.bfloat16)
    partner = jnp.dot(place, arrived, preferred_element_type=jnp.float32)

    ramp = space_ramp.astype(jnp.float32)
    keep = ramp / (ramp + ramp[::-1])
    take = ramp[::-1] / (ramp + ramp[::-1])
    dep = jnp.asarray(strip_depth(frames))
    in_strip = (dep >= 0)[:, None]
    dep_c = jnp.maximum(dep, 0)
    w_keep = keep[dep_c][:, None]
    w_take = take[dep_c][:, None]
    own = tile_out.astype(jnp.float32)
    spaced = jnp.where(in_strip, w_keep * own + w_take * partner, own).astype(jnp.bfloat16)

    rim = OVT * S * S
    low = spaced[:rim]
    high = spaced[tokens - rim :]
    count = lax.axis_size("tm")
    lower = lax.ppermute(high, "tm", [(i, i + 1) for i in range(count - 1)])
    upper = lax.ppermute(low, "tm", [(i + 1, i) for i in range(count - 1)])
    span_id = lax.axis_index("tm")
    has_lower = span_id > 0
    has_upper = span_id < count - 1
    tramp = time_ramp.astype(jnp.float32)
    hold = tramp / (tramp + tramp[::-1])
    pass_ = tramp[::-1] / (tramp + tramp[::-1])
    per_frame = jnp.arange(rim, dtype=jnp.int32) // (S * S)
    hold_low = hold[per_frame][:, None]
    pass_low = pass_[per_frame][:, None]
    hold_high = hold[OVT - 1 - per_frame][:, None]
    pass_high = pass_[OVT - 1 - per_frame][:, None]
    low_f = low.astype(jnp.float32)
    high_f = high.astype(jnp.float32)
    low_mix = jnp.where(has_lower, hold_low * low_f + pass_low * lower.astype(jnp.float32), low_f)
    high_mix = jnp.where(
        has_upper, hold_high * high_f + pass_high * upper.astype(jnp.float32), high_f
    )
    result = jnp.concatenate(
        [low_mix.astype(jnp.bfloat16), spaced[rim : tokens - rim], high_mix.astype(jnp.bfloat16)],
        axis=0,
    )
    return result.reshape(1, 1, tokens, D)


def solution(mesh):
    return jax.shard_map(
        per_device,
        mesh=mesh,
        in_specs=(
            P(("groups", "tm"), "face", None, None),
            P("groups", None),
            P("face", None),
            P(None, "face"),
            P(),
            P(),
            P(),
        ),
        out_specs=P(("groups", "tm"), "face", None, None),
        check_vma=False,
    )
```

time: 223 us -> 183 us (0.82)
  waiting for transfers between devices: 64.3 us -> 18.6 us
  local copies, waits for them, and re-layouts: 62 us -> 35.4 us
  other arithmetic: 25.9 us -> 45.7 us
  matrix products: 39.2 us -> 54.7 us
  between operations: 21.2 us -> 13.5 us
  starting transfers between devices: 8.71 us -> 12.9 us
    rev x9 -> x2, local copies, waits for them, and re-layouts: 28.7 us -> 1.36 us  [the longest x1 1.26 us: per_device(): keep = ramp / (ramp + ramp[::-1])]
    ppermute x6 -> x12, waiting for transfers between devices: 41 us -> 18.6 us  [the longest x4 12.8 us: per_device(): lax.ppermute(sent, 'face', [(i, (i + shift) % n) for i in range(n)])]
    all_gather x2 -> x0, waiting for transfers between devices: 21.9 us -> none  [the longest x1 21.9 us: per_device(): lax.all_gather(w_qkv, 'face', axis=0, tiled=True)]
    gather x0 -> x5, other arithmetic: none -> 12.3 us  [the longest x1 2.48 us: per_device(): hold_high = hold[OVT - 1 - per_frame][:, None]]
    scatter x4 -> x0, local copies, waits for them, and re-layouts: 12.2 us -> none  [the longest x1 6.36 us: put_strips(): block = block.at[:, :OVS, middle].set(strips[0])]
    add x0 -> x9, local copies, waits for them, and re-layouts: none -> 11.6 us  [the longest x8 11 us: cell_token(): return frame * (S * S) + row * S + col]
    dot_general x2 -> x7, matrix products: 12.3 us -> 22.6 us  [the longest x4 14.7 us: per_device(): jnp.dot(lax.dynamic_index_in_dim(moved_parts, index, 0, keepdims=False),...]
    select_n x0 -> x10, other arithmetic: none -> 5.89 us  [the longest x8 4.4 us: cell_token(): jnp.where(edge == 2, depth, S - 1 - depth)]
  transfers between devices with their start and end apart: 8 -> 12, of which waited for: 6 -> 6; matrix products, arithmetic and copies ran while one was open for 28% -> 39% of each run, Pallas kernels for 0% -> 0%
where the time goes in v1:
time: 183 us; the launch traced here: 181 us
  matrix products  54.7 us (30%)
  other arithmetic  45.7 us (25%)
  local copies, waits for them, and re-layouts  35.4 us (19%)
  waiting for transfers between devices  18.6 us (10%)
  between operations  13.5 us (7%)
  starting transfers between devices  12.9 us (7%)
    dot_general x8, matrix products, one_head(): jnp.dot(probabilities, valset, preferred_element_type=jnp.float32)  18.9 us
    dot_general x4, matrix products, per_device(): jnp.dot(lax.dynamic_index_in_dim(moved_parts, index, 0, keepdims=False),...  14.7 us
    dot_general x8, matrix products, one_head(): jnp.dot(queries, keyset.T, preferred_element_type=jnp.float32)  13.2 us
    ppermute x4, waiting for transfers between devices, per_device(): lax.ppermute(sent, 'face', [(i, (i + shift) % n) for i in range(n)])  12.8 us
    add x8, local copies, waits for them, and re-layouts, cell_token(): return frame * (S * S) + row * S + col  11 us
    reshape x1, local copies, waits for them, and re-layouts, attend(): qkv_all.reshape(tokens, 3, head_count, head_size).transpose(1, 2, 0, 3)  6.31 us
    squeeze x1, local copies, waits for them, and re-layouts, attend(): outputs = lax.map(one_head, (stacked[0], stacked[1], stacked[2]))  5.27 us
    reduce_sum x8, other arithmetic, one_head(): row_sum = jnp.sum(weights, axis=-1, keepdims=True)  4.53 us
  transfers between devices with their start and end apart: 12, of which 6 were waited for; matrix products, arithmetic and copies ran while one was open for 39% of the time, Pallas kernels for 0%

profile of v1, /device:TPU:0, one launch (start us, length us, event | category | flops | bytes accessed | tf_op | source)
XLA Modules:
  0.0 180.9 jit_solution(10082752999630973510)
XLA Ops:
  0.0 2.9 %collective-permute-start.1 = (bf16[288,1728]{1,0:T(8,128)(2,1)}, bf16[288,1728]{1,0:T(8,128)(2,1)}, u32[]{:S(2)}, u32[]{:S(2)}) collective-permute-start(bf16[288,1728]{1,0:T(8,128)(2,1)} %param.12), channel_id=1, source_target_pairs={{2,0},{3,1},{0,2},{1,3},{6,4},{7,5},{4,6},{5,7},{10,8},{11,9},{8,1... | collective-permute-start | bytes 2985992 | tf_op jit(solution)/shard_map/ppermute | solution.py:57
  3.5 1.9 %convert_reduce_fusion = f32[896]{0:T(1024)S(1)} fusion(bf16[1,1,896,1152]{3,2,1,0:T(8,128)(2,1)} %param.10), kind=kLoop, calls=%fused_computation.31 | loop fusion | flops 2063488 | bytes 2067968 | tf_op jit(solution)/shard_map/reduce_sum | solution.py:25
  5.5 2.9 %copy.10 = f32[1,1,896,1152]{2,3,1,0:T(8,128)} copy(bf16[1,1,896,1152]{3,2,1,0:T(8,128)(2,1)S(1)} %copy-done.1) | data formatting | bytes 6193152 | tf_op jit(solution)/shard_map/convert_element_type | solution.py:115
  31.6 3.3 %fusion.54 = (s32[]{:T(128)}, s32[]{:T(128)}, s32[]{:T(128)}, s32[]{:T(128)}) fusion(s32[4]{0:T(128)S(1)} %copy-done.7, s32[]{:T(128)} %get-tuple-element.115, s32[]{:T(128)} %get-tuple-element.114, s32[]{:T(128)} %get-tuple-element.113, s32[]{:T(128)} %get-tuple-element.116), kind=kLoop, calls=%fused_computation.157 | loop fusion | flops 44 | bytes 48 | tf_op jit(solution)/shard_map/reduce_sum | solution.py:128
  44.7 1.4 add.470
  48.8 1.4 add.443
  50.2 1.4 add.448
  53.0 1.4 add.458
  59.4 2.9 %add_convert_fusion.1 = bf16[896,4,288]{0,2,1:T(8,128)(2,1)S(1)} fusion(f32[896,4,288]{0,2,1:T(8,128)} %bitcast.97, f32[4,288]{1,0:T(4,128)} %add.422, f32[4,288]{1,0:T(4,128)} %mul.208, f32[896]{0:T(1024)S(1)} %add_rsqrt_fusion, f32[896]{0:T(1024)S(1)} %broadcast_multiply_fusion), kind=kLoop, calls=%fused_computation.28 | loop fusion | flops 5160960 | bytes 6209536 | tf_op jit(solution)/shard_map/convert_element_type | solution.py:28
  63.1 2.0 %fusion.39 = f32[896,1728]{0,1:T(8,128)S(1)} fusion(bf16[288,1728]{1,0:T(8,128)(2,1)S(1)} %copy-done.4, bf16[896,4,288]{0,2,1:T(8,128)(2,1)S(1)} %add_convert_fusion.1, s32[]{:T(128)S(6)} %select_n.480), kind=kOutput, calls=%fused_computation.61 | convolution fusion | flops 891813888 | bytes 7741444 | tf_op jit(solution)/shard_map/dot_general | solution.py:94
  67.8 3.7 %fusion.35 = f32[896,1728]{0,1:T(8,128)S(1)} fusion(bf16[288,1728]{1,0:T(8,128)(2,1)} %collective-permute-done.1, bf16[896,4,288]{0,2,1:T(8,128)(2,1)S(1)} %add_convert_fusion.1, s32[]{:T(128)S(6)} %select_n.483), kind=kOutput, calls=%fused_computation.57 | convolution fusion | flops 891813888 | bytes 7704580 | tf_op jit(solution)/shard_map/dot_general | solution.py:94
  71.6 3.2 %fusion.37 = f32[896,1728]{0,1:T(8,128)S(1)} fusion(bf16[288,1728]{1,0:T(8,128)(2,1)} %collective-permute-done, bf16[896,4,288]{0,2,1:T(8,128)(2,1)S(1)} %add_convert_fusion.1, s32[]{:T(128)S(6)} %select_n.481), kind=kOutput, calls=%fused_computation.59 | convolution fusion | flops 891813888 | bytes 7704580 | tf_op jit(solution)/shard_map/dot_general | solution.py:94
  74.8 5.8 %add_convert_fusion = bf16[896,1728]{0,1:T(8,128)(2,1)} fusion(f32[896,1728]{0,1:T(8,128)S(1)} %fusion.35, f32[896,1728]{0,1:T(8,128)S(1)} %fusion.39, f32[896,1728]{0,1:T(8,128)S(1)} %fusion.37, bf16[288,1728]{1,0:T(8,128)(2,1)} %collective-permute-done.2, bf16[896,4,288]{0,2,1:T(8,128)(2,1)S(1)} %add_convert_fusion.1, s32[]{:T(128)S(6)} %select_n.485), kind=kOutput, calls=%fused_computation.18 | convolution fusion | flops 898007040 | bytes 23187460 | tf_op jit(solution)/shard_map/dot_general | solution.py:94
  80.6 6.3 %copy.11 = bf16[896,3,8,72]{3,0,2,1:T(8,128)(2,1)} copy(bf16[896,3,8,72]{0,3,2,1:T(8,128)(2,1)} %bitcast.98) | data formatting | bytes 6193152 | tf_op jit(solution)/shard_map/reshape | solution.py:33
  86.9 5.3 %slice_bitcast_fusion = (bf16[8,896,72]{2,1,0:T(8,128)(2,1)}, bf16[8,896,72]{2,1,0:T(8,128)(2,1)}, bf16[8,896,72]{2,1,0:T(8,128)(2,1)}) fusion(bf16[3,8,896,72]{3,2,1,0:T(8,128)(2,1)} %bitcast.96), kind=kLoop, calls=%fused_computation.34 | loop fusion | bytes 6193152 | tf_op jit(solution)/shard_map/squeeze | solution.py:48
  92.2 36.7 %while.10 = (s32[]{:T(128)}, bf16[8,896,72]{1,2,0:T(8,128)(2,1)}, bf16[8,896,72]{2,1,0:T(8,128)(2,1)}, bf16[8,896,72]{2,1,0:T(8,128)(2,1)}, bf16[8,896,72]{2,1,0:T(8,128)(2,1)}, /*index=5*/s32[]{:T(128)}) while((s32[]{:T(128)}, bf16[8,896,72]{1,2,0:T(8,128)(2,1)}, bf16[8,896,72]{2,1,0:T(8,128)(2,1)}, bf16[8,896,72]{2,1,0:T(8,128)(2,1)}, ...), condition=%wide.region_5.6_spmd, body=%wide.region_2.5_spmd.sunk | while | flops 238499072 | bytes 10470981 | solution.py:48
  92.2 1.7 multiply_reduce_fusion.2
  94.5 2.4 %fusion.77 = bf16[8,896,72]{1,2,0:T(8,128)(2,1)} fusion(bf16[8,896,72]{1,2,0:T(8,128)(2,1)} %get-tuple-element.161, s32[]{:T(128)} %get-tuple-element.160, f32[896,896]{0,1:T(8,128)S(1)} %get-tuple-element.152, f32[896]{0:T(1024)S(1)} %fusion.76, f32[896]{0:T(1024)S(1)} %get-tuple-element.153, bf16[8,896,72]{2,1,0:T(8,128)(2,1)} %get-tuple-element.170), kind=kOutput, calls=%fused_computation.7.clone.1 | convolution fusion | flops 118881280 | bytes 3577856 | tf_op jit(solution)/shard_map/while/body/eval_jaxpr/dot_general | solution.py:44
  96.9 1.6 multiply_reduce_fusion.2
  99.1 2.4 %fusion.77 = bf16[8,896,72]{1,2,0:T(8,128)(2,1)} fusion(bf16[8,896,72]{1,2,0:T(8,128)(2,1)} %get-tuple-element.161, s32[]{:T(128)} %get-tuple-element.160, f32[896,896]{0,1:T(8,128)S(1)} %get-tuple-element.152, f32[896]{0:T(1024)S(1)} %fusion.76, f32[896]{0:T(1024)S(1)} %get-tuple-element.153, bf16[8,896,72]{2,1,0:T(8,128)(2,1)} %get-tuple-element.170), kind=kOutput, calls=%fused_computation.7.clone.1 | convolution fusion | flops 118881280 | bytes 3577856 | tf_op jit(solution)/shard_map/while/body/eval_jaxpr/dot_general | solution.py:44
  101.5 1.6 multiply_reduce_fusion.2
  103.7 2.4 %fusion.77 = bf16[8,896,72]{1,2,0:T(8,128)(2,1)} fusion(bf16[8,896,72]{1,2,0:T(8,128)(2,1)} %get-tuple-element.161, s32[]{:T(128)} %get-tuple-element.160, f32[896,896]{0,1:T(8,128)S(1)} %get-tuple-element.152, f32[896]{0:T(1024)S(1)} %fusion.76, f32[896]{0:T(1024)S(1)} %get-tuple-element.153, bf16[8,896,72]{2,1,0:T(8,128)(2,1)} %get-tuple-element.170), kind=kOutput, calls=%fused_computation.7.clone.1 | convolution fusion | flops 118881280 | bytes 3577856 | tf_op jit(solution)/shard_map/while/body/eval_jaxpr/dot_general | solution.py:44
  106.1 1.6 multiply_reduce_fusion.2
  108.3 2.4 %fusion.77 = bf16[8,896,72]{1,2,0:T(8,128)(2,1)} fusion(bf16[8,896,72]{1,2,0:T(8,128)(2,1)} %get-tuple-element.161, s32[]{:T(128)} %get-tuple-element.160, f32[896,896]{0,1:T(8,128)S(1)} %get-tuple-element.152, f32[896]{0:T(1024)S(1)} %fusion.76, f32[896]{0:T(1024)S(1)} %get-tuple-element.153, bf16[8,896,72]{2,1,0:T(8,128)(2,1)} %get-tuple-element.170), kind=kOutput, calls=%fused_computation.7.clone.1 | convolution fusion | flops 118881280 | bytes 3577856 | tf_op jit(solution)/shard_map/while/body/eval_jaxpr/dot_general | solution.py:44
  110.6 1.6 multiply_reduce_fusion.2
  112.8 2.4 %fusion.77 = bf16[8,896,72]{1,2,0:T(8,128)(2,1)} fusion(bf16[8,896,72]{1,2,0:T(8,128)(2,1)} %get-tuple-element.161, s32[]{:T(128)} %get-tuple-element.160, f32[896,896]{0,1:T(8,128)S(1)} %get-tuple-element.152, f32[896]{0:T(1024)S(1)} %fusion.76, f32[896]{0:T(1024)S(1)} %get-tuple-element.153, bf16[8,896,72]{2,1,0:T(8,128)(2,1)} %get-tuple-element.170), kind=kOutput, calls=%fused_computation.7.clone.1 | convolution fusion | flops 118881280 | bytes 3577856 | tf_op jit(solution)/shard_map/while/body/eval_jaxpr/dot_general | solution.py:44
  115.2 1.6 multiply_reduce_fusion.2
  117.4 2.3 %fusion.77 = bf16[8,896,72]{1,2,0:T(8,128)(2,1)} fusion(bf16[8,896,72]{1,2,0:T(8,128)(2,1)} %get-tuple-element.161, s32[]{:T(128)} %get-tuple-element.160, f32[896,896]{0,1:T(8,128)S(1)} %get-tuple-element.152, f32[896]{0:T(1024)S(1)} %fusion.76, f32[896]{0:T(1024)S(1)} %get-tuple-element.153, bf16[8,896,72]{2,1,0:T(8,128)(2,1)} %get-tuple-element.170), kind=kOutput, calls=%fused_computation.7.clone.1 | convolution fusion | flops 118881280 | bytes 3577856 | tf_op jit(solution)/shard_map/while/body/eval_jaxpr/dot_general | solution.py:44
  119.8 1.6 multiply_reduce_fusion.2
  122.0 2.4 %fusion.77 = bf16[8,896,72]{1,2,0:T(8,128)(2,1)} fusion(bf16[8,896,72]{1,2,0:T(8,128)(2,1)} %get-tuple-element.161, s32[]{:T(128)} %get-tuple-element.160, f32[896,896]{0,1:T(8,128)S(1)} %get-tuple-element.152, f32[896]{0:T(1024)S(1)} %fusion.76, f32[896]{0:T(1024)S(1)} %get-tuple-element.153, bf16[8,896,72]{2,1,0:T(8,128)(2,1)} %get-tuple-element.170), kind=kOutput, calls=%fused_computation.7.clone.1 | convolution fusion | flops 118881280 | bytes 3577856 | tf_op jit(solution)/shard_map/while/body/eval_jaxpr/dot_general | solution.py:44
  124.3 1.6 multiply_reduce_fusion.2
  126.6 2.4 %fusion.77 = bf16[8,896,72]{1,2,0:T(8,128)(2,1)} fusion(bf16[8,896,72]{1,2,0:T(8,128)(2,1)} %get-tuple-element.161, s32[]{:T(128)} %get-tuple-element.160, f32[896,896]{0,1:T(8,128)S(1)} %get-tuple-element.152, f32[896]{0:T(1024)S(1)} %fusion.76, f32[896]{0:T(1024)S(1)} %get-tuple-element.153, bf16[8,896,72]{2,1,0:T(8,128)(2,1)} %get-tuple-element.170), kind=kOutput, calls=%fused_computation.7.clone.1 | convolution fusion | flops 118881280 | bytes 3577856 | tf_op jit(solution)/shard_map/while/body/eval_jaxpr/dot_general | solution.py:44
  128.9 3.2 %fusion.19 = bf16[896,1152]{1,0:T(8,128)(2,1)S(1)} fusion(bf16[896,576]{0,1:T(8,128)(2,1)} %bitcast.23, bf16[576,1152]{0,1:T(8,128)(2,1)S(1)} %bitcast.99, bf16[1,1,896,1152]{3,2,1,0:T(8,128)(2,1)S(1)} %copy-done.1, f32[1152]{0:T(1024)S(1)} %copy-done.6), kind=kOutput, calls=%fused_computation.29 | convolution fusion | flops 1193213952 | bytes 6492672 | tf_op jit(solution)/shard_map/dot_general | solution.py:114
  133.8 1.6 collective-permute-start.6
  137.7 2.5 %broadcast_select_fusion.1 = (f32[896]{0:T(1024)S(1)}, f32[896]{0:T(1024)S(1)}) fusion(pred[896]{0:T(1024)(128)(4,1)S(1)} %copy-done.17, f32[]{:T(128)} %bitcast.10, f32[]{:T(128)} %bitcast.9, f32[]{:T(128)} %bitcast.31, f32[]{:T(128)} %bitcast.30), kind=kLoop, calls=%fused_computation.107 | loop fusion | flops 1792 | bytes 8080 | tf_op jit(solution)/shard_map/gather | solution.py:156
  140.1 1.9 %collective-permute-done.6 = bf16[112,1152]{1,0:T(8,128)(2,1)S(1)} collective-permute-done((bf16[112,1152]{1,0:T(8,128)(2,1)S(1)}, bf16[112,1152]{1,0:T(8,128)(2,1)S(1)}, u32[]{:S(2)}, u32[]{:S(2)}) %collective-permute-start.6) | collective-permute-done | bytes 258080 | tf_op jit(solution)/shard_map/ppermute | solution.py:144
  142.0 1.9 %collective-permute-done.7 = bf16[112,1152]{1,0:T(8,128)(2,1)S(1)} collective-permute-done((bf16[112,1152]{1,0:T(8,128)(2,1)S(1)}, bf16[112,1152]{1,0:T(8,128)(2,1)S(1)}, u32[]{:S(2)}, u32[]{:S(2)}) %collective-permute-start.7) | collective-permute-done | bytes 258080 | tf_op jit(solution)/shard_map/ppermute | solution.py:144
  143.9 3.6 %collective-permute-done.8 = bf16[112,1152]{1,0:T(8,128)(2,1)S(1)} collective-permute-done((bf16[112,1152]{1,0:T(8,128)(2,1)S(1)}, bf16[112,1152]{1,0:T(8,128)(2,1)S(1)}, u32[]{:S(2)}, u32[]{:S(2)}) %collective-permute-start.8) | collective-permute-done | bytes 258080 | tf_op jit(solution)/shard_map/ppermute | solution.py:144
  147.5 5.4 %collective-permute-done.9 = bf16[112,1152]{1,0:T(8,128)(2,1)S(1)} collective-permute-done((bf16[112,1152]{1,0:T(8,128)(2,1)S(1)}, bf16[112,1152]{1,0:T(8,128)(2,1)S(1)}, u32[]{:S(2)}, u32[]{:S(2)}) %collective-permute-start.9) | collective-permute-done | bytes 258080 | tf_op jit(solution)/shard_map/ppermute | solution.py:144
  152.9 3.3 %fusion.20 = bf16[896,1152]{1,0:T(8,128)(2,1)S(1)} fusion(bf16[896,1152]{1,0:T(8,128)(2,1)} %copy-done.20, f32[896]{0:T(1024)S(1)} %get-tuple-element.78, f32[896]{0:T(1024)S(1)} %get-tuple-element.77, pred[896]{0:T(1024)(128)(4,1)S(1)} %copy-done.19, bf16[112,1152]{1,0:T(8,128)(2,1)S(1)} %collective-permute-done.9, ...), kind=kOutput, calls=%fused_computation.30 | convolution fusion | flops 935567360 | bytes 5170816 | tf_op jit(solution)/shard_map/dot_general | solution.py:148
  157.3 3.8 %collective-permute-start.10 = (bf16[256,1152]{1,0:T(8,128)(2,1)}, bf16[256,1152]{1,0:T(8,128)(2,1)S(1)}, u32[]{:S(2)}, u32[]{:S(2)}) collective-permute-start(bf16[256,1152]{1,0:T(8,128)(2,1)} %get-tuple-element.61), channel_id=1, source_target_pairs={{0,4},{4,8},{8,12},{1,5},{5,9},{9,13},{2,6},{6,10},{10,14},{3,7},{... | collective-permute-start | bytes 1769480 | tf_op jit(solution)/shard_map/ppermute | solution.py:165
  163.1 2.5 %compare_select_fusion.9 = f32[256,1]{0,1:T(1,128)S(1)} fusion(f32[]{:T(128)} %bitcast.33, f32[]{:T(128)} %bitcast.34, f32[]{:T(128)} %bitcast.36, f32[]{:T(128)} %bitcast.35), kind=kLoop, calls=%fused_computation.98 | loop fusion | flops 4352 | bytes 1040 | tf_op jit(solution)/shard_map/gather | solution.py:175
  165.5 2.5 %compare_select_fusion.3 = f32[256,1]{0,1:T(1,128)S(1)} fusion(f32[]{:T(128)} %bitcast.33, f32[]{:T(128)} %bitcast.34, f32[]{:T(128)} %bitcast.36, f32[]{:T(128)} %bitcast.35), kind=kLoop, calls=%fused_computation.92 | loop fusion | flops 4608 | bytes 1040 | tf_op jit(solution)/shard_map/gather | solution.py:177
  168.0 2.5 %compare_select_fusion.2 = f32[256,1]{0,1:T(1,128)S(1)} fusion(f32[]{:T(128)} %bitcast.4, f32[]{:T(128)} %bitcast.5, f32[]{:T(128)} %bitcast.7, f32[]{:T(128)} %bitcast.6), kind=kLoop, calls=%fused_computation.91 | loop fusion | flops 4608 | bytes 1040 | tf_op jit(solution)/shard_map/gather | solution.py:176
  170.5 2.5 %compare_select_fusion.8 = f32[256,1]{0,1:T(1,128)S(1)} fusion(f32[]{:T(128)} %bitcast.4, f32[]{:T(128)} %bitcast.5, f32[]{:T(128)} %bitcast.7, f32[]{:T(128)} %bitcast.6), kind=kLoop, calls=%fused_computation.97 | loop fusion | flops 4352 | bytes 1040 | tf_op jit(solution)/shard_map/gather | solution.py:174
  173.1 1.8 collective-permute-done.10
  174.8 4.1 %collective-permute-done.11 = bf16[256,1152]{1,0:T(8,128)(2,1)S(1)} collective-permute-done((bf16[256,1152]{1,0:T(8,128)(2,1)}, bf16[256,1152]{1,0:T(8,128)(2,1)S(1)}, u32[]{:S(2)}, u32[]{:S(2)}) %collective-permute-start.11) | collective-permute-done | bytes 589856 | tf_op jit(solution)/shard_map/ppermute | solution.py:166
  179.5 1.5 maximum_bitcast_fusion
  (122 shorter events, 45.1 us)
Async XLA Ops:
  0.0 8.3 %copy-start = (s32[4,4,4]{2,1,0:T(4,128)S(1)}, s32[4,4,4]{2,1,0:T(4,128)}, u32[]{:S(2)}) copy-start(s32[4,4,4]{2,1,0:T(4,128)} %param.14) | copy-start | bytes 772
  0.0 5.5 %copy-start.1 = (bf16[1,1,896,1152]{3,2,1,0:T(8,128)(2,1)S(1)}, bf16[1,1,896,1152]{3,2,1,0:T(8,128)(2,1)}, u32[]{:S(2)}) copy-start(bf16[1,1,896,1152]{3,2,1,0:T(8,128)(2,1)} %param.10) | copy-start | bytes 6193156
  0.0 67.2 %collective-permute-start.1 = (bf16[288,1728]{1,0:T(8,128)(2,1)}, bf16[288,1728]{1,0:T(8,128)(2,1)}, u32[]{:S(2)}, u32[]{:S(2)}) collective-permute-start(bf16[288,1728]{1,0:T(8,128)(2,1)} %param.12), channel_id=1, source_target_pairs={{2,0},{3,1},{0,2},{1,3},{6,4},{7,5},{4,6},{5,7},{10,8},{11,9},{8,1... | collective-permute-start | bytes 2985992 | tf_op jit(solution)/shard_map/ppermute | solution.py:57
  2.9 68.7 %collective-permute-start = (bf16[288,1728]{1,0:T(8,128)(2,1)}, bf16[288,1728]{1,0:T(8,128)(2,1)}, u32[]{:S(2)}, u32[]{:S(2)}) collective-permute-start(bf16[288,1728]{1,0:T(8,128)(2,1)} %param.12), channel_id=1, source_target_pairs={{1,0},{0,1},{3,2},{2,3},{5,4},{4,5},{7,6},{6,7},{9,8},{8,9},{11,10... | collective-permute-start | bytes 2985992 | tf_op jit(solution)/shard_map/ppermute | solution.py:57
  2.9 62.2 %collective-permute-start.3 = (bf16[576,288]{0,1:T(8,128)(2,1)}, bf16[576,288]{0,1:T(8,128)(2,1)}, u32[]{:S(2)}, u32[]{:S(2)}) collective-permute-start(bf16[576,288]{0,1:T(8,128)(2,1)} %param.13), channel_id=1, source_target_pairs={{1,0},{0,1},{3,2},{2,3},{5,4},{4,5},{7,6},{6,7},{9,8},{8,9},{11,10... | collective-permute-start | bytes 995336 | tf_op jit(solution)/shard_map/ppermute | solution.py:57
  3.5 61.6 %collective-permute-start.4 = (bf16[576,288]{0,1:T(8,128)(2,1)}, bf16[576,288]{0,1:T(8,128)(2,1)}, u32[]{:S(2)}, u32[]{:S(2)}) collective-permute-start(bf16[576,288]{0,1:T(8,128)(2,1)} %param.13), channel_id=1, source_target_pairs={{2,0},{3,1},{0,2},{1,3},{6,4},{7,5},{4,6},{5,7},{10,8},{11,9},{8,1... | collective-permute-start | bytes 995336 | tf_op jit(solution)/shard_map/ppermute | solution.py:57
  5.5 22.3 %copy-start.5 = (f32[3,1152]{1,0:T(4,128)S(1)}, f32[3,1152]{1,0:T(4,128)}, u32[]{:S(2)}) copy-start(f32[3,1152]{1,0:T(4,128)} %param.11) | copy-start | bytes 41476
  29.8 1.9 %copy-start.7 = (s32[4]{0:T(128)S(1)}, s32[4]{0:T(128)}, u32[]{:S(2)}) copy-start(s32[4]{0:T(128)} %slice_reduce_fusion.2) | copy-start | bytes 52
  59.4 3.0 %copy-start.13 = (s32[112]{0:T(128)S(1)}, s32[112]{0:T(128)}, u32[]{:S(2)}) copy-start(s32[112]{0:T(128)} %add.464) | copy-start | bytes 1348
  59.4 3.0 %copy-start.14 = (s32[112]{0:T(128)S(1)}, s32[112]{0:T(128)}, u32[]{:S(2)}) copy-start(s32[112]{0:T(128)} %add.470) | copy-start | bytes 1348
  59.4 3.0 %copy-start.15 = (s32[112]{0:T(128)S(1)}, s32[112]{0:T(128)}, u32[]{:S(2)}) copy-start(s32[112]{0:T(128)} %add.476) | copy-start | bytes 1348
  59.4 3.0 %copy-start.16 = (s32[112]{0:T(128)S(1)}, s32[112]{0:T(128)}, u32[]{:S(2)}) copy-start(s32[112]{0:T(128)} %add.482) | copy-start | bytes 1348
  59.4 3.6 %copy-start.4 = (bf16[288,1728]{1,0:T(8,128)(2,1)S(1)}, bf16[288,1728]{1,0:T(8,128)(2,1)}, u32[]{:S(2)}) copy-start(bf16[288,1728]{1,0:T(8,128)(2,1)} %param.12) | copy-start | bytes 2985988
  65.0 2.7 %collective-permute-start.5 = (bf16[576,288]{0,1:T(8,128)(2,1)}, bf16[576,288]{0,1:T(8,128)(2,1)S(1)}, u32[]{:S(2)}, u32[]{:S(2)}) collective-permute-start(bf16[576,288]{0,1:T(8,128)(2,1)} %collective-permute-done.4), channel_id=1, source_target_pairs={{1,0},{0,1},{3,2},{2,3},{5,4},{4,5},{7,6},{6,7},{9,8},{8,9},{11,10... | collective-permute-start | bytes 995336 | tf_op jit(solution)/shard_map/ppermute | solution.py:57
  67.2 7.6 %collective-permute-start.2 = (bf16[288,1728]{1,0:T(8,128)(2,1)}, bf16[288,1728]{1,0:T(8,128)(2,1)}, u32[]{:S(2)}, u32[]{:S(2)}) collective-permute-start(bf16[288,1728]{1,0:T(8,128)(2,1)} %collective-permute-done.1), channel_id=1, source_target_pairs={{1,0},{0,1},{3,2},{2,3},{5,4},{4,5},{7,6},{6,7},{9,8},{8,9},{11,10... | collective-permute-start | bytes 2985992 | tf_op jit(solution)/shard_map/ppermute | solution.py:57
  67.8 3.8 %copy-start.2 = (bf16[4,576,288]{1,2,0:T(8,128)(2,1)}, bf16[4,576,288]{1,2,0:T(8,128)(2,1)S(1)}, u32[]{:S(2)}) copy-start(bf16[4,576,288]{1,2,0:T(8,128)(2,1)S(1)} %bitcast_dynamic-update-slice_fusion) | copy-start | bytes 3981316
  92.2 36.7 %copy-start.3 = (bf16[4,576,288]{1,2,0:T(8,128)(2,1)S(1)}, bf16[4,576,288]{1,2,0:T(8,128)(2,1)}, u32[]{:S(2)}) copy-start(bf16[4,576,288]{1,2,0:T(8,128)(2,1)} %copy-done.2) | copy-start | bytes 3981316
  92.2 36.7 %copy-start.6 = (f32[1152]{0:T(1024)S(1)}, f32[1152]{0:T(1024)}, u32[]{:S(2)}) copy-start(f32[1152]{0:T(1024)} %get-tuple-element.33) | copy-start | bytes 13828
  128.9 3.3 %copy-start.8 = (s32[448]{0:T(512)S(1)}, s32[448]{0:T(512)}, u32[]{:S(2)}) copy-start(s32[448]{0:T(512)} %pad_add_fusion.1) | copy-start | bytes 5380
  132.2 1.4 copy-start.20
  133.6 3.9 %copy-start.9 = (s32[112]{0:T(128)S(1)}, s32[112]{0:T(128)}, u32[]{:S(2)}) copy-start(s32[112]{0:T(128)} %add.443) | copy-start | bytes 1348
  133.6 3.9 %copy-start.10 = (s32[112]{0:T(128)S(1)}, s32[112]{0:T(128)}, u32[]{:S(2)}) copy-start(s32[112]{0:T(128)} %add.448) | copy-start | bytes 1348
  133.6 3.9 %copy-start.11 = (s32[112]{0:T(128)S(1)}, s32[112]{0:T(128)}, u32[]{:S(2)}) copy-start(s32[112]{0:T(128)} %add.453) | copy-start | bytes 1348
  133.6 3.8 %copy-start.12 = (s32[112]{0:T(128)S(1)}, s32[112]{0:T(128)}, u32[]{:S(2)}) copy-start(s32[112]{0:T(128)} %add.458) | copy-start | bytes 1348
  133.6 3.9 %copy-start.18 = (s32[4]{0:T(128)S(1)}, s32[4]{0:T(128)}, u32[]{:S(2)}) copy-start(s32[4]{0:T(128)} %param.16) | copy-start | bytes 52
  133.7 4.0 %copy-start.17 = (pred[896]{0:T(1024)(128)(4,1)S(1)}, pred[896]{0:T(1024)(128)(4,1)}, u32[]{:S(2)}) copy-start(pred[896]{0:T(1024)(128)(4,1)} %constant.163) | copy-start | bytes 2692
  133.7 19.3 %copy-start.19 = (pred[896]{0:T(1024)(128)(4,1)S(1)}, pred[896]{0:T(1024)(128)(4,1)}, u32[]{:S(2)}) copy-start(pred[896]{0:T(1024)(128)(4,1)} %constant.139) | copy-start | bytes 2692
  133.8 8.2 %collective-permute-start.6 = (bf16[112,1152]{1,0:T(8,128)(2,1)S(1)}, bf16[112,1152]{1,0:T(8,128)(2,1)S(1)}, u32[]{:S(2)}, u32[]{:S(2)}) collective-permute-start(bf16[112,1152]{1,0:T(8,128)(2,1)S(1)} %get-tuple-element.63), channel_id=1, source_target_pairs={{0,3},{1,0},{2,1},{3,2},{4,7},{5,4},{6,5},{7,6},{8,11},{9,8},{10,9... | collective-permute-start | bytes 774152 | tf_op jit(solution)/shard_map/ppermute | solution.py:144
  135.4 8.5 %collective-permute-start.7 = (bf16[112,1152]{1,0:T(8,128)(2,1)S(1)}, bf16[112,1152]{1,0:T(8,128)(2,1)S(1)}, u32[]{:S(2)}, u32[]{:S(2)}) collective-permute-start(bf16[112,1152]{1,0:T(8,128)(2,1)S(1)} %get-tuple-element.66), channel_id=1, source_target_pairs={{0,1},{1,2},{2,3},{3,0},{4,5},{5,6},{6,7},{7,4},{8,9},{9,10},{10,1... | collective-permute-start | bytes 774152 | tf_op jit(solution)/shard_map/ppermute | solution.py:144
  135.4 12.1 %collective-permute-start.8 = (bf16[112,1152]{1,0:T(8,128)(2,1)S(1)}, bf16[112,1152]{1,0:T(8,128)(2,1)S(1)}, u32[]{:S(2)}, u32[]{:S(2)}) collective-permute-start(bf16[112,1152]{1,0:T(8,128)(2,1)S(1)} %get-tuple-element.65), channel_id=1, source_target_pairs={{0,2},{1,3},{2,0},{3,1},{4,6},{5,7},{6,4},{7,5},{8,10},{9,11},{10,... | collective-permute-start | bytes 774152 | tf_op jit(solution)/shard_map/ppermute | solution.py:144
  136.3 16.7 %collective-permute-start.9 = (bf16[112,1152]{1,0:T(8,128)(2,1)S(1)}, bf16[112,1152]{1,0:T(8,128)(2,1)S(1)}, u32[]{:S(2)}, u32[]{:S(2)}) collective-permute-start(bf16[112,1152]{1,0:T(8,128)(2,1)S(1)} %get-tuple-element.64), channel_id=1, source_target_pairs={{0,2},{1,3},{2,0},{3,1},{4,6},{5,7},{6,4},{7,5},{8,10},{9,11},{10,... | collective-permute-start | bytes 774152 | tf_op jit(solution)/shard_map/ppermute | solution.py:144
  157.3 17.5 %collective-permute-start.10 = (bf16[256,1152]{1,0:T(8,128)(2,1)}, bf16[256,1152]{1,0:T(8,128)(2,1)S(1)}, u32[]{:S(2)}, u32[]{:S(2)}) collective-permute-start(bf16[256,1152]{1,0:T(8,128)(2,1)} %get-tuple-element.61), channel_id=1, source_target_pairs={{0,4},{4,8},{8,12},{1,5},{5,9},{9,13},{2,6},{6,10},{10,14},{3,7},{... | collective-permute-start | bytes 1769480 | tf_op jit(solution)/shard_map/ppermute | solution.py:165
  161.1 17.8 %collective-permute-start.11 = (bf16[256,1152]{1,0:T(8,128)(2,1)}, bf16[256,1152]{1,0:T(8,128)(2,1)S(1)}, u32[]{:S(2)}, u32[]{:S(2)}) collective-permute-start(bf16[256,1152]{1,0:T(8,128)(2,1)} %get-tuple-element.62), channel_id=1, source_target_pairs={{4,0},{8,4},{12,8},{5,1},{9,5},{13,9},{6,2},{10,6},{14,10},{7,3},{... | collective-permute-start | bytes 1769480 | tf_op jit(solution)/shard_map/ppermute | solution.py:166

commit v2 on v1

--- a/solution.py
+++ b/solution.py
@@ -64,10 +64,22 @@
     return pieces
 
 
-def cell_token(edge, frame, depth, pos):
-    row = jnp.where(edge == 0, depth, jnp.where(edge == 1, S - 1 - depth, OVS + pos))
-    col = jnp.where(edge < 2, OVS + pos, jnp.where(edge == 2, depth, S - 1 - depth))
-    return frame * (S * S) + row * S + col
+def strip_tables(frames):
+    frame, depth, pos = np.meshgrid(
+        np.arange(frames), np.arange(OVS), np.arange(MID), indexing="ij"
+    )
+
+    def token(edge, d, t):
+        row = (d, S - 1 - d, OVS + t, OVS + t)[edge]
+        col = (OVS + t, OVS + t, d, S - 1 - d)[edge]
+        return (frame * (S * S) + row * S + col).reshape(-1)
+
+    recv = np.stack([token(e, depth, pos) for e in range(4)])
+    send = np.stack(
+        [[token(e, OVS - 1 - depth, pos if flip == 0 else MID - 1 - pos) for flip in range(2)]
+         for e in range(4)]
+    )
+    return recv.astype(np.int32), send.astype(np.int32)
 
 
 def strip_depth(frames):
@@ -117,22 +129,15 @@
     my_rows = lax.dynamic_index_in_dim(edge_table, lax.axis_index("face"), 0, keepdims=False)
     flips = my_rows[:, 2]
     routes = my_rows[:, 3]
-    edge_ids = jnp.arange(4, dtype=jnp.int32)
-    frame = jnp.arange(frames, dtype=jnp.int32)[:, None, None]
-    depth = jnp.arange(OVS, dtype=jnp.int32)[None, :, None]
-    pos = jnp.arange(MID, dtype=jnp.int32)[None, None, :]
-    send_cells = []
-    recv_cells = []
-    for route_id in range(4):
-        sender = jnp.sum(edge_ids * (routes == PARTNER_ROUTE[route_id]))
-        flip = jnp.sum(flips * (edge_ids == sender))
-        mapped_pos = jnp.where(flip > 0, MID - 1 - pos, pos)
-        send_cells.append(cell_token(sender, frame, OVS - 1 - depth, mapped_pos).reshape(-1))
-        target = jnp.sum(edge_ids * (routes == route_id))
-        recv_cells.append(cell_token(target, frame, depth, pos).reshape(-1))
+    recv_table, send_table = strip_tables(frames)
+    send_by_edge = jnp.where(flips[:, None] > 0, send_table[:, 1], send_table[:, 0])
+    send_match = routes[None, :] == jnp.asarray(PARTNER_ROUTE, jnp.int32)[:, None]
+    send_cells = jnp.sum(jnp.where(send_match[:, :, None], send_by_edge[None], 0), axis=1)
+    recv_match = routes[None, :] == jnp.arange(4, dtype=jnp.int32)[:, None]
+    recv_cells = jnp.sum(jnp.where(recv_match[:, :, None], recv_table[None], 0), axis=1)
+    send_cells = send_cells.reshape(-1)
+    recv_cells = recv_cells.reshape(-1)
     token_ids = jnp.arange(tokens, dtype=jnp.int32)
-    send_cells = jnp.concatenate(send_cells)
-    recv_cells = jnp.concatenate(recv_cells)
     pick = (send_cells[:, None] == token_ids[None, :]).astype(jnp.bfloat16)
     outgoing = jnp.dot(pick, tile_out, preferred_element_type=jnp.float32).astype(jnp.bfloat16)
     strip_len = frames * OVS * MID
@@ -150,11 +155,10 @@
     ramp = space_ramp.astype(jnp.float32)
     keep = ramp / (ramp + ramp[::-1])
     take = ramp[::-1] / (ramp + ramp[::-1])
-    dep = jnp.asarray(strip_depth(frames))
-    in_strip = (dep >= 0)[:, None]
-    dep_c = jnp.maximum(dep, 0)
-    w_keep = keep[dep_c][:, None]
-    w_take = take[dep_c][:, None]
+    dep = strip_depth(frames)[:, None]
+    w_keep = jnp.where(dep == 0, keep[0], keep[1])
+    w_take = jnp.where(dep == 0, take[0], take[1])
+    in_strip = dep >= 0
     own = tile_out.astype(jnp.float32)
     spaced = jnp.where(in_strip, w_keep * own + w_take * partner, own).astype(jnp.bfloat16)
 
@@ -170,17 +174,19 @@
     tramp = time_ramp.astype(jnp.float32)
     hold = tramp / (tramp + tramp[::-1])
     pass_ = tramp[::-1] / (tramp + tramp[::-1])
-    per_frame = jnp.arange(rim, dtype=jnp.int32) // (S * S)
-    hold_low = hold[per_frame][:, None]
-    pass_low = pass_[per_frame][:, None]
-    hold_high = hold[OVT - 1 - per_frame][:, None]
-    pass_high = pass_[OVT - 1 - per_frame][:, None]
-    low_f = low.astype(jnp.float32)
-    high_f = high.astype(jnp.float32)
-    low_mix = jnp.where(has_lower, hold_low * low_f + pass_low * lower.astype(jnp.float32), low_f)
+    blocks = (OVT, S * S, D)
+    low_f = low.astype(jnp.float32).reshape(blocks)
+    high_f = high.astype(jnp.float32).reshape(blocks)
+    hold_low = hold[:, None, None]
+    pass_low = pass_[:, None, None]
+    hold_high = hold[::-1][:, None, None]
+    pass_high = pass_[::-1][:, None, None]
+    low_mix = jnp.where(
+        has_lower, hold_low * low_f + pass_low * lower.astype(jnp.float32).reshape(blocks), low_f
+    ).reshape(rim, D)
     high_mix = jnp.where(
-        has_upper, hold_high * high_f + pass_high * upper.astype(jnp.float32), high_f
-    )
+        has_upper, hold_high * high_f + pass_high * upper.astype(jnp.float32).reshape(blocks), high_f
+    ).reshape(rim, D)
     result = jnp.concatenate(
         [low_mix.astype(jnp.bfloat16), spaced[rim : tokens - rim], high_mix.astype(jnp.bfloat16)],
         axis=0,

time: 183 us -> 146 us (0.80)
  other arithmetic: 45.7 us -> 16.5 us
  waiting for transfers between devices: 18.6 us -> 42.1 us
  between operations: 13.5 us -> 0.3 us
  local copies, waits for them, and re-layouts: 35.4 us -> 24.4 us
  matrix products: 54.7 us -> 48.9 us
    ppermute x6, waiting for transfers between devices: 0.02 us -> 14.5 us  [fetch(): return lax.ppermute(x, 'face', [(src_of(i), i) for i in range(n)])]
    gather x5 -> x0, other arithmetic: 12.3 us -> none  [the longest x1 2.48 us: per_device(): hold_high = hold[OVT - 1 - per_frame][:, None]]
    add x8 -> x0, local copies, waits for them, and re-layouts: 11 us -> none  [cell_token(): return frame * (S * S) + row * S + col]
    ppermute x1, waiting for transfers between devices: 1.75 us -> 11.4 us  [per_device(): lower = lax.ppermute(high, 'tm', [(i, i + 1) for i in range(count - 1)])]
    dot_general x8, matrix products: 18.9 us -> 13.7 us  [one_head(): jnp.dot(probabilities, valset, preferred_element_type=jnp.float32)]
    reduce_sum x3 -> x2, other arithmetic: 4.76 us -> 0.18 us  [the longest x1 0.09 us: per_device(): jnp.sum(jnp.where(recv_match[:, :, None], recv_table[None], 0), axis=1)]
    add x6 -> x0, other arithmetic: 3.49 us -> none  [the longest x5 2.15 us: cell_token(): OVS + pos]
    select_n x10 -> x2, other arithmetic: 5.89 us -> 2.58 us  [the longest x1 2.51 us: per_device(): w_keep = jnp.where(dep == 0, keep[0], keep[1])]
  transfers between devices with their start and end apart: 12 -> 12, of which waited for: 6 -> 7; matrix products, arithmetic and copies ran while one was open for 39% -> 21% of each run, Pallas kernels for 0% -> 0%
where the time goes in v2:
time: 146 us; the launch traced here: 145 us
  matrix products  48.9 us (33%)
  waiting for transfers between devices  42.1 us (29%)
  local copies, waits for them, and re-layouts  24.4 us (17%)
  other arithmetic  16.5 us (11%)
  starting transfers between devices  12.6 us (9%)
    ppermute x6, waiting for transfers between devices, fetch(): return lax.ppermute(x, 'face', [(src_of(i), i) for i in range(n)])  14.5 us
    dot_general x4, matrix products, per_device(): jnp.dot(lax.dynamic_index_in_dim(moved_parts, index, 0, keepdims=False),...  14 us
    dot_general x8, matrix products, one_head(): jnp.dot(probabilities, valset, preferred_element_type=jnp.float32)  13.7 us
    dot_general x8, matrix products, one_head(): jnp.dot(queries, keyset.T, preferred_element_type=jnp.float32)  13.1 us
    ppermute x4, waiting for transfers between devices, per_device(): lax.ppermute(sent, 'face', [(i, (i + shift) % n) for i in range(n)])  12.1 us
    ppermute x1, waiting for transfers between devices, per_device(): lower = lax.ppermute(high, 'tm', [(i, i + 1) for i in range(count - 1)])  11.4 us
    reshape x1, local copies, waits for them, and re-layouts, attend(): qkv_all.reshape(tokens, 3, head_count, head_size).transpose(1, 2, 0, 3)  6.31 us
    squeeze x1, local copies, waits for them, and re-layouts, attend(): outputs = lax.map(one_head, (stacked[0], stacked[1], stacked[2]))  5.35 us
  transfers between devices with their start and end apart: 12, of which 7 were waited for; matrix products, arithmetic and copies ran while one was open for 21% of the time, Pallas kernels for 0%

profile of v2, /device:TPU:0, one launch (start us, length us, event | category | flops | bytes accessed | tf_op | source)
XLA Modules:
  0.0 145.0 jit_solution(17654898327347398655)
XLA Ops:
  0.0 2.9 %collective-permute-start.1 = (bf16[288,1728]{1,0:T(8,128)(2,1)}, bf16[288,1728]{1,0:T(8,128)(2,1)}, u32[]{:S(2)}, u32[]{:S(2)}) collective-permute-start(bf16[288,1728]{1,0:T(8,128)(2,1)} %param.18), channel_id=1, source_target_pairs={{2,0},{3,1},{0,2},{1,3},{6,4},{7,5},{4,6},{5,7},{10,8},{11,9},{8,1... | collective-permute-start | bytes 2985992 | tf_op jit(solution)/shard_map/ppermute | solution.py:57
  3.5 1.9 %convert_reduce_fusion = f32[896]{0:T(1024)S(1)} fusion(bf16[1,1,896,1152]{3,2,1,0:T(8,128)(2,1)} %param.16), kind=kLoop, calls=%fused_computation.31 | loop fusion | flops 2063488 | bytes 2067968 | tf_op jit(solution)/shard_map/reduce_sum | solution.py:25
  5.5 2.9 %copy.18 = f32[1,1,896,1152]{2,3,1,0:T(8,128)} copy(bf16[1,1,896,1152]{3,2,1,0:T(8,128)(2,1)S(1)} %copy-done.1) | data formatting | bytes 6193152 | tf_op jit(solution)/shard_map/convert_element_type | solution.py:127
  9.7 1.2 broadcast_in_dim.118
  12.0 4.2 %add_convert_fusion.1 = bf16[896,4,288]{0,2,1:T(8,128)(2,1)} fusion(f32[896,4,288]{0,2,1:T(8,128)} %bitcast.85, f32[4,288]{1,0:T(4,128)S(1)} %add.106, f32[4,288]{1,0:T(4,128)S(1)} %mul.114, f32[896]{0:T(1024)S(1)} %add_rsqrt_fusion, f32[896]{0:T(1024)S(1)} %broadcast_multiply_fusion), kind=kLoop, calls=%fused_computation.28 | loop fusion | flops 5160960 | bytes 6209536 | tf_op jit(solution)/shard_map/convert_element_type | solution.py:28
  16.4 3.0 %fusion.39 = f32[896,1728]{0,1:T(8,128)S(1)} fusion(bf16[288,1728]{1,0:T(8,128)(2,1)S(1)} %copy-done.3, bf16[896,4,288]{0,2,1:T(8,128)(2,1)} %add_convert_fusion.1, s32[]{:T(128)S(6)} %select_n.76), kind=kOutput, calls=%fused_computation.61 | convolution fusion | flops 891813888 | bytes 7704580 | tf_op jit(solution)/shard_map/dot_general | solution.py:106
  19.4 14.5 %collective-permute-done.4 = bf16[576,288]{0,1:T(8,128)(2,1)} collective-permute-done((bf16[576,288]{0,1:T(8,128)(2,1)}, bf16[576,288]{0,1:T(8,128)(2,1)}, u32[]{:S(2)}, u32[]{:S(2)}) %collective-permute-start.4) | collective-permute-done | bytes 331808 | tf_op jit(solution)/shard_map/ppermute | solution.py:57
  34.0 1.8 %bitcast_dynamic-update-slice_fusion.2 = bf16[4,576,288]{1,2,0:T(8,128)(2,1)} fusion(bf16[4,576,288]{1,2,0:T(8,128)(2,1)} %bitcast_dynamic-update-slice_fusion.3, s32[]{:T(128)S(6)} %select_n.77, bf16[576,288]{0,1:T(8,128)(2,1)} %collective-permute-done.3), kind=kLoop, calls=%fused_computation.69 | loop fusion | bytes 737284 | tf_op jit(solution)/shard_map/jit(dynamic_update_index_in_dim)/dynamic_update_slice | solution.py:122
  35.7 1.8 %bitcast_dynamic-update-slice_fusion.1 = bf16[4,576,288]{1,2,0:T(8,128)(2,1)} fusion(bf16[4,576,288]{1,2,0:T(8,128)(2,1)} %bitcast_dynamic-update-slice_fusion.2, s32[]{:T(128)S(6)} %select_n.79, bf16[576,288]{0,1:T(8,128)(2,1)} %collective-permute-done.4), kind=kLoop, calls=%fused_computation.68 | loop fusion | bytes 737284 | tf_op jit(solution)/shard_map/jit(dynamic_update_index_in_dim)/dynamic_update_slice | solution.py:122
  38.8 3.2 %fusion.35 = f32[896,1728]{0,1:T(8,128)S(1)} fusion(bf16[288,1728]{1,0:T(8,128)(2,1)} %collective-permute-done.1, bf16[896,4,288]{0,2,1:T(8,128)(2,1)S(1)} %copy-done.2, s32[]{:T(128)S(6)} %select_n.79), kind=kOutput, calls=%fused_computation.57 | convolution fusion | flops 891813888 | bytes 7704580 | tf_op jit(solution)/shard_map/dot_general | solution.py:106
  42.0 3.2 %fusion.37 = f32[896,1728]{0,1:T(8,128)S(1)} fusion(bf16[288,1728]{1,0:T(8,128)(2,1)} %collective-permute-done, bf16[896,4,288]{0,2,1:T(8,128)(2,1)S(1)} %copy-done.2, s32[]{:T(128)S(6)} %select_n.77), kind=kOutput, calls=%fused_computation.59 | convolution fusion | flops 891813888 | bytes 7704580 | tf_op jit(solution)/shard_map/dot_general | solution.py:106
  45.3 4.6 %add_convert_fusion = bf16[896,1728]{0,1:T(8,128)(2,1)} fusion(f32[896,1728]{0,1:T(8,128)S(1)} %fusion.35, f32[896,1728]{0,1:T(8,128)S(1)} %fusion.39, f32[896,1728]{0,1:T(8,128)S(1)} %fusion.37, bf16[288,1728]{1,0:T(8,128)(2,1)S(1)} %collective-permute-done.2, bf16[896,4,288]{0,2,1:T(8,128)(2,1)S(1)} %copy-done.2, s32[]{:T(128)S(6)} %select_n.81), kind=kOutput, calls=%fused_computation.18 | convolution fusion | flops 898007040 | bytes 23224324 | tf_op jit(solution)/shard_map/dot_general | solution.py:106
  49.8 6.3 %copy.19 = bf16[896,3,8,72]{3,0,2,1:T(8,128)(2,1)} copy(bf16[896,3,8,72]{0,3,2,1:T(8,128)(2,1)} %bitcast.86) | data formatting | bytes 6193152 | tf_op jit(solution)/shard_map/reshape | solution.py:33
  56.2 5.3 %slice_bitcast_fusion = (bf16[8,896,72]{2,1,0:T(8,128)(2,1)}, bf16[8,896,72]{2,1,0:T(8,128)(2,1)}, bf16[8,896,72]{2,1,0:T(8,128)(2,1)}) fusion(bf16[3,8,896,72]{3,2,1,0:T(8,128)(2,1)} %bitcast.84), kind=kLoop, calls=%fused_computation.34 | loop fusion | bytes 6193152 | tf_op jit(solution)/shard_map/squeeze | solution.py:48
  61.5 31.6 %while.10 = (s32[]{:T(128)}, bf16[8,896,72]{1,2,0:T(8,128)(2,1)S(1)}, bf16[8,896,72]{2,1,0:T(8,128)(2,1)}, bf16[8,896,72]{2,1,0:T(8,128)(2,1)}, bf16[8,896,72]{2,1,0:T(8,128)(2,1)}, /*index=5*/s32[]{:T(128)}) while((s32[]{:T(128)}, bf16[8,896,72]{1,2,0:T(8,128)(2,1)S(1)}, bf16[8,896,72]{2,1,0:T(8,128)(2,1)}, bf16[8,896,72]{2,1,0:T(8,128)(2,1)}, ...), condition=%wide.region_5.6_spmd, body=%wide.region_2.5_spmd.sunk | while | flops 238499072 | bytes 10472005 | solution.py:48
  61.5 1.6 %multiply_reduce_fusion.2 = (f32[896]{0:T(1024)S(1)}, f32[896,896]{0,1:T(8,128)S(1)}) fusion(bf16[8,896,72]{2,1,0:T(8,128)(2,1)} %get-tuple-element.123, s32[]{:T(128)} %get-tuple-element.114, bf16[8,896,72]{2,1,0:T(8,128)(2,1)} %get-tuple-element.122), kind=kOutput, calls=%fused_computation.2.clone.1 | convolution fusion | flops 117210240 | bytes 3674624 | tf_op jit(solution)/shard_map/while/body/eval_jaxpr/dot_general | solution.py:37
  63.7 1.7 %fusion.68 = bf16[8,896,72]{1,2,0:T(8,128)(2,1)S(1)} fusion(bf16[8,896,72]{1,2,0:T(8,128)(2,1)S(1)} %get-tuple-element.115, s32[]{:T(128)} %get-tuple-element.114, f32[896,896]{0,1:T(8,128)S(1)} %get-tuple-element.106, f32[896]{0:T(1024)S(1)} %fusion.67, f32[896]{0:T(1024)S(1)} %get-tuple-element.107, bf16[8,896,72]{2,1,0:T(8,128)(2,1)} %get-tuple-element.124), kind=kOutput, calls=%fused_computation.7.clone.1 | convolution fusion | flops 118881280 | bytes 3578880 | tf_op jit(solution)/shard_map/while/body/eval_jaxpr/dot_general | solution.py:44
  65.4 1.6 %multiply_reduce_fusion.2 = (f32[896]{0:T(1024)S(1)}, f32[896,896]{0,1:T(8,128)S(1)}) fusion(bf16[8,896,72]{2,1,0:T(8,128)(2,1)} %get-tuple-element.123, s32[]{:T(128)} %get-tuple-element.114, bf16[8,896,72]{2,1,0:T(8,128)(2,1)} %get-tuple-element.122), kind=kOutput, calls=%fused_computation.2.clone.1 | convolution fusion | flops 117210240 | bytes 3674624 | tf_op jit(solution)/shard_map/while/body/eval_jaxpr/dot_general | solution.py:37
  67.7 1.7 %fusion.68 = bf16[8,896,72]{1,2,0:T(8,128)(2,1)S(1)} fusion(bf16[8,896,72]{1,2,0:T(8,128)(2,1)S(1)} %get-tuple-element.115, s32[]{:T(128)} %get-tuple-element.114, f32[896,896]{0,1:T(8,128)S(1)} %get-tuple-element.106, f32[896]{0:T(1024)S(1)} %fusion.67, f32[896]{0:T(1024)S(1)} %get-tuple-element.107, bf16[8,896,72]{2,1,0:T(8,128)(2,1)} %get-tuple-element.124), kind=kOutput, calls=%fused_computation.7.clone.1 | convolution fusion | flops 118881280 | bytes 3578880 | tf_op jit(solution)/shard_map/while/body/eval_jaxpr/dot_general | solution.py:44
  69.4 1.6 %multiply_reduce_fusion.2 = (f32[896]{0:T(1024)S(1)}, f32[896,896]{0,1:T(8,128)S(1)}) fusion(bf16[8,896,72]{2,1,0:T(8,128)(2,1)} %get-tuple-element.123, s32[]{:T(128)} %get-tuple-element.114, bf16[8,896,72]{2,1,0:T(8,128)(2,1)} %get-tuple-element.122), kind=kOutput, calls=%fused_computation.2.clone.1 | convolution fusion | flops 117210240 | bytes 3674624 | tf_op jit(solution)/shard_map/while/body/eval_jaxpr/dot_general | solution.py:37
  71.6 1.7 %fusion.68 = bf16[8,896,72]{1,2,0:T(8,128)(2,1)S(1)} fusion(bf16[8,896,72]{1,2,0:T(8,128)(2,1)S(1)} %get-tuple-element.115, s32[]{:T(128)} %get-tuple-element.114, f32[896,896]{0,1:T(8,128)S(1)} %get-tuple-element.106, f32[896]{0:T(1024)S(1)} %fusion.67, f32[896]{0:T(1024)S(1)} %get-tuple-element.107, bf16[8,896,72]{2,1,0:T(8,128)(2,1)} %get-tuple-element.124), kind=kOutput, calls=%fused_computation.7.clone.1 | convolution fusion | flops 118881280 | bytes 3578880 | tf_op jit(solution)/shard_map/while/body/eval_jaxpr/dot_general | solution.py:44
  73.3 1.6 %multiply_reduce_fusion.2 = (f32[896]{0:T(1024)S(1)}, f32[896,896]{0,1:T(8,128)S(1)}) fusion(bf16[8,896,72]{2,1,0:T(8,128)(2,1)} %get-tuple-element.123, s32[]{:T(128)} %get-tuple-element.114, bf16[8,896,72]{2,1,0:T(8,128)(2,1)} %get-tuple-element.122), kind=kOutput, calls=%fused_computation.2.clone.1 | convolution fusion | flops 117210240 | bytes 3674624 | tf_op jit(solution)/shard_map/while/body/eval_jaxpr/dot_general | solution.py:37
  75.6 1.7 %fusion.68 = bf16[8,896,72]{1,2,0:T(8,128)(2,1)S(1)} fusion(bf16[8,896,72]{1,2,0:T(8,128)(2,1)S(1)} %get-tuple-element.115, s32[]{:T(128)} %get-tuple-element.114, f32[896,896]{0,1:T(8,128)S(1)} %get-tuple-element.106, f32[896]{0:T(1024)S(1)} %fusion.67, f32[896]{0:T(1024)S(1)} %get-tuple-element.107, bf16[8,896,72]{2,1,0:T(8,128)(2,1)} %get-tuple-element.124), kind=kOutput, calls=%fused_computation.7.clone.1 | convolution fusion | flops 118881280 | bytes 3578880 | tf_op jit(solution)/shard_map/while/body/eval_jaxpr/dot_general | solution.py:44
  77.3 1.6 %multiply_reduce_fusion.2 = (f32[896]{0:T(1024)S(1)}, f32[896,896]{0,1:T(8,128)S(1)}) fusion(bf16[8,896,72]{2,1,0:T(8,128)(2,1)} %get-tuple-element.123, s32[]{:T(128)} %get-tuple-element.114, bf16[8,896,72]{2,1,0:T(8,128)(2,1)} %get-tuple-element.122), kind=kOutput, calls=%fused_computation.2.clone.1 | convolution fusion | flops 117210240 | bytes 3674624 | tf_op jit(solution)/shard_map/while/body/eval_jaxpr/dot_general | solution.py:37
  79.5 1.7 %fusion.68 = bf16[8,896,72]{1,2,0:T(8,128)(2,1)S(1)} fusion(bf16[8,896,72]{1,2,0:T(8,128)(2,1)S(1)} %get-tuple-element.115, s32[]{:T(128)} %get-tuple-element.114, f32[896,896]{0,1:T(8,128)S(1)} %get-tuple-element.106, f32[896]{0:T(1024)S(1)} %fusion.67, f32[896]{0:T(1024)S(1)} %get-tuple-element.107, bf16[8,896,72]{2,1,0:T(8,128)(2,1)} %get-tuple-element.124), kind=kOutput, calls=%fused_computation.7.clone.1 | convolution fusion | flops 118881280 | bytes 3578880 | tf_op jit(solution)/shard_map/while/body/eval_jaxpr/dot_general | solution.py:44
  81.2 1.6 %multiply_reduce_fusion.2 = (f32[896]{0:T(1024)S(1)}, f32[896,896]{0,1:T(8,128)S(1)}) fusion(bf16[8,896,72]{2,1,0:T(8,128)(2,1)} %get-tuple-element.123, s32[]{:T(128)} %get-tuple-element.114, bf16[8,896,72]{2,1,0:T(8,128)(2,1)} %get-tuple-element.122), kind=kOutput, calls=%fused_computation.2.clone.1 | convolution fusion | flops 117210240 | bytes 3674624 | tf_op jit(solution)/shard_map/while/body/eval_jaxpr/dot_general | solution.py:37
  83.5 1.7 %fusion.68 = bf16[8,896,72]{1,2,0:T(8,128)(2,1)S(1)} fusion(bf16[8,896,72]{1,2,0:T(8,128)(2,1)S(1)} %get-tuple-element.115, s32[]{:T(128)} %get-tuple-element.114, f32[896,896]{0,1:T(8,128)S(1)} %get-tuple-element.106, f32[896]{0:T(1024)S(1)} %fusion.67, f32[896]{0:T(1024)S(1)} %get-tuple-element.107, bf16[8,896,72]{2,1,0:T(8,128)(2,1)} %get-tuple-element.124), kind=kOutput, calls=%fused_computation.7.clone.1 | convolution fusion | flops 118881280 | bytes 3578880 | tf_op jit(solution)/shard_map/while/body/eval_jaxpr/dot_general | solution.py:44
  85.2 1.6 %multiply_reduce_fusion.2 = (f32[896]{0:T(1024)S(1)}, f32[896,896]{0,1:T(8,128)S(1)}) fusion(bf16[8,896,72]{2,1,0:T(8,128)(2,1)} %get-tuple-element.123, s32[]{:T(128)} %get-tuple-element.114, bf16[8,896,72]{2,1,0:T(8,128)(2,1)} %get-tuple-element.122), kind=kOutput, calls=%fused_computation.2.clone.1 | convolution fusion | flops 117210240 | bytes 3674624 | tf_op jit(solution)/shard_map/while/body/eval_jaxpr/dot_general | solution.py:37
  87.4 1.7 %fusion.68 = bf16[8,896,72]{1,2,0:T(8,128)(2,1)S(1)} fusion(bf16[8,896,72]{1,2,0:T(8,128)(2,1)S(1)} %get-tuple-element.115, s32[]{:T(128)} %get-tuple-element.114, f32[896,896]{0,1:T(8,128)S(1)} %get-tuple-element.106, f32[896]{0:T(1024)S(1)} %fusion.67, f32[896]{0:T(1024)S(1)} %get-tuple-element.107, bf16[8,896,72]{2,1,0:T(8,128)(2,1)} %get-tuple-element.124), kind=kOutput, calls=%fused_computation.7.clone.1 | convolution fusion | flops 118881280 | bytes 3578880 | tf_op jit(solution)/shard_map/while/body/eval_jaxpr/dot_general | solution.py:44
  89.1 1.6 %multiply_reduce_fusion.2 = (f32[896]{0:T(1024)S(1)}, f32[896,896]{0,1:T(8,128)S(1)}) fusion(bf16[8,896,72]{2,1,0:T(8,128)(2,1)} %get-tuple-element.123, s32[]{:T(128)} %get-tuple-element.114, bf16[8,896,72]{2,1,0:T(8,128)(2,1)} %get-tuple-element.122), kind=kOutput, calls=%fused_computation.2.clone.1 | convolution fusion | flops 117210240 | bytes 3674624 | tf_op jit(solution)/shard_map/while/body/eval_jaxpr/dot_general | solution.py:37
  91.4 1.7 %fusion.68 = bf16[8,896,72]{1,2,0:T(8,128)(2,1)S(1)} fusion(bf16[8,896,72]{1,2,0:T(8,128)(2,1)S(1)} %get-tuple-element.115, s32[]{:T(128)} %get-tuple-element.114, f32[896,896]{0,1:T(8,128)S(1)} %get-tuple-element.106, f32[896]{0:T(1024)S(1)} %fusion.67, f32[896]{0:T(1024)S(1)} %get-tuple-element.107, bf16[8,896,72]{2,1,0:T(8,128)(2,1)} %get-tuple-element.124), kind=kOutput, calls=%fused_computation.7.clone.1 | convolution fusion | flops 118881280 | bytes 3578880 | tf_op jit(solution)/shard_map/while/body/eval_jaxpr/dot_general | solution.py:44
  93.1 3.4 %fusion.19 = bf16[896,1152]{1,0:T(8,128)(2,1)S(1)} fusion(bf16[896,576]{0,1:T(8,128)(2,1)S(1)} %bitcast.87, bf16[576,1152]{0,1:T(8,128)(2,1)} %bitcast.24, bf16[1,1,896,1152]{3,2,1,0:T(8,128)(2,1)S(1)} %copy-done.1, f32[1152]{0:T(1024)S(1)} %get-tuple-element.33), kind=kOutput, calls=%fused_computation.29 | convolution fusion | flops 1193213952 | bytes 6492672 | tf_op jit(solution)/shard_map/dot_general | solution.py:126
  96.5 1.4 convolution_convert_fusion
  98.1 1.4 collective-permute-start.6
  99.5 0.8 collective-permute-start.8
  100.3 1.2 collective-permute-start.9
  102.4 2.5 %select_reduce_fusion.3 = (f32[896]{0:T(1024)S(1)}, f32[896]{0:T(1024)S(1)}) fusion(pred[896,1]{0,1:T(4,128)(4,1)S(1)} %copy-done.6, f32[]{:T(128)} %bitcast.5, f32[]{:T(128)} %bitcast.4, f32[]{:T(128)} %bitcast.26, f32[]{:T(128)} %bitcast.25), kind=kLoop, calls=%fused_computation.78 | loop fusion | flops 1792 | bytes 8080 | tf_op jit(solution)/shard_map/jit(_where)/select_n | solution.py:159
  104.9 1.2 collective-permute-done.6
  106.1 1.9 %collective-permute-done.7 = bf16[112,1152]{1,0:T(8,128)(2,1)S(1)} collective-permute-done((bf16[112,1152]{1,0:T(8,128)(2,1)S(1)}, bf16[112,1152]{1,0:T(8,128)(2,1)S(1)}, u32[]{:S(2)}, u32[]{:S(2)}) %collective-permute-start.7) | collective-permute-done | bytes 258080 | tf_op jit(solution)/shard_map/ppermute | solution.py:149
  108.0 3.6 %collective-permute-done.8 = bf16[112,1152]{1,0:T(8,128)(2,1)S(1)} collective-permute-done((bf16[112,1152]{1,0:T(8,128)(2,1)S(1)}, bf16[112,1152]{1,0:T(8,128)(2,1)S(1)}, u32[]{:S(2)}, u32[]{:S(2)}) %collective-permute-start.8) | collective-permute-done | bytes 258080 | tf_op jit(solution)/shard_map/ppermute | solution.py:149
  111.6 5.3 %collective-permute-done.9 = bf16[112,1152]{1,0:T(8,128)(2,1)S(1)} collective-permute-done((bf16[112,1152]{1,0:T(8,128)(2,1)S(1)}, bf16[112,1152]{1,0:T(8,128)(2,1)S(1)}, u32[]{:S(2)}, u32[]{:S(2)}) %collective-permute-start.9) | collective-permute-done | bytes 258080 | tf_op jit(solution)/shard_map/ppermute | solution.py:149
  117.0 3.3 %fusion.20 = bf16[896,1152]{1,0:T(8,128)(2,1)S(1)} fusion(bf16[896,1152]{1,0:T(8,128)(2,1)} %copy-done.15, f32[896]{0:T(1024)S(1)} %get-tuple-element.37, f32[896]{0:T(1024)S(1)} %get-tuple-element.36, pred[896]{0:T(1024)(128)(4,1)S(1)} %copy-done.14, bf16[112,1152]{1,0:T(8,128)(2,1)S(1)} %collective-permute-done.9, ...), kind=kOutput, calls=%fused_computation.30 | convolution fusion | flops 935567360 | bytes 5170816 | tf_op jit(solution)/shard_map/dot_general | solution.py:153
  120.2 1.1 fusion.52
  121.3 3.8 %collective-permute-start.10 = (bf16[256,1152]{1,0:T(8,128)(2,1)}, bf16[256,1152]{1,0:T(8,128)(2,1)S(1)}, u32[]{:S(2)}, u32[]{:S(2)}) collective-permute-start(bf16[256,1152]{1,0:T(8,128)(2,1)} %get-tuple-element.55), channel_id=1, source_target_pairs={{0,4},{4,8},{8,12},{1,5},{5,9},{9,13},{2,6},{6,10},{10,14},{3,7},{... | collective-permute-start | bytes 1769480 | tf_op jit(solution)/shard_map/ppermute | solution.py:169
  125.1 1.3 collective-permute-start.11
  127.4 11.4 %collective-permute-done.10 = bf16[256,1152]{1,0:T(8,128)(2,1)S(1)} collective-permute-done((bf16[256,1152]{1,0:T(8,128)(2,1)}, bf16[256,1152]{1,0:T(8,128)(2,1)S(1)}, u32[]{:S(2)}, u32[]{:S(2)}) %collective-permute-start.10) | collective-permute-done | bytes 589856 | tf_op jit(solution)/shard_map/ppermute | solution.py:169
  138.9 4.0 %collective-permute-done.11 = bf16[256,1152]{1,0:T(8,128)(2,1)S(1)} collective-permute-done((bf16[256,1152]{1,0:T(8,128)(2,1)}, bf16[256,1152]{1,0:T(8,128)(2,1)S(1)}, u32[]{:S(2)}, u32[]{:S(2)}) %collective-permute-start.11) | collective-permute-done | bytes 589856 | tf_op jit(solution)/shard_map/ppermute | solution.py:170
  143.5 1.5 %maximum_bitcast_fusion = bf16[1,1,896,1152]{3,2,1,0:T(8,128)(2,1)} fusion(bf16[256,1152]{1,0:T(8,128)(2,1)S(1)} %get-tuple-element.54, bf16[384,1152]{1,0:T(8,128)(2,1)S(1)} %slice.85, bf16[256,1152]{1,0:T(8,128)(2,1)S(1)} %get-tuple-element.53), kind=kLoop, calls=%fused_computation.33 | loop fusion | flops 6193152 | bytes 4128768 | tf_op jit(solution)/shard_map/reshape | solution.py:194
  (89 shorter events, 11.5 us)
Async XLA Ops:
  0.0 8.3 %copy-start = (s32[4,4,4]{2,1,0:T(4,128)S(1)}, s32[4,4,4]{2,1,0:T(4,128)}, u32[]{:S(2)}) copy-start(s32[4,4,4]{2,1,0:T(4,128)} %param.20) | copy-start | bytes 772
  0.0 5.5 %copy-start.1 = (bf16[1,1,896,1152]{3,2,1,0:T(8,128)(2,1)S(1)}, bf16[1,1,896,1152]{3,2,1,0:T(8,128)(2,1)}, u32[]{:S(2)}) copy-start(bf16[1,1,896,1152]{3,2,1,0:T(8,128)(2,1)} %param.16) | copy-start | bytes 6193156
  0.0 37.5 %collective-permute-start.1 = (bf16[288,1728]{1,0:T(8,128)(2,1)}, bf16[288,1728]{1,0:T(8,128)(2,1)}, u32[]{:S(2)}, u32[]{:S(2)}) collective-permute-start(bf16[288,1728]{1,0:T(8,128)(2,1)} %param.18), channel_id=1, source_target_pairs={{2,0},{3,1},{0,2},{1,3},{6,4},{7,5},{4,6},{5,7},{10,8},{11,9},{8,1... | collective-permute-start | bytes 2985992 | tf_op jit(solution)/shard_map/ppermute | solution.py:57
  2.9 39.1 %collective-permute-start = (bf16[288,1728]{1,0:T(8,128)(2,1)}, bf16[288,1728]{1,0:T(8,128)(2,1)}, u32[]{:S(2)}, u32[]{:S(2)}) collective-permute-start(bf16[288,1728]{1,0:T(8,128)(2,1)} %param.18), channel_id=1, source_target_pairs={{1,0},{0,1},{3,2},{2,3},{5,4},{4,5},{7,6},{6,7},{9,8},{8,9},{11,10... | collective-permute-start | bytes 2985992 | tf_op jit(solution)/shard_map/ppermute | solution.py:57
  2.9 31.0 %collective-permute-start.3 = (bf16[576,288]{0,1:T(8,128)(2,1)}, bf16[576,288]{0,1:T(8,128)(2,1)}, u32[]{:S(2)}, u32[]{:S(2)}) collective-permute-start(bf16[576,288]{0,1:T(8,128)(2,1)} %param.19), channel_id=1, source_target_pairs={{1,0},{0,1},{3,2},{2,3},{5,4},{4,5},{7,6},{6,7},{9,8},{8,9},{11,10... | collective-permute-start | bytes 995336 | tf_op jit(solution)/shard_map/ppermute | solution.py:57
  3.5 30.5 %collective-permute-start.4 = (bf16[576,288]{0,1:T(8,128)(2,1)}, bf16[576,288]{0,1:T(8,128)(2,1)}, u32[]{:S(2)}, u32[]{:S(2)}) collective-permute-start(bf16[576,288]{0,1:T(8,128)(2,1)} %param.19), channel_id=1, source_target_pairs={{2,0},{3,1},{0,2},{1,3},{6,4},{7,5},{4,6},{5,7},{10,8},{11,9},{8,1... | collective-permute-start | bytes 995336 | tf_op jit(solution)/shard_map/ppermute | solution.py:57
  5.5 3.3 %copy-start.5 = (f32[3,1152]{1,0:T(4,128)S(1)}, f32[3,1152]{1,0:T(4,128)}, u32[]{:S(2)}) copy-start(f32[3,1152]{1,0:T(4,128)} %param.17) | copy-start | bytes 41476
  8.3 2.6 %copy-start.4 = (bf16[576,288]{0,1:T(8,128)(2,1)S(1)}, bf16[576,288]{0,1:T(8,128)(2,1)}, u32[]{:S(2)}) copy-start(bf16[576,288]{0,1:T(8,128)(2,1)} %param.19) | copy-start | bytes 995332
  8.9 2.8 %copy-start.10 = (s32[2]{0:T(128)S(1)}, s32[2]{0:T(128)}, u32[]{:S(2)}) copy-start(s32[2]{0:T(128)} %param.21) | copy-start | bytes 28
  9.0 2.9 %copy-start.12 = (s32[4]{0:T(128)S(1)}, s32[4]{0:T(128)}, u32[]{:S(2)}) copy-start(s32[4]{0:T(128)} %constant.103.clone) | copy-start | bytes 52
  9.0 3.0 %copy-start.8 = (s32[4,112]{1,0:T(4,128)S(1)}, s32[4,112]{1,0:T(4,128)}, u32[]{:S(2)}) copy-start(s32[4,112]{1,0:T(4,128)} %constant.101.clone) | copy-start | bytes 5380
  9.0 2.9 %copy-start.9 = (s32[4,112]{1,0:T(4,128)S(1)}, s32[4,112]{1,0:T(4,128)}, u32[]{:S(2)}) copy-start(s32[4,112]{1,0:T(4,128)} %constant.102.clone) | copy-start | bytes 5380
  12.0 4.4 %copy-start.3 = (bf16[288,1728]{1,0:T(8,128)(2,1)S(1)}, bf16[288,1728]{1,0:T(8,128)(2,1)}, u32[]{:S(2)}) copy-start(bf16[288,1728]{1,0:T(8,128)(2,1)} %param.18) | copy-start | bytes 2985988
  19.4 19.4 %copy-start.2 = (bf16[896,4,288]{0,2,1:T(8,128)(2,1)S(1)}, bf16[896,4,288]{0,2,1:T(8,128)(2,1)}, u32[]{:S(2)}) copy-start(bf16[896,4,288]{0,2,1:T(8,128)(2,1)} %add_convert_fusion.1) | copy-start | bytes 6193156
  34.0 4.1 %collective-permute-start.5 = (bf16[576,288]{0,1:T(8,128)(2,1)}, bf16[576,288]{0,1:T(8,128)(2,1)S(1)}, u32[]{:S(2)}, u32[]{:S(2)}) collective-permute-start(bf16[576,288]{0,1:T(8,128)(2,1)} %collective-permute-done.4), channel_id=1, source_target_pairs={{1,0},{0,1},{3,2},{2,3},{5,4},{4,5},{7,6},{6,7},{9,8},{8,9},{11,10... | collective-permute-start | bytes 995336 | tf_op jit(solution)/shard_map/ppermute | solution.py:57
  37.5 7.8 %collective-permute-start.2 = (bf16[288,1728]{1,0:T(8,128)(2,1)}, bf16[288,1728]{1,0:T(8,128)(2,1)S(1)}, u32[]{:S(2)}, u32[]{:S(2)}) collective-permute-start(bf16[288,1728]{1,0:T(8,128)(2,1)} %collective-permute-done.1), channel_id=1, source_target_pairs={{1,0},{0,1},{3,2},{2,3},{5,4},{4,5},{7,6},{6,7},{9,8},{8,9},{11,10... | collective-permute-start | bytes 2985992 | tf_op jit(solution)/shard_map/ppermute | solution.py:57
  56.2 5.4 %copy-start.13 = (bf16[8,896,72]{1,2,0:T(8,128)(2,1)S(1)}, bf16[8,896,72]{1,2,0:T(8,128)(2,1)}, u32[]{:S(2)}) copy-start(bf16[8,896,72]{1,2,0:T(8,128)(2,1)} %custom-call) | copy-start | bytes 3096580
  96.5 1.4 copy-start.15
  97.9 3.6 %copy-start.7 = (s32[4,112]{1,0:T(4,128)S(1)}, s32[4,112]{1,0:T(4,128)}, u32[]{:S(2)}) copy-start(s32[4,112]{1,0:T(4,128)} %constant.110) | copy-start | bytes 5380
  98.0 4.4 %copy-start.6 = (pred[896,1]{0,1:T(4,128)(4,1)S(1)}, pred[896,1]{0,1:T(4,128)(4,1)}, u32[]{:S(2)}) copy-start(pred[896,1]{0,1:T(4,128)(4,1)} %constant.105.clone) | copy-start | bytes 2692
  98.0 19.0 %copy-start.14 = (pred[896]{0:T(1024)(128)(4,1)S(1)}, pred[896]{0:T(1024)(128)(4,1)}, u32[]{:S(2)}) copy-start(pred[896]{0:T(1024)(128)(4,1)} %constant.109) | copy-start | bytes 2692
  98.1 8.0 %collective-permute-start.6 = (bf16[112,1152]{1,0:T(8,128)(2,1)S(1)}, bf16[112,1152]{1,0:T(8,128)(2,1)S(1)}, u32[]{:S(2)}, u32[]{:S(2)}) collective-permute-start(bf16[112,1152]{1,0:T(8,128)(2,1)S(1)} %get-tuple-element.57), channel_id=1, source_target_pairs={{0,3},{1,0},{2,1},{3,2},{4,7},{5,4},{6,5},{7,6},{8,11},{9,8},{10,9... | collective-permute-start | bytes 774152 | tf_op jit(solution)/shard_map/ppermute | solution.py:149
  99.5 8.5 %collective-permute-start.7 = (bf16[112,1152]{1,0:T(8,128)(2,1)S(1)}, bf16[112,1152]{1,0:T(8,128)(2,1)S(1)}, u32[]{:S(2)}, u32[]{:S(2)}) collective-permute-start(bf16[112,1152]{1,0:T(8,128)(2,1)S(1)} %get-tuple-element.60), channel_id=1, source_target_pairs={{0,1},{1,2},{2,3},{3,0},{4,5},{5,6},{6,7},{7,4},{8,9},{9,10},{10,1... | collective-permute-start | bytes 774152 | tf_op jit(solution)/shard_map/ppermute | solution.py:149
  99.5 12.1 %collective-permute-start.8 = (bf16[112,1152]{1,0:T(8,128)(2,1)S(1)}, bf16[112,1152]{1,0:T(8,128)(2,1)S(1)}, u32[]{:S(2)}, u32[]{:S(2)}) collective-permute-start(bf16[112,1152]{1,0:T(8,128)(2,1)S(1)} %get-tuple-element.59), channel_id=1, source_target_pairs={{0,2},{1,3},{2,0},{3,1},{4,6},{5,7},{6,4},{7,5},{8,10},{9,11},{10,... | collective-permute-start | bytes 774152 | tf_op jit(solution)/shard_map/ppermute | solution.py:149
  100.3 16.7 %collective-permute-start.9 = (bf16[112,1152]{1,0:T(8,128)(2,1)S(1)}, bf16[112,1152]{1,0:T(8,128)(2,1)S(1)}, u32[]{:S(2)}, u32[]{:S(2)}) collective-permute-start(bf16[112,1152]{1,0:T(8,128)(2,1)S(1)} %get-tuple-element.58), channel_id=1, source_target_pairs={{0,2},{1,3},{2,0},{3,1},{4,6},{5,7},{6,4},{7,5},{8,10},{9,11},{10,... | collective-permute-start | bytes 774152 | tf_op jit(solution)/shard_map/ppermute | solution.py:149
  120.2 6.2 %copy-start.11 = (s32[4]{0:T(128)S(1)}, s32[4]{0:T(128)}, u32[]{:S(2)}) copy-start(s32[4]{0:T(128)} %param.22) | copy-start | bytes 52
  121.3 17.5 %collective-permute-start.10 = (bf16[256,1152]{1,0:T(8,128)(2,1)}, bf16[256,1152]{1,0:T(8,128)(2,1)S(1)}, u32[]{:S(2)}, u32[]{:S(2)}) collective-permute-start(bf16[256,1152]{1,0:T(8,128)(2,1)} %get-tuple-element.55), channel_id=1, source_target_pairs={{0,4},{4,8},{8,12},{1,5},{5,9},{9,13},{2,6},{6,10},{10,14},{3,7},{... | collective-permute-start | bytes 1769480 | tf_op jit(solution)/shard_map/ppermute | solution.py:169
  125.1 17.8 %collective-permute-start.11 = (bf16[256,1152]{1,0:T(8,128)(2,1)}, bf16[256,1152]{1,0:T(8,128)(2,1)S(1)}, u32[]{:S(2)}, u32[]{:S(2)}) collective-permute-start(bf16[256,1152]{1,0:T(8,128)(2,1)} %get-tuple-element.56), channel_id=1, source_target_pairs={{4,0},{8,4},{12,8},{5,1},{9,5},{13,9},{6,2},{10,6},{14,10},{7,3},{... | collective-permute-start | bytes 1769480 | tf_op jit(solution)/shard_map/ppermute | solution.py:170

commit v3 on v2

--- a/solution.py
+++ b/solution.py
@@ -28,10 +28,7 @@
     return (normed * (1.0 + modulation[1]) + modulation[0]).astype(jnp.bfloat16)
 
 
-def attend(qkv_all, head_count, head_size):
-    tokens = qkv_all.shape[0]
-    stacked = qkv_all.reshape(tokens, 3, head_count, head_size).transpose(1, 2, 0, 3)
-
+def attend(queries_all, keys_all, values_all, head_size):
     def one_head(operands):
         queries, keyset, valset = operands
         scores = jnp.dot(queries, keyset.T, preferred_element_type=jnp.float32) * (
@@ -45,8 +42,9 @@
             jnp.bfloat16
         )
 
-    outputs = lax.map(one_head, (stacked[0], stacked[1], stacked[2]))
-    return outputs.transpose(1, 0, 2).reshape(tokens, head_count * head_size)
+    outputs = lax.map(one_head, (queries_all, keys_all, values_all))
+    heads, tokens, size = outputs.shape
+    return outputs.transpose(1, 0, 2).reshape(tokens, heads * size)
 
 
 def face_pieces(shard):
@@ -122,52 +120,82 @@
         out_stack = lax.dynamic_update_index_in_dim(out_stack, piece, index, 0)
     w_out_full = out_stack.transpose(1, 0, 2).reshape(w_out.shape[0], n * w_out.shape[1])
 
-    mixed = attend(qkv_all, HEADS, HD)
-    projected = jnp.dot(mixed, w_out_full, preferred_element_type=jnp.float32)
-    tile_out = (block_in.astype(jnp.float32) + modulation[2] * projected).astype(jnp.bfloat16)
+    stacked = qkv_all.reshape(tokens, 3, HEADS, HD).transpose(1, 2, 0, 3)
+    rim = OVT * S * S
+    queries = stacked[0]
+    rim_queries = jnp.concatenate([queries[:, :rim], queries[:, tokens - rim :]], axis=1)
+    mid_queries = queries[:, rim : tokens - rim]
+    rim_in = jnp.concatenate([block_in[:rim], block_in[tokens - rim :]], axis=0)
+    mid_in = block_in[rim : tokens - rim]
+
+    def project(mixed, part_in):
+        projected = jnp.dot(mixed, w_out_full, preferred_element_type=jnp.float32)
+        return (part_in.astype(jnp.float32) + modulation[2] * projected).astype(jnp.bfloat16)
 
     my_rows = lax.dynamic_index_in_dim(edge_table, lax.axis_index("face"), 0, keepdims=False)
     flips = my_rows[:, 2]
     routes = my_rows[:, 3]
-    recv_table, send_table = strip_tables(frames)
-    send_by_edge = jnp.where(flips[:, None] > 0, send_table[:, 1], send_table[:, 0])
     send_match = routes[None, :] == jnp.asarray(PARTNER_ROUTE, jnp.int32)[:, None]
-    send_cells = jnp.sum(jnp.where(send_match[:, :, None], send_by_edge[None], 0), axis=1)
     recv_match = routes[None, :] == jnp.arange(4, dtype=jnp.int32)[:, None]
-    recv_cells = jnp.sum(jnp.where(recv_match[:, :, None], recv_table[None], 0), axis=1)
-    send_cells = send_cells.reshape(-1)
-    recv_cells = recv_cells.reshape(-1)
-    token_ids = jnp.arange(tokens, dtype=jnp.int32)
-    pick = (send_cells[:, None] == token_ids[None, :]).astype(jnp.bfloat16)
-    outgoing = jnp.dot(pick, tile_out, preferred_element_type=jnp.float32).astype(jnp.bfloat16)
-    strip_len = frames * OVS * MID
-    arrived = []
-    for route_id in range(4):
-        sent = outgoing[route_id * strip_len : (route_id + 1) * strip_len]
-        shift = -OFFSETS[route_id]
-        arrived.append(
-            lax.ppermute(sent, "face", [(i, (i + shift) % n) for i in range(n)])
-        )
-    arrived = jnp.concatenate(arrived, axis=0)
-    place = (token_ids[:, None] == recv_cells[None, :]).astype(jnp.bfloat16)
-    partner = jnp.dot(place, arrived, preferred_element_type=jnp.float32)
-
     ramp = space_ramp.astype(jnp.float32)
     keep = ramp / (ramp + ramp[::-1])
     take = ramp[::-1] / (ramp + ramp[::-1])
-    dep = strip_depth(frames)[:, None]
-    w_keep = jnp.where(dep == 0, keep[0], keep[1])
-    w_take = jnp.where(dep == 0, take[0], take[1])
-    in_strip = dep >= 0
-    own = tile_out.astype(jnp.float32)
-    spaced = jnp.where(in_strip, w_keep * own + w_take * partner, own).astype(jnp.bfloat16)
-
-    rim = OVT * S * S
-    low = spaced[:rim]
-    high = spaced[tokens - rim :]
+
+    def strips_out(tile_out):
+        part_tokens = tile_out.shape[0]
+        part_frames = part_tokens // (S * S)
+        recv_table, send_table = strip_tables(part_frames)
+        send_by_edge = jnp.where(flips[:, None] > 0, send_table[:, 1], send_table[:, 0])
+        send_cells = jnp.sum(jnp.where(send_match[:, :, None], send_by_edge[None], 0), axis=1)
+        send_cells = send_cells.reshape(-1)
+        token_ids = jnp.arange(part_tokens, dtype=jnp.int32)
+        pick = (send_cells[:, None] == token_ids[None, :]).astype(jnp.bfloat16)
+        return jnp.dot(pick, tile_out, preferred_element_type=jnp.float32).astype(jnp.bfloat16)
+
+    def strips_in(outgoing):
+        strip_len = outgoing.shape[0] // 4
+        arrived = []
+        for route_id in range(4):
+            sent = outgoing[route_id * strip_len : (route_id + 1) * strip_len]
+            shift = -OFFSETS[route_id]
+            arrived.append(
+                lax.ppermute(sent, "face", [(i, (i + shift) % n) for i in range(n)])
+            )
+        return jnp.concatenate(arrived, axis=0)
+
+    def space_blend(tile_out, arrived):
+        part_tokens = tile_out.shape[0]
+        part_frames = part_tokens // (S * S)
+        recv_table, _ = strip_tables(part_frames)
+        recv_cells = jnp.sum(jnp.where(recv_match[:, :, None], recv_table[None], 0), axis=1)
+        recv_cells = recv_cells.reshape(-1)
+        token_ids = jnp.arange(part_tokens, dtype=jnp.int32)
+        place = (token_ids[:, None] == recv_cells[None, :]).astype(jnp.bfloat16)
+        partner = jnp.dot(place, arrived, preferred_element_type=jnp.float32)
+        dep = strip_depth(part_frames)[:, None]
+        w_keep = jnp.where(dep == 0, keep[0], keep[1])
+        w_take = jnp.where(dep == 0, take[0], take[1])
+        own = tile_out.astype(jnp.float32)
+        return jnp.where(dep >= 0, w_keep * own + w_take * partner, own).astype(jnp.bfloat16)
+
+    keys_all, values_all = stacked[1], stacked[2]
+    half = HEADS // 2
+    tile_rim = project(attend(rim_queries, keys_all, values_all, HD), rim_in)
+    outgoing_rim = strips_out(tile_rim)
+    arrived_rim = strips_in(outgoing_rim)
+    mid_first, outgoing_rim = lax.optimization_barrier((mid_queries[:half], outgoing_rim))
+    heads_first = attend(mid_first, keys_all[:half], values_all[:half], HD)
+    arrived_rim, heads_first = lax.optimization_barrier((arrived_rim, heads_first))
+    spaced_rim = space_blend(tile_rim, arrived_rim)
+    low, high = lax.optimization_barrier((spaced_rim[:rim], spaced_rim[rim:]))
     count = lax.axis_size("tm")
     lower = lax.ppermute(high, "tm", [(i, i + 1) for i in range(count - 1)])
     upper = lax.ppermute(low, "tm", [(i + 1, i) for i in range(count - 1)])
+    mid_second, low, high = lax.optimization_barrier((mid_queries[half:], low, high))
+    heads_second = attend(mid_second, keys_all[half:], values_all[half:], HD)
+    tile_mid = project(jnp.concatenate([heads_first, heads_second], axis=1), mid_in)
+    spaced_mid = space_blend(tile_mid, strips_in(strips_out(tile_mid)))
+
     span_id = lax.axis_index("tm")
     has_lower = span_id > 0
     has_upper = span_id < count - 1
@@ -188,8 +216,7 @@
         has_upper, hold_high * high_f + pass_high * upper.astype(jnp.float32).reshape(blocks), high_f
     ).reshape(rim, D)
     result = jnp.concatenate(
-        [low_mix.astype(jnp.bfloat16), spaced[rim : tokens - rim], high_mix.astype(jnp.bfloat16)],
-        axis=0,
+        [low_mix.astype(jnp.bfloat16), spaced_mid, high_mix.astype(jnp.bfloat16)], axis=0
     )
     return result.reshape(1, 1, tokens, D)
 

time: 146 us -> 177 us (1.21)
  waiting for transfers between devices: 42.1 us -> 14.9 us
  matrix products: 48.9 us -> 71.2 us
  local copies, waits for them, and re-layouts: 24.4 us -> 41.1 us
  other arithmetic: 16.5 us -> 32.2 us
  starting transfers between devices: 12.6 us -> 15.6 us
    dot_general x8 -> x16, matrix products: 13.7 us -> 30.2 us  [one_head(): jnp.dot(probabilities, valset, preferred_element_type=jnp.float32)]
    ppermute x6, waiting for transfers between devices: 14.5 us -> 0.02 us  [fetch(): return lax.ppermute(x, 'face', [(src_of(i), i) for i in range(n)])]
    ppermute x1, waiting for transfers between devices: 11.4 us -> 0.01 us  [per_device(): lower = lax.ppermute(high, 'tm', [(i, i + 1) for i in range(count - 1)])]
    ppermute x4 -> x8, waiting for transfers between devices: 12.1 us -> 2.43 us  [strips_in(): lax.ppermute(sent, 'face', [(i, (i + shift) % n) for i in range(n)])]
    ppermute x1, waiting for transfers between devices: 4.04 us -> 12.4 us  [per_device(): upper = lax.ppermute(low, 'tm', [(i + 1, i) for i in range(count - 1)])]
    dot_general x8 -> x16, matrix products: 13.1 us -> 18.7 us  [one_head(): jnp.dot(queries, keyset.T, preferred_element_type=jnp.float32)]
    select_n x2 -> x4, other arithmetic: 2.58 us -> 7.06 us  [the longest x2 5.52 us: space_blend(): w_keep = jnp.where(dep == 0, keep[0], keep[1])]
    eq x2 -> x4, local copies, waits for them, and re-layouts: 0.17 us -> 4.6 us  [the longest x2 2.64 us: strips_out(): pick = (send_cells[:, None] == token_ids[None, :]).astype(jnp.bfloat16)]
  transfers between devices with their start and end apart: 12 -> 16, of which waited for: 7 -> 2; matrix products, arithmetic and copies ran while one was open for 21% -> 49% of each run, Pallas kernels for 0% -> 0%
where the time goes in v3:
time: 177 us; the launch traced here: 176 us
  matrix products  71.2 us (40%)
  local copies, waits for them, and re-layouts  41.1 us (23%)
  other arithmetic  32.2 us (18%)
  starting transfers between devices  15.6 us (9%)
  waiting for transfers between devices  14.9 us (8%)
    dot_general x16, matrix products, one_head(): jnp.dot(probabilities, valset, preferred_element_type=jnp.float32)  30.2 us
    dot_general x16, matrix products, one_head(): jnp.dot(queries, keyset.T, preferred_element_type=jnp.float32)  18.7 us
    dot_general x4, matrix products, per_device(): jnp.dot(lax.dynamic_index_in_dim(moved_parts, index, 0, keepdims=False),...  14.3 us
    ppermute x1, waiting for transfers between devices, per_device(): upper = lax.ppermute(low, 'tm', [(i + 1, i) for i in range(count - 1)])  12.4 us
    reduce_sum x16, other arithmetic, one_head(): row_sum = jnp.sum(weights, axis=-1, keepdims=True)  7.24 us
    ppermute x8, starting transfers between devices, strips_in(): lax.ppermute(sent, 'face', [(i, (i + shift) % n) for i in range(n)])  6.78 us
    dot_general x2, matrix products, project(): projected = jnp.dot(mixed, w_out_full, preferred_element_type=jnp.float32)  5.74 us
    select_n x2, other arithmetic, space_blend(): w_keep = jnp.where(dep == 0, keep[0], keep[1])  5.52 us
  transfers between devices with their start and end apart: 16, of which 2 were waited for; matrix products, arithmetic and copies ran while one was open for 49% of the time, Pallas kernels for 0%

profile of v3, /device:TPU:0, one launch (start us, length us, event | category | flops | bytes accessed | tf_op | source)
XLA Modules:
  0.0 175.7 jit_solution(10112417485047478054)
XLA Ops:
  0.0 2.9 %collective-permute-start.1 = (bf16[288,1728]{1,0:T(8,128)(2,1)}, bf16[288,1728]{1,0:T(8,128)(2,1)}, u32[]{:S(2)}, u32[]{:S(2)}) collective-permute-start(bf16[288,1728]{1,0:T(8,128)(2,1)} %param.28), channel_id=1, source_target_pairs={{2,0},{3,1},{0,2},{1,3},{6,4},{7,5},{4,6},{5,7},{10,8},{11,9},{8,1... | collective-permute-start | bytes 2985992 | tf_op jit(solution)/shard_map/ppermute | solution.py:55
  3.5 2.9 %copy.24 = bf16[1,1,896,1152]{2,3,1,0:T(8,128)(2,1)S(1)} copy(bf16[1,1,896,1152]{3,2,1,0:T(8,128)(2,1)} %param.26) | data formatting | bytes 4128768 | tf_op args[0]
  6.4 2.4 %slice_bitcast_fusion.8 = (bf16[256,1152]{1,0:T(8,128)(2,1)}, bf16[256,1152]{1,0:T(8,128)(2,1)}) fusion(bf16[1,1,896,1152]{3,2,1,0:T(8,128)(2,1)} %param.26), kind=kLoop, calls=%fused_computation.90 | loop fusion | bytes 2359296 | tf_op jit(solution)/shard_map/slice | solution.py:128
  38.8 2.8 %add_convert_fusion.1 = bf16[896,4,288]{0,2,1:T(8,128)(2,1)} fusion(f32[4,288]{1,0:T(4,128)S(1)} %add.117, f32[4,288]{1,0:T(4,128)} %mul.144, f32[896]{0:T(1024)S(1)} %add_rsqrt_fusion, f32[896]{0:T(1024)S(1)} %broadcast_multiply_fusion, bf16[896,4,288]{0,2,1:T(8,128)(2,1)S(1)} %bitcast.160), kind=kLoop, calls=%fused_computation.51 | loop fusion | flops 6193152 | bytes 4145152 | tf_op jit(solution)/shard_map/convert_element_type | solution.py:28
  41.6 3.0 %broadcast_select_fusion.1 = (f32[512,1]{0,1:T(1,128)}, f32[512,1]{0,1:T(1,128)}) fusion(pred[512,1]{0,1:T(4,128)(4,1)S(1)} %copy-done.21, f32[]{:T(128)} %bitcast.22, f32[]{:T(128)} %bitcast.21, f32[]{:T(128)} %bitcast.37, f32[]{:T(128)} %bitcast.36), kind=kLoop, calls=%fused_computation.147 | loop fusion | flops 1024 | bytes 4624 | tf_op jit(solution)/shard_map/jit(_where)/select_n | solution.py:176
  47.9 3.3 %fusion.56 = f32[896,1728]{0,1:T(8,128)S(1)} fusion(bf16[288,1728]{1,0:T(8,128)(2,1)} %param.28, bf16[896,4,288]{0,2,1:T(8,128)(2,1)} %add_convert_fusion.1, s32[]{:T(128)S(6)} %select_n.98), kind=kOutput, calls=%fused_computation.98 | convolution fusion | flops 891813888 | bytes 7741444 | tf_op jit(solution)/shard_map/dot_general | solution.py:104
  54.1 3.7 %fusion.52 = f32[896,1728]{0,1:T(8,128)S(1)} fusion(bf16[288,1728]{1,0:T(8,128)(2,1)} %collective-permute-done.1, bf16[896,4,288]{0,2,1:T(8,128)(2,1)S(1)} %copy-done.3, s32[]{:T(128)S(6)} %select_n.101), kind=kOutput, calls=%fused_computation.94 | convolution fusion | flops 891813888 | bytes 7704580 | tf_op jit(solution)/shard_map/dot_general | solution.py:104
  57.9 3.2 %fusion.54 = f32[896,1728]{0,1:T(8,128)S(1)} fusion(bf16[288,1728]{1,0:T(8,128)(2,1)} %collective-permute-done, bf16[896,4,288]{0,2,1:T(8,128)(2,1)S(1)} %copy-done.3, s32[]{:T(128)S(6)} %select_n.99), kind=kOutput, calls=%fused_computation.96 | convolution fusion | flops 891813888 | bytes 7704580 | tf_op jit(solution)/shard_map/dot_general | solution.py:104
  61.1 4.0 %add_convert_fusion = bf16[896,1728]{0,1:T(8,128)(2,1)S(1)} fusion(f32[896,1728]{0,1:T(8,128)S(1)} %fusion.52, f32[896,1728]{0,1:T(8,128)S(1)} %fusion.56, f32[896,1728]{0,1:T(8,128)S(1)} %fusion.54, bf16[288,1728]{1,0:T(8,128)(2,1)S(1)} %collective-permute-done.2, bf16[896,4,288]{0,2,1:T(8,128)(2,1)} %add_convert_fusion.1, s32[]{:T(128)S(6)} %select_n.103), kind=kOutput, calls=%fused_computation.47 | convolution fusion | flops 898007040 | bytes 23187460 | tf_op jit(solution)/shard_map/dot_general | solution.py:104
  65.1 4.5 %copy.25 = bf16[896,3,8,72]{3,0,2,1:T(8,128)(2,1)} copy(bf16[896,3,8,72]{0,3,2,1:T(8,128)(2,1)S(1)} %bitcast.161) | data formatting | bytes 6193152 | tf_op jit(solution)/shard_map/reshape | solution.py:123
  69.6 4.5 %slice_bitcast_fusion = (bf16[8,896,72]{2,1,0:T(8,128)(2,1)}, bf16[8,896,72]{2,1,0:T(8,128)(2,1)S(1)}, bf16[8,896,72]{2,1,0:T(8,128)(2,1)S(1)}) fusion(bf16[3,8,896,72]{3,2,1,0:T(8,128)(2,1)} %bitcast.158), kind=kLoop, calls=%fused_computation.72 | loop fusion | bytes 6193152 | tf_op jit(solution)/shard_map/squeeze | solution.py:181
  74.2 1.6 slice_bitcast_fusion.3
  76.9 33.2 %while.30 = (s32[]{:T(128)}, bf16[8,512,72]{1,2,0:T(8,128)(2,1)}, bf16[8,512,72]{2,1,0:T(8,128)(2,1)}, bf16[8,896,72]{2,1,0:T(8,128)(2,1)S(1)}, bf16[8,896,72]{2,1,0:T(8,128)(2,1)}, /*index=5*/s32[]{:T(128)}) while((s32[]{:T(128)}, bf16[8,512,72]{1,2,0:T(8,128)(2,1)}, bf16[8,512,72]{2,1,0:T(8,128)(2,1)}, bf16[8,896,72]{2,1,0:T(8,128)(2,1)S(1)}, ...), condition=%wide.region_5.6_spmd, body=%wide.region_2.5_spmd.sunk | while | flops 136285184 | bytes 6180933 | solution.py:45
  77.0 1.4 multiply_reduce_fusion.2
  78.9 2.2 %fusion.116 = bf16[8,512,72]{1,2,0:T(8,128)(2,1)} fusion(bf16[8,512,72]{1,2,0:T(8,128)(2,1)} %get-tuple-element.297, s32[]{:T(128)} %get-tuple-element.296, f32[512,896]{1,0:T(8,128)S(1)} %get-tuple-element.274, f32[512]{0:T(512)S(1)} %fusion.115, f32[512]{0:T(512)S(1)} %get-tuple-element.275, bf16[8,896,72]{2,1,0:T(8,128)(2,1)} %get-tuple-element.306), kind=kOutput, calls=%fused_computation.6.clone.1 | convolution fusion | flops 67932160 | bytes 2143232 | tf_op jit(solution)/shard_map/while/body/eval_jaxpr/dot_general | solution.py:41
  81.1 1.4 multiply_reduce_fusion.2
  83.0 2.2 %fusion.116 = bf16[8,512,72]{1,2,0:T(8,128)(2,1)} fusion(bf16[8,512,72]{1,2,0:T(8,128)(2,1)} %get-tuple-element.297, s32[]{:T(128)} %get-tuple-element.296, f32[512,896]{1,0:T(8,128)S(1)} %get-tuple-element.274, f32[512]{0:T(512)S(1)} %fusion.115, f32[512]{0:T(512)S(1)} %get-tuple-element.275, bf16[8,896,72]{2,1,0:T(8,128)(2,1)} %get-tuple-element.306), kind=kOutput, calls=%fused_computation.6.clone.1 | convolution fusion | flops 67932160 | bytes 2143232 | tf_op jit(solution)/shard_map/while/body/eval_jaxpr/dot_general | solution.py:41
  85.3 1.4 multiply_reduce_fusion.2
  87.2 2.2 %fusion.116 = bf16[8,512,72]{1,2,0:T(8,128)(2,1)} fusion(bf16[8,512,72]{1,2,0:T(8,128)(2,1)} %get-tuple-element.297, s32[]{:T(128)} %get-tuple-element.296, f32[512,896]{1,0:T(8,128)S(1)} %get-tuple-element.274, f32[512]{0:T(512)S(1)} %fusion.115, f32[512]{0:T(512)S(1)} %get-tuple-element.275, bf16[8,896,72]{2,1,0:T(8,128)(2,1)} %get-tuple-element.306), kind=kOutput, calls=%fused_computation.6.clone.1 | convolution fusion | flops 67932160 | bytes 2143232 | tf_op jit(solution)/shard_map/while/body/eval_jaxpr/dot_general | solution.py:41
  89.4 1.4 multiply_reduce_fusion.2
  91.3 2.2 %fusion.116 = bf16[8,512,72]{1,2,0:T(8,128)(2,1)} fusion(bf16[8,512,72]{1,2,0:T(8,128)(2,1)} %get-tuple-element.297, s32[]{:T(128)} %get-tuple-element.296, f32[512,896]{1,0:T(8,128)S(1)} %get-tuple-element.274, f32[512]{0:T(512)S(1)} %fusion.115, f32[512]{0:T(512)S(1)} %get-tuple-element.275, bf16[8,896,72]{2,1,0:T(8,128)(2,1)} %get-tuple-element.306), kind=kOutput, calls=%fused_computation.6.clone.1 | convolution fusion | flops 67932160 | bytes 2143232 | tf_op jit(solution)/shard_map/while/body/eval_jaxpr/dot_general | solution.py:41
  95.5 2.3 %fusion.116 = bf16[8,512,72]{1,2,0:T(8,128)(2,1)} fusion(bf16[8,512,72]{1,2,0:T(8,128)(2,1)} %get-tuple-element.297, s32[]{:T(128)} %get-tuple-element.296, f32[512,896]{1,0:T(8,128)S(1)} %get-tuple-element.274, f32[512]{0:T(512)S(1)} %fusion.115, f32[512]{0:T(512)S(1)} %get-tuple-element.275, bf16[8,896,72]{2,1,0:T(8,128)(2,1)} %get-tuple-element.306), kind=kOutput, calls=%fused_computation.6.clone.1 | convolution fusion | flops 67932160 | bytes 2143232 | tf_op jit(solution)/shard_map/while/body/eval_jaxpr/dot_general | solution.py:41
  99.6 2.2 %fusion.116 = bf16[8,512,72]{1,2,0:T(8,128)(2,1)} fusion(bf16[8,512,72]{1,2,0:T(8,128)(2,1)} %get-tuple-element.297, s32[]{:T(128)} %get-tuple-element.296, f32[512,896]{1,0:T(8,128)S(1)} %get-tuple-element.274, f32[512]{0:T(512)S(1)} %fusion.115, f32[512]{0:T(512)S(1)} %get-tuple-element.275, bf16[8,896,72]{2,1,0:T(8,128)(2,1)} %get-tuple-element.306), kind=kOutput, calls=%fused_computation.6.clone.1 | convolution fusion | flops 67932160 | bytes 2143232 | tf_op jit(solution)/shard_map/while/body/eval_jaxpr/dot_general | solution.py:41
  101.9 1.4 multiply_reduce_fusion.2
  103.8 2.2 %fusion.116 = bf16[8,512,72]{1,2,0:T(8,128)(2,1)} fusion(bf16[8,512,72]{1,2,0:T(8,128)(2,1)} %get-tuple-element.297, s32[]{:T(128)} %get-tuple-element.296, f32[512,896]{1,0:T(8,128)S(1)} %get-tuple-element.274, f32[512]{0:T(512)S(1)} %fusion.115, f32[512]{0:T(512)S(1)} %get-tuple-element.275, bf16[8,896,72]{2,1,0:T(8,128)(2,1)} %get-tuple-element.306), kind=kOutput, calls=%fused_computation.6.clone.1 | convolution fusion | flops 67932160 | bytes 2143232 | tf_op jit(solution)/shard_map/while/body/eval_jaxpr/dot_general | solution.py:41
  106.0 1.4 multiply_reduce_fusion.2
  107.9 2.2 %fusion.116 = bf16[8,512,72]{1,2,0:T(8,128)(2,1)} fusion(bf16[8,512,72]{1,2,0:T(8,128)(2,1)} %get-tuple-element.297, s32[]{:T(128)} %get-tuple-element.296, f32[512,896]{1,0:T(8,128)S(1)} %get-tuple-element.274, f32[512]{0:T(512)S(1)} %fusion.115, f32[512]{0:T(512)S(1)} %get-tuple-element.275, bf16[8,896,72]{2,1,0:T(8,128)(2,1)} %get-tuple-element.306), kind=kOutput, calls=%fused_computation.6.clone.1 | convolution fusion | flops 67932160 | bytes 2143232 | tf_op jit(solution)/shard_map/while/body/eval_jaxpr/dot_general | solution.py:41
  110.2 3.1 %fusion.43 = bf16[512,1152]{1,0:T(8,128)(2,1)S(1)} fusion(bf16[512,576]{0,1:T(8,128)(2,1)} %bitcast.29, bf16[576,1152]{0,1:T(8,128)(2,1)} %bitcast.162, bf16[256,1152]{1,0:T(8,128)(2,1)} %get-tuple-element.154, bf16[256,1152]{1,0:T(8,128)(2,1)} %get-tuple-element.153, f32[1152]{0:T(1024)S(1)} %copy-done.8), kind=kOutput, calls=%fused_computation.62 | convolution fusion | flops 683606016 | bytes 4280832 | tf_op jit(solution)/shard_map/dot_general | solution.py:132
  114.6 1.7 collective-permute-start.6
  118.5 13.5 %while.31 = (s32[]{:T(128)}, bf16[4,384,72]{1,2,0:T(8,128)(2,1)S(1)}, bf16[4,384,72]{2,1,0:T(8,128)(2,1)S(1)}, bf16[4,896,72]{2,1,0:T(8,128)(2,1)}, bf16[4,896,72]{2,1,0:T(8,128)(2,1)}, /*index=5*/s32[]{:T(128)}) while((s32[]{:T(128)}, bf16[4,384,72]{1,2,0:T(8,128)(2,1)S(1)}, bf16[4,384,72]{2,1,0:T(8,128)(2,1)S(1)}, ...), condition=%wide.region_11.12_spmd, body=%wide.region_8.11_spmd.sunk | while | flops 101525760 | bytes 4751941 | solution.py:45
  118.5 1.4 fusion.118
  120.3 1.5 fusion.120
  121.8 1.4 fusion.118
  123.6 1.5 fusion.120
  127.0 1.5 fusion.120
  130.4 1.5 fusion.120
  134.7 3.5 %collective-permute-start.10 = (bf16[256,1152]{1,0:T(8,128)(2,1)S(1)}, bf16[256,1152]{1,0:T(8,128)(2,1)S(1)}, u32[]{:S(2)}, u32[]{:S(2)}) collective-permute-start(bf16[256,1152]{1,0:T(8,128)(2,1)S(1)} %get-tuple-element.104), channel_id=1, source_target_pairs={{0,4},{4,8},{8,12},{1,5},{5,9},{9,13},{2,6},{6,10},{10,14},{3,7},{... | collective-permute-start | bytes 1769480 | tf_op jit(solution)/shard_map/ppermute | solution.py:192
  138.3 9.7 %while.32 = (s32[]{:T(128)}, bf16[4,384,72]{1,2,0:T(8,128)(2,1)S(1)}, bf16[4,384,72]{2,1,0:T(8,128)(2,1)S(1)}, bf16[4,896,72]{2,1,0:T(8,128)(2,1)S(1)}, bf16[4,896,72]{2,1,0:T(8,128)(2,1)}, /*index=5*/s32[]{:T(128)}) while((s32[]{:T(128)}, bf16[4,384,72]{1,2,0:T(8,128)(2,1)S(1)}, bf16[4,384,72]{2,1,0:T(8,128)(2,1)S(1)}, ...), condition=%wide.region_15.16_spmd, body=%wide.region_12.15_spmd.sunk | while | flops 101525760 | bytes 4751941 | solution.py:45
  139.1 1.5 fusion.124
  141.6 1.5 fusion.124
  144.0 1.5 fusion.124
  146.4 1.5 fusion.124
  148.0 2.7 %fusion.45 = bf16[384,1152]{1,0:T(8,128)(2,1)S(1)} fusion(bf16[576,1152]{0,1:T(8,128)(2,1)} %bitcast.163, f32[1152]{0:T(1024)S(1)} %copy-done.8, bf16[1,1,896,1152]{3,2,1,0:T(8,128)(2,1)} %param.26, bf16[384,288]{0,1:T(8,128)(2,1)S(1)} %bitcast.164, bf16[384,288]{0,1:T(8,128)(2,1)} %bitcast.165), kind=kOutput, calls=%fused_computation.65 | convolution fusion | flops 512262144 | bytes 3543552 | tf_op jit(solution)/shard_map/dot_general | solution.py:132
  152.7 1.5 collective-permute-start.14
  154.2 2.5 %select_reduce_fusion.5 = (f32[384]{0:T(512)S(1)}, f32[384]{0:T(512)S(1)}) fusion(pred[384,1]{0,1:T(4,128)(4,1)S(1)} %copy-done.22, f32[]{:T(128)} %bitcast.22, f32[]{:T(128)} %bitcast.21, f32[]{:T(128)} %bitcast.37, f32[]{:T(128)} %bitcast.36), kind=kLoop, calls=%fused_computation.144 | loop fusion | flops 768 | bytes 3472 | tf_op jit(solution)/shard_map/jit(_where)/select_n | solution.py:176
  158.1 2.4 %collective-permute-done.14 = bf16[48,1152]{1,0:T(8,128)(2,1)S(1)} collective-permute-done((bf16[48,1152]{1,0:T(8,128)(2,1)S(1)}, bf16[48,1152]{1,0:T(8,128)(2,1)S(1)}, u32[]{:S(2)}, u32[]{:S(2)}) %collective-permute-start.14) | collective-permute-done | bytes 110624 | tf_op jit(solution)/shard_map/ppermute | solution.py:162
  161.4 12.4 %collective-permute-done.15 = bf16[256,1152]{1,0:T(8,128)(2,1)S(1)} collective-permute-done((bf16[256,1152]{1,0:T(8,128)(2,1)S(1)}, bf16[256,1152]{1,0:T(8,128)(2,1)S(1)}, u32[]{:S(2)}, u32[]{:S(2)}) %collective-permute-start.15) | collective-permute-done | bytes 589856 | tf_op jit(solution)/shard_map/ppermute | solution.py:193
  174.2 1.5 maximum_bitcast_fusion
  (162 shorter events, 63.4 us)
Async XLA Ops:
  0.0 8.8 %copy-start = (s32[4,4,4]{2,1,0:T(4,128)S(1)}, s32[4,4,4]{2,1,0:T(4,128)}, u32[]{:S(2)}) copy-start(s32[4,4,4]{2,1,0:T(4,128)} %param.30) | copy-start | bytes 772
  0.0 53.6 %collective-permute-start.1 = (bf16[288,1728]{1,0:T(8,128)(2,1)}, bf16[288,1728]{1,0:T(8,128)(2,1)}, u32[]{:S(2)}, u32[]{:S(2)}) collective-permute-start(bf16[288,1728]{1,0:T(8,128)(2,1)} %param.28), channel_id=1, source_target_pairs={{2,0},{3,1},{0,2},{1,3},{6,4},{7,5},{4,6},{5,7},{10,8},{11,9},{8,1... | collective-permute-start | bytes 2985992 | tf_op jit(solution)/shard_map/ppermute | solution.py:55
  2.9 54.9 %collective-permute-start = (bf16[288,1728]{1,0:T(8,128)(2,1)}, bf16[288,1728]{1,0:T(8,128)(2,1)}, u32[]{:S(2)}, u32[]{:S(2)}) collective-permute-start(bf16[288,1728]{1,0:T(8,128)(2,1)} %param.28), channel_id=1, source_target_pairs={{1,0},{0,1},{3,2},{2,3},{5,4},{4,5},{7,6},{6,7},{9,8},{8,9},{11,10... | collective-permute-start | bytes 2985992 | tf_op jit(solution)/shard_map/ppermute | solution.py:55
  2.9 48.5 %collective-permute-start.3 = (bf16[576,288]{0,1:T(8,128)(2,1)}, bf16[576,288]{0,1:T(8,128)(2,1)}, u32[]{:S(2)}, u32[]{:S(2)}) collective-permute-start(bf16[576,288]{0,1:T(8,128)(2,1)} %param.29), channel_id=1, source_target_pairs={{1,0},{0,1},{3,2},{2,3},{5,4},{4,5},{7,6},{6,7},{9,8},{8,9},{11,10... | collective-permute-start | bytes 995336 | tf_op jit(solution)/shard_map/ppermute | solution.py:55
  3.5 47.9 %collective-permute-start.4 = (bf16[576,288]{0,1:T(8,128)(2,1)}, bf16[576,288]{0,1:T(8,128)(2,1)}, u32[]{:S(2)}, u32[]{:S(2)}) collective-permute-start(bf16[576,288]{0,1:T(8,128)(2,1)} %param.29), channel_id=1, source_target_pairs={{2,0},{3,1},{0,2},{1,3},{6,4},{7,5},{4,6},{5,7},{10,8},{11,9},{8,1... | collective-permute-start | bytes 995336 | tf_op jit(solution)/shard_map/ppermute | solution.py:55
  10.2 1.0 copy-start.7
  14.4 2.1 %copy-start.9 = (pred[4,4]{1,0:T(4,128)(4,1)}, pred[4,4]{1,0:T(4,128)(4,1)S(1)}, u32[]{:S(2)}) copy-start(pred[4,4]{1,0:T(4,128)(4,1)S(1)} %get-tuple-element.175) | copy-start | bytes 52
  14.4 2.1 %copy-start.11 = (pred[4,4]{1,0:T(4,128)(4,1)}, pred[4,4]{1,0:T(4,128)(4,1)S(1)}, u32[]{:S(2)}) copy-start(pred[4,4]{1,0:T(4,128)(4,1)S(1)} %get-tuple-element.176) | copy-start | bytes 52
  38.8 2.8 %copy-start.21 = (pred[512,1]{0,1:T(4,128)(4,1)S(1)}, pred[512,1]{0,1:T(4,128)(4,1)}, u32[]{:S(2)}) copy-start(pred[512,1]{0,1:T(4,128)(4,1)} %constant.150.clone) | copy-start | bytes 1540
  38.8 5.9 %copy-start.10 = (pred[4,4]{1,0:T(4,128)(4,1)S(1)}, pred[4,4]{1,0:T(4,128)(4,1)}, u32[]{:S(2)}) copy-start(pred[4,4]{1,0:T(4,128)(4,1)} %copy-done.9) | copy-start | bytes 52
  38.8 5.9 %copy-start.18 = (s32[4,48]{1,0:T(4,128)S(1)}, s32[4,48]{1,0:T(4,128)}, u32[]{:S(2)}) copy-start(s32[4,48]{1,0:T(4,128)} %constant.162) | copy-start | bytes 2308
  51.3 2.8 %copy-start.3 = (bf16[896,4,288]{0,2,1:T(8,128)(2,1)S(1)}, bf16[896,4,288]{0,2,1:T(8,128)(2,1)}, u32[]{:S(2)}) copy-start(bf16[896,4,288]{0,2,1:T(8,128)(2,1)} %add_convert_fusion.1) | copy-start | bytes 6193156
  51.3 2.7 %collective-permute-start.5 = (bf16[576,288]{0,1:T(8,128)(2,1)}, bf16[576,288]{0,1:T(8,128)(2,1)S(1)}, u32[]{:S(2)}, u32[]{:S(2)}) collective-permute-start(bf16[576,288]{0,1:T(8,128)(2,1)} %collective-permute-done.4), channel_id=1, source_target_pairs={{1,0},{0,1},{3,2},{2,3},{5,4},{4,5},{7,6},{6,7},{9,8},{8,9},{11,10... | collective-permute-start | bytes 995336 | tf_op jit(solution)/shard_map/ppermute | solution.py:55
  53.6 7.5 %collective-permute-start.2 = (bf16[288,1728]{1,0:T(8,128)(2,1)}, bf16[288,1728]{1,0:T(8,128)(2,1)S(1)}, u32[]{:S(2)}, u32[]{:S(2)}) collective-permute-start(bf16[288,1728]{1,0:T(8,128)(2,1)} %collective-permute-done.1), channel_id=1, source_target_pairs={{1,0},{0,1},{3,2},{2,3},{5,4},{4,5},{7,6},{6,7},{9,8},{8,9},{11,10... | collective-permute-start | bytes 2985992 | tf_op jit(solution)/shard_map/ppermute | solution.py:55
  54.1 3.8 %copy-start.4 = (bf16[4,576,288]{1,2,0:T(8,128)(2,1)}, bf16[4,576,288]{1,2,0:T(8,128)(2,1)S(1)}, u32[]{:S(2)}) copy-start(bf16[4,576,288]{1,2,0:T(8,128)(2,1)S(1)} %bitcast_dynamic-update-slice_fusion) | copy-start | bytes 3981316
  69.6 4.6 %copy-start.2 = (bf16[896,3,8,72]{3,0,2,1:T(8,128)(2,1)S(1)}, bf16[896,3,8,72]{3,0,2,1:T(8,128)(2,1)}, u32[]{:S(2)}) copy-start(bf16[896,3,8,72]{3,0,2,1:T(8,128)(2,1)} %copy.25) | copy-start | bytes 9289732
  76.9 33.2 %copy-start.8 = (f32[1152]{0:T(1024)S(1)}, f32[1152]{0:T(1024)}, u32[]{:S(2)}) copy-start(f32[1152]{0:T(1024)} %get-tuple-element.105) | copy-start | bytes 13828
  110.2 3.1 %copy-start.17 = (s32[256]{0:T(256)S(1)}, s32[256]{0:T(256)}, u32[]{:S(2)}) copy-start(s32[256]{0:T(256)} %eq.109) | copy-start | bytes 3076
  114.6 17.3 %collective-permute-start.6 = (bf16[64,1152]{1,0:T(8,128)(2,1)}, bf16[64,1152]{1,0:T(8,128)(2,1)S(1)}, u32[]{:S(2)}, u32[]{:S(2)}) collective-permute-start(bf16[64,1152]{1,0:T(8,128)(2,1)} %get-tuple-element.161), channel_id=1, source_target_pairs={{0,3},{1,0},{2,1},{3,2},{4,7},{5,4},{6,5},{7,6},{8,11},{9,8},{10,9... | collective-permute-start | bytes 442376 | tf_op jit(solution)/shard_map/ppermute | solution.py:162
  116.3 15.6 %collective-permute-start.7 = (bf16[64,1152]{1,0:T(8,128)(2,1)}, bf16[64,1152]{1,0:T(8,128)(2,1)}, u32[]{:S(2)}, u32[]{:S(2)}) collective-permute-start(bf16[64,1152]{1,0:T(8,128)(2,1)} %get-tuple-element.164), channel_id=1, source_target_pairs={{0,1},{1,2},{2,3},{3,0},{4,5},{5,6},{6,7},{7,4},{8,9},{9,10},{10,1... | collective-permute-start | bytes 442376 | tf_op jit(solution)/shard_map/ppermute | solution.py:162
  116.3 15.6 %collective-permute-start.8 = (bf16[64,1152]{1,0:T(8,128)(2,1)}, bf16[64,1152]{1,0:T(8,128)(2,1)}, u32[]{:S(2)}, u32[]{:S(2)}) collective-permute-start(bf16[64,1152]{1,0:T(8,128)(2,1)} %get-tuple-element.163), channel_id=1, source_target_pairs={{0,2},{1,3},{2,0},{3,1},{4,6},{5,7},{6,4},{7,5},{8,10},{9,11},{10,... | collective-permute-start | bytes 442376 | tf_op jit(solution)/shard_map/ppermute | solution.py:162
  117.1 15.6 %collective-permute-start.9 = (bf16[64,1152]{1,0:T(8,128)(2,1)S(1)}, bf16[64,1152]{1,0:T(8,128)(2,1)}, u32[]{:S(2)}, u32[]{:S(2)}) collective-permute-start(bf16[64,1152]{1,0:T(8,128)(2,1)S(1)} %get-tuple-element.162), channel_id=1, source_target_pairs={{0,2},{1,3},{2,0},{3,1},{4,6},{5,7},{6,4},{7,5},{8,10},{9,11},{10,... | collective-permute-start | bytes 442376 | tf_op jit(solution)/shard_map/ppermute | solution.py:162
  118.4 15.4 %copy-start.19 = (f32[512,1]{0,1:T(1,128)S(1)}, f32[512,1]{0,1:T(1,128)}, u32[]{:S(2)}) copy-start(f32[512,1]{0,1:T(1,128)} %get-tuple-element.169) | copy-start | bytes 6148
  118.4 15.4 %copy-start.20 = (f32[512,1]{0,1:T(1,128)S(1)}, f32[512,1]{0,1:T(1,128)}, u32[]{:S(2)}) copy-start(f32[512,1]{0,1:T(1,128)} %get-tuple-element.170) | copy-start | bytes 6148
  118.4 15.4 %copy-start.24 = (s32[256]{0:T(256)S(1)}, s32[256]{0:T(256)}, u32[]{:S(2)}) copy-start(s32[256]{0:T(256)} %eq.104) | copy-start | bytes 3076
  118.4 15.4 %copy-start.26 = (pred[512]{0:T(512)(128)(4,1)S(1)}, pred[512]{0:T(512)(128)(4,1)}, u32[]{:S(2)}) copy-start(pred[512]{0:T(512)(128)(4,1)} %constant.159) | copy-start | bytes 1540
  131.9 0.7 copy-start.5
  131.9 0.7 copy-start.6
  134.7 26.3 %collective-permute-start.10 = (bf16[256,1152]{1,0:T(8,128)(2,1)S(1)}, bf16[256,1152]{1,0:T(8,128)(2,1)S(1)}, u32[]{:S(2)}, u32[]{:S(2)}) collective-permute-start(bf16[256,1152]{1,0:T(8,128)(2,1)S(1)} %get-tuple-element.104), channel_id=1, source_target_pairs={{0,4},{4,8},{8,12},{1,5},{5,9},{9,13},{2,6},{6,10},{10,14},{3,7},{... | collective-permute-start | bytes 1769480 | tf_op jit(solution)/shard_map/ppermute | solution.py:192
  148.0 2.7 %copy-start.16 = (s32[192]{0:T(256)S(1)}, s32[192]{0:T(256)}, u32[]{:S(2)}) copy-start(s32[192]{0:T(256)} %eq.117) | copy-start | bytes 2308
  150.7 3.5 %copy-start.22 = (pred[384,1]{0,1:T(4,128)(4,1)S(1)}, pred[384,1]{0,1:T(4,128)(4,1)}, u32[]{:S(2)}) copy-start(pred[384,1]{0,1:T(4,128)(4,1)} %constant.155.clone) | copy-start | bytes 1156
  150.7 9.8 %copy-start.23 = (s32[192]{0:T(256)S(1)}, s32[192]{0:T(256)}, u32[]{:S(2)}) copy-start(s32[192]{0:T(256)} %eq.114) | copy-start | bytes 2308
  150.7 9.7 %copy-start.25 = (pred[384]{0:T(512)(128)(4,1)S(1)}, pred[384]{0:T(512)(128)(4,1)}, u32[]{:S(2)}) copy-start(pred[384]{0:T(512)(128)(4,1)} %constant.161) | copy-start | bytes 1156
  151.2 5.5 %collective-permute-start.11 = (bf16[48,1152]{1,0:T(8,128)(2,1)S(1)}, bf16[48,1152]{1,0:T(8,128)(2,1)S(1)}, u32[]{:S(2)}, u32[]{:S(2)}) collective-permute-start(bf16[48,1152]{1,0:T(8,128)(2,1)S(1)} %get-tuple-element.165), channel_id=1, source_target_pairs={{0,3},{1,0},{2,1},{3,2},{4,7},{5,4},{6,5},{7,6},{8,11},{9,8},{10,9... | collective-permute-start | bytes 331784 | tf_op jit(solution)/shard_map/ppermute | solution.py:162
  152.1 5.9 %collective-permute-start.12 = (bf16[48,1152]{1,0:T(8,128)(2,1)S(1)}, bf16[48,1152]{1,0:T(8,128)(2,1)S(1)}, u32[]{:S(2)}, u32[]{:S(2)}) collective-permute-start(bf16[48,1152]{1,0:T(8,128)(2,1)S(1)} %get-tuple-element.168), channel_id=1, source_target_pairs={{0,1},{1,2},{2,3},{3,0},{4,5},{5,6},{6,7},{7,4},{8,9},{9,10},{10,1... | collective-permute-start | bytes 331784 | tf_op jit(solution)/shard_map/ppermute | solution.py:162
  152.1 5.9 %collective-permute-start.13 = (bf16[48,1152]{1,0:T(8,128)(2,1)S(1)}, bf16[48,1152]{1,0:T(8,128)(2,1)S(1)}, u32[]{:S(2)}, u32[]{:S(2)}) collective-permute-start(bf16[48,1152]{1,0:T(8,128)(2,1)S(1)} %get-tuple-element.167), channel_id=1, source_target_pairs={{0,2},{1,3},{2,0},{3,1},{4,6},{5,7},{6,4},{7,5},{8,10},{9,11},{10,... | collective-permute-start | bytes 331784 | tf_op jit(solution)/shard_map/ppermute | solution.py:162
  152.7 7.7 %collective-permute-start.14 = (bf16[48,1152]{1,0:T(8,128)(2,1)S(1)}, bf16[48,1152]{1,0:T(8,128)(2,1)S(1)}, u32[]{:S(2)}, u32[]{:S(2)}) collective-permute-start(bf16[48,1152]{1,0:T(8,128)(2,1)S(1)} %get-tuple-element.166), channel_id=1, source_target_pairs={{0,2},{1,3},{2,0},{3,1},{4,6},{5,7},{6,4},{7,5},{8,10},{9,11},{10,... | collective-permute-start | bytes 331784 | tf_op jit(solution)/shard_map/ppermute | solution.py:162
  156.7 17.2 %collective-permute-start.15 = (bf16[256,1152]{1,0:T(8,128)(2,1)S(1)}, bf16[256,1152]{1,0:T(8,128)(2,1)S(1)}, u32[]{:S(2)}, u32[]{:S(2)}) collective-permute-start(bf16[256,1152]{1,0:T(8,128)(2,1)S(1)} %get-tuple-element.100), channel_id=1, source_target_pairs={{4,0},{8,4},{12,8},{5,1},{9,5},{13,9},{6,2},{10,6},{14,10},{7,3},{... | collective-permute-start | bytes 1769480 | tf_op jit(solution)/shard_map/ppermute | solution.py:193
  160.4 0.6 copy-start.12
  160.4 0.7 copy-start.13
  160.4 13.4 %copy-start.14 = (f32[256]{0:T(256)S(1)}, f32[256]{0:T(256)}, u32[]{:S(2)}) copy-start(f32[256]{0:T(256)} %mul.170) | copy-start | bytes 3076
  160.4 13.4 %copy-start.15 = (f32[256]{0:T(256)S(1)}, f32[256]{0:T(256)}, u32[]{:S(2)}) copy-start(f32[256]{0:T(256)} %mul.174) | copy-start | bytes 3076
  173.9 1.8 %copy-start.1 = (s32[4,4,4]{2,1,0:T(4,128)S(1)}, s32[4,4,4]{2,1,0:T(4,128)}, u32[]{:S(2)}) copy-start(s32[4,4,4]{2,1,0:T(4,128)} %param.30) | copy-start | bytes 772

commit v4 on v3

--- a/solution.py
+++ b/solution.py
@@ -4,6 +4,8 @@
 import jax.numpy as jnp
 import numpy as np
 from jax import lax
+from jax.experimental import pallas as pl
+from jax.experimental.pallas import tpu as pltpu
 from jax.sharding import PartitionSpec as P
 
 D = 1152
@@ -28,23 +30,52 @@
     return (normed * (1.0 + modulation[1]) + modulation[0]).astype(jnp.bfloat16)
 
 
-def attend(queries_all, keys_all, values_all, head_size):
-    def one_head(operands):
-        queries, keyset, valset = operands
-        scores = jnp.dot(queries, keyset.T, preferred_element_type=jnp.float32) * (
-            1.0 / math.sqrt(head_size)
+def attention_kernel(q_ref, k_ref, v_ref, w_ref, x_ref, g_ref, o_ref, acc_ref):
+    head = pl.program_id(1)
+
+    @pl.when(head == 0)
+    def _():
+        acc_ref[...] = jnp.zeros_like(acc_ref)
+
+    scores = lax.dot_general(
+        q_ref[0], k_ref[0], (((1,), (1,)), ((), ())), preferred_element_type=jnp.float32
+    ) * (1.0 / math.sqrt(HD))
+    row_max = jnp.max(scores, axis=-1, keepdims=True)
+    weights = jnp.exp(scores - row_max)
+    row_sum = jnp.sum(weights, axis=-1, keepdims=True)
+    probabilities = (weights * (1.0 / row_sum)).astype(jnp.bfloat16)
+    mixed = jnp.dot(probabilities, v_ref[0], preferred_element_type=jnp.float32).astype(
+        jnp.bfloat16
+    )
+    acc_ref[...] += jnp.dot(mixed, w_ref[...], preferred_element_type=jnp.float32)
+
+    @pl.when(head == pl.num_programs(1) - 1)
+    def _():
+        o_ref[...] = (x_ref[...].astype(jnp.float32) + g_ref[...] * acc_ref[...]).astype(
+            o_ref.dtype
         )
-        row_max = jnp.max(scores, axis=-1, keepdims=True)
-        weights = jnp.exp(scores - row_max)
-        row_sum = jnp.sum(weights, axis=-1, keepdims=True)
-        probabilities = (weights / row_sum).astype(jnp.bfloat16)
-        return jnp.dot(probabilities, valset, preferred_element_type=jnp.float32).astype(
-            jnp.bfloat16
-        )
-
-    outputs = lax.map(one_head, (queries_all, keys_all, values_all))
-    heads, tokens, size = outputs.shape
-    return outputs.transpose(1, 0, 2).reshape(tokens, heads * size)
+
+
+def attend_project(queries, keys, values, w_out_full, block_in, gate):
+    heads, tokens, size = keys.shape
+    chunk = queries.shape[1]
+    width = block_in.shape[1]
+    return pl.pallas_call(
+        attention_kernel,
+        grid=(1, heads),
+        in_specs=[
+            pl.BlockSpec((1, chunk, size), lambda i, h: (h, i, 0)),
+            pl.BlockSpec((1, tokens, size), lambda i, h: (h, 0, 0)),
+            pl.BlockSpec((1, tokens, size), lambda i, h: (h, 0, 0)),
+            pl.BlockSpec((size, width), lambda i, h: (h, 0)),
+            pl.BlockSpec((chunk, width), lambda i, h: (i, 0)),
+            pl.BlockSpec((1, width), lambda i, h: (0, 0)),
+        ],
+        out_specs=pl.BlockSpec((chunk, width), lambda i, h: (i, 0)),
+        out_shape=jax.ShapeDtypeStruct(block_in.shape, block_in.dtype),
+        scratch_shapes=[pltpu.VMEM((chunk, width), jnp.float32)],
+        compiler_params=pltpu.CompilerParams(dimension_semantics=("arbitrary", "arbitrary")),
+    )(queries, keys, values, w_out_full, block_in, gate.reshape(1, width))
 
 
 def face_pieces(shard):
@@ -121,16 +152,13 @@
     w_out_full = out_stack.transpose(1, 0, 2).reshape(w_out.shape[0], n * w_out.shape[1])
 
     stacked = qkv_all.reshape(tokens, 3, HEADS, HD).transpose(1, 2, 0, 3)
+    queries, keys, values = stacked[0], stacked[1], stacked[2]
     rim = OVT * S * S
-    queries = stacked[0]
-    rim_queries = jnp.concatenate([queries[:, :rim], queries[:, tokens - rim :]], axis=1)
-    mid_queries = queries[:, rim : tokens - rim]
-    rim_in = jnp.concatenate([block_in[:rim], block_in[tokens - rim :]], axis=0)
-    mid_in = block_in[rim : tokens - rim]
-
-    def project(mixed, part_in):
-        projected = jnp.dot(mixed, w_out_full, preferred_element_type=jnp.float32)
-        return (part_in.astype(jnp.float32) + modulation[2] * projected).astype(jnp.bfloat16)
+    mid_a = rim + ((tokens - 2 * rim) // (2 * S * S)) * (S * S)
+    gate = modulation[2]
+
+    def tile_part(part_queries, part_in):
+        return attend_project(part_queries, keys, values, w_out_full, part_in, gate)
 
     my_rows = lax.dynamic_index_in_dim(edge_table, lax.axis_index("face"), 0, keepdims=False)
     flips = my_rows[:, 2]
@@ -144,7 +172,7 @@
     def strips_out(tile_out):
         part_tokens = tile_out.shape[0]
         part_frames = part_tokens // (S * S)
-        recv_table, send_table = strip_tables(part_frames)
+        _, send_table = strip_tables(part_frames)
         send_by_edge = jnp.where(flips[:, None] > 0, send_table[:, 1], send_table[:, 0])
         send_cells = jnp.sum(jnp.where(send_match[:, :, None], send_by_edge[None], 0), axis=1)
         send_cells = send_cells.reshape(-1)
@@ -178,22 +206,24 @@
         own = tile_out.astype(jnp.float32)
         return jnp.where(dep >= 0, w_keep * own + w_take * partner, own).astype(jnp.bfloat16)
 
-    keys_all, values_all = stacked[1], stacked[2]
-    half = HEADS // 2
-    tile_rim = project(attend(rim_queries, keys_all, values_all, HD), rim_in)
+    rim_queries = jnp.concatenate([queries[:, :rim], queries[:, tokens - rim :]], axis=1)
+    rim_in = jnp.concatenate([block_in[:rim], block_in[tokens - rim :]], axis=0)
+    tile_rim = tile_part(rim_queries, rim_in)
     outgoing_rim = strips_out(tile_rim)
     arrived_rim = strips_in(outgoing_rim)
-    mid_first, outgoing_rim = lax.optimization_barrier((mid_queries[:half], outgoing_rim))
-    heads_first = attend(mid_first, keys_all[:half], values_all[:half], HD)
-    arrived_rim, heads_first = lax.optimization_barrier((arrived_rim, heads_first))
+    first_queries, outgoing_rim = lax.optimization_barrier((queries[:, rim:mid_a], outgoing_rim))
+    tile_first = tile_part(first_queries, block_in[rim:mid_a])
+    arrived_rim, tile_first = lax.optimization_barrier((arrived_rim, tile_first))
     spaced_rim = space_blend(tile_rim, arrived_rim)
     low, high = lax.optimization_barrier((spaced_rim[:rim], spaced_rim[rim:]))
     count = lax.axis_size("tm")
     lower = lax.ppermute(high, "tm", [(i, i + 1) for i in range(count - 1)])
     upper = lax.ppermute(low, "tm", [(i + 1, i) for i in range(count - 1)])
-    mid_second, low, high = lax.optimization_barrier((mid_queries[half:], low, high))
-    heads_second = attend(mid_second, keys_all[half:], values_all[half:], HD)
-    tile_mid = project(jnp.concatenate([heads_first, heads_second], axis=1), mid_in)
+    second_queries, low, high = lax.optimization_barrier(
+        (queries[:, mid_a : tokens - rim], low, high)
+    )
+    tile_second = tile_part(second_queries, block_in[mid_a : tokens - rim])
+    tile_mid = jnp.concatenate([tile_first, tile_second], axis=0)
     spaced_mid = space_blend(tile_mid, strips_in(strips_out(tile_mid)))
 
     span_id = lax.axis_index("tm")

time: 177 us -> 137 us (0.77)
  matrix products: 71.2 us -> 20.2 us
  Pallas kernels: 0 us -> 38.9 us
  other arithmetic: 32.2 us -> 13.2 us
  local copies, waits for them, and re-layouts: 41.1 us -> 27.8 us
  waiting for transfers between devices: 14.9 us -> 20.2 us
    dot_general x34 -> x0, matrix products: 54.6 us -> none  [the longest x16 30.2 us: one_head(): jnp.dot(probabilities, valset, preferred_element_type=jnp.float32)]
    pallas_call x0 -> x3, Pallas kernels: none -> 38.9 us  [attend_project(): pl.pallas_call(attention_kernel, grid=(1, heads), in_specs=[pl.BlockSpec(...]
    reduce_sum x16 -> x0, other arithmetic: 7.24 us -> none  [one_head(): row_sum = jnp.sum(weights, axis=-1, keepdims=True)]
    ppermute x6, waiting for transfers between devices: 0.02 us -> 5.25 us  [fetch(): return lax.ppermute(x, 'face', [(src_of(i), i) for i in range(n)])]
    reduce_sum x2, other arithmetic: 2.71 us -> 0.19 us  [strips_out(): jnp.sum(jnp.where(send_match[:, :, None], send_by_edge[None], 0), axis=1)]
    mul x2, local copies, waits for them, and re-layouts: 2.63 us -> 0.15 us  [per_device(): pass_low * lower.astype(jnp.float32).reshape(blocks)]
    mul x2, local copies, waits for them, and re-layouts: 2.49 us -> 0.15 us  [per_device(): hold_low * low_f + pass_low * lower.astype(jnp.float32).reshape(blocks)]
    dot_general x2, matrix products: 1.02 us -> 3.34 us  [strips_out(): jnp.dot(pick, tile_out, preferred_element_type=jnp.float32)]
  transfers between devices with their start and end apart: 16 -> 16, of which waited for: 2 -> 3; matrix products, arithmetic and copies ran while one was open for 49% -> 30% of each run, Pallas kernels for 0% -> 16%
where the time goes in v4:
time: 137 us; the launch traced here: 136 us
  Pallas kernels  38.9 us (28%)
  local copies, waits for them, and re-layouts  27.8 us (20%)
  matrix products  20.2 us (15%)
  waiting for transfers between devices  20.2 us (15%)
  starting transfers between devices  15.4 us (11%)
  other arithmetic  13.2 us (10%)
    pallas_call x3, Pallas kernels, attend_project(): pl.pallas_call(attention_kernel, grid=(1, heads), in_specs=[pl.BlockSpec(...  38.9 us
    dot_general x4, matrix products, per_device(): jnp.dot(lax.dynamic_index_in_dim(moved_parts, index, 0, keepdims=False),...  15.5 us
    ppermute x1, waiting for transfers between devices, per_device(): upper = lax.ppermute(low, 'tm', [(i + 1, i) for i in range(count - 1)])  12.6 us
    ppermute x8, starting transfers between devices, strips_in(): lax.ppermute(sent, 'face', [(i, (i + shift) % n) for i in range(n)])  6.5 us
    select_n x2, other arithmetic, space_blend(): w_keep = jnp.where(dep == 0, keep[0], keep[1])  5.67 us
    ppermute x6, waiting for transfers between devices, fetch(): return lax.ppermute(x, 'face', [(src_of(i), i) for i in range(n)])  5.25 us
    squeeze x1, local copies, waits for them, and re-layouts, per_device(): queries, keys, values = (stacked[0], stacked[1], stacked[2])  4.93 us
    reshape x1, local copies, waits for them, and re-layouts, per_device(): stacked = qkv_all.reshape(tokens, 3, HEADS, HD).transpose(1, 2, 0, 3)  4.31 us
  transfers between devices with their start and end apart: 16, of which 3 were waited for; matrix products, arithmetic and copies ran while one was open for 30% of the time, Pallas kernels for 16%

profile of v4, /device:TPU:0, one launch (start us, length us, event | category | flops | bytes accessed | tf_op | source)
XLA Modules:
  0.0 136.2 jit_solution(5860157273666197134)
XLA Ops:
  0.0 2.9 %collective-permute-start.1 = (bf16[288,1728]{1,0:T(8,128)(2,1)}, bf16[288,1728]{1,0:T(8,128)(2,1)}, u32[]{:S(2)}, u32[]{:S(2)}) collective-permute-start(bf16[288,1728]{1,0:T(8,128)(2,1)} %param.22), channel_id=1, source_target_pairs={{2,0},{3,1},{0,2},{1,3},{6,4},{7,5},{4,6},{5,7},{10,8},{11,9},{8,1... | collective-permute-start | bytes 2985992 | tf_op jit(solution)/shard_map/ppermute | solution.py:86
  3.5 2.9 %copy.30 = bf16[1,1,896,1152]{2,3,1,0:T(8,128)(2,1)S(1)} copy(bf16[1,1,896,1152]{3,2,1,0:T(8,128)(2,1)} %param.20) | data formatting | bytes 4128768 | tf_op args[0]
  6.4 1.3 slice_bitcast_fusion.4
  8.2 2.2 %slice_bitcast_fusion.5 = (bf16[192,1152]{1,0:T(8,128)(2,1)}, bf16[192,1152]{1,0:T(8,128)(2,1)}) fusion(bf16[1,1,896,1152]{3,2,1,0:T(8,128)(2,1)} %param.20), kind=kLoop, calls=%fused_computation.56 | loop fusion | bytes 1769472 | tf_op jit(solution)/shard_map/slice | solution.py:225
  10.7 0.6 fusion.1
  11.3 0.6 add_reduce_fusion
  12.1 0.8 add_convert_fusion.1
  13.3 4.6 %fusion.17 = f32[896,1728]{0,1:T(8,128)} fusion(bf16[288,1728]{1,0:T(8,128)(2,1)S(1)} %copy-done.4, bf16[896,4,288]{0,2,1:T(8,128)(2,1)S(1)} %add_convert_fusion.1, s32[]{:T(128)S(6)} %select_n.98), kind=kOutput, calls=%fused_computation.43 | convolution fusion | flops 891813888 | bytes 7741444 | tf_op jit(solution)/shard_map/dot_general | solution.py:135
  18.8 0.6 fusion.47
  19.6 3.1 %broadcast_select_fusion.1 = (f32[512,1]{0,1:T(1,128)}, f32[512,1]{0,1:T(1,128)}) fusion(pred[512,1]{0,1:T(4,128)(4,1)S(1)} %copy-done.20, f32[]{:T(128)} %bitcast.10, f32[]{:T(128)} %bitcast.9, f32[]{:T(128)} %bitcast.23, f32[]{:T(128)} %bitcast.22), kind=kLoop, calls=%fused_computation.90 | loop fusion | flops 1024 | bytes 4624 | tf_op jit(solution)/shard_map/jit(_where)/select_n | solution.py:204
  23.0 0.7 eq.109
  23.7 0.6 eq.104
  24.8 0.7 eq.117
  25.5 0.7 eq.114
  26.2 0.7 mul.138
  27.0 0.7 mul.142
  27.6 1.1 pad_maximum_fusion.x_ref
  28.7 5.2 %collective-permute-done.4 = bf16[576,288]{0,1:T(8,128)(2,1)} collective-permute-done((bf16[576,288]{0,1:T(8,128)(2,1)}, bf16[576,288]{0,1:T(8,128)(2,1)}, u32[]{:S(2)}, u32[]{:S(2)}) %collective-permute-start.4) | collective-permute-done | bytes 331808 | tf_op jit(solution)/shard_map/ppermute | solution.py:86
  34.0 1.0 bitcast_dynamic-update-slice_fusion.2
  35.0 1.2 bitcast_dynamic-update-slice_fusion.1
  36.2 0.6 collective-permute-start.2
  36.8 1.9 %copy.32.w_ref = bf16[576,1152]{1,0:T(8,128)(2,1)} copy(bf16[576,1152]{0,1:T(8,128)(2,1)S(1)} %bitcast.68) | data formatting | bytes 2654208 | tf_op jit(solution)/shard_map/reshape | solution.py:152
  38.7 3.3 %fusion.13 = f32[896,1728]{0,1:T(8,128)S(1)} fusion(bf16[288,1728]{1,0:T(8,128)(2,1)} %collective-permute-done.1, bf16[896,4,288]{0,2,1:T(8,128)(2,1)S(1)} %copy-done.2, s32[]{:T(128)S(6)} %select_n.101), kind=kOutput, calls=%fused_computation.39 | convolution fusion | flops 891813888 | bytes 7704580 | tf_op jit(solution)/shard_map/dot_general | solution.py:135
  42.1 3.3 %fusion.15 = f32[896,1728]{0,1:T(8,128)S(1)} fusion(bf16[288,1728]{1,0:T(8,128)(2,1)} %collective-permute-done, bf16[896,4,288]{0,2,1:T(8,128)(2,1)S(1)} %copy-done.2, s32[]{:T(128)S(6)} %select_n.99), kind=kOutput, calls=%fused_computation.41 | convolution fusion | flops 891813888 | bytes 7704580 | tf_op jit(solution)/shard_map/dot_general | solution.py:135
  45.5 4.3 %add_convert_fusion = bf16[896,1728]{0,1:T(8,128)(2,1)S(1)} fusion(f32[896,1728]{0,1:T(8,128)S(1)} %fusion.13, f32[896,1728]{0,1:T(8,128)S(1)} %bitcast.65, f32[896,1728]{0,1:T(8,128)S(1)} %fusion.15, bf16[288,1728]{1,0:T(8,128)(2,1)} %collective-permute-done.2, bf16[896,4,288]{0,2,1:T(8,128)(2,1)} %copy-done.1, s32[]{:T(128)S(6)} %select_n.103), kind=kOutput, calls=%fused_computation | convolution fusion | flops 898007040 | bytes 23224324 | tf_op jit(solution)/shard_map/dot_general | solution.py:135
  49.8 4.3 %copy.31 = bf16[896,3,8,72]{3,0,2,1:T(8,128)(2,1)} copy(bf16[896,3,8,72]{0,3,2,1:T(8,128)(2,1)S(1)} %bitcast.67) | data formatting | bytes 6193152 | tf_op jit(solution)/shard_map/reshape | solution.py:154
  54.1 4.9 %slice_bitcast_fusion = (bf16[8,896,72]{2,1,0:T(8,128)(2,1)}, bf16[8,896,72]{2,1,0:T(8,128)(2,1)}, bf16[8,896,72]{2,1,0:T(8,128)(2,1)S(1)}) fusion(bf16[3,8,896,72]{3,2,1,0:T(8,128)(2,1)} %bitcast.66), kind=kLoop, calls=%fused_computation.19 | loop fusion | bytes 6193152 | tf_op jit(solution)/shard_map/squeeze | solution.py:155
  59.1 1.2 pad_maximum_fusion.1.q_ref
  60.3 17.5 %shard_map.190 = bf16[512,1152]{1,0:T(8,128)(2,1)} custom-call(bf16[8,512,72]{2,1,0:T(8,128)(2,1)} %pad_maximum_fusion.1.q_ref, bf16[8,896,72]{2,1,0:T(8,128)(2,1)} %get-tuple-element.26.k_ref, bf16[8,896,72]{2,1,0:T(8,128)(2,1)} %get-tuple-element.25.v_ref, bf16[576,1152]{1,0:T(8,128)(2,1)} %copy.32.w_ref, bf16[512,1152]{1,0:T(8,128)(2,1)} %pad_maximum_fusion.x_ref, ...), custom_call_target="tpu_custom_call" | custom-call | tf_op jit(solution)/shard_map/pallas_call | solution.py:63
  77.8 1.8 %convolution_convert_fusion = bf16[256,1152]{1,0:T(8,128)(2,1)S(1)} fusion(bf16[512,1152]{1,0:T(8,128)(2,1)} %shard_map.190, s32[256]{0:T(256)S(1)} %copy-done.11), kind=kOutput, calls=%fused_computation.14 | convolution fusion | flops 302415872 | bytes 1770496 | tf_op jit(solution)/shard_map/dot_general | solution.py:181
  79.7 1.4 %collective-permute-start.6 = (bf16[64,1152]{1,0:T(8,128)(2,1)S(1)}, bf16[64,1152]{1,0:T(8,128)(2,1)S(1)}, u32[]{:S(2)}, u32[]{:S(2)}) collective-permute-start(bf16[64,1152]{1,0:T(8,128)(2,1)S(1)} %get-tuple-element.38), channel_id=1, source_target_pairs={{0,3},{1,0},{2,1},{3,2},{4,7},{5,4},{6,5},{7,6},{8,11},{9,8},{10,9... | collective-permute-start | bytes 442376 | tf_op jit(solution)/shard_map/ppermute | solution.py:190
  81.1 0.8 collective-permute-start.8
  81.9 1.2 collective-permute-start.9
  83.2 0.9 fusion.42
  84.1 10.9 %shard_map.191 = bf16[192,1152]{1,0:T(8,128)(2,1)} custom-call(bf16[8,192,72]{2,1,0:T(8,128)(2,1)} %get-tuple-element.13.q_ref, bf16[8,896,72]{2,1,0:T(8,128)(2,1)} %get-tuple-element.26.k_ref, bf16[8,896,72]{2,1,0:T(8,128)(2,1)} %get-tuple-element.25.v_ref, bf16[576,1152]{1,0:T(8,128)(2,1)} %copy.32.w_ref, bf16[192,1152]{1,0:T(8,128)(2,1)} %get-tuple-element.29.x_ref, ...), custom_call_target="tpu_custom_call" | custom-call | tf_op jit(solution)/shard_map/pallas_call | solution.py:63
  95.1 0.7 fusion.6
  95.9 3.5 %collective-permute-start.10 = (bf16[256,1152]{1,0:T(8,128)(2,1)S(1)}, bf16[256,1152]{1,0:T(8,128)(2,1)S(1)}, u32[]{:S(2)}, u32[]{:S(2)}) collective-permute-start(bf16[256,1152]{1,0:T(8,128)(2,1)S(1)} %get-tuple-element.20), channel_id=1, source_target_pairs={{0,4},{4,8},{8,12},{1,5},{5,9},{9,13},{2,6},{6,10},{10,14},{3,7},{... | collective-permute-start | bytes 1769480 | tf_op jit(solution)/shard_map/ppermute | solution.py:220
  99.5 10.5 %shard_map.192 = bf16[192,1152]{1,0:T(8,128)(2,1)} custom-call(bf16[8,192,72]{2,1,0:T(8,128)(2,1)} %get-tuple-element.19.q_ref, bf16[8,896,72]{2,1,0:T(8,128)(2,1)} %get-tuple-element.26.k_ref, bf16[8,896,72]{2,1,0:T(8,128)(2,1)} %get-tuple-element.25.v_ref, bf16[576,1152]{1,0:T(8,128)(2,1)} %copy.32.w_ref, bf16[192,1152]{1,0:T(8,128)(2,1)} %get-tuple-element.28.x_ref, ...), custom_call_target="tpu_custom_call" | custom-call | tf_op jit(solution)/shard_map/pallas_call | solution.py:63
  110.1 1.5 %convolution_convert_fusion.1 = bf16[192,1152]{1,0:T(8,128)(2,1)S(1)} fusion(bf16[192,1152]{1,0:T(8,128)(2,1)} %shard_map.192, bf16[192,1152]{1,0:T(8,128)(2,1)S(1)} %copy-done.5, s32[192]{0:T(256)S(1)} %copy-done.23), kind=kOutput, calls=%fused_computation.15 | convolution fusion | flops 171933696 | bytes 1327872 | tf_op jit(solution)/shard_map/dot_general | solution.py:181
  111.7 1.0 collective-permute-start.11
  112.6 0.6 collective-permute-start.13
  113.2 1.5 %collective-permute-start.14 = (bf16[48,1152]{1,0:T(8,128)(2,1)S(1)}, bf16[48,1152]{1,0:T(8,128)(2,1)S(1)}, u32[]{:S(2)}, u32[]{:S(2)}) collective-permute-start(bf16[48,1152]{1,0:T(8,128)(2,1)S(1)} %get-tuple-element.43), channel_id=1, source_target_pairs={{0,2},{1,3},{2,0},{3,1},{4,6},{5,7},{6,4},{7,5},{8,10},{9,11},{10,... | collective-permute-start | bytes 331784 | tf_op jit(solution)/shard_map/ppermute | solution.py:190
  114.7 2.5 %select_reduce_fusion.5 = (f32[384]{0:T(512)S(1)}, f32[384]{0:T(512)S(1)}) fusion(pred[384,1]{0,1:T(4,128)(4,1)S(1)} %copy-done.21, f32[]{:T(128)} %bitcast.10, f32[]{:T(128)} %bitcast.9, f32[]{:T(128)} %bitcast.23, f32[]{:T(128)} %bitcast.22), kind=kLoop, calls=%fused_computation.87 | loop fusion | flops 768 | bytes 3472 | tf_op jit(solution)/shard_map/jit(_where)/select_n | solution.py:204
  117.2 1.3 collective-permute-start.15
  118.6 2.3 %collective-permute-done.14 = bf16[48,1152]{1,0:T(8,128)(2,1)S(1)} collective-permute-done((bf16[48,1152]{1,0:T(8,128)(2,1)S(1)}, bf16[48,1152]{1,0:T(8,128)(2,1)S(1)}, u32[]{:S(2)}, u32[]{:S(2)}) %collective-permute-start.14) | collective-permute-done | bytes 110624 | tf_op jit(solution)/shard_map/ppermute | solution.py:190
  120.9 0.6 fusion.7
  121.8 12.6 %collective-permute-done.15 = bf16[256,1152]{1,0:T(8,128)(2,1)S(1)} collective-permute-done((bf16[256,1152]{1,0:T(8,128)(2,1)S(1)}, bf16[256,1152]{1,0:T(8,128)(2,1)S(1)}, u32[]{:S(2)}, u32[]{:S(2)}) %collective-permute-start.15) | collective-permute-done | bytes 589856 | tf_op jit(solution)/shard_map/ppermute | solution.py:221
  134.8 1.5 %maximum_bitcast_fusion = bf16[1,1,896,1152]{3,2,1,0:T(8,128)(2,1)} fusion(bf16[256,1152]{1,0:T(8,128)(2,1)S(1)} %fusion.11, bf16[384,1152]{1,0:T(8,128)(2,1)S(1)} %fusion.7, bf16[256,1152]{1,0:T(8,128)(2,1)S(1)} %fusion.9), kind=kLoop, calls=%fused_computation.17 | loop fusion | flops 6193152 | bytes 4128768 | tf_op jit(solution)/shard_map/reshape | solution.py:251
  (122 shorter events, 5.0 us)
Async XLA Ops:
  0.0 7.8 %copy-start = (s32[4,4,4]{2,1,0:T(4,128)S(1)}, s32[4,4,4]{2,1,0:T(4,128)}, u32[]{:S(2)}) copy-start(s32[4,4,4]{2,1,0:T(4,128)} %param.24) | copy-start | bytes 772
  0.0 36.2 %collective-permute-start.1 = (bf16[288,1728]{1,0:T(8,128)(2,1)}, bf16[288,1728]{1,0:T(8,128)(2,1)}, u32[]{:S(2)}, u32[]{:S(2)}) collective-permute-start(bf16[288,1728]{1,0:T(8,128)(2,1)} %param.22), channel_id=1, source_target_pairs={{2,0},{3,1},{0,2},{1,3},{6,4},{7,5},{4,6},{5,7},{10,8},{11,9},{8,1... | collective-permute-start | bytes 2985992 | tf_op jit(solution)/shard_map/ppermute | solution.py:86
  2.9 39.1 %collective-permute-start = (bf16[288,1728]{1,0:T(8,128)(2,1)}, bf16[288,1728]{1,0:T(8,128)(2,1)}, u32[]{:S(2)}, u32[]{:S(2)}) collective-permute-start(bf16[288,1728]{1,0:T(8,128)(2,1)} %param.22), channel_id=1, source_target_pairs={{1,0},{0,1},{3,2},{2,3},{5,4},{4,5},{7,6},{6,7},{9,8},{8,9},{11,10... | collective-permute-start | bytes 2985992 | tf_op jit(solution)/shard_map/ppermute | solution.py:86
  2.9 31.0 %collective-permute-start.3 = (bf16[576,288]{0,1:T(8,128)(2,1)}, bf16[576,288]{0,1:T(8,128)(2,1)}, u32[]{:S(2)}, u32[]{:S(2)}) collective-permute-start(bf16[576,288]{0,1:T(8,128)(2,1)} %param.23), channel_id=1, source_target_pairs={{1,0},{0,1},{3,2},{2,3},{5,4},{4,5},{7,6},{6,7},{9,8},{8,9},{11,10... | collective-permute-start | bytes 995336 | tf_op jit(solution)/shard_map/ppermute | solution.py:86
  3.5 30.5 %collective-permute-start.4 = (bf16[576,288]{0,1:T(8,128)(2,1)}, bf16[576,288]{0,1:T(8,128)(2,1)}, u32[]{:S(2)}, u32[]{:S(2)}) collective-permute-start(bf16[576,288]{0,1:T(8,128)(2,1)} %param.23), channel_id=1, source_target_pairs={{2,0},{3,1},{0,2},{1,3},{6,4},{7,5},{4,6},{5,7},{10,8},{11,9},{8,1... | collective-permute-start | bytes 995336 | tf_op jit(solution)/shard_map/ppermute | solution.py:86
  10.3 1.0 copy-start.8
  12.1 1.2 copy-start.4
  13.3 4.6 %copy-start.1 = (bf16[896,4,288]{0,2,1:T(8,128)(2,1)}, bf16[896,4,288]{0,2,1:T(8,128)(2,1)S(1)}, u32[]{:S(2)}) copy-start(bf16[896,4,288]{0,2,1:T(8,128)(2,1)S(1)} %add_convert_fusion.1) | copy-start | bytes 6193156
  13.3 4.8 %copy-start.7 = (bf16[576,288]{0,1:T(8,128)(2,1)S(1)}, bf16[576,288]{0,1:T(8,128)(2,1)}, u32[]{:S(2)}) copy-start(bf16[576,288]{0,1:T(8,128)(2,1)} %param.23) | copy-start | bytes 995332
  17.9 0.7 copy-start.25
  17.9 0.8 copy-start.26
  17.9 0.9 copy-start.27
  17.9 1.6 %copy-start.15 = (s32[4,64]{1,0:T(4,128)S(1)}, s32[4,64]{1,0:T(4,128)}, u32[]{:S(2)}) copy-start(s32[4,64]{1,0:T(4,128)} %constant.94.clone) | copy-start | bytes 3076
  17.9 1.5 %copy-start.16 = (s32[4,64]{1,0:T(4,128)S(1)}, s32[4,64]{1,0:T(4,128)}, u32[]{:S(2)}) copy-start(s32[4,64]{1,0:T(4,128)} %constant.95.clone) | copy-start | bytes 3076
  17.9 1.6 %copy-start.13 = (s32[4,48]{1,0:T(4,128)S(1)}, s32[4,48]{1,0:T(4,128)}, u32[]{:S(2)}) copy-start(s32[4,48]{1,0:T(4,128)} %constant.100.clone) | copy-start | bytes 2308
  17.9 1.6 %copy-start.14 = (s32[4,48]{1,0:T(4,128)S(1)}, s32[4,48]{1,0:T(4,128)}, u32[]{:S(2)}) copy-start(s32[4,48]{1,0:T(4,128)} %constant.99.clone) | copy-start | bytes 2308
  17.9 1.7 %copy-start.20 = (pred[512,1]{0,1:T(4,128)(4,1)S(1)}, pred[512,1]{0,1:T(4,128)(4,1)}, u32[]{:S(2)}) copy-start(pred[512,1]{0,1:T(4,128)(4,1)} %constant.97.clone) | copy-start | bytes 1540
  17.9 4.9 %copy-start.19 = (s32[4,64]{1,0:T(4,128)S(1)}, s32[4,64]{1,0:T(4,128)}, u32[]{:S(2)}) copy-start(s32[4,64]{1,0:T(4,128)} %constant.107) | copy-start | bytes 3076
  17.9 5.0 %copy-start.12 = (s32[4,48]{1,0:T(4,128)S(1)}, s32[4,48]{1,0:T(4,128)}, u32[]{:S(2)}) copy-start(s32[4,48]{1,0:T(4,128)} %constant.109) | copy-start | bytes 2308
  34.0 2.8 %collective-permute-start.5 = (bf16[576,288]{0,1:T(8,128)(2,1)}, bf16[576,288]{0,1:T(8,128)(2,1)S(1)}, u32[]{:S(2)}, u32[]{:S(2)}) collective-permute-start(bf16[576,288]{0,1:T(8,128)(2,1)} %collective-permute-done.4), channel_id=1, source_target_pairs={{1,0},{0,1},{3,2},{2,3},{5,4},{4,5},{7,6},{6,7},{9,8},{8,9},{11,10... | collective-permute-start | bytes 995336 | tf_op jit(solution)/shard_map/ppermute | solution.py:86
  35.0 3.7 %copy-start.2 = (bf16[896,4,288]{0,2,1:T(8,128)(2,1)S(1)}, bf16[896,4,288]{0,2,1:T(8,128)(2,1)}, u32[]{:S(2)}) copy-start(bf16[896,4,288]{0,2,1:T(8,128)(2,1)} %copy-done.1) | copy-start | bytes 6193156
  36.2 9.2 %collective-permute-start.2 = (bf16[288,1728]{1,0:T(8,128)(2,1)}, bf16[288,1728]{1,0:T(8,128)(2,1)}, u32[]{:S(2)}, u32[]{:S(2)}) collective-permute-start(bf16[288,1728]{1,0:T(8,128)(2,1)} %collective-permute-done.1), channel_id=1, source_target_pairs={{1,0},{0,1},{3,2},{2,3},{5,4},{4,5},{7,6},{6,7},{9,8},{8,9},{11,10... | collective-permute-start | bytes 2985992 | tf_op jit(solution)/shard_map/ppermute | solution.py:86
  38.7 6.7 %slice-start = ((s8[6193152]{0:T(1024)(128)(4,1)}), s8[4194304]{0:T(1024)(128)(4,1)S(1)}, s32[]{:S(2)}) async-start(s8[6193152]{0:T(1024)(128)(4,1)} %bitcast.64), calls=%async_computation | async-start | bytes 8388608
  42.1 3.4 %slice-start.1 = ((s8[6193152]{0:T(1024)(128)(4,1)}), s8[1998848]{0:T(1024)(128)(4,1)S(1)}, s32[]{:S(2)}) async-start(s8[6193152]{0:T(1024)(128)(4,1)} %bitcast.64), calls=%async_computation.1 | async-start | bytes 3997696
  60.3 17.5 %copy-start.11 = (s32[256]{0:T(256)S(1)}, s32[256]{0:T(256)}, u32[]{:S(2)}) copy-start(s32[256]{0:T(256)} %eq.109) | copy-start | bytes 3076
  79.7 15.3 %collective-permute-start.6 = (bf16[64,1152]{1,0:T(8,128)(2,1)S(1)}, bf16[64,1152]{1,0:T(8,128)(2,1)S(1)}, u32[]{:S(2)}, u32[]{:S(2)}) collective-permute-start(bf16[64,1152]{1,0:T(8,128)(2,1)S(1)} %get-tuple-element.38), channel_id=1, source_target_pairs={{0,3},{1,0},{2,1},{3,2},{4,7},{5,4},{6,5},{7,6},{8,11},{9,8},{10,9... | collective-permute-start | bytes 442376 | tf_op jit(solution)/shard_map/ppermute | solution.py:190
  81.1 13.9 %collective-permute-start.7 = (bf16[64,1152]{1,0:T(8,128)(2,1)S(1)}, bf16[64,1152]{1,0:T(8,128)(2,1)S(1)}, u32[]{:S(2)}, u32[]{:S(2)}) collective-permute-start(bf16[64,1152]{1,0:T(8,128)(2,1)S(1)} %get-tuple-element.41), channel_id=1, source_target_pairs={{0,1},{1,2},{2,3},{3,0},{4,5},{5,6},{6,7},{7,4},{8,9},{9,10},{10,1... | collective-permute-start | bytes 442376 | tf_op jit(solution)/shard_map/ppermute | solution.py:190
  81.1 13.9 %collective-permute-start.8 = (bf16[64,1152]{1,0:T(8,128)(2,1)S(1)}, bf16[64,1152]{1,0:T(8,128)(2,1)S(1)}, u32[]{:S(2)}, u32[]{:S(2)}) collective-permute-start(bf16[64,1152]{1,0:T(8,128)(2,1)S(1)} %get-tuple-element.40), channel_id=1, source_target_pairs={{0,2},{1,3},{2,0},{3,1},{4,6},{5,7},{6,4},{7,5},{8,10},{9,11},{10,... | collective-permute-start | bytes 442376 | tf_op jit(solution)/shard_map/ppermute | solution.py:190
  81.9 13.1 %collective-permute-start.9 = (bf16[64,1152]{1,0:T(8,128)(2,1)S(1)}, bf16[64,1152]{1,0:T(8,128)(2,1)S(1)}, u32[]{:S(2)}, u32[]{:S(2)}) collective-permute-start(bf16[64,1152]{1,0:T(8,128)(2,1)S(1)} %get-tuple-element.39), channel_id=1, source_target_pairs={{0,2},{1,3},{2,0},{3,1},{4,6},{5,7},{6,4},{7,5},{8,10},{9,11},{10,... | collective-permute-start | bytes 442376 | tf_op jit(solution)/shard_map/ppermute | solution.py:190
  84.1 11.0 %copy-start.3 = (bf16[512,1152]{1,0:T(8,128)(2,1)S(1)}, bf16[512,1152]{1,0:T(8,128)(2,1)}, u32[]{:S(2)}) copy-start(bf16[512,1152]{1,0:T(8,128)(2,1)} %shard_map.190) | copy-start | bytes 3538948
  84.1 11.0 %copy-start.17 = (f32[512,1]{0,1:T(1,128)S(1)}, f32[512,1]{0,1:T(1,128)}, u32[]{:S(2)}) copy-start(f32[512,1]{0,1:T(1,128)} %get-tuple-element.47) | copy-start | bytes 6148
  84.1 11.0 %copy-start.18 = (f32[512,1]{0,1:T(1,128)S(1)}, f32[512,1]{0,1:T(1,128)}, u32[]{:S(2)}) copy-start(f32[512,1]{0,1:T(1,128)} %get-tuple-element.48) | copy-start | bytes 6148
  84.1 11.0 %copy-start.24 = (s32[256]{0:T(256)S(1)}, s32[256]{0:T(256)}, u32[]{:S(2)}) copy-start(s32[256]{0:T(256)} %eq.104) | copy-start | bytes 3076
  84.1 11.0 %copy-start.29 = (pred[512]{0:T(512)(128)(4,1)S(1)}, pred[512]{0:T(512)(128)(4,1)}, u32[]{:S(2)}) copy-start(pred[512]{0:T(512)(128)(4,1)} %constant.106) | copy-start | bytes 1540
  95.9 25.5 %collective-permute-start.10 = (bf16[256,1152]{1,0:T(8,128)(2,1)S(1)}, bf16[256,1152]{1,0:T(8,128)(2,1)S(1)}, u32[]{:S(2)}, u32[]{:S(2)}) collective-permute-start(bf16[256,1152]{1,0:T(8,128)(2,1)S(1)} %get-tuple-element.20), channel_id=1, source_target_pairs={{0,4},{4,8},{8,12},{1,5},{5,9},{9,13},{2,6},{6,10},{10,14},{3,7},{... | collective-permute-start | bytes 1769480 | tf_op jit(solution)/shard_map/ppermute | solution.py:220
  99.5 10.6 %copy-start.5 = (bf16[192,1152]{1,0:T(8,128)(2,1)S(1)}, bf16[192,1152]{1,0:T(8,128)(2,1)}, u32[]{:S(2)}) copy-start(bf16[192,1152]{1,0:T(8,128)(2,1)} %shard_map.191) | copy-start | bytes 1327108
  99.5 10.6 %copy-start.23 = (s32[192]{0:T(256)S(1)}, s32[192]{0:T(256)}, u32[]{:S(2)}) copy-start(s32[192]{0:T(256)} %eq.117) | copy-start | bytes 2308
  110.0 4.6 %copy-start.21 = (pred[384,1]{0,1:T(4,128)(4,1)S(1)}, pred[384,1]{0,1:T(4,128)(4,1)}, u32[]{:S(2)}) copy-start(pred[384,1]{0,1:T(4,128)(4,1)} %constant.102.clone) | copy-start | bytes 1156
  110.1 10.8 %copy-start.6 = (bf16[192,1152]{1,0:T(8,128)(2,1)S(1)}, bf16[192,1152]{1,0:T(8,128)(2,1)}, u32[]{:S(2)}) copy-start(bf16[192,1152]{1,0:T(8,128)(2,1)} %shard_map.192) | copy-start | bytes 1327108
  110.1 10.8 %copy-start.22 = (s32[192]{0:T(256)S(1)}, s32[192]{0:T(256)}, u32[]{:S(2)}) copy-start(s32[192]{0:T(256)} %eq.114) | copy-start | bytes 2308
  110.1 10.8 %copy-start.28 = (pred[384]{0:T(512)(128)(4,1)S(1)}, pred[384]{0:T(512)(128)(4,1)}, u32[]{:S(2)}) copy-start(pred[384]{0:T(512)(128)(4,1)} %constant.108) | copy-start | bytes 1156
  111.7 5.6 %collective-permute-start.11 = (bf16[48,1152]{1,0:T(8,128)(2,1)S(1)}, bf16[48,1152]{1,0:T(8,128)(2,1)S(1)}, u32[]{:S(2)}, u32[]{:S(2)}) collective-permute-start(bf16[48,1152]{1,0:T(8,128)(2,1)S(1)} %get-tuple-element.42), channel_id=1, source_target_pairs={{0,3},{1,0},{2,1},{3,2},{4,7},{5,4},{6,5},{7,6},{8,11},{9,8},{10,9... | collective-permute-start | bytes 331784 | tf_op jit(solution)/shard_map/ppermute | solution.py:190
  112.6 5.9 %collective-permute-start.12 = (bf16[48,1152]{1,0:T(8,128)(2,1)S(1)}, bf16[48,1152]{1,0:T(8,128)(2,1)S(1)}, u32[]{:S(2)}, u32[]{:S(2)}) collective-permute-start(bf16[48,1152]{1,0:T(8,128)(2,1)S(1)} %get-tuple-element.45), channel_id=1, source_target_pairs={{0,1},{1,2},{2,3},{3,0},{4,5},{5,6},{6,7},{7,4},{8,9},{9,10},{10,1... | collective-permute-start | bytes 331784 | tf_op jit(solution)/shard_map/ppermute | solution.py:190
  112.6 5.9 %collective-permute-start.13 = (bf16[48,1152]{1,0:T(8,128)(2,1)S(1)}, bf16[48,1152]{1,0:T(8,128)(2,1)S(1)}, u32[]{:S(2)}, u32[]{:S(2)}) collective-permute-start(bf16[48,1152]{1,0:T(8,128)(2,1)S(1)} %get-tuple-element.44), channel_id=1, source_target_pairs={{0,2},{1,3},{2,0},{3,1},{4,6},{5,7},{6,4},{7,5},{8,10},{9,11},{10,... | collective-permute-start | bytes 331784 | tf_op jit(solution)/shard_map/ppermute | solution.py:190
  113.2 7.7 %collective-permute-start.14 = (bf16[48,1152]{1,0:T(8,128)(2,1)S(1)}, bf16[48,1152]{1,0:T(8,128)(2,1)S(1)}, u32[]{:S(2)}, u32[]{:S(2)}) collective-permute-start(bf16[48,1152]{1,0:T(8,128)(2,1)S(1)} %get-tuple-element.43), channel_id=1, source_target_pairs={{0,2},{1,3},{2,0},{3,1},{4,6},{5,7},{6,4},{7,5},{8,10},{9,11},{10,... | collective-permute-start | bytes 331784 | tf_op jit(solution)/shard_map/ppermute | solution.py:190
  117.2 17.2 %collective-permute-start.15 = (bf16[256,1152]{1,0:T(8,128)(2,1)S(1)}, bf16[256,1152]{1,0:T(8,128)(2,1)S(1)}, u32[]{:S(2)}, u32[]{:S(2)}) collective-permute-start(bf16[256,1152]{1,0:T(8,128)(2,1)S(1)} %get-tuple-element.17), channel_id=1, source_target_pairs={{4,0},{8,4},{12,8},{5,1},{9,5},{13,9},{6,2},{10,6},{14,10},{7,3},{... | collective-permute-start | bytes 1769480 | tf_op jit(solution)/shard_map/ppermute | solution.py:221
  120.9 13.5 %copy-start.9 = (f32[256]{0:T(256)S(1)}, f32[256]{0:T(256)}, u32[]{:S(2)}) copy-start(f32[256]{0:T(256)} %mul.138) | copy-start | bytes 3076
  120.9 13.5 %copy-start.10 = (f32[256]{0:T(256)S(1)}, f32[256]{0:T(256)}, u32[]{:S(2)}) copy-start(f32[256]{0:T(256)} %mul.142) | copy-start | bytes 3076

commit v5 on v4

--- a/solution.py
+++ b/solution.py
@@ -37,9 +37,9 @@
     def _():
         acc_ref[...] = jnp.zeros_like(acc_ref)
 
-    scores = lax.dot_general(
-        q_ref[0], k_ref[0], (((1,), (1,)), ((), ())), preferred_element_type=jnp.float32
-    ) * (1.0 / math.sqrt(HD))
+    scores = jnp.dot(q_ref[0], k_ref[0], preferred_element_type=jnp.float32) * (
+        1.0 / math.sqrt(HD)
+    )
     row_max = jnp.max(scores, axis=-1, keepdims=True)
     weights = jnp.exp(scores - row_max)
     row_sum = jnp.sum(weights, axis=-1, keepdims=True)
@@ -57,7 +57,7 @@
 
 
 def attend_project(queries, keys, values, w_out_full, block_in, gate):
-    heads, tokens, size = keys.shape
+    heads, size, tokens = keys.shape
     chunk = queries.shape[1]
     width = block_in.shape[1]
     return pl.pallas_call(
@@ -65,7 +65,7 @@
         grid=(1, heads),
         in_specs=[
             pl.BlockSpec((1, chunk, size), lambda i, h: (h, i, 0)),
-            pl.BlockSpec((1, tokens, size), lambda i, h: (h, 0, 0)),
+            pl.BlockSpec((1, size, tokens), lambda i, h: (h, 0, 0)),
             pl.BlockSpec((1, tokens, size), lambda i, h: (h, 0, 0)),
             pl.BlockSpec((size, width), lambda i, h: (h, 0)),
             pl.BlockSpec((chunk, width), lambda i, h: (i, 0)),
@@ -151,8 +151,10 @@
         out_stack = lax.dynamic_update_index_in_dim(out_stack, piece, index, 0)
     w_out_full = out_stack.transpose(1, 0, 2).reshape(w_out.shape[0], n * w_out.shape[1])
 
-    stacked = qkv_all.reshape(tokens, 3, HEADS, HD).transpose(1, 2, 0, 3)
-    queries, keys, values = stacked[0], stacked[1], stacked[2]
+    split = qkv_all.reshape(tokens, 3, HEADS, HD)
+    queries = split[:, 0].transpose(1, 0, 2)
+    keys = split[:, 1].transpose(1, 2, 0)
+    values = split[:, 2].transpose(1, 0, 2)
     rim = OVT * S * S
     mid_a = rim + ((tokens - 2 * rim) // (2 * S * S)) * (S * S)
     gate = modulation[2]
@@ -223,6 +225,7 @@
         (queries[:, mid_a : tokens - rim], low, high)
     )
     tile_second = tile_part(second_queries, block_in[mid_a : tokens - rim])
+    lower, upper, tile_second = lax.optimization_barrier((lower, upper, tile_second))
     tile_mid = jnp.concatenate([tile_first, tile_second], axis=0)
     spaced_mid = space_blend(tile_mid, strips_in(strips_out(tile_mid)))
 

time: 137 us -> 130 us (0.949)
  waiting for transfers between devices: 20.2 us -> 16.3 us
    ppermute x1, waiting for transfers between devices: 12.6 us -> 1.36 us  [per_device(): upper = lax.ppermute(low, 'tm', [(i + 1, i) for i in range(count - 1)])]
    squeeze x1 -> x0, local copies, waits for them, and re-layouts: 4.93 us -> none  [per_device(): queries, keys, values = (stacked[0], stacked[1], stacked[2])]
    reshape x1 -> x0, local copies, waits for them, and re-layouts: 4.31 us -> none  [per_device(): stacked = qkv_all.reshape(tokens, 3, HEADS, HD).transpose(1, 2, 0, 3)]
    ppermute x8, waiting for transfers between devices: 2.36 us -> 6.01 us  [strips_in(): lax.ppermute(sent, 'face', [(i, (i + shift) % n) for i in range(n)])]
    ppermute x6, waiting for transfers between devices: 5.25 us -> 8.89 us  [fetch(): return lax.ppermute(x, 'face', [(src_of(i), i) for i in range(n)])]
    unnamed x65 -> x50, local copies, waits for them, and re-layouts: 3.83 us -> 7.04 us
    dynamic_update_slice x4, local copies, waits for them, and re-layouts: 2.31 us -> 5.24 us  [per_device(): out_stack = lax.dynamic_update_index_in_dim(out_stack, piece, index, 0)]
    slice x0 -> x1, local copies, waits for them, and re-layouts: none -> 1.57 us  [per_device(): values = split[:, 2].transpose(1, 0, 2)]
  transfers between devices with their start and end apart: 16 -> 16, of which waited for: 3 -> 6; matrix products, arithmetic and copies ran while one was open for 30% -> 31% of each run, Pallas kernels for 16% -> 16%
where the time goes in v5:
time: 130 us; the launch traced here: 129 us
  Pallas kernels  38.1 us (29%)
  local copies, waits for them, and re-layouts  26.6 us (20%)
  matrix products  18.9 us (15%)
  waiting for transfers between devices  16.3 us (13%)
  starting transfers between devices  15.2 us (12%)
  other arithmetic  13.8 us (11%)
    pallas_call x3, Pallas kernels, attend_project(): pl.pallas_call(attention_kernel, grid=(1, heads), in_specs=[pl.BlockSpec(...  38.1 us
    dot_general x4, matrix products, per_device(): jnp.dot(lax.dynamic_index_in_dim(moved_parts, index, 0, keepdims=False),...  15.4 us
    ppermute x6, waiting for transfers between devices, fetch(): return lax.ppermute(x, 'face', [(src_of(i), i) for i in range(n)])  8.89 us
    unnamed x50, local copies, waits for them, and re-layouts  7.04 us
    ppermute x8, starting transfers between devices, strips_in(): lax.ppermute(sent, 'face', [(i, (i + shift) % n) for i in range(n)])  6.36 us
    ppermute x8, waiting for transfers between devices, strips_in(): lax.ppermute(sent, 'face', [(i, (i + shift) % n) for i in range(n)])  6.01 us
    dynamic_update_slice x4, local copies, waits for them, and re-layouts, per_device(): out_stack = lax.dynamic_update_index_in_dim(out_stack, piece, index, 0)  5.24 us
    select_n x2, other arithmetic, space_blend(): w_keep = jnp.where(dep == 0, keep[0], keep[1])  5.23 us
  transfers between devices with their start and end apart: 16, of which 6 were waited for; matrix products, arithmetic and copies ran while one was open for 31% of the time, Pallas kernels for 16%

profile of v5, /device:TPU:0, one launch (start us, length us, event | category | flops | bytes accessed | tf_op | source)
XLA Modules:
  0.0 129.3 jit_solution(2952789971215076889)
XLA Ops:
  0.0 2.9 %collective-permute-start.1 = (bf16[288,1728]{1,0:T(8,128)(2,1)}, bf16[288,1728]{1,0:T(8,128)(2,1)}, u32[]{:S(2)}, u32[]{:S(2)}) collective-permute-start(bf16[288,1728]{1,0:T(8,128)(2,1)} %param.22), channel_id=1, source_target_pairs={{2,0},{3,1},{0,2},{1,3},{6,4},{7,5},{4,6},{5,7},{10,8},{11,9},{8,1... | collective-permute-start | bytes 2985992 | tf_op jit(solution)/shard_map/ppermute | solution.py:86
  3.5 2.9 %copy.34 = bf16[1,1,896,1152]{2,3,1,0:T(8,128)(2,1)S(1)} copy(bf16[1,1,896,1152]{3,2,1,0:T(8,128)(2,1)} %param.20) | data formatting | bytes 4128768 | tf_op args[0]
  6.4 1.3 %slice_bitcast_fusion.2 = (bf16[256,1152]{1,0:T(8,128)(2,1)S(1)}, bf16[256,1152]{1,0:T(8,128)(2,1)S(1)}) fusion(bf16[1,1,896,1152]{3,2,1,0:T(8,128)(2,1)} %param.20), kind=kLoop, calls=%fused_computation.32 | loop fusion | bytes 2359296 | tf_op jit(solution)/shard_map/slice | solution.py:212
  8.2 2.1 %slice_bitcast_fusion.3 = (bf16[192,1152]{1,0:T(8,128)(2,1)}, bf16[192,1152]{1,0:T(8,128)(2,1)}) fusion(bf16[1,1,896,1152]{3,2,1,0:T(8,128)(2,1)} %param.20), kind=kLoop, calls=%fused_computation.53 | loop fusion | bytes 1769472 | tf_op jit(solution)/shard_map/slice | solution.py:227
  10.7 0.6 fusion.1
  11.3 0.6 add_reduce_fusion
  12.0 0.8 add_convert_fusion.1
  13.3 4.6 %fusion.17 = f32[896,1728]{0,1:T(8,128)} fusion(bf16[288,1728]{1,0:T(8,128)(2,1)S(1)} %copy-done.5, bf16[896,4,288]{0,2,1:T(8,128)(2,1)S(1)} %add_convert_fusion.1, s32[]{:T(128)S(6)} %select_n.98), kind=kOutput, calls=%fused_computation.40 | convolution fusion | flops 891813888 | bytes 7741444 | tf_op jit(solution)/shard_map/dot_general | solution.py:135
  17.9 1.2 broadcast_in_dim.185
  19.2 0.8 bitcast_dynamic-update-slice_fusion.3
  20.1 0.7 fusion.47
  20.9 2.6 %broadcast_select_fusion.1 = (f32[512,1]{0,1:T(1,128)S(1)}, f32[512,1]{0,1:T(1,128)S(1)}) fusion(pred[512,1]{0,1:T(4,128)(4,1)S(1)} %copy-done.14, f32[]{:T(128)} %bitcast.10, f32[]{:T(128)} %bitcast.9, f32[]{:T(128)} %bitcast.26, f32[]{:T(128)} %bitcast.25), kind=kLoop, calls=%fused_computation.89 | loop fusion | flops 1024 | bytes 4624 | tf_op jit(solution)/shard_map/jit(_where)/select_n | solution.py:206
  24.0 1.1 pad_maximum_fusion.x_ref
  25.1 8.9 %collective-permute-done.4 = bf16[576,288]{0,1:T(8,128)(2,1)} collective-permute-done((bf16[576,288]{0,1:T(8,128)(2,1)}, bf16[576,288]{0,1:T(8,128)(2,1)}, u32[]{:S(2)}, u32[]{:S(2)}) %collective-permute-start.4) | collective-permute-done | bytes 331808 | tf_op jit(solution)/shard_map/ppermute | solution.py:86
  34.0 1.8 %bitcast_dynamic-update-slice_fusion.2 = bf16[4,576,288]{1,2,0:T(8,128)(2,1)} fusion(bf16[4,576,288]{1,2,0:T(8,128)(2,1)} %bitcast_dynamic-update-slice_fusion.3, s32[]{:T(128)S(6)} %select_n.99, bf16[576,288]{0,1:T(8,128)(2,1)} %collective-permute-done.3), kind=kLoop, calls=%fused_computation.58 | loop fusion | bytes 737284 | tf_op jit(solution)/shard_map/jit(dynamic_update_index_in_dim)/dynamic_update_slice | solution.py:151
  35.7 1.9 %bitcast_dynamic-update-slice_fusion.1 = bf16[4,576,288]{1,2,0:T(8,128)(2,1)} fusion(bf16[4,576,288]{1,2,0:T(8,128)(2,1)} %bitcast_dynamic-update-slice_fusion.2, s32[]{:T(128)S(6)} %select_n.101, bf16[576,288]{0,1:T(8,128)(2,1)} %collective-permute-done.4), kind=kLoop, calls=%fused_computation.57 | loop fusion | bytes 737284 | tf_op jit(solution)/shard_map/jit(dynamic_update_index_in_dim)/dynamic_update_slice | solution.py:151
  38.2 0.8 bitcast_dynamic-update-slice_fusion
  39.0 2.6 %copy.37.w_ref = bf16[576,1152]{1,0:T(8,128)(2,1)} copy(bf16[576,1152]{0,1:T(8,128)(2,1)} %bitcast.22) | data formatting | bytes 2654208 | tf_op jit(solution)/shard_map/reshape | solution.py:152
  41.6 3.4 %fusion.13 = f32[896,1728]{0,1:T(8,128)S(1)} fusion(bf16[288,1728]{1,0:T(8,128)(2,1)} %collective-permute-done.1, bf16[896,4,288]{0,2,1:T(8,128)(2,1)S(1)} %copy-done.2, s32[]{:T(128)S(6)} %select_n.101), kind=kOutput, calls=%fused_computation.36 | convolution fusion | flops 891813888 | bytes 7704580 | tf_op jit(solution)/shard_map/dot_general | solution.py:135
  45.0 3.3 %fusion.15 = f32[896,1728]{0,1:T(8,128)S(1)} fusion(bf16[288,1728]{1,0:T(8,128)(2,1)} %collective-permute-done, bf16[896,4,288]{0,2,1:T(8,128)(2,1)S(1)} %copy-done.2, s32[]{:T(128)S(6)} %select_n.99), kind=kOutput, calls=%fused_computation.38 | convolution fusion | flops 891813888 | bytes 7704580 | tf_op jit(solution)/shard_map/dot_general | solution.py:135
  48.3 4.1 %add_convert_fusion = bf16[896,1728]{0,1:T(8,128)(2,1)S(1)} fusion(f32[896,1728]{0,1:T(8,128)S(1)} %fusion.13, f32[896,1728]{0,1:T(8,128)S(1)} %bitcast.72, f32[896,1728]{0,1:T(8,128)S(1)} %fusion.15, bf16[288,1728]{1,0:T(8,128)(2,1)} %collective-permute-done.2, bf16[896,4,288]{0,2,1:T(8,128)(2,1)S(1)} %copy-done.2, s32[]{:T(128)S(6)} %select_n.103), kind=kOutput, calls=%fused_computation | convolution fusion | flops 898007040 | bytes 23187460 | tf_op jit(solution)/shard_map/dot_general | solution.py:135
  52.5 1.6 %fusion.41 = (bf16[896,1,8,72]{0,3,2,1:T(8,128)(2,1)S(1)}, bf16[896,1,8,72]{0,3,2,1:T(8,128)(2,1)}, bf16[8,72,896]{2,1,0:T(8,128)(2,1)}) fusion(bf16[896,3,8,72]{0,3,2,1:T(8,128)(2,1)S(1)} %bitcast.73), kind=kLoop, calls=%fused_computation.97 | loop fusion | bytes 6193152 | tf_op jit(solution)/shard_map/slice | solution.py:157
  54.1 1.9 %copy.40 = bf16[896,1,8,72]{3,0,2,1:T(8,128)(2,1)S(1)} copy(bf16[896,1,8,72]{0,3,2,1:T(8,128)(2,1)} %get-tuple-element.32) | data formatting | bytes 2064384
  56.0 0.9 fusion.43
  56.9 1.7 %copy.41 = bf16[896,1,8,72]{3,0,2,1:T(8,128)(2,1)} copy(bf16[896,1,8,72]{0,3,2,1:T(8,128)(2,1)S(1)} %get-tuple-element.31) | data formatting | bytes 2064384
  58.5 2.2 %pad_maximum_fusion.1.q_ref = bf16[8,512,72]{2,1,0:T(8,128)(2,1)} fusion(bf16[8,256,72]{2,1,0:T(8,128)(2,1)} %get-tuple-element.41, bf16[8,256,72]{2,1,0:T(8,128)(2,1)S(1)} %get-tuple-element.40), kind=kLoop, calls=%fused_computation.28 | loop fusion | flops 1179648 | bytes 1179648 | tf_op jit(solution)/shard_map/concatenate | solution.py:211
  60.7 17.2 %shard_map.190 = bf16[512,1152]{1,0:T(8,128)(2,1)} custom-call(bf16[8,512,72]{2,1,0:T(8,128)(2,1)} %pad_maximum_fusion.1.q_ref, bf16[8,72,896]{2,1,0:T(8,128)(2,1)} %get-tuple-element.33.k_ref, bf16[8,896,72]{2,1,0:T(8,128)(2,1)} %bitcast.68, bf16[576,1152]{1,0:T(8,128)(2,1)} %copy.37.w_ref, bf16[512,1152]{1,0:T(8,128)(2,1)} %pad_maximum_fusion.x_ref, ...), custom_call_target="tpu_custom_call" | custom-call | tf_op jit(solution)/shard_map/pallas_call | solution.py:63
  77.9 1.8 %convolution_convert_fusion = bf16[256,1152]{1,0:T(8,128)(2,1)S(1)} fusion(bf16[512,1152]{1,0:T(8,128)(2,1)} %shard_map.190, s32[256]{0:T(256)S(1)} %eq.109), kind=kOutput, calls=%fused_computation.14 | convolution fusion | flops 302415872 | bytes 1770496 | tf_op jit(solution)/shard_map/dot_general | solution.py:183
  79.8 1.4 %collective-permute-start.6 = (bf16[64,1152]{1,0:T(8,128)(2,1)S(1)}, bf16[64,1152]{1,0:T(8,128)(2,1)S(1)}, u32[]{:S(2)}, u32[]{:S(2)}) collective-permute-start(bf16[64,1152]{1,0:T(8,128)(2,1)S(1)} %get-tuple-element.44), channel_id=1, source_target_pairs={{0,3},{1,0},{2,1},{3,2},{4,7},{5,4},{6,5},{7,6},{8,11},{9,8},{10,9... | collective-permute-start | bytes 442376 | tf_op jit(solution)/shard_map/ppermute | solution.py:192
  81.2 0.9 collective-permute-start.8
  82.1 1.2 collective-permute-start.9
  83.3 1.0 fusion.42
  84.3 10.5 %shard_map.191 = bf16[192,1152]{1,0:T(8,128)(2,1)} custom-call(bf16[8,192,72]{2,1,0:T(8,128)(2,1)} %get-tuple-element.16.q_ref, bf16[8,72,896]{2,1,0:T(8,128)(2,1)} %get-tuple-element.33.k_ref, bf16[8,896,72]{2,1,0:T(8,128)(2,1)} %bitcast.69, bf16[576,1152]{1,0:T(8,128)(2,1)} %copy.37.w_ref, bf16[192,1152]{1,0:T(8,128)(2,1)} %get-tuple-element.35.x_ref, ...), custom_call_target="tpu_custom_call" | custom-call | tf_op jit(solution)/shard_map/pallas_call | solution.py:63
  94.9 0.7 fusion.6
  95.8 3.5 %collective-permute-start.10 = (bf16[256,1152]{1,0:T(8,128)(2,1)S(1)}, bf16[256,1152]{1,0:T(8,128)(2,1)S(1)}, u32[]{:S(2)}, u32[]{:S(2)}) collective-permute-start(bf16[256,1152]{1,0:T(8,128)(2,1)S(1)} %get-tuple-element.25), channel_id=1, source_target_pairs={{0,4},{4,8},{8,12},{1,5},{5,9},{9,13},{2,6},{6,10},{10,14},{3,7},{... | collective-permute-start | bytes 1769480 | tf_op jit(solution)/shard_map/ppermute | solution.py:222
  99.3 1.3 collective-permute-start.11
  101.8 2.6 %select_reduce_fusion.5 = (f32[384]{0:T(512)S(1)}, f32[384]{0:T(512)S(1)}) fusion(pred[384,1]{0,1:T(4,128)(4,1)S(1)} %copy-done.15, f32[]{:T(128)} %bitcast.10, f32[]{:T(128)} %bitcast.9, f32[]{:T(128)} %bitcast.26, f32[]{:T(128)} %bitcast.25), kind=kLoop, calls=%fused_computation.86 | loop fusion | flops 768 | bytes 3472 | tf_op jit(solution)/shard_map/jit(_where)/select_n | solution.py:206
  104.4 10.3 %shard_map.192 = bf16[192,1152]{1,0:T(8,128)(2,1)} custom-call(bf16[8,192,72]{2,1,0:T(8,128)(2,1)} %get-tuple-element.21.q_ref, bf16[8,72,896]{2,1,0:T(8,128)(2,1)} %get-tuple-element.33.k_ref, bf16[8,896,72]{2,1,0:T(8,128)(2,1)} %bitcast.70, bf16[576,1152]{1,0:T(8,128)(2,1)} %copy.37.w_ref, bf16[192,1152]{1,0:T(8,128)(2,1)} %get-tuple-element.34.x_ref, ...), custom_call_target="tpu_custom_call" | custom-call | tf_op jit(solution)/shard_map/pallas_call | solution.py:63
  114.8 1.4 %collective-permute-done.11 = bf16[256,1152]{1,0:T(8,128)(2,1)S(1)} collective-permute-done((bf16[256,1152]{1,0:T(8,128)(2,1)S(1)}, bf16[256,1152]{1,0:T(8,128)(2,1)S(1)}, u32[]{:S(2)}, u32[]{:S(2)}) %collective-permute-start.11) | collective-permute-done | bytes 589856 | tf_op jit(solution)/shard_map/ppermute | solution.py:223
  116.2 1.1 constant_dynamic-update-slice_fusion
  117.7 0.8 collective-permute-start.12
  118.6 1.2 collective-permute-start.14
  119.8 0.8 collective-permute-start.15
  121.8 2.1 %collective-permute-done.13 = bf16[48,1152]{1,0:T(8,128)(2,1)S(1)} collective-permute-done((bf16[48,1152]{1,0:T(8,128)(2,1)S(1)}, bf16[48,1152]{1,0:T(8,128)(2,1)S(1)}, u32[]{:S(2)}, u32[]{:S(2)}) %collective-permute-start.13) | collective-permute-done | bytes 110624 | tf_op jit(solution)/shard_map/ppermute | solution.py:192
  123.9 1.0 collective-permute-done.14
  124.9 2.4 %collective-permute-done.15 = bf16[48,1152]{1,0:T(8,128)(2,1)S(1)} collective-permute-done((bf16[48,1152]{1,0:T(8,128)(2,1)S(1)}, bf16[48,1152]{1,0:T(8,128)(2,1)S(1)}, u32[]{:S(2)}, u32[]{:S(2)}) %collective-permute-start.15) | collective-permute-done | bytes 110624 | tf_op jit(solution)/shard_map/ppermute | solution.py:192
  127.3 0.5 fusion.7
  127.9 1.5 %maximum_bitcast_fusion = bf16[1,1,896,1152]{3,2,1,0:T(8,128)(2,1)} fusion(bf16[256,1152]{1,0:T(8,128)(2,1)S(1)} %fusion.11, bf16[384,1152]{1,0:T(8,128)(2,1)S(1)} %fusion.7, bf16[256,1152]{1,0:T(8,128)(2,1)S(1)} %fusion.9), kind=kLoop, calls=%fused_computation.17 | loop fusion | flops 6193152 | bytes 4128768 | tf_op jit(solution)/shard_map/reshape | solution.py:254
  (107 shorter events, 6.3 us)
Async XLA Ops:
  0.0 7.8 %copy-start = (s32[4,4,4]{2,1,0:T(4,128)S(1)}, s32[4,4,4]{2,1,0:T(4,128)}, u32[]{:S(2)}) copy-start(s32[4,4,4]{2,1,0:T(4,128)} %param.24) | copy-start | bytes 772
  0.0 37.6 %collective-permute-start.1 = (bf16[288,1728]{1,0:T(8,128)(2,1)}, bf16[288,1728]{1,0:T(8,128)(2,1)}, u32[]{:S(2)}, u32[]{:S(2)}) collective-permute-start(bf16[288,1728]{1,0:T(8,128)(2,1)} %param.22), channel_id=1, source_target_pairs={{2,0},{3,1},{0,2},{1,3},{6,4},{7,5},{4,6},{5,7},{10,8},{11,9},{8,1... | collective-permute-start | bytes 2985992 | tf_op jit(solution)/shard_map/ppermute | solution.py:86
  2.9 42.0 %collective-permute-start = (bf16[288,1728]{1,0:T(8,128)(2,1)}, bf16[288,1728]{1,0:T(8,128)(2,1)}, u32[]{:S(2)}, u32[]{:S(2)}) collective-permute-start(bf16[288,1728]{1,0:T(8,128)(2,1)} %param.22), channel_id=1, source_target_pairs={{1,0},{0,1},{3,2},{2,3},{5,4},{4,5},{7,6},{6,7},{9,8},{8,9},{11,10... | collective-permute-start | bytes 2985992 | tf_op jit(solution)/shard_map/ppermute | solution.py:86
  2.9 31.0 %collective-permute-start.3 = (bf16[576,288]{0,1:T(8,128)(2,1)}, bf16[576,288]{0,1:T(8,128)(2,1)}, u32[]{:S(2)}, u32[]{:S(2)}) collective-permute-start(bf16[576,288]{0,1:T(8,128)(2,1)} %param.23), channel_id=1, source_target_pairs={{1,0},{0,1},{3,2},{2,3},{5,4},{4,5},{7,6},{6,7},{9,8},{8,9},{11,10... | collective-permute-start | bytes 995336 | tf_op jit(solution)/shard_map/ppermute | solution.py:86
  3.5 30.5 %collective-permute-start.4 = (bf16[576,288]{0,1:T(8,128)(2,1)}, bf16[576,288]{0,1:T(8,128)(2,1)}, u32[]{:S(2)}, u32[]{:S(2)}) collective-permute-start(bf16[576,288]{0,1:T(8,128)(2,1)} %param.23), channel_id=1, source_target_pairs={{2,0},{3,1},{0,2},{1,3},{6,4},{7,5},{4,6},{5,7},{10,8},{11,9},{8,1... | collective-permute-start | bytes 995336 | tf_op jit(solution)/shard_map/ppermute | solution.py:86
  10.3 1.0 copy-start.7
  12.0 1.2 copy-start.5
  13.3 4.6 %copy-start.1 = (bf16[896,4,288]{0,2,1:T(8,128)(2,1)}, bf16[896,4,288]{0,2,1:T(8,128)(2,1)S(1)}, u32[]{:S(2)}) copy-start(bf16[896,4,288]{0,2,1:T(8,128)(2,1)S(1)} %add_convert_fusion.1) | copy-start | bytes 6193156
  13.3 5.9 %copy-start.6 = (bf16[576,288]{0,1:T(8,128)(2,1)S(1)}, bf16[576,288]{0,1:T(8,128)(2,1)}, u32[]{:S(2)}) copy-start(bf16[576,288]{0,1:T(8,128)(2,1)} %param.23) | copy-start | bytes 995332
  17.8 2.1 %copy-start.16 = (s32[2]{0:T(128)S(1)}, s32[2]{0:T(128)}, u32[]{:S(2)}) copy-start(s32[2]{0:T(128)} %param.25) | copy-start | bytes 28
  17.8 2.9 %copy-start.11 = (s32[4,64]{1,0:T(4,128)S(1)}, s32[4,64]{1,0:T(4,128)}, u32[]{:S(2)}) copy-start(s32[4,64]{1,0:T(4,128)} %constant.94.clone) | copy-start | bytes 3076
  17.8 2.9 %copy-start.12 = (s32[4,64]{1,0:T(4,128)S(1)}, s32[4,64]{1,0:T(4,128)}, u32[]{:S(2)}) copy-start(s32[4,64]{1,0:T(4,128)} %constant.95.clone) | copy-start | bytes 3076
  17.8 3.0 %copy-start.9 = (s32[4,48]{1,0:T(4,128)S(1)}, s32[4,48]{1,0:T(4,128)}, u32[]{:S(2)}) copy-start(s32[4,48]{1,0:T(4,128)} %constant.100.clone) | copy-start | bytes 2308
  17.9 3.0 %copy-start.10 = (s32[4,48]{1,0:T(4,128)S(1)}, s32[4,48]{1,0:T(4,128)}, u32[]{:S(2)}) copy-start(s32[4,48]{1,0:T(4,128)} %constant.99.clone) | copy-start | bytes 2308
  17.9 3.0 %copy-start.14 = (pred[512,1]{0,1:T(4,128)(4,1)S(1)}, pred[512,1]{0,1:T(4,128)(4,1)}, u32[]{:S(2)}) copy-start(pred[512,1]{0,1:T(4,128)(4,1)} %constant.97.clone) | copy-start | bytes 1540
  17.9 5.6 %copy-start.18 = (s32[4]{0:T(128)S(1)}, s32[4]{0:T(128)}, u32[]{:S(2)}) copy-start(s32[4]{0:T(128)} %constant.93.clone) | copy-start | bytes 52
  17.9 5.7 %copy-start.13 = (s32[4,64]{1,0:T(4,128)S(1)}, s32[4,64]{1,0:T(4,128)}, u32[]{:S(2)}) copy-start(s32[4,64]{1,0:T(4,128)} %constant.107) | copy-start | bytes 3076
  17.9 6.0 %copy-start.17 = (s32[4]{0:T(128)S(1)}, s32[4]{0:T(128)}, u32[]{:S(2)}) copy-start(s32[4]{0:T(128)} %param.26) | copy-start | bytes 52
  34.0 4.2 %collective-permute-start.5 = (bf16[576,288]{0,1:T(8,128)(2,1)}, bf16[576,288]{0,1:T(8,128)(2,1)S(1)}, u32[]{:S(2)}, u32[]{:S(2)}) collective-permute-start(bf16[576,288]{0,1:T(8,128)(2,1)} %collective-permute-done.4), channel_id=1, source_target_pairs={{1,0},{0,1},{3,2},{2,3},{5,4},{4,5},{7,6},{6,7},{9,8},{8,9},{11,10... | collective-permute-start | bytes 995336 | tf_op jit(solution)/shard_map/ppermute | solution.py:86
  35.7 5.8 %copy-start.2 = (bf16[896,4,288]{0,2,1:T(8,128)(2,1)S(1)}, bf16[896,4,288]{0,2,1:T(8,128)(2,1)}, u32[]{:S(2)}) copy-start(bf16[896,4,288]{0,2,1:T(8,128)(2,1)} %copy-done.1) | copy-start | bytes 6193156
  37.6 10.7 %collective-permute-start.2 = (bf16[288,1728]{1,0:T(8,128)(2,1)}, bf16[288,1728]{1,0:T(8,128)(2,1)}, u32[]{:S(2)}, u32[]{:S(2)}) collective-permute-start(bf16[288,1728]{1,0:T(8,128)(2,1)} %collective-permute-done.1), channel_id=1, source_target_pairs={{1,0},{0,1},{3,2},{2,3},{5,4},{4,5},{7,6},{6,7},{9,8},{8,9},{11,10... | collective-permute-start | bytes 2985992 | tf_op jit(solution)/shard_map/ppermute | solution.py:86
  41.6 6.7 %slice-start = ((s8[6193152]{0:T(1024)(128)(4,1)}), s8[4194304]{0:T(1024)(128)(4,1)S(1)}, s32[]{:S(2)}) async-start(s8[6193152]{0:T(1024)(128)(4,1)} %bitcast.71), calls=%async_computation | async-start | bytes 8388608
  44.9 3.4 %slice-start.1 = ((s8[6193152]{0:T(1024)(128)(4,1)}), s8[1998848]{0:T(1024)(128)(4,1)S(1)}, s32[]{:S(2)}) async-start(s8[6193152]{0:T(1024)(128)(4,1)} %bitcast.71), calls=%async_computation.1 | async-start | bytes 3997696
  79.8 15.0 %collective-permute-start.6 = (bf16[64,1152]{1,0:T(8,128)(2,1)S(1)}, bf16[64,1152]{1,0:T(8,128)(2,1)S(1)}, u32[]{:S(2)}, u32[]{:S(2)}) collective-permute-start(bf16[64,1152]{1,0:T(8,128)(2,1)S(1)} %get-tuple-element.44), channel_id=1, source_target_pairs={{0,3},{1,0},{2,1},{3,2},{4,7},{5,4},{6,5},{7,6},{8,11},{9,8},{10,9... | collective-permute-start | bytes 442376 | tf_op jit(solution)/shard_map/ppermute | solution.py:192
  81.2 13.6 %collective-permute-start.7 = (bf16[64,1152]{1,0:T(8,128)(2,1)S(1)}, bf16[64,1152]{1,0:T(8,128)(2,1)S(1)}, u32[]{:S(2)}, u32[]{:S(2)}) collective-permute-start(bf16[64,1152]{1,0:T(8,128)(2,1)S(1)} %get-tuple-element.47), channel_id=1, source_target_pairs={{0,1},{1,2},{2,3},{3,0},{4,5},{5,6},{6,7},{7,4},{8,9},{9,10},{10,1... | collective-permute-start | bytes 442376 | tf_op jit(solution)/shard_map/ppermute | solution.py:192
  81.2 13.6 %collective-permute-start.8 = (bf16[64,1152]{1,0:T(8,128)(2,1)S(1)}, bf16[64,1152]{1,0:T(8,128)(2,1)S(1)}, u32[]{:S(2)}, u32[]{:S(2)}) collective-permute-start(bf16[64,1152]{1,0:T(8,128)(2,1)S(1)} %get-tuple-element.46), channel_id=1, source_target_pairs={{0,2},{1,3},{2,0},{3,1},{4,6},{5,7},{6,4},{7,5},{8,10},{9,11},{10,... | collective-permute-start | bytes 442376 | tf_op jit(solution)/shard_map/ppermute | solution.py:192
  82.1 12.7 %collective-permute-start.9 = (bf16[64,1152]{1,0:T(8,128)(2,1)S(1)}, bf16[64,1152]{1,0:T(8,128)(2,1)S(1)}, u32[]{:S(2)}, u32[]{:S(2)}) collective-permute-start(bf16[64,1152]{1,0:T(8,128)(2,1)S(1)} %get-tuple-element.45), channel_id=1, source_target_pairs={{0,2},{1,3},{2,0},{3,1},{4,6},{5,7},{6,4},{7,5},{8,10},{9,11},{10,... | collective-permute-start | bytes 442376 | tf_op jit(solution)/shard_map/ppermute | solution.py:192
  84.3 10.6 %copy-start.3 = (bf16[512,1152]{1,0:T(8,128)(2,1)S(1)}, bf16[512,1152]{1,0:T(8,128)(2,1)}, u32[]{:S(2)}) copy-start(bf16[512,1152]{1,0:T(8,128)(2,1)} %shard_map.190) | copy-start | bytes 3538948
  84.3 10.6 %copy-start.20 = (pred[512]{0:T(512)(128)(4,1)S(1)}, pred[512]{0:T(512)(128)(4,1)}, u32[]{:S(2)}) copy-start(pred[512]{0:T(512)(128)(4,1)} %constant.106) | copy-start | bytes 1540
  95.6 5.7 %copy-start.8 = (s32[4,48]{1,0:T(4,128)S(1)}, s32[4,48]{1,0:T(4,128)}, u32[]{:S(2)}) copy-start(s32[4,48]{1,0:T(4,128)} %constant.109) | copy-start | bytes 2308
  95.6 6.2 %copy-start.15 = (pred[384,1]{0,1:T(4,128)(4,1)S(1)}, pred[384,1]{0,1:T(4,128)(4,1)}, u32[]{:S(2)}) copy-start(pred[384,1]{0,1:T(4,128)(4,1)} %constant.102.clone) | copy-start | bytes 1156
  95.8 19.0 %collective-permute-start.10 = (bf16[256,1152]{1,0:T(8,128)(2,1)S(1)}, bf16[256,1152]{1,0:T(8,128)(2,1)S(1)}, u32[]{:S(2)}, u32[]{:S(2)}) collective-permute-start(bf16[256,1152]{1,0:T(8,128)(2,1)S(1)} %get-tuple-element.25), channel_id=1, source_target_pairs={{0,4},{4,8},{8,12},{1,5},{5,9},{9,13},{2,6},{6,10},{10,14},{3,7},{... | collective-permute-start | bytes 1769480 | tf_op jit(solution)/shard_map/ppermute | solution.py:222
  99.3 16.9 %collective-permute-start.11 = (bf16[256,1152]{1,0:T(8,128)(2,1)S(1)}, bf16[256,1152]{1,0:T(8,128)(2,1)S(1)}, u32[]{:S(2)}, u32[]{:S(2)}) collective-permute-start(bf16[256,1152]{1,0:T(8,128)(2,1)S(1)} %get-tuple-element.20), channel_id=1, source_target_pairs={{4,0},{8,4},{12,8},{5,1},{9,5},{13,9},{6,2},{10,6},{14,10},{7,3},{... | collective-permute-start | bytes 1769480 | tf_op jit(solution)/shard_map/ppermute | solution.py:223
  104.4 10.3 %copy-start.4 = (bf16[192,1152]{1,0:T(8,128)(2,1)S(1)}, bf16[192,1152]{1,0:T(8,128)(2,1)}, u32[]{:S(2)}) copy-start(bf16[192,1152]{1,0:T(8,128)(2,1)} %shard_map.191) | copy-start | bytes 1327108
  117.7 9.6 %copy-start.19 = (pred[384]{0:T(512)(128)(4,1)S(1)}, pred[384]{0:T(512)(128)(4,1)}, u32[]{:S(2)}) copy-start(pred[384]{0:T(512)(128)(4,1)} %constant.108) | copy-start | bytes 1156
  117.7 4.0 %collective-permute-start.12 = (bf16[48,1152]{1,0:T(8,128)(2,1)S(1)}, bf16[48,1152]{1,0:T(8,128)(2,1)S(1)}, u32[]{:S(2)}, u32[]{:S(2)}) collective-permute-start(bf16[48,1152]{1,0:T(8,128)(2,1)S(1)} %get-tuple-element.48), channel_id=1, source_target_pairs={{0,3},{1,0},{2,1},{3,2},{4,7},{5,4},{6,5},{7,6},{8,11},{9,8},{10,9... | collective-permute-start | bytes 331784 | tf_op jit(solution)/shard_map/ppermute | solution.py:192
  118.6 5.3 %collective-permute-start.13 = (bf16[48,1152]{1,0:T(8,128)(2,1)S(1)}, bf16[48,1152]{1,0:T(8,128)(2,1)S(1)}, u32[]{:S(2)}, u32[]{:S(2)}) collective-permute-start(bf16[48,1152]{1,0:T(8,128)(2,1)S(1)} %get-tuple-element.51), channel_id=1, source_target_pairs={{0,1},{1,2},{2,3},{3,0},{4,5},{5,6},{6,7},{7,4},{8,9},{9,10},{10,1... | collective-permute-start | bytes 331784 | tf_op jit(solution)/shard_map/ppermute | solution.py:192
  118.6 6.4 %collective-permute-start.14 = (bf16[48,1152]{1,0:T(8,128)(2,1)S(1)}, bf16[48,1152]{1,0:T(8,128)(2,1)S(1)}, u32[]{:S(2)}, u32[]{:S(2)}) collective-permute-start(bf16[48,1152]{1,0:T(8,128)(2,1)S(1)} %get-tuple-element.50), channel_id=1, source_target_pairs={{0,2},{1,3},{2,0},{3,1},{4,6},{5,7},{6,4},{7,5},{8,10},{9,11},{10,... | collective-permute-start | bytes 331784 | tf_op jit(solution)/shard_map/ppermute | solution.py:192
  119.8 7.5 %collective-permute-start.15 = (bf16[48,1152]{1,0:T(8,128)(2,1)S(1)}, bf16[48,1152]{1,0:T(8,128)(2,1)S(1)}, u32[]{:S(2)}, u32[]{:S(2)}) collective-permute-start(bf16[48,1152]{1,0:T(8,128)(2,1)S(1)} %get-tuple-element.49), channel_id=1, source_target_pairs={{0,2},{1,3},{2,0},{3,1},{4,6},{5,7},{6,4},{7,5},{8,10},{9,11},{10,... | collective-permute-start | bytes 331784 | tf_op jit(solution)/shard_map/ppermute | solution.py:192

commit v6 on v5

--- a/solution.py
+++ b/solution.py
@@ -128,10 +128,12 @@
     n = lax.axis_size("face")
     rows = w_qkv.shape[0]
     moved = modulate(block_in, modulation)
+    qkv_pieces = face_pieces(w_qkv)
+    w_out_late, _ = lax.optimization_barrier((w_out, [piece for piece, _ in qkv_pieces]))
     if n <= 4:
         moved_parts = moved.reshape(tokens, n, rows).transpose(1, 0, 2)
         qkv_sums = None
-        for piece, index in face_pieces(w_qkv):
+        for piece, index in qkv_pieces:
             part = jnp.dot(
                 lax.dynamic_index_in_dim(moved_parts, index, 0, keepdims=False),
                 piece,
@@ -140,14 +142,14 @@
             qkv_sums = part if qkv_sums is None else qkv_sums + part
     else:
         qkv_stack = jnp.zeros((n,) + w_qkv.shape, w_qkv.dtype)
-        for piece, index in face_pieces(w_qkv):
+        for piece, index in qkv_pieces:
             qkv_stack = lax.dynamic_update_index_in_dim(qkv_stack, piece, index, 0)
         w_qkv_full = qkv_stack.reshape(n * rows, w_qkv.shape[1])
         qkv_sums = jnp.dot(moved, w_qkv_full, preferred_element_type=jnp.float32)
     qkv_all = qkv_sums.astype(jnp.bfloat16)
 
     out_stack = jnp.zeros((n,) + w_out.shape, w_out.dtype)
-    for piece, index in face_pieces(w_out):
+    for piece, index in face_pieces(w_out_late):
         out_stack = lax.dynamic_update_index_in_dim(out_stack, piece, index, 0)
     w_out_full = out_stack.transpose(1, 0, 2).reshape(w_out.shape[0], n * w_out.shape[1])
 

time: 130 us -> 125 us (0.962)
  local copies, waits for them, and re-layouts: 26.6 us -> 22.2 us
  matrix products: 18.9 us -> 15.9 us
  waiting for transfers between devices: 16.3 us -> 18.6 us
    dot_general x4, matrix products: 15.4 us -> 12.3 us  [per_device(): jnp.dot(lax.dynamic_index_in_dim(moved_parts, index, 0, keepdims=False),...]
    dynamic_update_slice x4, local copies, waits for them, and re-layouts: 5.24 us -> 3.17 us  [per_device(): out_stack = lax.dynamic_update_index_in_dim(out_stack, piece, index, 0)]
    unnamed x50 -> x42, local copies, waits for them, and re-layouts: 7.04 us -> 6.6 us
  transfers between devices with their start and end apart: 16 -> 16, of which waited for: 6 -> 5; matrix products, arithmetic and copies ran while one was open for 31% -> 35% of each run, Pallas kernels for 16% -> 17%
where the time goes in v6:
time: 125 us; the launch traced here: 124 us
  Pallas kernels  37.8 us (30%)
  local copies, waits for them, and re-layouts  22.2 us (18%)
  waiting for transfers between devices  18.6 us (15%)
  matrix products  15.9 us (13%)
  starting transfers between devices  15.5 us (12%)
  other arithmetic  13.6 us (11%)
    pallas_call x3, Pallas kernels, attend_project(): pl.pallas_call(attention_kernel, grid=(1, heads), in_specs=[pl.BlockSpec(...  37.8 us
    dot_general x4, matrix products, per_device(): jnp.dot(lax.dynamic_index_in_dim(moved_parts, index, 0, keepdims=False),...  12.3 us
    ppermute x6, waiting for transfers between devices, fetch(): return lax.ppermute(x, 'face', [(src_of(i), i) for i in range(n)])  9.17 us
    ppermute x8, waiting for transfers between devices, strips_in(): lax.ppermute(sent, 'face', [(i, (i + shift) % n) for i in range(n)])  6.94 us
    unnamed x42, local copies, waits for them, and re-layouts  6.6 us
    ppermute x6, starting transfers between devices, fetch(): return lax.ppermute(x, 'face', [(src_of(i), i) for i in range(n)])  5.33 us
    ppermute x8, starting transfers between devices, strips_in(): lax.ppermute(sent, 'face', [(i, (i + shift) % n) for i in range(n)])  5.21 us
    select_n x2, other arithmetic, space_blend(): w_keep = jnp.where(dep == 0, keep[0], keep[1])  5.03 us
  transfers between devices with their start and end apart: 16, of which 5 were waited for; matrix products, arithmetic and copies ran while one was open for 35% of the time, Pallas kernels for 17%

profile of v6, /device:TPU:0, one launch (start us, length us, event | category | flops | bytes accessed | tf_op | source)
XLA Modules:
  0.0 124.0 jit_solution(15384844852071948315)
XLA Ops:
  0.0 2.9 %collective-permute-start.1 = (bf16[288,1728]{1,0:T(8,128)(2,1)}, bf16[288,1728]{1,0:T(8,128)(2,1)}, u32[]{:S(2)}, u32[]{:S(2)}) collective-permute-start(bf16[288,1728]{1,0:T(8,128)(2,1)} %param.22), channel_id=1, source_target_pairs={{2,0},{3,1},{0,2},{1,3},{6,4},{7,5},{4,6},{5,7},{10,8},{11,9},{8,1... | collective-permute-start | bytes 2985992 | tf_op jit(solution)/shard_map/ppermute | solution.py:86
  2.9 2.9 %copy.34 = bf16[1,1,896,1152]{2,3,1,0:T(8,128)(2,1)S(1)} copy(bf16[1,1,896,1152]{3,2,1,0:T(8,128)(2,1)} %param.20) | data formatting | bytes 4128768 | tf_op args[0]
  5.8 1.3 %slice_bitcast_fusion.2 = (bf16[256,1152]{1,0:T(8,128)(2,1)S(1)}, bf16[256,1152]{1,0:T(8,128)(2,1)S(1)}) fusion(bf16[1,1,896,1152]{3,2,1,0:T(8,128)(2,1)} %param.20), kind=kLoop, calls=%fused_computation.32 | loop fusion | bytes 2359296 | tf_op jit(solution)/shard_map/slice | solution.py:214
  8.0 0.6 fusion.1
  8.7 0.6 add_reduce_fusion
  10.1 1.1 pad_maximum_fusion.x_ref
  11.3 0.8 add_convert_fusion.1
  12.0 0.7 fusion.47
  12.8 2.1 %slice_bitcast_fusion.3 = (bf16[192,1152]{1,0:T(8,128)(2,1)}, bf16[192,1152]{1,0:T(8,128)(2,1)}) fusion(bf16[1,1,896,1152]{3,2,1,0:T(8,128)(2,1)} %param.20), kind=kLoop, calls=%fused_computation.53 | loop fusion | bytes 1769472 | tf_op jit(solution)/shard_map/slice | solution.py:229
  14.9 2.0 %fusion.17 = f32[896,1728]{0,1:T(8,128)S(1)} fusion(bf16[288,1728]{1,0:T(8,128)(2,1)S(1)} %copy-done.4, bf16[896,4,288]{0,2,1:T(8,128)(2,1)S(1)} %add_convert_fusion.1, s32[]{:T(128)S(6)} %select_n.98), kind=kOutput, calls=%fused_computation.40 | convolution fusion | flops 891813888 | bytes 7741444 | tf_op jit(solution)/shard_map/dot_general | solution.py:137
  16.9 9.2 %collective-permute-done.1 = bf16[288,1728]{1,0:T(8,128)(2,1)} collective-permute-done((bf16[288,1728]{1,0:T(8,128)(2,1)}, bf16[288,1728]{1,0:T(8,128)(2,1)}, u32[]{:S(2)}, u32[]{:S(2)}) %collective-permute-start.1) | collective-permute-done | bytes 995360 | tf_op jit(solution)/shard_map/ppermute | solution.py:86
  26.1 2.5 %broadcast_select_fusion.1 = (f32[512,1]{0,1:T(1,128)S(1)}, f32[512,1]{0,1:T(1,128)S(1)}) fusion(pred[512,1]{0,1:T(4,128)(4,1)S(1)} %copy-done.11, f32[]{:T(128)} %bitcast.10, f32[]{:T(128)} %bitcast.9, f32[]{:T(128)} %bitcast.26, f32[]{:T(128)} %bitcast.25), kind=kLoop, calls=%fused_computation.89 | loop fusion | flops 1024 | bytes 4624 | tf_op jit(solution)/shard_map/jit(_where)/select_n | solution.py:208
  28.6 3.2 %fusion.13 = f32[896,1728]{0,1:T(8,128)S(1)} fusion(bf16[288,1728]{1,0:T(8,128)(2,1)} %collective-permute-done.1, bf16[896,4,288]{0,2,1:T(8,128)(2,1)S(1)} %add_convert_fusion.1, s32[]{:T(128)S(6)} %select_n.101), kind=kOutput, calls=%fused_computation.36 | convolution fusion | flops 891813888 | bytes 7704580 | tf_op jit(solution)/shard_map/dot_general | solution.py:137
  31.8 3.2 %fusion.15 = f32[896,1728]{0,1:T(8,128)S(1)} fusion(bf16[288,1728]{1,0:T(8,128)(2,1)} %collective-permute-done, bf16[896,4,288]{0,2,1:T(8,128)(2,1)S(1)} %add_convert_fusion.1, s32[]{:T(128)S(6)} %select_n.99), kind=kOutput, calls=%fused_computation.38 | convolution fusion | flops 891813888 | bytes 7704580 | tf_op jit(solution)/shard_map/dot_general | solution.py:137
  35.0 0.6 collective-permute-start.3
  35.6 1.7 %collective-permute-start.4 = (bf16[576,288]{0,1:T(8,128)(2,1)}, bf16[576,288]{0,1:T(8,128)(2,1)}, u32[]{:S(2)}, u32[]{:S(2)}) collective-permute-start(bf16[576,288]{0,1:T(8,128)(2,1)} %param.23), channel_id=1, source_target_pairs={{2,0},{3,1},{0,2},{1,3},{6,4},{7,5},{4,6},{5,7},{10,8},{11,9},{8,1... | collective-permute-start | bytes 995336 | tf_op jit(solution)/shard_map/ppermute | solution.py:86
  37.3 4.0 %add_convert_fusion = bf16[896,1728]{0,1:T(8,128)(2,1)S(1)} fusion(f32[896,1728]{0,1:T(8,128)S(1)} %fusion.13, f32[896,1728]{0,1:T(8,128)S(1)} %fusion.17, f32[896,1728]{0,1:T(8,128)S(1)} %fusion.15, bf16[288,1728]{1,0:T(8,128)(2,1)S(1)} %collective-permute-done.2, bf16[896,4,288]{0,2,1:T(8,128)(2,1)} %copy-done.1, s32[]{:T(128)S(6)} %select_n.103), kind=kOutput, calls=%fused_computation | convolution fusion | flops 898007040 | bytes 23187460 | tf_op jit(solution)/shard_map/dot_general | solution.py:137
  41.3 1.6 %fusion.41 = (bf16[896,1,8,72]{0,3,2,1:T(8,128)(2,1)S(1)}, bf16[896,1,8,72]{0,3,2,1:T(8,128)(2,1)}, bf16[8,72,896]{2,1,0:T(8,128)(2,1)}) fusion(bf16[896,3,8,72]{0,3,2,1:T(8,128)(2,1)S(1)} %bitcast.71), kind=kLoop, calls=%fused_computation.97 | loop fusion | bytes 6193152 | tf_op jit(solution)/shard_map/slice | solution.py:159
  42.9 1.9 %copy.40 = bf16[896,1,8,72]{3,0,2,1:T(8,128)(2,1)S(1)} copy(bf16[896,1,8,72]{0,3,2,1:T(8,128)(2,1)} %get-tuple-element.34) | data formatting | bytes 2064384
  44.8 0.9 fusion.43
  45.7 1.7 %copy.41 = bf16[896,1,8,72]{3,0,2,1:T(8,128)(2,1)} copy(bf16[896,1,8,72]{0,3,2,1:T(8,128)(2,1)S(1)} %get-tuple-element.33) | data formatting | bytes 2064384
  47.4 2.2 %pad_maximum_fusion.1.q_ref = bf16[8,512,72]{2,1,0:T(8,128)(2,1)} fusion(bf16[8,256,72]{2,1,0:T(8,128)(2,1)} %get-tuple-element.43, bf16[8,256,72]{2,1,0:T(8,128)(2,1)S(1)} %get-tuple-element.42), kind=kLoop, calls=%fused_computation.28 | loop fusion | flops 1179648 | bytes 1179648 | tf_op jit(solution)/shard_map/concatenate | solution.py:213
  49.7 1.0 bitcast_dynamic-update-slice_fusion.3
  50.8 1.0 bitcast_dynamic-update-slice_fusion.2
  51.9 1.0 bitcast_dynamic-update-slice_fusion.1
  53.0 1.8 %copy.37.w_ref = bf16[576,1152]{1,0:T(8,128)(2,1)} copy(bf16[576,1152]{0,1:T(8,128)(2,1)S(1)} %bitcast.74) | data formatting | bytes 2654208 | tf_op jit(solution)/shard_map/reshape | solution.py:154
  54.8 17.2 %shard_map.190 = bf16[512,1152]{1,0:T(8,128)(2,1)} custom-call(bf16[8,512,72]{2,1,0:T(8,128)(2,1)} %pad_maximum_fusion.1.q_ref, bf16[8,72,896]{2,1,0:T(8,128)(2,1)} %get-tuple-element.35.k_ref, bf16[8,896,72]{2,1,0:T(8,128)(2,1)} %bitcast.68, bf16[576,1152]{1,0:T(8,128)(2,1)} %copy.37.w_ref, bf16[512,1152]{1,0:T(8,128)(2,1)} %pad_maximum_fusion.x_ref, ...), custom_call_target="tpu_custom_call" | custom-call | tf_op jit(solution)/shard_map/pallas_call | solution.py:63
  72.0 1.8 %convolution_convert_fusion = bf16[256,1152]{1,0:T(8,128)(2,1)S(1)} fusion(bf16[512,1152]{1,0:T(8,128)(2,1)} %shard_map.190, s32[256]{0:T(256)S(1)} %eq.109), kind=kOutput, calls=%fused_computation.14 | convolution fusion | flops 302415872 | bytes 1770496 | tf_op jit(solution)/shard_map/dot_general | solution.py:185
  74.5 1.6 %collective-permute-start.8 = (bf16[64,1152]{1,0:T(8,128)(2,1)S(1)}, bf16[64,1152]{1,0:T(8,128)(2,1)S(1)}, u32[]{:S(2)}, u32[]{:S(2)}) collective-permute-start(bf16[64,1152]{1,0:T(8,128)(2,1)S(1)} %get-tuple-element.48), channel_id=1, source_target_pairs={{0,2},{1,3},{2,0},{3,1},{4,6},{5,7},{6,4},{7,5},{8,10},{9,11},{10,... | collective-permute-start | bytes 442376 | tf_op jit(solution)/shard_map/ppermute | solution.py:194
  76.1 0.4 collective-permute-start.9
  76.5 0.9 fusion.42
  77.5 10.3 %shard_map.191 = bf16[192,1152]{1,0:T(8,128)(2,1)} custom-call(bf16[8,192,72]{2,1,0:T(8,128)(2,1)} %get-tuple-element.18.q_ref, bf16[8,72,896]{2,1,0:T(8,128)(2,1)} %get-tuple-element.35.k_ref, bf16[8,896,72]{2,1,0:T(8,128)(2,1)} %bitcast.69, bf16[576,1152]{1,0:T(8,128)(2,1)} %copy.37.w_ref, bf16[192,1152]{1,0:T(8,128)(2,1)} %get-tuple-element.37.x_ref, ...), custom_call_target="tpu_custom_call" | custom-call | tf_op jit(solution)/shard_map/pallas_call | solution.py:63
  87.9 0.7 fusion.6
  88.7 3.6 %collective-permute-start.10 = (bf16[256,1152]{1,0:T(8,128)(2,1)S(1)}, bf16[256,1152]{1,0:T(8,128)(2,1)S(1)}, u32[]{:S(2)}, u32[]{:S(2)}) collective-permute-start(bf16[256,1152]{1,0:T(8,128)(2,1)S(1)} %get-tuple-element.27), channel_id=1, source_target_pairs={{0,4},{4,8},{8,12},{1,5},{5,9},{9,13},{2,6},{6,10},{10,14},{3,7},{... | collective-permute-start | bytes 1769480 | tf_op jit(solution)/shard_map/ppermute | solution.py:224
  92.4 1.3 %collective-permute-start.11 = (bf16[256,1152]{1,0:T(8,128)(2,1)S(1)}, bf16[256,1152]{1,0:T(8,128)(2,1)S(1)}, u32[]{:S(2)}, u32[]{:S(2)}) collective-permute-start(bf16[256,1152]{1,0:T(8,128)(2,1)S(1)} %get-tuple-element.22), channel_id=1, source_target_pairs={{4,0},{8,4},{12,8},{5,1},{9,5},{13,9},{6,2},{10,6},{14,10},{7,3},{... | collective-permute-start | bytes 1769480 | tf_op jit(solution)/shard_map/ppermute | solution.py:225
  94.9 2.5 %select_reduce_fusion.5 = (f32[384]{0:T(512)S(1)}, f32[384]{0:T(512)S(1)}) fusion(pred[384,1]{0,1:T(4,128)(4,1)S(1)} %copy-done.13, f32[]{:T(128)} %bitcast.10, f32[]{:T(128)} %bitcast.9, f32[]{:T(128)} %bitcast.26, f32[]{:T(128)} %bitcast.25), kind=kLoop, calls=%fused_computation.86 | loop fusion | flops 768 | bytes 3472 | tf_op jit(solution)/shard_map/jit(_where)/select_n | solution.py:208
  97.4 10.3 %shard_map.192 = bf16[192,1152]{1,0:T(8,128)(2,1)} custom-call(bf16[8,192,72]{2,1,0:T(8,128)(2,1)} %get-tuple-element.23.q_ref, bf16[8,72,896]{2,1,0:T(8,128)(2,1)} %get-tuple-element.35.k_ref, bf16[8,896,72]{2,1,0:T(8,128)(2,1)} %bitcast.70, bf16[576,1152]{1,0:T(8,128)(2,1)} %copy.37.w_ref, bf16[192,1152]{1,0:T(8,128)(2,1)} %get-tuple-element.36.x_ref, ...), custom_call_target="tpu_custom_call" | custom-call | tf_op jit(solution)/shard_map/pallas_call | solution.py:63
  107.7 2.5 %collective-permute-done.11 = bf16[256,1152]{1,0:T(8,128)(2,1)S(1)} collective-permute-done((bf16[256,1152]{1,0:T(8,128)(2,1)S(1)}, bf16[256,1152]{1,0:T(8,128)(2,1)S(1)}, u32[]{:S(2)}, u32[]{:S(2)}) %collective-permute-start.11) | collective-permute-done | bytes 589856 | tf_op jit(solution)/shard_map/ppermute | solution.py:225
  110.2 1.1 constant_dynamic-update-slice_fusion
  111.3 0.5 convolution_convert_fusion.1
  111.9 0.5 collective-permute-start.13
  112.4 1.0 collective-permute-start.14
  113.4 1.0 collective-permute-start.15
  115.1 2.2 %collective-permute-done.13 = bf16[48,1152]{1,0:T(8,128)(2,1)S(1)} collective-permute-done((bf16[48,1152]{1,0:T(8,128)(2,1)S(1)}, bf16[48,1152]{1,0:T(8,128)(2,1)S(1)}, u32[]{:S(2)}, u32[]{:S(2)}) %collective-permute-start.13) | collective-permute-done | bytes 110624 | tf_op jit(solution)/shard_map/ppermute | solution.py:194
  117.3 2.4 %collective-permute-done.14 = bf16[48,1152]{1,0:T(8,128)(2,1)S(1)} collective-permute-done((bf16[48,1152]{1,0:T(8,128)(2,1)S(1)}, bf16[48,1152]{1,0:T(8,128)(2,1)S(1)}, u32[]{:S(2)}, u32[]{:S(2)}) %collective-permute-start.14) | collective-permute-done | bytes 110624 | tf_op jit(solution)/shard_map/ppermute | solution.py:194
  119.7 2.4 %collective-permute-done.15 = bf16[48,1152]{1,0:T(8,128)(2,1)S(1)} collective-permute-done((bf16[48,1152]{1,0:T(8,128)(2,1)S(1)}, bf16[48,1152]{1,0:T(8,128)(2,1)S(1)}, u32[]{:S(2)}, u32[]{:S(2)}) %collective-permute-start.15) | collective-permute-done | bytes 110624 | tf_op jit(solution)/shard_map/ppermute | solution.py:194
  122.0 0.5 fusion.7
  122.6 1.5 %maximum_bitcast_fusion = bf16[1,1,896,1152]{3,2,1,0:T(8,128)(2,1)} fusion(bf16[256,1152]{1,0:T(8,128)(2,1)S(1)} %fusion.11, bf16[384,1152]{1,0:T(8,128)(2,1)S(1)} %fusion.7, bf16[256,1152]{1,0:T(8,128)(2,1)S(1)} %fusion.9), kind=kLoop, calls=%fused_computation.17 | loop fusion | flops 6193152 | bytes 4128768 | tf_op jit(solution)/shard_map/reshape | solution.py:256
  (98 shorter events, 4.7 us)
Async XLA Ops:
  0.0 7.2 %copy-start = (s32[4,4,4]{2,1,0:T(4,128)S(1)}, s32[4,4,4]{2,1,0:T(4,128)}, u32[]{:S(2)}) copy-start(s32[4,4,4]{2,1,0:T(4,128)} %param.24) | copy-start | bytes 772
  0.0 26.1 %collective-permute-start.1 = (bf16[288,1728]{1,0:T(8,128)(2,1)}, bf16[288,1728]{1,0:T(8,128)(2,1)}, u32[]{:S(2)}, u32[]{:S(2)}) collective-permute-start(bf16[288,1728]{1,0:T(8,128)(2,1)} %param.22), channel_id=1, source_target_pairs={{2,0},{3,1},{0,2},{1,3},{6,4},{7,5},{4,6},{5,7},{10,8},{11,9},{8,1... | collective-permute-start | bytes 2985992 | tf_op jit(solution)/shard_map/ppermute | solution.py:86
  2.9 28.8 %collective-permute-start = (bf16[288,1728]{1,0:T(8,128)(2,1)}, bf16[288,1728]{1,0:T(8,128)(2,1)}, u32[]{:S(2)}, u32[]{:S(2)}) collective-permute-start(bf16[288,1728]{1,0:T(8,128)(2,1)} %param.22), channel_id=1, source_target_pairs={{1,0},{0,1},{3,2},{2,3},{5,4},{4,5},{7,6},{6,7},{9,8},{8,9},{11,10... | collective-permute-start | bytes 2985992 | tf_op jit(solution)/shard_map/ppermute | solution.py:86
  7.6 1.1 copy-start.5
  7.6 1.8 %copy-start.16 = (s32[4]{0:T(128)S(1)}, s32[4]{0:T(128)}, u32[]{:S(2)}) copy-start(s32[4]{0:T(128)} %constant.93.clone) | copy-start | bytes 52
  7.6 1.9 %copy-start.9 = (s32[4,64]{1,0:T(4,128)S(1)}, s32[4,64]{1,0:T(4,128)}, u32[]{:S(2)}) copy-start(s32[4,64]{1,0:T(4,128)} %constant.94.clone) | copy-start | bytes 3076
  7.6 1.9 %copy-start.10 = (s32[4,64]{1,0:T(4,128)S(1)}, s32[4,64]{1,0:T(4,128)}, u32[]{:S(2)}) copy-start(s32[4,64]{1,0:T(4,128)} %constant.95.clone) | copy-start | bytes 3076
  7.6 2.0 %copy-start.12 = (s32[4,64]{1,0:T(4,128)S(1)}, s32[4,64]{1,0:T(4,128)}, u32[]{:S(2)}) copy-start(s32[4,64]{1,0:T(4,128)} %constant.107) | copy-start | bytes 3076
  7.6 2.2 %copy-start.14 = (s32[2]{0:T(128)S(1)}, s32[2]{0:T(128)}, u32[]{:S(2)}) copy-start(s32[2]{0:T(128)} %param.25) | copy-start | bytes 28
  7.6 2.3 %copy-start.15 = (s32[4]{0:T(128)S(1)}, s32[4]{0:T(128)}, u32[]{:S(2)}) copy-start(s32[4]{0:T(128)} %param.26) | copy-start | bytes 52
  8.0 3.2 %copy-start.7 = (s32[4,48]{1,0:T(4,128)S(1)}, s32[4,48]{1,0:T(4,128)}, u32[]{:S(2)}) copy-start(s32[4,48]{1,0:T(4,128)} %constant.100.clone) | copy-start | bytes 2308
  8.0 3.1 %copy-start.8 = (s32[4,48]{1,0:T(4,128)S(1)}, s32[4,48]{1,0:T(4,128)}, u32[]{:S(2)}) copy-start(s32[4,48]{1,0:T(4,128)} %constant.99.clone) | copy-start | bytes 2308
  11.2 3.7 %copy-start.4 = (bf16[288,1728]{1,0:T(8,128)(2,1)S(1)}, bf16[288,1728]{1,0:T(8,128)(2,1)}, u32[]{:S(2)}) copy-start(bf16[288,1728]{1,0:T(8,128)(2,1)} %param.22) | copy-start | bytes 2985988
  12.0 19.8 %copy-start.1 = (bf16[896,4,288]{0,2,1:T(8,128)(2,1)}, bf16[896,4,288]{0,2,1:T(8,128)(2,1)S(1)}, u32[]{:S(2)}) copy-start(bf16[896,4,288]{0,2,1:T(8,128)(2,1)S(1)} %add_convert_fusion.1) | copy-start | bytes 6193156
  14.9 11.1 %copy-start.11 = (pred[512,1]{0,1:T(4,128)(4,1)S(1)}, pred[512,1]{0,1:T(4,128)(4,1)}, u32[]{:S(2)}) copy-start(pred[512,1]{0,1:T(4,128)(4,1)} %constant.97.clone) | copy-start | bytes 1540
  26.1 9.0 %collective-permute-start.2 = (bf16[288,1728]{1,0:T(8,128)(2,1)}, bf16[288,1728]{1,0:T(8,128)(2,1)S(1)}, u32[]{:S(2)}, u32[]{:S(2)}) collective-permute-start(bf16[288,1728]{1,0:T(8,128)(2,1)} %collective-permute-done.1), channel_id=1, source_target_pairs={{1,0},{0,1},{3,2},{2,3},{5,4},{4,5},{7,6},{6,7},{9,8},{8,9},{11,10... | collective-permute-start | bytes 2985992 | tf_op jit(solution)/shard_map/ppermute | solution.py:86
  35.0 15.8 %collective-permute-start.3 = (bf16[576,288]{0,1:T(8,128)(2,1)}, bf16[576,288]{0,1:T(8,128)(2,1)}, u32[]{:S(2)}, u32[]{:S(2)}) collective-permute-start(bf16[576,288]{0,1:T(8,128)(2,1)} %param.23), channel_id=1, source_target_pairs={{1,0},{0,1},{3,2},{2,3},{5,4},{4,5},{7,6},{6,7},{9,8},{8,9},{11,10... | collective-permute-start | bytes 995336 | tf_op jit(solution)/shard_map/ppermute | solution.py:86
  35.6 15.1 %collective-permute-start.4 = (bf16[576,288]{0,1:T(8,128)(2,1)}, bf16[576,288]{0,1:T(8,128)(2,1)}, u32[]{:S(2)}, u32[]{:S(2)}) collective-permute-start(bf16[576,288]{0,1:T(8,128)(2,1)} %param.23), channel_id=1, source_target_pairs={{2,0},{3,1},{0,2},{1,3},{6,4},{7,5},{4,6},{5,7},{10,8},{11,9},{8,1... | collective-permute-start | bytes 995336 | tf_op jit(solution)/shard_map/ppermute | solution.py:86
  50.7 2.2 %collective-permute-start.5 = (bf16[576,288]{0,1:T(8,128)(2,1)}, bf16[576,288]{0,1:T(8,128)(2,1)S(1)}, u32[]{:S(2)}, u32[]{:S(2)}) collective-permute-start(bf16[576,288]{0,1:T(8,128)(2,1)} %collective-permute-done.4), channel_id=1, source_target_pairs={{1,0},{0,1},{3,2},{2,3},{5,4},{4,5},{7,6},{6,7},{9,8},{8,9},{11,10... | collective-permute-start | bytes 995336 | tf_op jit(solution)/shard_map/ppermute | solution.py:86
  73.9 13.9 %collective-permute-start.6 = (bf16[64,1152]{1,0:T(8,128)(2,1)S(1)}, bf16[64,1152]{1,0:T(8,128)(2,1)S(1)}, u32[]{:S(2)}, u32[]{:S(2)}) collective-permute-start(bf16[64,1152]{1,0:T(8,128)(2,1)S(1)} %get-tuple-element.46), channel_id=1, source_target_pairs={{0,3},{1,0},{2,1},{3,2},{4,7},{5,4},{6,5},{7,6},{8,11},{9,8},{10,9... | collective-permute-start | bytes 442376 | tf_op jit(solution)/shard_map/ppermute | solution.py:194
  74.3 13.5 %collective-permute-start.7 = (bf16[64,1152]{1,0:T(8,128)(2,1)S(1)}, bf16[64,1152]{1,0:T(8,128)(2,1)S(1)}, u32[]{:S(2)}, u32[]{:S(2)}) collective-permute-start(bf16[64,1152]{1,0:T(8,128)(2,1)S(1)} %get-tuple-element.49), channel_id=1, source_target_pairs={{0,1},{1,2},{2,3},{3,0},{4,5},{5,6},{6,7},{7,4},{8,9},{9,10},{10,1... | collective-permute-start | bytes 442376 | tf_op jit(solution)/shard_map/ppermute | solution.py:194
  74.5 13.3 %collective-permute-start.8 = (bf16[64,1152]{1,0:T(8,128)(2,1)S(1)}, bf16[64,1152]{1,0:T(8,128)(2,1)S(1)}, u32[]{:S(2)}, u32[]{:S(2)}) collective-permute-start(bf16[64,1152]{1,0:T(8,128)(2,1)S(1)} %get-tuple-element.48), channel_id=1, source_target_pairs={{0,2},{1,3},{2,0},{3,1},{4,6},{5,7},{6,4},{7,5},{8,10},{9,11},{10,... | collective-permute-start | bytes 442376 | tf_op jit(solution)/shard_map/ppermute | solution.py:194
  76.1 11.7 %collective-permute-start.9 = (bf16[64,1152]{1,0:T(8,128)(2,1)S(1)}, bf16[64,1152]{1,0:T(8,128)(2,1)S(1)}, u32[]{:S(2)}, u32[]{:S(2)}) collective-permute-start(bf16[64,1152]{1,0:T(8,128)(2,1)S(1)} %get-tuple-element.47), channel_id=1, source_target_pairs={{0,2},{1,3},{2,0},{3,1},{4,6},{5,7},{6,4},{7,5},{8,10},{9,11},{10,... | collective-permute-start | bytes 442376 | tf_op jit(solution)/shard_map/ppermute | solution.py:194
  77.5 10.4 %copy-start.2 = (bf16[512,1152]{1,0:T(8,128)(2,1)S(1)}, bf16[512,1152]{1,0:T(8,128)(2,1)}, u32[]{:S(2)}) copy-start(bf16[512,1152]{1,0:T(8,128)(2,1)} %shard_map.190) | copy-start | bytes 3538948
  77.5 10.4 %copy-start.18 = (pred[512]{0:T(512)(128)(4,1)S(1)}, pred[512]{0:T(512)(128)(4,1)}, u32[]{:S(2)}) copy-start(pred[512]{0:T(512)(128)(4,1)} %constant.106) | copy-start | bytes 1540
  88.6 5.8 %copy-start.6 = (s32[4,48]{1,0:T(4,128)S(1)}, s32[4,48]{1,0:T(4,128)}, u32[]{:S(2)}) copy-start(s32[4,48]{1,0:T(4,128)} %constant.109) | copy-start | bytes 2308
  88.6 6.2 %copy-start.13 = (pred[384,1]{0,1:T(4,128)(4,1)S(1)}, pred[384,1]{0,1:T(4,128)(4,1)}, u32[]{:S(2)}) copy-start(pred[384,1]{0,1:T(4,128)(4,1)} %constant.102.clone) | copy-start | bytes 1156
  88.7 19.0 %collective-permute-start.10 = (bf16[256,1152]{1,0:T(8,128)(2,1)S(1)}, bf16[256,1152]{1,0:T(8,128)(2,1)S(1)}, u32[]{:S(2)}, u32[]{:S(2)}) collective-permute-start(bf16[256,1152]{1,0:T(8,128)(2,1)S(1)} %get-tuple-element.27), channel_id=1, source_target_pairs={{0,4},{4,8},{8,12},{1,5},{5,9},{9,13},{2,6},{6,10},{10,14},{3,7},{... | collective-permute-start | bytes 1769480 | tf_op jit(solution)/shard_map/ppermute | solution.py:224
  92.4 17.9 %collective-permute-start.11 = (bf16[256,1152]{1,0:T(8,128)(2,1)S(1)}, bf16[256,1152]{1,0:T(8,128)(2,1)S(1)}, u32[]{:S(2)}, u32[]{:S(2)}) collective-permute-start(bf16[256,1152]{1,0:T(8,128)(2,1)S(1)} %get-tuple-element.22), channel_id=1, source_target_pairs={{4,0},{8,4},{12,8},{5,1},{9,5},{13,9},{6,2},{10,6},{14,10},{7,3},{... | collective-permute-start | bytes 1769480 | tf_op jit(solution)/shard_map/ppermute | solution.py:225
  97.4 10.3 %copy-start.3 = (bf16[192,1152]{1,0:T(8,128)(2,1)S(1)}, bf16[192,1152]{1,0:T(8,128)(2,1)}, u32[]{:S(2)}) copy-start(bf16[192,1152]{1,0:T(8,128)(2,1)} %shard_map.191) | copy-start | bytes 1327108
  111.8 10.3 %copy-start.17 = (pred[384]{0:T(512)(128)(4,1)S(1)}, pred[384]{0:T(512)(128)(4,1)}, u32[]{:S(2)}) copy-start(pred[384]{0:T(512)(128)(4,1)} %constant.108) | copy-start | bytes 1156
  111.8 3.3 %collective-permute-start.12 = (bf16[48,1152]{1,0:T(8,128)(2,1)S(1)}, bf16[48,1152]{1,0:T(8,128)(2,1)S(1)}, u32[]{:S(2)}, u32[]{:S(2)}) collective-permute-start(bf16[48,1152]{1,0:T(8,128)(2,1)S(1)} %get-tuple-element.50), channel_id=1, source_target_pairs={{0,3},{1,0},{2,1},{3,2},{4,7},{5,4},{6,5},{7,6},{8,11},{9,8},{10,9... | collective-permute-start | bytes 331784 | tf_op jit(solution)/shard_map/ppermute | solution.py:194
  111.9 5.4 %collective-permute-start.13 = (bf16[48,1152]{1,0:T(8,128)(2,1)S(1)}, bf16[48,1152]{1,0:T(8,128)(2,1)S(1)}, u32[]{:S(2)}, u32[]{:S(2)}) collective-permute-start(bf16[48,1152]{1,0:T(8,128)(2,1)S(1)} %get-tuple-element.53), channel_id=1, source_target_pairs={{0,1},{1,2},{2,3},{3,0},{4,5},{5,6},{6,7},{7,4},{8,9},{9,10},{10,1... | collective-permute-start | bytes 331784 | tf_op jit(solution)/shard_map/ppermute | solution.py:194
  112.4 7.3 %collective-permute-start.14 = (bf16[48,1152]{1,0:T(8,128)(2,1)S(1)}, bf16[48,1152]{1,0:T(8,128)(2,1)S(1)}, u32[]{:S(2)}, u32[]{:S(2)}) collective-permute-start(bf16[48,1152]{1,0:T(8,128)(2,1)S(1)} %get-tuple-element.52), channel_id=1, source_target_pairs={{0,2},{1,3},{2,0},{3,1},{4,6},{5,7},{6,4},{7,5},{8,10},{9,11},{10,... | collective-permute-start | bytes 331784 | tf_op jit(solution)/shard_map/ppermute | solution.py:194
  113.4 8.6 %collective-permute-start.15 = (bf16[48,1152]{1,0:T(8,128)(2,1)S(1)}, bf16[48,1152]{1,0:T(8,128)(2,1)S(1)}, u32[]{:S(2)}, u32[]{:S(2)}) collective-permute-start(bf16[48,1152]{1,0:T(8,128)(2,1)S(1)} %get-tuple-element.51), channel_id=1, source_target_pairs={{0,2},{1,3},{2,0},{3,1},{4,6},{5,7},{6,4},{7,5},{8,10},{9,11},{10,... | collective-permute-start | bytes 331784 | tf_op jit(solution)/shard_map/ppermute | solution.py:194

commit v7 on v6

--- a/solution.py
+++ b/solution.py
@@ -131,12 +131,23 @@
     qkv_pieces = face_pieces(w_qkv)
     w_out_late, _ = lax.optimization_barrier((w_out, [piece for piece, _ in qkv_pieces]))
     if n <= 4:
-        moved_parts = moved.reshape(tokens, n, rows).transpose(1, 0, 2)
+        me = lax.axis_index("face")
+        core = me % 2
+        chips = n // 2
+        moved_chips = moved.reshape(tokens, chips, 2 * rows).transpose(1, 0, 2)
+
+        def chip_weight(same_core, other_core):
+            stack = jnp.zeros((2,) + w_qkv.shape, w_qkv.dtype)
+            stack = lax.dynamic_update_index_in_dim(stack, same_core, core, 0)
+            stack = lax.dynamic_update_index_in_dim(stack, other_core, 1 - core, 0)
+            return stack.reshape(2 * rows, w_qkv.shape[1])
+
         qkv_sums = None
-        for piece, index in qkv_pieces:
+        for j in range(chips):
+            weight = chip_weight(qkv_pieces[2 * j][0], qkv_pieces[2 * j + 1][0])
             part = jnp.dot(
-                lax.dynamic_index_in_dim(moved_parts, index, 0, keepdims=False),
-                piece,
+                lax.dynamic_index_in_dim(moved_chips, (me // 2 + j) % chips, 0, keepdims=False),
+                weight,
                 preferred_element_type=jnp.float32,
             )
             qkv_sums = part if qkv_sums is None else qkv_sums + part

time: 125 us -> 122 us (0.976)
  matrix products: 15.9 us -> 9.67 us
  local copies, waits for them, and re-layouts: 22.2 us -> 25.3 us
    dot_general x4 -> x2, matrix products: 12.3 us -> 6.12 us  [per_device(): jnp.dot(lax.dynamic_index_in_dim(moved_chips, (me // 2 + j) % chips, 0, k...]
    dynamic_update_slice x0 -> x4, local copies, waits for them, and re-layouts: none -> 2.81 us  [the longest x2 1.41 us: chip_weight(): stack = lax.dynamic_update_index_in_dim(stack, same_core, core, 0)]
    unnamed x42 -> x40, local copies, waits for them, and re-layouts: 6.6 us -> 6.59 us
  transfers between devices with their start and end apart: 16 -> 16, of which waited for: 5 -> 5; matrix products, arithmetic and copies ran while one was open for 35% -> 33% of each run, Pallas kernels for 17% -> 17%
where the time goes in v7:
time: 122 us; the launch traced here: 121 us
  Pallas kernels  37.8 us (31%)
  local copies, waits for them, and re-layouts  25.3 us (21%)
  waiting for transfers between devices  18.4 us (15%)
  starting transfers between devices  15.5 us (13%)
  other arithmetic  13.8 us (11%)
  matrix products  9.67 us (8%)
    pallas_call x3, Pallas kernels, attend_project(): pl.pallas_call(attention_kernel, grid=(1, heads), in_specs=[pl.BlockSpec(...  37.8 us
    ppermute x6, waiting for transfers between devices, fetch(): return lax.ppermute(x, 'face', [(src_of(i), i) for i in range(n)])  8.96 us
    ppermute x8, waiting for transfers between devices, strips_in(): lax.ppermute(sent, 'face', [(i, (i + shift) % n) for i in range(n)])  6.93 us
    unnamed x40, local copies, waits for them, and re-layouts  6.59 us
    dot_general x2, matrix products, per_device(): jnp.dot(lax.dynamic_index_in_dim(moved_chips, (me // 2 + j) % chips, 0, k...  6.12 us
    ppermute x6, starting transfers between devices, fetch(): return lax.ppermute(x, 'face', [(src_of(i), i) for i in range(n)])  5.4 us
    ppermute x8, starting transfers between devices, strips_in(): lax.ppermute(sent, 'face', [(i, (i + shift) % n) for i in range(n)])  5.21 us
    select_n x2, other arithmetic, space_blend(): w_keep = jnp.where(dep == 0, keep[0], keep[1])  5.19 us
  transfers between devices with their start and end apart: 16, of which 5 were waited for; matrix products, arithmetic and copies ran while one was open for 33% of the time, Pallas kernels for 17%

profile of v7, /device:TPU:0, one launch (start us, length us, event | category | flops | bytes accessed | tf_op | source)
XLA Modules:
  0.0 120.9 jit_solution(944555680431990459)
XLA Ops:
  0.0 0.5 collective-permute-start
  0.5 2.6 %collective-permute-start.1 = (bf16[288,1728]{1,0:T(8,128)(2,1)}, bf16[288,1728]{1,0:T(8,128)(2,1)}, u32[]{:S(2)}, u32[]{:S(2)}) collective-permute-start(bf16[288,1728]{1,0:T(8,128)(2,1)} %param.22), channel_id=1, source_target_pairs={{2,0},{3,1},{0,2},{1,3},{6,4},{7,5},{4,6},{5,7},{10,8},{11,9},{8,1... | collective-permute-start | bytes 2985992 | tf_op jit(solution)/shard_map/ppermute | solution.py:86
  3.0 2.9 %copy.34 = bf16[1,1,896,1152]{2,3,1,0:T(8,128)(2,1)S(1)} copy(bf16[1,1,896,1152]{3,2,1,0:T(8,128)(2,1)} %param.20) | data formatting | bytes 4128768 | tf_op args[0]
  5.9 1.3 %slice_bitcast_fusion.2 = (bf16[256,1152]{1,0:T(8,128)(2,1)S(1)}, bf16[256,1152]{1,0:T(8,128)(2,1)S(1)}) fusion(bf16[1,1,896,1152]{3,2,1,0:T(8,128)(2,1)} %param.20), kind=kLoop, calls=%fused_computation.41 | loop fusion | bytes 2359296 | tf_op jit(solution)/shard_map/slice | solution.py:225
  8.1 0.6 fusion.1
  8.7 0.6 add_reduce_fusion
  10.1 1.1 pad_maximum_fusion.x_ref
  11.2 0.6 fusion.39
  11.9 0.8 add_convert_fusion.1
  12.7 2.6 %broadcast_select_fusion.1 = (f32[512,1]{0,1:T(1,128)S(1)}, f32[512,1]{0,1:T(1,128)S(1)}) fusion(pred[512,1]{0,1:T(4,128)(4,1)S(1)} %copy-done.10, f32[]{:T(128)} %bitcast.14, f32[]{:T(128)} %bitcast.13, f32[]{:T(128)} %bitcast.30, f32[]{:T(128)} %bitcast.29), kind=kLoop, calls=%fused_computation.85 | loop fusion | flops 1024 | bytes 4624 | tf_op jit(solution)/shard_map/jit(_where)/select_n | solution.py:219
  15.6 2.2 %slice_bitcast_fusion.3 = (bf16[192,1152]{1,0:T(8,128)(2,1)}, bf16[192,1152]{1,0:T(8,128)(2,1)}) fusion(bf16[1,1,896,1152]{3,2,1,0:T(8,128)(2,1)} %param.20), kind=kLoop, calls=%fused_computation.51 | loop fusion | bytes 1769472 | tf_op jit(solution)/shard_map/slice | solution.py:240
  17.8 8.9 %collective-permute-done.1 = bf16[288,1728]{1,0:T(8,128)(2,1)} collective-permute-done((bf16[288,1728]{1,0:T(8,128)(2,1)}, bf16[288,1728]{1,0:T(8,128)(2,1)}, u32[]{:S(2)}, u32[]{:S(2)}) %collective-permute-start.1) | collective-permute-done | bytes 995360 | tf_op jit(solution)/shard_map/ppermute | solution.py:86
  26.7 1.3 %bitcast_dynamic-update-slice_fusion.2 = bf16[2,288,1728]{2,1,0:T(8,128)(2,1)S(1)} fusion(bf16[2,288,1728]{2,1,0:T(8,128)(2,1)S(1)} %bitcast_dynamic-update-slice_fusion.3, s32[]{:T(128)S(6)} %select_n.127, bf16[288,1728]{1,0:T(8,128)(2,1)} %collective-permute-done), kind=kLoop, calls=%fused_computation.33 | loop fusion | bytes 2027524 | tf_op jit(solution)/shard_map/jit(dynamic_update_index_in_dim)/dynamic_update_slice | solution.py:142
  28.1 2.9 %fusion.13 = f32[896,1728]{0,1:T(8,128)S(1)} fusion(bf16[576,1728]{1,0:T(8,128)(2,1)S(1)} %bitcast.78, bf16[896,2,576]{0,2,1:T(8,128)(2,1)S(1)} %add_convert_fusion.1, s32[]{:T(128)S(6)} %select_n.124), kind=kOutput, calls=%fused_computation.35 | convolution fusion | flops 1783627776 | bytes 9289732 | tf_op jit(solution)/shard_map/dot_general | solution.py:148
  31.1 1.3 %bitcast_dynamic-update-slice_fusion.1 = bf16[2,288,1728]{2,1,0:T(8,128)(2,1)S(1)} fusion(bf16[2,288,1728]{2,1,0:T(8,128)(2,1)S(1)} %broadcast.91.clone.1, s32[]{:T(128)S(6)} %select_n.126, bf16[288,1728]{1,0:T(8,128)(2,1)} %collective-permute-done.1), kind=kLoop, calls=%fused_computation.31 | loop fusion | bytes 2027524 | tf_op jit(solution)/shard_map/jit(dynamic_update_index_in_dim)/dynamic_update_slice | solution.py:141
  32.4 0.6 collective-permute-start.3
  33.0 1.7 %collective-permute-start.4 = (bf16[576,288]{0,1:T(8,128)(2,1)}, bf16[576,288]{0,1:T(8,128)(2,1)}, u32[]{:S(2)}, u32[]{:S(2)}) collective-permute-start(bf16[576,288]{0,1:T(8,128)(2,1)} %param.23), channel_id=1, source_target_pairs={{2,0},{3,1},{0,2},{1,3},{6,4},{7,5},{4,6},{5,7},{10,8},{11,9},{8,1... | collective-permute-start | bytes 995336 | tf_op jit(solution)/shard_map/ppermute | solution.py:86
  34.8 3.2 %add_convert_fusion = bf16[896,1728]{0,1:T(8,128)(2,1)S(1)} fusion(f32[896,1728]{0,1:T(8,128)S(1)} %fusion.13, bf16[576,1728]{1,0:T(8,128)(2,1)S(1)} %bitcast.77, bf16[896,2,576]{0,2,1:T(8,128)(2,1)S(1)} %add_convert_fusion.1, s32[]{:T(128)S(6)} %select_n.129), kind=kOutput, calls=%fused_computation | convolution fusion | flops 1786724352 | bytes 12386308 | tf_op jit(solution)/shard_map/dot_general | solution.py:148
  38.1 1.6 %fusion.33 = (bf16[896,1,8,72]{0,3,2,1:T(8,128)(2,1)S(1)}, bf16[896,1,8,72]{0,3,2,1:T(8,128)(2,1)}, bf16[8,72,896]{2,1,0:T(8,128)(2,1)}) fusion(bf16[896,3,8,72]{0,3,2,1:T(8,128)(2,1)S(1)} %bitcast.76), kind=kLoop, calls=%fused_computation.93 | loop fusion | bytes 6193152 | tf_op jit(solution)/shard_map/slice | solution.py:170
  39.7 1.9 %copy.40 = bf16[896,1,8,72]{3,0,2,1:T(8,128)(2,1)S(1)} copy(bf16[896,1,8,72]{0,3,2,1:T(8,128)(2,1)} %get-tuple-element.34) | data formatting | bytes 2064384
  41.6 0.9 fusion.35
  42.5 1.7 %copy.41 = bf16[896,1,8,72]{3,0,2,1:T(8,128)(2,1)} copy(bf16[896,1,8,72]{0,3,2,1:T(8,128)(2,1)S(1)} %get-tuple-element.33) | data formatting | bytes 2064384
  44.1 2.2 %pad_maximum_fusion.1.q_ref = bf16[8,512,72]{2,1,0:T(8,128)(2,1)} fusion(bf16[8,256,72]{2,1,0:T(8,128)(2,1)} %get-tuple-element.43, bf16[8,256,72]{2,1,0:T(8,128)(2,1)S(1)} %get-tuple-element.42), kind=kLoop, calls=%fused_computation.28 | loop fusion | flops 1179648 | bytes 1179648 | tf_op jit(solution)/shard_map/concatenate | solution.py:224
  46.5 1.0 bitcast_dynamic-update-slice_fusion.7
  47.6 1.0 bitcast_dynamic-update-slice_fusion.6
  48.7 1.0 bitcast_dynamic-update-slice_fusion.5
  49.8 1.9 %copy.37.w_ref = bf16[576,1152]{1,0:T(8,128)(2,1)} copy(bf16[576,1152]{0,1:T(8,128)(2,1)S(1)} %bitcast.75) | data formatting | bytes 2654208 | tf_op jit(solution)/shard_map/reshape | solution.py:165
  51.6 17.2 %shard_map.190 = bf16[512,1152]{1,0:T(8,128)(2,1)} custom-call(bf16[8,512,72]{2,1,0:T(8,128)(2,1)} %pad_maximum_fusion.1.q_ref, bf16[8,72,896]{2,1,0:T(8,128)(2,1)} %get-tuple-element.35.k_ref, bf16[8,896,72]{2,1,0:T(8,128)(2,1)} %bitcast.70, bf16[576,1152]{1,0:T(8,128)(2,1)} %copy.37.w_ref, bf16[512,1152]{1,0:T(8,128)(2,1)} %pad_maximum_fusion.x_ref, ...), custom_call_target="tpu_custom_call" | custom-call | tf_op jit(solution)/shard_map/pallas_call | solution.py:63
  68.8 1.8 %convolution_convert_fusion = bf16[256,1152]{1,0:T(8,128)(2,1)S(1)} fusion(bf16[512,1152]{1,0:T(8,128)(2,1)} %shard_map.190, s32[256]{0:T(256)S(1)} %eq.110), kind=kOutput, calls=%fused_computation.14 | convolution fusion | flops 302415872 | bytes 1770496 | tf_op jit(solution)/shard_map/dot_general | solution.py:196
  71.3 1.6 %collective-permute-start.8 = (bf16[64,1152]{1,0:T(8,128)(2,1)S(1)}, bf16[64,1152]{1,0:T(8,128)(2,1)S(1)}, u32[]{:S(2)}, u32[]{:S(2)}) collective-permute-start(bf16[64,1152]{1,0:T(8,128)(2,1)S(1)} %get-tuple-element.48), channel_id=1, source_target_pairs={{0,2},{1,3},{2,0},{3,1},{4,6},{5,7},{6,4},{7,5},{8,10},{9,11},{10,... | collective-permute-start | bytes 442376 | tf_op jit(solution)/shard_map/ppermute | solution.py:205
  73.3 1.0 fusion.34
  74.3 10.3 %shard_map.191 = bf16[192,1152]{1,0:T(8,128)(2,1)} custom-call(bf16[8,192,72]{2,1,0:T(8,128)(2,1)} %get-tuple-element.18.q_ref, bf16[8,72,896]{2,1,0:T(8,128)(2,1)} %get-tuple-element.35.k_ref, bf16[8,896,72]{2,1,0:T(8,128)(2,1)} %bitcast.71, bf16[576,1152]{1,0:T(8,128)(2,1)} %copy.37.w_ref, bf16[192,1152]{1,0:T(8,128)(2,1)} %get-tuple-element.37.x_ref, ...), custom_call_target="tpu_custom_call" | custom-call | tf_op jit(solution)/shard_map/pallas_call | solution.py:63
  84.7 0.7 fusion.6
  85.6 3.6 %collective-permute-start.10 = (bf16[256,1152]{1,0:T(8,128)(2,1)S(1)}, bf16[256,1152]{1,0:T(8,128)(2,1)S(1)}, u32[]{:S(2)}, u32[]{:S(2)}) collective-permute-start(bf16[256,1152]{1,0:T(8,128)(2,1)S(1)} %get-tuple-element.27), channel_id=1, source_target_pairs={{0,4},{4,8},{8,12},{1,5},{5,9},{9,13},{2,6},{6,10},{10,14},{3,7},{... | collective-permute-start | bytes 1769480 | tf_op jit(solution)/shard_map/ppermute | solution.py:235
  89.2 1.3 %collective-permute-start.11 = (bf16[256,1152]{1,0:T(8,128)(2,1)S(1)}, bf16[256,1152]{1,0:T(8,128)(2,1)S(1)}, u32[]{:S(2)}, u32[]{:S(2)}) collective-permute-start(bf16[256,1152]{1,0:T(8,128)(2,1)S(1)} %get-tuple-element.22), channel_id=1, source_target_pairs={{4,0},{8,4},{12,8},{5,1},{9,5},{13,9},{6,2},{10,6},{14,10},{7,3},{... | collective-permute-start | bytes 1769480 | tf_op jit(solution)/shard_map/ppermute | solution.py:236
  91.7 2.6 %select_reduce_fusion.5 = (f32[384]{0:T(512)S(1)}, f32[384]{0:T(512)S(1)}) fusion(pred[384,1]{0,1:T(4,128)(4,1)S(1)} %copy-done.12, f32[]{:T(128)} %bitcast.14, f32[]{:T(128)} %bitcast.13, f32[]{:T(128)} %bitcast.30, f32[]{:T(128)} %bitcast.29), kind=kLoop, calls=%fused_computation.82 | loop fusion | flops 768 | bytes 3472 | tf_op jit(solution)/shard_map/jit(_where)/select_n | solution.py:219
  94.3 10.3 %shard_map.192 = bf16[192,1152]{1,0:T(8,128)(2,1)} custom-call(bf16[8,192,72]{2,1,0:T(8,128)(2,1)} %get-tuple-element.23.q_ref, bf16[8,72,896]{2,1,0:T(8,128)(2,1)} %get-tuple-element.35.k_ref, bf16[8,896,72]{2,1,0:T(8,128)(2,1)} %bitcast.72, bf16[576,1152]{1,0:T(8,128)(2,1)} %copy.37.w_ref, bf16[192,1152]{1,0:T(8,128)(2,1)} %get-tuple-element.36.x_ref, ...), custom_call_target="tpu_custom_call" | custom-call | tf_op jit(solution)/shard_map/pallas_call | solution.py:63
  104.6 2.5 %collective-permute-done.11 = bf16[256,1152]{1,0:T(8,128)(2,1)S(1)} collective-permute-done((bf16[256,1152]{1,0:T(8,128)(2,1)S(1)}, bf16[256,1152]{1,0:T(8,128)(2,1)S(1)}, u32[]{:S(2)}, u32[]{:S(2)}) %collective-permute-start.11) | collective-permute-done | bytes 589856 | tf_op jit(solution)/shard_map/ppermute | solution.py:236
  107.1 1.1 constant_dynamic-update-slice_fusion
  108.1 0.5 convolution_convert_fusion.1
  108.7 0.5 collective-permute-start.13
  109.2 1.0 collective-permute-start.14
  110.2 1.0 collective-permute-start.15
  111.9 2.2 %collective-permute-done.13 = bf16[48,1152]{1,0:T(8,128)(2,1)S(1)} collective-permute-done((bf16[48,1152]{1,0:T(8,128)(2,1)S(1)}, bf16[48,1152]{1,0:T(8,128)(2,1)S(1)}, u32[]{:S(2)}, u32[]{:S(2)}) %collective-permute-start.13) | collective-permute-done | bytes 110624 | tf_op jit(solution)/shard_map/ppermute | solution.py:205
  114.1 2.4 %collective-permute-done.14 = bf16[48,1152]{1,0:T(8,128)(2,1)S(1)} collective-permute-done((bf16[48,1152]{1,0:T(8,128)(2,1)S(1)}, bf16[48,1152]{1,0:T(8,128)(2,1)S(1)}, u32[]{:S(2)}, u32[]{:S(2)}) %collective-permute-start.14) | collective-permute-done | bytes 110624 | tf_op jit(solution)/shard_map/ppermute | solution.py:205
  116.5 2.4 %collective-permute-done.15 = bf16[48,1152]{1,0:T(8,128)(2,1)S(1)} collective-permute-done((bf16[48,1152]{1,0:T(8,128)(2,1)S(1)}, bf16[48,1152]{1,0:T(8,128)(2,1)S(1)}, u32[]{:S(2)}, u32[]{:S(2)}) %collective-permute-start.15) | collective-permute-done | bytes 110624 | tf_op jit(solution)/shard_map/ppermute | solution.py:205
  118.8 0.5 fusion.7
  119.4 1.5 %maximum_bitcast_fusion = bf16[1,1,896,1152]{3,2,1,0:T(8,128)(2,1)} fusion(bf16[256,1152]{1,0:T(8,128)(2,1)S(1)} %fusion.11, bf16[384,1152]{1,0:T(8,128)(2,1)S(1)} %fusion.7, bf16[256,1152]{1,0:T(8,128)(2,1)S(1)} %fusion.9), kind=kLoop, calls=%fused_computation.17 | loop fusion | flops 6193152 | bytes 4128768 | tf_op jit(solution)/shard_map/reshape | solution.py:267
  (100 shorter events, 5.6 us)
Async XLA Ops:
  0.0 7.2 %copy-start = (s32[4,4,4]{2,1,0:T(4,128)S(1)}, s32[4,4,4]{2,1,0:T(4,128)}, u32[]{:S(2)}) copy-start(s32[4,4,4]{2,1,0:T(4,128)} %param.24) | copy-start | bytes 772
  0.0 26.7 %collective-permute-start = (bf16[288,1728]{1,0:T(8,128)(2,1)}, bf16[288,1728]{1,0:T(8,128)(2,1)}, u32[]{:S(2)}, u32[]{:S(2)}) collective-permute-start(bf16[288,1728]{1,0:T(8,128)(2,1)} %param.22), channel_id=1, source_target_pairs={{1,0},{0,1},{3,2},{2,3},{5,4},{4,5},{7,6},{6,7},{9,8},{8,9},{11,10... | collective-permute-start | bytes 2985992 | tf_op jit(solution)/shard_map/ppermute | solution.py:86
  0.5 26.3 %collective-permute-start.1 = (bf16[288,1728]{1,0:T(8,128)(2,1)}, bf16[288,1728]{1,0:T(8,128)(2,1)}, u32[]{:S(2)}, u32[]{:S(2)}) collective-permute-start(bf16[288,1728]{1,0:T(8,128)(2,1)} %param.22), channel_id=1, source_target_pairs={{2,0},{3,1},{0,2},{1,3},{6,4},{7,5},{4,6},{5,7},{10,8},{11,9},{8,1... | collective-permute-start | bytes 2985992 | tf_op jit(solution)/shard_map/ppermute | solution.py:86
  7.6 1.1 copy-start.4
  7.7 1.8 %copy-start.15 = (s32[4]{0:T(128)S(1)}, s32[4]{0:T(128)}, u32[]{:S(2)}) copy-start(s32[4]{0:T(128)} %constant.125.clone) | copy-start | bytes 52
  7.7 1.9 %copy-start.8 = (s32[4,64]{1,0:T(4,128)S(1)}, s32[4,64]{1,0:T(4,128)}, u32[]{:S(2)}) copy-start(s32[4,64]{1,0:T(4,128)} %constant.126.clone) | copy-start | bytes 3076
  7.7 1.9 %copy-start.9 = (s32[4,64]{1,0:T(4,128)S(1)}, s32[4,64]{1,0:T(4,128)}, u32[]{:S(2)}) copy-start(s32[4,64]{1,0:T(4,128)} %constant.127.clone) | copy-start | bytes 3076
  7.7 2.0 %copy-start.11 = (s32[4,64]{1,0:T(4,128)S(1)}, s32[4,64]{1,0:T(4,128)}, u32[]{:S(2)}) copy-start(s32[4,64]{1,0:T(4,128)} %constant.139) | copy-start | bytes 3076
  7.7 2.2 %copy-start.13 = (s32[2]{0:T(128)S(1)}, s32[2]{0:T(128)}, u32[]{:S(2)}) copy-start(s32[2]{0:T(128)} %param.25) | copy-start | bytes 28
  7.7 2.3 %copy-start.14 = (s32[4]{0:T(128)S(1)}, s32[4]{0:T(128)}, u32[]{:S(2)}) copy-start(s32[4]{0:T(128)} %param.26) | copy-start | bytes 52
  8.1 3.8 %copy-start.6 = (s32[4,48]{1,0:T(4,128)S(1)}, s32[4,48]{1,0:T(4,128)}, u32[]{:S(2)}) copy-start(s32[4,48]{1,0:T(4,128)} %constant.131.clone) | copy-start | bytes 2308
  8.1 3.8 %copy-start.7 = (s32[4,48]{1,0:T(4,128)S(1)}, s32[4,48]{1,0:T(4,128)}, u32[]{:S(2)}) copy-start(s32[4,48]{1,0:T(4,128)} %constant.132.clone) | copy-start | bytes 2308
  11.9 0.8 copy-start.10
  12.7 2.8 %copy-start.3 = (bf16[288,1728]{1,0:T(8,128)(2,1)S(1)}, bf16[288,1728]{1,0:T(8,128)(2,1)}, u32[]{:S(2)}) copy-start(bf16[288,1728]{1,0:T(8,128)(2,1)} %param.22) | copy-start | bytes 2985988
  26.7 5.7 %collective-permute-start.2 = (bf16[288,1728]{1,0:T(8,128)(2,1)}, bf16[288,1728]{1,0:T(8,128)(2,1)S(1)}, u32[]{:S(2)}, u32[]{:S(2)}) collective-permute-start(bf16[288,1728]{1,0:T(8,128)(2,1)} %collective-permute-done.1), channel_id=1, source_target_pairs={{1,0},{0,1},{3,2},{2,3},{5,4},{4,5},{7,6},{6,7},{9,8},{8,9},{11,10... | collective-permute-start | bytes 2985992 | tf_op jit(solution)/shard_map/ppermute | solution.py:86
  32.4 15.2 %collective-permute-start.3 = (bf16[576,288]{0,1:T(8,128)(2,1)}, bf16[576,288]{0,1:T(8,128)(2,1)}, u32[]{:S(2)}, u32[]{:S(2)}) collective-permute-start(bf16[576,288]{0,1:T(8,128)(2,1)} %param.23), channel_id=1, source_target_pairs={{1,0},{0,1},{3,2},{2,3},{5,4},{4,5},{7,6},{6,7},{9,8},{8,9},{11,10... | collective-permute-start | bytes 995336 | tf_op jit(solution)/shard_map/ppermute | solution.py:86
  33.0 14.5 %collective-permute-start.4 = (bf16[576,288]{0,1:T(8,128)(2,1)}, bf16[576,288]{0,1:T(8,128)(2,1)}, u32[]{:S(2)}, u32[]{:S(2)}) collective-permute-start(bf16[576,288]{0,1:T(8,128)(2,1)} %param.23), channel_id=1, source_target_pairs={{2,0},{3,1},{0,2},{1,3},{6,4},{7,5},{4,6},{5,7},{10,8},{11,9},{8,1... | collective-permute-start | bytes 995336 | tf_op jit(solution)/shard_map/ppermute | solution.py:86
  47.5 2.2 %collective-permute-start.5 = (bf16[576,288]{0,1:T(8,128)(2,1)}, bf16[576,288]{0,1:T(8,128)(2,1)S(1)}, u32[]{:S(2)}, u32[]{:S(2)}) collective-permute-start(bf16[576,288]{0,1:T(8,128)(2,1)} %collective-permute-done.4), channel_id=1, source_target_pairs={{1,0},{0,1},{3,2},{2,3},{5,4},{4,5},{7,6},{6,7},{9,8},{8,9},{11,10... | collective-permute-start | bytes 995336 | tf_op jit(solution)/shard_map/ppermute | solution.py:86
  70.7 13.9 %collective-permute-start.6 = (bf16[64,1152]{1,0:T(8,128)(2,1)S(1)}, bf16[64,1152]{1,0:T(8,128)(2,1)S(1)}, u32[]{:S(2)}, u32[]{:S(2)}) collective-permute-start(bf16[64,1152]{1,0:T(8,128)(2,1)S(1)} %get-tuple-element.46), channel_id=1, source_target_pairs={{0,3},{1,0},{2,1},{3,2},{4,7},{5,4},{6,5},{7,6},{8,11},{9,8},{10,9... | collective-permute-start | bytes 442376 | tf_op jit(solution)/shard_map/ppermute | solution.py:205
  71.1 13.5 %collective-permute-start.7 = (bf16[64,1152]{1,0:T(8,128)(2,1)S(1)}, bf16[64,1152]{1,0:T(8,128)(2,1)S(1)}, u32[]{:S(2)}, u32[]{:S(2)}) collective-permute-start(bf16[64,1152]{1,0:T(8,128)(2,1)S(1)} %get-tuple-element.49), channel_id=1, source_target_pairs={{0,1},{1,2},{2,3},{3,0},{4,5},{5,6},{6,7},{7,4},{8,9},{9,10},{10,1... | collective-permute-start | bytes 442376 | tf_op jit(solution)/shard_map/ppermute | solution.py:205
  71.3 13.3 %collective-permute-start.8 = (bf16[64,1152]{1,0:T(8,128)(2,1)S(1)}, bf16[64,1152]{1,0:T(8,128)(2,1)S(1)}, u32[]{:S(2)}, u32[]{:S(2)}) collective-permute-start(bf16[64,1152]{1,0:T(8,128)(2,1)S(1)} %get-tuple-element.48), channel_id=1, source_target_pairs={{0,2},{1,3},{2,0},{3,1},{4,6},{5,7},{6,4},{7,5},{8,10},{9,11},{10,... | collective-permute-start | bytes 442376 | tf_op jit(solution)/shard_map/ppermute | solution.py:205
  72.9 11.7 %collective-permute-start.9 = (bf16[64,1152]{1,0:T(8,128)(2,1)S(1)}, bf16[64,1152]{1,0:T(8,128)(2,1)S(1)}, u32[]{:S(2)}, u32[]{:S(2)}) collective-permute-start(bf16[64,1152]{1,0:T(8,128)(2,1)S(1)} %get-tuple-element.47), channel_id=1, source_target_pairs={{0,2},{1,3},{2,0},{3,1},{4,6},{5,7},{6,4},{7,5},{8,10},{9,11},{10,... | collective-permute-start | bytes 442376 | tf_op jit(solution)/shard_map/ppermute | solution.py:205
  74.3 10.4 %copy-start.1 = (bf16[512,1152]{1,0:T(8,128)(2,1)S(1)}, bf16[512,1152]{1,0:T(8,128)(2,1)}, u32[]{:S(2)}) copy-start(bf16[512,1152]{1,0:T(8,128)(2,1)} %shard_map.190) | copy-start | bytes 3538948
  74.3 10.4 %copy-start.17 = (pred[512]{0:T(512)(128)(4,1)S(1)}, pred[512]{0:T(512)(128)(4,1)}, u32[]{:S(2)}) copy-start(pred[512]{0:T(512)(128)(4,1)} %constant.138) | copy-start | bytes 1540
  85.4 5.8 %copy-start.5 = (s32[4,48]{1,0:T(4,128)S(1)}, s32[4,48]{1,0:T(4,128)}, u32[]{:S(2)}) copy-start(s32[4,48]{1,0:T(4,128)} %constant.141) | copy-start | bytes 2308
  85.4 6.2 %copy-start.12 = (pred[384,1]{0,1:T(4,128)(4,1)S(1)}, pred[384,1]{0,1:T(4,128)(4,1)}, u32[]{:S(2)}) copy-start(pred[384,1]{0,1:T(4,128)(4,1)} %constant.134.clone) | copy-start | bytes 1156
  85.6 19.0 %collective-permute-start.10 = (bf16[256,1152]{1,0:T(8,128)(2,1)S(1)}, bf16[256,1152]{1,0:T(8,128)(2,1)S(1)}, u32[]{:S(2)}, u32[]{:S(2)}) collective-permute-start(bf16[256,1152]{1,0:T(8,128)(2,1)S(1)} %get-tuple-element.27), channel_id=1, source_target_pairs={{0,4},{4,8},{8,12},{1,5},{5,9},{9,13},{2,6},{6,10},{10,14},{3,7},{... | collective-permute-start | bytes 1769480 | tf_op jit(solution)/shard_map/ppermute | solution.py:235
  89.2 17.9 %collective-permute-start.11 = (bf16[256,1152]{1,0:T(8,128)(2,1)S(1)}, bf16[256,1152]{1,0:T(8,128)(2,1)S(1)}, u32[]{:S(2)}, u32[]{:S(2)}) collective-permute-start(bf16[256,1152]{1,0:T(8,128)(2,1)S(1)} %get-tuple-element.22), channel_id=1, source_target_pairs={{4,0},{8,4},{12,8},{5,1},{9,5},{13,9},{6,2},{10,6},{14,10},{7,3},{... | collective-permute-start | bytes 1769480 | tf_op jit(solution)/shard_map/ppermute | solution.py:236
  94.2 10.3 %copy-start.2 = (bf16[192,1152]{1,0:T(8,128)(2,1)S(1)}, bf16[192,1152]{1,0:T(8,128)(2,1)}, u32[]{:S(2)}) copy-start(bf16[192,1152]{1,0:T(8,128)(2,1)} %shard_map.191) | copy-start | bytes 1327108
  108.6 10.3 %copy-start.16 = (pred[384]{0:T(512)(128)(4,1)S(1)}, pred[384]{0:T(512)(128)(4,1)}, u32[]{:S(2)}) copy-start(pred[384]{0:T(512)(128)(4,1)} %constant.140) | copy-start | bytes 1156
  108.6 3.3 %collective-permute-start.12 = (bf16[48,1152]{1,0:T(8,128)(2,1)S(1)}, bf16[48,1152]{1,0:T(8,128)(2,1)S(1)}, u32[]{:S(2)}, u32[]{:S(2)}) collective-permute-start(bf16[48,1152]{1,0:T(8,128)(2,1)S(1)} %get-tuple-element.50), channel_id=1, source_target_pairs={{0,3},{1,0},{2,1},{3,2},{4,7},{5,4},{6,5},{7,6},{8,11},{9,8},{10,9... | collective-permute-start | bytes 331784 | tf_op jit(solution)/shard_map/ppermute | solution.py:205
  108.7 5.4 %collective-permute-start.13 = (bf16[48,1152]{1,0:T(8,128)(2,1)S(1)}, bf16[48,1152]{1,0:T(8,128)(2,1)S(1)}, u32[]{:S(2)}, u32[]{:S(2)}) collective-permute-start(bf16[48,1152]{1,0:T(8,128)(2,1)S(1)} %get-tuple-element.53), channel_id=1, source_target_pairs={{0,1},{1,2},{2,3},{3,0},{4,5},{5,6},{6,7},{7,4},{8,9},{9,10},{10,1... | collective-permute-start | bytes 331784 | tf_op jit(solution)/shard_map/ppermute | solution.py:205
  109.2 7.3 %collective-permute-start.14 = (bf16[48,1152]{1,0:T(8,128)(2,1)S(1)}, bf16[48,1152]{1,0:T(8,128)(2,1)S(1)}, u32[]{:S(2)}, u32[]{:S(2)}) collective-permute-start(bf16[48,1152]{1,0:T(8,128)(2,1)S(1)} %get-tuple-element.52), channel_id=1, source_target_pairs={{0,2},{1,3},{2,0},{3,1},{4,6},{5,7},{6,4},{7,5},{8,10},{9,11},{10,... | collective-permute-start | bytes 331784 | tf_op jit(solution)/shard_map/ppermute | solution.py:205
  110.2 8.6 %collective-permute-start.15 = (bf16[48,1152]{1,0:T(8,128)(2,1)S(1)}, bf16[48,1152]{1,0:T(8,128)(2,1)S(1)}, u32[]{:S(2)}, u32[]{:S(2)}) collective-permute-start(bf16[48,1152]{1,0:T(8,128)(2,1)S(1)} %get-tuple-element.51), channel_id=1, source_target_pairs={{0,2},{1,3},{2,0},{3,1},{4,6},{5,7},{6,4},{7,5},{8,10},{9,11},{10,... | collective-permute-start | bytes 331784 | tf_op jit(solution)/shard_map/ppermute | solution.py:205

commit v8 on v7

--- a/solution.py
+++ b/solution.py
@@ -128,13 +128,14 @@
     n = lax.axis_size("face")
     rows = w_qkv.shape[0]
     moved = modulate(block_in, modulation)
-    qkv_pieces = face_pieces(w_qkv)
-    w_out_late, _ = lax.optimization_barrier((w_out, [piece for piece, _ in qkv_pieces]))
-    if n <= 4:
+    if n == 4:
         me = lax.axis_index("face")
         core = me % 2
-        chips = n // 2
-        moved_chips = moved.reshape(tokens, chips, 2 * rows).transpose(1, 0, 2)
+
+        def fetch(x, src_of):
+            return lax.ppermute(x, "face", [(src_of(i), i) for i in range(n)])
+
+        moved_chips = moved.reshape(tokens, 2, 2 * rows).transpose(1, 0, 2)
 
         def chip_weight(same_core, other_core):
             stack = jnp.zeros((2,) + w_qkv.shape, w_qkv.dtype)
@@ -142,16 +143,23 @@
             stack = lax.dynamic_update_index_in_dim(stack, other_core, 1 - core, 0)
             return stack.reshape(2 * rows, w_qkv.shape[1])
 
-        qkv_sums = None
-        for j in range(chips):
-            weight = chip_weight(qkv_pieces[2 * j][0], qkv_pieces[2 * j + 1][0])
-            part = jnp.dot(
-                lax.dynamic_index_in_dim(moved_chips, (me // 2 + j) % chips, 0, keepdims=False),
+        def chip_part(chip, weight):
+            return jnp.dot(
+                lax.dynamic_index_in_dim(moved_chips, chip, 0, keepdims=False),
                 weight,
                 preferred_element_type=jnp.float32,
             )
-            qkv_sums = part if qkv_sums is None else qkv_sums + part
+
+        sib = fetch(w_qkv, lambda i: i ^ 1)
+        far = fetch(w_qkv, lambda i: (i + 2) % n)
+        local = chip_part(me // 2, chip_weight(w_qkv, sib))
+        local, far = lax.optimization_barrier((local, far))
+        fwd = fetch(far, lambda i: i ^ 1)
+        qkv_sums = local + chip_part(1 - me // 2, chip_weight(far, fwd))
+        w_out_late, _ = lax.optimization_barrier((w_out, (far, fwd)))
     else:
+        qkv_pieces = face_pieces(w_qkv)
+        w_out_late, _ = lax.optimization_barrier((w_out, [piece for piece, _ in qkv_pieces]))
         qkv_stack = jnp.zeros((n,) + w_qkv.shape, w_qkv.dtype)
         for piece, index in qkv_pieces:
             qkv_stack = lax.dynamic_update_index_in_dim(qkv_stack, piece, index, 0)

time: 122 us -> 120 us (0.984)
  waiting for transfers between devices: 18.4 us -> 9.99 us
  local copies, waits for them, and re-layouts: 25.3 us -> 28.5 us
  other arithmetic: 13.8 us -> 15.9 us
  matrix products: 9.67 us -> 10.9 us
    ppermute x6, waiting for transfers between devices: 8.96 us -> 0.67 us  [fetch(): return lax.ppermute(x, 'face', [(src_of(i), i) for i in range(n)])]
    convert_element_type x1, other arithmetic: 0.78 us -> 2.14 us  [modulate(): return (normed * (1.0 + modulation[1]) + modulation[0]).astype(jnp.bfloat16)]
    another operation x2, local copies, waits for them, and re-layouts: 0.27 us -> 1.57 us
    unnamed x40 -> x42, local copies, waits for them, and re-layouts: 6.59 us -> 6.74 us
  transfers between devices with their start and end apart: 16 -> 16, of which waited for: 5 -> 5; matrix products, arithmetic and copies ran while one was open for 33% -> 39% of each run, Pallas kernels for 17% -> 17%
where the time goes in v8:
time: 120 us; the launch traced here: 119 us
  Pallas kernels  37.8 us (31%)
  local copies, waits for them, and re-layouts  28.5 us (24%)
  other arithmetic  15.9 us (13%)
  starting transfers between devices  15.5 us (13%)
  matrix products  10.9 us (9%)
  waiting for transfers between devices  9.99 us (8%)
    pallas_call x3, Pallas kernels, attend_project(): pl.pallas_call(attention_kernel, grid=(1, heads), in_specs=[pl.BlockSpec(...  37.8 us
    dot_general x2, matrix products, chip_part(): jnp.dot(lax.dynamic_index_in_dim(moved_chips, chip, 0, keepdims=False), w...  7.33 us
    ppermute x8, waiting for transfers between devices, strips_in(): lax.ppermute(sent, 'face', [(i, (i + shift) % n) for i in range(n)])  6.89 us
    unnamed x42, local copies, waits for them, and re-layouts  6.74 us
    ppermute x6, starting transfers between devices, fetch(): return lax.ppermute(x, 'face', [(src_of(i), i) for i in range(n)])  5.4 us
    ppermute x8, starting transfers between devices, strips_in(): lax.ppermute(sent, 'face', [(i, (i + shift) % n) for i in range(n)])  5.2 us
    select_n x2, other arithmetic, space_blend(): w_keep = jnp.where(dep == 0, keep[0], keep[1])  5.14 us
    ppermute x1, starting transfers between devices, per_device(): lower = lax.ppermute(high, 'tm', [(i, i + 1) for i in range(count - 1)])  3.64 us
  transfers between devices with their start and end apart: 16, of which 5 were waited for; matrix products, arithmetic and copies ran while one was open for 39% of the time, Pallas kernels for 17%

profile of v8, /device:TPU:0, one launch (start us, length us, event | category | flops | bytes accessed | tf_op | source)
XLA Modules:
  0.0 119.1 jit_solution(10412441025971286368)
XLA Ops:
  0.5 2.6 %collective-permute-start.1 = (bf16[288,1728]{1,0:T(8,128)(2,1)}, bf16[288,1728]{1,0:T(8,128)(2,1)}, u32[]{:S(2)}, u32[]{:S(2)}) collective-permute-start(bf16[288,1728]{1,0:T(8,128)(2,1)} %param.22), channel_id=1, source_target_pairs={{2,0},{3,1},{0,2},{1,3},{6,4},{7,5},{4,6},{5,7},{10,8},{11,9},{8,1... | collective-permute-start | bytes 2985992 | tf_op jit(solution)/shard_map/ppermute | solution.py:136
  3.0 2.9 %copy.34 = bf16[1,1,896,1152]{2,3,1,0:T(8,128)(2,1)S(1)} copy(bf16[1,1,896,1152]{3,2,1,0:T(8,128)(2,1)} %param.20) | data formatting | bytes 4128768 | tf_op args[0]
  5.9 1.3 %slice_bitcast_fusion.2 = (bf16[256,1152]{1,0:T(8,128)(2,1)S(1)}, bf16[256,1152]{1,0:T(8,128)(2,1)S(1)}) fusion(bf16[1,1,896,1152]{3,2,1,0:T(8,128)(2,1)} %param.20), kind=kLoop, calls=%fused_computation.42 | loop fusion | bytes 2359296 | tf_op jit(solution)/shard_map/slice | solution.py:233
  8.1 0.6 fusion.1
  8.7 0.6 add_reduce_fusion
  9.4 1.1 pad_maximum_fusion.x_ref
  10.5 0.7 fusion.40
  11.4 2.6 %broadcast_select_fusion.1 = (f32[512,1]{0,1:T(1,128)S(1)}, f32[512,1]{0,1:T(1,128)S(1)}) fusion(pred[512,1]{0,1:T(4,128)(4,1)S(1)} %copy-done.12, f32[]{:T(128)} %bitcast.14, f32[]{:T(128)} %bitcast.13, f32[]{:T(128)} %bitcast.30, f32[]{:T(128)} %bitcast.29), kind=kLoop, calls=%fused_computation.86 | loop fusion | flops 1024 | bytes 4624 | tf_op jit(solution)/shard_map/jit(_where)/select_n | solution.py:227
  14.2 2.1 %add_convert_fusion.1 = bf16[896,2,576]{0,2,1:T(8,128)(2,1)} fusion(f32[2,576]{1,0:T(2,128)S(1)} %add.109, f32[2,576]{1,0:T(2,128)S(1)} %mul.117, f32[896]{0:T(1024)S(1)} %add_rsqrt_fusion, f32[896]{0:T(1024)S(1)} %broadcast_multiply_fusion, bf16[896,2,576]{0,2,1:T(8,128)(2,1)S(1)} %bitcast.69), kind=kLoop, calls=%fused_computation.4 | loop fusion | flops 6193152 | bytes 4145152 | tf_op jit(solution)/shard_map/convert_element_type | solution.py:30
  16.3 1.4 %broadcast.89.clone = bf16[2,288,1728]{2,1,0:T(8,128)(2,1)} broadcast(bf16[]{:T(256)} %constant.115.clone.1), dimensions={} | broadcast | bytes 1990658 | tf_op jit(solution)/shard_map/broadcast.4
  17.9 1.0 bitcast_dynamic-update-slice_fusion.3
  19.4 2.2 %bitcast_dynamic-update-slice_fusion.2 = bf16[2,288,1728]{2,1,0:T(8,128)(2,1)} fusion(bf16[2,288,1728]{2,1,0:T(8,128)(2,1)} %bitcast_dynamic-update-slice_fusion.3, s32[]{:T(128)S(6)} %select_n.118, bf16[288,1728]{1,0:T(8,128)(2,1)} %collective-permute-done), kind=kLoop, calls=%fused_computation.34 | loop fusion | bytes 2064388 | tf_op jit(solution)/shard_map/jit(dynamic_update_index_in_dim)/dynamic_update_slice | solution.py:143
  21.6 4.5 %fusion.14 = f32[896,1728]{0,1:T(8,128)S(1)} fusion(bf16[576,1728]{1,0:T(8,128)(2,1)} %bitcast.5, bf16[896,2,576]{0,2,1:T(8,128)(2,1)S(1)} %copy-done.2, s32[]{:T(128)S(6)} %select_n.115), kind=kOutput, calls=%fused_computation.36 | convolution fusion | flops 1783627776 | bytes 9216004 | tf_op jit(solution)/shard_map/dot_general | solution.py:147
  26.1 0.7 collective-permute-done.1
  26.7 2.1 %slice_bitcast_fusion.3 = (bf16[192,1152]{1,0:T(8,128)(2,1)}, bf16[192,1152]{1,0:T(8,128)(2,1)}) fusion(bf16[1,1,896,1152]{3,2,1,0:T(8,128)(2,1)} %param.20), kind=kLoop, calls=%fused_computation.52 | loop fusion | bytes 1769472 | tf_op jit(solution)/shard_map/slice | solution.py:248
  29.0 1.3 %bitcast_dynamic-update-slice_fusion.1 = bf16[2,288,1728]{2,1,0:T(8,128)(2,1)S(1)} fusion(bf16[2,288,1728]{2,1,0:T(8,128)(2,1)S(1)} %broadcast.89, s32[]{:T(128)S(6)} %select_n.117, bf16[288,1728]{1,0:T(8,128)(2,1)} %collective-permute-done.1), kind=kLoop, calls=%fused_computation.31 | loop fusion | bytes 2027524 | tf_op jit(solution)/shard_map/jit(dynamic_update_index_in_dim)/dynamic_update_slice | solution.py:142
  30.3 0.6 collective-permute-start.3
  30.9 1.7 %collective-permute-start.4 = (bf16[576,288]{0,1:T(8,128)(2,1)}, bf16[576,288]{0,1:T(8,128)(2,1)}, u32[]{:S(2)}, u32[]{:S(2)}) collective-permute-start(bf16[576,288]{0,1:T(8,128)(2,1)} %param.23), channel_id=1, source_target_pairs={{2,0},{3,1},{0,2},{1,3},{6,4},{7,5},{4,6},{5,7},{10,8},{11,9},{8,1... | collective-permute-start | bytes 995336 | tf_op jit(solution)/shard_map/ppermute | solution.py:86
  32.7 2.9 %fusion.12 = f32[896,1728]{0,1:T(8,128)S(1)} fusion(bf16[576,1728]{1,0:T(8,128)(2,1)S(1)} %bitcast.77, bf16[896,2,576]{0,2,1:T(8,128)(2,1)S(1)} %copy-done.2, s32[]{:T(128)S(6)} %select_n.119), kind=kOutput, calls=%fused_computation.32 | convolution fusion | flops 1783627776 | bytes 9289732 | tf_op jit(solution)/shard_map/dot_general | solution.py:147
  35.6 0.8 add_convert_fusion
  36.4 1.6 %fusion.34 = (bf16[896,1,8,72]{0,3,2,1:T(8,128)(2,1)S(1)}, bf16[896,1,8,72]{0,3,2,1:T(8,128)(2,1)}, bf16[8,72,896]{2,1,0:T(8,128)(2,1)}) fusion(bf16[896,3,8,72]{0,3,2,1:T(8,128)(2,1)S(1)} %bitcast.73), kind=kLoop, calls=%fused_computation.94 | loop fusion | bytes 6193152 | tf_op jit(solution)/shard_map/slice | solution.py:178
  38.0 1.9 %copy.40 = bf16[896,1,8,72]{3,0,2,1:T(8,128)(2,1)S(1)} copy(bf16[896,1,8,72]{0,3,2,1:T(8,128)(2,1)} %get-tuple-element.38) | data formatting | bytes 2064384
  40.0 0.9 fusion.36
  40.8 1.7 %copy.41 = bf16[896,1,8,72]{3,0,2,1:T(8,128)(2,1)} copy(bf16[896,1,8,72]{0,3,2,1:T(8,128)(2,1)S(1)} %get-tuple-element.37) | data formatting | bytes 2064384
  42.5 2.2 %pad_maximum_fusion.1.q_ref = bf16[8,512,72]{2,1,0:T(8,128)(2,1)} fusion(bf16[8,256,72]{2,1,0:T(8,128)(2,1)} %get-tuple-element.47, bf16[8,256,72]{2,1,0:T(8,128)(2,1)S(1)} %get-tuple-element.46), kind=kLoop, calls=%fused_computation.28 | loop fusion | flops 1179648 | bytes 1179648 | tf_op jit(solution)/shard_map/concatenate | solution.py:232
  44.9 1.0 bitcast_dynamic-update-slice_fusion.7
  46.0 1.0 bitcast_dynamic-update-slice_fusion.6
  47.0 1.0 bitcast_dynamic-update-slice_fusion.5
  48.2 1.8 %copy.37.w_ref = bf16[576,1152]{1,0:T(8,128)(2,1)} copy(bf16[576,1152]{0,1:T(8,128)(2,1)S(1)} %bitcast.76) | data formatting | bytes 2654208 | tf_op jit(solution)/shard_map/reshape | solution.py:173
  49.9 17.2 %shard_map.190 = bf16[512,1152]{1,0:T(8,128)(2,1)} custom-call(bf16[8,512,72]{2,1,0:T(8,128)(2,1)} %pad_maximum_fusion.1.q_ref, bf16[8,72,896]{2,1,0:T(8,128)(2,1)} %get-tuple-element.39.k_ref, bf16[8,896,72]{2,1,0:T(8,128)(2,1)} %bitcast.70, bf16[576,1152]{1,0:T(8,128)(2,1)} %copy.37.w_ref, bf16[512,1152]{1,0:T(8,128)(2,1)} %pad_maximum_fusion.x_ref, ...), custom_call_target="tpu_custom_call" | custom-call | tf_op jit(solution)/shard_map/pallas_call | solution.py:63
  67.2 1.8 %convolution_convert_fusion = bf16[256,1152]{1,0:T(8,128)(2,1)S(1)} fusion(bf16[512,1152]{1,0:T(8,128)(2,1)} %shard_map.190, s32[256]{0:T(256)S(1)} %eq.108), kind=kOutput, calls=%fused_computation.14 | convolution fusion | flops 302415872 | bytes 1770496 | tf_op jit(solution)/shard_map/dot_general | solution.py:204
  69.6 1.6 %collective-permute-start.8 = (bf16[64,1152]{1,0:T(8,128)(2,1)S(1)}, bf16[64,1152]{1,0:T(8,128)(2,1)S(1)}, u32[]{:S(2)}, u32[]{:S(2)}) collective-permute-start(bf16[64,1152]{1,0:T(8,128)(2,1)S(1)} %get-tuple-element.52), channel_id=1, source_target_pairs={{0,2},{1,3},{2,0},{3,1},{4,6},{5,7},{6,4},{7,5},{8,10},{9,11},{10,... | collective-permute-start | bytes 442376 | tf_op jit(solution)/shard_map/ppermute | solution.py:213
  71.7 0.9 fusion.35
  72.6 10.3 %shard_map.191 = bf16[192,1152]{1,0:T(8,128)(2,1)} custom-call(bf16[8,192,72]{2,1,0:T(8,128)(2,1)} %get-tuple-element.22.q_ref, bf16[8,72,896]{2,1,0:T(8,128)(2,1)} %get-tuple-element.39.k_ref, bf16[8,896,72]{2,1,0:T(8,128)(2,1)} %bitcast.71, bf16[576,1152]{1,0:T(8,128)(2,1)} %copy.37.w_ref, bf16[192,1152]{1,0:T(8,128)(2,1)} %get-tuple-element.41.x_ref, ...), custom_call_target="tpu_custom_call" | custom-call | tf_op jit(solution)/shard_map/pallas_call | solution.py:63
  83.0 0.7 fusion.6
  83.9 3.6 %collective-permute-start.10 = (bf16[256,1152]{1,0:T(8,128)(2,1)S(1)}, bf16[256,1152]{1,0:T(8,128)(2,1)S(1)}, u32[]{:S(2)}, u32[]{:S(2)}) collective-permute-start(bf16[256,1152]{1,0:T(8,128)(2,1)S(1)} %get-tuple-element.31), channel_id=1, source_target_pairs={{0,4},{4,8},{8,12},{1,5},{5,9},{9,13},{2,6},{6,10},{10,14},{3,7},{... | collective-permute-start | bytes 1769480 | tf_op jit(solution)/shard_map/ppermute | solution.py:243
  87.5 1.3 %collective-permute-start.11 = (bf16[256,1152]{1,0:T(8,128)(2,1)S(1)}, bf16[256,1152]{1,0:T(8,128)(2,1)S(1)}, u32[]{:S(2)}, u32[]{:S(2)}) collective-permute-start(bf16[256,1152]{1,0:T(8,128)(2,1)S(1)} %get-tuple-element.26), channel_id=1, source_target_pairs={{4,0},{8,4},{12,8},{5,1},{9,5},{13,9},{6,2},{10,6},{14,10},{7,3},{... | collective-permute-start | bytes 1769480 | tf_op jit(solution)/shard_map/ppermute | solution.py:244
  90.0 2.6 %select_reduce_fusion.5 = (f32[384]{0:T(512)S(1)}, f32[384]{0:T(512)S(1)}) fusion(pred[384,1]{0,1:T(4,128)(4,1)S(1)} %copy-done.13, f32[]{:T(128)} %bitcast.14, f32[]{:T(128)} %bitcast.13, f32[]{:T(128)} %bitcast.30, f32[]{:T(128)} %bitcast.29), kind=kLoop, calls=%fused_computation.83 | loop fusion | flops 768 | bytes 3472 | tf_op jit(solution)/shard_map/jit(_where)/select_n | solution.py:227
  92.6 10.3 %shard_map.192 = bf16[192,1152]{1,0:T(8,128)(2,1)} custom-call(bf16[8,192,72]{2,1,0:T(8,128)(2,1)} %get-tuple-element.27.q_ref, bf16[8,72,896]{2,1,0:T(8,128)(2,1)} %get-tuple-element.39.k_ref, bf16[8,896,72]{2,1,0:T(8,128)(2,1)} %bitcast.72, bf16[576,1152]{1,0:T(8,128)(2,1)} %copy.37.w_ref, bf16[192,1152]{1,0:T(8,128)(2,1)} %get-tuple-element.40.x_ref, ...), custom_call_target="tpu_custom_call" | custom-call | tf_op jit(solution)/shard_map/pallas_call | solution.py:63
  102.9 2.4 %collective-permute-done.11 = bf16[256,1152]{1,0:T(8,128)(2,1)S(1)} collective-permute-done((bf16[256,1152]{1,0:T(8,128)(2,1)S(1)}, bf16[256,1152]{1,0:T(8,128)(2,1)S(1)}, u32[]{:S(2)}, u32[]{:S(2)}) %collective-permute-start.11) | collective-permute-done | bytes 589856 | tf_op jit(solution)/shard_map/ppermute | solution.py:244
  105.4 1.1 constant_dynamic-update-slice_fusion
  107.5 1.0 collective-permute-start.14
  108.5 1.0 collective-permute-start.15
  110.2 2.2 %collective-permute-done.13 = bf16[48,1152]{1,0:T(8,128)(2,1)S(1)} collective-permute-done((bf16[48,1152]{1,0:T(8,128)(2,1)S(1)}, bf16[48,1152]{1,0:T(8,128)(2,1)S(1)}, u32[]{:S(2)}, u32[]{:S(2)}) %collective-permute-start.13) | collective-permute-done | bytes 110624 | tf_op jit(solution)/shard_map/ppermute | solution.py:213
  112.4 2.3 %collective-permute-done.14 = bf16[48,1152]{1,0:T(8,128)(2,1)S(1)} collective-permute-done((bf16[48,1152]{1,0:T(8,128)(2,1)S(1)}, bf16[48,1152]{1,0:T(8,128)(2,1)S(1)}, u32[]{:S(2)}, u32[]{:S(2)}) %collective-permute-start.14) | collective-permute-done | bytes 110624 | tf_op jit(solution)/shard_map/ppermute | solution.py:213
  114.7 2.4 %collective-permute-done.15 = bf16[48,1152]{1,0:T(8,128)(2,1)S(1)} collective-permute-done((bf16[48,1152]{1,0:T(8,128)(2,1)S(1)}, bf16[48,1152]{1,0:T(8,128)(2,1)S(1)}, u32[]{:S(2)}, u32[]{:S(2)}) %collective-permute-start.15) | collective-permute-done | bytes 110624 | tf_op jit(solution)/shard_map/ppermute | solution.py:213
  117.1 0.5 fusion.7
  117.7 1.5 %maximum_bitcast_fusion = bf16[1,1,896,1152]{3,2,1,0:T(8,128)(2,1)} fusion(bf16[256,1152]{1,0:T(8,128)(2,1)S(1)} %fusion.11, bf16[384,1152]{1,0:T(8,128)(2,1)S(1)} %fusion.7, bf16[256,1152]{1,0:T(8,128)(2,1)S(1)} %fusion.9), kind=kLoop, calls=%fused_computation.17 | loop fusion | flops 6193152 | bytes 4128768 | tf_op jit(solution)/shard_map/reshape | solution.py:275
  (103 shorter events, 6.9 us)
Async XLA Ops:
  0.0 7.2 %copy-start = (s32[4,4,4]{2,1,0:T(4,128)S(1)}, s32[4,4,4]{2,1,0:T(4,128)}, u32[]{:S(2)}) copy-start(s32[4,4,4]{2,1,0:T(4,128)} %param.24) | copy-start | bytes 772
  0.0 19.4 %collective-permute-start = (bf16[288,1728]{1,0:T(8,128)(2,1)}, bf16[288,1728]{1,0:T(8,128)(2,1)}, u32[]{:S(2)}, u32[]{:S(2)}) collective-permute-start(bf16[288,1728]{1,0:T(8,128)(2,1)} %param.22), channel_id=1, source_target_pairs={{1,0},{0,1},{3,2},{2,3},{5,4},{4,5},{7,6},{6,7},{9,8},{8,9},{11,10... | collective-permute-start | bytes 2985992 | tf_op jit(solution)/shard_map/ppermute | solution.py:136
  0.5 26.3 %collective-permute-start.1 = (bf16[288,1728]{1,0:T(8,128)(2,1)}, bf16[288,1728]{1,0:T(8,128)(2,1)}, u32[]{:S(2)}, u32[]{:S(2)}) collective-permute-start(bf16[288,1728]{1,0:T(8,128)(2,1)} %param.22), channel_id=1, source_target_pairs={{2,0},{3,1},{0,2},{1,3},{6,4},{7,5},{4,6},{5,7},{10,8},{11,9},{8,1... | collective-permute-start | bytes 2985992 | tf_op jit(solution)/shard_map/ppermute | solution.py:136
  7.6 1.1 copy-start.5
  7.6 1.7 %copy-start.14 = (s32[2]{0:T(128)S(1)}, s32[2]{0:T(128)}, u32[]{:S(2)}) copy-start(s32[2]{0:T(128)} %param.25) | copy-start | bytes 28
  8.0 3.2 %copy-start.9 = (s32[4,64]{1,0:T(4,128)S(1)}, s32[4,64]{1,0:T(4,128)}, u32[]{:S(2)}) copy-start(s32[4,64]{1,0:T(4,128)} %constant.119.clone) | copy-start | bytes 3076
  8.0 3.2 %copy-start.10 = (s32[4,64]{1,0:T(4,128)S(1)}, s32[4,64]{1,0:T(4,128)}, u32[]{:S(2)}) copy-start(s32[4,64]{1,0:T(4,128)} %constant.120.clone) | copy-start | bytes 3076
  8.1 3.2 %copy-start.7 = (s32[4,48]{1,0:T(4,128)S(1)}, s32[4,48]{1,0:T(4,128)}, u32[]{:S(2)}) copy-start(s32[4,48]{1,0:T(4,128)} %constant.124.clone) | copy-start | bytes 2308
  8.1 3.2 %copy-start.8 = (s32[4,48]{1,0:T(4,128)S(1)}, s32[4,48]{1,0:T(4,128)}, u32[]{:S(2)}) copy-start(s32[4,48]{1,0:T(4,128)} %constant.125.clone) | copy-start | bytes 2308
  8.1 3.3 %copy-start.12 = (pred[512,1]{0,1:T(4,128)(4,1)S(1)}, pred[512,1]{0,1:T(4,128)(4,1)}, u32[]{:S(2)}) copy-start(pred[512,1]{0,1:T(4,128)(4,1)} %constant.122.clone) | copy-start | bytes 1540
  8.1 5.8 %copy-start.16 = (s32[4]{0:T(128)S(1)}, s32[4]{0:T(128)}, u32[]{:S(2)}) copy-start(s32[4]{0:T(128)} %constant.118.clone) | copy-start | bytes 52
  16.3 1.6 %copy-start.4 = (bf16[288,1728]{1,0:T(8,128)(2,1)S(1)}, bf16[288,1728]{1,0:T(8,128)(2,1)}, u32[]{:S(2)}) copy-start(bf16[288,1728]{1,0:T(8,128)(2,1)} %param.22) | copy-start | bytes 2985988
  16.3 2.6 %copy-start.11 = (s32[4,64]{1,0:T(4,128)S(1)}, s32[4,64]{1,0:T(4,128)}, u32[]{:S(2)}) copy-start(s32[4,64]{1,0:T(4,128)} %constant.132) | copy-start | bytes 3076
  16.3 3.0 %copy-start.15 = (s32[4]{0:T(128)S(1)}, s32[4]{0:T(128)}, u32[]{:S(2)}) copy-start(s32[4]{0:T(128)} %param.26) | copy-start | bytes 52
  17.9 3.7 %copy-start.2 = (bf16[896,2,576]{0,2,1:T(8,128)(2,1)S(1)}, bf16[896,2,576]{0,2,1:T(8,128)(2,1)}, u32[]{:S(2)}) copy-start(bf16[896,2,576]{0,2,1:T(8,128)(2,1)} %add_convert_fusion.1) | copy-start | bytes 6193156
  26.7 3.6 %collective-permute-start.2 = (bf16[288,1728]{1,0:T(8,128)(2,1)}, bf16[288,1728]{1,0:T(8,128)(2,1)S(1)}, u32[]{:S(2)}, u32[]{:S(2)}) collective-permute-start(bf16[288,1728]{1,0:T(8,128)(2,1)} %collective-permute-done.1), channel_id=1, source_target_pairs={{1,0},{0,1},{3,2},{2,3},{5,4},{4,5},{7,6},{6,7},{9,8},{8,9},{11,10... | collective-permute-start | bytes 2985992 | tf_op jit(solution)/shard_map/ppermute | solution.py:136
  30.3 15.7 %collective-permute-start.3 = (bf16[576,288]{0,1:T(8,128)(2,1)}, bf16[576,288]{0,1:T(8,128)(2,1)}, u32[]{:S(2)}, u32[]{:S(2)}) collective-permute-start(bf16[576,288]{0,1:T(8,128)(2,1)} %param.23), channel_id=1, source_target_pairs={{1,0},{0,1},{3,2},{2,3},{5,4},{4,5},{7,6},{6,7},{9,8},{8,9},{11,10... | collective-permute-start | bytes 995336 | tf_op jit(solution)/shard_map/ppermute | solution.py:86
  30.9 15.0 %collective-permute-start.4 = (bf16[576,288]{0,1:T(8,128)(2,1)}, bf16[576,288]{0,1:T(8,128)(2,1)}, u32[]{:S(2)}, u32[]{:S(2)}) collective-permute-start(bf16[576,288]{0,1:T(8,128)(2,1)} %param.23), channel_id=1, source_target_pairs={{2,0},{3,1},{0,2},{1,3},{6,4},{7,5},{4,6},{5,7},{10,8},{11,9},{8,1... | collective-permute-start | bytes 995336 | tf_op jit(solution)/shard_map/ppermute | solution.py:86
  45.9 2.2 %collective-permute-start.5 = (bf16[576,288]{0,1:T(8,128)(2,1)}, bf16[576,288]{0,1:T(8,128)(2,1)S(1)}, u32[]{:S(2)}, u32[]{:S(2)}) collective-permute-start(bf16[576,288]{0,1:T(8,128)(2,1)} %collective-permute-done.4), channel_id=1, source_target_pairs={{1,0},{0,1},{3,2},{2,3},{5,4},{4,5},{7,6},{6,7},{9,8},{8,9},{11,10... | collective-permute-start | bytes 995336 | tf_op jit(solution)/shard_map/ppermute | solution.py:86
  69.1 13.9 %collective-permute-start.6 = (bf16[64,1152]{1,0:T(8,128)(2,1)S(1)}, bf16[64,1152]{1,0:T(8,128)(2,1)S(1)}, u32[]{:S(2)}, u32[]{:S(2)}) collective-permute-start(bf16[64,1152]{1,0:T(8,128)(2,1)S(1)} %get-tuple-element.50), channel_id=1, source_target_pairs={{0,3},{1,0},{2,1},{3,2},{4,7},{5,4},{6,5},{7,6},{8,11},{9,8},{10,9... | collective-permute-start | bytes 442376 | tf_op jit(solution)/shard_map/ppermute | solution.py:213
  69.5 13.5 %collective-permute-start.7 = (bf16[64,1152]{1,0:T(8,128)(2,1)S(1)}, bf16[64,1152]{1,0:T(8,128)(2,1)S(1)}, u32[]{:S(2)}, u32[]{:S(2)}) collective-permute-start(bf16[64,1152]{1,0:T(8,128)(2,1)S(1)} %get-tuple-element.53), channel_id=1, source_target_pairs={{0,1},{1,2},{2,3},{3,0},{4,5},{5,6},{6,7},{7,4},{8,9},{9,10},{10,1... | collective-permute-start | bytes 442376 | tf_op jit(solution)/shard_map/ppermute | solution.py:213
  69.6 13.3 %collective-permute-start.8 = (bf16[64,1152]{1,0:T(8,128)(2,1)S(1)}, bf16[64,1152]{1,0:T(8,128)(2,1)S(1)}, u32[]{:S(2)}, u32[]{:S(2)}) collective-permute-start(bf16[64,1152]{1,0:T(8,128)(2,1)S(1)} %get-tuple-element.52), channel_id=1, source_target_pairs={{0,2},{1,3},{2,0},{3,1},{4,6},{5,7},{6,4},{7,5},{8,10},{9,11},{10,... | collective-permute-start | bytes 442376 | tf_op jit(solution)/shard_map/ppermute | solution.py:213
  71.2 11.7 %collective-permute-start.9 = (bf16[64,1152]{1,0:T(8,128)(2,1)S(1)}, bf16[64,1152]{1,0:T(8,128)(2,1)S(1)}, u32[]{:S(2)}, u32[]{:S(2)}) collective-permute-start(bf16[64,1152]{1,0:T(8,128)(2,1)S(1)} %get-tuple-element.51), channel_id=1, source_target_pairs={{0,2},{1,3},{2,0},{3,1},{4,6},{5,7},{6,4},{7,5},{8,10},{9,11},{10,... | collective-permute-start | bytes 442376 | tf_op jit(solution)/shard_map/ppermute | solution.py:213
  72.6 10.4 %copy-start.1 = (bf16[512,1152]{1,0:T(8,128)(2,1)S(1)}, bf16[512,1152]{1,0:T(8,128)(2,1)}, u32[]{:S(2)}) copy-start(bf16[512,1152]{1,0:T(8,128)(2,1)} %shard_map.190) | copy-start | bytes 3538948
  72.6 10.4 %copy-start.18 = (pred[512]{0:T(512)(128)(4,1)S(1)}, pred[512]{0:T(512)(128)(4,1)}, u32[]{:S(2)}) copy-start(pred[512]{0:T(512)(128)(4,1)} %constant.131) | copy-start | bytes 1540
  83.8 5.8 %copy-start.6 = (s32[4,48]{1,0:T(4,128)S(1)}, s32[4,48]{1,0:T(4,128)}, u32[]{:S(2)}) copy-start(s32[4,48]{1,0:T(4,128)} %constant.134) | copy-start | bytes 2308
  83.8 6.2 %copy-start.13 = (pred[384,1]{0,1:T(4,128)(4,1)S(1)}, pred[384,1]{0,1:T(4,128)(4,1)}, u32[]{:S(2)}) copy-start(pred[384,1]{0,1:T(4,128)(4,1)} %constant.127.clone) | copy-start | bytes 1156
  83.9 19.0 %collective-permute-start.10 = (bf16[256,1152]{1,0:T(8,128)(2,1)S(1)}, bf16[256,1152]{1,0:T(8,128)(2,1)S(1)}, u32[]{:S(2)}, u32[]{:S(2)}) collective-permute-start(bf16[256,1152]{1,0:T(8,128)(2,1)S(1)} %get-tuple-element.31), channel_id=1, source_target_pairs={{0,4},{4,8},{8,12},{1,5},{5,9},{9,13},{2,6},{6,10},{10,14},{3,7},{... | collective-permute-start | bytes 1769480 | tf_op jit(solution)/shard_map/ppermute | solution.py:243
  87.5 17.8 %collective-permute-start.11 = (bf16[256,1152]{1,0:T(8,128)(2,1)S(1)}, bf16[256,1152]{1,0:T(8,128)(2,1)S(1)}, u32[]{:S(2)}, u32[]{:S(2)}) collective-permute-start(bf16[256,1152]{1,0:T(8,128)(2,1)S(1)} %get-tuple-element.26), channel_id=1, source_target_pairs={{4,0},{8,4},{12,8},{5,1},{9,5},{13,9},{6,2},{10,6},{14,10},{7,3},{... | collective-permute-start | bytes 1769480 | tf_op jit(solution)/shard_map/ppermute | solution.py:244
  92.6 10.3 %copy-start.3 = (bf16[192,1152]{1,0:T(8,128)(2,1)S(1)}, bf16[192,1152]{1,0:T(8,128)(2,1)}, u32[]{:S(2)}) copy-start(bf16[192,1152]{1,0:T(8,128)(2,1)} %shard_map.191) | copy-start | bytes 1327108
  106.9 10.2 %copy-start.17 = (pred[384]{0:T(512)(128)(4,1)S(1)}, pred[384]{0:T(512)(128)(4,1)}, u32[]{:S(2)}) copy-start(pred[384]{0:T(512)(128)(4,1)} %constant.133) | copy-start | bytes 1156
  107.0 3.3 %collective-permute-start.12 = (bf16[48,1152]{1,0:T(8,128)(2,1)S(1)}, bf16[48,1152]{1,0:T(8,128)(2,1)S(1)}, u32[]{:S(2)}, u32[]{:S(2)}) collective-permute-start(bf16[48,1152]{1,0:T(8,128)(2,1)S(1)} %get-tuple-element.54), channel_id=1, source_target_pairs={{0,3},{1,0},{2,1},{3,2},{4,7},{5,4},{6,5},{7,6},{8,11},{9,8},{10,9... | collective-permute-start | bytes 331784 | tf_op jit(solution)/shard_map/ppermute | solution.py:213
  107.0 5.4 %collective-permute-start.13 = (bf16[48,1152]{1,0:T(8,128)(2,1)S(1)}, bf16[48,1152]{1,0:T(8,128)(2,1)S(1)}, u32[]{:S(2)}, u32[]{:S(2)}) collective-permute-start(bf16[48,1152]{1,0:T(8,128)(2,1)S(1)} %get-tuple-element.57), channel_id=1, source_target_pairs={{0,1},{1,2},{2,3},{3,0},{4,5},{5,6},{6,7},{7,4},{8,9},{9,10},{10,1... | collective-permute-start | bytes 331784 | tf_op jit(solution)/shard_map/ppermute | solution.py:213
  107.5 7.2 %collective-permute-start.14 = (bf16[48,1152]{1,0:T(8,128)(2,1)S(1)}, bf16[48,1152]{1,0:T(8,128)(2,1)S(1)}, u32[]{:S(2)}, u32[]{:S(2)}) collective-permute-start(bf16[48,1152]{1,0:T(8,128)(2,1)S(1)} %get-tuple-element.56), channel_id=1, source_target_pairs={{0,2},{1,3},{2,0},{3,1},{4,6},{5,7},{6,4},{7,5},{8,10},{9,11},{10,... | collective-permute-start | bytes 331784 | tf_op jit(solution)/shard_map/ppermute | solution.py:213
  108.5 8.6 %collective-permute-start.15 = (bf16[48,1152]{1,0:T(8,128)(2,1)S(1)}, bf16[48,1152]{1,0:T(8,128)(2,1)S(1)}, u32[]{:S(2)}, u32[]{:S(2)}) collective-permute-start(bf16[48,1152]{1,0:T(8,128)(2,1)S(1)} %get-tuple-element.55), channel_id=1, source_target_pairs={{0,2},{1,3},{2,0},{3,1},{4,6},{5,7},{6,4},{7,5},{8,10},{9,11},{10,... | collective-permute-start | bytes 331784 | tf_op jit(solution)/shard_map/ppermute | solution.py:213

commit v9 on v8

--- a/solution.py
+++ b/solution.py
@@ -30,26 +30,36 @@
     return (normed * (1.0 + modulation[1]) + modulation[0]).astype(jnp.bfloat16)
 
 
-def attention_kernel(q_ref, k_ref, v_ref, w_ref, x_ref, g_ref, o_ref, acc_ref):
-    head = pl.program_id(1)
-
-    @pl.when(head == 0)
+HEADS_PER_STEP = 2
+
+
+def attention_kernel(*refs):
+    x_ref, g_ref, o_ref, acc_ref = refs[-4:]
+    per_head = refs[:-4]
+    step = pl.program_id(1)
+
+    @pl.when(step == 0)
     def _():
         acc_ref[...] = jnp.zeros_like(acc_ref)
 
-    scores = jnp.dot(q_ref[0], k_ref[0], preferred_element_type=jnp.float32) * (
-        1.0 / math.sqrt(HD)
-    )
-    row_max = jnp.max(scores, axis=-1, keepdims=True)
-    weights = jnp.exp(scores - row_max)
-    row_sum = jnp.sum(weights, axis=-1, keepdims=True)
-    probabilities = (weights * (1.0 / row_sum)).astype(jnp.bfloat16)
-    mixed = jnp.dot(probabilities, v_ref[0], preferred_element_type=jnp.float32).astype(
-        jnp.bfloat16
-    )
-    acc_ref[...] += jnp.dot(mixed, w_ref[...], preferred_element_type=jnp.float32)
-
-    @pl.when(head == pl.num_programs(1) - 1)
+    total = None
+    for j in range(HEADS_PER_STEP):
+        q_ref, k_ref, v_ref, w_ref = per_head[4 * j : 4 * j + 4]
+        scores = jnp.dot(q_ref[0], k_ref[0], preferred_element_type=jnp.float32) * (
+            1.0 / math.sqrt(HD)
+        )
+        row_max = jnp.max(scores, axis=-1, keepdims=True)
+        weights = jnp.exp(scores - row_max)
+        row_sum = jnp.sum(weights, axis=-1, keepdims=True)
+        probabilities = (weights * (1.0 / row_sum)).astype(jnp.bfloat16)
+        mixed = jnp.dot(probabilities, v_ref[0], preferred_element_type=jnp.float32).astype(
+            jnp.bfloat16
+        )
+        part = jnp.dot(mixed, w_ref[...], preferred_element_type=jnp.float32)
+        total = part if total is None else total + part
+    acc_ref[...] += total
+
+    @pl.when(step == pl.num_programs(1) - 1)
     def _():
         o_ref[...] = (x_ref[...].astype(jnp.float32) + g_ref[...] * acc_ref[...]).astype(
             o_ref.dtype
@@ -60,22 +70,30 @@
     heads, size, tokens = keys.shape
     chunk = queries.shape[1]
     width = block_in.shape[1]
+    hb = HEADS_PER_STEP
+    in_specs = []
+    operands = []
+    for j in range(hb):
+        in_specs += [
+            pl.BlockSpec((1, chunk, size), lambda i, h, j=j: (hb * h + j, i, 0)),
+            pl.BlockSpec((1, size, tokens), lambda i, h, j=j: (hb * h + j, 0, 0)),
+            pl.BlockSpec((1, tokens, size), lambda i, h, j=j: (hb * h + j, 0, 0)),
+            pl.BlockSpec((size, width), lambda i, h, j=j: (hb * h + j, 0)),
+        ]
+        operands += [queries, keys, values, w_out_full]
+    in_specs += [
+        pl.BlockSpec((chunk, width), lambda i, h: (i, 0)),
+        pl.BlockSpec((1, width), lambda i, h: (0, 0)),
+    ]
     return pl.pallas_call(
         attention_kernel,
-        grid=(1, heads),
-        in_specs=[
-            pl.BlockSpec((1, chunk, size), lambda i, h: (h, i, 0)),
-            pl.BlockSpec((1, size, tokens), lambda i, h: (h, 0, 0)),
-            pl.BlockSpec((1, tokens, size), lambda i, h: (h, 0, 0)),
-            pl.BlockSpec((size, width), lambda i, h: (h, 0)),
-            pl.BlockSpec((chunk, width), lambda i, h: (i, 0)),
-            pl.BlockSpec((1, width), lambda i, h: (0, 0)),
-        ],
+        grid=(1, heads // hb),
+        in_specs=in_specs,
         out_specs=pl.BlockSpec((chunk, width), lambda i, h: (i, 0)),
         out_shape=jax.ShapeDtypeStruct(block_in.shape, block_in.dtype),
         scratch_shapes=[pltpu.VMEM((chunk, width), jnp.float32)],
         compiler_params=pltpu.CompilerParams(dimension_semantics=("arbitrary", "arbitrary")),
-    )(queries, keys, values, w_out_full, block_in, gate.reshape(1, width))
+    )(*operands, block_in, gate.reshape(1, width))
 
 
 def face_pieces(shard):

time: 120 us -> 118 us (0.983)
  Pallas kernels: 37.8 us -> 35.1 us
    pallas_call x3, Pallas kernels: 37.8 us -> 35.1 us  [attend_project(): pl.pallas_call(attention_kernel, grid=(1, heads // hb), in_specs=in_specs...]
  transfers between devices with their start and end apart: 16 -> 16, of which waited for: 5 -> 6; matrix products, arithmetic and copies ran while one was open for 39% -> 40% of each run, Pallas kernels for 17% -> 16%
where the time goes in v9:
time: 118 us; the launch traced here: 117 us
  Pallas kernels  35.1 us (30%)
  local copies, waits for them, and re-layouts  28.5 us (24%)
  other arithmetic  15.9 us (13%)
  starting transfers between devices  15.7 us (13%)
  matrix products  10.9 us (9%)
  waiting for transfers between devices  10.6 us (9%)
    pallas_call x3, Pallas kernels, attend_project(): pl.pallas_call(attention_kernel, grid=(1, heads // hb), in_specs=in_specs...  35.1 us
    dot_general x2, matrix products, chip_part(): jnp.dot(lax.dynamic_index_in_dim(moved_chips, chip, 0, keepdims=False), w...  7.33 us
    unnamed x42, local copies, waits for them, and re-layouts  6.74 us
    ppermute x8, waiting for transfers between devices, strips_in(): lax.ppermute(sent, 'face', [(i, (i + shift) % n) for i in range(n)])  6.63 us
    ppermute x6, starting transfers between devices, fetch(): return lax.ppermute(x, 'face', [(src_of(i), i) for i in range(n)])  5.4 us
    ppermute x8, starting transfers between devices, strips_in(): lax.ppermute(sent, 'face', [(i, (i + shift) % n) for i in range(n)])  5.21 us
    select_n x2, other arithmetic, space_blend(): w_keep = jnp.where(dep == 0, keep[0], keep[1])  5.14 us
    ppermute x1, starting transfers between devices, per_device(): lower = lax.ppermute(high, 'tm', [(i, i + 1) for i in range(count - 1)])  3.78 us
  transfers between devices with their start and end apart: 16, of which 6 were waited for; matrix products, arithmetic and copies ran while one was open for 40% of the time, Pallas kernels for 16%

profile of v9, /device:TPU:0, one launch (start us, length us, event | category | flops | bytes accessed | tf_op | source)
XLA Modules:
  0.0 117.2 jit_solution(12639852250715967056)
XLA Ops:
  0.5 2.6 %collective-permute-start.1 = (bf16[288,1728]{1,0:T(8,128)(2,1)}, bf16[288,1728]{1,0:T(8,128)(2,1)}, u32[]{:S(2)}, u32[]{:S(2)}) collective-permute-start(bf16[288,1728]{1,0:T(8,128)(2,1)} %param.22), channel_id=1, source_target_pairs={{2,0},{3,1},{0,2},{1,3},{6,4},{7,5},{4,6},{5,7},{10,8},{11,9},{8,1... | collective-permute-start | bytes 2985992 | tf_op jit(solution)/shard_map/ppermute | solution.py:154
  3.0 2.9 %copy.40 = bf16[1,1,896,1152]{2,3,1,0:T(8,128)(2,1)S(1)} copy(bf16[1,1,896,1152]{3,2,1,0:T(8,128)(2,1)} %param.20) | data formatting | bytes 4128768 | tf_op args[0]
  5.9 1.3 %slice_bitcast_fusion.2 = (bf16[256,1152]{1,0:T(8,128)(2,1)S(1)}, bf16[256,1152]{1,0:T(8,128)(2,1)S(1)}) fusion(bf16[1,1,896,1152]{3,2,1,0:T(8,128)(2,1)} %param.20), kind=kLoop, calls=%fused_computation.42 | loop fusion | bytes 2359296 | tf_op jit(solution)/shard_map/slice | solution.py:251
  8.1 0.6 fusion.1
  8.7 0.6 add_reduce_fusion
  9.4 1.1 pad_maximum_fusion.refs_8_
  10.5 0.7 fusion.40
  11.4 2.6 %broadcast_select_fusion.1 = (f32[512,1]{0,1:T(1,128)S(1)}, f32[512,1]{0,1:T(1,128)S(1)}) fusion(pred[512,1]{0,1:T(4,128)(4,1)S(1)} %copy-done.12, f32[]{:T(128)} %bitcast.14, f32[]{:T(128)} %bitcast.13, f32[]{:T(128)} %bitcast.31, f32[]{:T(128)} %bitcast.30), kind=kLoop, calls=%fused_computation.86 | loop fusion | flops 1024 | bytes 4624 | tf_op jit(solution)/shard_map/jit(_where)/select_n | solution.py:245
  14.2 2.1 %add_convert_fusion.1 = bf16[896,2,576]{0,2,1:T(8,128)(2,1)} fusion(f32[2,576]{1,0:T(2,128)S(1)} %add.109, f32[2,576]{1,0:T(2,128)S(1)} %mul.117, f32[896]{0:T(1024)S(1)} %add_rsqrt_fusion, f32[896]{0:T(1024)S(1)} %broadcast_multiply_fusion, bf16[896,2,576]{0,2,1:T(8,128)(2,1)S(1)} %bitcast.75), kind=kLoop, calls=%fused_computation.4 | loop fusion | flops 6193152 | bytes 4145152 | tf_op jit(solution)/shard_map/convert_element_type | solution.py:30
  16.3 1.4 %broadcast.89.clone = bf16[2,288,1728]{2,1,0:T(8,128)(2,1)} broadcast(bf16[]{:T(256)} %constant.115.clone.1), dimensions={} | broadcast | bytes 1990658 | tf_op jit(solution)/shard_map/broadcast.4
  17.9 1.0 bitcast_dynamic-update-slice_fusion.3
  19.4 2.2 %bitcast_dynamic-update-slice_fusion.2 = bf16[2,288,1728]{2,1,0:T(8,128)(2,1)} fusion(bf16[2,288,1728]{2,1,0:T(8,128)(2,1)} %bitcast_dynamic-update-slice_fusion.3, s32[]{:T(128)S(6)} %select_n.118, bf16[288,1728]{1,0:T(8,128)(2,1)} %collective-permute-done), kind=kLoop, calls=%fused_computation.34 | loop fusion | bytes 2064388 | tf_op jit(solution)/shard_map/jit(dynamic_update_index_in_dim)/dynamic_update_slice | solution.py:161
  21.6 4.5 %fusion.14 = f32[896,1728]{0,1:T(8,128)S(1)} fusion(bf16[576,1728]{1,0:T(8,128)(2,1)} %bitcast.5, bf16[896,2,576]{0,2,1:T(8,128)(2,1)S(1)} %copy-done.2, s32[]{:T(128)S(6)} %select_n.115), kind=kOutput, calls=%fused_computation.36 | convolution fusion | flops 1783627776 | bytes 9216004 | tf_op jit(solution)/shard_map/dot_general | solution.py:165
  26.1 0.7 collective-permute-done.1
  26.7 2.1 %slice_bitcast_fusion.3 = (bf16[192,1152]{1,0:T(8,128)(2,1)}, bf16[192,1152]{1,0:T(8,128)(2,1)}) fusion(bf16[1,1,896,1152]{3,2,1,0:T(8,128)(2,1)} %param.20), kind=kLoop, calls=%fused_computation.52 | loop fusion | bytes 1769472 | tf_op jit(solution)/shard_map/slice | solution.py:266
  29.0 1.3 %bitcast_dynamic-update-slice_fusion.1 = bf16[2,288,1728]{2,1,0:T(8,128)(2,1)S(1)} fusion(bf16[2,288,1728]{2,1,0:T(8,128)(2,1)S(1)} %broadcast.89, s32[]{:T(128)S(6)} %select_n.117, bf16[288,1728]{1,0:T(8,128)(2,1)} %collective-permute-done.1), kind=kLoop, calls=%fused_computation.31 | loop fusion | bytes 2027524 | tf_op jit(solution)/shard_map/jit(dynamic_update_index_in_dim)/dynamic_update_slice | solution.py:160
  30.3 0.6 collective-permute-start.3
  30.9 1.7 %collective-permute-start.4 = (bf16[576,288]{0,1:T(8,128)(2,1)}, bf16[576,288]{0,1:T(8,128)(2,1)}, u32[]{:S(2)}, u32[]{:S(2)}) collective-permute-start(bf16[576,288]{0,1:T(8,128)(2,1)} %param.23), channel_id=1, source_target_pairs={{2,0},{3,1},{0,2},{1,3},{6,4},{7,5},{4,6},{5,7},{10,8},{11,9},{8,1... | collective-permute-start | bytes 995336 | tf_op jit(solution)/shard_map/ppermute | solution.py:104
  32.7 2.9 %fusion.12 = f32[896,1728]{0,1:T(8,128)S(1)} fusion(bf16[576,1728]{1,0:T(8,128)(2,1)S(1)} %bitcast.80, bf16[896,2,576]{0,2,1:T(8,128)(2,1)S(1)} %copy-done.2, s32[]{:T(128)S(6)} %select_n.119), kind=kOutput, calls=%fused_computation.32 | convolution fusion | flops 1783627776 | bytes 9289732 | tf_op jit(solution)/shard_map/dot_general | solution.py:165
  35.6 0.8 add_convert_fusion
  36.4 1.6 %fusion.34 = (bf16[896,1,8,72]{0,3,2,1:T(8,128)(2,1)S(1)}, bf16[896,1,8,72]{0,3,2,1:T(8,128)(2,1)}, bf16[8,72,896]{2,1,0:T(8,128)(2,1)}) fusion(bf16[896,3,8,72]{0,3,2,1:T(8,128)(2,1)S(1)} %bitcast.76), kind=kLoop, calls=%fused_computation.94 | loop fusion | bytes 6193152 | tf_op jit(solution)/shard_map/slice | solution.py:196
  38.0 1.9 %copy.49 = bf16[896,1,8,72]{3,0,2,1:T(8,128)(2,1)S(1)} copy(bf16[896,1,8,72]{0,3,2,1:T(8,128)(2,1)} %get-tuple-element.38) | data formatting | bytes 2064384
  40.0 0.9 fusion.36
  40.8 1.7 %copy.50 = bf16[896,1,8,72]{3,0,2,1:T(8,128)(2,1)} copy(bf16[896,1,8,72]{0,3,2,1:T(8,128)(2,1)S(1)} %get-tuple-element.37) | data formatting | bytes 2064384
  42.5 2.2 %pad_maximum_fusion.1.refs_0_.refs_4_ = bf16[8,512,72]{2,1,0:T(8,128)(2,1)} fusion(bf16[8,256,72]{2,1,0:T(8,128)(2,1)} %get-tuple-element.47, bf16[8,256,72]{2,1,0:T(8,128)(2,1)S(1)} %get-tuple-element.46), kind=kLoop, calls=%fused_computation.28 | loop fusion | flops 1179648 | bytes 1179648 | tf_op jit(solution)/shard_map/concatenate | solution.py:250
  44.9 1.0 bitcast_dynamic-update-slice_fusion.7
  46.0 1.0 bitcast_dynamic-update-slice_fusion.6
  47.0 1.0 bitcast_dynamic-update-slice_fusion.5
  48.2 1.8 %copy.43.refs_3_.refs_7_ = bf16[576,1152]{1,0:T(8,128)(2,1)} copy(bf16[576,1152]{0,1:T(8,128)(2,1)S(1)} %bitcast.79) | data formatting | bytes 2654208 | tf_op jit(solution)/shard_map/reshape | solution.py:191
  49.9 17.0 %shard_map.190 = bf16[512,1152]{1,0:T(8,128)(2,1)} custom-call(bf16[8,512,72]{2,1,0:T(8,128)(2,1)} %pad_maximum_fusion.1.refs_0_.refs_4_, bf16[8,72,896]{2,1,0:T(8,128)(2,1)} %get-tuple-element.39.refs_1_.refs_5_, bf16[8,896,72]{2,1,0:T(8,128)(2,1)} %bitcast.69, bf16[576,1152]{1,0:T(8,128)(2,1)} %copy.43.refs_3_.refs_7_, ...), custom_call_target="tpu_custom_call" | custom-call | tf_op jit(solution)/shard_map/pallas_call | solution.py:88
  66.9 1.8 %convolution_convert_fusion = bf16[256,1152]{1,0:T(8,128)(2,1)S(1)} fusion(bf16[512,1152]{1,0:T(8,128)(2,1)} %shard_map.190, s32[256]{0:T(256)S(1)} %eq.108), kind=kOutput, calls=%fused_computation.14 | convolution fusion | flops 302415872 | bytes 1770496 | tf_op jit(solution)/shard_map/dot_general | solution.py:222
  69.4 1.6 %collective-permute-start.8 = (bf16[64,1152]{1,0:T(8,128)(2,1)S(1)}, bf16[64,1152]{1,0:T(8,128)(2,1)S(1)}, u32[]{:S(2)}, u32[]{:S(2)}) collective-permute-start(bf16[64,1152]{1,0:T(8,128)(2,1)S(1)} %get-tuple-element.52), channel_id=1, source_target_pairs={{0,2},{1,3},{2,0},{3,1},{4,6},{5,7},{6,4},{7,5},{8,10},{9,11},{10,... | collective-permute-start | bytes 442376 | tf_op jit(solution)/shard_map/ppermute | solution.py:231
  71.4 0.9 fusion.35
  72.4 9.1 %shard_map.191 = bf16[192,1152]{1,0:T(8,128)(2,1)} custom-call(bf16[8,192,72]{2,1,0:T(8,128)(2,1)} %get-tuple-element.22.refs_0_.refs_4_, bf16[8,72,896]{2,1,0:T(8,128)(2,1)} %get-tuple-element.39.refs_1_.refs_5_, bf16[8,896,72]{2,1,0:T(8,128)(2,1)} %bitcast.71, bf16[576,1152]{1,0:T(8,128)(2,1)} %copy.43.refs_3_.refs_7_, ...), custom_call_target="tpu_custom_call" | custom-call | tf_op jit(solution)/shard_map/pallas_call | solution.py:88
  81.7 0.7 fusion.6
  82.6 3.8 %collective-permute-start.10 = (bf16[256,1152]{1,0:T(8,128)(2,1)S(1)}, bf16[256,1152]{1,0:T(8,128)(2,1)S(1)}, u32[]{:S(2)}, u32[]{:S(2)}) collective-permute-start(bf16[256,1152]{1,0:T(8,128)(2,1)S(1)} %get-tuple-element.31), channel_id=1, source_target_pairs={{0,4},{4,8},{8,12},{1,5},{5,9},{9,13},{2,6},{6,10},{10,14},{3,7},{... | collective-permute-start | bytes 1769480 | tf_op jit(solution)/shard_map/ppermute | solution.py:261
  86.4 1.3 %collective-permute-start.11 = (bf16[256,1152]{1,0:T(8,128)(2,1)S(1)}, bf16[256,1152]{1,0:T(8,128)(2,1)S(1)}, u32[]{:S(2)}, u32[]{:S(2)}) collective-permute-start(bf16[256,1152]{1,0:T(8,128)(2,1)S(1)} %get-tuple-element.26), channel_id=1, source_target_pairs={{4,0},{8,4},{12,8},{5,1},{9,5},{13,9},{6,2},{10,6},{14,10},{7,3},{... | collective-permute-start | bytes 1769480 | tf_op jit(solution)/shard_map/ppermute | solution.py:262
  88.9 2.6 %select_reduce_fusion.5 = (f32[384]{0:T(512)S(1)}, f32[384]{0:T(512)S(1)}) fusion(pred[384,1]{0,1:T(4,128)(4,1)S(1)} %copy-done.13, f32[]{:T(128)} %bitcast.14, f32[]{:T(128)} %bitcast.13, f32[]{:T(128)} %bitcast.31, f32[]{:T(128)} %bitcast.30), kind=kLoop, calls=%fused_computation.83 | loop fusion | flops 768 | bytes 3472 | tf_op jit(solution)/shard_map/jit(_where)/select_n | solution.py:245
  91.5 9.1 %shard_map.192 = bf16[192,1152]{1,0:T(8,128)(2,1)} custom-call(bf16[8,192,72]{2,1,0:T(8,128)(2,1)} %get-tuple-element.27.refs_0_.refs_4_, bf16[8,72,896]{2,1,0:T(8,128)(2,1)} %get-tuple-element.39.refs_1_.refs_5_, bf16[8,896,72]{2,1,0:T(8,128)(2,1)} %bitcast.73, bf16[576,1152]{1,0:T(8,128)(2,1)} %copy.43.refs_3_.refs_7_, ...), custom_call_target="tpu_custom_call" | custom-call | tf_op jit(solution)/shard_map/pallas_call | solution.py:88
  100.6 3.3 %collective-permute-done.11 = bf16[256,1152]{1,0:T(8,128)(2,1)S(1)} collective-permute-done((bf16[256,1152]{1,0:T(8,128)(2,1)S(1)}, bf16[256,1152]{1,0:T(8,128)(2,1)S(1)}, u32[]{:S(2)}, u32[]{:S(2)}) %collective-permute-start.11) | collective-permute-done | bytes 589856 | tf_op jit(solution)/shard_map/ppermute | solution.py:262
  103.9 1.1 constant_dynamic-update-slice_fusion
  106.1 0.8 collective-permute-start.14
  106.9 1.2 %collective-permute-start.15 = (bf16[48,1152]{1,0:T(8,128)(2,1)S(1)}, bf16[48,1152]{1,0:T(8,128)(2,1)S(1)}, u32[]{:S(2)}, u32[]{:S(2)}) collective-permute-start(bf16[48,1152]{1,0:T(8,128)(2,1)S(1)} %get-tuple-element.55), channel_id=1, source_target_pairs={{0,2},{1,3},{2,0},{3,1},{4,6},{5,7},{6,4},{7,5},{8,10},{9,11},{10,... | collective-permute-start | bytes 331784 | tf_op jit(solution)/shard_map/ppermute | solution.py:231
  108.8 2.2 %collective-permute-done.13 = bf16[48,1152]{1,0:T(8,128)(2,1)S(1)} collective-permute-done((bf16[48,1152]{1,0:T(8,128)(2,1)S(1)}, bf16[48,1152]{1,0:T(8,128)(2,1)S(1)}, u32[]{:S(2)}, u32[]{:S(2)}) %collective-permute-start.13) | collective-permute-done | bytes 110624 | tf_op jit(solution)/shard_map/ppermute | solution.py:231
  111.0 1.9 %collective-permute-done.14 = bf16[48,1152]{1,0:T(8,128)(2,1)S(1)} collective-permute-done((bf16[48,1152]{1,0:T(8,128)(2,1)S(1)}, bf16[48,1152]{1,0:T(8,128)(2,1)S(1)}, u32[]{:S(2)}, u32[]{:S(2)}) %collective-permute-start.14) | collective-permute-done | bytes 110624 | tf_op jit(solution)/shard_map/ppermute | solution.py:231
  112.9 2.4 %collective-permute-done.15 = bf16[48,1152]{1,0:T(8,128)(2,1)S(1)} collective-permute-done((bf16[48,1152]{1,0:T(8,128)(2,1)S(1)}, bf16[48,1152]{1,0:T(8,128)(2,1)S(1)}, u32[]{:S(2)}, u32[]{:S(2)}) %collective-permute-start.15) | collective-permute-done | bytes 110624 | tf_op jit(solution)/shard_map/ppermute | solution.py:231
  115.2 0.5 fusion.7
  115.8 1.5 %maximum_bitcast_fusion = bf16[1,1,896,1152]{3,2,1,0:T(8,128)(2,1)} fusion(bf16[256,1152]{1,0:T(8,128)(2,1)S(1)} %fusion.11, bf16[384,1152]{1,0:T(8,128)(2,1)S(1)} %fusion.7, bf16[256,1152]{1,0:T(8,128)(2,1)S(1)} %fusion.9), kind=kLoop, calls=%fused_computation.17 | loop fusion | flops 6193152 | bytes 4128768 | tf_op jit(solution)/shard_map/reshape | solution.py:293
  (103 shorter events, 7.1 us)
Async XLA Ops:
  0.0 7.2 %copy-start = (s32[4,4,4]{2,1,0:T(4,128)S(1)}, s32[4,4,4]{2,1,0:T(4,128)}, u32[]{:S(2)}) copy-start(s32[4,4,4]{2,1,0:T(4,128)} %param.24) | copy-start | bytes 772
  0.0 19.4 %collective-permute-start = (bf16[288,1728]{1,0:T(8,128)(2,1)}, bf16[288,1728]{1,0:T(8,128)(2,1)}, u32[]{:S(2)}, u32[]{:S(2)}) collective-permute-start(bf16[288,1728]{1,0:T(8,128)(2,1)} %param.22), channel_id=1, source_target_pairs={{1,0},{0,1},{3,2},{2,3},{5,4},{4,5},{7,6},{6,7},{9,8},{8,9},{11,10... | collective-permute-start | bytes 2985992 | tf_op jit(solution)/shard_map/ppermute | solution.py:154
  0.5 26.3 %collective-permute-start.1 = (bf16[288,1728]{1,0:T(8,128)(2,1)}, bf16[288,1728]{1,0:T(8,128)(2,1)}, u32[]{:S(2)}, u32[]{:S(2)}) collective-permute-start(bf16[288,1728]{1,0:T(8,128)(2,1)} %param.22), channel_id=1, source_target_pairs={{2,0},{3,1},{0,2},{1,3},{6,4},{7,5},{4,6},{5,7},{10,8},{11,9},{8,1... | collective-permute-start | bytes 2985992 | tf_op jit(solution)/shard_map/ppermute | solution.py:154
  7.6 1.1 copy-start.5
  7.6 1.7 %copy-start.14 = (s32[2]{0:T(128)S(1)}, s32[2]{0:T(128)}, u32[]{:S(2)}) copy-start(s32[2]{0:T(128)} %param.25) | copy-start | bytes 28
  8.0 3.2 %copy-start.9 = (s32[4,64]{1,0:T(4,128)S(1)}, s32[4,64]{1,0:T(4,128)}, u32[]{:S(2)}) copy-start(s32[4,64]{1,0:T(4,128)} %constant.119.clone) | copy-start | bytes 3076
  8.0 3.2 %copy-start.10 = (s32[4,64]{1,0:T(4,128)S(1)}, s32[4,64]{1,0:T(4,128)}, u32[]{:S(2)}) copy-start(s32[4,64]{1,0:T(4,128)} %constant.120.clone) | copy-start | bytes 3076
  8.1 3.2 %copy-start.7 = (s32[4,48]{1,0:T(4,128)S(1)}, s32[4,48]{1,0:T(4,128)}, u32[]{:S(2)}) copy-start(s32[4,48]{1,0:T(4,128)} %constant.124.clone) | copy-start | bytes 2308
  8.1 3.2 %copy-start.8 = (s32[4,48]{1,0:T(4,128)S(1)}, s32[4,48]{1,0:T(4,128)}, u32[]{:S(2)}) copy-start(s32[4,48]{1,0:T(4,128)} %constant.125.clone) | copy-start | bytes 2308
  8.1 3.3 %copy-start.12 = (pred[512,1]{0,1:T(4,128)(4,1)S(1)}, pred[512,1]{0,1:T(4,128)(4,1)}, u32[]{:S(2)}) copy-start(pred[512,1]{0,1:T(4,128)(4,1)} %constant.122.clone) | copy-start | bytes 1540
  8.1 5.8 %copy-start.16 = (s32[4]{0:T(128)S(1)}, s32[4]{0:T(128)}, u32[]{:S(2)}) copy-start(s32[4]{0:T(128)} %constant.118.clone) | copy-start | bytes 52
  16.3 1.6 %copy-start.4 = (bf16[288,1728]{1,0:T(8,128)(2,1)S(1)}, bf16[288,1728]{1,0:T(8,128)(2,1)}, u32[]{:S(2)}) copy-start(bf16[288,1728]{1,0:T(8,128)(2,1)} %param.22) | copy-start | bytes 2985988
  16.3 2.6 %copy-start.11 = (s32[4,64]{1,0:T(4,128)S(1)}, s32[4,64]{1,0:T(4,128)}, u32[]{:S(2)}) copy-start(s32[4,64]{1,0:T(4,128)} %constant.132) | copy-start | bytes 3076
  16.3 3.0 %copy-start.15 = (s32[4]{0:T(128)S(1)}, s32[4]{0:T(128)}, u32[]{:S(2)}) copy-start(s32[4]{0:T(128)} %param.26) | copy-start | bytes 52
  17.9 3.7 %copy-start.2 = (bf16[896,2,576]{0,2,1:T(8,128)(2,1)S(1)}, bf16[896,2,576]{0,2,1:T(8,128)(2,1)}, u32[]{:S(2)}) copy-start(bf16[896,2,576]{0,2,1:T(8,128)(2,1)} %add_convert_fusion.1) | copy-start | bytes 6193156
  26.7 3.6 %collective-permute-start.2 = (bf16[288,1728]{1,0:T(8,128)(2,1)}, bf16[288,1728]{1,0:T(8,128)(2,1)S(1)}, u32[]{:S(2)}, u32[]{:S(2)}) collective-permute-start(bf16[288,1728]{1,0:T(8,128)(2,1)} %collective-permute-done.1), channel_id=1, source_target_pairs={{1,0},{0,1},{3,2},{2,3},{5,4},{4,5},{7,6},{6,7},{9,8},{8,9},{11,10... | collective-permute-start | bytes 2985992 | tf_op jit(solution)/shard_map/ppermute | solution.py:154
  30.3 15.7 %collective-permute-start.3 = (bf16[576,288]{0,1:T(8,128)(2,1)}, bf16[576,288]{0,1:T(8,128)(2,1)}, u32[]{:S(2)}, u32[]{:S(2)}) collective-permute-start(bf16[576,288]{0,1:T(8,128)(2,1)} %param.23), channel_id=1, source_target_pairs={{1,0},{0,1},{3,2},{2,3},{5,4},{4,5},{7,6},{6,7},{9,8},{8,9},{11,10... | collective-permute-start | bytes 995336 | tf_op jit(solution)/shard_map/ppermute | solution.py:104
  30.9 15.0 %collective-permute-start.4 = (bf16[576,288]{0,1:T(8,128)(2,1)}, bf16[576,288]{0,1:T(8,128)(2,1)}, u32[]{:S(2)}, u32[]{:S(2)}) collective-permute-start(bf16[576,288]{0,1:T(8,128)(2,1)} %param.23), channel_id=1, source_target_pairs={{2,0},{3,1},{0,2},{1,3},{6,4},{7,5},{4,6},{5,7},{10,8},{11,9},{8,1... | collective-permute-start | bytes 995336 | tf_op jit(solution)/shard_map/ppermute | solution.py:104
  45.9 2.2 %collective-permute-start.5 = (bf16[576,288]{0,1:T(8,128)(2,1)}, bf16[576,288]{0,1:T(8,128)(2,1)S(1)}, u32[]{:S(2)}, u32[]{:S(2)}) collective-permute-start(bf16[576,288]{0,1:T(8,128)(2,1)} %collective-permute-done.4), channel_id=1, source_target_pairs={{1,0},{0,1},{3,2},{2,3},{5,4},{4,5},{7,6},{6,7},{9,8},{8,9},{11,10... | collective-permute-start | bytes 995336 | tf_op jit(solution)/shard_map/ppermute | solution.py:104
  68.8 12.7 %collective-permute-start.6 = (bf16[64,1152]{1,0:T(8,128)(2,1)S(1)}, bf16[64,1152]{1,0:T(8,128)(2,1)S(1)}, u32[]{:S(2)}, u32[]{:S(2)}) collective-permute-start(bf16[64,1152]{1,0:T(8,128)(2,1)S(1)} %get-tuple-element.50), channel_id=1, source_target_pairs={{0,3},{1,0},{2,1},{3,2},{4,7},{5,4},{6,5},{7,6},{8,11},{9,8},{10,9... | collective-permute-start | bytes 442376 | tf_op jit(solution)/shard_map/ppermute | solution.py:231
  69.2 12.3 %collective-permute-start.7 = (bf16[64,1152]{1,0:T(8,128)(2,1)S(1)}, bf16[64,1152]{1,0:T(8,128)(2,1)S(1)}, u32[]{:S(2)}, u32[]{:S(2)}) collective-permute-start(bf16[64,1152]{1,0:T(8,128)(2,1)S(1)} %get-tuple-element.53), channel_id=1, source_target_pairs={{0,1},{1,2},{2,3},{3,0},{4,5},{5,6},{6,7},{7,4},{8,9},{9,10},{10,1... | collective-permute-start | bytes 442376 | tf_op jit(solution)/shard_map/ppermute | solution.py:231
  69.4 12.1 %collective-permute-start.8 = (bf16[64,1152]{1,0:T(8,128)(2,1)S(1)}, bf16[64,1152]{1,0:T(8,128)(2,1)S(1)}, u32[]{:S(2)}, u32[]{:S(2)}) collective-permute-start(bf16[64,1152]{1,0:T(8,128)(2,1)S(1)} %get-tuple-element.52), channel_id=1, source_target_pairs={{0,2},{1,3},{2,0},{3,1},{4,6},{5,7},{6,4},{7,5},{8,10},{9,11},{10,... | collective-permute-start | bytes 442376 | tf_op jit(solution)/shard_map/ppermute | solution.py:231
  71.0 10.7 %collective-permute-start.9 = (bf16[64,1152]{1,0:T(8,128)(2,1)S(1)}, bf16[64,1152]{1,0:T(8,128)(2,1)S(1)}, u32[]{:S(2)}, u32[]{:S(2)}) collective-permute-start(bf16[64,1152]{1,0:T(8,128)(2,1)S(1)} %get-tuple-element.51), channel_id=1, source_target_pairs={{0,2},{1,3},{2,0},{3,1},{4,6},{5,7},{6,4},{7,5},{8,10},{9,11},{10,... | collective-permute-start | bytes 442376 | tf_op jit(solution)/shard_map/ppermute | solution.py:231
  72.4 9.4 %copy-start.1 = (bf16[512,1152]{1,0:T(8,128)(2,1)S(1)}, bf16[512,1152]{1,0:T(8,128)(2,1)}, u32[]{:S(2)}) copy-start(bf16[512,1152]{1,0:T(8,128)(2,1)} %shard_map.190) | copy-start | bytes 3538948
  72.4 9.4 %copy-start.18 = (pred[512]{0:T(512)(128)(4,1)S(1)}, pred[512]{0:T(512)(128)(4,1)}, u32[]{:S(2)}) copy-start(pred[512]{0:T(512)(128)(4,1)} %constant.131) | copy-start | bytes 1540
  82.5 5.9 %copy-start.6 = (s32[4,48]{1,0:T(4,128)S(1)}, s32[4,48]{1,0:T(4,128)}, u32[]{:S(2)}) copy-start(s32[4,48]{1,0:T(4,128)} %constant.134) | copy-start | bytes 2308
  82.5 6.4 %copy-start.13 = (pred[384,1]{0,1:T(4,128)(4,1)S(1)}, pred[384,1]{0,1:T(4,128)(4,1)}, u32[]{:S(2)}) copy-start(pred[384,1]{0,1:T(4,128)(4,1)} %constant.127.clone) | copy-start | bytes 1156
  82.6 18.0 %collective-permute-start.10 = (bf16[256,1152]{1,0:T(8,128)(2,1)S(1)}, bf16[256,1152]{1,0:T(8,128)(2,1)S(1)}, u32[]{:S(2)}, u32[]{:S(2)}) collective-permute-start(bf16[256,1152]{1,0:T(8,128)(2,1)S(1)} %get-tuple-element.31), channel_id=1, source_target_pairs={{0,4},{4,8},{8,12},{1,5},{5,9},{9,13},{2,6},{6,10},{10,14},{3,7},{... | collective-permute-start | bytes 1769480 | tf_op jit(solution)/shard_map/ppermute | solution.py:261
  86.4 17.6 %collective-permute-start.11 = (bf16[256,1152]{1,0:T(8,128)(2,1)S(1)}, bf16[256,1152]{1,0:T(8,128)(2,1)S(1)}, u32[]{:S(2)}, u32[]{:S(2)}) collective-permute-start(bf16[256,1152]{1,0:T(8,128)(2,1)S(1)} %get-tuple-element.26), channel_id=1, source_target_pairs={{4,0},{8,4},{12,8},{5,1},{9,5},{13,9},{6,2},{10,6},{14,10},{7,3},{... | collective-permute-start | bytes 1769480 | tf_op jit(solution)/shard_map/ppermute | solution.py:262
  91.4 9.1 %copy-start.3 = (bf16[192,1152]{1,0:T(8,128)(2,1)S(1)}, bf16[192,1152]{1,0:T(8,128)(2,1)}, u32[]{:S(2)}) copy-start(bf16[192,1152]{1,0:T(8,128)(2,1)} %shard_map.191) | copy-start | bytes 1327108
  105.5 9.8 %copy-start.17 = (pred[384]{0:T(512)(128)(4,1)S(1)}, pred[384]{0:T(512)(128)(4,1)}, u32[]{:S(2)}) copy-start(pred[384]{0:T(512)(128)(4,1)} %constant.133) | copy-start | bytes 1156
  105.5 3.3 %collective-permute-start.12 = (bf16[48,1152]{1,0:T(8,128)(2,1)S(1)}, bf16[48,1152]{1,0:T(8,128)(2,1)S(1)}, u32[]{:S(2)}, u32[]{:S(2)}) collective-permute-start(bf16[48,1152]{1,0:T(8,128)(2,1)S(1)} %get-tuple-element.54), channel_id=1, source_target_pairs={{0,3},{1,0},{2,1},{3,2},{4,7},{5,4},{6,5},{7,6},{8,11},{9,8},{10,9... | collective-permute-start | bytes 331784 | tf_op jit(solution)/shard_map/ppermute | solution.py:231
  105.6 5.4 %collective-permute-start.13 = (bf16[48,1152]{1,0:T(8,128)(2,1)S(1)}, bf16[48,1152]{1,0:T(8,128)(2,1)S(1)}, u32[]{:S(2)}, u32[]{:S(2)}) collective-permute-start(bf16[48,1152]{1,0:T(8,128)(2,1)S(1)} %get-tuple-element.57), channel_id=1, source_target_pairs={{0,1},{1,2},{2,3},{3,0},{4,5},{5,6},{6,7},{7,4},{8,9},{9,10},{10,1... | collective-permute-start | bytes 331784 | tf_op jit(solution)/shard_map/ppermute | solution.py:231
  106.1 6.8 %collective-permute-start.14 = (bf16[48,1152]{1,0:T(8,128)(2,1)S(1)}, bf16[48,1152]{1,0:T(8,128)(2,1)S(1)}, u32[]{:S(2)}, u32[]{:S(2)}) collective-permute-start(bf16[48,1152]{1,0:T(8,128)(2,1)S(1)} %get-tuple-element.56), channel_id=1, source_target_pairs={{0,2},{1,3},{2,0},{3,1},{4,6},{5,7},{6,4},{7,5},{8,10},{9,11},{10,... | collective-permute-start | bytes 331784 | tf_op jit(solution)/shard_map/ppermute | solution.py:231
  106.9 8.4 %collective-permute-start.15 = (bf16[48,1152]{1,0:T(8,128)(2,1)S(1)}, bf16[48,1152]{1,0:T(8,128)(2,1)S(1)}, u32[]{:S(2)}, u32[]{:S(2)}) collective-permute-start(bf16[48,1152]{1,0:T(8,128)(2,1)S(1)} %get-tuple-element.55), channel_id=1, source_target_pairs={{0,2},{1,3},{2,0},{3,1},{4,6},{5,7},{6,4},{7,5},{8,10},{9,11},{10,... | collective-permute-start | bytes 331784 | tf_op jit(solution)/shard_map/ppermute | solution.py:231

commit v10 on v8

--- a/solution.py
+++ b/solution.py
@@ -30,28 +30,19 @@
     return (normed * (1.0 + modulation[1]) + modulation[0]).astype(jnp.bfloat16)
 
 
-def attention_kernel(q_ref, k_ref, v_ref, w_ref, x_ref, g_ref, o_ref, acc_ref):
-    head = pl.program_id(1)
-
-    @pl.when(head == 0)
-    def _():
-        acc_ref[...] = jnp.zeros_like(acc_ref)
-
-    scores = jnp.dot(q_ref[0], k_ref[0], preferred_element_type=jnp.float32) * (
-        1.0 / math.sqrt(HD)
-    )
-    row_max = jnp.max(scores, axis=-1, keepdims=True)
-    weights = jnp.exp(scores - row_max)
-    row_sum = jnp.sum(weights, axis=-1, keepdims=True)
-    probabilities = (weights * (1.0 / row_sum)).astype(jnp.bfloat16)
-    mixed = jnp.dot(probabilities, v_ref[0], preferred_element_type=jnp.float32).astype(
-        jnp.bfloat16
-    )
-    acc_ref[...] += jnp.dot(mixed, w_ref[...], preferred_element_type=jnp.float32)
-
-    @pl.when(head == pl.num_programs(1) - 1)
-    def _():
-        o_ref[...] = (x_ref[...].astype(jnp.float32) + g_ref[...] * acc_ref[...]).astype(
+HEADS_PER_STEP = 2
+
+
+def attention_kernel(q_ref, k_ref, v_ref, o_ref):
+    for j in range(HEADS_PER_STEP):
+        scores = jnp.dot(q_ref[j], k_ref[j], preferred_element_type=jnp.float32) * (
+            1.0 / math.sqrt(HD)
+        )
+        row_max = jnp.max(scores, axis=-1, keepdims=True)
+        weights = jnp.exp(scores - row_max)
+        row_sum = jnp.sum(weights, axis=-1, keepdims=True)
+        probabilities = (weights * (1.0 / row_sum)).astype(jnp.bfloat16)
+        o_ref[j] = jnp.dot(probabilities, v_ref[j], preferred_element_type=jnp.float32).astype(
             o_ref.dtype
         )
 
@@ -59,23 +50,22 @@
 def attend_project(queries, keys, values, w_out_full, block_in, gate):
     heads, size, tokens = keys.shape
     chunk = queries.shape[1]
-    width = block_in.shape[1]
-    return pl.pallas_call(
+    hb = HEADS_PER_STEP
+    mixed = pl.pallas_call(
         attention_kernel,
-        grid=(1, heads),
+        grid=(heads // hb,),
         in_specs=[
-            pl.BlockSpec((1, chunk, size), lambda i, h: (h, i, 0)),
-            pl.BlockSpec((1, size, tokens), lambda i, h: (h, 0, 0)),
-            pl.BlockSpec((1, tokens, size), lambda i, h: (h, 0, 0)),
-            pl.BlockSpec((size, width), lambda i, h: (h, 0)),
-            pl.BlockSpec((chunk, width), lambda i, h: (i, 0)),
-            pl.BlockSpec((1, width), lambda i, h: (0, 0)),
+            pl.BlockSpec((hb, chunk, size), lambda h: (h, 0, 0)),
+            pl.BlockSpec((hb, size, tokens), lambda h: (h, 0, 0)),
+            pl.BlockSpec((hb, tokens, size), lambda h: (h, 0, 0)),
         ],
-        out_specs=pl.BlockSpec((chunk, width), lambda i, h: (i, 0)),
-        out_shape=jax.ShapeDtypeStruct(block_in.shape, block_in.dtype),
-        scratch_shapes=[pltpu.VMEM((chunk, width), jnp.float32)],
-        compiler_params=pltpu.CompilerParams(dimension_semantics=("arbitrary", "arbitrary")),
-    )(queries, keys, values, w_out_full, block_in, gate.reshape(1, width))
+        out_specs=pl.BlockSpec((hb, chunk, size), lambda h: (h, 0, 0)),
+        out_shape=jax.ShapeDtypeStruct(queries.shape, queries.dtype),
+        compiler_params=pltpu.CompilerParams(dimension_semantics=("arbitrary",)),
+    )(queries, keys, values)
+    mixed = mixed.transpose(1, 0, 2).reshape(chunk, heads * size)
+    projected = jnp.dot(mixed, w_out_full, preferred_element_type=jnp.float32)
+    return (block_in.astype(jnp.float32) + gate * projected).astype(block_in.dtype)
 
 
 def face_pieces(shard):

time: 120 us -> 121 us (level)
  Pallas kernels: 37.8 us -> 24.7 us
  waiting for transfers between devices: 9.99 us -> 16.4 us
  matrix products: 10.9 us -> 15.2 us
  local copies, waits for them, and re-layouts: 28.5 us -> 31.5 us
    pallas_call x3, Pallas kernels: 37.8 us -> 24.7 us  [attend_project(): pl.pallas_call(attention_kernel, grid=(heads // hb,), in_specs=[pl.BlockS...]
    dot_general x0 -> x3, matrix products: none -> 5.49 us  [attend_project(): projected = jnp.dot(mixed, w_out_full, preferred_element_type=jnp.float32)]
    ppermute x8, waiting for transfers between devices: 6.89 us -> 12.3 us  [strips_in(): lax.ppermute(sent, 'face', [(i, (i + shift) % n) for i in range(n)])]
    transpose x0 -> x3, local copies, waits for them, and re-layouts: none -> 5.37 us  [attend_project(): mixed = mixed.transpose(1, 0, 2).reshape(chunk, heads * size)]
    ppermute x6, waiting for transfers between devices: 0.67 us -> 3.61 us  [fetch(): return lax.ppermute(x, 'face', [(src_of(i), i) for i in range(n)])]
    slice x1 -> x0, local copies, waits for them, and re-layouts: 2.13 us -> none  [per_device(): tile_second = tile_part(second_queries, block_in[mid_a:tokens - rim])]
    unnamed x42 -> x50, local copies, waits for them, and re-layouts: 6.74 us -> 8.79 us
    ppermute x1, waiting for transfers between devices: 2.43 us -> 0.46 us  [per_device(): upper = lax.ppermute(low, 'tm', [(i + 1, i) for i in range(count - 1)])]
  transfers between devices with their start and end apart: 16 -> 16, of which waited for: 5 -> 9; matrix products, arithmetic and copies ran while one was open for 39% -> 45% of each run, Pallas kernels for 17% -> 15%
where the time goes in v10:
time: 121 us; the launch traced here: 120 us
  local copies, waits for them, and re-layouts  31.5 us (26%)
  Pallas kernels  24.7 us (20%)
  waiting for transfers between devices  16.4 us (14%)
  starting transfers between devices  16.2 us (13%)
  matrix products  15.2 us (13%)
  other arithmetic  15.1 us (12%)
    pallas_call x3, Pallas kernels, attend_project(): pl.pallas_call(attention_kernel, grid=(heads // hb,), in_specs=[pl.BlockS...  24.7 us
    ppermute x8, waiting for transfers between devices, strips_in(): lax.ppermute(sent, 'face', [(i, (i + shift) % n) for i in range(n)])  12.3 us
    unnamed x50, local copies, waits for them, and re-layouts  8.79 us
    dot_general x2, matrix products, chip_part(): jnp.dot(lax.dynamic_index_in_dim(moved_chips, chip, 0, keepdims=False), w...  7.48 us
    dot_general x3, matrix products, attend_project(): projected = jnp.dot(mixed, w_out_full, preferred_element_type=jnp.float32)  5.49 us
    transpose x3, local copies, waits for them, and re-layouts, attend_project(): mixed = mixed.transpose(1, 0, 2).reshape(chunk, heads * size)  5.37 us
    ppermute x8, starting transfers between devices, strips_in(): lax.ppermute(sent, 'face', [(i, (i + shift) % n) for i in range(n)])  5.21 us
    ppermute x6, starting transfers between devices, fetch(): return lax.ppermute(x, 'face', [(src_of(i), i) for i in range(n)])  5.11 us
  transfers between devices with their start and end apart: 16, of which 9 were waited for; matrix products, arithmetic and copies ran while one was open for 45% of the time, Pallas kernels for 15%

profile of v10, /device:TPU:0, one launch (start us, length us, event | category | flops | bytes accessed | tf_op | source)
XLA Modules:
  0.0 119.7 jit_solution(6629196324663720511)
XLA Ops:
  0.5 2.6 %collective-permute-start.1 = (bf16[288,1728]{1,0:T(8,128)(2,1)}, bf16[288,1728]{1,0:T(8,128)(2,1)}, u32[]{:S(2)}, u32[]{:S(2)}) collective-permute-start(bf16[288,1728]{1,0:T(8,128)(2,1)} %param.22), channel_id=1, source_target_pairs={{2,0},{3,1},{0,2},{1,3},{6,4},{7,5},{4,6},{5,7},{10,8},{11,9},{8,1... | collective-permute-start | bytes 2985992 | tf_op jit(solution)/shard_map/ppermute | solution.py:126
  3.4 2.9 %copy.30 = bf16[1,1,896,1152]{2,3,1,0:T(8,128)(2,1)S(1)} copy(bf16[1,1,896,1152]{3,2,1,0:T(8,128)(2,1)} %param.20) | data formatting | bytes 4128768 | tf_op args[0]
  8.7 2.5 %broadcast_select_fusion.1 = (f32[512,1]{0,1:T(1,128)S(1)}, f32[512,1]{0,1:T(1,128)S(1)}) fusion(pred[512,1]{0,1:T(4,128)(4,1)S(1)} %copy-done.15, f32[]{:T(128)} %bitcast.14, f32[]{:T(128)} %bitcast.13, f32[]{:T(128)} %bitcast.32, f32[]{:T(128)} %bitcast.31), kind=kLoop, calls=%fused_computation.93 | loop fusion | flops 1024 | bytes 4624 | tf_op jit(solution)/shard_map/jit(_where)/select_n | solution.py:217
  11.5 2.1 %add_convert_fusion.1 = bf16[896,2,576]{0,2,1:T(8,128)(2,1)} fusion(f32[2,576]{1,0:T(2,128)S(1)} %add.118, f32[2,576]{1,0:T(2,128)S(1)} %mul.141, f32[896]{0:T(1024)S(1)} %add_rsqrt_fusion, f32[896]{0:T(1024)S(1)} %broadcast_multiply_fusion, bf16[896,2,576]{0,2,1:T(8,128)(2,1)S(1)} %bitcast.83), kind=kLoop, calls=%fused_computation.4 | loop fusion | flops 6193152 | bytes 4145152 | tf_op jit(solution)/shard_map/convert_element_type | solution.py:30
  13.6 1.4 %broadcast.89.clone = bf16[2,288,1728]{2,1,0:T(8,128)(2,1)} broadcast(bf16[]{:T(256)} %constant.115.clone.1), dimensions={} | broadcast | bytes 1990658 | tf_op jit(solution)/shard_map/broadcast.4
  15.2 1.0 bitcast_dynamic-update-slice_fusion.3
  16.5 2.2 %bitcast_dynamic-update-slice_fusion.2 = bf16[2,288,1728]{2,1,0:T(8,128)(2,1)} fusion(bf16[2,288,1728]{2,1,0:T(8,128)(2,1)} %bitcast_dynamic-update-slice_fusion.3, s32[]{:T(128)S(6)} %select_n.118, bf16[288,1728]{1,0:T(8,128)(2,1)} %collective-permute-done), kind=kLoop, calls=%fused_computation.42 | loop fusion | bytes 2064388 | tf_op jit(solution)/shard_map/jit(dynamic_update_index_in_dim)/dynamic_update_slice | solution.py:133
  18.8 4.6 %fusion.20 = f32[896,1728]{0,1:T(8,128)S(1)} fusion(bf16[576,1728]{1,0:T(8,128)(2,1)} %bitcast.5, bf16[896,2,576]{0,2,1:T(8,128)(2,1)S(1)} %copy-done.2, s32[]{:T(128)S(6)} %select_n.115), kind=kOutput, calls=%fused_computation.44 | convolution fusion | flops 1783627776 | bytes 9216004 | tf_op jit(solution)/shard_map/dot_general | solution.py:137
  23.4 3.4 %collective-permute-done.1 = bf16[288,1728]{1,0:T(8,128)(2,1)} collective-permute-done((bf16[288,1728]{1,0:T(8,128)(2,1)}, bf16[288,1728]{1,0:T(8,128)(2,1)}, u32[]{:S(2)}, u32[]{:S(2)}) %collective-permute-start.1) | collective-permute-done | bytes 995360 | tf_op jit(solution)/shard_map/ppermute | solution.py:126
  26.7 1.2 slice_bitcast_fusion.2
  28.0 1.3 %bitcast_dynamic-update-slice_fusion.1 = bf16[2,288,1728]{2,1,0:T(8,128)(2,1)S(1)} fusion(bf16[2,288,1728]{2,1,0:T(8,128)(2,1)S(1)} %broadcast.89, s32[]{:T(128)S(6)} %select_n.117, bf16[288,1728]{1,0:T(8,128)(2,1)} %collective-permute-done.1), kind=kLoop, calls=%fused_computation.39 | loop fusion | bytes 2027524 | tf_op jit(solution)/shard_map/jit(dynamic_update_index_in_dim)/dynamic_update_slice | solution.py:132
  29.9 1.7 %collective-permute-start.4 = (bf16[576,288]{0,1:T(8,128)(2,1)}, bf16[576,288]{0,1:T(8,128)(2,1)}, u32[]{:S(2)}, u32[]{:S(2)}) collective-permute-start(bf16[576,288]{0,1:T(8,128)(2,1)} %param.23), channel_id=1, source_target_pairs={{2,0},{3,1},{0,2},{1,3},{6,4},{7,5},{4,6},{5,7},{10,8},{11,9},{8,1... | collective-permute-start | bytes 995336 | tf_op jit(solution)/shard_map/ppermute | solution.py:76
  31.8 1.0 bitcast_dynamic-update-slice_fusion.7
  33.0 1.0 copy-done.3
  34.0 2.9 %fusion.18 = f32[896,1728]{0,1:T(8,128)S(1)} fusion(bf16[576,1728]{1,0:T(8,128)(2,1)S(1)} %bitcast.91, bf16[896,2,576]{0,2,1:T(8,128)(2,1)S(1)} %copy-done.2, s32[]{:T(128)S(6)} %select_n.119), kind=kOutput, calls=%fused_computation.40 | convolution fusion | flops 1783627776 | bytes 9289732 | tf_op jit(solution)/shard_map/dot_general | solution.py:137
  36.8 0.8 add_convert_fusion
  37.7 1.6 %fusion.40 = (bf16[896,1,8,72]{0,3,2,1:T(8,128)(2,1)S(1)}, bf16[896,1,8,72]{0,3,2,1:T(8,128)(2,1)}, bf16[8,72,896]{2,1,0:T(8,128)(2,1)}) fusion(bf16[896,3,8,72]{0,3,2,1:T(8,128)(2,1)S(1)} %bitcast.87), kind=kLoop, calls=%fused_computation.101 | loop fusion | bytes 6193152 | tf_op jit(solution)/shard_map/slice | solution.py:168
  39.3 1.9 %copy.36 = bf16[896,1,8,72]{3,0,2,1:T(8,128)(2,1)S(1)} copy(bf16[896,1,8,72]{0,3,2,1:T(8,128)(2,1)} %get-tuple-element.39) | data formatting | bytes 2064384
  41.2 0.9 fusion.42
  42.1 1.7 %copy.37 = bf16[896,1,8,72]{3,0,2,1:T(8,128)(2,1)} copy(bf16[896,1,8,72]{0,3,2,1:T(8,128)(2,1)S(1)} %get-tuple-element.38) | data formatting | bytes 2064384
  43.7 2.2 %pad_maximum_fusion.q_ref = bf16[8,512,72]{2,1,0:T(8,128)(2,1)} fusion(bf16[8,256,72]{2,1,0:T(8,128)(2,1)} %get-tuple-element.46, bf16[8,256,72]{2,1,0:T(8,128)(2,1)S(1)} %get-tuple-element.45), kind=kLoop, calls=%fused_computation.36 | loop fusion | flops 1179648 | bytes 1179648 | tf_op jit(solution)/shard_map/concatenate | solution.py:222
  45.9 11.4 %shard_map.190 = bf16[8,512,72]{2,1,0:T(8,128)(2,1)} custom-call(bf16[8,512,72]{2,1,0:T(8,128)(2,1)} %pad_maximum_fusion.q_ref, bf16[8,72,896]{2,1,0:T(8,128)(2,1)} %get-tuple-element.40.k_ref, bf16[8,896,72]{2,1,0:T(8,128)(2,1)} %bitcast.84), custom_call_target="tpu_custom_call" | custom-call | tf_op jit(solution)/shard_map/pallas_call | solution.py:54
  57.3 2.3 %copy.33 = bf16[512,8,72]{0,2,1:T(8,128)(2,1)} copy(bf16[512,8,72]{2,0,1:T(8,128)(2,1)} %bitcast.90) | data formatting | bytes 1179648 | tf_op jit(solution)/shard_map/transpose | solution.py:66
  59.6 1.0 fusion.41
  60.6 1.0 bitcast_dynamic-update-slice_fusion.6
  61.6 1.0 bitcast_dynamic-update-slice_fusion.5
  62.8 1.2 %fusion.7 = bf16[512,1152]{1,0:T(8,128)(2,1)S(1)} fusion(bf16[512,576]{0,1:T(8,128)(2,1)S(1)} %bitcast.97, bf16[576,1152]{0,1:T(8,128)(2,1)S(1)} %bitcast.94, bf16[256,1152]{1,0:T(8,128)(2,1)S(1)} %copy-done.8, bf16[256,1152]{1,0:T(8,128)(2,1)S(1)} %copy-done.7, f32[1152]{0:T(1024)S(1)} %get-tuple-element.33), kind=kOutput, calls=%fused_computation.13 | convolution fusion | flops 683606016 | bytes 4280832 | tf_op jit(solution)/shard_map/dot_general | solution.py:67
  65.3 6.7 %shard_map.191 = bf16[8,192,72]{2,1,0:T(8,128)(2,1)} custom-call(bf16[8,192,72]{2,1,0:T(8,128)(2,1)} %get-tuple-element.22.q_ref, bf16[8,72,896]{2,1,0:T(8,128)(2,1)} %get-tuple-element.40.k_ref, bf16[8,896,72]{2,1,0:T(8,128)(2,1)} %bitcast.85), custom_call_target="tpu_custom_call" | custom-call | tf_op jit(solution)/shard_map/pallas_call | solution.py:54
  71.9 1.2 copy.34
  73.8 1.6 %collective-permute-start.8 = (bf16[64,1152]{1,0:T(8,128)(2,1)S(1)}, bf16[64,1152]{1,0:T(8,128)(2,1)S(1)}, u32[]{:S(2)}, u32[]{:S(2)}) collective-permute-start(bf16[64,1152]{1,0:T(8,128)(2,1)S(1)} %get-tuple-element.51), channel_id=1, source_target_pairs={{0,2},{1,3},{2,0},{3,1},{4,6},{5,7},{6,4},{7,5},{8,10},{9,11},{10,... | collective-permute-start | bytes 442376 | tf_op jit(solution)/shard_map/ppermute | solution.py:203
  75.8 2.5 %fusion.12 = bf16[192,1152]{1,0:T(8,128)(2,1)} fusion(bf16[192,576]{0,1:T(8,128)(2,1)S(1)} %bitcast.98, bf16[576,1152]{0,1:T(8,128)(2,1)S(1)} %bitcast.95, f32[1152]{0:T(1024)S(1)} %get-tuple-element.33, bf16[1,1,896,1152]{3,2,1,0:T(8,128)(2,1)} %param.20), kind=kOutput, calls=%fused_computation.22 | convolution fusion | flops 255688704 | bytes 2437632 | tf_op jit(solution)/shard_map/dot_general | solution.py:67
  78.3 1.0 collective-permute-done.7
  79.3 4.0 %collective-permute-done.8 = bf16[64,1152]{1,0:T(8,128)(2,1)S(1)} collective-permute-done((bf16[64,1152]{1,0:T(8,128)(2,1)S(1)}, bf16[64,1152]{1,0:T(8,128)(2,1)S(1)}, u32[]{:S(2)}, u32[]{:S(2)}) %collective-permute-start.8) | collective-permute-done | bytes 147488 | tf_op jit(solution)/shard_map/ppermute | solution.py:203
  83.3 2.7 %collective-permute-done.9 = bf16[64,1152]{1,0:T(8,128)(2,1)S(1)} collective-permute-done((bf16[64,1152]{1,0:T(8,128)(2,1)S(1)}, bf16[64,1152]{1,0:T(8,128)(2,1)S(1)}, u32[]{:S(2)}, u32[]{:S(2)}) %collective-permute-start.9) | collective-permute-done | bytes 147488 | tf_op jit(solution)/shard_map/ppermute | solution.py:203
  87.0 4.6 %collective-permute-start.10 = (bf16[256,1152]{1,0:T(8,128)(2,1)S(1)}, bf16[256,1152]{1,0:T(8,128)(2,1)}, u32[]{:S(2)}, u32[]{:S(2)}) collective-permute-start(bf16[256,1152]{1,0:T(8,128)(2,1)S(1)} %get-tuple-element.31), channel_id=1, source_target_pairs={{0,4},{4,8},{8,12},{1,5},{5,9},{9,13},{2,6},{6,10},{10,14},{3,7},{... | collective-permute-start | bytes 1769480 | tf_op jit(solution)/shard_map/ppermute | solution.py:233
  91.5 1.3 %collective-permute-start.11 = (bf16[256,1152]{1,0:T(8,128)(2,1)S(1)}, bf16[256,1152]{1,0:T(8,128)(2,1)S(1)}, u32[]{:S(2)}, u32[]{:S(2)}) collective-permute-start(bf16[256,1152]{1,0:T(8,128)(2,1)S(1)} %get-tuple-element.26), channel_id=1, source_target_pairs={{4,0},{8,4},{12,8},{5,1},{9,5},{13,9},{6,2},{10,6},{14,10},{7,3},{... | collective-permute-start | bytes 1769480 | tf_op jit(solution)/shard_map/ppermute | solution.py:234
  92.8 2.5 %select_reduce_fusion.5 = (f32[384]{0:T(512)S(1)}, f32[384]{0:T(512)S(1)}) fusion(pred[384,1]{0,1:T(4,128)(4,1)S(1)} %copy-done.17, f32[]{:T(128)} %bitcast.14, f32[]{:T(128)} %bitcast.13, f32[]{:T(128)} %bitcast.32, f32[]{:T(128)} %bitcast.31), kind=kLoop, calls=%fused_computation.90 | loop fusion | flops 768 | bytes 3472 | tf_op jit(solution)/shard_map/jit(_where)/select_n | solution.py:217
  96.3 6.7 %shard_map.192 = bf16[8,192,72]{2,1,0:T(8,128)(2,1)} custom-call(bf16[8,192,72]{2,1,0:T(8,128)(2,1)} %get-tuple-element.27.q_ref, bf16[8,72,896]{2,1,0:T(8,128)(2,1)} %get-tuple-element.40.k_ref, bf16[8,896,72]{2,1,0:T(8,128)(2,1)} %bitcast.86), custom_call_target="tpu_custom_call" | custom-call | tf_op jit(solution)/shard_map/pallas_call | solution.py:54
  103.0 1.9 %copy.35 = bf16[192,8,72]{0,2,1:T(8,128)(2,1)} copy(bf16[192,8,72]{2,0,1:T(8,128)(2,1)} %bitcast.92) | data formatting | bytes 442368 | tf_op jit(solution)/shard_map/transpose | solution.py:66
  104.9 1.0 constant_dynamic-update-slice_fusion.1
  105.9 1.8 %fusion.13 = bf16[192,1152]{1,0:T(8,128)(2,1)S(1)} fusion(bf16[192,576]{0,1:T(8,128)(2,1)} %bitcast.99, bf16[576,1152]{0,1:T(8,128)(2,1)S(1)} %bitcast.96, bf16[1,1,896,1152]{3,2,1,0:T(8,128)(2,1)} %param.20, f32[1152]{0:T(1024)S(1)} %get-tuple-element.33), kind=kOutput, calls=%fused_computation.23 | convolution fusion | flops 255688704 | bytes 2437632 | tf_op jit(solution)/shard_map/dot_general | solution.py:67
  109.3 0.7 collective-permute-start.14
  110.1 1.3 %collective-permute-start.15 = (bf16[48,1152]{1,0:T(8,128)(2,1)S(1)}, bf16[48,1152]{1,0:T(8,128)(2,1)S(1)}, u32[]{:S(2)}, u32[]{:S(2)}) collective-permute-start(bf16[48,1152]{1,0:T(8,128)(2,1)S(1)} %get-tuple-element.54), channel_id=1, source_target_pairs={{0,2},{1,3},{2,0},{3,1},{4,6},{5,7},{6,4},{7,5},{8,10},{9,11},{10,... | collective-permute-start | bytes 331784 | tf_op jit(solution)/shard_map/ppermute | solution.py:203
  111.4 1.4 %fusion.15 = bf16[256,1152]{1,0:T(8,128)(2,1)S(1)} fusion(bf16[256,1152]{1,0:T(8,128)(2,1)S(1)} %get-tuple-element.26, bf16[256,1152]{1,0:T(8,128)(2,1)} %collective-permute-done.10, f32[256]{0:T(256)S(1)} %mul.157, f32[256]{0:T(256)S(1)} %mul.137, pred[]{:T(512)S(6)} %gt.7), kind=kLoop, calls=%fused_computation.33 | loop fusion | flops 2064384 | bytes 1771521 | tf_op jit(solution)/shard_map/convert_element_type | solution.py:263
  113.1 1.0 collective-permute-done.13
  114.1 1.2 %collective-permute-done.14 = bf16[48,1152]{1,0:T(8,128)(2,1)S(1)} collective-permute-done((bf16[48,1152]{1,0:T(8,128)(2,1)S(1)}, bf16[48,1152]{1,0:T(8,128)(2,1)S(1)}, u32[]{:S(2)}, u32[]{:S(2)}) %collective-permute-start.14) | collective-permute-done | bytes 110624 | tf_op jit(solution)/shard_map/ppermute | solution.py:203
  115.3 2.4 %collective-permute-done.15 = bf16[48,1152]{1,0:T(8,128)(2,1)S(1)} collective-permute-done((bf16[48,1152]{1,0:T(8,128)(2,1)S(1)}, bf16[48,1152]{1,0:T(8,128)(2,1)S(1)}, u32[]{:S(2)}, u32[]{:S(2)}) %collective-permute-start.15) | collective-permute-done | bytes 110624 | tf_op jit(solution)/shard_map/ppermute | solution.py:203
  118.2 1.5 %maximum_bitcast_fusion = bf16[1,1,896,1152]{3,2,1,0:T(8,128)(2,1)} fusion(bf16[256,1152]{1,0:T(8,128)(2,1)S(1)} %fusion.17, bf16[384,1152]{1,0:T(8,128)(2,1)S(1)} %fusion.9, bf16[256,1152]{1,0:T(8,128)(2,1)S(1)} %fusion.15), kind=kLoop, calls=%fused_computation.26 | loop fusion | flops 6193152 | bytes 4128768 | tf_op jit(solution)/shard_map/reshape | solution.py:265
  (114 shorter events, 11.4 us)
Async XLA Ops:
  0.0 3.0 %copy-start = (s32[4,4,4]{2,1,0:T(4,128)S(1)}, s32[4,4,4]{2,1,0:T(4,128)}, u32[]{:S(2)}) copy-start(s32[4,4,4]{2,1,0:T(4,128)} %param.24) | copy-start | bytes 772
  0.0 16.5 %collective-permute-start = (bf16[288,1728]{1,0:T(8,128)(2,1)}, bf16[288,1728]{1,0:T(8,128)(2,1)}, u32[]{:S(2)}, u32[]{:S(2)}) collective-permute-start(bf16[288,1728]{1,0:T(8,128)(2,1)} %param.22), channel_id=1, source_target_pairs={{1,0},{0,1},{3,2},{2,3},{5,4},{4,5},{7,6},{6,7},{9,8},{8,9},{11,10... | collective-permute-start | bytes 2985992 | tf_op jit(solution)/shard_map/ppermute | solution.py:126
  0.5 26.3 %collective-permute-start.1 = (bf16[288,1728]{1,0:T(8,128)(2,1)}, bf16[288,1728]{1,0:T(8,128)(2,1)}, u32[]{:S(2)}, u32[]{:S(2)}) collective-permute-start(bf16[288,1728]{1,0:T(8,128)(2,1)} %param.22), channel_id=1, source_target_pairs={{2,0},{3,1},{0,2},{1,3},{6,4},{7,5},{4,6},{5,7},{10,8},{11,9},{8,1... | collective-permute-start | bytes 2985992 | tf_op jit(solution)/shard_map/ppermute | solution.py:126
  6.3 1.1 copy-start.9
  6.3 1.2 copy-start.18
  6.3 1.3 %copy-start.19 = (s32[4]{0:T(128)S(1)}, s32[4]{0:T(128)}, u32[]{:S(2)}) copy-start(s32[4]{0:T(128)} %param.26) | copy-start | bytes 52
  6.3 1.4 %copy-start.20 = (s32[4]{0:T(128)S(1)}, s32[4]{0:T(128)}, u32[]{:S(2)}) copy-start(s32[4]{0:T(128)} %constant.118.clone) | copy-start | bytes 52
  6.3 2.1 %copy-start.13 = (s32[4,64]{1,0:T(4,128)S(1)}, s32[4,64]{1,0:T(4,128)}, u32[]{:S(2)}) copy-start(s32[4,64]{1,0:T(4,128)} %constant.119.clone) | copy-start | bytes 3076
  6.3 2.1 %copy-start.14 = (s32[4,64]{1,0:T(4,128)S(1)}, s32[4,64]{1,0:T(4,128)}, u32[]{:S(2)}) copy-start(s32[4,64]{1,0:T(4,128)} %constant.120.clone) | copy-start | bytes 3076
  6.4 2.2 %copy-start.11 = (s32[4,48]{1,0:T(4,128)S(1)}, s32[4,48]{1,0:T(4,128)}, u32[]{:S(2)}) copy-start(s32[4,48]{1,0:T(4,128)} %constant.124.clone) | copy-start | bytes 2308
  6.4 2.1 %copy-start.12 = (s32[4,48]{1,0:T(4,128)S(1)}, s32[4,48]{1,0:T(4,128)}, u32[]{:S(2)}) copy-start(s32[4,48]{1,0:T(4,128)} %constant.125.clone) | copy-start | bytes 2308
  6.4 2.2 %copy-start.16 = (s32[4,64]{1,0:T(4,128)S(1)}, s32[4,64]{1,0:T(4,128)}, u32[]{:S(2)}) copy-start(s32[4,64]{1,0:T(4,128)} %constant.132) | copy-start | bytes 3076
  6.4 2.3 %copy-start.15 = (pred[512,1]{0,1:T(4,128)(4,1)S(1)}, pred[512,1]{0,1:T(4,128)(4,1)}, u32[]{:S(2)}) copy-start(pred[512,1]{0,1:T(4,128)(4,1)} %constant.122.clone) | copy-start | bytes 1540
  13.6 1.6 %copy-start.5 = (bf16[288,1728]{1,0:T(8,128)(2,1)S(1)}, bf16[288,1728]{1,0:T(8,128)(2,1)}, u32[]{:S(2)}) copy-start(bf16[288,1728]{1,0:T(8,128)(2,1)} %param.22) | copy-start | bytes 2985988
  13.6 2.6 %copy-start.10 = (s32[4,48]{1,0:T(4,128)S(1)}, s32[4,48]{1,0:T(4,128)}, u32[]{:S(2)}) copy-start(s32[4,48]{1,0:T(4,128)} %constant.134) | copy-start | bytes 2308
  15.2 3.6 %copy-start.2 = (bf16[896,2,576]{0,2,1:T(8,128)(2,1)S(1)}, bf16[896,2,576]{0,2,1:T(8,128)(2,1)}, u32[]{:S(2)}) copy-start(bf16[896,2,576]{0,2,1:T(8,128)(2,1)} %add_convert_fusion.1) | copy-start | bytes 6193156
  18.8 8.0 %copy-start.1 = (bf16[1,1,896,1152]{3,2,1,0:T(8,128)(2,1)S(1)}, bf16[1,1,896,1152]{3,2,1,0:T(8,128)(2,1)}, u32[]{:S(2)}) copy-start(bf16[1,1,896,1152]{3,2,1,0:T(8,128)(2,1)} %param.20) | copy-start | bytes 6193156
  26.7 2.8 %collective-permute-start.2 = (bf16[288,1728]{1,0:T(8,128)(2,1)}, bf16[288,1728]{1,0:T(8,128)(2,1)S(1)}, u32[]{:S(2)}, u32[]{:S(2)}) collective-permute-start(bf16[288,1728]{1,0:T(8,128)(2,1)} %collective-permute-done.1), channel_id=1, source_target_pairs={{1,0},{0,1},{3,2},{2,3},{5,4},{4,5},{7,6},{6,7},{9,8},{8,9},{11,10... | collective-permute-start | bytes 2985992 | tf_op jit(solution)/shard_map/ppermute | solution.py:126
  29.6 31.0 %collective-permute-start.3 = (bf16[576,288]{0,1:T(8,128)(2,1)}, bf16[576,288]{0,1:T(8,128)(2,1)}, u32[]{:S(2)}, u32[]{:S(2)}) collective-permute-start(bf16[576,288]{0,1:T(8,128)(2,1)} %param.23), channel_id=1, source_target_pairs={{1,0},{0,1},{3,2},{2,3},{5,4},{4,5},{7,6},{6,7},{9,8},{8,9},{11,10... | collective-permute-start | bytes 995336 | tf_op jit(solution)/shard_map/ppermute | solution.py:76
  29.9 30.6 %collective-permute-start.4 = (bf16[576,288]{0,1:T(8,128)(2,1)}, bf16[576,288]{0,1:T(8,128)(2,1)}, u32[]{:S(2)}, u32[]{:S(2)}) collective-permute-start(bf16[576,288]{0,1:T(8,128)(2,1)} %param.23), channel_id=1, source_target_pairs={{2,0},{3,1},{0,2},{1,3},{6,4},{7,5},{4,6},{5,7},{10,8},{11,9},{8,1... | collective-permute-start | bytes 995336 | tf_op jit(solution)/shard_map/ppermute | solution.py:76
  32.8 1.1 copy-start.3
  57.3 3.3 %copy-start.4 = (bf16[4,576,288]{1,2,0:T(8,128)(2,1)S(1)}, bf16[4,576,288]{1,2,0:T(8,128)(2,1)}, u32[]{:S(2)}) copy-start(bf16[4,576,288]{1,2,0:T(8,128)(2,1)} %copy-done.3) | copy-start | bytes 3981316
  59.6 3.1 %copy-start.6 = (bf16[512,8,72]{0,2,1:T(8,128)(2,1)S(1)}, bf16[512,8,72]{0,2,1:T(8,128)(2,1)}, u32[]{:S(2)}) copy-start(bf16[512,8,72]{0,2,1:T(8,128)(2,1)} %copy.33) | copy-start | bytes 1769476
  59.6 3.1 %copy-start.7 = (bf16[256,1152]{1,0:T(8,128)(2,1)S(1)}, bf16[256,1152]{1,0:T(8,128)(2,1)}, u32[]{:S(2)}) copy-start(bf16[256,1152]{1,0:T(8,128)(2,1)} %get-tuple-element.41) | copy-start | bytes 1769476
  59.6 3.2 %copy-start.8 = (bf16[256,1152]{1,0:T(8,128)(2,1)S(1)}, bf16[256,1152]{1,0:T(8,128)(2,1)}, u32[]{:S(2)}) copy-start(bf16[256,1152]{1,0:T(8,128)(2,1)} %get-tuple-element.42) | copy-start | bytes 1769476
  60.6 2.1 %collective-permute-start.5 = (bf16[576,288]{0,1:T(8,128)(2,1)}, bf16[576,288]{0,1:T(8,128)(2,1)S(1)}, u32[]{:S(2)}, u32[]{:S(2)}) collective-permute-start(bf16[576,288]{0,1:T(8,128)(2,1)} %collective-permute-done.4), channel_id=1, source_target_pairs={{1,0},{0,1},{3,2},{2,3},{5,4},{4,5},{7,6},{6,7},{9,8},{8,9},{11,10... | collective-permute-start | bytes 995336 | tf_op jit(solution)/shard_map/ppermute | solution.py:76
  73.1 13.0 %copy-start.22 = (pred[512]{0:T(512)(128)(4,1)S(1)}, pred[512]{0:T(512)(128)(4,1)}, u32[]{:S(2)}) copy-start(pred[512]{0:T(512)(128)(4,1)} %constant.131) | copy-start | bytes 1540
  73.2 5.1 %collective-permute-start.6 = (bf16[64,1152]{1,0:T(8,128)(2,1)}, bf16[64,1152]{1,0:T(8,128)(2,1)S(1)}, u32[]{:S(2)}, u32[]{:S(2)}) collective-permute-start(bf16[64,1152]{1,0:T(8,128)(2,1)} %get-tuple-element.49), channel_id=1, source_target_pairs={{0,3},{1,0},{2,1},{3,2},{4,7},{5,4},{6,5},{7,6},{8,11},{9,8},{10,9... | collective-permute-start | bytes 442376 | tf_op jit(solution)/shard_map/ppermute | solution.py:203
  73.6 5.7 %collective-permute-start.7 = (bf16[64,1152]{1,0:T(8,128)(2,1)S(1)}, bf16[64,1152]{1,0:T(8,128)(2,1)S(1)}, u32[]{:S(2)}, u32[]{:S(2)}) collective-permute-start(bf16[64,1152]{1,0:T(8,128)(2,1)S(1)} %get-tuple-element.52), channel_id=1, source_target_pairs={{0,1},{1,2},{2,3},{3,0},{4,5},{5,6},{6,7},{7,4},{8,9},{9,10},{10,1... | collective-permute-start | bytes 442376 | tf_op jit(solution)/shard_map/ppermute | solution.py:203
  73.8 9.6 %collective-permute-start.8 = (bf16[64,1152]{1,0:T(8,128)(2,1)S(1)}, bf16[64,1152]{1,0:T(8,128)(2,1)S(1)}, u32[]{:S(2)}, u32[]{:S(2)}) collective-permute-start(bf16[64,1152]{1,0:T(8,128)(2,1)S(1)} %get-tuple-element.51), channel_id=1, source_target_pairs={{0,2},{1,3},{2,0},{3,1},{4,6},{5,7},{6,4},{7,5},{8,10},{9,11},{10,... | collective-permute-start | bytes 442376 | tf_op jit(solution)/shard_map/ppermute | solution.py:203
  75.4 10.7 %collective-permute-start.9 = (bf16[64,1152]{1,0:T(8,128)(2,1)S(1)}, bf16[64,1152]{1,0:T(8,128)(2,1)S(1)}, u32[]{:S(2)}, u32[]{:S(2)}) collective-permute-start(bf16[64,1152]{1,0:T(8,128)(2,1)S(1)} %get-tuple-element.50), channel_id=1, source_target_pairs={{0,2},{1,3},{2,0},{3,1},{4,6},{5,7},{6,4},{7,5},{8,10},{9,11},{10,... | collective-permute-start | bytes 442376 | tf_op jit(solution)/shard_map/ppermute | solution.py:203
  86.8 6.0 %copy-start.17 = (pred[384,1]{0,1:T(4,128)(4,1)S(1)}, pred[384,1]{0,1:T(4,128)(4,1)}, u32[]{:S(2)}) copy-start(pred[384,1]{0,1:T(4,128)(4,1)} %constant.127.clone) | copy-start | bytes 1156
  87.0 20.8 %collective-permute-start.10 = (bf16[256,1152]{1,0:T(8,128)(2,1)S(1)}, bf16[256,1152]{1,0:T(8,128)(2,1)}, u32[]{:S(2)}, u32[]{:S(2)}) collective-permute-start(bf16[256,1152]{1,0:T(8,128)(2,1)S(1)} %get-tuple-element.31), channel_id=1, source_target_pairs={{0,4},{4,8},{8,12},{1,5},{5,9},{9,13},{2,6},{6,10},{10,14},{3,7},{... | collective-permute-start | bytes 1769480 | tf_op jit(solution)/shard_map/ppermute | solution.py:233
  91.5 16.7 %collective-permute-start.11 = (bf16[256,1152]{1,0:T(8,128)(2,1)S(1)}, bf16[256,1152]{1,0:T(8,128)(2,1)S(1)}, u32[]{:S(2)}, u32[]{:S(2)}) collective-permute-start(bf16[256,1152]{1,0:T(8,128)(2,1)S(1)} %get-tuple-element.26), channel_id=1, source_target_pairs={{4,0},{8,4},{12,8},{5,1},{9,5},{13,9},{6,2},{10,6},{14,10},{7,3},{... | collective-permute-start | bytes 1769480 | tf_op jit(solution)/shard_map/ppermute | solution.py:234
  108.7 8.9 %copy-start.21 = (pred[384]{0:T(512)(128)(4,1)S(1)}, pred[384]{0:T(512)(128)(4,1)}, u32[]{:S(2)}) copy-start(pred[384]{0:T(512)(128)(4,1)} %constant.133) | copy-start | bytes 1156
  108.8 4.3 %collective-permute-start.12 = (bf16[48,1152]{1,0:T(8,128)(2,1)S(1)}, bf16[48,1152]{1,0:T(8,128)(2,1)S(1)}, u32[]{:S(2)}, u32[]{:S(2)}) collective-permute-start(bf16[48,1152]{1,0:T(8,128)(2,1)S(1)} %get-tuple-element.53), channel_id=1, source_target_pairs={{0,3},{1,0},{2,1},{3,2},{4,7},{5,4},{6,5},{7,6},{8,11},{9,8},{10,9... | collective-permute-start | bytes 331784 | tf_op jit(solution)/shard_map/ppermute | solution.py:203
  108.8 5.2 %collective-permute-start.13 = (bf16[48,1152]{1,0:T(8,128)(2,1)S(1)}, bf16[48,1152]{1,0:T(8,128)(2,1)S(1)}, u32[]{:S(2)}, u32[]{:S(2)}) collective-permute-start(bf16[48,1152]{1,0:T(8,128)(2,1)S(1)} %get-tuple-element.56), channel_id=1, source_target_pairs={{0,1},{1,2},{2,3},{3,0},{4,5},{5,6},{6,7},{7,4},{8,9},{9,10},{10,1... | collective-permute-start | bytes 331784 | tf_op jit(solution)/shard_map/ppermute | solution.py:203
  109.3 5.9 %collective-permute-start.14 = (bf16[48,1152]{1,0:T(8,128)(2,1)S(1)}, bf16[48,1152]{1,0:T(8,128)(2,1)S(1)}, u32[]{:S(2)}, u32[]{:S(2)}) collective-permute-start(bf16[48,1152]{1,0:T(8,128)(2,1)S(1)} %get-tuple-element.55), channel_id=1, source_target_pairs={{0,2},{1,3},{2,0},{3,1},{4,6},{5,7},{6,4},{7,5},{8,10},{9,11},{10,... | collective-permute-start | bytes 331784 | tf_op jit(solution)/shard_map/ppermute | solution.py:203
  110.1 7.6 %collective-permute-start.15 = (bf16[48,1152]{1,0:T(8,128)(2,1)S(1)}, bf16[48,1152]{1,0:T(8,128)(2,1)S(1)}, u32[]{:S(2)}, u32[]{:S(2)}) collective-permute-start(bf16[48,1152]{1,0:T(8,128)(2,1)S(1)} %get-tuple-element.54), channel_id=1, source_target_pairs={{0,2},{1,3},{2,0},{3,1},{4,6},{5,7},{6,4},{7,5},{8,10},{9,11},{10,... | collective-permute-start | bytes 331784 | tf_op jit(solution)/shard_map/ppermute | solution.py:203

commit v11 on v10

--- a/solution.py
+++ b/solution.py
@@ -30,11 +30,8 @@
     return (normed * (1.0 + modulation[1]) + modulation[0]).astype(jnp.bfloat16)
 
 
-HEADS_PER_STEP = 2
-
-
 def attention_kernel(q_ref, k_ref, v_ref, o_ref):
-    for j in range(HEADS_PER_STEP):
+    for j in range(q_ref.shape[0]):
         scores = jnp.dot(q_ref[j], k_ref[j], preferred_element_type=jnp.float32) * (
             1.0 / math.sqrt(HD)
         )
@@ -42,28 +39,18 @@
         weights = jnp.exp(scores - row_max)
         row_sum = jnp.sum(weights, axis=-1, keepdims=True)
         probabilities = (weights * (1.0 / row_sum)).astype(jnp.bfloat16)
-        o_ref[j] = jnp.dot(probabilities, v_ref[j], preferred_element_type=jnp.float32).astype(
-            o_ref.dtype
-        )
+        o_ref[:, j * HD : (j + 1) * HD] = jnp.dot(
+            probabilities, v_ref[j], preferred_element_type=jnp.float32
+        ).astype(o_ref.dtype)
 
 
 def attend_project(queries, keys, values, w_out_full, block_in, gate):
     heads, size, tokens = keys.shape
     chunk = queries.shape[1]
-    hb = HEADS_PER_STEP
     mixed = pl.pallas_call(
         attention_kernel,
-        grid=(heads // hb,),
-        in_specs=[
-            pl.BlockSpec((hb, chunk, size), lambda h: (h, 0, 0)),
-            pl.BlockSpec((hb, size, tokens), lambda h: (h, 0, 0)),
-            pl.BlockSpec((hb, tokens, size), lambda h: (h, 0, 0)),
-        ],
-        out_specs=pl.BlockSpec((hb, chunk, size), lambda h: (h, 0, 0)),
-        out_shape=jax.ShapeDtypeStruct(queries.shape, queries.dtype),
-        compiler_params=pltpu.CompilerParams(dimension_semantics=("arbitrary",)),
+        out_shape=jax.ShapeDtypeStruct((chunk, heads * size), queries.dtype),
     )(queries, keys, values)
-    mixed = mixed.transpose(1, 0, 2).reshape(chunk, heads * size)
     projected = jnp.dot(mixed, w_out_full, preferred_element_type=jnp.float32)
     return (block_in.astype(jnp.float32) + gate * projected).astype(block_in.dtype)
 

time: 121 us -> 137 us (1.13)
  local copies, waits for them, and re-layouts: 31.5 us -> 45.5 us
  other arithmetic: 15.1 us -> 19.6 us
  waiting for transfers between devices: 16.4 us -> 13.3 us
    transpose x3 -> x0, local copies, waits for them, and re-layouts: 5.37 us -> none  [attend_project(): mixed = mixed.transpose(1, 0, 2).reshape(chunk, heads * size)]
    unnamed x50 -> x76, local copies, waits for them, and re-layouts: 8.79 us -> 11.7 us
    ppermute x6, waiting for transfers between devices: 3.61 us -> 0.85 us  [fetch(): return lax.ppermute(x, 'face', [(src_of(i), i) for i in range(n)])]
    mul x2, local copies, waits for them, and re-layouts: 0.15 us -> 2.66 us  [per_device(): pass_low * lower.astype(jnp.float32).reshape(blocks)]
    mul x2, local copies, waits for them, and re-layouts: 0.15 us -> 2.6 us  [per_device(): hold_low * low_f + pass_low * lower.astype(jnp.float32).reshape(blocks)]
    mul x2, local copies, waits for them, and re-layouts: 0.15 us -> 2.59 us  [per_device(): pass_high * upper.astype(jnp.float32).reshape(blocks)]
    mul x2, local copies, waits for them, and re-layouts: 0.15 us -> 2.57 us  [per_device(): hold_high * high_f + pass_high * upper.astype(jnp.float32).reshape(blocks)]
    eq x2, local copies, waits for them, and re-layouts: 0.16 us -> 2.02 us  [strips_out(): pick = (send_cells[:, None] == token_ids[None, :]).astype(jnp.bfloat16)]
  transfers between devices with their start and end apart: 16 -> 16, of which waited for: 9 -> 7; matrix products, arithmetic and copies ran while one was open for 45% -> 52% of each run, Pallas kernels for 15% -> 13%
where the time goes in v11:
time: 137 us; the launch traced here: 136 us
  local copies, waits for them, and re-layouts  45.5 us (33%)
  Pallas kernels  25.4 us (19%)
  other arithmetic  19.6 us (14%)
  starting transfers between devices  16.2 us (12%)
  matrix products  15.2 us (11%)
  waiting for transfers between devices  13.3 us (10%)
    pallas_call x3, Pallas kernels, attend_project(): pl.pallas_call(attention_kernel, out_shape=jax.ShapeDtypeStruct((chunk, h...  25.4 us
    ppermute x8, waiting for transfers between devices, strips_in(): lax.ppermute(sent, 'face', [(i, (i + shift) % n) for i in range(n)])  12.4 us
    unnamed x76, local copies, waits for them, and re-layouts  11.7 us
    dot_general x2, matrix products, chip_part(): jnp.dot(lax.dynamic_index_in_dim(moved_chips, chip, 0, keepdims=False), w...  7.76 us
    select_n x2, other arithmetic, space_blend(): w_keep = jnp.where(dep == 0, keep[0], keep[1])  6.21 us
    ppermute x8, starting transfers between devices, strips_in(): lax.ppermute(sent, 'face', [(i, (i + shift) % n) for i in range(n)])  5.21 us
    dot_general x3, matrix products, attend_project(): projected = jnp.dot(mixed, w_out_full, preferred_element_type=jnp.float32)  5.14 us
    ppermute x6, starting transfers between devices, fetch(): return lax.ppermute(x, 'face', [(src_of(i), i) for i in range(n)])  5.1 us
  transfers between devices with their start and end apart: 16, of which 7 were waited for; matrix products, arithmetic and copies ran while one was open for 52% of the time, Pallas kernels for 13%

profile of v11, /device:TPU:0, one launch (start us, length us, event | category | flops | bytes accessed | tf_op | source)
XLA Modules:
  0.0 135.8 jit_solution(5600629281384097163)
XLA Ops:
  0.5 2.6 %collective-permute-start.1 = (bf16[288,1728]{1,0:T(8,128)(2,1)}, bf16[288,1728]{1,0:T(8,128)(2,1)}, u32[]{:S(2)}, u32[]{:S(2)}) collective-permute-start(bf16[288,1728]{1,0:T(8,128)(2,1)} %param.22), channel_id=1, source_target_pairs={{2,0},{3,1},{0,2},{1,3},{6,4},{7,5},{4,6},{5,7},{10,8},{11,9},{8,1... | collective-permute-start | bytes 2985992 | tf_op jit(solution)/shard_map/ppermute | solution.py:113
  3.4 2.9 %copy.27 = bf16[1,1,896,1152]{2,3,1,0:T(8,128)(2,1)S(1)} copy(bf16[1,1,896,1152]{3,2,1,0:T(8,128)(2,1)} %param.20) | data formatting | bytes 4128768 | tf_op args[0]
  9.3 3.1 %broadcast_select_fusion.1 = (f32[512,1]{0,1:T(1,128)}, f32[512,1]{0,1:T(1,128)}) fusion(pred[512,1]{0,1:T(4,128)(4,1)S(1)} %copy-done.26, f32[]{:T(128)} %bitcast.14, f32[]{:T(128)} %bitcast.13, f32[]{:T(128)} %bitcast.30, f32[]{:T(128)} %bitcast.29), kind=kLoop, calls=%fused_computation.93 | loop fusion | flops 1024 | bytes 4624 | tf_op jit(solution)/shard_map/jit(_where)/select_n | solution.py:204
  13.2 2.1 %add_convert_fusion.1 = bf16[896,2,576]{0,2,1:T(8,128)(2,1)} fusion(f32[2,576]{1,0:T(2,128)S(1)} %add.118, f32[2,576]{1,0:T(2,128)S(1)} %mul.141, f32[896]{0:T(1024)S(1)} %add_rsqrt_fusion, f32[896]{0:T(1024)S(1)} %broadcast_multiply_fusion, bf16[896,2,576]{0,2,1:T(8,128)(2,1)S(1)} %bitcast.77), kind=kLoop, calls=%fused_computation.4 | loop fusion | flops 6193152 | bytes 4145152 | tf_op jit(solution)/shard_map/convert_element_type | solution.py:30
  18.6 1.3 bitcast_dynamic-update-slice_fusion.2
  20.0 1.3 copy-done.3
  21.3 4.9 %fusion.20 = f32[896,1728]{0,1:T(8,128)S(1)} fusion(bf16[576,1728]{1,0:T(8,128)(2,1)} %bitcast.88, bf16[896,2,576]{0,2,1:T(8,128)(2,1)} %add_convert_fusion.1, s32[]{:T(128)S(6)} %select_n.115), kind=kOutput, calls=%fused_computation.44 | convolution fusion | flops 1783627776 | bytes 9289732 | tf_op jit(solution)/shard_map/dot_general | solution.py:124
  26.7 1.1 slice_bitcast_fusion.2
  28.0 1.3 bitcast_dynamic-update-slice_fusion.1
  29.9 1.7 %collective-permute-start.4 = (bf16[576,288]{0,1:T(8,128)(2,1)}, bf16[576,288]{0,1:T(8,128)(2,1)}, u32[]{:S(2)}, u32[]{:S(2)}) collective-permute-start(bf16[576,288]{0,1:T(8,128)(2,1)} %param.23), channel_id=1, source_target_pairs={{2,0},{3,1},{0,2},{1,3},{6,4},{7,5},{4,6},{5,7},{10,8},{11,9},{8,1... | collective-permute-start | bytes 995336 | tf_op jit(solution)/shard_map/ppermute | solution.py:63
  32.9 2.9 %fusion.18 = f32[896,1728]{0,1:T(8,128)S(1)} fusion(bf16[576,1728]{1,0:T(8,128)(2,1)S(1)} %bitcast.87, bf16[896,2,576]{0,2,1:T(8,128)(2,1)S(1)} %copy-done.2, s32[]{:T(128)S(6)} %select_n.119), kind=kOutput, calls=%fused_computation.40 | convolution fusion | flops 1783627776 | bytes 9289732 | tf_op jit(solution)/shard_map/dot_general | solution.py:124
  36.6 1.7 %fusion.40 = (bf16[896,1,8,72]{0,3,2,1:T(8,128)(2,1)}, bf16[896,1,8,72]{0,3,2,1:T(8,128)(2,1)}, bf16[8,72,896]{2,1,0:T(8,128)(2,1)}) fusion(bf16[896,3,8,72]{0,3,2,1:T(8,128)(2,1)S(1)} %bitcast.84), kind=kLoop, calls=%fused_computation.101 | loop fusion | bytes 6193152 | tf_op jit(solution)/shard_map/slice | solution.py:155
  38.3 2.6 %copy.30 = bf16[896,1,8,72]{3,0,2,1:T(8,128)(2,1)} copy(bf16[896,1,8,72]{0,3,2,1:T(8,128)(2,1)} %get-tuple-element.39) | data formatting | bytes 2064384
  40.9 2.3 %fusion.42 = (bf16[8,256,72]{2,1,0:T(8,128)(2,1)}, bf16[8,256,72]{2,1,0:T(8,128)(2,1)}) fusion(bf16[8,896,72]{2,1,0:T(8,128)(2,1)} %bitcast.85), kind=kLoop, calls=%fused_computation.103 | loop fusion | bytes 1179648 | tf_op jit(solution)/shard_map/slice | solution.py:209
  43.2 2.6 %copy.31 = bf16[896,1,8,72]{3,0,2,1:T(8,128)(2,1)} copy(bf16[896,1,8,72]{0,3,2,1:T(8,128)(2,1)} %get-tuple-element.38) | data formatting | bytes 2064384
  45.8 2.4 %pad_maximum_fusion.q_ref = bf16[8,512,72]{2,1,0:T(8,128)(2,1)} fusion(bf16[8,256,72]{2,1,0:T(8,128)(2,1)} %get-tuple-element.46, bf16[8,256,72]{2,1,0:T(8,128)(2,1)} %get-tuple-element.45), kind=kLoop, calls=%fused_computation.36 | loop fusion | flops 1179648 | bytes 1179648 | tf_op jit(solution)/shard_map/concatenate | solution.py:209
  48.2 11.2 %shard_map.190 = bf16[512,576]{1,0:T(8,128)(2,1)} custom-call(bf16[8,512,72]{2,1,0:T(8,128)(2,1)} %pad_maximum_fusion.q_ref, bf16[8,72,896]{2,1,0:T(8,128)(2,1)} %get-tuple-element.40.k_ref, bf16[8,896,72]{2,1,0:T(8,128)(2,1)} %bitcast.78), custom_call_target="tpu_custom_call" | custom-call | tf_op jit(solution)/shard_map/pallas_call | solution.py:50
  59.4 2.2 %fusion.41 = (bf16[8,192,72]{2,1,0:T(8,128)(2,1)}, bf16[8,192,72]{2,1,0:T(8,128)(2,1)}) fusion(bf16[8,896,72]{2,1,0:T(8,128)(2,1)} %bitcast.86), kind=kLoop, calls=%fused_computation.102 | loop fusion | bytes 884736 | tf_op jit(solution)/shard_map/slice | solution.py:214
  63.8 1.2 fusion.7
  66.4 7.2 %shard_map.191 = bf16[192,576]{1,0:T(8,128)(2,1)} custom-call(bf16[8,192,72]{2,1,0:T(8,128)(2,1)} %get-tuple-element.22.q_ref, bf16[8,72,896]{2,1,0:T(8,128)(2,1)} %get-tuple-element.40.k_ref, bf16[8,896,72]{2,1,0:T(8,128)(2,1)} %bitcast.79), custom_call_target="tpu_custom_call" | custom-call | tf_op jit(solution)/shard_map/pallas_call | solution.py:50
  74.3 1.6 %collective-permute-start.8 = (bf16[64,1152]{1,0:T(8,128)(2,1)}, bf16[64,1152]{1,0:T(8,128)(2,1)S(1)}, u32[]{:S(2)}, u32[]{:S(2)}) collective-permute-start(bf16[64,1152]{1,0:T(8,128)(2,1)} %get-tuple-element.51), channel_id=1, source_target_pairs={{0,2},{1,3},{2,0},{3,1},{4,6},{5,7},{6,4},{7,5},{8,10},{9,11},{10,... | collective-permute-start | bytes 442376 | tf_op jit(solution)/shard_map/ppermute | solution.py:190
  76.3 2.3 %fusion.12 = bf16[192,1152]{1,0:T(8,128)(2,1)} fusion(bf16[192,576]{1,0:T(8,128)(2,1)} %shard_map.191, bf16[576,1152]{0,1:T(8,128)(2,1)S(1)} %bitcast.82, f32[1152]{0:T(1024)S(1)} %get-tuple-element.33, bf16[1,1,896,1152]{3,2,1,0:T(8,128)(2,1)S(1)} %copy-done.1), kind=kOutput, calls=%fused_computation.22 | convolution fusion | flops 255688704 | bytes 2437632 | tf_op jit(solution)/shard_map/dot_general | solution.py:54
  78.6 1.5 %collective-permute-done.7 = bf16[64,1152]{1,0:T(8,128)(2,1)S(1)} collective-permute-done((bf16[64,1152]{1,0:T(8,128)(2,1)}, bf16[64,1152]{1,0:T(8,128)(2,1)S(1)}, u32[]{:S(2)}, u32[]{:S(2)}) %collective-permute-start.7) | collective-permute-done | bytes 147488 | tf_op jit(solution)/shard_map/ppermute | solution.py:190
  80.2 3.7 %collective-permute-done.8 = bf16[64,1152]{1,0:T(8,128)(2,1)S(1)} collective-permute-done((bf16[64,1152]{1,0:T(8,128)(2,1)}, bf16[64,1152]{1,0:T(8,128)(2,1)S(1)}, u32[]{:S(2)}, u32[]{:S(2)}) %collective-permute-start.8) | collective-permute-done | bytes 147488 | tf_op jit(solution)/shard_map/ppermute | solution.py:190
  83.9 2.9 %collective-permute-done.9 = bf16[64,1152]{1,0:T(8,128)(2,1)S(1)} collective-permute-done((bf16[64,1152]{1,0:T(8,128)(2,1)}, bf16[64,1152]{1,0:T(8,128)(2,1)S(1)}, u32[]{:S(2)}, u32[]{:S(2)}) %collective-permute-start.9) | collective-permute-done | bytes 147488 | tf_op jit(solution)/shard_map/ppermute | solution.py:190
  87.6 1.1 fusion.43
  88.7 4.6 %collective-permute-start.10 = (bf16[256,1152]{1,0:T(8,128)(2,1)}, bf16[256,1152]{1,0:T(8,128)(2,1)}, u32[]{:S(2)}, u32[]{:S(2)}) collective-permute-start(bf16[256,1152]{1,0:T(8,128)(2,1)} %get-tuple-element.31), channel_id=1, source_target_pairs={{0,4},{4,8},{8,12},{1,5},{5,9},{9,13},{2,6},{6,10},{10,14},{3,7},{... | collective-permute-start | bytes 1769480 | tf_op jit(solution)/shard_map/ppermute | solution.py:220
  93.3 1.3 collective-permute-start.11
  94.6 3.1 %select_reduce_fusion.5 = (f32[384]{0:T(512)}, f32[384]{0:T(512)}) fusion(pred[384,1]{0,1:T(4,128)(4,1)S(1)} %copy-done.28, f32[]{:T(128)} %bitcast.14, f32[]{:T(128)} %bitcast.13, f32[]{:T(128)} %bitcast.30, f32[]{:T(128)} %bitcast.29), kind=kLoop, calls=%fused_computation.90 | loop fusion | flops 768 | bytes 3472 | tf_op jit(solution)/shard_map/jit(_where)/select_n | solution.py:204
  97.7 1.2 rev.18
  98.9 1.3 mul.136
  100.2 1.3 mul.137
  101.5 1.3 rev.19
  102.8 1.3 mul.156
  104.1 1.3 mul.157
  105.5 1.4 eq.116
  106.8 1.3 eq.113
  108.2 1.2 mul.167
  109.4 1.3 mul.168
  110.7 1.3 mul.171
  112.1 1.3 mul.172
  113.3 7.0 %shard_map.192 = bf16[192,576]{1,0:T(8,128)(2,1)} custom-call(bf16[8,192,72]{2,1,0:T(8,128)(2,1)} %get-tuple-element.27.q_ref, bf16[8,72,896]{2,1,0:T(8,128)(2,1)} %get-tuple-element.40.k_ref, bf16[8,896,72]{2,1,0:T(8,128)(2,1)} %bitcast.80), custom_call_target="tpu_custom_call" | custom-call | tf_op jit(solution)/shard_map/pallas_call | solution.py:50
  121.4 1.6 %fusion.13 = bf16[192,1152]{1,0:T(8,128)(2,1)S(1)} fusion(bf16[192,576]{1,0:T(8,128)(2,1)} %shard_map.192, bf16[576,1152]{0,1:T(8,128)(2,1)S(1)} %bitcast.83, bf16[1,1,896,1152]{3,2,1,0:T(8,128)(2,1)S(1)} %copy-done.1, f32[1152]{0:T(1024)S(1)} %get-tuple-element.33), kind=kOutput, calls=%fused_computation.23 | convolution fusion | flops 255688704 | bytes 2437632 | tf_op jit(solution)/shard_map/dot_general | solution.py:54
  126.2 1.6 %fusion.15 = bf16[256,1152]{1,0:T(8,128)(2,1)S(1)} fusion(bf16[256,1152]{1,0:T(8,128)(2,1)} %get-tuple-element.26, bf16[256,1152]{1,0:T(8,128)(2,1)} %collective-permute-done.10, f32[256]{0:T(256)S(1)} %copy-done.13, f32[256]{0:T(256)S(1)} %copy-done.12, pred[]{:T(512)S(6)} %gt.7), kind=kLoop, calls=%fused_computation.33 | loop fusion | flops 2064384 | bytes 1771521 | tf_op jit(solution)/shard_map/convert_element_type | solution.py:250
  127.8 1.6 %fusion.17 = bf16[256,1152]{1,0:T(8,128)(2,1)S(1)} fusion(bf16[256,1152]{1,0:T(8,128)(2,1)} %get-tuple-element.31, bf16[256,1152]{1,0:T(8,128)(2,1)} %collective-permute-done.11, f32[256]{0:T(256)S(1)} %copy-done.15, f32[256]{0:T(256)S(1)} %copy-done.14, pred[]{:T(512)S(6)} %lt.56), kind=kLoop, calls=%fused_computation.35 | loop fusion | flops 2064384 | bytes 1771521 | tf_op jit(solution)/shard_map/convert_element_type | solution.py:250
  129.4 1.9 %collective-permute-done.14 = bf16[48,1152]{1,0:T(8,128)(2,1)S(1)} collective-permute-done((bf16[48,1152]{1,0:T(8,128)(2,1)S(1)}, bf16[48,1152]{1,0:T(8,128)(2,1)S(1)}, u32[]{:S(2)}, u32[]{:S(2)}) %collective-permute-start.14) | collective-permute-done | bytes 110624 | tf_op jit(solution)/shard_map/ppermute | solution.py:190
  131.4 2.4 %collective-permute-done.15 = bf16[48,1152]{1,0:T(8,128)(2,1)S(1)} collective-permute-done((bf16[48,1152]{1,0:T(8,128)(2,1)S(1)}, bf16[48,1152]{1,0:T(8,128)(2,1)S(1)}, u32[]{:S(2)}, u32[]{:S(2)}) %collective-permute-start.15) | collective-permute-done | bytes 110624 | tf_op jit(solution)/shard_map/ppermute | solution.py:190
  134.3 1.5 %maximum_bitcast_fusion = bf16[1,1,896,1152]{3,2,1,0:T(8,128)(2,1)} fusion(bf16[256,1152]{1,0:T(8,128)(2,1)S(1)} %fusion.17, bf16[384,1152]{1,0:T(8,128)(2,1)S(1)} %fusion.9, bf16[256,1152]{1,0:T(8,128)(2,1)S(1)} %fusion.15), kind=kLoop, calls=%fused_computation.26 | loop fusion | flops 6193152 | bytes 4128768 | tf_op jit(solution)/shard_map/reshape | solution.py:252
  (137 shorter events, 21.3 us)
Async XLA Ops:
  0.0 3.0 %copy-start = (s32[4,4,4]{2,1,0:T(4,128)S(1)}, s32[4,4,4]{2,1,0:T(4,128)}, u32[]{:S(2)}) copy-start(s32[4,4,4]{2,1,0:T(4,128)} %param.24) | copy-start | bytes 772
  0.0 18.6 %collective-permute-start = (bf16[288,1728]{1,0:T(8,128)(2,1)}, bf16[288,1728]{1,0:T(8,128)(2,1)}, u32[]{:S(2)}, u32[]{:S(2)}) collective-permute-start(bf16[288,1728]{1,0:T(8,128)(2,1)} %param.22), channel_id=1, source_target_pairs={{1,0},{0,1},{3,2},{2,3},{5,4},{4,5},{7,6},{6,7},{9,8},{8,9},{11,10... | collective-permute-start | bytes 2985992 | tf_op jit(solution)/shard_map/ppermute | solution.py:113
  0.5 26.3 %collective-permute-start.1 = (bf16[288,1728]{1,0:T(8,128)(2,1)}, bf16[288,1728]{1,0:T(8,128)(2,1)}, u32[]{:S(2)}, u32[]{:S(2)}) collective-permute-start(bf16[288,1728]{1,0:T(8,128)(2,1)} %param.22), channel_id=1, source_target_pairs={{2,0},{3,1},{0,2},{1,3},{6,4},{7,5},{4,6},{5,7},{10,8},{11,9},{8,1... | collective-permute-start | bytes 2985992 | tf_op jit(solution)/shard_map/ppermute | solution.py:113
  6.3 1.3 copy-start.32
  6.3 2.0 %copy-start.33 = (s32[4]{0:T(128)S(1)}, s32[4]{0:T(128)}, u32[]{:S(2)}) copy-start(s32[4]{0:T(128)} %constant.118.clone) | copy-start | bytes 52
  6.3 2.7 %copy-start.20 = (s32[4,64]{1,0:T(4,128)S(1)}, s32[4,64]{1,0:T(4,128)}, u32[]{:S(2)}) copy-start(s32[4,64]{1,0:T(4,128)} %constant.119.clone) | copy-start | bytes 3076
  6.3 2.7 %copy-start.21 = (s32[4,64]{1,0:T(4,128)S(1)}, s32[4,64]{1,0:T(4,128)}, u32[]{:S(2)}) copy-start(s32[4,64]{1,0:T(4,128)} %constant.120.clone) | copy-start | bytes 3076
  6.4 2.7 %copy-start.18 = (s32[4,48]{1,0:T(4,128)S(1)}, s32[4,48]{1,0:T(4,128)}, u32[]{:S(2)}) copy-start(s32[4,48]{1,0:T(4,128)} %constant.124.clone) | copy-start | bytes 2308
  6.4 2.7 %copy-start.19 = (s32[4,48]{1,0:T(4,128)S(1)}, s32[4,48]{1,0:T(4,128)}, u32[]{:S(2)}) copy-start(s32[4,48]{1,0:T(4,128)} %constant.125.clone) | copy-start | bytes 2308
  6.4 2.8 %copy-start.27 = (s32[4,64]{1,0:T(4,128)S(1)}, s32[4,64]{1,0:T(4,128)}, u32[]{:S(2)}) copy-start(s32[4,64]{1,0:T(4,128)} %constant.132) | copy-start | bytes 3076
  6.4 2.9 %copy-start.26 = (pred[512,1]{0,1:T(4,128)(4,1)S(1)}, pred[512,1]{0,1:T(4,128)(4,1)}, u32[]{:S(2)}) copy-start(pred[512,1]{0,1:T(4,128)(4,1)} %constant.122.clone) | copy-start | bytes 1540
  15.3 1.3 copy-start.17
  19.9 1.3 copy-start.3
  21.3 5.5 %copy-start.1 = (bf16[1,1,896,1152]{3,2,1,0:T(8,128)(2,1)S(1)}, bf16[1,1,896,1152]{3,2,1,0:T(8,128)(2,1)}, u32[]{:S(2)}) copy-start(bf16[1,1,896,1152]{3,2,1,0:T(8,128)(2,1)} %param.20) | copy-start | bytes 6193156
  26.7 2.8 %collective-permute-start.2 = (bf16[288,1728]{1,0:T(8,128)(2,1)}, bf16[288,1728]{1,0:T(8,128)(2,1)S(1)}, u32[]{:S(2)}, u32[]{:S(2)}) collective-permute-start(bf16[288,1728]{1,0:T(8,128)(2,1)} %collective-permute-done.1), channel_id=1, source_target_pairs={{1,0},{0,1},{3,2},{2,3},{5,4},{4,5},{7,6},{6,7},{9,8},{8,9},{11,10... | collective-permute-start | bytes 2985992 | tf_op jit(solution)/shard_map/ppermute | solution.py:113
  29.3 3.6 %copy-start.2 = (bf16[896,2,576]{0,2,1:T(8,128)(2,1)S(1)}, bf16[896,2,576]{0,2,1:T(8,128)(2,1)}, u32[]{:S(2)}) copy-start(bf16[896,2,576]{0,2,1:T(8,128)(2,1)} %add_convert_fusion.1) | copy-start | bytes 6193156
  29.6 32.0 %collective-permute-start.3 = (bf16[576,288]{0,1:T(8,128)(2,1)}, bf16[576,288]{0,1:T(8,128)(2,1)}, u32[]{:S(2)}, u32[]{:S(2)}) collective-permute-start(bf16[576,288]{0,1:T(8,128)(2,1)} %param.23), channel_id=1, source_target_pairs={{1,0},{0,1},{3,2},{2,3},{5,4},{4,5},{7,6},{6,7},{9,8},{8,9},{11,10... | collective-permute-start | bytes 995336 | tf_op jit(solution)/shard_map/ppermute | solution.py:63
  29.9 31.7 %collective-permute-start.4 = (bf16[576,288]{0,1:T(8,128)(2,1)}, bf16[576,288]{0,1:T(8,128)(2,1)}, u32[]{:S(2)}, u32[]{:S(2)}) collective-permute-start(bf16[576,288]{0,1:T(8,128)(2,1)} %param.23), channel_id=1, source_target_pairs={{2,0},{3,1},{0,2},{1,3},{6,4},{7,5},{4,6},{5,7},{10,8},{11,9},{8,1... | collective-permute-start | bytes 995336 | tf_op jit(solution)/shard_map/ppermute | solution.py:63
  59.4 4.4 %copy-start.7 = (bf16[512,576]{1,0:T(8,128)(2,1)S(1)}, bf16[512,576]{1,0:T(8,128)(2,1)}, u32[]{:S(2)}) copy-start(bf16[512,576]{1,0:T(8,128)(2,1)} %shard_map.190) | copy-start | bytes 1769476
  59.4 4.4 %copy-start.8 = (bf16[256,1152]{1,0:T(8,128)(2,1)S(1)}, bf16[256,1152]{1,0:T(8,128)(2,1)}, u32[]{:S(2)}) copy-start(bf16[256,1152]{1,0:T(8,128)(2,1)} %get-tuple-element.41) | copy-start | bytes 1769476
  59.4 4.4 %copy-start.9 = (bf16[256,1152]{1,0:T(8,128)(2,1)S(1)}, bf16[256,1152]{1,0:T(8,128)(2,1)}, u32[]{:S(2)}) copy-start(bf16[256,1152]{1,0:T(8,128)(2,1)} %get-tuple-element.42) | copy-start | bytes 1769476
  61.6 2.1 %collective-permute-start.5 = (bf16[576,288]{0,1:T(8,128)(2,1)}, bf16[576,288]{0,1:T(8,128)(2,1)S(1)}, u32[]{:S(2)}, u32[]{:S(2)}) collective-permute-start(bf16[576,288]{0,1:T(8,128)(2,1)} %collective-permute-done.4), channel_id=1, source_target_pairs={{1,0},{0,1},{3,2},{2,3},{5,4},{4,5},{7,6},{6,7},{9,8},{8,9},{11,10... | collective-permute-start | bytes 995336 | tf_op jit(solution)/shard_map/ppermute | solution.py:63
  65.0 1.4 %copy-start.4 = (bf16[512,1152]{1,0:T(8,128)(2,1)}, bf16[512,1152]{1,0:T(8,128)(2,1)S(1)}, u32[]{:S(2)}) copy-start(bf16[512,1152]{1,0:T(8,128)(2,1)S(1)} %fusion.7) | copy-start | bytes 3538948
  73.6 13.2 %copy-start.5 = (bf16[512,1152]{1,0:T(8,128)(2,1)S(1)}, bf16[512,1152]{1,0:T(8,128)(2,1)}, u32[]{:S(2)}) copy-start(bf16[512,1152]{1,0:T(8,128)(2,1)} %copy-done.4) | copy-start | bytes 3538948
  73.6 13.2 %copy-start.22 = (f32[512,1]{0,1:T(1,128)S(1)}, f32[512,1]{0,1:T(1,128)}, u32[]{:S(2)}) copy-start(f32[512,1]{0,1:T(1,128)} %get-tuple-element.57) | copy-start | bytes 6148
  73.6 13.2 %copy-start.23 = (f32[512,1]{0,1:T(1,128)S(1)}, f32[512,1]{0,1:T(1,128)}, u32[]{:S(2)}) copy-start(f32[512,1]{0,1:T(1,128)} %get-tuple-element.58) | copy-start | bytes 6148
  73.6 13.2 %copy-start.29 = (s32[256]{0:T(256)S(1)}, s32[256]{0:T(256)}, u32[]{:S(2)}) copy-start(s32[256]{0:T(256)} %eq.103) | copy-start | bytes 3076
  73.6 13.2 %copy-start.35 = (pred[512]{0:T(512)(128)(4,1)S(1)}, pred[512]{0:T(512)(128)(4,1)}, u32[]{:S(2)}) copy-start(pred[512]{0:T(512)(128)(4,1)} %constant.131) | copy-start | bytes 1540
  73.7 5.0 %collective-permute-start.6 = (bf16[64,1152]{1,0:T(8,128)(2,1)}, bf16[64,1152]{1,0:T(8,128)(2,1)S(1)}, u32[]{:S(2)}, u32[]{:S(2)}) collective-permute-start(bf16[64,1152]{1,0:T(8,128)(2,1)} %get-tuple-element.49), channel_id=1, source_target_pairs={{0,3},{1,0},{2,1},{3,2},{4,7},{5,4},{6,5},{7,6},{8,11},{9,8},{10,9... | collective-permute-start | bytes 442376 | tf_op jit(solution)/shard_map/ppermute | solution.py:190
  74.1 6.1 %collective-permute-start.7 = (bf16[64,1152]{1,0:T(8,128)(2,1)}, bf16[64,1152]{1,0:T(8,128)(2,1)S(1)}, u32[]{:S(2)}, u32[]{:S(2)}) collective-permute-start(bf16[64,1152]{1,0:T(8,128)(2,1)} %get-tuple-element.52), channel_id=1, source_target_pairs={{0,1},{1,2},{2,3},{3,0},{4,5},{5,6},{6,7},{7,4},{8,9},{9,10},{10,1... | collective-permute-start | bytes 442376 | tf_op jit(solution)/shard_map/ppermute | solution.py:190
  74.3 9.6 %collective-permute-start.8 = (bf16[64,1152]{1,0:T(8,128)(2,1)}, bf16[64,1152]{1,0:T(8,128)(2,1)S(1)}, u32[]{:S(2)}, u32[]{:S(2)}) collective-permute-start(bf16[64,1152]{1,0:T(8,128)(2,1)} %get-tuple-element.51), channel_id=1, source_target_pairs={{0,2},{1,3},{2,0},{3,1},{4,6},{5,7},{6,4},{7,5},{8,10},{9,11},{10,... | collective-permute-start | bytes 442376 | tf_op jit(solution)/shard_map/ppermute | solution.py:190
  75.9 10.9 %collective-permute-start.9 = (bf16[64,1152]{1,0:T(8,128)(2,1)}, bf16[64,1152]{1,0:T(8,128)(2,1)S(1)}, u32[]{:S(2)}, u32[]{:S(2)}) collective-permute-start(bf16[64,1152]{1,0:T(8,128)(2,1)} %get-tuple-element.50), channel_id=1, source_target_pairs={{0,2},{1,3},{2,0},{3,1},{4,6},{5,7},{6,4},{7,5},{8,10},{9,11},{10,... | collective-permute-start | bytes 442376 | tf_op jit(solution)/shard_map/ppermute | solution.py:190
  87.6 7.0 %copy-start.28 = (pred[384,1]{0,1:T(4,128)(4,1)S(1)}, pred[384,1]{0,1:T(4,128)(4,1)}, u32[]{:S(2)}) copy-start(pred[384,1]{0,1:T(4,128)(4,1)} %constant.127.clone) | copy-start | bytes 1156
  88.7 34.3 %collective-permute-start.10 = (bf16[256,1152]{1,0:T(8,128)(2,1)}, bf16[256,1152]{1,0:T(8,128)(2,1)}, u32[]{:S(2)}, u32[]{:S(2)}) collective-permute-start(bf16[256,1152]{1,0:T(8,128)(2,1)} %get-tuple-element.31), channel_id=1, source_target_pairs={{0,4},{4,8},{8,12},{1,5},{5,9},{9,13},{2,6},{6,10},{10,14},{3,7},{... | collective-permute-start | bytes 1769480 | tf_op jit(solution)/shard_map/ppermute | solution.py:220
  93.3 29.7 %collective-permute-start.11 = (bf16[256,1152]{1,0:T(8,128)(2,1)}, bf16[256,1152]{1,0:T(8,128)(2,1)}, u32[]{:S(2)}, u32[]{:S(2)}) collective-permute-start(bf16[256,1152]{1,0:T(8,128)(2,1)} %get-tuple-element.26), channel_id=1, source_target_pairs={{4,0},{8,4},{12,8},{5,1},{9,5},{13,9},{6,2},{10,6},{14,10},{7,3},{... | collective-permute-start | bytes 1769480 | tf_op jit(solution)/shard_map/ppermute | solution.py:221
  120.3 2.7 %copy-start.16 = (s32[192]{0:T(256)S(1)}, s32[192]{0:T(256)}, u32[]{:S(2)}) copy-start(s32[192]{0:T(256)} %eq.116) | copy-start | bytes 2308
  123.0 3.3 %copy-start.12 = (f32[256]{0:T(256)S(1)}, f32[256]{0:T(256)}, u32[]{:S(2)}) copy-start(f32[256]{0:T(256)} %mul.137) | copy-start | bytes 3076
  123.0 3.3 %copy-start.13 = (f32[256]{0:T(256)S(1)}, f32[256]{0:T(256)}, u32[]{:S(2)}) copy-start(f32[256]{0:T(256)} %mul.157) | copy-start | bytes 3076
  123.1 4.7 %copy-start.14 = (f32[256]{0:T(256)S(1)}, f32[256]{0:T(256)}, u32[]{:S(2)}) copy-start(f32[256]{0:T(256)} %mul.168) | copy-start | bytes 3076
  123.1 4.7 %copy-start.15 = (f32[256]{0:T(256)S(1)}, f32[256]{0:T(256)}, u32[]{:S(2)}) copy-start(f32[256]{0:T(256)} %mul.172) | copy-start | bytes 3076
  123.6 10.2 %copy-start.24 = (f32[384]{0:T(512)S(1)}, f32[384]{0:T(512)}, u32[]{:S(2)}) copy-start(f32[384]{0:T(512)} %get-tuple-element.36) | copy-start | bytes 4612
  123.6 10.2 %copy-start.25 = (f32[384]{0:T(512)S(1)}, f32[384]{0:T(512)}, u32[]{:S(2)}) copy-start(f32[384]{0:T(512)} %get-tuple-element.37) | copy-start | bytes 4612
  123.6 10.2 %copy-start.30 = (s32[192]{0:T(256)S(1)}, s32[192]{0:T(256)}, u32[]{:S(2)}) copy-start(s32[192]{0:T(256)} %eq.113) | copy-start | bytes 2308
  123.6 10.2 %copy-start.34 = (pred[384]{0:T(512)(128)(4,1)S(1)}, pred[384]{0:T(512)(128)(4,1)}, u32[]{:S(2)}) copy-start(pred[384]{0:T(512)(128)(4,1)} %constant.133) | copy-start | bytes 1156
  123.7 5.8 %collective-permute-start.12 = (bf16[48,1152]{1,0:T(8,128)(2,1)S(1)}, bf16[48,1152]{1,0:T(8,128)(2,1)S(1)}, u32[]{:S(2)}, u32[]{:S(2)}) collective-permute-start(bf16[48,1152]{1,0:T(8,128)(2,1)S(1)} %get-tuple-element.53), channel_id=1, source_target_pairs={{0,3},{1,0},{2,1},{3,2},{4,7},{5,4},{6,5},{7,6},{8,11},{9,8},{10,9... | collective-permute-start | bytes 331784 | tf_op jit(solution)/shard_map/ppermute | solution.py:190
  123.7 5.7 %collective-permute-start.13 = (bf16[48,1152]{1,0:T(8,128)(2,1)S(1)}, bf16[48,1152]{1,0:T(8,128)(2,1)S(1)}, u32[]{:S(2)}, u32[]{:S(2)}) collective-permute-start(bf16[48,1152]{1,0:T(8,128)(2,1)S(1)} %get-tuple-element.56), channel_id=1, source_target_pairs={{0,1},{1,2},{2,3},{3,0},{4,5},{5,6},{6,7},{7,4},{8,9},{9,10},{10,1... | collective-permute-start | bytes 331784 | tf_op jit(solution)/shard_map/ppermute | solution.py:190
  124.2 7.2 %collective-permute-start.14 = (bf16[48,1152]{1,0:T(8,128)(2,1)S(1)}, bf16[48,1152]{1,0:T(8,128)(2,1)S(1)}, u32[]{:S(2)}, u32[]{:S(2)}) collective-permute-start(bf16[48,1152]{1,0:T(8,128)(2,1)S(1)} %get-tuple-element.55), channel_id=1, source_target_pairs={{0,2},{1,3},{2,0},{3,1},{4,6},{5,7},{6,4},{7,5},{8,10},{9,11},{10,... | collective-permute-start | bytes 331784 | tf_op jit(solution)/shard_map/ppermute | solution.py:190
  125.2 8.6 %collective-permute-start.15 = (bf16[48,1152]{1,0:T(8,128)(2,1)S(1)}, bf16[48,1152]{1,0:T(8,128)(2,1)S(1)}, u32[]{:S(2)}, u32[]{:S(2)}) collective-permute-start(bf16[48,1152]{1,0:T(8,128)(2,1)S(1)} %get-tuple-element.54), channel_id=1, source_target_pairs={{0,2},{1,3},{2,0},{3,1},{4,6},{5,7},{6,4},{7,5},{8,10},{9,11},{10,... | collective-permute-start | bytes 331784 | tf_op jit(solution)/shard_map/ppermute | solution.py:190
  (4 other events, 4.7 us)

commit v12 on v9

--- a/solution.py
+++ b/solution.py
@@ -242,10 +242,13 @@
         place = (token_ids[:, None] == recv_cells[None, :]).astype(jnp.bfloat16)
         partner = jnp.dot(place, arrived, preferred_element_type=jnp.float32)
         dep = strip_depth(part_frames)[:, None]
-        w_keep = jnp.where(dep == 0, keep[0], keep[1])
-        w_take = jnp.where(dep == 0, take[0], take[1])
         own = tile_out.astype(jnp.float32)
-        return jnp.where(dep >= 0, w_keep * own + w_take * partner, own).astype(jnp.bfloat16)
+        mixed = jnp.where(
+            dep == 0,
+            keep[0] * own + take[0] * partner,
+            jnp.where(dep == 1, keep[1] * own + take[1] * partner, own),
+        )
+        return mixed.astype(jnp.bfloat16)
 
     rim_queries = jnp.concatenate([queries[:, :rim], queries[:, tokens - rim :]], axis=1)
     rim_in = jnp.concatenate([block_in[:rim], block_in[tokens - rim :]], axis=0)
@@ -260,13 +263,22 @@
     count = lax.axis_size("tm")
     lower = lax.ppermute(high, "tm", [(i, i + 1) for i in range(count - 1)])
     upper = lax.ppermute(low, "tm", [(i + 1, i) for i in range(count - 1)])
-    second_queries, low, high = lax.optimization_barrier(
-        (queries[:, mid_a : tokens - rim], low, high)
+    outgoing_first = strips_out(tile_first)
+    arrived_first = strips_in(outgoing_first)
+    second_queries, low, high, outgoing_first = lax.optimization_barrier(
+        (queries[:, mid_a : tokens - rim], low, high, outgoing_first)
     )
     tile_second = tile_part(second_queries, block_in[mid_a : tokens - rim])
-    lower, upper, tile_second = lax.optimization_barrier((lower, upper, tile_second))
-    tile_mid = jnp.concatenate([tile_first, tile_second], axis=0)
-    spaced_mid = space_blend(tile_mid, strips_in(strips_out(tile_mid)))
+    lower, upper, arrived_first, tile_second = lax.optimization_barrier(
+        (lower, upper, arrived_first, tile_second)
+    )
+    spaced_mid = jnp.concatenate(
+        [
+            space_blend(tile_first, arrived_first),
+            space_blend(tile_second, strips_in(strips_out(tile_second))),
+        ],
+        axis=0,
+    )
 
     span_id = lax.axis_index("tm")
     has_lower = span_id > 0

time: 118 us -> 120 us (1.017)
  matrix products: 10.9 us -> 20.5 us
  waiting for transfers between devices: 10.6 us -> 5.08 us
  other arithmetic: 15.9 us -> 10.8 us
  starting transfers between devices: 15.7 us -> 19.9 us
    dot_general x2 -> x3, matrix products: 1.27 us -> 9.78 us  [space_blend(): partner = jnp.dot(place, arrived, preferred_element_type=jnp.float32)]
    ppermute x8 -> x12, waiting for transfers between devices: 6.63 us -> 0.47 us  [strips_in(): lax.ppermute(sent, 'face', [(i, (i + shift) % n) for i in range(n)])]
    select_n x2 -> x0, other arithmetic: 5.14 us -> none  [space_blend(): w_keep = jnp.where(dep == 0, keep[0], keep[1])]
    ppermute x8 -> x12, starting transfers between devices: 5.21 us -> 9.32 us  [strips_in(): lax.ppermute(sent, 'face', [(i, (i + shift) % n) for i in range(n)])]
    ppermute x6, waiting for transfers between devices: 0.67 us -> 3.1 us  [fetch(): return lax.ppermute(x, 'face', [(src_of(i), i) for i in range(n)])]
    ppermute x1, waiting for transfers between devices: 3.33 us -> 1.51 us  [per_device(): upper = lax.ppermute(low, 'tm', [(i + 1, i) for i in range(count - 1)])]
    dot_general x2 -> x3, matrix products: 2.27 us -> 3.36 us  [strips_out(): jnp.dot(pick, tile_out, preferred_element_type=jnp.float32)]
    unnamed x42 -> x43, local copies, waits for them, and re-layouts: 6.74 us -> 6.71 us
  transfers between devices with their start and end apart: 16 -> 20, of which waited for: 6 -> 4; matrix products, arithmetic and copies ran while one was open for 40% -> 38% of each run, Pallas kernels for 16% -> 15%
where the time goes in v12:
time: 120 us; the launch traced here: 119 us
  Pallas kernels  35.1 us (29%)
  local copies, waits for them, and re-layouts  27.4 us (23%)
  matrix products  20.5 us (17%)
  starting transfers between devices  19.9 us (17%)
  other arithmetic  10.8 us (9%)
  waiting for transfers between devices  5.08 us (4%)
    pallas_call x3, Pallas kernels, attend_project(): pl.pallas_call(attention_kernel, grid=(1, heads // hb), in_specs=in_specs...  35.1 us
    dot_general x3, matrix products, space_blend(): partner = jnp.dot(place, arrived, preferred_element_type=jnp.float32)  9.78 us
    ppermute x12, starting transfers between devices, strips_in(): lax.ppermute(sent, 'face', [(i, (i + shift) % n) for i in range(n)])  9.32 us
    dot_general x2, matrix products, chip_part(): jnp.dot(lax.dynamic_index_in_dim(moved_chips, chip, 0, keepdims=False), w...  7.34 us
    unnamed x43, local copies, waits for them, and re-layouts  6.71 us
    ppermute x6, starting transfers between devices, fetch(): return lax.ppermute(x, 'face', [(src_of(i), i) for i in range(n)])  5.4 us
    ppermute x1, starting transfers between devices, per_device(): lower = lax.ppermute(high, 'tm', [(i, i + 1) for i in range(count - 1)])  3.89 us
    dot_general x3, matrix products, strips_out(): jnp.dot(pick, tile_out, preferred_element_type=jnp.float32)  3.36 us
  transfers between devices with their start and end apart: 20, of which 4 were waited for; matrix products, arithmetic and copies ran while one was open for 38% of the time, Pallas kernels for 15%

profile of v12, /device:TPU:0, one launch (start us, length us, event | category | flops | bytes accessed | tf_op | source)
XLA Modules:
  0.0 119.3 jit_solution(17756095148335005014)
XLA Ops:
  0.5 2.6 %collective-permute-start.1 = (bf16[288,1728]{1,0:T(8,128)(2,1)}, bf16[288,1728]{1,0:T(8,128)(2,1)}, u32[]{:S(2)}, u32[]{:S(2)}) collective-permute-start(bf16[288,1728]{1,0:T(8,128)(2,1)} %param.25), channel_id=1, source_target_pairs={{2,0},{3,1},{0,2},{1,3},{6,4},{7,5},{4,6},{5,7},{10,8},{11,9},{8,1... | collective-permute-start | bytes 2985992 | tf_op jit(solution)/shard_map/ppermute | solution.py:154
  3.0 2.9 %copy.43 = bf16[1,1,896,1152]{2,3,1,0:T(8,128)(2,1)S(1)} copy(bf16[1,1,896,1152]{3,2,1,0:T(8,128)(2,1)} %param.23) | data formatting | bytes 4128768 | tf_op args[0]
  5.9 1.3 %slice_bitcast_fusion.2 = (bf16[256,1152]{1,0:T(8,128)(2,1)S(1)}, bf16[256,1152]{1,0:T(8,128)(2,1)S(1)}) fusion(bf16[1,1,896,1152]{3,2,1,0:T(8,128)(2,1)} %param.23), kind=kLoop, calls=%fused_computation.54 | loop fusion | bytes 2359296 | tf_op jit(solution)/shard_map/slice | solution.py:254
  8.1 0.6 fusion.1
  8.7 0.6 add_reduce_fusion
  9.4 1.2 pad_maximum_fusion.refs_8_
  11.2 2.1 %add_convert_fusion.1 = bf16[896,2,576]{0,2,1:T(8,128)(2,1)} fusion(f32[2,576]{1,0:T(2,128)S(1)} %add.121, f32[2,576]{1,0:T(2,128)S(1)} %mul.141, f32[896]{0:T(1024)S(1)} %add_rsqrt_fusion, f32[896]{0:T(1024)S(1)} %broadcast_multiply_fusion, bf16[896,2,576]{0,2,1:T(8,128)(2,1)S(1)} %bitcast.75), kind=kLoop, calls=%fused_computation.4 | loop fusion | flops 6193152 | bytes 4145152 | tf_op jit(solution)/shard_map/convert_element_type | solution.py:30
  13.3 1.4 %broadcast.90.clone = bf16[2,288,1728]{2,1,0:T(8,128)(2,1)} broadcast(bf16[]{:T(256)} %constant.115.clone.1), dimensions={} | broadcast | bytes 1990658 | tf_op jit(solution)/shard_map/broadcast.4
  14.9 1.0 bitcast_dynamic-update-slice_fusion.3
  15.9 0.7 fusion.49
  16.9 2.2 %bitcast_dynamic-update-slice_fusion.2 = bf16[2,288,1728]{2,1,0:T(8,128)(2,1)} fusion(bf16[2,288,1728]{2,1,0:T(8,128)(2,1)} %bitcast_dynamic-update-slice_fusion.3, s32[]{:T(128)S(6)} %select_n.125, bf16[288,1728]{1,0:T(8,128)(2,1)} %collective-permute-done), kind=kLoop, calls=%fused_computation.38 | loop fusion | bytes 2064388 | tf_op jit(solution)/shard_map/jit(dynamic_update_index_in_dim)/dynamic_update_slice | solution.py:161
  19.2 4.5 %fusion.12 = f32[896,1728]{0,1:T(8,128)S(1)} fusion(bf16[576,1728]{1,0:T(8,128)(2,1)} %bitcast.5, bf16[896,2,576]{0,2,1:T(8,128)(2,1)S(1)} %copy-done.2, s32[]{:T(128)S(6)} %select_n.122), kind=kOutput, calls=%fused_computation.40 | convolution fusion | flops 1783627776 | bytes 9216004 | tf_op jit(solution)/shard_map/dot_general | solution.py:165
  23.6 3.1 %collective-permute-done.1 = bf16[288,1728]{1,0:T(8,128)(2,1)} collective-permute-done((bf16[288,1728]{1,0:T(8,128)(2,1)}, bf16[288,1728]{1,0:T(8,128)(2,1)}, u32[]{:S(2)}, u32[]{:S(2)}) %collective-permute-start.1) | collective-permute-done | bytes 995360 | tf_op jit(solution)/shard_map/ppermute | solution.py:154
  26.7 2.1 %slice_bitcast_fusion.3 = (bf16[192,1152]{1,0:T(8,128)(2,1)}, bf16[192,1152]{1,0:T(8,128)(2,1)}) fusion(bf16[1,1,896,1152]{3,2,1,0:T(8,128)(2,1)} %param.23), kind=kLoop, calls=%fused_computation.57 | loop fusion | bytes 1769472 | tf_op jit(solution)/shard_map/slice | solution.py:271
  29.0 1.3 %bitcast_dynamic-update-slice_fusion.1 = bf16[2,288,1728]{2,1,0:T(8,128)(2,1)S(1)} fusion(bf16[2,288,1728]{2,1,0:T(8,128)(2,1)S(1)} %broadcast.90, s32[]{:T(128)S(6)} %select_n.124, bf16[288,1728]{1,0:T(8,128)(2,1)} %collective-permute-done.1), kind=kLoop, calls=%fused_computation.35 | loop fusion | bytes 2027524 | tf_op jit(solution)/shard_map/jit(dynamic_update_index_in_dim)/dynamic_update_slice | solution.py:160
  30.3 0.6 collective-permute-start.3
  30.9 1.7 %collective-permute-start.4 = (bf16[576,288]{0,1:T(8,128)(2,1)}, bf16[576,288]{0,1:T(8,128)(2,1)}, u32[]{:S(2)}, u32[]{:S(2)}) collective-permute-start(bf16[576,288]{0,1:T(8,128)(2,1)} %param.26), channel_id=1, source_target_pairs={{2,0},{3,1},{0,2},{1,3},{6,4},{7,5},{4,6},{5,7},{10,8},{11,9},{8,1... | collective-permute-start | bytes 995336 | tf_op jit(solution)/shard_map/ppermute | solution.py:104
  32.8 2.9 %fusion.10 = f32[896,1728]{0,1:T(8,128)S(1)} fusion(bf16[576,1728]{1,0:T(8,128)(2,1)S(1)} %bitcast.80, bf16[896,2,576]{0,2,1:T(8,128)(2,1)S(1)} %copy-done.2, s32[]{:T(128)S(6)} %select_n.126), kind=kOutput, calls=%fused_computation.36 | convolution fusion | flops 1783627776 | bytes 9289732 | tf_op jit(solution)/shard_map/dot_general | solution.py:165
  35.6 0.8 add_convert_fusion
  36.5 1.6 %fusion.42 = (bf16[896,1,8,72]{0,3,2,1:T(8,128)(2,1)S(1)}, bf16[896,1,8,72]{0,3,2,1:T(8,128)(2,1)}, bf16[8,72,896]{2,1,0:T(8,128)(2,1)}) fusion(bf16[896,3,8,72]{0,3,2,1:T(8,128)(2,1)S(1)} %bitcast.76), kind=kLoop, calls=%fused_computation.103 | loop fusion | bytes 6193152 | tf_op jit(solution)/shard_map/slice | solution.py:196
  38.0 1.9 %copy.52 = bf16[896,1,8,72]{3,0,2,1:T(8,128)(2,1)S(1)} copy(bf16[896,1,8,72]{0,3,2,1:T(8,128)(2,1)} %get-tuple-element.38) | data formatting | bytes 2064384
  40.0 0.9 fusion.44
  40.8 1.7 %copy.53 = bf16[896,1,8,72]{3,0,2,1:T(8,128)(2,1)} copy(bf16[896,1,8,72]{0,3,2,1:T(8,128)(2,1)S(1)} %get-tuple-element.37) | data formatting | bytes 2064384
  42.5 2.2 %pad_maximum_fusion.1.refs_0_.refs_4_ = bf16[8,512,72]{2,1,0:T(8,128)(2,1)} fusion(bf16[8,256,72]{2,1,0:T(8,128)(2,1)} %get-tuple-element.47, bf16[8,256,72]{2,1,0:T(8,128)(2,1)S(1)} %get-tuple-element.46), kind=kLoop, calls=%fused_computation.32 | loop fusion | flops 1179648 | bytes 1179648 | tf_op jit(solution)/shard_map/concatenate | solution.py:253
  44.8 1.0 bitcast_dynamic-update-slice_fusion.7
  46.0 1.0 bitcast_dynamic-update-slice_fusion.6
  47.0 1.0 bitcast_dynamic-update-slice_fusion.5
  48.1 1.8 %copy.46.refs_3_.refs_7_ = bf16[576,1152]{1,0:T(8,128)(2,1)} copy(bf16[576,1152]{0,1:T(8,128)(2,1)S(1)} %bitcast.79) | data formatting | bytes 2654208 | tf_op jit(solution)/shard_map/reshape | solution.py:191
  49.9 17.0 %shard_map.217 = bf16[512,1152]{1,0:T(8,128)(2,1)} custom-call(bf16[8,512,72]{2,1,0:T(8,128)(2,1)} %pad_maximum_fusion.1.refs_0_.refs_4_, bf16[8,72,896]{2,1,0:T(8,128)(2,1)} %get-tuple-element.39.refs_1_.refs_5_, bf16[8,896,72]{2,1,0:T(8,128)(2,1)} %bitcast.69, bf16[576,1152]{1,0:T(8,128)(2,1)} %copy.46.refs_3_.refs_7_, ...), custom_call_target="tpu_custom_call" | custom-call | tf_op jit(solution)/shard_map/pallas_call | solution.py:88
  66.9 1.8 %convolution_convert_fusion = bf16[256,1152]{1,0:T(8,128)(2,1)S(1)} fusion(bf16[512,1152]{1,0:T(8,128)(2,1)} %shard_map.217, s32[256]{0:T(256)S(1)} %eq.138), kind=kOutput, calls=%fused_computation.8 | convolution fusion | flops 302415872 | bytes 1770496 | tf_op jit(solution)/shard_map/dot_general | solution.py:222
  69.4 1.6 %collective-permute-start.8 = (bf16[64,1152]{1,0:T(8,128)(2,1)S(1)}, bf16[64,1152]{1,0:T(8,128)(2,1)S(1)}, u32[]{:S(2)}, u32[]{:S(2)}) collective-permute-start(bf16[64,1152]{1,0:T(8,128)(2,1)S(1)} %get-tuple-element.52), channel_id=1, source_target_pairs={{0,2},{1,3},{2,0},{3,1},{4,6},{5,7},{6,4},{7,5},{8,10},{9,11},{10,... | collective-permute-start | bytes 442376 | tf_op jit(solution)/shard_map/ppermute | solution.py:231
  71.4 1.0 fusion.43
  72.4 9.1 %shard_map.218 = bf16[192,1152]{1,0:T(8,128)(2,1)} custom-call(bf16[8,192,72]{2,1,0:T(8,128)(2,1)} %get-tuple-element.23.refs_0_.refs_4_, bf16[8,72,896]{2,1,0:T(8,128)(2,1)} %get-tuple-element.39.refs_1_.refs_5_, bf16[8,896,72]{2,1,0:T(8,128)(2,1)} %bitcast.71, bf16[576,1152]{1,0:T(8,128)(2,1)} %copy.46.refs_3_.refs_7_, ...), custom_call_target="tpu_custom_call" | custom-call | tf_op jit(solution)/shard_map/pallas_call | solution.py:88
  81.7 3.6 %fusion.4 = bf16[512,1152]{1,0:T(8,128)(2,1)S(1)} fusion(bf16[512,1152]{1,0:T(8,128)(2,1)S(1)} %copy-done.1, bf16[256,1152]{1,0:T(8,128)(2,1)S(1)} %pad_maximum_fusion.2, f32[]{:T(128)} %bitcast.34, f32[]{:T(128)} %bitcast.33, f32[]{:T(128)} %bitcast.28, f32[]{:T(128)} %bitcast.13, pred[512]{0:T(512)(128)(4,1)S(1)} %copy-done.19, ...), kind=kOutput, calls=%fused_computation.11 | convolution fusion | flops 308019200 | bytes 2951184 | tf_op jit(solution)/shard_map/dot_general | solution.py:243
  85.5 3.9 %collective-permute-start.10 = (bf16[256,1152]{1,0:T(8,128)(2,1)S(1)}, bf16[256,1152]{1,0:T(8,128)(2,1)S(1)}, u32[]{:S(2)}, u32[]{:S(2)}) collective-permute-start(bf16[256,1152]{1,0:T(8,128)(2,1)S(1)} %get-tuple-element.33), channel_id=1, source_target_pairs={{0,4},{4,8},{8,12},{1,5},{5,9},{9,13},{2,6},{6,10},{10,14},{3,7},{... | collective-permute-start | bytes 1769480 | tf_op jit(solution)/shard_map/ppermute | solution.py:264
  89.4 1.3 %collective-permute-start.11 = (bf16[256,1152]{1,0:T(8,128)(2,1)S(1)}, bf16[256,1152]{1,0:T(8,128)(2,1)S(1)}, u32[]{:S(2)}, u32[]{:S(2)}) collective-permute-start(bf16[256,1152]{1,0:T(8,128)(2,1)S(1)} %get-tuple-element.28), channel_id=1, source_target_pairs={{4,0},{8,4},{12,8},{5,1},{9,5},{13,9},{6,2},{10,6},{14,10},{7,3},{... | collective-permute-start | bytes 1769480 | tf_op jit(solution)/shard_map/ppermute | solution.py:265
  91.0 0.6 collective-permute-start.12
  91.7 1.5 %collective-permute-start.14 = (bf16[24,1152]{1,0:T(8,128)(2,1)S(1)}, bf16[24,1152]{1,0:T(8,128)(2,1)S(1)}, u32[]{:S(2)}, u32[]{:S(2)}) collective-permute-start(bf16[24,1152]{1,0:T(8,128)(2,1)S(1)} %get-tuple-element.60), channel_id=1, source_target_pairs={{0,2},{1,3},{2,0},{3,1},{4,6},{5,7},{6,4},{7,5},{8,10},{9,11},{10,... | collective-permute-start | bytes 165896 | tf_op jit(solution)/shard_map/ppermute | solution.py:231
  93.5 1.9 %collective-permute-start.15 = (bf16[24,1152]{1,0:T(8,128)(2,1)S(1)}, bf16[24,1152]{1,0:T(8,128)(2,1)S(1)}, u32[]{:S(2)}, u32[]{:S(2)}) collective-permute-start(bf16[24,1152]{1,0:T(8,128)(2,1)S(1)} %get-tuple-element.59), channel_id=1, source_target_pairs={{0,2},{1,3},{2,0},{3,1},{4,6},{5,7},{6,4},{7,5},{8,10},{9,11},{10,... | collective-permute-start | bytes 165896 | tf_op jit(solution)/shard_map/ppermute | solution.py:231
  96.4 9.0 %shard_map.219 = bf16[192,1152]{1,0:T(8,128)(2,1)} custom-call(bf16[8,192,72]{2,1,0:T(8,128)(2,1)} %get-tuple-element.29.refs_0_.refs_4_, bf16[8,72,896]{2,1,0:T(8,128)(2,1)} %get-tuple-element.39.refs_1_.refs_5_, bf16[8,896,72]{2,1,0:T(8,128)(2,1)} %bitcast.73, bf16[576,1152]{1,0:T(8,128)(2,1)} %copy.46.refs_3_.refs_7_, ...), custom_call_target="tpu_custom_call" | custom-call | tf_op jit(solution)/shard_map/pallas_call | solution.py:88
  105.5 1.5 %collective-permute-done.11 = bf16[256,1152]{1,0:T(8,128)(2,1)S(1)} collective-permute-done((bf16[256,1152]{1,0:T(8,128)(2,1)S(1)}, bf16[256,1152]{1,0:T(8,128)(2,1)S(1)}, u32[]{:S(2)}, u32[]{:S(2)}) %collective-permute-start.11) | collective-permute-done | bytes 589856 | tf_op jit(solution)/shard_map/ppermute | solution.py:265
  107.0 1.3 %convolution_convert_fusion.1 = bf16[96,1152]{1,0:T(8,128)(2,1)S(1)} fusion(bf16[192,1152]{1,0:T(8,128)(2,1)} %shard_map.219, s32[96]{0:T(128)S(1)} %eq.142), kind=kOutput, calls=%fused_computation.13 | convolution fusion | flops 42596352 | bytes 663936 | tf_op jit(solution)/shard_map/dot_general | solution.py:222
  108.3 0.5 collective-permute-start.16
  108.9 0.8 collective-permute-start.18
  109.7 1.2 %collective-permute-start.19 = (bf16[24,1152]{1,0:T(8,128)(2,1)S(1)}, bf16[24,1152]{1,0:T(8,128)(2,1)S(1)}, u32[]{:S(2)}, u32[]{:S(2)}) collective-permute-start(bf16[24,1152]{1,0:T(8,128)(2,1)S(1)} %get-tuple-element.55), channel_id=1, source_target_pairs={{0,2},{1,3},{2,0},{3,1},{4,6},{5,7},{6,4},{7,5},{8,10},{9,11},{10,... | collective-permute-start | bytes 165896 | tf_op jit(solution)/shard_map/ppermute | solution.py:231
  111.6 3.1 %fusion.18 = bf16[192,1152]{1,0:T(8,128)(2,1)S(1)} fusion(bf16[192,1152]{1,0:T(8,128)(2,1)S(1)} %copy-done.3, bf16[96,1152]{1,0:T(8,128)(2,1)S(1)} %pad_maximum_fusion.3, f32[]{:T(128)} %bitcast.34, f32[]{:T(128)} %bitcast.33, f32[]{:T(128)} %bitcast.28, f32[]{:T(128)} %bitcast.13, pred[192]{0:T(512)(128)(4,1)S(1)} %copy-done.17, ...), kind=kOutput, calls=%fused_computation.46 | convolution fusion | flops 44697600 | bytes 1106704 | tf_op jit(solution)/shard_map/dot_general | solution.py:243
  114.7 3.1 %fusion.22 = bf16[192,1152]{1,0:T(8,128)(2,1)S(1)} fusion(bf16[192,1152]{1,0:T(8,128)(2,1)S(1)} %copy-done.4, f32[]{:T(128)} %bitcast.34, f32[]{:T(128)} %bitcast.33, f32[]{:T(128)} %bitcast.28, f32[]{:T(128)} %bitcast.13, pred[192]{0:T(512)(128)(4,1)S(1)} %copy-done.17, pred[192]{0:T(512)(128)(4,1)S(1)} %copy-done.16, ...), kind=kOutput, calls=%fused_computation.50 | convolution fusion | flops 45582336 | bytes 1106704 | tf_op jit(solution)/shard_map/dot_general | solution.py:243
  117.8 1.5 %maximum_bitcast_fusion = bf16[1,1,896,1152]{3,2,1,0:T(8,128)(2,1)} fusion(bf16[256,1152]{1,0:T(8,128)(2,1)S(1)} %fusion.9, bf16[192,1152]{1,0:T(8,128)(2,1)S(1)} %fusion.22, bf16[192,1152]{1,0:T(8,128)(2,1)S(1)} %fusion.18, bf16[256,1152]{1,0:T(8,128)(2,1)S(1)} %fusion.7), kind=kLoop, calls=%fused_computation.15 | loop fusion | flops 8257536 | bytes 4128768 | tf_op jit(solution)/shard_map/reshape | solution.py:305
  (113 shorter events, 6.7 us)
Async XLA Ops:
  0.0 7.2 %copy-start = (s32[4,4,4]{2,1,0:T(4,128)S(1)}, s32[4,4,4]{2,1,0:T(4,128)}, u32[]{:S(2)}) copy-start(s32[4,4,4]{2,1,0:T(4,128)} %param.27) | copy-start | bytes 772
  0.0 16.9 %collective-permute-start = (bf16[288,1728]{1,0:T(8,128)(2,1)}, bf16[288,1728]{1,0:T(8,128)(2,1)}, u32[]{:S(2)}, u32[]{:S(2)}) collective-permute-start(bf16[288,1728]{1,0:T(8,128)(2,1)} %param.25), channel_id=1, source_target_pairs={{1,0},{0,1},{3,2},{2,3},{5,4},{4,5},{7,6},{6,7},{9,8},{8,9},{11,10... | collective-permute-start | bytes 2985992 | tf_op jit(solution)/shard_map/ppermute | solution.py:154
  0.5 26.3 %collective-permute-start.1 = (bf16[288,1728]{1,0:T(8,128)(2,1)}, bf16[288,1728]{1,0:T(8,128)(2,1)}, u32[]{:S(2)}, u32[]{:S(2)}) collective-permute-start(bf16[288,1728]{1,0:T(8,128)(2,1)} %param.25), channel_id=1, source_target_pairs={{2,0},{3,1},{0,2},{1,3},{6,4},{7,5},{4,6},{5,7},{10,8},{11,9},{8,1... | collective-permute-start | bytes 2985992 | tf_op jit(solution)/shard_map/ppermute | solution.py:154
  7.6 1.1 copy-start.6
  7.6 1.7 %copy-start.13 = (s32[2]{0:T(128)S(1)}, s32[2]{0:T(128)}, u32[]{:S(2)}) copy-start(s32[2]{0:T(128)} %param.28) | copy-start | bytes 28
  8.0 2.6 %copy-start.15 = (s32[4]{0:T(128)S(1)}, s32[4]{0:T(128)}, u32[]{:S(2)}) copy-start(s32[4]{0:T(128)} %constant.118.clone) | copy-start | bytes 52
  8.0 2.6 %copy-start.10 = (s32[4,64]{1,0:T(4,128)S(1)}, s32[4,64]{1,0:T(4,128)}, u32[]{:S(2)}) copy-start(s32[4,64]{1,0:T(4,128)} %constant.119.clone) | copy-start | bytes 3076
  8.1 2.6 %copy-start.11 = (s32[4,64]{1,0:T(4,128)S(1)}, s32[4,64]{1,0:T(4,128)}, u32[]{:S(2)}) copy-start(s32[4,64]{1,0:T(4,128)} %constant.120.clone) | copy-start | bytes 3076
  8.1 2.7 %copy-start.8 = (s32[4,24]{1,0:T(4,128)S(1)}, s32[4,24]{1,0:T(4,128)}, u32[]{:S(2)}) copy-start(s32[4,24]{1,0:T(4,128)} %constant.124.clone) | copy-start | bytes 1156
  8.1 2.7 %copy-start.9 = (s32[4,24]{1,0:T(4,128)S(1)}, s32[4,24]{1,0:T(4,128)}, u32[]{:S(2)}) copy-start(s32[4,24]{1,0:T(4,128)} %constant.125.clone) | copy-start | bytes 1156
  8.1 2.7 %copy-start.12 = (s32[4,64]{1,0:T(4,128)S(1)}, s32[4,64]{1,0:T(4,128)}, u32[]{:S(2)}) copy-start(s32[4,64]{1,0:T(4,128)} %constant.132) | copy-start | bytes 3076
  13.3 1.6 %copy-start.5 = (bf16[288,1728]{1,0:T(8,128)(2,1)S(1)}, bf16[288,1728]{1,0:T(8,128)(2,1)}, u32[]{:S(2)}) copy-start(bf16[288,1728]{1,0:T(8,128)(2,1)} %param.25) | copy-start | bytes 2985988
  13.3 3.5 %copy-start.14 = (s32[4]{0:T(128)S(1)}, s32[4]{0:T(128)}, u32[]{:S(2)}) copy-start(s32[4]{0:T(128)} %param.29) | copy-start | bytes 52
  14.9 4.3 %copy-start.2 = (bf16[896,2,576]{0,2,1:T(8,128)(2,1)S(1)}, bf16[896,2,576]{0,2,1:T(8,128)(2,1)}, u32[]{:S(2)}) copy-start(bf16[896,2,576]{0,2,1:T(8,128)(2,1)} %add_convert_fusion.1) | copy-start | bytes 6193156
  26.7 3.6 %collective-permute-start.2 = (bf16[288,1728]{1,0:T(8,128)(2,1)}, bf16[288,1728]{1,0:T(8,128)(2,1)S(1)}, u32[]{:S(2)}, u32[]{:S(2)}) collective-permute-start(bf16[288,1728]{1,0:T(8,128)(2,1)} %collective-permute-done.1), channel_id=1, source_target_pairs={{1,0},{0,1},{3,2},{2,3},{5,4},{4,5},{7,6},{6,7},{9,8},{8,9},{11,10... | collective-permute-start | bytes 2985992 | tf_op jit(solution)/shard_map/ppermute | solution.py:154
  30.3 15.6 %collective-permute-start.3 = (bf16[576,288]{0,1:T(8,128)(2,1)}, bf16[576,288]{0,1:T(8,128)(2,1)}, u32[]{:S(2)}, u32[]{:S(2)}) collective-permute-start(bf16[576,288]{0,1:T(8,128)(2,1)} %param.26), channel_id=1, source_target_pairs={{1,0},{0,1},{3,2},{2,3},{5,4},{4,5},{7,6},{6,7},{9,8},{8,9},{11,10... | collective-permute-start | bytes 995336 | tf_op jit(solution)/shard_map/ppermute | solution.py:104
  30.9 15.0 %collective-permute-start.4 = (bf16[576,288]{0,1:T(8,128)(2,1)}, bf16[576,288]{0,1:T(8,128)(2,1)}, u32[]{:S(2)}, u32[]{:S(2)}) collective-permute-start(bf16[576,288]{0,1:T(8,128)(2,1)} %param.26), channel_id=1, source_target_pairs={{2,0},{3,1},{0,2},{1,3},{6,4},{7,5},{4,6},{5,7},{10,8},{11,9},{8,1... | collective-permute-start | bytes 995336 | tf_op jit(solution)/shard_map/ppermute | solution.py:104
  45.9 2.2 %collective-permute-start.5 = (bf16[576,288]{0,1:T(8,128)(2,1)}, bf16[576,288]{0,1:T(8,128)(2,1)S(1)}, u32[]{:S(2)}, u32[]{:S(2)}) collective-permute-start(bf16[576,288]{0,1:T(8,128)(2,1)} %collective-permute-done.4), channel_id=1, source_target_pairs={{1,0},{0,1},{3,2},{2,3},{5,4},{4,5},{7,6},{6,7},{9,8},{8,9},{11,10... | collective-permute-start | bytes 995336 | tf_op jit(solution)/shard_map/ppermute | solution.py:104
  68.8 12.7 %collective-permute-start.6 = (bf16[64,1152]{1,0:T(8,128)(2,1)S(1)}, bf16[64,1152]{1,0:T(8,128)(2,1)S(1)}, u32[]{:S(2)}, u32[]{:S(2)}) collective-permute-start(bf16[64,1152]{1,0:T(8,128)(2,1)S(1)} %get-tuple-element.50), channel_id=1, source_target_pairs={{0,3},{1,0},{2,1},{3,2},{4,7},{5,4},{6,5},{7,6},{8,11},{9,8},{10,9... | collective-permute-start | bytes 442376 | tf_op jit(solution)/shard_map/ppermute | solution.py:231
  69.2 12.3 %collective-permute-start.7 = (bf16[64,1152]{1,0:T(8,128)(2,1)S(1)}, bf16[64,1152]{1,0:T(8,128)(2,1)S(1)}, u32[]{:S(2)}, u32[]{:S(2)}) collective-permute-start(bf16[64,1152]{1,0:T(8,128)(2,1)S(1)} %get-tuple-element.53), channel_id=1, source_target_pairs={{0,1},{1,2},{2,3},{3,0},{4,5},{5,6},{6,7},{7,4},{8,9},{9,10},{10,1... | collective-permute-start | bytes 442376 | tf_op jit(solution)/shard_map/ppermute | solution.py:231
  69.4 12.1 %collective-permute-start.8 = (bf16[64,1152]{1,0:T(8,128)(2,1)S(1)}, bf16[64,1152]{1,0:T(8,128)(2,1)S(1)}, u32[]{:S(2)}, u32[]{:S(2)}) collective-permute-start(bf16[64,1152]{1,0:T(8,128)(2,1)S(1)} %get-tuple-element.52), channel_id=1, source_target_pairs={{0,2},{1,3},{2,0},{3,1},{4,6},{5,7},{6,4},{7,5},{8,10},{9,11},{10,... | collective-permute-start | bytes 442376 | tf_op jit(solution)/shard_map/ppermute | solution.py:231
  71.0 10.7 %collective-permute-start.9 = (bf16[64,1152]{1,0:T(8,128)(2,1)S(1)}, bf16[64,1152]{1,0:T(8,128)(2,1)S(1)}, u32[]{:S(2)}, u32[]{:S(2)}) collective-permute-start(bf16[64,1152]{1,0:T(8,128)(2,1)S(1)} %get-tuple-element.51), channel_id=1, source_target_pairs={{0,2},{1,3},{2,0},{3,1},{4,6},{5,7},{6,4},{7,5},{8,10},{9,11},{10,... | collective-permute-start | bytes 442376 | tf_op jit(solution)/shard_map/ppermute | solution.py:231
  72.4 9.4 %copy-start.1 = (bf16[512,1152]{1,0:T(8,128)(2,1)S(1)}, bf16[512,1152]{1,0:T(8,128)(2,1)}, u32[]{:S(2)}) copy-start(bf16[512,1152]{1,0:T(8,128)(2,1)} %shard_map.217) | copy-start | bytes 3538948
  72.4 9.4 %copy-start.18 = (pred[512]{0:T(512)(128)(4,1)S(1)}, pred[512]{0:T(512)(128)(4,1)}, u32[]{:S(2)}) copy-start(pred[512]{0:T(512)(128)(4,1)} %constant.131) | copy-start | bytes 1540
  72.4 9.4 %copy-start.19 = (pred[512]{0:T(512)(128)(4,1)S(1)}, pred[512]{0:T(512)(128)(4,1)}, u32[]{:S(2)}) copy-start(pred[512]{0:T(512)(128)(4,1)} %constant.133) | copy-start | bytes 1540
  85.4 5.3 %copy-start.3 = (bf16[192,1152]{1,0:T(8,128)(2,1)S(1)}, bf16[192,1152]{1,0:T(8,128)(2,1)}, u32[]{:S(2)}) copy-start(bf16[192,1152]{1,0:T(8,128)(2,1)} %shard_map.218) | copy-start | bytes 1327108
  85.4 10.0 %copy-start.7 = (s32[4,24]{1,0:T(4,128)S(1)}, s32[4,24]{1,0:T(4,128)}, u32[]{:S(2)}) copy-start(s32[4,24]{1,0:T(4,128)} %constant.135) | copy-start | bytes 1156
  85.5 20.0 %collective-permute-start.10 = (bf16[256,1152]{1,0:T(8,128)(2,1)S(1)}, bf16[256,1152]{1,0:T(8,128)(2,1)S(1)}, u32[]{:S(2)}, u32[]{:S(2)}) collective-permute-start(bf16[256,1152]{1,0:T(8,128)(2,1)S(1)} %get-tuple-element.33), channel_id=1, source_target_pairs={{0,4},{4,8},{8,12},{1,5},{5,9},{9,13},{2,6},{6,10},{10,14},{3,7},{... | collective-permute-start | bytes 1769480 | tf_op jit(solution)/shard_map/ppermute | solution.py:264
  89.4 17.6 %collective-permute-start.11 = (bf16[256,1152]{1,0:T(8,128)(2,1)S(1)}, bf16[256,1152]{1,0:T(8,128)(2,1)S(1)}, u32[]{:S(2)}, u32[]{:S(2)}) collective-permute-start(bf16[256,1152]{1,0:T(8,128)(2,1)S(1)} %get-tuple-element.28), channel_id=1, source_target_pairs={{4,0},{8,4},{12,8},{5,1},{9,5},{13,9},{6,2},{10,6},{14,10},{7,3},{... | collective-permute-start | bytes 1769480 | tf_op jit(solution)/shard_map/ppermute | solution.py:265
  91.0 2.4 %collective-permute-start.12 = (bf16[24,1152]{1,0:T(8,128)(2,1)S(1)}, bf16[24,1152]{1,0:T(8,128)(2,1)S(1)}, u32[]{:S(2)}, u32[]{:S(2)}) collective-permute-start(bf16[24,1152]{1,0:T(8,128)(2,1)S(1)} %get-tuple-element.58), channel_id=1, source_target_pairs={{0,3},{1,0},{2,1},{3,2},{4,7},{5,4},{6,5},{7,6},{8,11},{9,8},{10,9... | collective-permute-start | bytes 165896 | tf_op jit(solution)/shard_map/ppermute | solution.py:231
  91.7 13.8 %collective-permute-start.13 = (bf16[24,1152]{1,0:T(8,128)(2,1)S(1)}, bf16[24,1152]{1,0:T(8,128)(2,1)S(1)}, u32[]{:S(2)}, u32[]{:S(2)}) collective-permute-start(bf16[24,1152]{1,0:T(8,128)(2,1)S(1)} %get-tuple-element.61), channel_id=1, source_target_pairs={{0,1},{1,2},{2,3},{3,0},{4,5},{5,6},{6,7},{7,4},{8,9},{9,10},{10,1... | collective-permute-start | bytes 165896 | tf_op jit(solution)/shard_map/ppermute | solution.py:231
  91.7 13.8 %collective-permute-start.14 = (bf16[24,1152]{1,0:T(8,128)(2,1)S(1)}, bf16[24,1152]{1,0:T(8,128)(2,1)S(1)}, u32[]{:S(2)}, u32[]{:S(2)}) collective-permute-start(bf16[24,1152]{1,0:T(8,128)(2,1)S(1)} %get-tuple-element.60), channel_id=1, source_target_pairs={{0,2},{1,3},{2,0},{3,1},{4,6},{5,7},{6,4},{7,5},{8,10},{9,11},{10,... | collective-permute-start | bytes 165896 | tf_op jit(solution)/shard_map/ppermute | solution.py:231
  93.5 12.0 %collective-permute-start.15 = (bf16[24,1152]{1,0:T(8,128)(2,1)S(1)}, bf16[24,1152]{1,0:T(8,128)(2,1)S(1)}, u32[]{:S(2)}, u32[]{:S(2)}) collective-permute-start(bf16[24,1152]{1,0:T(8,128)(2,1)S(1)} %get-tuple-element.59), channel_id=1, source_target_pairs={{0,2},{1,3},{2,0},{3,1},{4,6},{5,7},{6,4},{7,5},{8,10},{9,11},{10,... | collective-permute-start | bytes 165896 | tf_op jit(solution)/shard_map/ppermute | solution.py:231
  108.3 3.3 %copy-start.16 = (pred[192]{0:T(512)(128)(4,1)S(1)}, pred[192]{0:T(512)(128)(4,1)}, u32[]{:S(2)}) copy-start(pred[192]{0:T(512)(128)(4,1)} %constant.134) | copy-start | bytes 580
  108.3 3.3 %copy-start.17 = (pred[192]{0:T(512)(128)(4,1)S(1)}, pred[192]{0:T(512)(128)(4,1)}, u32[]{:S(2)}) copy-start(pred[192]{0:T(512)(128)(4,1)} %constant.136) | copy-start | bytes 580
  108.3 6.4 %collective-permute-start.16 = (bf16[24,1152]{1,0:T(8,128)(2,1)S(1)}, bf16[24,1152]{1,0:T(8,128)(2,1)S(1)}, u32[]{:S(2)}, u32[]{:S(2)}) collective-permute-start(bf16[24,1152]{1,0:T(8,128)(2,1)S(1)} %get-tuple-element.54), channel_id=1, source_target_pairs={{0,3},{1,0},{2,1},{3,2},{4,7},{5,4},{6,5},{7,6},{8,11},{9,8},{10,9... | collective-permute-start | bytes 165896 | tf_op jit(solution)/shard_map/ppermute | solution.py:231
  108.8 5.9 %collective-permute-start.17 = (bf16[24,1152]{1,0:T(8,128)(2,1)S(1)}, bf16[24,1152]{1,0:T(8,128)(2,1)S(1)}, u32[]{:S(2)}, u32[]{:S(2)}) collective-permute-start(bf16[24,1152]{1,0:T(8,128)(2,1)S(1)} %get-tuple-element.57), channel_id=1, source_target_pairs={{0,1},{1,2},{2,3},{3,0},{4,5},{5,6},{6,7},{7,4},{8,9},{9,10},{10,1... | collective-permute-start | bytes 165896 | tf_op jit(solution)/shard_map/ppermute | solution.py:231
  108.9 5.8 %collective-permute-start.18 = (bf16[24,1152]{1,0:T(8,128)(2,1)S(1)}, bf16[24,1152]{1,0:T(8,128)(2,1)S(1)}, u32[]{:S(2)}, u32[]{:S(2)}) collective-permute-start(bf16[24,1152]{1,0:T(8,128)(2,1)S(1)} %get-tuple-element.56), channel_id=1, source_target_pairs={{0,2},{1,3},{2,0},{3,1},{4,6},{5,7},{6,4},{7,5},{8,10},{9,11},{10,... | collective-permute-start | bytes 165896 | tf_op jit(solution)/shard_map/ppermute | solution.py:231
  109.7 5.1 %collective-permute-start.19 = (bf16[24,1152]{1,0:T(8,128)(2,1)S(1)}, bf16[24,1152]{1,0:T(8,128)(2,1)S(1)}, u32[]{:S(2)}, u32[]{:S(2)}) collective-permute-start(bf16[24,1152]{1,0:T(8,128)(2,1)S(1)} %get-tuple-element.55), channel_id=1, source_target_pairs={{0,2},{1,3},{2,0},{3,1},{4,6},{5,7},{6,4},{7,5},{8,10},{9,11},{10,... | collective-permute-start | bytes 165896 | tf_op jit(solution)/shard_map/ppermute | solution.py:231
  111.2 3.5 %copy-start.4 = (bf16[192,1152]{1,0:T(8,128)(2,1)S(1)}, bf16[192,1152]{1,0:T(8,128)(2,1)}, u32[]{:S(2)}) copy-start(bf16[192,1152]{1,0:T(8,128)(2,1)} %shard_map.219) | copy-start | bytes 1327108

commit v13 on v12

--- a/solution.py
+++ b/solution.py
@@ -242,13 +242,10 @@
         place = (token_ids[:, None] == recv_cells[None, :]).astype(jnp.bfloat16)
         partner = jnp.dot(place, arrived, preferred_element_type=jnp.float32)
         dep = strip_depth(part_frames)[:, None]
+        w_keep = jnp.where(dep == 0, keep[0], keep[1])
+        w_take = jnp.where(dep == 0, take[0], take[1])
         own = tile_out.astype(jnp.float32)
-        mixed = jnp.where(
-            dep == 0,
-            keep[0] * own + take[0] * partner,
-            jnp.where(dep == 1, keep[1] * own + take[1] * partner, own),
-        )
-        return mixed.astype(jnp.bfloat16)
+        return jnp.where(dep >= 0, w_keep * own + w_take * partner, own).astype(jnp.bfloat16)
 
     rim_queries = jnp.concatenate([queries[:, :rim], queries[:, tokens - rim :]], axis=1)
     rim_in = jnp.concatenate([block_in[:rim], block_in[tokens - rim :]], axis=0)

time: 120 us -> 116 us (0.967)
  matrix products: 20.5 us -> 12.1 us
  other arithmetic: 10.8 us -> 15.9 us
  starting transfers between devices: 19.9 us -> 17.4 us
  waiting for transfers between devices: 5.08 us -> 6.58 us
    dot_general x3, matrix products: 9.78 us -> 1.39 us  [space_blend(): partner = jnp.dot(place, arrived, preferred_element_type=jnp.float32)]
    select_n x0 -> x2, other arithmetic: none -> 5.16 us  [space_blend(): w_keep = jnp.where(dep == 0, keep[0], keep[1])]
    ppermute x12, waiting for transfers between devices: 0.47 us -> 4.64 us  [strips_in(): lax.ppermute(sent, 'face', [(i, (i + shift) % n) for i in range(n)])]
    ppermute x6, waiting for transfers between devices: 3.1 us -> 0.02 us  [fetch(): return lax.ppermute(x, 'face', [(src_of(i), i) for i in range(n)])]
    ppermute x6, starting transfers between devices: 5.4 us -> 3.89 us  [fetch(): return lax.ppermute(x, 'face', [(src_of(i), i) for i in range(n)])]
  transfers between devices with their start and end apart: 20 -> 20, of which waited for: 4 -> 5; matrix products, arithmetic and copies ran while one was open for 38% -> 41% of each run, Pallas kernels for 15% -> 16%
where the time goes in v13:
time: 116 us; the launch traced here: 115 us
  Pallas kernels  35.1 us (30%)
  local copies, waits for them, and re-layouts  27.5 us (24%)
  starting transfers between devices  17.4 us (15%)
  other arithmetic  15.9 us (14%)
  matrix products  12.1 us (10%)
  waiting for transfers between devices  6.58 us (6%)
    pallas_call x3, Pallas kernels, attend_project(): pl.pallas_call(attention_kernel, grid=(1, heads // hb), in_specs=in_specs...  35.1 us
    ppermute x12, starting transfers between devices, strips_in(): lax.ppermute(sent, 'face', [(i, (i + shift) % n) for i in range(n)])  8.55 us
    dot_general x2, matrix products, chip_part(): jnp.dot(lax.dynamic_index_in_dim(moved_chips, chip, 0, keepdims=False), w...  7.33 us
    unnamed x43, local copies, waits for them, and re-layouts  6.72 us
    select_n x2, other arithmetic, space_blend(): w_keep = jnp.where(dep == 0, keep[0], keep[1])  5.16 us
    ppermute x12, waiting for transfers between devices, strips_in(): lax.ppermute(sent, 'face', [(i, (i + shift) % n) for i in range(n)])  4.64 us
    ppermute x6, starting transfers between devices, fetch(): return lax.ppermute(x, 'face', [(src_of(i), i) for i in range(n)])  3.89 us
    ppermute x1, starting transfers between devices, per_device(): lower = lax.ppermute(high, 'tm', [(i, i + 1) for i in range(count - 1)])  3.66 us
  transfers between devices with their start and end apart: 20, of which 5 were waited for; matrix products, arithmetic and copies ran while one was open for 41% of the time, Pallas kernels for 16%

profile of v13, /device:TPU:0, one launch (start us, length us, event | category | flops | bytes accessed | tf_op | source)
XLA Modules:
  0.0 115.1 jit_solution(15216677373949549801)
XLA Ops:
  0.5 2.6 %collective-permute-start.1 = (bf16[288,1728]{1,0:T(8,128)(2,1)}, bf16[288,1728]{1,0:T(8,128)(2,1)}, u32[]{:S(2)}, u32[]{:S(2)}) collective-permute-start(bf16[288,1728]{1,0:T(8,128)(2,1)} %param.28), channel_id=1, source_target_pairs={{2,0},{3,1},{0,2},{1,3},{6,4},{7,5},{4,6},{5,7},{10,8},{11,9},{8,1... | collective-permute-start | bytes 2985992 | tf_op jit(solution)/shard_map/ppermute | solution.py:154
  3.0 2.9 %copy.46 = bf16[1,1,896,1152]{2,3,1,0:T(8,128)(2,1)S(1)} copy(bf16[1,1,896,1152]{3,2,1,0:T(8,128)(2,1)} %param.26) | data formatting | bytes 4128768 | tf_op args[0]
  5.9 1.3 %slice_bitcast_fusion.2 = (bf16[256,1152]{1,0:T(8,128)(2,1)S(1)}, bf16[256,1152]{1,0:T(8,128)(2,1)S(1)}) fusion(bf16[1,1,896,1152]{3,2,1,0:T(8,128)(2,1)} %param.26), kind=kLoop, calls=%fused_computation.48 | loop fusion | bytes 2359296 | tf_op jit(solution)/shard_map/slice | solution.py:251
  8.1 0.6 fusion.1
  9.5 0.7 fusion.45
  10.1 2.6 %broadcast_select_fusion.1 = (f32[512,1]{0,1:T(1,128)S(1)}, f32[512,1]{0,1:T(1,128)S(1)}) fusion(pred[512,1]{0,1:T(4,128)(4,1)S(1)} %copy-done.13, f32[]{:T(128)} %bitcast.14, f32[]{:T(128)} %bitcast.13, f32[]{:T(128)} %bitcast.31, f32[]{:T(128)} %bitcast.30), kind=kLoop, calls=%fused_computation.91 | loop fusion | flops 1024 | bytes 4624 | tf_op jit(solution)/shard_map/jit(_where)/select_n | solution.py:245
  12.7 2.6 %broadcast_select_fusion.5 = (f32[192,1]{0,1:T(1,128)S(1)}, f32[192,1]{0,1:T(1,128)S(1)}) fusion(pred[192,1]{0,1:T(4,128)(4,1)S(1)} %copy-done.14, f32[]{:T(128)} %bitcast.14, f32[]{:T(128)} %bitcast.13, f32[]{:T(128)} %bitcast.31, f32[]{:T(128)} %bitcast.30), kind=kLoop, calls=%fused_computation.99 | loop fusion | flops 384 | bytes 1744 | tf_op jit(solution)/shard_map/jit(_where)/select_n | solution.py:245
  15.3 1.1 pad_maximum_fusion.refs_8_
  16.9 2.1 %add_convert_fusion.1 = bf16[896,2,576]{0,2,1:T(8,128)(2,1)} fusion(f32[2,576]{1,0:T(2,128)S(1)} %add.112, f32[2,576]{1,0:T(2,128)S(1)} %mul.137, f32[896]{0:T(1024)S(1)} %add_rsqrt_fusion, f32[896]{0:T(1024)S(1)} %broadcast_multiply_fusion, bf16[896,2,576]{0,2,1:T(8,128)(2,1)S(1)} %bitcast.79), kind=kLoop, calls=%fused_computation.4 | loop fusion | flops 6193152 | bytes 4145152 | tf_op jit(solution)/shard_map/convert_element_type | solution.py:30
  19.1 1.4 %broadcast.90.clone = bf16[2,288,1728]{2,1,0:T(8,128)(2,1)} broadcast(bf16[]{:T(256)} %constant.115.clone.1), dimensions={} | broadcast | bytes 1990658 | tf_op jit(solution)/shard_map/broadcast.4
  20.7 1.0 bitcast_dynamic-update-slice_fusion.3
  22.2 2.2 %bitcast_dynamic-update-slice_fusion.2 = bf16[2,288,1728]{2,1,0:T(8,128)(2,1)} fusion(bf16[2,288,1728]{2,1,0:T(8,128)(2,1)} %bitcast_dynamic-update-slice_fusion.3, s32[]{:T(128)S(6)} %select_n.136, bf16[288,1728]{1,0:T(8,128)(2,1)} %collective-permute-done), kind=kLoop, calls=%fused_computation.38 | loop fusion | bytes 2064388 | tf_op jit(solution)/shard_map/jit(dynamic_update_index_in_dim)/dynamic_update_slice | solution.py:161
  24.4 4.5 %fusion.14 = f32[896,1728]{0,1:T(8,128)S(1)} fusion(bf16[576,1728]{1,0:T(8,128)(2,1)} %bitcast.5, bf16[896,2,576]{0,2,1:T(8,128)(2,1)S(1)} %copy-done.2, s32[]{:T(128)S(6)} %select_n.133), kind=kOutput, calls=%fused_computation.40 | convolution fusion | flops 1783627776 | bytes 9216004 | tf_op jit(solution)/shard_map/dot_general | solution.py:165
  29.1 2.1 %slice_bitcast_fusion.3 = (bf16[192,1152]{1,0:T(8,128)(2,1)}, bf16[192,1152]{1,0:T(8,128)(2,1)}) fusion(bf16[1,1,896,1152]{3,2,1,0:T(8,128)(2,1)} %param.26), kind=kLoop, calls=%fused_computation.51 | loop fusion | bytes 1769472 | tf_op jit(solution)/shard_map/slice | solution.py:268
  31.4 1.3 %bitcast_dynamic-update-slice_fusion.1 = bf16[2,288,1728]{2,1,0:T(8,128)(2,1)S(1)} fusion(bf16[2,288,1728]{2,1,0:T(8,128)(2,1)S(1)} %broadcast.90, s32[]{:T(128)S(6)} %select_n.135, bf16[288,1728]{1,0:T(8,128)(2,1)} %collective-permute-done.1), kind=kLoop, calls=%fused_computation.35 | loop fusion | bytes 2027524 | tf_op jit(solution)/shard_map/jit(dynamic_update_index_in_dim)/dynamic_update_slice | solution.py:160
  33.3 2.9 %fusion.12 = f32[896,1728]{0,1:T(8,128)S(1)} fusion(bf16[576,1728]{1,0:T(8,128)(2,1)S(1)} %bitcast.84, bf16[896,2,576]{0,2,1:T(8,128)(2,1)S(1)} %copy-done.2, s32[]{:T(128)S(6)} %select_n.137), kind=kOutput, calls=%fused_computation.36 | convolution fusion | flops 1783627776 | bytes 9289732 | tf_op jit(solution)/shard_map/dot_general | solution.py:165
  36.2 0.8 add_convert_fusion
  37.0 1.6 %fusion.38 = (bf16[896,1,8,72]{0,3,2,1:T(8,128)(2,1)S(1)}, bf16[896,1,8,72]{0,3,2,1:T(8,128)(2,1)}, bf16[8,72,896]{2,1,0:T(8,128)(2,1)}) fusion(bf16[896,3,8,72]{0,3,2,1:T(8,128)(2,1)S(1)} %bitcast.80), kind=kLoop, calls=%fused_computation.101 | loop fusion | bytes 6193152 | tf_op jit(solution)/shard_map/slice | solution.py:196
  38.6 1.9 %copy.55 = bf16[896,1,8,72]{3,0,2,1:T(8,128)(2,1)S(1)} copy(bf16[896,1,8,72]{0,3,2,1:T(8,128)(2,1)} %get-tuple-element.38) | data formatting | bytes 2064384
  40.5 0.9 fusion.40
  41.4 1.7 %copy.56 = bf16[896,1,8,72]{3,0,2,1:T(8,128)(2,1)} copy(bf16[896,1,8,72]{0,3,2,1:T(8,128)(2,1)S(1)} %get-tuple-element.37) | data formatting | bytes 2064384
  43.0 2.2 %pad_maximum_fusion.1.refs_0_.refs_4_ = bf16[8,512,72]{2,1,0:T(8,128)(2,1)} fusion(bf16[8,256,72]{2,1,0:T(8,128)(2,1)} %get-tuple-element.47, bf16[8,256,72]{2,1,0:T(8,128)(2,1)S(1)} %get-tuple-element.46), kind=kLoop, calls=%fused_computation.32 | loop fusion | flops 1179648 | bytes 1179648 | tf_op jit(solution)/shard_map/concatenate | solution.py:250
  45.4 1.0 bitcast_dynamic-update-slice_fusion.7
  46.6 1.0 bitcast_dynamic-update-slice_fusion.6
  47.7 1.0 bitcast_dynamic-update-slice_fusion.5
  48.8 1.8 %copy.49.refs_3_.refs_7_ = bf16[576,1152]{1,0:T(8,128)(2,1)} copy(bf16[576,1152]{0,1:T(8,128)(2,1)S(1)} %bitcast.83) | data formatting | bytes 2654208 | tf_op jit(solution)/shard_map/reshape | solution.py:191
  50.6 17.0 %shard_map.244 = bf16[512,1152]{1,0:T(8,128)(2,1)} custom-call(bf16[8,512,72]{2,1,0:T(8,128)(2,1)} %pad_maximum_fusion.1.refs_0_.refs_4_, bf16[8,72,896]{2,1,0:T(8,128)(2,1)} %get-tuple-element.39.refs_1_.refs_5_, bf16[8,896,72]{2,1,0:T(8,128)(2,1)} %bitcast.73, bf16[576,1152]{1,0:T(8,128)(2,1)} %copy.49.refs_3_.refs_7_, ...), custom_call_target="tpu_custom_call" | custom-call | tf_op jit(solution)/shard_map/pallas_call | solution.py:88
  67.6 1.8 %convolution_convert_fusion = bf16[256,1152]{1,0:T(8,128)(2,1)S(1)} fusion(bf16[512,1152]{1,0:T(8,128)(2,1)} %shard_map.244, s32[256]{0:T(256)S(1)} %eq.138), kind=kOutput, calls=%fused_computation.14 | convolution fusion | flops 302415872 | bytes 1770496 | tf_op jit(solution)/shard_map/dot_general | solution.py:222
  69.5 2.0 %collective-permute-start.6 = (bf16[64,1152]{1,0:T(8,128)(2,1)S(1)}, bf16[64,1152]{1,0:T(8,128)(2,1)S(1)}, u32[]{:S(2)}, u32[]{:S(2)}) collective-permute-start(bf16[64,1152]{1,0:T(8,128)(2,1)S(1)} %get-tuple-element.50), channel_id=1, source_target_pairs={{0,3},{1,0},{2,1},{3,2},{4,7},{5,4},{6,5},{7,6},{8,11},{9,8},{10,9... | collective-permute-start | bytes 442376 | tf_op jit(solution)/shard_map/ppermute | solution.py:231
  71.9 1.6 %collective-permute-start.9 = (bf16[64,1152]{1,0:T(8,128)(2,1)S(1)}, bf16[64,1152]{1,0:T(8,128)(2,1)S(1)}, u32[]{:S(2)}, u32[]{:S(2)}) collective-permute-start(bf16[64,1152]{1,0:T(8,128)(2,1)S(1)} %get-tuple-element.51), channel_id=1, source_target_pairs={{0,2},{1,3},{2,0},{3,1},{4,6},{5,7},{6,4},{7,5},{8,10},{9,11},{10,... | collective-permute-start | bytes 442376 | tf_op jit(solution)/shard_map/ppermute | solution.py:231
  73.5 0.9 fusion.39
  74.5 9.1 %shard_map.245 = bf16[192,1152]{1,0:T(8,128)(2,1)} custom-call(bf16[8,192,72]{2,1,0:T(8,128)(2,1)} %get-tuple-element.23.refs_0_.refs_4_, bf16[8,72,896]{2,1,0:T(8,128)(2,1)} %get-tuple-element.39.refs_1_.refs_5_, bf16[8,896,72]{2,1,0:T(8,128)(2,1)} %bitcast.75, bf16[576,1152]{1,0:T(8,128)(2,1)} %copy.49.refs_3_.refs_7_, ...), custom_call_target="tpu_custom_call" | custom-call | tf_op jit(solution)/shard_map/pallas_call | solution.py:88
  83.7 0.7 fusion.4
  84.6 3.7 %collective-permute-start.10 = (bf16[256,1152]{1,0:T(8,128)(2,1)S(1)}, bf16[256,1152]{1,0:T(8,128)(2,1)S(1)}, u32[]{:S(2)}, u32[]{:S(2)}) collective-permute-start(bf16[256,1152]{1,0:T(8,128)(2,1)S(1)} %get-tuple-element.33), channel_id=1, source_target_pairs={{0,4},{4,8},{8,12},{1,5},{5,9},{9,13},{2,6},{6,10},{10,14},{3,7},{... | collective-permute-start | bytes 1769480 | tf_op jit(solution)/shard_map/ppermute | solution.py:261
  88.2 1.3 %collective-permute-start.11 = (bf16[256,1152]{1,0:T(8,128)(2,1)S(1)}, bf16[256,1152]{1,0:T(8,128)(2,1)S(1)}, u32[]{:S(2)}, u32[]{:S(2)}) collective-permute-start(bf16[256,1152]{1,0:T(8,128)(2,1)S(1)} %get-tuple-element.28), channel_id=1, source_target_pairs={{4,0},{8,4},{12,8},{5,1},{9,5},{13,9},{6,2},{10,6},{14,10},{7,3},{... | collective-permute-start | bytes 1769480 | tf_op jit(solution)/shard_map/ppermute | solution.py:262
  89.8 0.9 collective-permute-start.12
  90.8 0.6 collective-permute-start.14
  91.4 1.7 %collective-permute-done.12 = bf16[24,1152]{1,0:T(8,128)(2,1)S(1)} collective-permute-done((bf16[24,1152]{1,0:T(8,128)(2,1)S(1)}, bf16[24,1152]{1,0:T(8,128)(2,1)S(1)}, u32[]{:S(2)}, u32[]{:S(2)}) %collective-permute-start.12) | collective-permute-done | bytes 55328 | tf_op jit(solution)/shard_map/ppermute | solution.py:231
  94.1 9.0 %shard_map.246 = bf16[192,1152]{1,0:T(8,128)(2,1)} custom-call(bf16[8,192,72]{2,1,0:T(8,128)(2,1)} %get-tuple-element.29.refs_0_.refs_4_, bf16[8,72,896]{2,1,0:T(8,128)(2,1)} %get-tuple-element.39.refs_1_.refs_5_, bf16[8,896,72]{2,1,0:T(8,128)(2,1)} %bitcast.77, bf16[576,1152]{1,0:T(8,128)(2,1)} %copy.49.refs_3_.refs_7_, ...), custom_call_target="tpu_custom_call" | custom-call | tf_op jit(solution)/shard_map/pallas_call | solution.py:88
  103.2 1.9 %collective-permute-done.11 = bf16[256,1152]{1,0:T(8,128)(2,1)S(1)} collective-permute-done((bf16[256,1152]{1,0:T(8,128)(2,1)S(1)}, bf16[256,1152]{1,0:T(8,128)(2,1)S(1)}, u32[]{:S(2)}, u32[]{:S(2)}) %collective-permute-start.11) | collective-permute-done | bytes 589856 | tf_op jit(solution)/shard_map/ppermute | solution.py:262
  105.1 1.3 %convolution_convert_fusion.1 = bf16[96,1152]{1,0:T(8,128)(2,1)S(1)} fusion(bf16[192,1152]{1,0:T(8,128)(2,1)} %shard_map.246, s32[96]{0:T(128)S(1)} %eq.142), kind=kOutput, calls=%fused_computation.16 | convolution fusion | flops 42596352 | bytes 663936 | tf_op jit(solution)/shard_map/dot_general | solution.py:222
  106.4 0.8 collective-permute-start.16
  107.3 1.3 %collective-permute-start.18 = (bf16[24,1152]{1,0:T(8,128)(2,1)S(1)}, bf16[24,1152]{1,0:T(8,128)(2,1)S(1)}, u32[]{:S(2)}, u32[]{:S(2)}) collective-permute-start(bf16[24,1152]{1,0:T(8,128)(2,1)S(1)} %get-tuple-element.56), channel_id=1, source_target_pairs={{0,2},{1,3},{2,0},{3,1},{4,6},{5,7},{6,4},{7,5},{8,10},{9,11},{10,... | collective-permute-start | bytes 165896 | tf_op jit(solution)/shard_map/ppermute | solution.py:231
  108.5 0.8 collective-permute-start.19
  110.4 1.0 collective-permute-done.17
  111.4 0.6 collective-permute-done.18
  112.0 1.3 %collective-permute-done.19 = bf16[24,1152]{1,0:T(8,128)(2,1)S(1)} collective-permute-done((bf16[24,1152]{1,0:T(8,128)(2,1)S(1)}, bf16[24,1152]{1,0:T(8,128)(2,1)S(1)}, u32[]{:S(2)}, u32[]{:S(2)}) %collective-permute-start.19) | collective-permute-done | bytes 55328 | tf_op jit(solution)/shard_map/ppermute | solution.py:231
  113.7 1.5 %maximum_bitcast_fusion = bf16[1,1,896,1152]{3,2,1,0:T(8,128)(2,1)} fusion(bf16[256,1152]{1,0:T(8,128)(2,1)S(1)} %fusion.11, bf16[192,1152]{1,0:T(8,128)(2,1)S(1)} %fusion.19, bf16[192,1152]{1,0:T(8,128)(2,1)S(1)} %fusion.7, bf16[256,1152]{1,0:T(8,128)(2,1)S(1)} %fusion.9), kind=kLoop, calls=%fused_computation.18 | loop fusion | flops 8257536 | bytes 4128768 | tf_op jit(solution)/shard_map/reshape | solution.py:302
  (115 shorter events, 7.8 us)
Async XLA Ops:
  0.0 7.2 %copy-start = (s32[4,4,4]{2,1,0:T(4,128)S(1)}, s32[4,4,4]{2,1,0:T(4,128)}, u32[]{:S(2)}) copy-start(s32[4,4,4]{2,1,0:T(4,128)} %param.30) | copy-start | bytes 772
  0.0 22.2 %collective-permute-start = (bf16[288,1728]{1,0:T(8,128)(2,1)}, bf16[288,1728]{1,0:T(8,128)(2,1)}, u32[]{:S(2)}, u32[]{:S(2)}) collective-permute-start(bf16[288,1728]{1,0:T(8,128)(2,1)} %param.28), channel_id=1, source_target_pairs={{1,0},{0,1},{3,2},{2,3},{5,4},{4,5},{7,6},{6,7},{9,8},{8,9},{11,10... | collective-permute-start | bytes 2985992 | tf_op jit(solution)/shard_map/ppermute | solution.py:154
  0.5 28.4 %collective-permute-start.1 = (bf16[288,1728]{1,0:T(8,128)(2,1)}, bf16[288,1728]{1,0:T(8,128)(2,1)}, u32[]{:S(2)}, u32[]{:S(2)}) collective-permute-start(bf16[288,1728]{1,0:T(8,128)(2,1)} %param.28), channel_id=1, source_target_pairs={{2,0},{3,1},{0,2},{1,3},{6,4},{7,5},{4,6},{5,7},{10,8},{11,9},{8,1... | collective-permute-start | bytes 2985992 | tf_op jit(solution)/shard_map/ppermute | solution.py:154
  7.6 1.1 copy-start.6
  7.6 1.7 %copy-start.15 = (s32[2]{0:T(128)S(1)}, s32[2]{0:T(128)}, u32[]{:S(2)}) copy-start(s32[2]{0:T(128)} %param.31) | copy-start | bytes 28
  7.7 2.5 %copy-start.13 = (pred[512,1]{0,1:T(4,128)(4,1)S(1)}, pred[512,1]{0,1:T(4,128)(4,1)}, u32[]{:S(2)}) copy-start(pred[512,1]{0,1:T(4,128)(4,1)} %constant.122.clone) | copy-start | bytes 1540
  7.7 5.0 %copy-start.14 = (pred[192,1]{0,1:T(4,128)(4,1)S(1)}, pred[192,1]{0,1:T(4,128)(4,1)}, u32[]{:S(2)}) copy-start(pred[192,1]{0,1:T(4,128)(4,1)} %constant.127.clone) | copy-start | bytes 580
  8.1 8.4 %copy-start.17 = (s32[4]{0:T(128)S(1)}, s32[4]{0:T(128)}, u32[]{:S(2)}) copy-start(s32[4]{0:T(128)} %constant.118.clone) | copy-start | bytes 52
  8.1 8.4 %copy-start.10 = (s32[4,64]{1,0:T(4,128)S(1)}, s32[4,64]{1,0:T(4,128)}, u32[]{:S(2)}) copy-start(s32[4,64]{1,0:T(4,128)} %constant.119.clone) | copy-start | bytes 3076
  8.1 8.4 %copy-start.11 = (s32[4,64]{1,0:T(4,128)S(1)}, s32[4,64]{1,0:T(4,128)}, u32[]{:S(2)}) copy-start(s32[4,64]{1,0:T(4,128)} %constant.120.clone) | copy-start | bytes 3076
  8.1 8.5 %copy-start.8 = (s32[4,24]{1,0:T(4,128)S(1)}, s32[4,24]{1,0:T(4,128)}, u32[]{:S(2)}) copy-start(s32[4,24]{1,0:T(4,128)} %constant.124.clone) | copy-start | bytes 1156
  8.1 8.5 %copy-start.9 = (s32[4,24]{1,0:T(4,128)S(1)}, s32[4,24]{1,0:T(4,128)}, u32[]{:S(2)}) copy-start(s32[4,24]{1,0:T(4,128)} %constant.125.clone) | copy-start | bytes 1156
  8.1 8.5 %copy-start.12 = (s32[4,64]{1,0:T(4,128)S(1)}, s32[4,64]{1,0:T(4,128)}, u32[]{:S(2)}) copy-start(s32[4,64]{1,0:T(4,128)} %constant.132) | copy-start | bytes 3076
  19.1 1.6 %copy-start.5 = (bf16[288,1728]{1,0:T(8,128)(2,1)S(1)}, bf16[288,1728]{1,0:T(8,128)(2,1)}, u32[]{:S(2)}) copy-start(bf16[288,1728]{1,0:T(8,128)(2,1)} %param.28) | copy-start | bytes 2985988
  19.1 3.0 %copy-start.16 = (s32[4]{0:T(128)S(1)}, s32[4]{0:T(128)}, u32[]{:S(2)}) copy-start(s32[4]{0:T(128)} %param.32) | copy-start | bytes 52
  20.7 3.8 %copy-start.2 = (bf16[896,2,576]{0,2,1:T(8,128)(2,1)S(1)}, bf16[896,2,576]{0,2,1:T(8,128)(2,1)}, u32[]{:S(2)}) copy-start(bf16[896,2,576]{0,2,1:T(8,128)(2,1)} %add_convert_fusion.1) | copy-start | bytes 6193156
  28.9 3.8 %collective-permute-start.2 = (bf16[288,1728]{1,0:T(8,128)(2,1)}, bf16[288,1728]{1,0:T(8,128)(2,1)S(1)}, u32[]{:S(2)}, u32[]{:S(2)}) collective-permute-start(bf16[288,1728]{1,0:T(8,128)(2,1)} %collective-permute-done.1), channel_id=1, source_target_pairs={{1,0},{0,1},{3,2},{2,3},{5,4},{4,5},{7,6},{6,7},{9,8},{8,9},{11,10... | collective-permute-start | bytes 2985992 | tf_op jit(solution)/shard_map/ppermute | solution.py:154
  32.7 13.9 %collective-permute-start.3 = (bf16[576,288]{0,1:T(8,128)(2,1)}, bf16[576,288]{0,1:T(8,128)(2,1)}, u32[]{:S(2)}, u32[]{:S(2)}) collective-permute-start(bf16[576,288]{0,1:T(8,128)(2,1)} %param.29), channel_id=1, source_target_pairs={{1,0},{0,1},{3,2},{2,3},{5,4},{4,5},{7,6},{6,7},{9,8},{8,9},{11,10... | collective-permute-start | bytes 995336 | tf_op jit(solution)/shard_map/ppermute | solution.py:104
  33.2 13.3 %collective-permute-start.4 = (bf16[576,288]{0,1:T(8,128)(2,1)}, bf16[576,288]{0,1:T(8,128)(2,1)}, u32[]{:S(2)}, u32[]{:S(2)}) collective-permute-start(bf16[576,288]{0,1:T(8,128)(2,1)} %param.29), channel_id=1, source_target_pairs={{2,0},{3,1},{0,2},{1,3},{6,4},{7,5},{4,6},{5,7},{10,8},{11,9},{8,1... | collective-permute-start | bytes 995336 | tf_op jit(solution)/shard_map/ppermute | solution.py:104
  46.4 2.3 %collective-permute-start.5 = (bf16[576,288]{0,1:T(8,128)(2,1)}, bf16[576,288]{0,1:T(8,128)(2,1)S(1)}, u32[]{:S(2)}, u32[]{:S(2)}) collective-permute-start(bf16[576,288]{0,1:T(8,128)(2,1)} %collective-permute-done.4), channel_id=1, source_target_pairs={{1,0},{0,1},{3,2},{2,3},{5,4},{4,5},{7,6},{6,7},{9,8},{8,9},{11,10... | collective-permute-start | bytes 995336 | tf_op jit(solution)/shard_map/ppermute | solution.py:104
  69.5 14.1 %collective-permute-start.6 = (bf16[64,1152]{1,0:T(8,128)(2,1)S(1)}, bf16[64,1152]{1,0:T(8,128)(2,1)S(1)}, u32[]{:S(2)}, u32[]{:S(2)}) collective-permute-start(bf16[64,1152]{1,0:T(8,128)(2,1)S(1)} %get-tuple-element.50), channel_id=1, source_target_pairs={{0,3},{1,0},{2,1},{3,2},{4,7},{5,4},{6,5},{7,6},{8,11},{9,8},{10,9... | collective-permute-start | bytes 442376 | tf_op jit(solution)/shard_map/ppermute | solution.py:231
  71.5 12.1 %collective-permute-start.7 = (bf16[64,1152]{1,0:T(8,128)(2,1)S(1)}, bf16[64,1152]{1,0:T(8,128)(2,1)S(1)}, u32[]{:S(2)}, u32[]{:S(2)}) collective-permute-start(bf16[64,1152]{1,0:T(8,128)(2,1)S(1)} %get-tuple-element.53), channel_id=1, source_target_pairs={{0,1},{1,2},{2,3},{3,0},{4,5},{5,6},{6,7},{7,4},{8,9},{9,10},{10,1... | collective-permute-start | bytes 442376 | tf_op jit(solution)/shard_map/ppermute | solution.py:231
  71.5 12.1 %collective-permute-start.8 = (bf16[64,1152]{1,0:T(8,128)(2,1)S(1)}, bf16[64,1152]{1,0:T(8,128)(2,1)S(1)}, u32[]{:S(2)}, u32[]{:S(2)}) collective-permute-start(bf16[64,1152]{1,0:T(8,128)(2,1)S(1)} %get-tuple-element.52), channel_id=1, source_target_pairs={{0,2},{1,3},{2,0},{3,1},{4,6},{5,7},{6,4},{7,5},{8,10},{9,11},{10,... | collective-permute-start | bytes 442376 | tf_op jit(solution)/shard_map/ppermute | solution.py:231
  71.9 11.7 %collective-permute-start.9 = (bf16[64,1152]{1,0:T(8,128)(2,1)S(1)}, bf16[64,1152]{1,0:T(8,128)(2,1)S(1)}, u32[]{:S(2)}, u32[]{:S(2)}) collective-permute-start(bf16[64,1152]{1,0:T(8,128)(2,1)S(1)} %get-tuple-element.51), channel_id=1, source_target_pairs={{0,2},{1,3},{2,0},{3,1},{4,6},{5,7},{6,4},{7,5},{8,10},{9,11},{10,... | collective-permute-start | bytes 442376 | tf_op jit(solution)/shard_map/ppermute | solution.py:231
  74.5 9.2 %copy-start.1 = (bf16[512,1152]{1,0:T(8,128)(2,1)S(1)}, bf16[512,1152]{1,0:T(8,128)(2,1)}, u32[]{:S(2)}) copy-start(bf16[512,1152]{1,0:T(8,128)(2,1)} %shard_map.244) | copy-start | bytes 3538948
  74.5 9.2 %copy-start.19 = (pred[512]{0:T(512)(128)(4,1)S(1)}, pred[512]{0:T(512)(128)(4,1)}, u32[]{:S(2)}) copy-start(pred[512]{0:T(512)(128)(4,1)} %constant.131) | copy-start | bytes 1540
  84.4 5.1 %copy-start.3 = (bf16[192,1152]{1,0:T(8,128)(2,1)S(1)}, bf16[192,1152]{1,0:T(8,128)(2,1)}, u32[]{:S(2)}) copy-start(bf16[192,1152]{1,0:T(8,128)(2,1)} %shard_map.245) | copy-start | bytes 1327108
  84.4 8.7 %copy-start.7 = (s32[4,24]{1,0:T(4,128)S(1)}, s32[4,24]{1,0:T(4,128)}, u32[]{:S(2)}) copy-start(s32[4,24]{1,0:T(4,128)} %constant.134) | copy-start | bytes 1156
  84.6 18.6 %collective-permute-start.10 = (bf16[256,1152]{1,0:T(8,128)(2,1)S(1)}, bf16[256,1152]{1,0:T(8,128)(2,1)S(1)}, u32[]{:S(2)}, u32[]{:S(2)}) collective-permute-start(bf16[256,1152]{1,0:T(8,128)(2,1)S(1)} %get-tuple-element.33), channel_id=1, source_target_pairs={{0,4},{4,8},{8,12},{1,5},{5,9},{9,13},{2,6},{6,10},{10,14},{3,7},{... | collective-permute-start | bytes 1769480 | tf_op jit(solution)/shard_map/ppermute | solution.py:261
  88.2 16.9 %collective-permute-start.11 = (bf16[256,1152]{1,0:T(8,128)(2,1)S(1)}, bf16[256,1152]{1,0:T(8,128)(2,1)S(1)}, u32[]{:S(2)}, u32[]{:S(2)}) collective-permute-start(bf16[256,1152]{1,0:T(8,128)(2,1)S(1)} %get-tuple-element.28), channel_id=1, source_target_pairs={{4,0},{8,4},{12,8},{5,1},{9,5},{13,9},{6,2},{10,6},{14,10},{7,3},{... | collective-permute-start | bytes 1769480 | tf_op jit(solution)/shard_map/ppermute | solution.py:262
  89.8 3.2 %collective-permute-start.12 = (bf16[24,1152]{1,0:T(8,128)(2,1)S(1)}, bf16[24,1152]{1,0:T(8,128)(2,1)S(1)}, u32[]{:S(2)}, u32[]{:S(2)}) collective-permute-start(bf16[24,1152]{1,0:T(8,128)(2,1)S(1)} %get-tuple-element.58), channel_id=1, source_target_pairs={{0,3},{1,0},{2,1},{3,2},{4,7},{5,4},{6,5},{7,6},{8,11},{9,8},{10,9... | collective-permute-start | bytes 165896 | tf_op jit(solution)/shard_map/ppermute | solution.py:231
  90.8 12.4 %collective-permute-start.13 = (bf16[24,1152]{1,0:T(8,128)(2,1)S(1)}, bf16[24,1152]{1,0:T(8,128)(2,1)S(1)}, u32[]{:S(2)}, u32[]{:S(2)}) collective-permute-start(bf16[24,1152]{1,0:T(8,128)(2,1)S(1)} %get-tuple-element.61), channel_id=1, source_target_pairs={{0,1},{1,2},{2,3},{3,0},{4,5},{5,6},{6,7},{7,4},{8,9},{9,10},{10,1... | collective-permute-start | bytes 165896 | tf_op jit(solution)/shard_map/ppermute | solution.py:231
  90.8 12.4 %collective-permute-start.14 = (bf16[24,1152]{1,0:T(8,128)(2,1)S(1)}, bf16[24,1152]{1,0:T(8,128)(2,1)S(1)}, u32[]{:S(2)}, u32[]{:S(2)}) collective-permute-start(bf16[24,1152]{1,0:T(8,128)(2,1)S(1)} %get-tuple-element.60), channel_id=1, source_target_pairs={{0,2},{1,3},{2,0},{3,1},{4,6},{5,7},{6,4},{7,5},{8,10},{9,11},{10,... | collective-permute-start | bytes 165896 | tf_op jit(solution)/shard_map/ppermute | solution.py:231
  93.0 10.1 %collective-permute-start.15 = (bf16[24,1152]{1,0:T(8,128)(2,1)S(1)}, bf16[24,1152]{1,0:T(8,128)(2,1)S(1)}, u32[]{:S(2)}, u32[]{:S(2)}) collective-permute-start(bf16[24,1152]{1,0:T(8,128)(2,1)S(1)} %get-tuple-element.59), channel_id=1, source_target_pairs={{0,2},{1,3},{2,0},{3,1},{4,6},{5,7},{6,4},{7,5},{8,10},{9,11},{10,... | collective-permute-start | bytes 165896 | tf_op jit(solution)/shard_map/ppermute | solution.py:231
  106.4 3.6 %copy-start.18 = (pred[192]{0:T(512)(128)(4,1)S(1)}, pred[192]{0:T(512)(128)(4,1)}, u32[]{:S(2)}) copy-start(pred[192]{0:T(512)(128)(4,1)} %constant.133) | copy-start | bytes 580
  106.4 3.9 %collective-permute-start.16 = (bf16[24,1152]{1,0:T(8,128)(2,1)S(1)}, bf16[24,1152]{1,0:T(8,128)(2,1)S(1)}, u32[]{:S(2)}, u32[]{:S(2)}) collective-permute-start(bf16[24,1152]{1,0:T(8,128)(2,1)S(1)} %get-tuple-element.54), channel_id=1, source_target_pairs={{0,3},{1,0},{2,1},{3,2},{4,7},{5,4},{6,5},{7,6},{8,11},{9,8},{10,9... | collective-permute-start | bytes 165896 | tf_op jit(solution)/shard_map/ppermute | solution.py:231
  107.3 4.1 %collective-permute-start.17 = (bf16[24,1152]{1,0:T(8,128)(2,1)S(1)}, bf16[24,1152]{1,0:T(8,128)(2,1)S(1)}, u32[]{:S(2)}, u32[]{:S(2)}) collective-permute-start(bf16[24,1152]{1,0:T(8,128)(2,1)S(1)} %get-tuple-element.57), channel_id=1, source_target_pairs={{0,1},{1,2},{2,3},{3,0},{4,5},{5,6},{6,7},{7,4},{8,9},{9,10},{10,1... | collective-permute-start | bytes 165896 | tf_op jit(solution)/shard_map/ppermute | solution.py:231
  107.3 4.8 %collective-permute-start.18 = (bf16[24,1152]{1,0:T(8,128)(2,1)S(1)}, bf16[24,1152]{1,0:T(8,128)(2,1)S(1)}, u32[]{:S(2)}, u32[]{:S(2)}) collective-permute-start(bf16[24,1152]{1,0:T(8,128)(2,1)S(1)} %get-tuple-element.56), channel_id=1, source_target_pairs={{0,2},{1,3},{2,0},{3,1},{4,6},{5,7},{6,4},{7,5},{8,10},{9,11},{10,... | collective-permute-start | bytes 165896 | tf_op jit(solution)/shard_map/ppermute | solution.py:231
  108.5 4.8 %collective-permute-start.19 = (bf16[24,1152]{1,0:T(8,128)(2,1)S(1)}, bf16[24,1152]{1,0:T(8,128)(2,1)S(1)}, u32[]{:S(2)}, u32[]{:S(2)}) collective-permute-start(bf16[24,1152]{1,0:T(8,128)(2,1)S(1)} %get-tuple-element.55), channel_id=1, source_target_pairs={{0,2},{1,3},{2,0},{3,1},{4,6},{5,7},{6,4},{7,5},{8,10},{9,11},{10,... | collective-permute-start | bytes 165896 | tf_op jit(solution)/shard_map/ppermute | solution.py:231
  109.7 3.7 %copy-start.4 = (bf16[192,1152]{1,0:T(8,128)(2,1)S(1)}, bf16[192,1152]{1,0:T(8,128)(2,1)}, u32[]{:S(2)}) copy-start(bf16[192,1152]{1,0:T(8,128)(2,1)} %shard_map.246) | copy-start | bytes 1327108

commit v14 on v13

--- a/solution.py
+++ b/solution.py
@@ -241,11 +241,14 @@
         token_ids = jnp.arange(part_tokens, dtype=jnp.int32)
         place = (token_ids[:, None] == recv_cells[None, :]).astype(jnp.bfloat16)
         partner = jnp.dot(place, arrived, preferred_element_type=jnp.float32)
-        dep = strip_depth(part_frames)[:, None]
+        dep = strip_depth(1)[:, None]
         w_keep = jnp.where(dep == 0, keep[0], keep[1])
         w_take = jnp.where(dep == 0, take[0], take[1])
-        own = tile_out.astype(jnp.float32)
-        return jnp.where(dep >= 0, w_keep * own + w_take * partner, own).astype(jnp.bfloat16)
+        grid_shape = (part_frames, S * S, tile_out.shape[1])
+        own = tile_out.astype(jnp.float32).reshape(grid_shape)
+        partner = partner.reshape(grid_shape)
+        mixed = jnp.where(dep >= 0, w_keep * own + w_take * partner, own)
+        return mixed.reshape(tile_out.shape).astype(jnp.bfloat16)
 
     rim_queries = jnp.concatenate([queries[:, :rim], queries[:, tokens - rim :]], axis=1)
     rim_in = jnp.concatenate([block_in[:rim], block_in[tokens - rim :]], axis=0)

time: 116 us -> 115 us (level)
  starting transfers between devices: 17.4 us -> 20.1 us
  other arithmetic: 15.9 us -> 13.2 us
  waiting for transfers between devices: 6.58 us -> 4.79 us
    select_n x2 -> x0, other arithmetic: 5.16 us -> none  [space_blend(): w_keep = jnp.where(dep == 0, keep[0], keep[1])]
    mul x0 -> x1, other arithmetic: none -> 2.46 us  [space_blend(): mixed = jnp.where(dep >= 0, w_keep * own + w_take * partner, own)]
    ppermute x6, starting transfers between devices: 3.89 us -> 5.4 us  [fetch(): return lax.ppermute(x, 'face', [(src_of(i), i) for i in range(n)])]
    ppermute x12, waiting for transfers between devices: 4.64 us -> 3.23 us  [strips_in(): lax.ppermute(sent, 'face', [(i, (i + shift) % n) for i in range(n)])]
    unnamed x43 -> x39, local copies, waits for them, and re-layouts: 6.72 us -> 6.7 us
  transfers between devices with their start and end apart: 20 -> 20, of which waited for: 5 -> 7; matrix products, arithmetic and copies ran while one was open for 41% -> 40% of each run, Pallas kernels for 16% -> 16%
where the time goes in v14:
time: 115 us; the launch traced here: 114 us
  Pallas kernels  35.1 us (31%)
  local copies, waits for them, and re-layouts  28 us (24%)
  starting transfers between devices  20.1 us (17%)
  other arithmetic  13.2 us (11%)
  matrix products  12.1 us (11%)
  waiting for transfers between devices  4.79 us (4%)
    pallas_call x3, Pallas kernels, attend_project(): pl.pallas_call(attention_kernel, grid=(1, heads // hb), in_specs=in_specs...  35.1 us
    ppermute x12, starting transfers between devices, strips_in(): lax.ppermute(sent, 'face', [(i, (i + shift) % n) for i in range(n)])  9.51 us
    dot_general x2, matrix products, chip_part(): jnp.dot(lax.dynamic_index_in_dim(moved_chips, chip, 0, keepdims=False), w...  7.34 us
    unnamed x39, local copies, waits for them, and re-layouts  6.7 us
    ppermute x6, starting transfers between devices, fetch(): return lax.ppermute(x, 'face', [(src_of(i), i) for i in range(n)])  5.4 us
    ppermute x1, starting transfers between devices, per_device(): lower = lax.ppermute(high, 'tm', [(i, i + 1) for i in range(count - 1)])  3.91 us
    dot_general x3, matrix products, strips_out(): jnp.dot(pick, tile_out, preferred_element_type=jnp.float32)  3.36 us
    ppermute x12, waiting for transfers between devices, strips_in(): lax.ppermute(sent, 'face', [(i, (i + shift) % n) for i in range(n)])  3.23 us
  transfers between devices with their start and end apart: 20, of which 7 were waited for; matrix products, arithmetic and copies ran while one was open for 40% of the time, Pallas kernels for 16%

profile of v14, /device:TPU:0, one launch (start us, length us, event | category | flops | bytes accessed | tf_op | source)
XLA Modules:
  0.0 113.8 jit_solution(13344323894009887821)
XLA Ops:
  0.5 2.6 %collective-permute-start.1 = (bf16[288,1728]{1,0:T(8,128)(2,1)}, bf16[288,1728]{1,0:T(8,128)(2,1)}, u32[]{:S(2)}, u32[]{:S(2)}) collective-permute-start(bf16[288,1728]{1,0:T(8,128)(2,1)} %param.28), channel_id=1, source_target_pairs={{2,0},{3,1},{0,2},{1,3},{6,4},{7,5},{4,6},{5,7},{10,8},{11,9},{8,1... | collective-permute-start | bytes 2985992 | tf_op jit(solution)/shard_map/ppermute | solution.py:154
  3.0 2.9 %copy.46 = bf16[1,1,896,1152]{2,3,1,0:T(8,128)(2,1)S(1)} copy(bf16[1,1,896,1152]{3,2,1,0:T(8,128)(2,1)} %param.26) | data formatting | bytes 4128768 | tf_op args[0]
  5.9 1.3 %slice_bitcast_fusion.2 = (bf16[256,1152]{1,0:T(8,128)(2,1)S(1)}, bf16[256,1152]{1,0:T(8,128)(2,1)S(1)}) fusion(bf16[1,1,896,1152]{3,2,1,0:T(8,128)(2,1)} %param.26), kind=kLoop, calls=%fused_computation.48 | loop fusion | bytes 2359296 | tf_op jit(solution)/shard_map/slice | solution.py:254
  8.1 0.6 fusion.1
  8.7 0.6 add_reduce_fusion
  9.4 1.1 pad_maximum_fusion.refs_8_
  10.7 0.7 fusion.45
  11.5 2.5 %select_bitcast_fusion.1 = (f32[64]{0:T(128)S(1)}, f32[64]{0:T(128)S(1)}) fusion(pred[64,1]{0,1:T(4,128)(4,1)S(1)} %copy-done.13, f32[]{:T(128)} %bitcast.14, f32[]{:T(128)} %bitcast.13, f32[]{:T(128)} %bitcast.31, f32[]{:T(128)} %bitcast.30), kind=kLoop, calls=%fused_computation.97 | loop fusion | flops 128 | bytes 592 | tf_op jit(solution)/shard_map/mul | solution.py:250
  14.2 2.1 %add_convert_fusion.1 = bf16[896,2,576]{0,2,1:T(8,128)(2,1)} fusion(f32[2,576]{1,0:T(2,128)S(1)} %add.115, f32[2,576]{1,0:T(2,128)S(1)} %mul.167, f32[896]{0:T(1024)S(1)} %add_rsqrt_fusion, f32[896]{0:T(1024)S(1)} %broadcast_multiply_fusion, bf16[896,2,576]{0,2,1:T(8,128)(2,1)S(1)} %bitcast.79), kind=kLoop, calls=%fused_computation.4 | loop fusion | flops 6193152 | bytes 4145152 | tf_op jit(solution)/shard_map/convert_element_type | solution.py:30
  16.3 1.4 %broadcast.117.clone = bf16[2,288,1728]{2,1,0:T(8,128)(2,1)} broadcast(bf16[]{:T(256)} %constant.111.clone.1), dimensions={} | broadcast | bytes 1990658 | tf_op jit(solution)/shard_map/broadcast.4
  17.9 1.0 bitcast_dynamic-update-slice_fusion.3
  19.7 2.2 %bitcast_dynamic-update-slice_fusion.2 = bf16[2,288,1728]{2,1,0:T(8,128)(2,1)} fusion(bf16[2,288,1728]{2,1,0:T(8,128)(2,1)} %bitcast_dynamic-update-slice_fusion.3, s32[]{:T(128)S(6)} %select_n.138, bf16[288,1728]{1,0:T(8,128)(2,1)} %collective-permute-done), kind=kLoop, calls=%fused_computation.38 | loop fusion | bytes 2064388 | tf_op jit(solution)/shard_map/jit(dynamic_update_index_in_dim)/dynamic_update_slice | solution.py:161
  22.0 4.5 %fusion.14 = f32[896,1728]{0,1:T(8,128)S(1)} fusion(bf16[576,1728]{1,0:T(8,128)(2,1)} %bitcast.5, bf16[896,2,576]{0,2,1:T(8,128)(2,1)S(1)} %copy-done.2, s32[]{:T(128)S(6)} %select_n.135), kind=kOutput, calls=%fused_computation.40 | convolution fusion | flops 1783627776 | bytes 9216004 | tf_op jit(solution)/shard_map/dot_general | solution.py:165
  26.7 2.1 %slice_bitcast_fusion.3 = (bf16[192,1152]{1,0:T(8,128)(2,1)}, bf16[192,1152]{1,0:T(8,128)(2,1)}) fusion(bf16[1,1,896,1152]{3,2,1,0:T(8,128)(2,1)} %param.26), kind=kLoop, calls=%fused_computation.51 | loop fusion | bytes 1769472 | tf_op jit(solution)/shard_map/slice | solution.py:271
  29.0 1.3 %bitcast_dynamic-update-slice_fusion.1 = bf16[2,288,1728]{2,1,0:T(8,128)(2,1)S(1)} fusion(bf16[2,288,1728]{2,1,0:T(8,128)(2,1)S(1)} %broadcast.117, s32[]{:T(128)S(6)} %select_n.137, bf16[288,1728]{1,0:T(8,128)(2,1)} %collective-permute-done.1), kind=kLoop, calls=%fused_computation.35 | loop fusion | bytes 2027524 | tf_op jit(solution)/shard_map/jit(dynamic_update_index_in_dim)/dynamic_update_slice | solution.py:160
  30.4 0.6 collective-permute-start.3
  30.9 1.7 %collective-permute-start.4 = (bf16[576,288]{0,1:T(8,128)(2,1)}, bf16[576,288]{0,1:T(8,128)(2,1)}, u32[]{:S(2)}, u32[]{:S(2)}) collective-permute-start(bf16[576,288]{0,1:T(8,128)(2,1)} %param.29), channel_id=1, source_target_pairs={{2,0},{3,1},{0,2},{1,3},{6,4},{7,5},{4,6},{5,7},{10,8},{11,9},{8,1... | collective-permute-start | bytes 995336 | tf_op jit(solution)/shard_map/ppermute | solution.py:104
  32.8 2.9 %fusion.12 = f32[896,1728]{0,1:T(8,128)S(1)} fusion(bf16[576,1728]{1,0:T(8,128)(2,1)S(1)} %bitcast.84, bf16[896,2,576]{0,2,1:T(8,128)(2,1)S(1)} %copy-done.2, s32[]{:T(128)S(6)} %select_n.139), kind=kOutput, calls=%fused_computation.36 | convolution fusion | flops 1783627776 | bytes 9289732 | tf_op jit(solution)/shard_map/dot_general | solution.py:165
  35.6 0.8 add_convert_fusion
  36.5 1.6 %fusion.38 = (bf16[896,1,8,72]{0,3,2,1:T(8,128)(2,1)S(1)}, bf16[896,1,8,72]{0,3,2,1:T(8,128)(2,1)}, bf16[8,72,896]{2,1,0:T(8,128)(2,1)}) fusion(bf16[896,3,8,72]{0,3,2,1:T(8,128)(2,1)S(1)} %bitcast.80), kind=kLoop, calls=%fused_computation.99 | loop fusion | bytes 6193152 | tf_op jit(solution)/shard_map/slice | solution.py:196
  38.0 1.9 %copy.55 = bf16[896,1,8,72]{3,0,2,1:T(8,128)(2,1)S(1)} copy(bf16[896,1,8,72]{0,3,2,1:T(8,128)(2,1)} %get-tuple-element.38) | data formatting | bytes 2064384
  40.0 0.9 fusion.40
  40.9 1.7 %copy.56 = bf16[896,1,8,72]{3,0,2,1:T(8,128)(2,1)} copy(bf16[896,1,8,72]{0,3,2,1:T(8,128)(2,1)S(1)} %get-tuple-element.37) | data formatting | bytes 2064384
  42.5 2.2 %pad_maximum_fusion.1.refs_0_.refs_4_ = bf16[8,512,72]{2,1,0:T(8,128)(2,1)} fusion(bf16[8,256,72]{2,1,0:T(8,128)(2,1)} %get-tuple-element.47, bf16[8,256,72]{2,1,0:T(8,128)(2,1)S(1)} %get-tuple-element.46), kind=kLoop, calls=%fused_computation.32 | loop fusion | flops 1179648 | bytes 1179648 | tf_op jit(solution)/shard_map/concatenate | solution.py:253
  44.8 1.0 bitcast_dynamic-update-slice_fusion.7
  46.0 1.0 bitcast_dynamic-update-slice_fusion.6
  47.0 1.0 bitcast_dynamic-update-slice_fusion.5
  48.1 1.8 %copy.49.refs_3_.refs_7_ = bf16[576,1152]{1,0:T(8,128)(2,1)} copy(bf16[576,1152]{0,1:T(8,128)(2,1)S(1)} %bitcast.83) | data formatting | bytes 2654208 | tf_op jit(solution)/shard_map/reshape | solution.py:191
  49.9 17.0 %shard_map.253 = bf16[512,1152]{1,0:T(8,128)(2,1)} custom-call(bf16[8,512,72]{2,1,0:T(8,128)(2,1)} %pad_maximum_fusion.1.refs_0_.refs_4_, bf16[8,72,896]{2,1,0:T(8,128)(2,1)} %get-tuple-element.39.refs_1_.refs_5_, bf16[8,896,72]{2,1,0:T(8,128)(2,1)} %bitcast.73, bf16[576,1152]{1,0:T(8,128)(2,1)} %copy.49.refs_3_.refs_7_, ...), custom_call_target="tpu_custom_call" | custom-call | tf_op jit(solution)/shard_map/pallas_call | solution.py:88
  66.9 1.8 %convolution_convert_fusion = bf16[256,1152]{1,0:T(8,128)(2,1)S(1)} fusion(bf16[512,1152]{1,0:T(8,128)(2,1)} %shard_map.253, s32[256]{0:T(256)S(1)} %eq.138), kind=kOutput, calls=%fused_computation.14 | convolution fusion | flops 302415872 | bytes 1770496 | tf_op jit(solution)/shard_map/dot_general | solution.py:222
  69.4 1.6 %collective-permute-start.8 = (bf16[64,1152]{1,0:T(8,128)(2,1)S(1)}, bf16[64,1152]{1,0:T(8,128)(2,1)S(1)}, u32[]{:S(2)}, u32[]{:S(2)}) collective-permute-start(bf16[64,1152]{1,0:T(8,128)(2,1)S(1)} %get-tuple-element.52), channel_id=1, source_target_pairs={{0,2},{1,3},{2,0},{3,1},{4,6},{5,7},{6,4},{7,5},{8,10},{9,11},{10,... | collective-permute-start | bytes 442376 | tf_op jit(solution)/shard_map/ppermute | solution.py:231
  71.4 1.0 fusion.39
  72.4 9.1 %shard_map.254 = bf16[192,1152]{1,0:T(8,128)(2,1)} custom-call(bf16[8,192,72]{2,1,0:T(8,128)(2,1)} %get-tuple-element.23.refs_0_.refs_4_, bf16[8,72,896]{2,1,0:T(8,128)(2,1)} %get-tuple-element.39.refs_1_.refs_5_, bf16[8,896,72]{2,1,0:T(8,128)(2,1)} %bitcast.75, bf16[576,1152]{1,0:T(8,128)(2,1)} %copy.49.refs_3_.refs_7_, ...), custom_call_target="tpu_custom_call" | custom-call | tf_op jit(solution)/shard_map/pallas_call | solution.py:88
  81.7 0.7 fusion.4
  82.6 3.9 %collective-permute-start.10 = (bf16[256,1152]{1,0:T(8,128)(2,1)S(1)}, bf16[256,1152]{1,0:T(8,128)(2,1)S(1)}, u32[]{:S(2)}, u32[]{:S(2)}) collective-permute-start(bf16[256,1152]{1,0:T(8,128)(2,1)S(1)} %get-tuple-element.33), channel_id=1, source_target_pairs={{0,4},{4,8},{8,12},{1,5},{5,9},{9,13},{2,6},{6,10},{10,14},{3,7},{... | collective-permute-start | bytes 1769480 | tf_op jit(solution)/shard_map/ppermute | solution.py:264
  86.5 1.3 %collective-permute-start.11 = (bf16[256,1152]{1,0:T(8,128)(2,1)S(1)}, bf16[256,1152]{1,0:T(8,128)(2,1)S(1)}, u32[]{:S(2)}, u32[]{:S(2)}) collective-permute-start(bf16[256,1152]{1,0:T(8,128)(2,1)S(1)} %get-tuple-element.28), channel_id=1, source_target_pairs={{4,0},{8,4},{12,8},{5,1},{9,5},{13,9},{6,2},{10,6},{14,10},{7,3},{... | collective-permute-start | bytes 1769480 | tf_op jit(solution)/shard_map/ppermute | solution.py:265
  88.1 0.6 collective-permute-start.12
  88.7 1.6 %collective-permute-start.14 = (bf16[24,1152]{1,0:T(8,128)(2,1)S(1)}, bf16[24,1152]{1,0:T(8,128)(2,1)S(1)}, u32[]{:S(2)}, u32[]{:S(2)}) collective-permute-start(bf16[24,1152]{1,0:T(8,128)(2,1)S(1)} %get-tuple-element.60), channel_id=1, source_target_pairs={{0,2},{1,3},{2,0},{3,1},{4,6},{5,7},{6,4},{7,5},{8,10},{9,11},{10,... | collective-permute-start | bytes 165896 | tf_op jit(solution)/shard_map/ppermute | solution.py:231
  90.5 2.0 %collective-permute-start.15 = (bf16[24,1152]{1,0:T(8,128)(2,1)S(1)}, bf16[24,1152]{1,0:T(8,128)(2,1)S(1)}, u32[]{:S(2)}, u32[]{:S(2)}) collective-permute-start(bf16[24,1152]{1,0:T(8,128)(2,1)S(1)} %get-tuple-element.59), channel_id=1, source_target_pairs={{0,2},{1,3},{2,0},{3,1},{4,6},{5,7},{6,4},{7,5},{8,10},{9,11},{10,... | collective-permute-start | bytes 165896 | tf_op jit(solution)/shard_map/ppermute | solution.py:231
  93.7 9.0 %shard_map.255 = bf16[192,1152]{1,0:T(8,128)(2,1)} custom-call(bf16[8,192,72]{2,1,0:T(8,128)(2,1)} %get-tuple-element.29.refs_0_.refs_4_, bf16[8,72,896]{2,1,0:T(8,128)(2,1)} %get-tuple-element.39.refs_1_.refs_5_, bf16[8,896,72]{2,1,0:T(8,128)(2,1)} %bitcast.77, bf16[576,1152]{1,0:T(8,128)(2,1)} %copy.49.refs_3_.refs_7_, ...), custom_call_target="tpu_custom_call" | custom-call | tf_op jit(solution)/shard_map/pallas_call | solution.py:88
  102.8 1.2 %collective-permute-done.11 = bf16[256,1152]{1,0:T(8,128)(2,1)S(1)} collective-permute-done((bf16[256,1152]{1,0:T(8,128)(2,1)S(1)}, bf16[256,1152]{1,0:T(8,128)(2,1)S(1)}, u32[]{:S(2)}, u32[]{:S(2)}) %collective-permute-start.11) | collective-permute-done | bytes 589856 | tf_op jit(solution)/shard_map/ppermute | solution.py:265
  104.1 1.3 %convolution_convert_fusion.1 = bf16[96,1152]{1,0:T(8,128)(2,1)S(1)} fusion(bf16[192,1152]{1,0:T(8,128)(2,1)} %shard_map.255, s32[96]{0:T(128)S(1)} %eq.142), kind=kOutput, calls=%fused_computation.16 | convolution fusion | flops 42596352 | bytes 663936 | tf_op jit(solution)/shard_map/dot_general | solution.py:222
  105.4 0.7 collective-permute-start.16
  106.1 0.7 collective-permute-start.18
  106.7 1.4 %collective-permute-start.19 = (bf16[24,1152]{1,0:T(8,128)(2,1)S(1)}, bf16[24,1152]{1,0:T(8,128)(2,1)S(1)}, u32[]{:S(2)}, u32[]{:S(2)}) collective-permute-start(bf16[24,1152]{1,0:T(8,128)(2,1)S(1)} %get-tuple-element.55), channel_id=1, source_target_pairs={{0,2},{1,3},{2,0},{3,1},{4,6},{5,7},{6,4},{7,5},{8,10},{9,11},{10,... | collective-permute-start | bytes 165896 | tf_op jit(solution)/shard_map/ppermute | solution.py:231
  109.6 1.1 %collective-permute-done.18 = bf16[24,1152]{1,0:T(8,128)(2,1)S(1)} collective-permute-done((bf16[24,1152]{1,0:T(8,128)(2,1)S(1)}, bf16[24,1152]{1,0:T(8,128)(2,1)S(1)}, u32[]{:S(2)}, u32[]{:S(2)}) %collective-permute-start.18) | collective-permute-done | bytes 55328 | tf_op jit(solution)/shard_map/ppermute | solution.py:231
  110.8 1.2 %collective-permute-done.19 = bf16[24,1152]{1,0:T(8,128)(2,1)S(1)} collective-permute-done((bf16[24,1152]{1,0:T(8,128)(2,1)S(1)}, bf16[24,1152]{1,0:T(8,128)(2,1)S(1)}, u32[]{:S(2)}, u32[]{:S(2)}) %collective-permute-start.19) | collective-permute-done | bytes 55328 | tf_op jit(solution)/shard_map/ppermute | solution.py:231
  112.3 1.5 %maximum_bitcast_fusion = bf16[1,1,896,1152]{3,2,1,0:T(8,128)(2,1)} fusion(bf16[256,1152]{1,0:T(8,128)(2,1)S(1)} %fusion.11, bf16[192,1152]{1,0:T(8,128)(2,1)S(1)} %fusion.19, bf16[192,1152]{1,0:T(8,128)(2,1)S(1)} %fusion.7, bf16[256,1152]{1,0:T(8,128)(2,1)S(1)} %fusion.9), kind=kLoop, calls=%fused_computation.18 | loop fusion | flops 8257536 | bytes 4128768 | tf_op jit(solution)/shard_map/reshape | solution.py:305
  (122 shorter events, 8.5 us)
Async XLA Ops:
  0.0 7.2 %copy-start = (s32[4,4,4]{2,1,0:T(4,128)S(1)}, s32[4,4,4]{2,1,0:T(4,128)}, u32[]{:S(2)}) copy-start(s32[4,4,4]{2,1,0:T(4,128)} %param.30) | copy-start | bytes 772
  0.0 19.7 %collective-permute-start = (bf16[288,1728]{1,0:T(8,128)(2,1)}, bf16[288,1728]{1,0:T(8,128)(2,1)}, u32[]{:S(2)}, u32[]{:S(2)}) collective-permute-start(bf16[288,1728]{1,0:T(8,128)(2,1)} %param.28), channel_id=1, source_target_pairs={{1,0},{0,1},{3,2},{2,3},{5,4},{4,5},{7,6},{6,7},{9,8},{8,9},{11,10... | collective-permute-start | bytes 2985992 | tf_op jit(solution)/shard_map/ppermute | solution.py:154
  0.5 26.3 %collective-permute-start.1 = (bf16[288,1728]{1,0:T(8,128)(2,1)}, bf16[288,1728]{1,0:T(8,128)(2,1)}, u32[]{:S(2)}, u32[]{:S(2)}) collective-permute-start(bf16[288,1728]{1,0:T(8,128)(2,1)} %param.28), channel_id=1, source_target_pairs={{2,0},{3,1},{0,2},{1,3},{6,4},{7,5},{4,6},{5,7},{10,8},{11,9},{8,1... | collective-permute-start | bytes 2985992 | tf_op jit(solution)/shard_map/ppermute | solution.py:154
  7.6 1.1 copy-start.6
  7.6 1.7 %copy-start.14 = (s32[2]{0:T(128)S(1)}, s32[2]{0:T(128)}, u32[]{:S(2)}) copy-start(s32[2]{0:T(128)} %param.31) | copy-start | bytes 28
  8.0 2.6 %copy-start.16 = (s32[4]{0:T(128)S(1)}, s32[4]{0:T(128)}, u32[]{:S(2)}) copy-start(s32[4]{0:T(128)} %constant.114.clone) | copy-start | bytes 52
  8.0 3.3 %copy-start.10 = (s32[4,64]{1,0:T(4,128)S(1)}, s32[4,64]{1,0:T(4,128)}, u32[]{:S(2)}) copy-start(s32[4,64]{1,0:T(4,128)} %constant.115.clone) | copy-start | bytes 3076
  8.1 3.3 %copy-start.11 = (s32[4,64]{1,0:T(4,128)S(1)}, s32[4,64]{1,0:T(4,128)}, u32[]{:S(2)}) copy-start(s32[4,64]{1,0:T(4,128)} %constant.116.clone) | copy-start | bytes 3076
  8.1 3.3 %copy-start.8 = (s32[4,24]{1,0:T(4,128)S(1)}, s32[4,24]{1,0:T(4,128)}, u32[]{:S(2)}) copy-start(s32[4,24]{1,0:T(4,128)} %constant.120.clone) | copy-start | bytes 1156
  8.1 3.3 %copy-start.9 = (s32[4,24]{1,0:T(4,128)S(1)}, s32[4,24]{1,0:T(4,128)}, u32[]{:S(2)}) copy-start(s32[4,24]{1,0:T(4,128)} %constant.121.clone) | copy-start | bytes 1156
  8.1 3.4 %copy-start.13 = (pred[64,1]{0,1:T(4,128)(4,1)S(1)}, pred[64,1]{0,1:T(4,128)(4,1)}, u32[]{:S(2)}) copy-start(pred[64,1]{0,1:T(4,128)(4,1)} %constant.118.clone) | copy-start | bytes 196
  8.1 5.8 %copy-start.12 = (s32[4,64]{1,0:T(4,128)S(1)}, s32[4,64]{1,0:T(4,128)}, u32[]{:S(2)}) copy-start(s32[4,64]{1,0:T(4,128)} %constant.126) | copy-start | bytes 3076
  16.3 1.6 %copy-start.5 = (bf16[288,1728]{1,0:T(8,128)(2,1)S(1)}, bf16[288,1728]{1,0:T(8,128)(2,1)}, u32[]{:S(2)}) copy-start(bf16[288,1728]{1,0:T(8,128)(2,1)} %param.28) | copy-start | bytes 2985988
  16.3 3.1 %copy-start.17 = (pred[64]{0:T(512)(128)(4,1)S(1)}, pred[64]{0:T(512)(128)(4,1)}, u32[]{:S(2)}) copy-start(pred[64]{0:T(512)(128)(4,1)} %constant.125) | copy-start | bytes 196
  16.3 3.3 %copy-start.15 = (s32[4]{0:T(128)S(1)}, s32[4]{0:T(128)}, u32[]{:S(2)}) copy-start(s32[4]{0:T(128)} %param.32) | copy-start | bytes 52
  17.9 4.0 %copy-start.2 = (bf16[896,2,576]{0,2,1:T(8,128)(2,1)S(1)}, bf16[896,2,576]{0,2,1:T(8,128)(2,1)}, u32[]{:S(2)}) copy-start(bf16[896,2,576]{0,2,1:T(8,128)(2,1)} %add_convert_fusion.1) | copy-start | bytes 6193156
  26.7 3.6 %collective-permute-start.2 = (bf16[288,1728]{1,0:T(8,128)(2,1)}, bf16[288,1728]{1,0:T(8,128)(2,1)S(1)}, u32[]{:S(2)}, u32[]{:S(2)}) collective-permute-start(bf16[288,1728]{1,0:T(8,128)(2,1)} %collective-permute-done.1), channel_id=1, source_target_pairs={{1,0},{0,1},{3,2},{2,3},{5,4},{4,5},{7,6},{6,7},{9,8},{8,9},{11,10... | collective-permute-start | bytes 2985992 | tf_op jit(solution)/shard_map/ppermute | solution.py:154
  30.4 15.6 %collective-permute-start.3 = (bf16[576,288]{0,1:T(8,128)(2,1)}, bf16[576,288]{0,1:T(8,128)(2,1)}, u32[]{:S(2)}, u32[]{:S(2)}) collective-permute-start(bf16[576,288]{0,1:T(8,128)(2,1)} %param.29), channel_id=1, source_target_pairs={{1,0},{0,1},{3,2},{2,3},{5,4},{4,5},{7,6},{6,7},{9,8},{8,9},{11,10... | collective-permute-start | bytes 995336 | tf_op jit(solution)/shard_map/ppermute | solution.py:104
  30.9 15.0 %collective-permute-start.4 = (bf16[576,288]{0,1:T(8,128)(2,1)}, bf16[576,288]{0,1:T(8,128)(2,1)}, u32[]{:S(2)}, u32[]{:S(2)}) collective-permute-start(bf16[576,288]{0,1:T(8,128)(2,1)} %param.29), channel_id=1, source_target_pairs={{2,0},{3,1},{0,2},{1,3},{6,4},{7,5},{4,6},{5,7},{10,8},{11,9},{8,1... | collective-permute-start | bytes 995336 | tf_op jit(solution)/shard_map/ppermute | solution.py:104
  45.9 2.2 %collective-permute-start.5 = (bf16[576,288]{0,1:T(8,128)(2,1)}, bf16[576,288]{0,1:T(8,128)(2,1)S(1)}, u32[]{:S(2)}, u32[]{:S(2)}) collective-permute-start(bf16[576,288]{0,1:T(8,128)(2,1)} %collective-permute-done.4), channel_id=1, source_target_pairs={{1,0},{0,1},{3,2},{2,3},{5,4},{4,5},{7,6},{6,7},{9,8},{8,9},{11,10... | collective-permute-start | bytes 995336 | tf_op jit(solution)/shard_map/ppermute | solution.py:104
  68.8 12.7 %collective-permute-start.6 = (bf16[64,1152]{1,0:T(8,128)(2,1)S(1)}, bf16[64,1152]{1,0:T(8,128)(2,1)S(1)}, u32[]{:S(2)}, u32[]{:S(2)}) collective-permute-start(bf16[64,1152]{1,0:T(8,128)(2,1)S(1)} %get-tuple-element.50), channel_id=1, source_target_pairs={{0,3},{1,0},{2,1},{3,2},{4,7},{5,4},{6,5},{7,6},{8,11},{9,8},{10,9... | collective-permute-start | bytes 442376 | tf_op jit(solution)/shard_map/ppermute | solution.py:231
  69.2 12.3 %collective-permute-start.7 = (bf16[64,1152]{1,0:T(8,128)(2,1)S(1)}, bf16[64,1152]{1,0:T(8,128)(2,1)S(1)}, u32[]{:S(2)}, u32[]{:S(2)}) collective-permute-start(bf16[64,1152]{1,0:T(8,128)(2,1)S(1)} %get-tuple-element.53), channel_id=1, source_target_pairs={{0,1},{1,2},{2,3},{3,0},{4,5},{5,6},{6,7},{7,4},{8,9},{9,10},{10,1... | collective-permute-start | bytes 442376 | tf_op jit(solution)/shard_map/ppermute | solution.py:231
  69.4 12.1 %collective-permute-start.8 = (bf16[64,1152]{1,0:T(8,128)(2,1)S(1)}, bf16[64,1152]{1,0:T(8,128)(2,1)S(1)}, u32[]{:S(2)}, u32[]{:S(2)}) collective-permute-start(bf16[64,1152]{1,0:T(8,128)(2,1)S(1)} %get-tuple-element.52), channel_id=1, source_target_pairs={{0,2},{1,3},{2,0},{3,1},{4,6},{5,7},{6,4},{7,5},{8,10},{9,11},{10,... | collective-permute-start | bytes 442376 | tf_op jit(solution)/shard_map/ppermute | solution.py:231
  71.0 10.7 %collective-permute-start.9 = (bf16[64,1152]{1,0:T(8,128)(2,1)S(1)}, bf16[64,1152]{1,0:T(8,128)(2,1)S(1)}, u32[]{:S(2)}, u32[]{:S(2)}) collective-permute-start(bf16[64,1152]{1,0:T(8,128)(2,1)S(1)} %get-tuple-element.51), channel_id=1, source_target_pairs={{0,2},{1,3},{2,0},{3,1},{4,6},{5,7},{6,4},{7,5},{8,10},{9,11},{10,... | collective-permute-start | bytes 442376 | tf_op jit(solution)/shard_map/ppermute | solution.py:231
  72.4 9.3 %copy-start.1 = (bf16[512,1152]{1,0:T(8,128)(2,1)S(1)}, bf16[512,1152]{1,0:T(8,128)(2,1)}, u32[]{:S(2)}) copy-start(bf16[512,1152]{1,0:T(8,128)(2,1)} %shard_map.253) | copy-start | bytes 3538948
  82.5 5.3 %copy-start.3 = (bf16[192,1152]{1,0:T(8,128)(2,1)S(1)}, bf16[192,1152]{1,0:T(8,128)(2,1)}, u32[]{:S(2)}) copy-start(bf16[192,1152]{1,0:T(8,128)(2,1)} %shard_map.254) | copy-start | bytes 1327108
  82.5 10.0 %copy-start.7 = (s32[4,24]{1,0:T(4,128)S(1)}, s32[4,24]{1,0:T(4,128)}, u32[]{:S(2)}) copy-start(s32[4,24]{1,0:T(4,128)} %constant.127) | copy-start | bytes 1156
  82.6 20.2 %collective-permute-start.10 = (bf16[256,1152]{1,0:T(8,128)(2,1)S(1)}, bf16[256,1152]{1,0:T(8,128)(2,1)S(1)}, u32[]{:S(2)}, u32[]{:S(2)}) collective-permute-start(bf16[256,1152]{1,0:T(8,128)(2,1)S(1)} %get-tuple-element.33), channel_id=1, source_target_pairs={{0,4},{4,8},{8,12},{1,5},{5,9},{9,13},{2,6},{6,10},{10,14},{3,7},{... | collective-permute-start | bytes 1769480 | tf_op jit(solution)/shard_map/ppermute | solution.py:264
  86.5 17.6 %collective-permute-start.11 = (bf16[256,1152]{1,0:T(8,128)(2,1)S(1)}, bf16[256,1152]{1,0:T(8,128)(2,1)S(1)}, u32[]{:S(2)}, u32[]{:S(2)}) collective-permute-start(bf16[256,1152]{1,0:T(8,128)(2,1)S(1)} %get-tuple-element.28), channel_id=1, source_target_pairs={{4,0},{8,4},{12,8},{5,1},{9,5},{13,9},{6,2},{10,6},{14,10},{7,3},{... | collective-permute-start | bytes 1769480 | tf_op jit(solution)/shard_map/ppermute | solution.py:265
  88.1 2.4 %collective-permute-start.12 = (bf16[24,1152]{1,0:T(8,128)(2,1)S(1)}, bf16[24,1152]{1,0:T(8,128)(2,1)S(1)}, u32[]{:S(2)}, u32[]{:S(2)}) collective-permute-start(bf16[24,1152]{1,0:T(8,128)(2,1)S(1)} %get-tuple-element.58), channel_id=1, source_target_pairs={{0,3},{1,0},{2,1},{3,2},{4,7},{5,4},{6,5},{7,6},{8,11},{9,8},{10,9... | collective-permute-start | bytes 165896 | tf_op jit(solution)/shard_map/ppermute | solution.py:231
  88.7 14.0 %collective-permute-start.13 = (bf16[24,1152]{1,0:T(8,128)(2,1)S(1)}, bf16[24,1152]{1,0:T(8,128)(2,1)S(1)}, u32[]{:S(2)}, u32[]{:S(2)}) collective-permute-start(bf16[24,1152]{1,0:T(8,128)(2,1)S(1)} %get-tuple-element.61), channel_id=1, source_target_pairs={{0,1},{1,2},{2,3},{3,0},{4,5},{5,6},{6,7},{7,4},{8,9},{9,10},{10,1... | collective-permute-start | bytes 165896 | tf_op jit(solution)/shard_map/ppermute | solution.py:231
  88.7 14.0 %collective-permute-start.14 = (bf16[24,1152]{1,0:T(8,128)(2,1)S(1)}, bf16[24,1152]{1,0:T(8,128)(2,1)S(1)}, u32[]{:S(2)}, u32[]{:S(2)}) collective-permute-start(bf16[24,1152]{1,0:T(8,128)(2,1)S(1)} %get-tuple-element.60), channel_id=1, source_target_pairs={{0,2},{1,3},{2,0},{3,1},{4,6},{5,7},{6,4},{7,5},{8,10},{9,11},{10,... | collective-permute-start | bytes 165896 | tf_op jit(solution)/shard_map/ppermute | solution.py:231
  90.5 12.2 %collective-permute-start.15 = (bf16[24,1152]{1,0:T(8,128)(2,1)S(1)}, bf16[24,1152]{1,0:T(8,128)(2,1)S(1)}, u32[]{:S(2)}, u32[]{:S(2)}) collective-permute-start(bf16[24,1152]{1,0:T(8,128)(2,1)S(1)} %get-tuple-element.59), channel_id=1, source_target_pairs={{0,2},{1,3},{2,0},{3,1},{4,6},{5,7},{6,4},{7,5},{8,10},{9,11},{10,... | collective-permute-start | bytes 165896 | tf_op jit(solution)/shard_map/ppermute | solution.py:231
  105.4 3.8 %collective-permute-start.16 = (bf16[24,1152]{1,0:T(8,128)(2,1)S(1)}, bf16[24,1152]{1,0:T(8,128)(2,1)S(1)}, u32[]{:S(2)}, u32[]{:S(2)}) collective-permute-start(bf16[24,1152]{1,0:T(8,128)(2,1)S(1)} %get-tuple-element.54), channel_id=1, source_target_pairs={{0,3},{1,0},{2,1},{3,2},{4,7},{5,4},{6,5},{7,6},{8,11},{9,8},{10,9... | collective-permute-start | bytes 165896 | tf_op jit(solution)/shard_map/ppermute | solution.py:231
  106.1 3.6 %collective-permute-start.17 = (bf16[24,1152]{1,0:T(8,128)(2,1)S(1)}, bf16[24,1152]{1,0:T(8,128)(2,1)S(1)}, u32[]{:S(2)}, u32[]{:S(2)}) collective-permute-start(bf16[24,1152]{1,0:T(8,128)(2,1)S(1)} %get-tuple-element.57), channel_id=1, source_target_pairs={{0,1},{1,2},{2,3},{3,0},{4,5},{5,6},{6,7},{7,4},{8,9},{9,10},{10,1... | collective-permute-start | bytes 165896 | tf_op jit(solution)/shard_map/ppermute | solution.py:231
  106.1 4.7 %collective-permute-start.18 = (bf16[24,1152]{1,0:T(8,128)(2,1)S(1)}, bf16[24,1152]{1,0:T(8,128)(2,1)S(1)}, u32[]{:S(2)}, u32[]{:S(2)}) collective-permute-start(bf16[24,1152]{1,0:T(8,128)(2,1)S(1)} %get-tuple-element.56), channel_id=1, source_target_pairs={{0,2},{1,3},{2,0},{3,1},{4,6},{5,7},{6,4},{7,5},{8,10},{9,11},{10,... | collective-permute-start | bytes 165896 | tf_op jit(solution)/shard_map/ppermute | solution.py:231
  106.7 5.2 %collective-permute-start.19 = (bf16[24,1152]{1,0:T(8,128)(2,1)S(1)}, bf16[24,1152]{1,0:T(8,128)(2,1)S(1)}, u32[]{:S(2)}, u32[]{:S(2)}) collective-permute-start(bf16[24,1152]{1,0:T(8,128)(2,1)S(1)} %get-tuple-element.55), channel_id=1, source_target_pairs={{0,2},{1,3},{2,0},{3,1},{4,6},{5,7},{6,4},{7,5},{8,10},{9,11},{10,... | collective-permute-start | bytes 165896 | tf_op jit(solution)/shard_map/ppermute | solution.py:231
  108.5 3.5 %copy-start.4 = (bf16[192,1152]{1,0:T(8,128)(2,1)S(1)}, bf16[192,1152]{1,0:T(8,128)(2,1)}, u32[]{:S(2)}) copy-start(bf16[192,1152]{1,0:T(8,128)(2,1)} %shard_map.255) | copy-start | bytes 1327108

commit v15 on v14

--- a/solution.py
+++ b/solution.py
@@ -153,17 +153,13 @@
         def fetch(x, src_of):
             return lax.ppermute(x, "face", [(src_of(i), i) for i in range(n)])
 
-        moved_chips = moved.reshape(tokens, 2, 2 * rows).transpose(1, 0, 2)
-
         def chip_weight(same_core, other_core):
-            stack = jnp.zeros((2,) + w_qkv.shape, w_qkv.dtype)
-            stack = lax.dynamic_update_index_in_dim(stack, same_core, core, 0)
-            stack = lax.dynamic_update_index_in_dim(stack, other_core, 1 - core, 0)
-            return stack.reshape(2 * rows, w_qkv.shape[1])
+            tripled = jnp.concatenate([same_core, other_core, same_core], axis=0)
+            return lax.dynamic_slice_in_dim(tripled, core * rows, 2 * rows, axis=0)
 
         def chip_part(chip, weight):
             return jnp.dot(
-                lax.dynamic_index_in_dim(moved_chips, chip, 0, keepdims=False),
+                lax.dynamic_slice_in_dim(moved, chip * 2 * rows, 2 * rows, axis=1),
                 weight,
                 preferred_element_type=jnp.float32,
             )

time: 115 us -> 115 us (level)
  local copies, waits for them, and re-layouts: 28 us -> 16.5 us
  waiting for transfers between devices: 4.79 us -> 10.5 us
  matrix products: 12.1 us -> 17.8 us
    ppermute x6, waiting for transfers between devices: 0.32 us -> 7.14 us  [fetch(): return lax.ppermute(x, 'face', [(src_of(i), i) for i in range(n)])]
    dot_general x2, matrix products: 7.34 us -> 13 us  [chip_part(): jnp.dot(lax.dynamic_slice_in_dim(moved, chip * 2 * rows, 2 * rows, axis=1...]
    dynamic_update_slice x4 -> x0, local copies, waits for them, and re-layouts: 4.68 us -> none  [the longest x2 2.34 us: chip_weight(): stack = lax.dynamic_update_index_in_dim(stack, same_core, core, 0)]
    unnamed x39 -> x46, local copies, waits for them, and re-layouts: 6.7 us -> 4.02 us
    another operation x2 -> x0, local copies, waits for them, and re-layouts: 1.57 us -> none
    reduce_sum x1, other arithmetic: 0.36 us -> 1.92 us  [modulate(): center = jnp.mean(values, axis=-1, keepdims=True)]
    convert_element_type x1, other arithmetic: 2.12 us -> 0.83 us  [modulate(): return (normed * (1.0 + modulation[1]) + modulation[0]).astype(jnp.bfloat16)]
    slice x1, local copies, waits for them, and re-layouts: 1.34 us -> 0.09 us  [per_device(): rim_in = jnp.concatenate([block_in[:rim], block_in[tokens - rim:]], axis=0)]
  transfers between devices with their start and end apart: 20 -> 20, of which waited for: 7 -> 5; matrix products, arithmetic and copies ran while one was open for 40% -> 35% of each run, Pallas kernels for 16% -> 16%
where the time goes in v15:
time: 115 us; the launch traced here: 114 us
  Pallas kernels  35 us (30%)
  starting transfers between devices  20 us (17%)
  matrix products  17.8 us (15%)
  local copies, waits for them, and re-layouts  16.5 us (14%)
  other arithmetic  13.6 us (12%)
  waiting for transfers between devices  10.5 us (9%)
    pallas_call x3, Pallas kernels, attend_project(): pl.pallas_call(attention_kernel, grid=(1, heads // hb), in_specs=in_specs...  35 us
    dot_general x2, matrix products, chip_part(): jnp.dot(lax.dynamic_slice_in_dim(moved, chip * 2 * rows, 2 * rows, axis=1...  13 us
    ppermute x12, starting transfers between devices, strips_in(): lax.ppermute(sent, 'face', [(i, (i + shift) % n) for i in range(n)])  9.77 us
    ppermute x6, waiting for transfers between devices, fetch(): return lax.ppermute(x, 'face', [(src_of(i), i) for i in range(n)])  7.14 us
    ppermute x6, starting transfers between devices, fetch(): return lax.ppermute(x, 'face', [(src_of(i), i) for i in range(n)])  5.29 us
    unnamed x46, local copies, waits for them, and re-layouts  4.02 us
    ppermute x1, starting transfers between devices, per_device(): lower = lax.ppermute(high, 'tm', [(i, i + 1) for i in range(count - 1)])  3.66 us
    ppermute x12, waiting for transfers between devices, strips_in(): lax.ppermute(sent, 'face', [(i, (i + shift) % n) for i in range(n)])  3.39 us
  transfers between devices with their start and end apart: 20, of which 5 were waited for; matrix products, arithmetic and copies ran while one was open for 35% of the time, Pallas kernels for 16%

profile of v15, /device:TPU:0, one launch (start us, length us, event | category | flops | bytes accessed | tf_op | source)
XLA Modules:
  0.0 114.0 jit_solution(3402064345282417062)
XLA Ops:
  0.0 0.5 collective-permute-start
  0.5 2.6 %collective-permute-start.1 = (bf16[288,1728]{1,0:T(8,128)(2,1)}, bf16[288,1728]{1,0:T(8,128)(2,1)}, u32[]{:S(2)}, u32[]{:S(2)}) collective-permute-start(bf16[288,1728]{1,0:T(8,128)(2,1)} %param.28), channel_id=1, source_target_pairs={{2,0},{3,1},{0,2},{1,3},{6,4},{7,5},{4,6},{5,7},{10,8},{11,9},{8,1... | collective-permute-start | bytes 2985992 | tf_op jit(solution)/shard_map/ppermute | solution.py:154
  3.0 1.9 %convert_reduce_fusion = f32[896]{0:T(1024)S(1)} fusion(bf16[1,1,896,1152]{3,2,1,0:T(8,128)(2,1)} %param.26), kind=kLoop, calls=%fused_computation.1 | loop fusion | flops 2063488 | bytes 2067968 | tf_op jit(solution)/shard_map/reduce_sum | solution.py:27
  5.6 0.7 fusion.3
  6.5 0.7 fusion.56
  7.3 2.6 %select_bitcast_fusion.1 = (f32[64]{0:T(128)S(1)}, f32[64]{0:T(128)S(1)}) fusion(pred[64,1]{0,1:T(4,128)(4,1)S(1)} %copy-done.14, f32[]{:T(128)} %bitcast.5, f32[]{:T(128)} %bitcast.4, f32[]{:T(128)} %bitcast.22, f32[]{:T(128)} %bitcast.21), kind=kLoop, calls=%fused_computation.105 | loop fusion | flops 128 | bytes 592 | tf_op jit(solution)/shard_map/mul | solution.py:246
  9.9 0.6 add_reduce_fusion
  10.5 0.8 fusion.6
  11.7 8.0 %fusion.19 = f32[896,1728]{0,1:T(8,128)} fusion(s32[]{:T(128)S(6)} %select_n.131, bf16[288,1728]{1,0:T(8,128)(2,1)S(1)} %copy-done.18, bf16[288,1728]{1,0:T(8,128)(2,1)} %collective-permute-done, bf16[896,1152]{1,0:T(8,128)(2,1)S(1)} %fusion.6, s32[]{:T(128)S(6)} %select_n.129), kind=kOutput, calls=%fused_computation.34 | convolution fusion | flops 1789599744 | bytes 9367560 | tf_op jit(solution)/shard_map/dot_general | solution.py:161
  19.7 7.1 %collective-permute-done.1 = bf16[288,1728]{1,0:T(8,128)(2,1)} collective-permute-done((bf16[288,1728]{1,0:T(8,128)(2,1)}, bf16[288,1728]{1,0:T(8,128)(2,1)}, u32[]{:S(2)}, u32[]{:S(2)}) %collective-permute-start.1) | collective-permute-done | bytes 995360 | tf_op jit(solution)/shard_map/ppermute | solution.py:154
  27.5 1.1 pad_maximum_fusion.refs_8_
  28.6 1.0 slice_bitcast_fusion.3
  29.7 0.4 collective-permute-start.3
  30.2 1.8 %collective-permute-start.4 = (bf16[576,288]{0,1:T(8,128)(2,1)}, bf16[576,288]{0,1:T(8,128)(2,1)}, u32[]{:S(2)}, u32[]{:S(2)}) collective-permute-start(bf16[576,288]{0,1:T(8,128)(2,1)} %param.29), channel_id=1, source_target_pairs={{2,0},{3,1},{0,2},{1,3},{6,4},{7,5},{4,6},{5,7},{10,8},{11,9},{8,1... | collective-permute-start | bytes 995336 | tf_op jit(solution)/shard_map/ppermute | solution.py:104
  31.9 5.0 %fusion.15 = f32[896,1728]{0,1:T(8,128)S(1)} fusion(s32[]{:T(128)S(6)} %select_n.131, bf16[288,1728]{1,0:T(8,128)(2,1)} %collective-permute-done.1, bf16[288,1728]{1,0:T(8,128)(2,1)} %collective-permute-done.2, bf16[896,1152]{1,0:T(8,128)(2,1)S(1)} %copy-done.4, s32[]{:T(128)S(6)} %select_n.132), kind=kOutput, calls=%fused_computation.31 | convolution fusion | flops 1789599744 | bytes 9330696 | tf_op jit(solution)/shard_map/dot_general | solution.py:161
  37.0 0.8 add_convert_fusion
  37.8 1.6 %fusion.49 = (bf16[896,1,8,72]{0,3,2,1:T(8,128)(2,1)S(1)}, bf16[896,1,8,72]{0,3,2,1:T(8,128)(2,1)}, bf16[8,72,896]{2,1,0:T(8,128)(2,1)}) fusion(bf16[896,3,8,72]{0,3,2,1:T(8,128)(2,1)S(1)} %bitcast.69), kind=kLoop, calls=%fused_computation.109 | loop fusion | bytes 6193152 | tf_op jit(solution)/shard_map/slice | solution.py:192
  39.4 1.9 %copy.53 = bf16[896,1,8,72]{3,0,2,1:T(8,128)(2,1)S(1)} copy(bf16[896,1,8,72]{0,3,2,1:T(8,128)(2,1)} %get-tuple-element.38) | data formatting | bytes 2064384
  41.3 0.9 fusion.51
  42.2 1.7 %copy.54 = bf16[896,1,8,72]{3,0,2,1:T(8,128)(2,1)} copy(bf16[896,1,8,72]{0,3,2,1:T(8,128)(2,1)S(1)} %get-tuple-element.37) | data formatting | bytes 2064384
  43.8 2.2 %pad_maximum_fusion.1.refs_0_.refs_4_ = bf16[8,512,72]{2,1,0:T(8,128)(2,1)} fusion(bf16[8,256,72]{2,1,0:T(8,128)(2,1)} %get-tuple-element.47, bf16[8,256,72]{2,1,0:T(8,128)(2,1)S(1)} %get-tuple-element.46), kind=kLoop, calls=%fused_computation.50 | loop fusion | flops 1179648 | bytes 1179648 | tf_op jit(solution)/shard_map/concatenate | solution.py:249
  46.2 1.0 bitcast_dynamic-update-slice_fusion.3
  47.3 1.0 bitcast_dynamic-update-slice_fusion.2
  48.3 1.0 bitcast_dynamic-update-slice_fusion.1
  49.4 1.8 %copy.47.refs_3_.refs_7_ = bf16[576,1152]{1,0:T(8,128)(2,1)} copy(bf16[576,1152]{0,1:T(8,128)(2,1)S(1)} %bitcast.74) | data formatting | bytes 2654208 | tf_op jit(solution)/shard_map/reshape | solution.py:187
  51.3 16.9 %shard_map.253 = bf16[512,1152]{1,0:T(8,128)(2,1)} custom-call(bf16[8,512,72]{2,1,0:T(8,128)(2,1)} %pad_maximum_fusion.1.refs_0_.refs_4_, bf16[8,72,896]{2,1,0:T(8,128)(2,1)} %get-tuple-element.39.refs_1_.refs_5_, bf16[8,896,72]{2,1,0:T(8,128)(2,1)} %bitcast.63, bf16[576,1152]{1,0:T(8,128)(2,1)} %copy.47.refs_3_.refs_7_, ...), custom_call_target="tpu_custom_call" | custom-call | tf_op jit(solution)/shard_map/pallas_call | solution.py:88
  68.1 1.8 %convolution_convert_fusion = bf16[256,1152]{1,0:T(8,128)(2,1)S(1)} fusion(bf16[512,1152]{1,0:T(8,128)(2,1)} %shard_map.253, s32[256]{0:T(256)S(1)} %eq.138), kind=kOutput, calls=%fused_computation.25 | convolution fusion | flops 302415872 | bytes 1770496 | tf_op jit(solution)/shard_map/dot_general | solution.py:218
  70.0 0.7 collective-permute-start.9
  70.7 1.4 %collective-permute-start.8 = (bf16[64,1152]{1,0:T(8,128)(2,1)S(1)}, bf16[64,1152]{1,0:T(8,128)(2,1)S(1)}, u32[]{:S(2)}, u32[]{:S(2)}) collective-permute-start(bf16[64,1152]{1,0:T(8,128)(2,1)S(1)} %get-tuple-element.52), channel_id=1, source_target_pairs={{0,2},{1,3},{2,0},{3,1},{4,6},{5,7},{6,4},{7,5},{8,10},{9,11},{10,... | collective-permute-start | bytes 442376 | tf_op jit(solution)/shard_map/ppermute | solution.py:227
  72.1 1.7 %collective-permute-start.6 = (bf16[64,1152]{1,0:T(8,128)(2,1)S(1)}, bf16[64,1152]{1,0:T(8,128)(2,1)S(1)}, u32[]{:S(2)}, u32[]{:S(2)}) collective-permute-start(bf16[64,1152]{1,0:T(8,128)(2,1)S(1)} %get-tuple-element.50), channel_id=1, source_target_pairs={{0,3},{1,0},{2,1},{3,2},{4,7},{5,4},{6,5},{7,6},{8,11},{9,8},{10,9... | collective-permute-start | bytes 442376 | tf_op jit(solution)/shard_map/ppermute | solution.py:227
  73.9 1.0 fusion.50
  74.8 9.1 %shard_map.254 = bf16[192,1152]{1,0:T(8,128)(2,1)} custom-call(bf16[8,192,72]{2,1,0:T(8,128)(2,1)} %get-tuple-element.23.refs_0_.refs_4_, bf16[8,72,896]{2,1,0:T(8,128)(2,1)} %get-tuple-element.39.refs_1_.refs_5_, bf16[8,896,72]{2,1,0:T(8,128)(2,1)} %bitcast.65, bf16[576,1152]{1,0:T(8,128)(2,1)} %copy.47.refs_3_.refs_7_, ...), custom_call_target="tpu_custom_call" | custom-call | tf_op jit(solution)/shard_map/pallas_call | solution.py:88
  84.0 0.7 fusion.9
  84.9 3.7 %collective-permute-start.10 = (bf16[256,1152]{1,0:T(8,128)(2,1)S(1)}, bf16[256,1152]{1,0:T(8,128)(2,1)S(1)}, u32[]{:S(2)}, u32[]{:S(2)}) collective-permute-start(bf16[256,1152]{1,0:T(8,128)(2,1)S(1)} %get-tuple-element.33), channel_id=1, source_target_pairs={{0,4},{4,8},{8,12},{1,5},{5,9},{9,13},{2,6},{6,10},{10,14},{3,7},{... | collective-permute-start | bytes 1769480 | tf_op jit(solution)/shard_map/ppermute | solution.py:260
  88.6 1.3 %collective-permute-start.11 = (bf16[256,1152]{1,0:T(8,128)(2,1)S(1)}, bf16[256,1152]{1,0:T(8,128)(2,1)S(1)}, u32[]{:S(2)}, u32[]{:S(2)}) collective-permute-start(bf16[256,1152]{1,0:T(8,128)(2,1)S(1)} %get-tuple-element.28), channel_id=1, source_target_pairs={{4,0},{8,4},{12,8},{5,1},{9,5},{13,9},{6,2},{10,6},{14,10},{7,3},{... | collective-permute-start | bytes 1769480 | tf_op jit(solution)/shard_map/ppermute | solution.py:261
  90.2 1.0 collective-permute-start.15
  91.2 1.1 collective-permute-start.14
  92.3 2.1 %collective-permute-done.15 = bf16[24,1152]{1,0:T(8,128)(2,1)S(1)} collective-permute-done((bf16[24,1152]{1,0:T(8,128)(2,1)S(1)}, bf16[24,1152]{1,0:T(8,128)(2,1)S(1)}, u32[]{:S(2)}, u32[]{:S(2)}) %collective-permute-start.15) | collective-permute-done | bytes 55328 | tf_op jit(solution)/shard_map/ppermute | solution.py:227
  95.7 9.0 %shard_map.255 = bf16[192,1152]{1,0:T(8,128)(2,1)} custom-call(bf16[8,192,72]{2,1,0:T(8,128)(2,1)} %get-tuple-element.29.refs_0_.refs_4_, bf16[8,72,896]{2,1,0:T(8,128)(2,1)} %get-tuple-element.39.refs_1_.refs_5_, bf16[8,896,72]{2,1,0:T(8,128)(2,1)} %bitcast.67, bf16[576,1152]{1,0:T(8,128)(2,1)} %copy.47.refs_3_.refs_7_, ...), custom_call_target="tpu_custom_call" | custom-call | tf_op jit(solution)/shard_map/pallas_call | solution.py:88
  104.8 1.3 %convolution_convert_fusion.1 = bf16[96,1152]{1,0:T(8,128)(2,1)S(1)} fusion(bf16[192,1152]{1,0:T(8,128)(2,1)} %shard_map.255, s32[96]{0:T(128)S(1)} %eq.142), kind=kOutput, calls=%fused_computation.27 | convolution fusion | flops 42596352 | bytes 663936 | tf_op jit(solution)/shard_map/dot_general | solution.py:218
  106.1 1.1 collective-permute-start.19
  107.2 1.0 collective-permute-start.18
  108.2 1.7 %collective-permute-start.16 = (bf16[24,1152]{1,0:T(8,128)(2,1)S(1)}, bf16[24,1152]{1,0:T(8,128)(2,1)S(1)}, u32[]{:S(2)}, u32[]{:S(2)}) collective-permute-start(bf16[24,1152]{1,0:T(8,128)(2,1)S(1)} %get-tuple-element.54), channel_id=1, source_target_pairs={{0,3},{1,0},{2,1},{3,2},{4,7},{5,4},{6,5},{7,6},{8,11},{9,8},{10,9... | collective-permute-start | bytes 165896 | tf_op jit(solution)/shard_map/ppermute | solution.py:227
  110.3 0.3 fusion.22
  110.6 0.3 fusion.12
  111.0 1.0 collective-permute-done.18
  112.2 0.3 fusion.28
  112.6 1.5 %maximum_bitcast_fusion = bf16[1,1,896,1152]{3,2,1,0:T(8,128)(2,1)} fusion(bf16[256,1152]{1,0:T(8,128)(2,1)S(1)} %fusion.24, bf16[192,1152]{1,0:T(8,128)(2,1)S(1)} %fusion.28, bf16[192,1152]{1,0:T(8,128)(2,1)S(1)} %fusion.12, bf16[256,1152]{1,0:T(8,128)(2,1)S(1)} %fusion.22), kind=kLoop, calls=%fused_computation.35 | loop fusion | flops 8257536 | bytes 4128768 | tf_op jit(solution)/shard_map/reshape | solution.py:301
  (122 shorter events, 4.7 us)
Async XLA Ops:
  0.0 5.1 %copy-start = (s32[4,4,4]{2,1,0:T(4,128)S(1)}, s32[4,4,4]{2,1,0:T(4,128)}, u32[]{:S(2)}) copy-start(s32[4,4,4]{2,1,0:T(4,128)} %param.30) | copy-start | bytes 772
  0.0 4.9 %copy-start.1 = (bf16[1,1,896,1152]{3,2,1,0:T(8,128)(2,1)S(1)}, bf16[1,1,896,1152]{3,2,1,0:T(8,128)(2,1)}, u32[]{:S(2)}) copy-start(bf16[1,1,896,1152]{3,2,1,0:T(8,128)(2,1)} %param.26) | copy-start | bytes 6193156
  0.0 11.4 %collective-permute-start = (bf16[288,1728]{1,0:T(8,128)(2,1)}, bf16[288,1728]{1,0:T(8,128)(2,1)}, u32[]{:S(2)}, u32[]{:S(2)}) collective-permute-start(bf16[288,1728]{1,0:T(8,128)(2,1)} %param.28), channel_id=1, source_target_pairs={{1,0},{0,1},{3,2},{2,3},{5,4},{4,5},{7,6},{6,7},{9,8},{8,9},{11,10... | collective-permute-start | bytes 2985992 | tf_op jit(solution)/shard_map/ppermute | solution.py:154
  0.5 26.3 %collective-permute-start.1 = (bf16[288,1728]{1,0:T(8,128)(2,1)}, bf16[288,1728]{1,0:T(8,128)(2,1)}, u32[]{:S(2)}, u32[]{:S(2)}) collective-permute-start(bf16[288,1728]{1,0:T(8,128)(2,1)} %param.28), channel_id=1, source_target_pairs={{2,0},{3,1},{0,2},{1,3},{6,4},{7,5},{4,6},{5,7},{10,8},{11,9},{8,1... | collective-permute-start | bytes 2985992 | tf_op jit(solution)/shard_map/ppermute | solution.py:154
  4.9 1.3 %copy-start.15 = (s32[2]{0:T(128)S(1)}, s32[2]{0:T(128)}, u32[]{:S(2)}) copy-start(s32[2]{0:T(128)} %param.31) | copy-start | bytes 28
  5.0 1.4 %copy-start.17 = (s32[4]{0:T(128)S(1)}, s32[4]{0:T(128)}, u32[]{:S(2)}) copy-start(s32[4]{0:T(128)} %constant.104.clone) | copy-start | bytes 52
  5.0 2.2 %copy-start.11 = (s32[4,64]{1,0:T(4,128)S(1)}, s32[4,64]{1,0:T(4,128)}, u32[]{:S(2)}) copy-start(s32[4,64]{1,0:T(4,128)} %constant.105.clone) | copy-start | bytes 3076
  5.0 2.2 %copy-start.12 = (s32[4,64]{1,0:T(4,128)S(1)}, s32[4,64]{1,0:T(4,128)}, u32[]{:S(2)}) copy-start(s32[4,64]{1,0:T(4,128)} %constant.106.clone) | copy-start | bytes 3076
  5.0 2.2 %copy-start.9 = (s32[4,24]{1,0:T(4,128)S(1)}, s32[4,24]{1,0:T(4,128)}, u32[]{:S(2)}) copy-start(s32[4,24]{1,0:T(4,128)} %constant.110.clone) | copy-start | bytes 1156
  5.0 2.2 %copy-start.10 = (s32[4,24]{1,0:T(4,128)S(1)}, s32[4,24]{1,0:T(4,128)}, u32[]{:S(2)}) copy-start(s32[4,24]{1,0:T(4,128)} %constant.111.clone) | copy-start | bytes 1156
  5.0 2.3 %copy-start.14 = (pred[64,1]{0,1:T(4,128)(4,1)S(1)}, pred[64,1]{0,1:T(4,128)(4,1)}, u32[]{:S(2)}) copy-start(pred[64,1]{0,1:T(4,128)(4,1)} %constant.108.clone) | copy-start | bytes 196
  5.0 4.8 %copy-start.7 = (f32[3,1152]{1,0:T(4,128)S(1)}, f32[3,1152]{1,0:T(4,128)}, u32[]{:S(2)}) copy-start(f32[3,1152]{1,0:T(4,128)} %param.27) | copy-start | bytes 41476
  10.5 1.2 %copy-start.18 = (bf16[288,1728]{1,0:T(8,128)(2,1)S(1)}, bf16[288,1728]{1,0:T(8,128)(2,1)}, u32[]{:S(2)}) copy-start(bf16[288,1728]{1,0:T(8,128)(2,1)} %param.28) | copy-start | bytes 2985988
  11.3 8.4 %copy-start.3 = (bf16[896,1152]{1,0:T(8,128)(2,1)}, bf16[896,1152]{1,0:T(8,128)(2,1)S(1)}, u32[]{:S(2)}) copy-start(bf16[896,1152]{1,0:T(8,128)(2,1)S(1)} %fusion.6) | copy-start | bytes 6193156
  11.3 15.4 %copy-start.13 = (s32[4,64]{1,0:T(4,128)S(1)}, s32[4,64]{1,0:T(4,128)}, u32[]{:S(2)}) copy-start(s32[4,64]{1,0:T(4,128)} %constant.116) | copy-start | bytes 3076
  11.3 15.7 %copy-start.19 = (pred[64]{0:T(512)(128)(4,1)S(1)}, pred[64]{0:T(512)(128)(4,1)}, u32[]{:S(2)}) copy-start(pred[64]{0:T(512)(128)(4,1)} %constant.115) | copy-start | bytes 196
  11.4 16.1 %copy-start.16 = (s32[4]{0:T(128)S(1)}, s32[4]{0:T(128)}, u32[]{:S(2)}) copy-start(s32[4]{0:T(128)} %param.32) | copy-start | bytes 52
  26.7 3.0 %collective-permute-start.2 = (bf16[288,1728]{1,0:T(8,128)(2,1)}, bf16[288,1728]{1,0:T(8,128)(2,1)}, u32[]{:S(2)}, u32[]{:S(2)}) collective-permute-start(bf16[288,1728]{1,0:T(8,128)(2,1)} %collective-permute-done.1), channel_id=1, source_target_pairs={{1,0},{0,1},{3,2},{2,3},{5,4},{4,5},{7,6},{6,7},{9,8},{8,9},{11,10... | collective-permute-start | bytes 2985992 | tf_op jit(solution)/shard_map/ppermute | solution.py:154
  27.5 4.4 %copy-start.4 = (bf16[896,1152]{1,0:T(8,128)(2,1)S(1)}, bf16[896,1152]{1,0:T(8,128)(2,1)}, u32[]{:S(2)}) copy-start(bf16[896,1152]{1,0:T(8,128)(2,1)} %copy-done.3) | copy-start | bytes 6193156
  28.6 8.3 %slice-start = ((s8[6193152]{0:T(1024)(128)(4,1)}), s8[4194304]{0:T(1024)(128)(4,1)S(1)}, s32[]{:S(2)}) async-start(s8[6193152]{0:T(1024)(128)(4,1)} %bitcast.72), calls=%async_computation | async-start | bytes 8388608
  29.7 7.3 %slice-start.1 = ((s8[6193152]{0:T(1024)(128)(4,1)}), s8[1998848]{0:T(1024)(128)(4,1)S(1)}, s32[]{:S(2)}) async-start(s8[6193152]{0:T(1024)(128)(4,1)} %bitcast.72), calls=%async_computation.1 | async-start | bytes 3997696
  29.7 17.6 %collective-permute-start.3 = (bf16[576,288]{0,1:T(8,128)(2,1)}, bf16[576,288]{0,1:T(8,128)(2,1)}, u32[]{:S(2)}, u32[]{:S(2)}) collective-permute-start(bf16[576,288]{0,1:T(8,128)(2,1)} %param.29), channel_id=1, source_target_pairs={{1,0},{0,1},{3,2},{2,3},{5,4},{4,5},{7,6},{6,7},{9,8},{8,9},{11,10... | collective-permute-start | bytes 995336 | tf_op jit(solution)/shard_map/ppermute | solution.py:104
  30.2 17.0 %collective-permute-start.4 = (bf16[576,288]{0,1:T(8,128)(2,1)}, bf16[576,288]{0,1:T(8,128)(2,1)}, u32[]{:S(2)}, u32[]{:S(2)}) collective-permute-start(bf16[576,288]{0,1:T(8,128)(2,1)} %param.29), channel_id=1, source_target_pairs={{2,0},{3,1},{0,2},{1,3},{6,4},{7,5},{4,6},{5,7},{10,8},{11,9},{8,1... | collective-permute-start | bytes 995336 | tf_op jit(solution)/shard_map/ppermute | solution.py:104
  47.2 2.2 %collective-permute-start.5 = (bf16[576,288]{0,1:T(8,128)(2,1)}, bf16[576,288]{0,1:T(8,128)(2,1)S(1)}, u32[]{:S(2)}, u32[]{:S(2)}) collective-permute-start(bf16[576,288]{0,1:T(8,128)(2,1)} %collective-permute-done.4), channel_id=1, source_target_pairs={{1,0},{0,1},{3,2},{2,3},{5,4},{4,5},{7,6},{6,7},{9,8},{8,9},{11,10... | collective-permute-start | bytes 995336 | tf_op jit(solution)/shard_map/ppermute | solution.py:104
  70.0 13.9 %collective-permute-start.9 = (bf16[64,1152]{1,0:T(8,128)(2,1)S(1)}, bf16[64,1152]{1,0:T(8,128)(2,1)S(1)}, u32[]{:S(2)}, u32[]{:S(2)}) collective-permute-start(bf16[64,1152]{1,0:T(8,128)(2,1)S(1)} %get-tuple-element.51), channel_id=1, source_target_pairs={{0,2},{1,3},{2,0},{3,1},{4,6},{5,7},{6,4},{7,5},{8,10},{9,11},{10,... | collective-permute-start | bytes 442376 | tf_op jit(solution)/shard_map/ppermute | solution.py:227
  70.7 13.2 %collective-permute-start.8 = (bf16[64,1152]{1,0:T(8,128)(2,1)S(1)}, bf16[64,1152]{1,0:T(8,128)(2,1)S(1)}, u32[]{:S(2)}, u32[]{:S(2)}) collective-permute-start(bf16[64,1152]{1,0:T(8,128)(2,1)S(1)} %get-tuple-element.52), channel_id=1, source_target_pairs={{0,2},{1,3},{2,0},{3,1},{4,6},{5,7},{6,4},{7,5},{8,10},{9,11},{10,... | collective-permute-start | bytes 442376 | tf_op jit(solution)/shard_map/ppermute | solution.py:227
  72.1 11.9 %collective-permute-start.7 = (bf16[64,1152]{1,0:T(8,128)(2,1)S(1)}, bf16[64,1152]{1,0:T(8,128)(2,1)S(1)}, u32[]{:S(2)}, u32[]{:S(2)}) collective-permute-start(bf16[64,1152]{1,0:T(8,128)(2,1)S(1)} %get-tuple-element.53), channel_id=1, source_target_pairs={{0,1},{1,2},{2,3},{3,0},{4,5},{5,6},{6,7},{7,4},{8,9},{9,10},{10,1... | collective-permute-start | bytes 442376 | tf_op jit(solution)/shard_map/ppermute | solution.py:227
  72.1 11.9 %collective-permute-start.6 = (bf16[64,1152]{1,0:T(8,128)(2,1)S(1)}, bf16[64,1152]{1,0:T(8,128)(2,1)S(1)}, u32[]{:S(2)}, u32[]{:S(2)}) collective-permute-start(bf16[64,1152]{1,0:T(8,128)(2,1)S(1)} %get-tuple-element.50), channel_id=1, source_target_pairs={{0,3},{1,0},{2,1},{3,2},{4,7},{5,4},{6,5},{7,6},{8,11},{9,8},{10,9... | collective-permute-start | bytes 442376 | tf_op jit(solution)/shard_map/ppermute | solution.py:227
  74.8 9.2 %copy-start.2 = (bf16[512,1152]{1,0:T(8,128)(2,1)S(1)}, bf16[512,1152]{1,0:T(8,128)(2,1)}, u32[]{:S(2)}) copy-start(bf16[512,1152]{1,0:T(8,128)(2,1)} %shard_map.253) | copy-start | bytes 3538948
  84.8 5.1 %copy-start.5 = (bf16[192,1152]{1,0:T(8,128)(2,1)S(1)}, bf16[192,1152]{1,0:T(8,128)(2,1)}, u32[]{:S(2)}) copy-start(bf16[192,1152]{1,0:T(8,128)(2,1)} %shard_map.254) | copy-start | bytes 1327108
  84.8 9.6 %copy-start.8 = (s32[4,24]{1,0:T(4,128)S(1)}, s32[4,24]{1,0:T(4,128)}, u32[]{:S(2)}) copy-start(s32[4,24]{1,0:T(4,128)} %constant.117) | copy-start | bytes 1156
  84.9 19.8 %collective-permute-start.10 = (bf16[256,1152]{1,0:T(8,128)(2,1)S(1)}, bf16[256,1152]{1,0:T(8,128)(2,1)S(1)}, u32[]{:S(2)}, u32[]{:S(2)}) collective-permute-start(bf16[256,1152]{1,0:T(8,128)(2,1)S(1)} %get-tuple-element.33), channel_id=1, source_target_pairs={{0,4},{4,8},{8,12},{1,5},{5,9},{9,13},{2,6},{6,10},{10,14},{3,7},{... | collective-permute-start | bytes 1769480 | tf_op jit(solution)/shard_map/ppermute | solution.py:260
  88.6 16.2 %collective-permute-start.11 = (bf16[256,1152]{1,0:T(8,128)(2,1)S(1)}, bf16[256,1152]{1,0:T(8,128)(2,1)S(1)}, u32[]{:S(2)}, u32[]{:S(2)}) collective-permute-start(bf16[256,1152]{1,0:T(8,128)(2,1)S(1)} %get-tuple-element.28), channel_id=1, source_target_pairs={{4,0},{8,4},{12,8},{5,1},{9,5},{13,9},{6,2},{10,6},{14,10},{7,3},{... | collective-permute-start | bytes 1769480 | tf_op jit(solution)/shard_map/ppermute | solution.py:261
  90.2 4.2 %collective-permute-start.15 = (bf16[24,1152]{1,0:T(8,128)(2,1)S(1)}, bf16[24,1152]{1,0:T(8,128)(2,1)S(1)}, u32[]{:S(2)}, u32[]{:S(2)}) collective-permute-start(bf16[24,1152]{1,0:T(8,128)(2,1)S(1)} %get-tuple-element.59), channel_id=1, source_target_pairs={{0,2},{1,3},{2,0},{3,1},{4,6},{5,7},{6,4},{7,5},{8,10},{9,11},{10,... | collective-permute-start | bytes 165896 | tf_op jit(solution)/shard_map/ppermute | solution.py:227
  91.2 13.5 %collective-permute-start.14 = (bf16[24,1152]{1,0:T(8,128)(2,1)S(1)}, bf16[24,1152]{1,0:T(8,128)(2,1)S(1)}, u32[]{:S(2)}, u32[]{:S(2)}) collective-permute-start(bf16[24,1152]{1,0:T(8,128)(2,1)S(1)} %get-tuple-element.60), channel_id=1, source_target_pairs={{0,2},{1,3},{2,0},{3,1},{4,6},{5,7},{6,4},{7,5},{8,10},{9,11},{10,... | collective-permute-start | bytes 165896 | tf_op jit(solution)/shard_map/ppermute | solution.py:227
  92.3 12.4 %collective-permute-start.13 = (bf16[24,1152]{1,0:T(8,128)(2,1)S(1)}, bf16[24,1152]{1,0:T(8,128)(2,1)S(1)}, u32[]{:S(2)}, u32[]{:S(2)}) collective-permute-start(bf16[24,1152]{1,0:T(8,128)(2,1)S(1)} %get-tuple-element.61), channel_id=1, source_target_pairs={{0,1},{1,2},{2,3},{3,0},{4,5},{5,6},{6,7},{7,4},{8,9},{9,10},{10,1... | collective-permute-start | bytes 165896 | tf_op jit(solution)/shard_map/ppermute | solution.py:227
  94.4 10.3 %collective-permute-start.12 = (bf16[24,1152]{1,0:T(8,128)(2,1)S(1)}, bf16[24,1152]{1,0:T(8,128)(2,1)S(1)}, u32[]{:S(2)}, u32[]{:S(2)}) collective-permute-start(bf16[24,1152]{1,0:T(8,128)(2,1)S(1)} %get-tuple-element.58), channel_id=1, source_target_pairs={{0,3},{1,0},{2,1},{3,2},{4,7},{5,4},{6,5},{7,6},{8,11},{9,8},{10,9... | collective-permute-start | bytes 165896 | tf_op jit(solution)/shard_map/ppermute | solution.py:227
  106.1 4.9 %collective-permute-start.19 = (bf16[24,1152]{1,0:T(8,128)(2,1)S(1)}, bf16[24,1152]{1,0:T(8,128)(2,1)S(1)}, u32[]{:S(2)}, u32[]{:S(2)}) collective-permute-start(bf16[24,1152]{1,0:T(8,128)(2,1)S(1)} %get-tuple-element.55), channel_id=1, source_target_pairs={{0,2},{1,3},{2,0},{3,1},{4,6},{5,7},{6,4},{7,5},{8,10},{9,11},{10,... | collective-permute-start | bytes 165896 | tf_op jit(solution)/shard_map/ppermute | solution.py:227
  107.2 4.8 %collective-permute-start.18 = (bf16[24,1152]{1,0:T(8,128)(2,1)S(1)}, bf16[24,1152]{1,0:T(8,128)(2,1)S(1)}, u32[]{:S(2)}, u32[]{:S(2)}) collective-permute-start(bf16[24,1152]{1,0:T(8,128)(2,1)S(1)} %get-tuple-element.56), channel_id=1, source_target_pairs={{0,2},{1,3},{2,0},{3,1},{4,6},{5,7},{6,4},{7,5},{8,10},{9,11},{10,... | collective-permute-start | bytes 165896 | tf_op jit(solution)/shard_map/ppermute | solution.py:227
  108.2 4.0 %collective-permute-start.17 = (bf16[24,1152]{1,0:T(8,128)(2,1)S(1)}, bf16[24,1152]{1,0:T(8,128)(2,1)S(1)}, u32[]{:S(2)}, u32[]{:S(2)}) collective-permute-start(bf16[24,1152]{1,0:T(8,128)(2,1)S(1)} %get-tuple-element.57), channel_id=1, source_target_pairs={{0,1},{1,2},{2,3},{3,0},{4,5},{5,6},{6,7},{7,4},{8,9},{9,10},{10,1... | collective-permute-start | bytes 165896 | tf_op jit(solution)/shard_map/ppermute | solution.py:227
  108.2 4.0 %collective-permute-start.16 = (bf16[24,1152]{1,0:T(8,128)(2,1)S(1)}, bf16[24,1152]{1,0:T(8,128)(2,1)S(1)}, u32[]{:S(2)}, u32[]{:S(2)}) collective-permute-start(bf16[24,1152]{1,0:T(8,128)(2,1)S(1)} %get-tuple-element.54), channel_id=1, source_target_pairs={{0,3},{1,0},{2,1},{3,2},{4,7},{5,4},{6,5},{7,6},{8,11},{9,8},{10,9... | collective-permute-start | bytes 165896 | tf_op jit(solution)/shard_map/ppermute | solution.py:227
  110.2 2.0 %copy-start.6 = (bf16[192,1152]{1,0:T(8,128)(2,1)S(1)}, bf16[192,1152]{1,0:T(8,128)(2,1)}, u32[]{:S(2)}) copy-start(bf16[192,1152]{1,0:T(8,128)(2,1)} %shard_map.255) | copy-start | bytes 1327108

commit v16 on v14

--- a/solution.py
+++ b/solution.py
@@ -145,6 +145,10 @@
     frames = tokens // (S * S)
     n = lax.axis_size("face")
     rows = w_qkv.shape[0]
+    rim = OVT * S * S
+    block_in = jnp.concatenate(
+        [block_in[:rim], block_in[tokens - rim :], block_in[rim : tokens - rim]], axis=0
+    )
     moved = modulate(block_in, modulation)
     if n == 4:
         me = lax.axis_index("face")
@@ -194,8 +198,7 @@
     queries = split[:, 0].transpose(1, 0, 2)
     keys = split[:, 1].transpose(1, 2, 0)
     values = split[:, 2].transpose(1, 0, 2)
-    rim = OVT * S * S
-    mid_a = rim + ((tokens - 2 * rim) // (2 * S * S)) * (S * S)
+    mid_a = 2 * rim + ((tokens - 2 * rim) // (2 * S * S)) * (S * S)
     gate = modulation[2]
 
     def tile_part(part_queries, part_in):
@@ -250,13 +253,13 @@
         mixed = jnp.where(dep >= 0, w_keep * own + w_take * partner, own)
         return mixed.reshape(tile_out.shape).astype(jnp.bfloat16)
 
-    rim_queries = jnp.concatenate([queries[:, :rim], queries[:, tokens - rim :]], axis=1)
-    rim_in = jnp.concatenate([block_in[:rim], block_in[tokens - rim :]], axis=0)
-    tile_rim = tile_part(rim_queries, rim_in)
+    tile_rim = tile_part(queries[:, : 2 * rim], block_in[: 2 * rim])
     outgoing_rim = strips_out(tile_rim)
     arrived_rim = strips_in(outgoing_rim)
-    first_queries, outgoing_rim = lax.optimization_barrier((queries[:, rim:mid_a], outgoing_rim))
-    tile_first = tile_part(first_queries, block_in[rim:mid_a])
+    first_queries, outgoing_rim = lax.optimization_barrier(
+        (queries[:, 2 * rim : mid_a], outgoing_rim)
+    )
+    tile_first = tile_part(first_queries, block_in[2 * rim : mid_a])
     arrived_rim, tile_first = lax.optimization_barrier((arrived_rim, tile_first))
     spaced_rim = space_blend(tile_rim, arrived_rim)
     low, high = lax.optimization_barrier((spaced_rim[:rim], spaced_rim[rim:]))
@@ -266,9 +269,9 @@
     outgoing_first = strips_out(tile_first)
     arrived_first = strips_in(outgoing_first)
     second_queries, low, high, outgoing_first = lax.optimization_barrier(
-        (queries[:, mid_a : tokens - rim], low, high, outgoing_first)
-    )
-    tile_second = tile_part(second_queries, block_in[mid_a : tokens - rim])
+        (queries[:, mid_a:], low, high, outgoing_first)
+    )
+    tile_second = tile_part(second_queries, block_in[mid_a:])
     lower, upper, arrived_first, tile_second = lax.optimization_barrier(
         (lower, upper, arrived_first, tile_second)
     )

time: 115 us -> 111 us (0.965)
  other arithmetic: 13.2 us -> 10.8 us
    concatenate x2 -> x1, other arithmetic: 3.35 us -> 1.12 us  [per_device(): jnp.concatenate([block_in[:rim], block_in[tokens - rim:], block_in[rim:to...]
    unnamed x39 -> x45, local copies, waits for them, and re-layouts: 6.7 us -> 4.71 us
    slice x4 -> x10, local copies, waits for them, and re-layouts: 5.33 us -> 6.47 us  [the longest x3 2.94 us: per_device(): block_in[:rim]]
  transfers between devices with their start and end apart: 20 -> 20, of which waited for: 7 -> 8; matrix products, arithmetic and copies ran while one was open for 40% -> 38% of each run, Pallas kernels for 16% -> 16%
where the time goes in v16:
time: 111 us
  Pallas kernels  35.1 us (32%)
  local copies, waits for them, and re-layouts  27.1 us (24%)
  starting transfers between devices  19.8 us (18%)
  matrix products  12.2 us (11%)
  other arithmetic  10.8 us (10%)
  waiting for transfers between devices  4.96 us (4%)
    pallas_call x3, Pallas kernels, attend_project(): pl.pallas_call(attention_kernel, grid=(1, heads // hb), in_specs=in_specs...  35.1 us
    ppermute x12, starting transfers between devices, strips_in(): lax.ppermute(sent, 'face', [(i, (i + shift) % n) for i in range(n)])  9.5 us
    dot_general x2, matrix products, chip_part(): jnp.dot(lax.dynamic_index_in_dim(moved_chips, chip, 0, keepdims=False), w...  7.48 us
    ppermute x6, starting transfers between devices, fetch(): return lax.ppermute(x, 'face', [(src_of(i), i) for i in range(n)])  5.13 us
    unnamed x45, local copies, waits for them, and re-layouts  4.71 us
    ppermute x1, starting transfers between devices, per_device(): lower = lax.ppermute(high, 'tm', [(i, i + 1) for i in range(count - 1)])  3.91 us
    dot_general x3, matrix products, strips_out(): jnp.dot(pick, tile_out, preferred_element_type=jnp.float32)  3.36 us
    ppermute x12, waiting for transfers between devices, strips_in(): lax.ppermute(sent, 'face', [(i, (i + shift) % n) for i in range(n)])  3.23 us
  transfers between devices with their start and end apart: 20, of which 8 were waited for; matrix products, arithmetic and copies ran while one was open for 38% of the time, Pallas kernels for 16%

profile of v16, /device:TPU:0, one launch (start us, length us, event | category | flops | bytes accessed | tf_op | source)
XLA Modules:
  0.0 110.6 jit_solution(8425320249171366157)
XLA Ops:
  0.0 0.5 collective-permute-start
  0.5 2.6 %collective-permute-start.1 = (bf16[288,1728]{1,0:T(8,128)(2,1)}, bf16[288,1728]{1,0:T(8,128)(2,1)}, u32[]{:S(2)}, u32[]{:S(2)}) collective-permute-start(bf16[288,1728]{1,0:T(8,128)(2,1)} %param.28), channel_id=1, source_target_pairs={{2,0},{3,1},{0,2},{1,3},{6,4},{7,5},{4,6},{5,7},{10,8},{11,9},{8,1... | collective-permute-start | bytes 2985992 | tf_op jit(solution)/shard_map/ppermute | solution.py:158
  3.0 2.4 %slice_bitcast_fusion.4 = (bf16[256,1152]{1,0:T(8,128)(2,1)S(1)}, bf16[256,1152]{1,0:T(8,128)(2,1)S(1)}, bf16[1,1,256,1152]{3,2,1,0:T(8,128)(2,1)}, bf16[1,1,256,1152]{3,2,1,0:T(8,128)(2,1)}) fusion(bf16[1,1,896,1152]{3,2,1,0:T(8,128)(2,1)} %param.26), kind=kLoop, calls=%fused_computation.98 | loop fusion | bytes 3538944 | tf_op jit(solution)/shard_map/slice | solution.py:150
  6.0 1.1 %pad_maximum_fusion.1.refs_8_ = bf16[512,1152]{1,0:T(8,128)(2,1)} fusion(bf16[256,1152]{1,0:T(8,128)(2,1)S(1)} %get-tuple-element.43, bf16[256,1152]{1,0:T(8,128)(2,1)S(1)} %get-tuple-element.42), kind=kLoop, calls=%fused_computation.29 | loop fusion | flops 2359296 | bytes 2359296 | tf_op jit(solution)/shard_map/concatenate | solution.py:149
  7.5 0.9 copy.63
  8.8 0.6 fusion.1
  9.5 0.6 add_reduce_fusion
  10.3 0.7 fusion.44
  11.1 2.6 %select_bitcast_fusion.1 = (f32[64]{0:T(128)S(1)}, f32[64]{0:T(128)S(1)}) fusion(pred[64,1]{0,1:T(4,128)(4,1)S(1)} %copy-done.16, f32[]{:T(128)} %bitcast.18, f32[]{:T(128)} %bitcast.17, f32[]{:T(128)} %bitcast.33, f32[]{:T(128)} %bitcast.32), kind=kLoop, calls=%fused_computation.95 | loop fusion | flops 128 | bytes 592 | tf_op jit(solution)/shard_map/mul | solution.py:253
  14.5 1.9 %add_convert_fusion.1 = bf16[896,2,576]{0,2,1:T(8,128)(2,1)} fusion(bf16[384,2,576]{0,2,1:T(8,128)(2,1)S(1)} %bitcast.77, bf16[256,2,576]{0,2,1:T(8,128)(2,1)S(1)} %bitcast.83, bf16[256,2,576]{0,2,1:T(8,128)(2,1)S(1)} %bitcast.82, f32[2,576]{1,0:T(2,128)S(1)} %add.115, f32[2,576]{1,0:T(2,128)S(1)} %mul.167, f32[896]{0:T(1024)S(1)} %add_rsqrt_fusion, ...), kind=kLoop, calls=%fused_computation.5 | loop fusion | flops 11354112 | bytes 4145152 | tf_op jit(solution)/shard_map/convert_element_type | solution.py:30
  16.3 1.4 %broadcast.117.clone = bf16[2,288,1728]{2,1,0:T(8,128)(2,1)} broadcast(bf16[]{:T(256)} %constant.111.clone.1), dimensions={} | broadcast | bytes 1990658 | tf_op jit(solution)/shard_map/broadcast.4
  17.9 1.0 bitcast_dynamic-update-slice_fusion.3
  19.7 2.2 %bitcast_dynamic-update-slice_fusion.2 = bf16[2,288,1728]{2,1,0:T(8,128)(2,1)} fusion(bf16[2,288,1728]{2,1,0:T(8,128)(2,1)} %bitcast_dynamic-update-slice_fusion.3, s32[]{:T(128)S(6)} %select_n.138, bf16[288,1728]{1,0:T(8,128)(2,1)} %collective-permute-done), kind=kLoop, calls=%fused_computation.38 | loop fusion | bytes 2064388 | tf_op jit(solution)/shard_map/jit(dynamic_update_index_in_dim)/dynamic_update_slice | solution.py:165
  22.0 4.6 %fusion.14 = f32[896,1728]{0,1:T(8,128)S(1)} fusion(bf16[576,1728]{1,0:T(8,128)(2,1)} %bitcast.9, bf16[896,2,576]{0,2,1:T(8,128)(2,1)S(1)} %copy-done.5, s32[]{:T(128)S(6)} %select_n.135), kind=kOutput, calls=%fused_computation.40 | convolution fusion | flops 1783627776 | bytes 9216004 | tf_op jit(solution)/shard_map/dot_general | solution.py:169
  26.8 1.0 slice_bitcast_fusion.1
  28.0 1.3 %bitcast_dynamic-update-slice_fusion.1 = bf16[2,288,1728]{2,1,0:T(8,128)(2,1)S(1)} fusion(bf16[2,288,1728]{2,1,0:T(8,128)(2,1)S(1)} %broadcast.117, s32[]{:T(128)S(6)} %select_n.137, bf16[288,1728]{1,0:T(8,128)(2,1)} %collective-permute-done.1), kind=kLoop, calls=%fused_computation.35 | loop fusion | bytes 2027524 | tf_op jit(solution)/shard_map/jit(dynamic_update_index_in_dim)/dynamic_update_slice | solution.py:164
  29.8 1.7 %collective-permute-start.4 = (bf16[576,288]{0,1:T(8,128)(2,1)}, bf16[576,288]{0,1:T(8,128)(2,1)}, u32[]{:S(2)}, u32[]{:S(2)}) collective-permute-start(bf16[576,288]{0,1:T(8,128)(2,1)} %param.29), channel_id=1, source_target_pairs={{2,0},{3,1},{0,2},{1,3},{6,4},{7,5},{4,6},{5,7},{10,8},{11,9},{8,1... | collective-permute-start | bytes 995336 | tf_op jit(solution)/shard_map/ppermute | solution.py:104
  31.6 2.9 %fusion.12 = f32[896,1728]{0,1:T(8,128)S(1)} fusion(bf16[576,1728]{1,0:T(8,128)(2,1)S(1)} %bitcast.84, bf16[896,2,576]{0,2,1:T(8,128)(2,1)S(1)} %copy-done.5, s32[]{:T(128)S(6)} %select_n.139), kind=kOutput, calls=%fused_computation.36 | convolution fusion | flops 1783627776 | bytes 9289732 | tf_op jit(solution)/shard_map/dot_general | solution.py:169
  34.5 0.8 add_convert_fusion
  35.3 1.6 %fusion.38 = (bf16[896,1,8,72]{0,3,2,1:T(8,128)(2,1)S(1)}, bf16[896,1,8,72]{0,3,2,1:T(8,128)(2,1)}, bf16[8,72,896]{2,1,0:T(8,128)(2,1)}) fusion(bf16[896,3,8,72]{0,3,2,1:T(8,128)(2,1)S(1)} %bitcast.78), kind=kLoop, calls=%fused_computation.99 | loop fusion | bytes 6193152 | tf_op jit(solution)/shard_map/slice | solution.py:200
  36.9 1.9 %copy.64 = bf16[896,1,8,72]{3,0,2,1:T(8,128)(2,1)S(1)} copy(bf16[896,1,8,72]{0,3,2,1:T(8,128)(2,1)} %get-tuple-element.38) | data formatting | bytes 2064384
  38.8 1.1 slice.170.refs_0_.refs_4_
  39.9 1.7 %copy.65 = bf16[896,1,8,72]{3,0,2,1:T(8,128)(2,1)} copy(bf16[896,1,8,72]{0,3,2,1:T(8,128)(2,1)S(1)} %get-tuple-element.37) | data formatting | bytes 2064384
  41.6 1.0 bitcast_dynamic-update-slice_fusion.7
  42.8 1.0 bitcast_dynamic-update-slice_fusion.6
  43.8 1.0 bitcast_dynamic-update-slice_fusion.5
  45.0 1.8 %copy.57.refs_3_.refs_7_ = bf16[576,1152]{1,0:T(8,128)(2,1)} copy(bf16[576,1152]{0,1:T(8,128)(2,1)S(1)} %bitcast.81) | data formatting | bytes 2654208 | tf_op jit(solution)/shard_map/reshape | solution.py:195
  46.8 17.0 %shard_map.253 = bf16[512,1152]{1,0:T(8,128)(2,1)} custom-call(bf16[8,512,72]{2,1,0:T(8,128)(2,1)} %slice.170.refs_0_.refs_4_, bf16[8,72,896]{2,1,0:T(8,128)(2,1)} %get-tuple-element.39.refs_1_.refs_5_, bf16[8,896,72]{2,1,0:T(8,128)(2,1)} %bitcast.69, bf16[576,1152]{1,0:T(8,128)(2,1)} %copy.57.refs_3_.refs_7_, bf16[8,512,72]{2,1,0:T(8,128)(2,1)} %slice.170.refs_0_.refs_4_, ...), custom_call_target="tpu_custom_call" | custom-call | tf_op jit(solution)/shard_map/pallas_call | solution.py:88
  63.7 1.8 %convolution_convert_fusion = bf16[256,1152]{1,0:T(8,128)(2,1)S(1)} fusion(bf16[512,1152]{1,0:T(8,128)(2,1)} %shard_map.253, s32[256]{0:T(256)S(1)} %eq.138), kind=kOutput, calls=%fused_computation.15 | convolution fusion | flops 302415872 | bytes 1770496 | tf_op jit(solution)/shard_map/dot_general | solution.py:225
  66.2 1.6 %collective-permute-start.8 = (bf16[64,1152]{1,0:T(8,128)(2,1)S(1)}, bf16[64,1152]{1,0:T(8,128)(2,1)S(1)}, u32[]{:S(2)}, u32[]{:S(2)}) collective-permute-start(bf16[64,1152]{1,0:T(8,128)(2,1)S(1)} %get-tuple-element.52), channel_id=1, source_target_pairs={{0,2},{1,3},{2,0},{3,1},{4,6},{5,7},{6,4},{7,5},{8,10},{9,11},{10,... | collective-permute-start | bytes 442376 | tf_op jit(solution)/shard_map/ppermute | solution.py:234
  68.2 1.0 fusion.39
  69.2 9.1 %shard_map.254 = bf16[192,1152]{1,0:T(8,128)(2,1)} custom-call(bf16[8,192,72]{2,1,0:T(8,128)(2,1)} %get-tuple-element.23.refs_0_.refs_4_, bf16[8,72,896]{2,1,0:T(8,128)(2,1)} %get-tuple-element.39.refs_1_.refs_5_, bf16[8,896,72]{2,1,0:T(8,128)(2,1)} %bitcast.71, bf16[576,1152]{1,0:T(8,128)(2,1)} %copy.57.refs_3_.refs_7_, ...), custom_call_target="tpu_custom_call" | custom-call | tf_op jit(solution)/shard_map/pallas_call | solution.py:88
  78.5 0.7 fusion.4
  79.4 3.9 %collective-permute-start.10 = (bf16[256,1152]{1,0:T(8,128)(2,1)S(1)}, bf16[256,1152]{1,0:T(8,128)(2,1)S(1)}, u32[]{:S(2)}, u32[]{:S(2)}) collective-permute-start(bf16[256,1152]{1,0:T(8,128)(2,1)S(1)} %get-tuple-element.33), channel_id=1, source_target_pairs={{0,4},{4,8},{8,12},{1,5},{5,9},{9,13},{2,6},{6,10},{10,14},{3,7},{... | collective-permute-start | bytes 1769480 | tf_op jit(solution)/shard_map/ppermute | solution.py:267
  83.3 1.3 %collective-permute-start.11 = (bf16[256,1152]{1,0:T(8,128)(2,1)S(1)}, bf16[256,1152]{1,0:T(8,128)(2,1)S(1)}, u32[]{:S(2)}, u32[]{:S(2)}) collective-permute-start(bf16[256,1152]{1,0:T(8,128)(2,1)S(1)} %get-tuple-element.28), channel_id=1, source_target_pairs={{4,0},{8,4},{12,8},{5,1},{9,5},{13,9},{6,2},{10,6},{14,10},{7,3},{... | collective-permute-start | bytes 1769480 | tf_op jit(solution)/shard_map/ppermute | solution.py:268
  84.9 0.6 collective-permute-start.12
  85.5 1.5 %collective-permute-start.14 = (bf16[24,1152]{1,0:T(8,128)(2,1)S(1)}, bf16[24,1152]{1,0:T(8,128)(2,1)S(1)}, u32[]{:S(2)}, u32[]{:S(2)}) collective-permute-start(bf16[24,1152]{1,0:T(8,128)(2,1)S(1)} %get-tuple-element.60), channel_id=1, source_target_pairs={{0,2},{1,3},{2,0},{3,1},{4,6},{5,7},{6,4},{7,5},{8,10},{9,11},{10,... | collective-permute-start | bytes 165896 | tf_op jit(solution)/shard_map/ppermute | solution.py:234
  87.3 1.9 %collective-permute-start.15 = (bf16[24,1152]{1,0:T(8,128)(2,1)S(1)}, bf16[24,1152]{1,0:T(8,128)(2,1)S(1)}, u32[]{:S(2)}, u32[]{:S(2)}) collective-permute-start(bf16[24,1152]{1,0:T(8,128)(2,1)S(1)} %get-tuple-element.59), channel_id=1, source_target_pairs={{0,2},{1,3},{2,0},{3,1},{4,6},{5,7},{6,4},{7,5},{8,10},{9,11},{10,... | collective-permute-start | bytes 165896 | tf_op jit(solution)/shard_map/ppermute | solution.py:234
  90.5 9.0 %shard_map.255 = bf16[192,1152]{1,0:T(8,128)(2,1)} custom-call(bf16[8,192,72]{2,1,0:T(8,128)(2,1)} %get-tuple-element.29.refs_0_.refs_4_, bf16[8,72,896]{2,1,0:T(8,128)(2,1)} %get-tuple-element.39.refs_1_.refs_5_, bf16[8,896,72]{2,1,0:T(8,128)(2,1)} %bitcast.73, bf16[576,1152]{1,0:T(8,128)(2,1)} %copy.57.refs_3_.refs_7_, ...), custom_call_target="tpu_custom_call" | custom-call | tf_op jit(solution)/shard_map/pallas_call | solution.py:88
  99.6 1.2 %collective-permute-done.11 = bf16[256,1152]{1,0:T(8,128)(2,1)S(1)} collective-permute-done((bf16[256,1152]{1,0:T(8,128)(2,1)S(1)}, bf16[256,1152]{1,0:T(8,128)(2,1)S(1)}, u32[]{:S(2)}, u32[]{:S(2)}) %collective-permute-start.11) | collective-permute-done | bytes 589856 | tf_op jit(solution)/shard_map/ppermute | solution.py:268
  100.9 1.3 %convolution_convert_fusion.1 = bf16[96,1152]{1,0:T(8,128)(2,1)S(1)} fusion(bf16[192,1152]{1,0:T(8,128)(2,1)} %shard_map.255, s32[96]{0:T(128)S(1)} %eq.142), kind=kOutput, calls=%fused_computation.17 | convolution fusion | flops 42596352 | bytes 663936 | tf_op jit(solution)/shard_map/dot_general | solution.py:225
  102.2 0.7 collective-permute-start.16
  102.9 0.7 collective-permute-start.18
  103.6 1.4 %collective-permute-start.19 = (bf16[24,1152]{1,0:T(8,128)(2,1)S(1)}, bf16[24,1152]{1,0:T(8,128)(2,1)S(1)}, u32[]{:S(2)}, u32[]{:S(2)}) collective-permute-start(bf16[24,1152]{1,0:T(8,128)(2,1)S(1)} %get-tuple-element.55), channel_id=1, source_target_pairs={{0,2},{1,3},{2,0},{3,1},{4,6},{5,7},{6,4},{7,5},{8,10},{9,11},{10,... | collective-permute-start | bytes 165896 | tf_op jit(solution)/shard_map/ppermute | solution.py:234
  106.0 0.5 collective-permute-done.17
  106.5 1.1 %collective-permute-done.18 = bf16[24,1152]{1,0:T(8,128)(2,1)S(1)} collective-permute-done((bf16[24,1152]{1,0:T(8,128)(2,1)S(1)}, bf16[24,1152]{1,0:T(8,128)(2,1)S(1)}, u32[]{:S(2)}, u32[]{:S(2)}) %collective-permute-start.18) | collective-permute-done | bytes 55328 | tf_op jit(solution)/shard_map/ppermute | solution.py:234
  107.6 1.2 %collective-permute-done.19 = bf16[24,1152]{1,0:T(8,128)(2,1)S(1)} collective-permute-done((bf16[24,1152]{1,0:T(8,128)(2,1)S(1)}, bf16[24,1152]{1,0:T(8,128)(2,1)S(1)}, u32[]{:S(2)}, u32[]{:S(2)}) %collective-permute-start.19) | collective-permute-done | bytes 55328 | tf_op jit(solution)/shard_map/ppermute | solution.py:234
  109.1 1.5 %maximum_bitcast_fusion = bf16[1,1,896,1152]{3,2,1,0:T(8,128)(2,1)} fusion(bf16[256,1152]{1,0:T(8,128)(2,1)S(1)} %fusion.11, bf16[192,1152]{1,0:T(8,128)(2,1)S(1)} %fusion.19, bf16[192,1152]{1,0:T(8,128)(2,1)S(1)} %fusion.7, bf16[256,1152]{1,0:T(8,128)(2,1)S(1)} %fusion.9), kind=kLoop, calls=%fused_computation.20 | loop fusion | flops 8257536 | bytes 4128768 | tf_op jit(solution)/shard_map/reshape | solution.py:308
  (133 shorter events, 9.1 us)
Async XLA Ops:
  0.0 7.1 %copy-start = (s32[4,4,4]{2,1,0:T(4,128)S(1)}, s32[4,4,4]{2,1,0:T(4,128)}, u32[]{:S(2)}) copy-start(s32[4,4,4]{2,1,0:T(4,128)} %param.30) | copy-start | bytes 772
  0.0 19.7 %collective-permute-start = (bf16[288,1728]{1,0:T(8,128)(2,1)}, bf16[288,1728]{1,0:T(8,128)(2,1)}, u32[]{:S(2)}, u32[]{:S(2)}) collective-permute-start(bf16[288,1728]{1,0:T(8,128)(2,1)} %param.28), channel_id=1, source_target_pairs={{1,0},{0,1},{3,2},{2,3},{5,4},{4,5},{7,6},{6,7},{9,8},{8,9},{11,10... | collective-permute-start | bytes 2985992 | tf_op jit(solution)/shard_map/ppermute | solution.py:158
  0.5 26.3 %collective-permute-start.1 = (bf16[288,1728]{1,0:T(8,128)(2,1)}, bf16[288,1728]{1,0:T(8,128)(2,1)}, u32[]{:S(2)}, u32[]{:S(2)}) collective-permute-start(bf16[288,1728]{1,0:T(8,128)(2,1)} %param.28), channel_id=1, source_target_pairs={{2,0},{3,1},{0,2},{1,3},{6,4},{7,5},{4,6},{5,7},{10,8},{11,9},{8,1... | collective-permute-start | bytes 2985992 | tf_op jit(solution)/shard_map/ppermute | solution.py:158
  5.7 1.8 %slice-start = ((bf16[1,1,896,1152]{3,2,1,0:T(8,128)(2,1)}), bf16[1,1,384,1152]{3,2,1,0:T(8,128)(2,1)S(1)}, s32[]{:S(2)}) async-start(bf16[1,1,896,1152]{3,2,1,0:T(8,128)(2,1)} %param.26), calls=%async_computation | async-start | bytes 1769472 | tf_op jit(solution)/shard_map/slice | solution.py:150
  8.3 1.1 %copy-start.9 = (f32[3,1152]{1,0:T(4,128)S(1)}, f32[3,1152]{1,0:T(4,128)}, u32[]{:S(2)}) copy-start(f32[3,1152]{1,0:T(4,128)} %param.27) | copy-start | bytes 41476
  8.4 1.7 %copy-start.17 = (s32[2]{0:T(128)S(1)}, s32[2]{0:T(128)}, u32[]{:S(2)}) copy-start(s32[2]{0:T(128)} %param.31) | copy-start | bytes 28
  8.4 1.8 %copy-start.19 = (s32[4]{0:T(128)S(1)}, s32[4]{0:T(128)}, u32[]{:S(2)}) copy-start(s32[4]{0:T(128)} %constant.114.clone) | copy-start | bytes 52
  8.4 2.5 %copy-start.13 = (s32[4,64]{1,0:T(4,128)S(1)}, s32[4,64]{1,0:T(4,128)}, u32[]{:S(2)}) copy-start(s32[4,64]{1,0:T(4,128)} %constant.115.clone) | copy-start | bytes 3076
  8.4 2.5 %copy-start.14 = (s32[4,64]{1,0:T(4,128)S(1)}, s32[4,64]{1,0:T(4,128)}, u32[]{:S(2)}) copy-start(s32[4,64]{1,0:T(4,128)} %constant.116.clone) | copy-start | bytes 3076
  8.4 2.6 %copy-start.11 = (s32[4,24]{1,0:T(4,128)S(1)}, s32[4,24]{1,0:T(4,128)}, u32[]{:S(2)}) copy-start(s32[4,24]{1,0:T(4,128)} %constant.120.clone) | copy-start | bytes 1156
  8.4 2.6 %copy-start.12 = (s32[4,24]{1,0:T(4,128)S(1)}, s32[4,24]{1,0:T(4,128)}, u32[]{:S(2)}) copy-start(s32[4,24]{1,0:T(4,128)} %constant.121.clone) | copy-start | bytes 1156
  8.4 2.6 %copy-start.16 = (pred[64,1]{0,1:T(4,128)(4,1)S(1)}, pred[64,1]{0,1:T(4,128)(4,1)}, u32[]{:S(2)}) copy-start(pred[64,1]{0,1:T(4,128)(4,1)} %constant.118.clone) | copy-start | bytes 196
  8.4 5.2 %copy-start.15 = (s32[4,64]{1,0:T(4,128)S(1)}, s32[4,64]{1,0:T(4,128)}, u32[]{:S(2)}) copy-start(s32[4,64]{1,0:T(4,128)} %constant.126) | copy-start | bytes 3076
  8.5 5.3 %copy-start.4 = (bf16[1,1,256,1152]{3,2,1,0:T(8,128)(2,1)S(1)}, bf16[1,1,256,1152]{3,2,1,0:T(8,128)(2,1)}, u32[]{:S(2)}) copy-start(bf16[1,1,256,1152]{3,2,1,0:T(8,128)(2,1)} %get-tuple-element.45) | copy-start | bytes 1769476
  8.8 5.2 %copy-start.3 = (bf16[1,1,256,1152]{3,2,1,0:T(8,128)(2,1)S(1)}, bf16[1,1,256,1152]{3,2,1,0:T(8,128)(2,1)}, u32[]{:S(2)}) copy-start(bf16[1,1,256,1152]{3,2,1,0:T(8,128)(2,1)} %get-tuple-element.44) | copy-start | bytes 1769476
  16.3 1.6 %copy-start.8 = (bf16[288,1728]{1,0:T(8,128)(2,1)S(1)}, bf16[288,1728]{1,0:T(8,128)(2,1)}, u32[]{:S(2)}) copy-start(bf16[288,1728]{1,0:T(8,128)(2,1)} %param.28) | copy-start | bytes 2985988
  16.3 3.1 %copy-start.20 = (pred[64]{0:T(512)(128)(4,1)S(1)}, pred[64]{0:T(512)(128)(4,1)}, u32[]{:S(2)}) copy-start(pred[64]{0:T(512)(128)(4,1)} %constant.125) | copy-start | bytes 196
  16.3 3.3 %copy-start.18 = (s32[4]{0:T(128)S(1)}, s32[4]{0:T(128)}, u32[]{:S(2)}) copy-start(s32[4]{0:T(128)} %param.32) | copy-start | bytes 52
  17.9 4.0 %copy-start.5 = (bf16[896,2,576]{0,2,1:T(8,128)(2,1)S(1)}, bf16[896,2,576]{0,2,1:T(8,128)(2,1)}, u32[]{:S(2)}) copy-start(bf16[896,2,576]{0,2,1:T(8,128)(2,1)} %add_convert_fusion.1) | copy-start | bytes 6193156
  22.0 4.9 %copy-start.2 = (bf16[1,1,896,1152]{3,2,1,0:T(8,128)(2,1)S(1)}, bf16[1,1,896,1152]{3,2,1,0:T(8,128)(2,1)}, u32[]{:S(2)}) copy-start(bf16[1,1,896,1152]{3,2,1,0:T(8,128)(2,1)} %param.26) | copy-start | bytes 6193156
  26.7 2.8 %collective-permute-start.2 = (bf16[288,1728]{1,0:T(8,128)(2,1)}, bf16[288,1728]{1,0:T(8,128)(2,1)S(1)}, u32[]{:S(2)}, u32[]{:S(2)}) collective-permute-start(bf16[288,1728]{1,0:T(8,128)(2,1)} %collective-permute-done.1), channel_id=1, source_target_pairs={{1,0},{0,1},{3,2},{2,3},{5,4},{4,5},{7,6},{6,7},{9,8},{8,9},{11,10... | collective-permute-start | bytes 2985992 | tf_op jit(solution)/shard_map/ppermute | solution.py:158
  29.6 13.2 %collective-permute-start.3 = (bf16[576,288]{0,1:T(8,128)(2,1)}, bf16[576,288]{0,1:T(8,128)(2,1)}, u32[]{:S(2)}, u32[]{:S(2)}) collective-permute-start(bf16[576,288]{0,1:T(8,128)(2,1)} %param.29), channel_id=1, source_target_pairs={{1,0},{0,1},{3,2},{2,3},{5,4},{4,5},{7,6},{6,7},{9,8},{8,9},{11,10... | collective-permute-start | bytes 995336 | tf_op jit(solution)/shard_map/ppermute | solution.py:104
  29.8 12.9 %collective-permute-start.4 = (bf16[576,288]{0,1:T(8,128)(2,1)}, bf16[576,288]{0,1:T(8,128)(2,1)}, u32[]{:S(2)}, u32[]{:S(2)}) collective-permute-start(bf16[576,288]{0,1:T(8,128)(2,1)} %param.29), channel_id=1, source_target_pairs={{2,0},{3,1},{0,2},{1,3},{6,4},{7,5},{4,6},{5,7},{10,8},{11,9},{8,1... | collective-permute-start | bytes 995336 | tf_op jit(solution)/shard_map/ppermute | solution.py:104
  42.7 2.2 %collective-permute-start.5 = (bf16[576,288]{0,1:T(8,128)(2,1)}, bf16[576,288]{0,1:T(8,128)(2,1)S(1)}, u32[]{:S(2)}, u32[]{:S(2)}) collective-permute-start(bf16[576,288]{0,1:T(8,128)(2,1)} %collective-permute-done.4), channel_id=1, source_target_pairs={{1,0},{0,1},{3,2},{2,3},{5,4},{4,5},{7,6},{6,7},{9,8},{8,9},{11,10... | collective-permute-start | bytes 995336 | tf_op jit(solution)/shard_map/ppermute | solution.py:104
  65.6 12.7 %collective-permute-start.6 = (bf16[64,1152]{1,0:T(8,128)(2,1)S(1)}, bf16[64,1152]{1,0:T(8,128)(2,1)S(1)}, u32[]{:S(2)}, u32[]{:S(2)}) collective-permute-start(bf16[64,1152]{1,0:T(8,128)(2,1)S(1)} %get-tuple-element.50), channel_id=1, source_target_pairs={{0,3},{1,0},{2,1},{3,2},{4,7},{5,4},{6,5},{7,6},{8,11},{9,8},{10,9... | collective-permute-start | bytes 442376 | tf_op jit(solution)/shard_map/ppermute | solution.py:234
  66.0 12.3 %collective-permute-start.7 = (bf16[64,1152]{1,0:T(8,128)(2,1)S(1)}, bf16[64,1152]{1,0:T(8,128)(2,1)S(1)}, u32[]{:S(2)}, u32[]{:S(2)}) collective-permute-start(bf16[64,1152]{1,0:T(8,128)(2,1)S(1)} %get-tuple-element.53), channel_id=1, source_target_pairs={{0,1},{1,2},{2,3},{3,0},{4,5},{5,6},{6,7},{7,4},{8,9},{9,10},{10,1... | collective-permute-start | bytes 442376 | tf_op jit(solution)/shard_map/ppermute | solution.py:234
  66.2 12.1 %collective-permute-start.8 = (bf16[64,1152]{1,0:T(8,128)(2,1)S(1)}, bf16[64,1152]{1,0:T(8,128)(2,1)S(1)}, u32[]{:S(2)}, u32[]{:S(2)}) collective-permute-start(bf16[64,1152]{1,0:T(8,128)(2,1)S(1)} %get-tuple-element.52), channel_id=1, source_target_pairs={{0,2},{1,3},{2,0},{3,1},{4,6},{5,7},{6,4},{7,5},{8,10},{9,11},{10,... | collective-permute-start | bytes 442376 | tf_op jit(solution)/shard_map/ppermute | solution.py:234
  67.8 10.7 %collective-permute-start.9 = (bf16[64,1152]{1,0:T(8,128)(2,1)S(1)}, bf16[64,1152]{1,0:T(8,128)(2,1)S(1)}, u32[]{:S(2)}, u32[]{:S(2)}) collective-permute-start(bf16[64,1152]{1,0:T(8,128)(2,1)S(1)} %get-tuple-element.51), channel_id=1, source_target_pairs={{0,2},{1,3},{2,0},{3,1},{4,6},{5,7},{6,4},{7,5},{8,10},{9,11},{10,... | collective-permute-start | bytes 442376 | tf_op jit(solution)/shard_map/ppermute | solution.py:234
  69.2 9.3 %copy-start.1 = (bf16[512,1152]{1,0:T(8,128)(2,1)S(1)}, bf16[512,1152]{1,0:T(8,128)(2,1)}, u32[]{:S(2)}) copy-start(bf16[512,1152]{1,0:T(8,128)(2,1)} %shard_map.253) | copy-start | bytes 3538948
  79.3 5.3 %copy-start.6 = (bf16[192,1152]{1,0:T(8,128)(2,1)S(1)}, bf16[192,1152]{1,0:T(8,128)(2,1)}, u32[]{:S(2)}) copy-start(bf16[192,1152]{1,0:T(8,128)(2,1)} %shard_map.254) | copy-start | bytes 1327108
  79.3 10.0 %copy-start.10 = (s32[4,24]{1,0:T(4,128)S(1)}, s32[4,24]{1,0:T(4,128)}, u32[]{:S(2)}) copy-start(s32[4,24]{1,0:T(4,128)} %constant.127) | copy-start | bytes 1156
  79.4 20.2 %collective-permute-start.10 = (bf16[256,1152]{1,0:T(8,128)(2,1)S(1)}, bf16[256,1152]{1,0:T(8,128)(2,1)S(1)}, u32[]{:S(2)}, u32[]{:S(2)}) collective-permute-start(bf16[256,1152]{1,0:T(8,128)(2,1)S(1)} %get-tuple-element.33), channel_id=1, source_target_pairs={{0,4},{4,8},{8,12},{1,5},{5,9},{9,13},{2,6},{6,10},{10,14},{3,7},{... | collective-permute-start | bytes 1769480 | tf_op jit(solution)/shard_map/ppermute | solution.py:267
  83.3 17.6 %collective-permute-start.11 = (bf16[256,1152]{1,0:T(8,128)(2,1)S(1)}, bf16[256,1152]{1,0:T(8,128)(2,1)S(1)}, u32[]{:S(2)}, u32[]{:S(2)}) collective-permute-start(bf16[256,1152]{1,0:T(8,128)(2,1)S(1)} %get-tuple-element.28), channel_id=1, source_target_pairs={{4,0},{8,4},{12,8},{5,1},{9,5},{13,9},{6,2},{10,6},{14,10},{7,3},{... | collective-permute-start | bytes 1769480 | tf_op jit(solution)/shard_map/ppermute | solution.py:268
  84.9 2.4 %collective-permute-start.12 = (bf16[24,1152]{1,0:T(8,128)(2,1)S(1)}, bf16[24,1152]{1,0:T(8,128)(2,1)S(1)}, u32[]{:S(2)}, u32[]{:S(2)}) collective-permute-start(bf16[24,1152]{1,0:T(8,128)(2,1)S(1)} %get-tuple-element.58), channel_id=1, source_target_pairs={{0,3},{1,0},{2,1},{3,2},{4,7},{5,4},{6,5},{7,6},{8,11},{9,8},{10,9... | collective-permute-start | bytes 165896 | tf_op jit(solution)/shard_map/ppermute | solution.py:234
  85.5 14.0 %collective-permute-start.13 = (bf16[24,1152]{1,0:T(8,128)(2,1)S(1)}, bf16[24,1152]{1,0:T(8,128)(2,1)S(1)}, u32[]{:S(2)}, u32[]{:S(2)}) collective-permute-start(bf16[24,1152]{1,0:T(8,128)(2,1)S(1)} %get-tuple-element.61), channel_id=1, source_target_pairs={{0,1},{1,2},{2,3},{3,0},{4,5},{5,6},{6,7},{7,4},{8,9},{9,10},{10,1... | collective-permute-start | bytes 165896 | tf_op jit(solution)/shard_map/ppermute | solution.py:234
  85.5 14.0 %collective-permute-start.14 = (bf16[24,1152]{1,0:T(8,128)(2,1)S(1)}, bf16[24,1152]{1,0:T(8,128)(2,1)S(1)}, u32[]{:S(2)}, u32[]{:S(2)}) collective-permute-start(bf16[24,1152]{1,0:T(8,128)(2,1)S(1)} %get-tuple-element.60), channel_id=1, source_target_pairs={{0,2},{1,3},{2,0},{3,1},{4,6},{5,7},{6,4},{7,5},{8,10},{9,11},{10,... | collective-permute-start | bytes 165896 | tf_op jit(solution)/shard_map/ppermute | solution.py:234
  87.3 12.2 %collective-permute-start.15 = (bf16[24,1152]{1,0:T(8,128)(2,1)S(1)}, bf16[24,1152]{1,0:T(8,128)(2,1)S(1)}, u32[]{:S(2)}, u32[]{:S(2)}) collective-permute-start(bf16[24,1152]{1,0:T(8,128)(2,1)S(1)} %get-tuple-element.59), channel_id=1, source_target_pairs={{0,2},{1,3},{2,0},{3,1},{4,6},{5,7},{6,4},{7,5},{8,10},{9,11},{10,... | collective-permute-start | bytes 165896 | tf_op jit(solution)/shard_map/ppermute | solution.py:234
  102.2 3.8 %collective-permute-start.16 = (bf16[24,1152]{1,0:T(8,128)(2,1)S(1)}, bf16[24,1152]{1,0:T(8,128)(2,1)S(1)}, u32[]{:S(2)}, u32[]{:S(2)}) collective-permute-start(bf16[24,1152]{1,0:T(8,128)(2,1)S(1)} %get-tuple-element.54), channel_id=1, source_target_pairs={{0,3},{1,0},{2,1},{3,2},{4,7},{5,4},{6,5},{7,6},{8,11},{9,8},{10,9... | collective-permute-start | bytes 165896 | tf_op jit(solution)/shard_map/ppermute | solution.py:234
  102.9 3.6 %collective-permute-start.17 = (bf16[24,1152]{1,0:T(8,128)(2,1)S(1)}, bf16[24,1152]{1,0:T(8,128)(2,1)S(1)}, u32[]{:S(2)}, u32[]{:S(2)}) collective-permute-start(bf16[24,1152]{1,0:T(8,128)(2,1)S(1)} %get-tuple-element.57), channel_id=1, source_target_pairs={{0,1},{1,2},{2,3},{3,0},{4,5},{5,6},{6,7},{7,4},{8,9},{9,10},{10,1... | collective-permute-start | bytes 165896 | tf_op jit(solution)/shard_map/ppermute | solution.py:234
  102.9 4.7 %collective-permute-start.18 = (bf16[24,1152]{1,0:T(8,128)(2,1)S(1)}, bf16[24,1152]{1,0:T(8,128)(2,1)S(1)}, u32[]{:S(2)}, u32[]{:S(2)}) collective-permute-start(bf16[24,1152]{1,0:T(8,128)(2,1)S(1)} %get-tuple-element.56), channel_id=1, source_target_pairs={{0,2},{1,3},{2,0},{3,1},{4,6},{5,7},{6,4},{7,5},{8,10},{9,11},{10,... | collective-permute-start | bytes 165896 | tf_op jit(solution)/shard_map/ppermute | solution.py:234
  103.6 5.2 %collective-permute-start.19 = (bf16[24,1152]{1,0:T(8,128)(2,1)S(1)}, bf16[24,1152]{1,0:T(8,128)(2,1)S(1)}, u32[]{:S(2)}, u32[]{:S(2)}) collective-permute-start(bf16[24,1152]{1,0:T(8,128)(2,1)S(1)} %get-tuple-element.55), channel_id=1, source_target_pairs={{0,2},{1,3},{2,0},{3,1},{4,6},{5,7},{6,4},{7,5},{8,10},{9,11},{10,... | collective-permute-start | bytes 165896 | tf_op jit(solution)/shard_map/ppermute | solution.py:234
  105.3 3.5 %copy-start.7 = (bf16[192,1152]{1,0:T(8,128)(2,1)S(1)}, bf16[192,1152]{1,0:T(8,128)(2,1)}, u32[]{:S(2)}) copy-start(bf16[192,1152]{1,0:T(8,128)(2,1)} %shard_map.255) | copy-start | bytes 1327108

commit v17 on v16

--- a/solution.py
+++ b/solution.py
@@ -160,10 +160,8 @@
         moved_chips = moved.reshape(tokens, 2, 2 * rows).transpose(1, 0, 2)
 
         def chip_weight(same_core, other_core):
-            stack = jnp.zeros((2,) + w_qkv.shape, w_qkv.dtype)
-            stack = lax.dynamic_update_index_in_dim(stack, same_core, core, 0)
-            stack = lax.dynamic_update_index_in_dim(stack, other_core, 1 - core, 0)
-            return stack.reshape(2 * rows, w_qkv.shape[1])
+            tripled = jnp.concatenate([same_core, other_core, same_core], axis=0)
+            return lax.dynamic_slice_in_dim(tripled, core * rows, 2 * rows, axis=0)
 
         def chip_part(chip, weight):
             return jnp.dot(

time: 111 us -> 113 us (1.018)
  matrix products: 12.2 us -> 17.7 us
  local copies, waits for them, and re-layouts: 27.1 us -> 23 us
    dot_general x2, matrix products: 7.48 us -> 12.9 us  [chip_part(): jnp.dot(lax.dynamic_index_in_dim(moved_chips, chip, 0, keepdims=False), w...]
    dynamic_update_slice x4 -> x0, local copies, waits for them, and re-layouts: 4.68 us -> none  [the longest x2 2.34 us: chip_weight(): stack = lax.dynamic_update_index_in_dim(stack, same_core, core, 0)]
    ppermute x6, waiting for transfers between devices: 0.48 us -> 2.08 us  [fetch(): return lax.ppermute(x, 'face', [(src_of(i), i) for i in range(n)])]
    another operation x2 -> x0, local copies, waits for them, and re-layouts: 1.57 us -> none
    ppermute x1, waiting for transfers between devices: 1.25 us -> 0.03 us  [per_device(): upper = lax.ppermute(low, 'tm', [(i + 1, i) for i in range(count - 1)])]
    unnamed x45 -> x47, local copies, waits for them, and re-layouts: 4.71 us -> 4.62 us
  transfers between devices with their start and end apart: 20 -> 20, of which waited for: 8 -> 5; matrix products, arithmetic and copies ran while one was open for 38% -> 38% of each run, Pallas kernels for 16% -> 16%
where the time goes in v17:
time: 113 us; the launch traced here: 112 us
  Pallas kernels  35.2 us (31%)
  local copies, waits for them, and re-layouts  23 us (20%)
  starting transfers between devices  20 us (18%)
  matrix products  17.7 us (16%)
  other arithmetic  10 us (9%)
  waiting for transfers between devices  5.5 us (5%)
    pallas_call x3, Pallas kernels, attend_project(): pl.pallas_call(attention_kernel, grid=(1, heads // hb), in_specs=in_specs...  35.2 us
    dot_general x2, matrix products, chip_part(): jnp.dot(lax.dynamic_index_in_dim(moved_chips, chip, 0, keepdims=False), w...  12.9 us
    ppermute x12, starting transfers between devices, strips_in(): lax.ppermute(sent, 'face', [(i, (i + shift) % n) for i in range(n)])  9.77 us
    ppermute x6, starting transfers between devices, fetch(): return lax.ppermute(x, 'face', [(src_of(i), i) for i in range(n)])  5.27 us
    unnamed x47, local copies, waits for them, and re-layouts  4.62 us
    slice x3, local copies, waits for them, and re-layouts, per_device(): block_in[:rim]  4.06 us
    ppermute x1, starting transfers between devices, per_device(): lower = lax.ppermute(high, 'tm', [(i, i + 1) for i in range(count - 1)])  3.65 us
    ppermute x12, waiting for transfers between devices, strips_in(): lax.ppermute(sent, 'face', [(i, (i + shift) % n) for i in range(n)])  3.39 us
  transfers between devices with their start and end apart: 20, of which 5 were waited for; matrix products, arithmetic and copies ran while one was open for 38% of the time, Pallas kernels for 16%

profile of v17, /device:TPU:0, one launch (start us, length us, event | category | flops | bytes accessed | tf_op | source)
XLA Modules:
  0.0 111.9 jit_solution(13649696044489836686)
XLA Ops:
  0.0 0.5 collective-permute-start
  0.5 2.6 %collective-permute-start.1 = (bf16[288,1728]{1,0:T(8,128)(2,1)}, bf16[288,1728]{1,0:T(8,128)(2,1)}, u32[]{:S(2)}, u32[]{:S(2)}) collective-permute-start(bf16[288,1728]{1,0:T(8,128)(2,1)} %param.28), channel_id=1, source_target_pairs={{2,0},{3,1},{0,2},{1,3},{6,4},{7,5},{4,6},{5,7},{10,8},{11,9},{8,1... | collective-permute-start | bytes 2985992 | tf_op jit(solution)/shard_map/ppermute | solution.py:158
  3.0 2.5 %slice_bitcast_fusion.4 = (bf16[256,1152]{1,0:T(8,128)(2,1)S(1)}, bf16[256,1152]{1,0:T(8,128)(2,1)S(1)}, bf16[1,1,256,1152]{3,2,1,0:T(8,128)(2,1)}, bf16[1,1,256,1152]{3,2,1,0:T(8,128)(2,1)}) fusion(bf16[1,1,896,1152]{3,2,1,0:T(8,128)(2,1)} %param.26), kind=kLoop, calls=%fused_computation.106 | loop fusion | bytes 3538944 | tf_op jit(solution)/shard_map/slice | solution.py:150
  5.9 0.9 copy.63
  6.8 0.6 add_reduce_fusion
  8.0 0.4 convert_reduce_fusion
  8.4 0.6 fusion.1
  9.1 0.7 fusion.52
  10.0 2.5 %select_bitcast_fusion.1 = (f32[64]{0:T(128)S(1)}, f32[64]{0:T(128)S(1)}) fusion(pred[64,1]{0,1:T(4,128)(4,1)S(1)} %copy-done.14, f32[]{:T(128)} %bitcast.12, f32[]{:T(128)} %bitcast.11, f32[]{:T(128)} %bitcast.27, f32[]{:T(128)} %bitcast.26), kind=kLoop, calls=%fused_computation.101 | loop fusion | flops 128 | bytes 592 | tf_op jit(solution)/shard_map/mul | solution.py:251
  12.6 1.3 %copy.51 = bf16[1,1,256,1152]{2,3,1,0:T(8,128)(2,1)S(1)} copy(bf16[1,1,256,1152]{3,2,1,0:T(8,128)(2,1)} %get-tuple-element.44) | data formatting | bytes 1179648 | tf_op jit(solution)/shard_map/slice | solution.py:150
  13.9 1.3 %copy.50 = bf16[1,1,256,1152]{2,3,1,0:T(8,128)(2,1)S(1)} copy(bf16[1,1,256,1152]{3,2,1,0:T(8,128)(2,1)} %get-tuple-element.45) | data formatting | bytes 1179648 | tf_op jit(solution)/shard_map/slice | solution.py:150
  15.4 1.1 add_convert_fusion.1
  16.6 8.1 %fusion.14 = f32[896,1728]{0,1:T(8,128)} fusion(s32[]{:T(128)S(6)} %select_n.132, bf16[288,1728]{1,0:T(8,128)(2,1)S(1)} %copy-done.18, bf16[288,1728]{1,0:T(8,128)(2,1)} %collective-permute-done, bf16[896,2,576]{0,2,1:T(8,128)(2,1)S(1)} %add_convert_fusion.1, s32[]{:T(128)S(6)} %select_n.130), kind=kOutput, calls=%fused_computation.30 | convolution fusion | flops 1789599744 | bytes 9252872 | tf_op jit(solution)/shard_map/dot_general | solution.py:167
  24.7 2.0 %collective-permute-done.1 = bf16[288,1728]{1,0:T(8,128)(2,1)} collective-permute-done((bf16[288,1728]{1,0:T(8,128)(2,1)}, bf16[288,1728]{1,0:T(8,128)(2,1)}, u32[]{:S(2)}, u32[]{:S(2)}) %collective-permute-start.1) | collective-permute-done | bytes 995360 | tf_op jit(solution)/shard_map/ppermute | solution.py:158
  27.5 1.1 pad_maximum_fusion.1.refs_8_
  28.7 1.0 slice_bitcast_fusion.1
  29.7 0.4 collective-permute-start.3
  30.2 1.7 %collective-permute-start.4 = (bf16[576,288]{0,1:T(8,128)(2,1)}, bf16[576,288]{0,1:T(8,128)(2,1)}, u32[]{:S(2)}, u32[]{:S(2)}) collective-permute-start(bf16[576,288]{0,1:T(8,128)(2,1)} %param.29), channel_id=1, source_target_pairs={{2,0},{3,1},{0,2},{1,3},{6,4},{7,5},{4,6},{5,7},{10,8},{11,9},{8,1... | collective-permute-start | bytes 995336 | tf_op jit(solution)/shard_map/ppermute | solution.py:104
  31.9 4.8 %fusion.10 = f32[896,1728]{0,1:T(8,128)S(1)} fusion(s32[]{:T(128)S(6)} %select_n.132, bf16[288,1728]{1,0:T(8,128)(2,1)} %collective-permute-done.1, bf16[288,1728]{1,0:T(8,128)(2,1)} %collective-permute-done.2, bf16[896,2,576]{0,2,1:T(8,128)(2,1)S(1)} %copy-done.4, s32[]{:T(128)S(6)} %select_n.133), kind=kOutput, calls=%fused_computation.27 | convolution fusion | flops 1789599744 | bytes 9216008 | tf_op jit(solution)/shard_map/dot_general | solution.py:167
  36.7 0.8 add_convert_fusion
  37.6 1.6 %fusion.46 = (bf16[896,1,8,72]{0,3,2,1:T(8,128)(2,1)S(1)}, bf16[896,1,8,72]{0,3,2,1:T(8,128)(2,1)}, bf16[8,72,896]{2,1,0:T(8,128)(2,1)}) fusion(bf16[896,3,8,72]{0,3,2,1:T(8,128)(2,1)S(1)} %bitcast.66), kind=kLoop, calls=%fused_computation.107 | loop fusion | bytes 6193152 | tf_op jit(solution)/shard_map/slice | solution.py:198
  39.1 1.9 %copy.64 = bf16[896,1,8,72]{3,0,2,1:T(8,128)(2,1)S(1)} copy(bf16[896,1,8,72]{0,3,2,1:T(8,128)(2,1)} %get-tuple-element.38) | data formatting | bytes 2064384
  41.1 1.1 slice.170.refs_0_.refs_4_
  42.1 1.7 %copy.65 = bf16[896,1,8,72]{3,0,2,1:T(8,128)(2,1)} copy(bf16[896,1,8,72]{0,3,2,1:T(8,128)(2,1)S(1)} %get-tuple-element.37) | data formatting | bytes 2064384
  43.9 1.0 bitcast_dynamic-update-slice_fusion.3
  45.0 1.0 bitcast_dynamic-update-slice_fusion.2
  46.1 1.0 bitcast_dynamic-update-slice_fusion.1
  47.2 1.8 %copy.57.refs_3_.refs_7_ = bf16[576,1152]{1,0:T(8,128)(2,1)} copy(bf16[576,1152]{0,1:T(8,128)(2,1)S(1)} %bitcast.71) | data formatting | bytes 2654208 | tf_op jit(solution)/shard_map/reshape | solution.py:193
  49.0 17.1 %shard_map.253 = bf16[512,1152]{1,0:T(8,128)(2,1)} custom-call(bf16[8,512,72]{2,1,0:T(8,128)(2,1)} %slice.170.refs_0_.refs_4_, bf16[8,72,896]{2,1,0:T(8,128)(2,1)} %get-tuple-element.39.refs_1_.refs_5_, bf16[8,896,72]{2,1,0:T(8,128)(2,1)} %bitcast.57, bf16[576,1152]{1,0:T(8,128)(2,1)} %copy.57.refs_3_.refs_7_, bf16[8,512,72]{2,1,0:T(8,128)(2,1)} %slice.170.refs_0_.refs_4_, ...), custom_call_target="tpu_custom_call" | custom-call | tf_op jit(solution)/shard_map/pallas_call | solution.py:88
  66.1 1.8 %convolution_convert_fusion = bf16[256,1152]{1,0:T(8,128)(2,1)S(1)} fusion(bf16[512,1152]{1,0:T(8,128)(2,1)} %shard_map.253, s32[256]{0:T(256)S(1)} %eq.138), kind=kOutput, calls=%fused_computation.21 | convolution fusion | flops 302415872 | bytes 1770496 | tf_op jit(solution)/shard_map/dot_general | solution.py:223
  67.9 0.7 collective-permute-start.9
  68.7 1.4 %collective-permute-start.8 = (bf16[64,1152]{1,0:T(8,128)(2,1)S(1)}, bf16[64,1152]{1,0:T(8,128)(2,1)S(1)}, u32[]{:S(2)}, u32[]{:S(2)}) collective-permute-start(bf16[64,1152]{1,0:T(8,128)(2,1)S(1)} %get-tuple-element.52), channel_id=1, source_target_pairs={{0,2},{1,3},{2,0},{3,1},{4,6},{5,7},{6,4},{7,5},{8,10},{9,11},{10,... | collective-permute-start | bytes 442376 | tf_op jit(solution)/shard_map/ppermute | solution.py:232
  70.0 1.7 %collective-permute-start.6 = (bf16[64,1152]{1,0:T(8,128)(2,1)S(1)}, bf16[64,1152]{1,0:T(8,128)(2,1)S(1)}, u32[]{:S(2)}, u32[]{:S(2)}) collective-permute-start(bf16[64,1152]{1,0:T(8,128)(2,1)S(1)} %get-tuple-element.50), channel_id=1, source_target_pairs={{0,3},{1,0},{2,1},{3,2},{4,7},{5,4},{6,5},{7,6},{8,11},{9,8},{10,9... | collective-permute-start | bytes 442376 | tf_op jit(solution)/shard_map/ppermute | solution.py:232
  71.8 1.0 fusion.47
  72.8 9.1 %shard_map.254 = bf16[192,1152]{1,0:T(8,128)(2,1)} custom-call(bf16[8,192,72]{2,1,0:T(8,128)(2,1)} %get-tuple-element.23.refs_0_.refs_4_, bf16[8,72,896]{2,1,0:T(8,128)(2,1)} %get-tuple-element.39.refs_1_.refs_5_, bf16[8,896,72]{2,1,0:T(8,128)(2,1)} %bitcast.59, bf16[576,1152]{1,0:T(8,128)(2,1)} %copy.57.refs_3_.refs_7_, ...), custom_call_target="tpu_custom_call" | custom-call | tf_op jit(solution)/shard_map/pallas_call | solution.py:88
  82.0 0.7 fusion.4
  82.8 3.6 %collective-permute-start.10 = (bf16[256,1152]{1,0:T(8,128)(2,1)S(1)}, bf16[256,1152]{1,0:T(8,128)(2,1)S(1)}, u32[]{:S(2)}, u32[]{:S(2)}) collective-permute-start(bf16[256,1152]{1,0:T(8,128)(2,1)S(1)} %get-tuple-element.33), channel_id=1, source_target_pairs={{0,4},{4,8},{8,12},{1,5},{5,9},{9,13},{2,6},{6,10},{10,14},{3,7},{... | collective-permute-start | bytes 1769480 | tf_op jit(solution)/shard_map/ppermute | solution.py:265
  86.5 1.3 %collective-permute-start.11 = (bf16[256,1152]{1,0:T(8,128)(2,1)S(1)}, bf16[256,1152]{1,0:T(8,128)(2,1)S(1)}, u32[]{:S(2)}, u32[]{:S(2)}) collective-permute-start(bf16[256,1152]{1,0:T(8,128)(2,1)S(1)} %get-tuple-element.28), channel_id=1, source_target_pairs={{4,0},{8,4},{12,8},{5,1},{9,5},{13,9},{6,2},{10,6},{14,10},{7,3},{... | collective-permute-start | bytes 1769480 | tf_op jit(solution)/shard_map/ppermute | solution.py:266
  88.1 1.0 collective-permute-start.15
  89.1 1.1 collective-permute-start.14
  90.2 2.1 %collective-permute-done.15 = bf16[24,1152]{1,0:T(8,128)(2,1)S(1)} collective-permute-done((bf16[24,1152]{1,0:T(8,128)(2,1)S(1)}, bf16[24,1152]{1,0:T(8,128)(2,1)S(1)}, u32[]{:S(2)}, u32[]{:S(2)}) %collective-permute-start.15) | collective-permute-done | bytes 55328 | tf_op jit(solution)/shard_map/ppermute | solution.py:232
  93.6 9.0 %shard_map.255 = bf16[192,1152]{1,0:T(8,128)(2,1)} custom-call(bf16[8,192,72]{2,1,0:T(8,128)(2,1)} %get-tuple-element.29.refs_0_.refs_4_, bf16[8,72,896]{2,1,0:T(8,128)(2,1)} %get-tuple-element.39.refs_1_.refs_5_, bf16[8,896,72]{2,1,0:T(8,128)(2,1)} %bitcast.61, bf16[576,1152]{1,0:T(8,128)(2,1)} %copy.57.refs_3_.refs_7_, ...), custom_call_target="tpu_custom_call" | custom-call | tf_op jit(solution)/shard_map/pallas_call | solution.py:88
  102.7 1.3 %convolution_convert_fusion.1 = bf16[96,1152]{1,0:T(8,128)(2,1)S(1)} fusion(bf16[192,1152]{1,0:T(8,128)(2,1)} %shard_map.255, s32[96]{0:T(128)S(1)} %eq.142), kind=kOutput, calls=%fused_computation.23 | convolution fusion | flops 42596352 | bytes 663936 | tf_op jit(solution)/shard_map/dot_general | solution.py:223
  104.0 1.1 %collective-permute-start.19 = (bf16[24,1152]{1,0:T(8,128)(2,1)S(1)}, bf16[24,1152]{1,0:T(8,128)(2,1)S(1)}, u32[]{:S(2)}, u32[]{:S(2)}) collective-permute-start(bf16[24,1152]{1,0:T(8,128)(2,1)S(1)} %get-tuple-element.55), channel_id=1, source_target_pairs={{0,2},{1,3},{2,0},{3,1},{4,6},{5,7},{6,4},{7,5},{8,10},{9,11},{10,... | collective-permute-start | bytes 165896 | tf_op jit(solution)/shard_map/ppermute | solution.py:232
  105.1 1.0 collective-permute-start.18
  106.1 1.7 %collective-permute-start.16 = (bf16[24,1152]{1,0:T(8,128)(2,1)S(1)}, bf16[24,1152]{1,0:T(8,128)(2,1)S(1)}, u32[]{:S(2)}, u32[]{:S(2)}) collective-permute-start(bf16[24,1152]{1,0:T(8,128)(2,1)S(1)} %get-tuple-element.54), channel_id=1, source_target_pairs={{0,3},{1,0},{2,1},{3,2},{4,7},{5,4},{6,5},{7,6},{8,11},{9,8},{10,9... | collective-permute-start | bytes 165896 | tf_op jit(solution)/shard_map/ppermute | solution.py:232
  108.9 1.0 collective-permute-done.18
  110.5 1.5 %maximum_bitcast_fusion = bf16[1,1,896,1152]{3,2,1,0:T(8,128)(2,1)} fusion(bf16[256,1152]{1,0:T(8,128)(2,1)S(1)} %fusion.19, bf16[192,1152]{1,0:T(8,128)(2,1)S(1)} %fusion.25, bf16[192,1152]{1,0:T(8,128)(2,1)S(1)} %fusion.7, bf16[256,1152]{1,0:T(8,128)(2,1)S(1)} %fusion.17), kind=kLoop, calls=%fused_computation.32 | loop fusion | flops 8257536 | bytes 4128768 | tf_op jit(solution)/shard_map/reshape | solution.py:306
  (130 shorter events, 6.1 us)
Async XLA Ops:
  0.0 5.5 %copy-start = (s32[4,4,4]{2,1,0:T(4,128)S(1)}, s32[4,4,4]{2,1,0:T(4,128)}, u32[]{:S(2)}) copy-start(s32[4,4,4]{2,1,0:T(4,128)} %param.30) | copy-start | bytes 772
  0.0 16.5 %collective-permute-start = (bf16[288,1728]{1,0:T(8,128)(2,1)}, bf16[288,1728]{1,0:T(8,128)(2,1)}, u32[]{:S(2)}, u32[]{:S(2)}) collective-permute-start(bf16[288,1728]{1,0:T(8,128)(2,1)} %param.28), channel_id=1, source_target_pairs={{1,0},{0,1},{3,2},{2,3},{5,4},{4,5},{7,6},{6,7},{9,8},{8,9},{11,10... | collective-permute-start | bytes 2985992 | tf_op jit(solution)/shard_map/ppermute | solution.py:158
  0.5 26.3 %collective-permute-start.1 = (bf16[288,1728]{1,0:T(8,128)(2,1)}, bf16[288,1728]{1,0:T(8,128)(2,1)}, u32[]{:S(2)}, u32[]{:S(2)}) collective-permute-start(bf16[288,1728]{1,0:T(8,128)(2,1)} %param.28), channel_id=1, source_target_pairs={{2,0},{3,1},{0,2},{1,3},{6,4},{7,5},{4,6},{5,7},{10,8},{11,9},{8,1... | collective-permute-start | bytes 2985992 | tf_op jit(solution)/shard_map/ppermute | solution.py:158
  3.0 2.9 %slice-start.2 = ((bf16[1,1,896,1152]{3,2,1,0:T(8,128)(2,1)}), bf16[1,1,384,1152]{3,2,1,0:T(8,128)(2,1)S(1)}, s32[]{:S(2)}) async-start(bf16[1,1,896,1152]{3,2,1,0:T(8,128)(2,1)} %param.26), calls=%async_computation.2 | async-start | bytes 1769472 | tf_op jit(solution)/shard_map/slice | solution.py:150
  3.0 3.8 %copy-start.7 = (f32[3,1152]{1,0:T(4,128)S(1)}, f32[3,1152]{1,0:T(4,128)}, u32[]{:S(2)}) copy-start(f32[3,1152]{1,0:T(4,128)} %param.27) | copy-start | bytes 41476
  7.9 1.1 copy-start.15
  7.9 1.8 %copy-start.11 = (s32[4,64]{1,0:T(4,128)S(1)}, s32[4,64]{1,0:T(4,128)}, u32[]{:S(2)}) copy-start(s32[4,64]{1,0:T(4,128)} %constant.107.clone) | copy-start | bytes 3076
  7.9 1.8 %copy-start.12 = (s32[4,64]{1,0:T(4,128)S(1)}, s32[4,64]{1,0:T(4,128)}, u32[]{:S(2)}) copy-start(s32[4,64]{1,0:T(4,128)} %constant.108.clone) | copy-start | bytes 3076
  7.9 1.9 %copy-start.9 = (s32[4,24]{1,0:T(4,128)S(1)}, s32[4,24]{1,0:T(4,128)}, u32[]{:S(2)}) copy-start(s32[4,24]{1,0:T(4,128)} %constant.112.clone) | copy-start | bytes 1156
  8.0 1.9 %copy-start.10 = (s32[4,24]{1,0:T(4,128)S(1)}, s32[4,24]{1,0:T(4,128)}, u32[]{:S(2)}) copy-start(s32[4,24]{1,0:T(4,128)} %constant.113.clone) | copy-start | bytes 1156
  8.0 1.9 %copy-start.17 = (s32[4]{0:T(128)S(1)}, s32[4]{0:T(128)}, u32[]{:S(2)}) copy-start(s32[4]{0:T(128)} %constant.106.clone) | copy-start | bytes 52
  8.0 2.0 %copy-start.14 = (pred[64,1]{0,1:T(4,128)(4,1)S(1)}, pred[64,1]{0,1:T(4,128)(4,1)}, u32[]{:S(2)}) copy-start(pred[64,1]{0,1:T(4,128)(4,1)} %constant.110.clone) | copy-start | bytes 196
  15.4 1.2 %copy-start.18 = (bf16[288,1728]{1,0:T(8,128)(2,1)S(1)}, bf16[288,1728]{1,0:T(8,128)(2,1)}, u32[]{:S(2)}) copy-start(bf16[288,1728]{1,0:T(8,128)(2,1)} %param.28) | copy-start | bytes 2985988
  16.5 8.2 %copy-start.3 = (bf16[896,2,576]{0,2,1:T(8,128)(2,1)}, bf16[896,2,576]{0,2,1:T(8,128)(2,1)S(1)}, u32[]{:S(2)}) copy-start(bf16[896,2,576]{0,2,1:T(8,128)(2,1)S(1)} %add_convert_fusion.1) | copy-start | bytes 6193156
  16.5 10.2 %copy-start.13 = (s32[4,64]{1,0:T(4,128)S(1)}, s32[4,64]{1,0:T(4,128)}, u32[]{:S(2)}) copy-start(s32[4,64]{1,0:T(4,128)} %constant.118) | copy-start | bytes 3076
  16.5 10.6 %copy-start.19 = (pred[64]{0:T(512)(128)(4,1)S(1)}, pred[64]{0:T(512)(128)(4,1)}, u32[]{:S(2)}) copy-start(pred[64]{0:T(512)(128)(4,1)} %constant.117) | copy-start | bytes 196
  16.5 10.9 %copy-start.16 = (s32[4]{0:T(128)S(1)}, s32[4]{0:T(128)}, u32[]{:S(2)}) copy-start(s32[4]{0:T(128)} %param.32) | copy-start | bytes 52
  24.7 3.9 %copy-start.2 = (bf16[1,1,896,1152]{3,2,1,0:T(8,128)(2,1)S(1)}, bf16[1,1,896,1152]{3,2,1,0:T(8,128)(2,1)}, u32[]{:S(2)}) copy-start(bf16[1,1,896,1152]{3,2,1,0:T(8,128)(2,1)} %param.26) | copy-start | bytes 6193156
  26.7 3.0 %collective-permute-start.2 = (bf16[288,1728]{1,0:T(8,128)(2,1)}, bf16[288,1728]{1,0:T(8,128)(2,1)}, u32[]{:S(2)}, u32[]{:S(2)}) collective-permute-start(bf16[288,1728]{1,0:T(8,128)(2,1)} %collective-permute-done.1), channel_id=1, source_target_pairs={{1,0},{0,1},{3,2},{2,3},{5,4},{4,5},{7,6},{6,7},{9,8},{8,9},{11,10... | collective-permute-start | bytes 2985992 | tf_op jit(solution)/shard_map/ppermute | solution.py:158
  27.5 4.4 %copy-start.4 = (bf16[896,2,576]{0,2,1:T(8,128)(2,1)S(1)}, bf16[896,2,576]{0,2,1:T(8,128)(2,1)}, u32[]{:S(2)}) copy-start(bf16[896,2,576]{0,2,1:T(8,128)(2,1)} %copy-done.3) | copy-start | bytes 6193156
  28.6 8.1 %slice-start = ((s8[6193152]{0:T(1024)(128)(4,1)}), s8[4194304]{0:T(1024)(128)(4,1)S(1)}, s32[]{:S(2)}) async-start(s8[6193152]{0:T(1024)(128)(4,1)} %bitcast.69), calls=%async_computation | async-start | bytes 8388608
  29.7 7.1 %slice-start.1 = ((s8[6193152]{0:T(1024)(128)(4,1)}), s8[1998848]{0:T(1024)(128)(4,1)S(1)}, s32[]{:S(2)}) async-start(s8[6193152]{0:T(1024)(128)(4,1)} %bitcast.69), calls=%async_computation.1 | async-start | bytes 3997696
  29.7 15.3 %collective-permute-start.3 = (bf16[576,288]{0,1:T(8,128)(2,1)}, bf16[576,288]{0,1:T(8,128)(2,1)}, u32[]{:S(2)}, u32[]{:S(2)}) collective-permute-start(bf16[576,288]{0,1:T(8,128)(2,1)} %param.29), channel_id=1, source_target_pairs={{1,0},{0,1},{3,2},{2,3},{5,4},{4,5},{7,6},{6,7},{9,8},{8,9},{11,10... | collective-permute-start | bytes 995336 | tf_op jit(solution)/shard_map/ppermute | solution.py:104
  30.2 14.8 %collective-permute-start.4 = (bf16[576,288]{0,1:T(8,128)(2,1)}, bf16[576,288]{0,1:T(8,128)(2,1)}, u32[]{:S(2)}, u32[]{:S(2)}) collective-permute-start(bf16[576,288]{0,1:T(8,128)(2,1)} %param.29), channel_id=1, source_target_pairs={{2,0},{3,1},{0,2},{1,3},{6,4},{7,5},{4,6},{5,7},{10,8},{11,9},{8,1... | collective-permute-start | bytes 995336 | tf_op jit(solution)/shard_map/ppermute | solution.py:104
  44.9 2.2 %collective-permute-start.5 = (bf16[576,288]{0,1:T(8,128)(2,1)}, bf16[576,288]{0,1:T(8,128)(2,1)S(1)}, u32[]{:S(2)}, u32[]{:S(2)}) collective-permute-start(bf16[576,288]{0,1:T(8,128)(2,1)} %collective-permute-done.4), channel_id=1, source_target_pairs={{1,0},{0,1},{3,2},{2,3},{5,4},{4,5},{7,6},{6,7},{9,8},{8,9},{11,10... | collective-permute-start | bytes 995336 | tf_op jit(solution)/shard_map/ppermute | solution.py:104
  67.9 13.9 %collective-permute-start.9 = (bf16[64,1152]{1,0:T(8,128)(2,1)S(1)}, bf16[64,1152]{1,0:T(8,128)(2,1)S(1)}, u32[]{:S(2)}, u32[]{:S(2)}) collective-permute-start(bf16[64,1152]{1,0:T(8,128)(2,1)S(1)} %get-tuple-element.51), channel_id=1, source_target_pairs={{0,2},{1,3},{2,0},{3,1},{4,6},{5,7},{6,4},{7,5},{8,10},{9,11},{10,... | collective-permute-start | bytes 442376 | tf_op jit(solution)/shard_map/ppermute | solution.py:232
  68.7 13.2 %collective-permute-start.8 = (bf16[64,1152]{1,0:T(8,128)(2,1)S(1)}, bf16[64,1152]{1,0:T(8,128)(2,1)S(1)}, u32[]{:S(2)}, u32[]{:S(2)}) collective-permute-start(bf16[64,1152]{1,0:T(8,128)(2,1)S(1)} %get-tuple-element.52), channel_id=1, source_target_pairs={{0,2},{1,3},{2,0},{3,1},{4,6},{5,7},{6,4},{7,5},{8,10},{9,11},{10,... | collective-permute-start | bytes 442376 | tf_op jit(solution)/shard_map/ppermute | solution.py:232
  70.0 11.9 %collective-permute-start.7 = (bf16[64,1152]{1,0:T(8,128)(2,1)S(1)}, bf16[64,1152]{1,0:T(8,128)(2,1)S(1)}, u32[]{:S(2)}, u32[]{:S(2)}) collective-permute-start(bf16[64,1152]{1,0:T(8,128)(2,1)S(1)} %get-tuple-element.53), channel_id=1, source_target_pairs={{0,1},{1,2},{2,3},{3,0},{4,5},{5,6},{6,7},{7,4},{8,9},{9,10},{10,1... | collective-permute-start | bytes 442376 | tf_op jit(solution)/shard_map/ppermute | solution.py:232
  70.0 11.9 %collective-permute-start.6 = (bf16[64,1152]{1,0:T(8,128)(2,1)S(1)}, bf16[64,1152]{1,0:T(8,128)(2,1)S(1)}, u32[]{:S(2)}, u32[]{:S(2)}) collective-permute-start(bf16[64,1152]{1,0:T(8,128)(2,1)S(1)} %get-tuple-element.50), channel_id=1, source_target_pairs={{0,3},{1,0},{2,1},{3,2},{4,7},{5,4},{6,5},{7,6},{8,11},{9,8},{10,9... | collective-permute-start | bytes 442376 | tf_op jit(solution)/shard_map/ppermute | solution.py:232
  72.8 9.2 %copy-start.1 = (bf16[512,1152]{1,0:T(8,128)(2,1)S(1)}, bf16[512,1152]{1,0:T(8,128)(2,1)}, u32[]{:S(2)}) copy-start(bf16[512,1152]{1,0:T(8,128)(2,1)} %shard_map.253) | copy-start | bytes 3538948
  82.7 5.1 %copy-start.5 = (bf16[192,1152]{1,0:T(8,128)(2,1)S(1)}, bf16[192,1152]{1,0:T(8,128)(2,1)}, u32[]{:S(2)}) copy-start(bf16[192,1152]{1,0:T(8,128)(2,1)} %shard_map.254) | copy-start | bytes 1327108
  82.7 9.6 %copy-start.8 = (s32[4,24]{1,0:T(4,128)S(1)}, s32[4,24]{1,0:T(4,128)}, u32[]{:S(2)}) copy-start(s32[4,24]{1,0:T(4,128)} %constant.119) | copy-start | bytes 1156
  82.8 19.8 %collective-permute-start.10 = (bf16[256,1152]{1,0:T(8,128)(2,1)S(1)}, bf16[256,1152]{1,0:T(8,128)(2,1)S(1)}, u32[]{:S(2)}, u32[]{:S(2)}) collective-permute-start(bf16[256,1152]{1,0:T(8,128)(2,1)S(1)} %get-tuple-element.33), channel_id=1, source_target_pairs={{0,4},{4,8},{8,12},{1,5},{5,9},{9,13},{2,6},{6,10},{10,14},{3,7},{... | collective-permute-start | bytes 1769480 | tf_op jit(solution)/shard_map/ppermute | solution.py:265
  86.5 16.2 %collective-permute-start.11 = (bf16[256,1152]{1,0:T(8,128)(2,1)S(1)}, bf16[256,1152]{1,0:T(8,128)(2,1)S(1)}, u32[]{:S(2)}, u32[]{:S(2)}) collective-permute-start(bf16[256,1152]{1,0:T(8,128)(2,1)S(1)} %get-tuple-element.28), channel_id=1, source_target_pairs={{4,0},{8,4},{12,8},{5,1},{9,5},{13,9},{6,2},{10,6},{14,10},{7,3},{... | collective-permute-start | bytes 1769480 | tf_op jit(solution)/shard_map/ppermute | solution.py:266
  88.1 4.2 %collective-permute-start.15 = (bf16[24,1152]{1,0:T(8,128)(2,1)S(1)}, bf16[24,1152]{1,0:T(8,128)(2,1)S(1)}, u32[]{:S(2)}, u32[]{:S(2)}) collective-permute-start(bf16[24,1152]{1,0:T(8,128)(2,1)S(1)} %get-tuple-element.59), channel_id=1, source_target_pairs={{0,2},{1,3},{2,0},{3,1},{4,6},{5,7},{6,4},{7,5},{8,10},{9,11},{10,... | collective-permute-start | bytes 165896 | tf_op jit(solution)/shard_map/ppermute | solution.py:232
  89.1 13.4 %collective-permute-start.14 = (bf16[24,1152]{1,0:T(8,128)(2,1)S(1)}, bf16[24,1152]{1,0:T(8,128)(2,1)S(1)}, u32[]{:S(2)}, u32[]{:S(2)}) collective-permute-start(bf16[24,1152]{1,0:T(8,128)(2,1)S(1)} %get-tuple-element.60), channel_id=1, source_target_pairs={{0,2},{1,3},{2,0},{3,1},{4,6},{5,7},{6,4},{7,5},{8,10},{9,11},{10,... | collective-permute-start | bytes 165896 | tf_op jit(solution)/shard_map/ppermute | solution.py:232
  90.2 12.4 %collective-permute-start.13 = (bf16[24,1152]{1,0:T(8,128)(2,1)S(1)}, bf16[24,1152]{1,0:T(8,128)(2,1)S(1)}, u32[]{:S(2)}, u32[]{:S(2)}) collective-permute-start(bf16[24,1152]{1,0:T(8,128)(2,1)S(1)} %get-tuple-element.61), channel_id=1, source_target_pairs={{0,1},{1,2},{2,3},{3,0},{4,5},{5,6},{6,7},{7,4},{8,9},{9,10},{10,1... | collective-permute-start | bytes 165896 | tf_op jit(solution)/shard_map/ppermute | solution.py:232
  92.3 10.3 %collective-permute-start.12 = (bf16[24,1152]{1,0:T(8,128)(2,1)S(1)}, bf16[24,1152]{1,0:T(8,128)(2,1)S(1)}, u32[]{:S(2)}, u32[]{:S(2)}) collective-permute-start(bf16[24,1152]{1,0:T(8,128)(2,1)S(1)} %get-tuple-element.58), channel_id=1, source_target_pairs={{0,3},{1,0},{2,1},{3,2},{4,7},{5,4},{6,5},{7,6},{8,11},{9,8},{10,9... | collective-permute-start | bytes 165896 | tf_op jit(solution)/shard_map/ppermute | solution.py:232
  104.0 4.9 %collective-permute-start.19 = (bf16[24,1152]{1,0:T(8,128)(2,1)S(1)}, bf16[24,1152]{1,0:T(8,128)(2,1)S(1)}, u32[]{:S(2)}, u32[]{:S(2)}) collective-permute-start(bf16[24,1152]{1,0:T(8,128)(2,1)S(1)} %get-tuple-element.55), channel_id=1, source_target_pairs={{0,2},{1,3},{2,0},{3,1},{4,6},{5,7},{6,4},{7,5},{8,10},{9,11},{10,... | collective-permute-start | bytes 165896 | tf_op jit(solution)/shard_map/ppermute | solution.py:232
  105.1 4.8 %collective-permute-start.18 = (bf16[24,1152]{1,0:T(8,128)(2,1)S(1)}, bf16[24,1152]{1,0:T(8,128)(2,1)S(1)}, u32[]{:S(2)}, u32[]{:S(2)}) collective-permute-start(bf16[24,1152]{1,0:T(8,128)(2,1)S(1)} %get-tuple-element.56), channel_id=1, source_target_pairs={{0,2},{1,3},{2,0},{3,1},{4,6},{5,7},{6,4},{7,5},{8,10},{9,11},{10,... | collective-permute-start | bytes 165896 | tf_op jit(solution)/shard_map/ppermute | solution.py:232
  106.1 4.0 %collective-permute-start.17 = (bf16[24,1152]{1,0:T(8,128)(2,1)S(1)}, bf16[24,1152]{1,0:T(8,128)(2,1)S(1)}, u32[]{:S(2)}, u32[]{:S(2)}) collective-permute-start(bf16[24,1152]{1,0:T(8,128)(2,1)S(1)} %get-tuple-element.57), channel_id=1, source_target_pairs={{0,1},{1,2},{2,3},{3,0},{4,5},{5,6},{6,7},{7,4},{8,9},{9,10},{10,1... | collective-permute-start | bytes 165896 | tf_op jit(solution)/shard_map/ppermute | solution.py:232
  106.1 4.0 %collective-permute-start.16 = (bf16[24,1152]{1,0:T(8,128)(2,1)S(1)}, bf16[24,1152]{1,0:T(8,128)(2,1)S(1)}, u32[]{:S(2)}, u32[]{:S(2)}) collective-permute-start(bf16[24,1152]{1,0:T(8,128)(2,1)S(1)} %get-tuple-element.54), channel_id=1, source_target_pairs={{0,3},{1,0},{2,1},{3,2},{4,7},{5,4},{6,5},{7,6},{8,11},{9,8},{10,9... | collective-permute-start | bytes 165896 | tf_op jit(solution)/shard_map/ppermute | solution.py:232
  108.1 2.0 %copy-start.6 = (bf16[192,1152]{1,0:T(8,128)(2,1)S(1)}, bf16[192,1152]{1,0:T(8,128)(2,1)}, u32[]{:S(2)}) copy-start(bf16[192,1152]{1,0:T(8,128)(2,1)} %shard_map.255) | copy-start | bytes 1327108

commit v18 on v16

--- a/solution.py
+++ b/solution.py
@@ -30,7 +30,7 @@
     return (normed * (1.0 + modulation[1]) + modulation[0]).astype(jnp.bfloat16)
 
 
-HEADS_PER_STEP = 2
+HEADS_PER_STEP = 4
 
 
 def attention_kernel(*refs):

time: 111 us -> 111 us (level)
  no operation moved by 1% of the time
where the time goes in v18:
time: 111 us; the launch traced here: 110 us
  Pallas kernels  34.8 us (31%)
  local copies, waits for them, and re-layouts  27.1 us (24%)
  starting transfers between devices  19.9 us (18%)
  matrix products  12.2 us (11%)
  other arithmetic  10.8 us (10%)
  waiting for transfers between devices  4.97 us (4%)
    pallas_call x3, Pallas kernels, attend_project(): pl.pallas_call(attention_kernel, grid=(1, heads // hb), in_specs=in_specs...  34.8 us
    ppermute x12, starting transfers between devices, strips_in(): lax.ppermute(sent, 'face', [(i, (i + shift) % n) for i in range(n)])  9.51 us
    dot_general x2, matrix products, chip_part(): jnp.dot(lax.dynamic_index_in_dim(moved_chips, chip, 0, keepdims=False), w...  7.48 us
    ppermute x6, starting transfers between devices, fetch(): return lax.ppermute(x, 'face', [(src_of(i), i) for i in range(n)])  5.13 us
    unnamed x45, local copies, waits for them, and re-layouts  4.71 us
    ppermute x1, starting transfers between devices, per_device(): lower = lax.ppermute(high, 'tm', [(i, i + 1) for i in range(count - 1)])  3.92 us
    dot_general x3, matrix products, strips_out(): jnp.dot(pick, tile_out, preferred_element_type=jnp.float32)  3.37 us
    ppermute x12, waiting for transfers between devices, strips_in(): lax.ppermute(sent, 'face', [(i, (i + shift) % n) for i in range(n)])  3.25 us
  transfers between devices with their start and end apart: 20, of which 8 were waited for; matrix products, arithmetic and copies ran while one was open for 38% of the time, Pallas kernels for 16%

profile of v18, /device:TPU:0, one launch (start us, length us, event | category | flops | bytes accessed | tf_op | source)
XLA Modules:
  0.0 110.4 jit_solution(7201643387057117506)
XLA Ops:
  0.0 0.5 collective-permute-start
  0.5 2.6 %collective-permute-start.1 = (bf16[288,1728]{1,0:T(8,128)(2,1)}, bf16[288,1728]{1,0:T(8,128)(2,1)}, u32[]{:S(2)}, u32[]{:S(2)}) collective-permute-start(bf16[288,1728]{1,0:T(8,128)(2,1)} %param.28), channel_id=1, source_target_pairs={{2,0},{3,1},{0,2},{1,3},{6,4},{7,5},{4,6},{5,7},{10,8},{11,9},{8,1... | collective-permute-start | bytes 2985992 | tf_op jit(solution)/shard_map/ppermute | solution.py:158
  3.0 2.4 %slice_bitcast_fusion.4 = (bf16[256,1152]{1,0:T(8,128)(2,1)S(1)}, bf16[256,1152]{1,0:T(8,128)(2,1)S(1)}, bf16[1,1,256,1152]{3,2,1,0:T(8,128)(2,1)}, bf16[1,1,256,1152]{3,2,1,0:T(8,128)(2,1)}) fusion(bf16[1,1,896,1152]{3,2,1,0:T(8,128)(2,1)} %param.26), kind=kLoop, calls=%fused_computation.98 | loop fusion | bytes 3538944 | tf_op jit(solution)/shard_map/slice | solution.py:150
  6.0 1.1 %pad_maximum_fusion.1.refs_16_ = bf16[512,1152]{1,0:T(8,128)(2,1)} fusion(bf16[256,1152]{1,0:T(8,128)(2,1)S(1)} %get-tuple-element.43, bf16[256,1152]{1,0:T(8,128)(2,1)S(1)} %get-tuple-element.42), kind=kLoop, calls=%fused_computation.29 | loop fusion | flops 2359296 | bytes 2359296 | tf_op jit(solution)/shard_map/concatenate | solution.py:149
  7.5 0.9 copy.81
  8.8 0.6 fusion.1
  9.5 0.6 add_reduce_fusion
  10.3 0.7 fusion.44
  11.1 2.6 %select_bitcast_fusion.1 = (f32[64]{0:T(128)S(1)}, f32[64]{0:T(128)S(1)}) fusion(pred[64,1]{0,1:T(4,128)(4,1)S(1)} %copy-done.16, f32[]{:T(128)} %bitcast.18, f32[]{:T(128)} %bitcast.17, f32[]{:T(128)} %bitcast.33, f32[]{:T(128)} %bitcast.32), kind=kLoop, calls=%fused_computation.95 | loop fusion | flops 128 | bytes 592 | tf_op jit(solution)/shard_map/mul | solution.py:253
  14.5 1.9 %add_convert_fusion.1 = bf16[896,2,576]{0,2,1:T(8,128)(2,1)} fusion(bf16[384,2,576]{0,2,1:T(8,128)(2,1)S(1)} %bitcast.83, bf16[256,2,576]{0,2,1:T(8,128)(2,1)S(1)} %bitcast.89, bf16[256,2,576]{0,2,1:T(8,128)(2,1)S(1)} %bitcast.88, f32[2,576]{1,0:T(2,128)S(1)} %add.115, f32[2,576]{1,0:T(2,128)S(1)} %mul.167, f32[896]{0:T(1024)S(1)} %add_rsqrt_fusion, ...), kind=kLoop, calls=%fused_computation.5 | loop fusion | flops 11354112 | bytes 4145152 | tf_op jit(solution)/shard_map/convert_element_type | solution.py:30
  16.3 1.4 %broadcast.117.clone = bf16[2,288,1728]{2,1,0:T(8,128)(2,1)} broadcast(bf16[]{:T(256)} %constant.111.clone.1), dimensions={} | broadcast | bytes 1990658 | tf_op jit(solution)/shard_map/broadcast.4
  17.9 1.0 bitcast_dynamic-update-slice_fusion.3
  19.7 2.2 %bitcast_dynamic-update-slice_fusion.2 = bf16[2,288,1728]{2,1,0:T(8,128)(2,1)} fusion(bf16[2,288,1728]{2,1,0:T(8,128)(2,1)} %bitcast_dynamic-update-slice_fusion.3, s32[]{:T(128)S(6)} %select_n.138, bf16[288,1728]{1,0:T(8,128)(2,1)} %collective-permute-done), kind=kLoop, calls=%fused_computation.38 | loop fusion | bytes 2064388 | tf_op jit(solution)/shard_map/jit(dynamic_update_index_in_dim)/dynamic_update_slice | solution.py:165
  22.0 4.6 %fusion.14 = f32[896,1728]{0,1:T(8,128)S(1)} fusion(bf16[576,1728]{1,0:T(8,128)(2,1)} %bitcast.9, bf16[896,2,576]{0,2,1:T(8,128)(2,1)S(1)} %copy-done.5, s32[]{:T(128)S(6)} %select_n.135), kind=kOutput, calls=%fused_computation.40 | convolution fusion | flops 1783627776 | bytes 9216004 | tf_op jit(solution)/shard_map/dot_general | solution.py:169
  26.8 1.0 slice_bitcast_fusion.1
  28.0 1.3 %bitcast_dynamic-update-slice_fusion.1 = bf16[2,288,1728]{2,1,0:T(8,128)(2,1)S(1)} fusion(bf16[2,288,1728]{2,1,0:T(8,128)(2,1)S(1)} %broadcast.117, s32[]{:T(128)S(6)} %select_n.137, bf16[288,1728]{1,0:T(8,128)(2,1)} %collective-permute-done.1), kind=kLoop, calls=%fused_computation.35 | loop fusion | bytes 2027524 | tf_op jit(solution)/shard_map/jit(dynamic_update_index_in_dim)/dynamic_update_slice | solution.py:164
  29.8 1.7 %collective-permute-start.4 = (bf16[576,288]{0,1:T(8,128)(2,1)}, bf16[576,288]{0,1:T(8,128)(2,1)}, u32[]{:S(2)}, u32[]{:S(2)}) collective-permute-start(bf16[576,288]{0,1:T(8,128)(2,1)} %param.29), channel_id=1, source_target_pairs={{2,0},{3,1},{0,2},{1,3},{6,4},{7,5},{4,6},{5,7},{10,8},{11,9},{8,1... | collective-permute-start | bytes 995336 | tf_op jit(solution)/shard_map/ppermute | solution.py:104
  31.6 2.9 %fusion.12 = f32[896,1728]{0,1:T(8,128)S(1)} fusion(bf16[576,1728]{1,0:T(8,128)(2,1)S(1)} %bitcast.90, bf16[896,2,576]{0,2,1:T(8,128)(2,1)S(1)} %copy-done.5, s32[]{:T(128)S(6)} %select_n.139), kind=kOutput, calls=%fused_computation.36 | convolution fusion | flops 1783627776 | bytes 9289732 | tf_op jit(solution)/shard_map/dot_general | solution.py:169
  34.5 0.8 add_convert_fusion
  35.3 1.6 %fusion.38 = (bf16[896,1,8,72]{0,3,2,1:T(8,128)(2,1)S(1)}, bf16[896,1,8,72]{0,3,2,1:T(8,128)(2,1)}, bf16[8,72,896]{2,1,0:T(8,128)(2,1)}) fusion(bf16[896,3,8,72]{0,3,2,1:T(8,128)(2,1)S(1)} %bitcast.84), kind=kLoop, calls=%fused_computation.99 | loop fusion | bytes 6193152 | tf_op jit(solution)/shard_map/slice | solution.py:200
  36.9 1.9 %copy.82 = bf16[896,1,8,72]{3,0,2,1:T(8,128)(2,1)S(1)} copy(bf16[896,1,8,72]{0,3,2,1:T(8,128)(2,1)} %get-tuple-element.38) | data formatting | bytes 2064384
  38.8 1.1 slice.170.refs_0_.refs_4_.refs_8_.refs_12_
  39.9 1.7 %copy.83 = bf16[896,1,8,72]{3,0,2,1:T(8,128)(2,1)} copy(bf16[896,1,8,72]{0,3,2,1:T(8,128)(2,1)S(1)} %get-tuple-element.37) | data formatting | bytes 2064384
  41.6 1.0 bitcast_dynamic-update-slice_fusion.7
  42.8 1.0 bitcast_dynamic-update-slice_fusion.6
  43.8 1.0 bitcast_dynamic-update-slice_fusion.5
  45.0 1.8 %copy.69.refs_3_.refs_7_.refs_11_.refs_15_ = bf16[576,1152]{1,0:T(8,128)(2,1)} copy(bf16[576,1152]{0,1:T(8,128)(2,1)S(1)} %bitcast.87) | data formatting | bytes 2654208 | tf_op jit(solution)/shard_map/reshape | solution.py:195
  46.8 16.7 %shard_map.253 = bf16[512,1152]{1,0:T(8,128)(2,1)} custom-call(bf16[8,512,72]{2,1,0:T(8,128)(2,1)} %slice.170.refs_0_.refs_4_.refs_8_.refs_12_, bf16[8,72,896]{2,1,0:T(8,128)(2,1)} %get-tuple-element.39.refs_1_.refs_5_.refs_9_.refs_13_, bf16[8,896,72]{2,1,0:T(8,128)(2,1)} %bitcast.69, bf16[576,1152]{1,0:T(8,128)(2,1)} %copy.69.refs_3_.refs_7_.refs_11_.refs_15_, ...), custom_call_target="tpu_custom_call" | custom-call | tf_op jit(solution)/shard_map/pallas_call | solution.py:88
  63.5 1.8 %convolution_convert_fusion = bf16[256,1152]{1,0:T(8,128)(2,1)S(1)} fusion(bf16[512,1152]{1,0:T(8,128)(2,1)} %shard_map.253, s32[256]{0:T(256)S(1)} %eq.138), kind=kOutput, calls=%fused_computation.15 | convolution fusion | flops 302415872 | bytes 1770496 | tf_op jit(solution)/shard_map/dot_general | solution.py:225
  66.0 1.6 %collective-permute-start.8 = (bf16[64,1152]{1,0:T(8,128)(2,1)S(1)}, bf16[64,1152]{1,0:T(8,128)(2,1)S(1)}, u32[]{:S(2)}, u32[]{:S(2)}) collective-permute-start(bf16[64,1152]{1,0:T(8,128)(2,1)S(1)} %get-tuple-element.52), channel_id=1, source_target_pairs={{0,2},{1,3},{2,0},{3,1},{4,6},{5,7},{6,4},{7,5},{8,10},{9,11},{10,... | collective-permute-start | bytes 442376 | tf_op jit(solution)/shard_map/ppermute | solution.py:234
  68.0 1.0 fusion.39
  69.0 9.1 %shard_map.254 = bf16[192,1152]{1,0:T(8,128)(2,1)} custom-call(bf16[8,192,72]{2,1,0:T(8,128)(2,1)} %get-tuple-element.23.refs_0_.refs_4_.refs_8_.refs_12_, bf16[8,72,896]{2,1,0:T(8,128)(2,1)} %get-tuple-element.39.refs_1_.refs_5_.refs_9_.refs_13_, bf16[8,896,72]{2,1,0:T(8,128)(2,1)} %bitcast.73, bf16[576,1152]{1,0:T(8,128)(2,1)} %copy.69.refs_3_.refs_7_.refs_11_.refs_15_, ...), custom_call_target="tpu_custom_call" | custom-call | tf_op jit(solution)/shard_map/pallas_call | solution.py:88
  78.3 0.7 fusion.4
  79.2 3.9 %collective-permute-start.10 = (bf16[256,1152]{1,0:T(8,128)(2,1)S(1)}, bf16[256,1152]{1,0:T(8,128)(2,1)S(1)}, u32[]{:S(2)}, u32[]{:S(2)}) collective-permute-start(bf16[256,1152]{1,0:T(8,128)(2,1)S(1)} %get-tuple-element.33), channel_id=1, source_target_pairs={{0,4},{4,8},{8,12},{1,5},{5,9},{9,13},{2,6},{6,10},{10,14},{3,7},{... | collective-permute-start | bytes 1769480 | tf_op jit(solution)/shard_map/ppermute | solution.py:267
  83.1 1.3 %collective-permute-start.11 = (bf16[256,1152]{1,0:T(8,128)(2,1)S(1)}, bf16[256,1152]{1,0:T(8,128)(2,1)S(1)}, u32[]{:S(2)}, u32[]{:S(2)}) collective-permute-start(bf16[256,1152]{1,0:T(8,128)(2,1)S(1)} %get-tuple-element.28), channel_id=1, source_target_pairs={{4,0},{8,4},{12,8},{5,1},{9,5},{13,9},{6,2},{10,6},{14,10},{7,3},{... | collective-permute-start | bytes 1769480 | tf_op jit(solution)/shard_map/ppermute | solution.py:268
  84.7 0.6 collective-permute-start.12
  85.5 1.4 %collective-permute-start.14 = (bf16[24,1152]{1,0:T(8,128)(2,1)S(1)}, bf16[24,1152]{1,0:T(8,128)(2,1)S(1)}, u32[]{:S(2)}, u32[]{:S(2)}) collective-permute-start(bf16[24,1152]{1,0:T(8,128)(2,1)S(1)} %get-tuple-element.60), channel_id=1, source_target_pairs={{0,2},{1,3},{2,0},{3,1},{4,6},{5,7},{6,4},{7,5},{8,10},{9,11},{10,... | collective-permute-start | bytes 165896 | tf_op jit(solution)/shard_map/ppermute | solution.py:234
  87.1 1.9 %collective-permute-start.15 = (bf16[24,1152]{1,0:T(8,128)(2,1)S(1)}, bf16[24,1152]{1,0:T(8,128)(2,1)S(1)}, u32[]{:S(2)}, u32[]{:S(2)}) collective-permute-start(bf16[24,1152]{1,0:T(8,128)(2,1)S(1)} %get-tuple-element.59), channel_id=1, source_target_pairs={{0,2},{1,3},{2,0},{3,1},{4,6},{5,7},{6,4},{7,5},{8,10},{9,11},{10,... | collective-permute-start | bytes 165896 | tf_op jit(solution)/shard_map/ppermute | solution.py:234
  90.3 9.0 %shard_map.255 = bf16[192,1152]{1,0:T(8,128)(2,1)} custom-call(bf16[8,192,72]{2,1,0:T(8,128)(2,1)} %get-tuple-element.29.refs_0_.refs_4_.refs_8_.refs_12_, bf16[8,72,896]{2,1,0:T(8,128)(2,1)} %get-tuple-element.39.refs_1_.refs_5_.refs_9_.refs_13_, bf16[8,896,72]{2,1,0:T(8,128)(2,1)} %bitcast.77, bf16[576,1152]{1,0:T(8,128)(2,1)} %copy.69.refs_3_.refs_7_.refs_11_.refs_15_, ...), custom_call_target="tpu_custom_call" | custom-call | tf_op jit(solution)/shard_map/pallas_call | solution.py:88
  99.4 1.2 %collective-permute-done.11 = bf16[256,1152]{1,0:T(8,128)(2,1)S(1)} collective-permute-done((bf16[256,1152]{1,0:T(8,128)(2,1)S(1)}, bf16[256,1152]{1,0:T(8,128)(2,1)S(1)}, u32[]{:S(2)}, u32[]{:S(2)}) %collective-permute-start.11) | collective-permute-done | bytes 589856 | tf_op jit(solution)/shard_map/ppermute | solution.py:268
  100.6 1.3 %convolution_convert_fusion.1 = bf16[96,1152]{1,0:T(8,128)(2,1)S(1)} fusion(bf16[192,1152]{1,0:T(8,128)(2,1)} %shard_map.255, s32[96]{0:T(128)S(1)} %eq.142), kind=kOutput, calls=%fused_computation.17 | convolution fusion | flops 42596352 | bytes 663936 | tf_op jit(solution)/shard_map/dot_general | solution.py:225
  102.0 0.7 collective-permute-start.16
  102.7 0.6 collective-permute-start.18
  103.3 1.4 %collective-permute-start.19 = (bf16[24,1152]{1,0:T(8,128)(2,1)S(1)}, bf16[24,1152]{1,0:T(8,128)(2,1)S(1)}, u32[]{:S(2)}, u32[]{:S(2)}) collective-permute-start(bf16[24,1152]{1,0:T(8,128)(2,1)S(1)} %get-tuple-element.55), channel_id=1, source_target_pairs={{0,2},{1,3},{2,0},{3,1},{4,6},{5,7},{6,4},{7,5},{8,10},{9,11},{10,... | collective-permute-start | bytes 165896 | tf_op jit(solution)/shard_map/ppermute | solution.py:234
  105.8 0.5 collective-permute-done.17
  106.3 1.1 %collective-permute-done.18 = bf16[24,1152]{1,0:T(8,128)(2,1)S(1)} collective-permute-done((bf16[24,1152]{1,0:T(8,128)(2,1)S(1)}, bf16[24,1152]{1,0:T(8,128)(2,1)S(1)}, u32[]{:S(2)}, u32[]{:S(2)}) %collective-permute-start.18) | collective-permute-done | bytes 55328 | tf_op jit(solution)/shard_map/ppermute | solution.py:234
  107.4 1.2 %collective-permute-done.19 = bf16[24,1152]{1,0:T(8,128)(2,1)S(1)} collective-permute-done((bf16[24,1152]{1,0:T(8,128)(2,1)S(1)}, bf16[24,1152]{1,0:T(8,128)(2,1)S(1)}, u32[]{:S(2)}, u32[]{:S(2)}) %collective-permute-start.19) | collective-permute-done | bytes 55328 | tf_op jit(solution)/shard_map/ppermute | solution.py:234
  108.9 1.5 %maximum_bitcast_fusion = bf16[1,1,896,1152]{3,2,1,0:T(8,128)(2,1)} fusion(bf16[256,1152]{1,0:T(8,128)(2,1)S(1)} %fusion.11, bf16[192,1152]{1,0:T(8,128)(2,1)S(1)} %fusion.19, bf16[192,1152]{1,0:T(8,128)(2,1)S(1)} %fusion.7, bf16[256,1152]{1,0:T(8,128)(2,1)S(1)} %fusion.9), kind=kLoop, calls=%fused_computation.20 | loop fusion | flops 8257536 | bytes 4128768 | tf_op jit(solution)/shard_map/reshape | solution.py:308
  (133 shorter events, 9.2 us)
Async XLA Ops:
  0.0 7.1 %copy-start = (s32[4,4,4]{2,1,0:T(4,128)S(1)}, s32[4,4,4]{2,1,0:T(4,128)}, u32[]{:S(2)}) copy-start(s32[4,4,4]{2,1,0:T(4,128)} %param.30) | copy-start | bytes 772
  0.0 19.7 %collective-permute-start = (bf16[288,1728]{1,0:T(8,128)(2,1)}, bf16[288,1728]{1,0:T(8,128)(2,1)}, u32[]{:S(2)}, u32[]{:S(2)}) collective-permute-start(bf16[288,1728]{1,0:T(8,128)(2,1)} %param.28), channel_id=1, source_target_pairs={{1,0},{0,1},{3,2},{2,3},{5,4},{4,5},{7,6},{6,7},{9,8},{8,9},{11,10... | collective-permute-start | bytes 2985992 | tf_op jit(solution)/shard_map/ppermute | solution.py:158
  0.5 26.3 %collective-permute-start.1 = (bf16[288,1728]{1,0:T(8,128)(2,1)}, bf16[288,1728]{1,0:T(8,128)(2,1)}, u32[]{:S(2)}, u32[]{:S(2)}) collective-permute-start(bf16[288,1728]{1,0:T(8,128)(2,1)} %param.28), channel_id=1, source_target_pairs={{2,0},{3,1},{0,2},{1,3},{6,4},{7,5},{4,6},{5,7},{10,8},{11,9},{8,1... | collective-permute-start | bytes 2985992 | tf_op jit(solution)/shard_map/ppermute | solution.py:158
  5.7 1.8 %slice-start = ((bf16[1,1,896,1152]{3,2,1,0:T(8,128)(2,1)}), bf16[1,1,384,1152]{3,2,1,0:T(8,128)(2,1)S(1)}, s32[]{:S(2)}) async-start(bf16[1,1,896,1152]{3,2,1,0:T(8,128)(2,1)} %param.26), calls=%async_computation | async-start | bytes 1769472 | tf_op jit(solution)/shard_map/slice | solution.py:150
  8.3 1.1 %copy-start.9 = (f32[3,1152]{1,0:T(4,128)S(1)}, f32[3,1152]{1,0:T(4,128)}, u32[]{:S(2)}) copy-start(f32[3,1152]{1,0:T(4,128)} %param.27) | copy-start | bytes 41476
  8.4 1.7 %copy-start.17 = (s32[2]{0:T(128)S(1)}, s32[2]{0:T(128)}, u32[]{:S(2)}) copy-start(s32[2]{0:T(128)} %param.31) | copy-start | bytes 28
  8.4 1.8 %copy-start.19 = (s32[4]{0:T(128)S(1)}, s32[4]{0:T(128)}, u32[]{:S(2)}) copy-start(s32[4]{0:T(128)} %constant.114.clone) | copy-start | bytes 52
  8.4 2.5 %copy-start.13 = (s32[4,64]{1,0:T(4,128)S(1)}, s32[4,64]{1,0:T(4,128)}, u32[]{:S(2)}) copy-start(s32[4,64]{1,0:T(4,128)} %constant.115.clone) | copy-start | bytes 3076
  8.4 2.5 %copy-start.14 = (s32[4,64]{1,0:T(4,128)S(1)}, s32[4,64]{1,0:T(4,128)}, u32[]{:S(2)}) copy-start(s32[4,64]{1,0:T(4,128)} %constant.116.clone) | copy-start | bytes 3076
  8.4 2.6 %copy-start.11 = (s32[4,24]{1,0:T(4,128)S(1)}, s32[4,24]{1,0:T(4,128)}, u32[]{:S(2)}) copy-start(s32[4,24]{1,0:T(4,128)} %constant.120.clone) | copy-start | bytes 1156
  8.4 2.6 %copy-start.12 = (s32[4,24]{1,0:T(4,128)S(1)}, s32[4,24]{1,0:T(4,128)}, u32[]{:S(2)}) copy-start(s32[4,24]{1,0:T(4,128)} %constant.121.clone) | copy-start | bytes 1156
  8.4 2.6 %copy-start.16 = (pred[64,1]{0,1:T(4,128)(4,1)S(1)}, pred[64,1]{0,1:T(4,128)(4,1)}, u32[]{:S(2)}) copy-start(pred[64,1]{0,1:T(4,128)(4,1)} %constant.118.clone) | copy-start | bytes 196
  8.4 5.2 %copy-start.15 = (s32[4,64]{1,0:T(4,128)S(1)}, s32[4,64]{1,0:T(4,128)}, u32[]{:S(2)}) copy-start(s32[4,64]{1,0:T(4,128)} %constant.126) | copy-start | bytes 3076
  8.5 5.3 %copy-start.4 = (bf16[1,1,256,1152]{3,2,1,0:T(8,128)(2,1)S(1)}, bf16[1,1,256,1152]{3,2,1,0:T(8,128)(2,1)}, u32[]{:S(2)}) copy-start(bf16[1,1,256,1152]{3,2,1,0:T(8,128)(2,1)} %get-tuple-element.45) | copy-start | bytes 1769476
  8.8 5.2 %copy-start.3 = (bf16[1,1,256,1152]{3,2,1,0:T(8,128)(2,1)S(1)}, bf16[1,1,256,1152]{3,2,1,0:T(8,128)(2,1)}, u32[]{:S(2)}) copy-start(bf16[1,1,256,1152]{3,2,1,0:T(8,128)(2,1)} %get-tuple-element.44) | copy-start | bytes 1769476
  16.3 1.6 %copy-start.8 = (bf16[288,1728]{1,0:T(8,128)(2,1)S(1)}, bf16[288,1728]{1,0:T(8,128)(2,1)}, u32[]{:S(2)}) copy-start(bf16[288,1728]{1,0:T(8,128)(2,1)} %param.28) | copy-start | bytes 2985988
  16.3 3.1 %copy-start.20 = (pred[64]{0:T(512)(128)(4,1)S(1)}, pred[64]{0:T(512)(128)(4,1)}, u32[]{:S(2)}) copy-start(pred[64]{0:T(512)(128)(4,1)} %constant.125) | copy-start | bytes 196
  16.3 3.3 %copy-start.18 = (s32[4]{0:T(128)S(1)}, s32[4]{0:T(128)}, u32[]{:S(2)}) copy-start(s32[4]{0:T(128)} %param.32) | copy-start | bytes 52
  17.9 4.0 %copy-start.5 = (bf16[896,2,576]{0,2,1:T(8,128)(2,1)S(1)}, bf16[896,2,576]{0,2,1:T(8,128)(2,1)}, u32[]{:S(2)}) copy-start(bf16[896,2,576]{0,2,1:T(8,128)(2,1)} %add_convert_fusion.1) | copy-start | bytes 6193156
  22.0 4.9 %copy-start.2 = (bf16[1,1,896,1152]{3,2,1,0:T(8,128)(2,1)S(1)}, bf16[1,1,896,1152]{3,2,1,0:T(8,128)(2,1)}, u32[]{:S(2)}) copy-start(bf16[1,1,896,1152]{3,2,1,0:T(8,128)(2,1)} %param.26) | copy-start | bytes 6193156
  26.7 2.8 %collective-permute-start.2 = (bf16[288,1728]{1,0:T(8,128)(2,1)}, bf16[288,1728]{1,0:T(8,128)(2,1)S(1)}, u32[]{:S(2)}, u32[]{:S(2)}) collective-permute-start(bf16[288,1728]{1,0:T(8,128)(2,1)} %collective-permute-done.1), channel_id=1, source_target_pairs={{1,0},{0,1},{3,2},{2,3},{5,4},{4,5},{7,6},{6,7},{9,8},{8,9},{11,10... | collective-permute-start | bytes 2985992 | tf_op jit(solution)/shard_map/ppermute | solution.py:158
  29.6 13.2 %collective-permute-start.3 = (bf16[576,288]{0,1:T(8,128)(2,1)}, bf16[576,288]{0,1:T(8,128)(2,1)}, u32[]{:S(2)}, u32[]{:S(2)}) collective-permute-start(bf16[576,288]{0,1:T(8,128)(2,1)} %param.29), channel_id=1, source_target_pairs={{1,0},{0,1},{3,2},{2,3},{5,4},{4,5},{7,6},{6,7},{9,8},{8,9},{11,10... | collective-permute-start | bytes 995336 | tf_op jit(solution)/shard_map/ppermute | solution.py:104
  29.8 12.9 %collective-permute-start.4 = (bf16[576,288]{0,1:T(8,128)(2,1)}, bf16[576,288]{0,1:T(8,128)(2,1)}, u32[]{:S(2)}, u32[]{:S(2)}) collective-permute-start(bf16[576,288]{0,1:T(8,128)(2,1)} %param.29), channel_id=1, source_target_pairs={{2,0},{3,1},{0,2},{1,3},{6,4},{7,5},{4,6},{5,7},{10,8},{11,9},{8,1... | collective-permute-start | bytes 995336 | tf_op jit(solution)/shard_map/ppermute | solution.py:104
  42.7 2.2 %collective-permute-start.5 = (bf16[576,288]{0,1:T(8,128)(2,1)}, bf16[576,288]{0,1:T(8,128)(2,1)S(1)}, u32[]{:S(2)}, u32[]{:S(2)}) collective-permute-start(bf16[576,288]{0,1:T(8,128)(2,1)} %collective-permute-done.4), channel_id=1, source_target_pairs={{1,0},{0,1},{3,2},{2,3},{5,4},{4,5},{7,6},{6,7},{9,8},{8,9},{11,10... | collective-permute-start | bytes 995336 | tf_op jit(solution)/shard_map/ppermute | solution.py:104
  65.4 12.7 %collective-permute-start.6 = (bf16[64,1152]{1,0:T(8,128)(2,1)S(1)}, bf16[64,1152]{1,0:T(8,128)(2,1)S(1)}, u32[]{:S(2)}, u32[]{:S(2)}) collective-permute-start(bf16[64,1152]{1,0:T(8,128)(2,1)S(1)} %get-tuple-element.50), channel_id=1, source_target_pairs={{0,3},{1,0},{2,1},{3,2},{4,7},{5,4},{6,5},{7,6},{8,11},{9,8},{10,9... | collective-permute-start | bytes 442376 | tf_op jit(solution)/shard_map/ppermute | solution.py:234
  65.8 12.3 %collective-permute-start.7 = (bf16[64,1152]{1,0:T(8,128)(2,1)S(1)}, bf16[64,1152]{1,0:T(8,128)(2,1)S(1)}, u32[]{:S(2)}, u32[]{:S(2)}) collective-permute-start(bf16[64,1152]{1,0:T(8,128)(2,1)S(1)} %get-tuple-element.53), channel_id=1, source_target_pairs={{0,1},{1,2},{2,3},{3,0},{4,5},{5,6},{6,7},{7,4},{8,9},{9,10},{10,1... | collective-permute-start | bytes 442376 | tf_op jit(solution)/shard_map/ppermute | solution.py:234
  66.0 12.1 %collective-permute-start.8 = (bf16[64,1152]{1,0:T(8,128)(2,1)S(1)}, bf16[64,1152]{1,0:T(8,128)(2,1)S(1)}, u32[]{:S(2)}, u32[]{:S(2)}) collective-permute-start(bf16[64,1152]{1,0:T(8,128)(2,1)S(1)} %get-tuple-element.52), channel_id=1, source_target_pairs={{0,2},{1,3},{2,0},{3,1},{4,6},{5,7},{6,4},{7,5},{8,10},{9,11},{10,... | collective-permute-start | bytes 442376 | tf_op jit(solution)/shard_map/ppermute | solution.py:234
  67.6 10.7 %collective-permute-start.9 = (bf16[64,1152]{1,0:T(8,128)(2,1)S(1)}, bf16[64,1152]{1,0:T(8,128)(2,1)S(1)}, u32[]{:S(2)}, u32[]{:S(2)}) collective-permute-start(bf16[64,1152]{1,0:T(8,128)(2,1)S(1)} %get-tuple-element.51), channel_id=1, source_target_pairs={{0,2},{1,3},{2,0},{3,1},{4,6},{5,7},{6,4},{7,5},{8,10},{9,11},{10,... | collective-permute-start | bytes 442376 | tf_op jit(solution)/shard_map/ppermute | solution.py:234
  69.0 9.4 %copy-start.1 = (bf16[512,1152]{1,0:T(8,128)(2,1)S(1)}, bf16[512,1152]{1,0:T(8,128)(2,1)}, u32[]{:S(2)}) copy-start(bf16[512,1152]{1,0:T(8,128)(2,1)} %shard_map.253) | copy-start | bytes 3538948
  79.0 5.4 %copy-start.6 = (bf16[192,1152]{1,0:T(8,128)(2,1)S(1)}, bf16[192,1152]{1,0:T(8,128)(2,1)}, u32[]{:S(2)}) copy-start(bf16[192,1152]{1,0:T(8,128)(2,1)} %shard_map.254) | copy-start | bytes 1327108
  79.0 10.0 %copy-start.10 = (s32[4,24]{1,0:T(4,128)S(1)}, s32[4,24]{1,0:T(4,128)}, u32[]{:S(2)}) copy-start(s32[4,24]{1,0:T(4,128)} %constant.127) | copy-start | bytes 1156
  79.2 20.2 %collective-permute-start.10 = (bf16[256,1152]{1,0:T(8,128)(2,1)S(1)}, bf16[256,1152]{1,0:T(8,128)(2,1)S(1)}, u32[]{:S(2)}, u32[]{:S(2)}) collective-permute-start(bf16[256,1152]{1,0:T(8,128)(2,1)S(1)} %get-tuple-element.33), channel_id=1, source_target_pairs={{0,4},{4,8},{8,12},{1,5},{5,9},{9,13},{2,6},{6,10},{10,14},{3,7},{... | collective-permute-start | bytes 1769480 | tf_op jit(solution)/shard_map/ppermute | solution.py:267
  83.1 17.6 %collective-permute-start.11 = (bf16[256,1152]{1,0:T(8,128)(2,1)S(1)}, bf16[256,1152]{1,0:T(8,128)(2,1)S(1)}, u32[]{:S(2)}, u32[]{:S(2)}) collective-permute-start(bf16[256,1152]{1,0:T(8,128)(2,1)S(1)} %get-tuple-element.28), channel_id=1, source_target_pairs={{4,0},{8,4},{12,8},{5,1},{9,5},{13,9},{6,2},{10,6},{14,10},{7,3},{... | collective-permute-start | bytes 1769480 | tf_op jit(solution)/shard_map/ppermute | solution.py:268
  84.7 2.4 %collective-permute-start.12 = (bf16[24,1152]{1,0:T(8,128)(2,1)S(1)}, bf16[24,1152]{1,0:T(8,128)(2,1)S(1)}, u32[]{:S(2)}, u32[]{:S(2)}) collective-permute-start(bf16[24,1152]{1,0:T(8,128)(2,1)S(1)} %get-tuple-element.58), channel_id=1, source_target_pairs={{0,3},{1,0},{2,1},{3,2},{4,7},{5,4},{6,5},{7,6},{8,11},{9,8},{10,9... | collective-permute-start | bytes 165896 | tf_op jit(solution)/shard_map/ppermute | solution.py:234
  85.3 14.0 %collective-permute-start.13 = (bf16[24,1152]{1,0:T(8,128)(2,1)S(1)}, bf16[24,1152]{1,0:T(8,128)(2,1)S(1)}, u32[]{:S(2)}, u32[]{:S(2)}) collective-permute-start(bf16[24,1152]{1,0:T(8,128)(2,1)S(1)} %get-tuple-element.61), channel_id=1, source_target_pairs={{0,1},{1,2},{2,3},{3,0},{4,5},{5,6},{6,7},{7,4},{8,9},{9,10},{10,1... | collective-permute-start | bytes 165896 | tf_op jit(solution)/shard_map/ppermute | solution.py:234
  85.5 13.9 %collective-permute-start.14 = (bf16[24,1152]{1,0:T(8,128)(2,1)S(1)}, bf16[24,1152]{1,0:T(8,128)(2,1)S(1)}, u32[]{:S(2)}, u32[]{:S(2)}) collective-permute-start(bf16[24,1152]{1,0:T(8,128)(2,1)S(1)} %get-tuple-element.60), channel_id=1, source_target_pairs={{0,2},{1,3},{2,0},{3,1},{4,6},{5,7},{6,4},{7,5},{8,10},{9,11},{10,... | collective-permute-start | bytes 165896 | tf_op jit(solution)/shard_map/ppermute | solution.py:234
  87.1 12.2 %collective-permute-start.15 = (bf16[24,1152]{1,0:T(8,128)(2,1)S(1)}, bf16[24,1152]{1,0:T(8,128)(2,1)S(1)}, u32[]{:S(2)}, u32[]{:S(2)}) collective-permute-start(bf16[24,1152]{1,0:T(8,128)(2,1)S(1)} %get-tuple-element.59), channel_id=1, source_target_pairs={{0,2},{1,3},{2,0},{3,1},{4,6},{5,7},{6,4},{7,5},{8,10},{9,11},{10,... | collective-permute-start | bytes 165896 | tf_op jit(solution)/shard_map/ppermute | solution.py:234
  102.0 3.8 %collective-permute-start.16 = (bf16[24,1152]{1,0:T(8,128)(2,1)S(1)}, bf16[24,1152]{1,0:T(8,128)(2,1)S(1)}, u32[]{:S(2)}, u32[]{:S(2)}) collective-permute-start(bf16[24,1152]{1,0:T(8,128)(2,1)S(1)} %get-tuple-element.54), channel_id=1, source_target_pairs={{0,3},{1,0},{2,1},{3,2},{4,7},{5,4},{6,5},{7,6},{8,11},{9,8},{10,9... | collective-permute-start | bytes 165896 | tf_op jit(solution)/shard_map/ppermute | solution.py:234
  102.7 3.6 %collective-permute-start.17 = (bf16[24,1152]{1,0:T(8,128)(2,1)S(1)}, bf16[24,1152]{1,0:T(8,128)(2,1)S(1)}, u32[]{:S(2)}, u32[]{:S(2)}) collective-permute-start(bf16[24,1152]{1,0:T(8,128)(2,1)S(1)} %get-tuple-element.57), channel_id=1, source_target_pairs={{0,1},{1,2},{2,3},{3,0},{4,5},{5,6},{6,7},{7,4},{8,9},{9,10},{10,1... | collective-permute-start | bytes 165896 | tf_op jit(solution)/shard_map/ppermute | solution.py:234
  102.7 4.7 %collective-permute-start.18 = (bf16[24,1152]{1,0:T(8,128)(2,1)S(1)}, bf16[24,1152]{1,0:T(8,128)(2,1)S(1)}, u32[]{:S(2)}, u32[]{:S(2)}) collective-permute-start(bf16[24,1152]{1,0:T(8,128)(2,1)S(1)} %get-tuple-element.56), channel_id=1, source_target_pairs={{0,2},{1,3},{2,0},{3,1},{4,6},{5,7},{6,4},{7,5},{8,10},{9,11},{10,... | collective-permute-start | bytes 165896 | tf_op jit(solution)/shard_map/ppermute | solution.py:234
  103.3 5.3 %collective-permute-start.19 = (bf16[24,1152]{1,0:T(8,128)(2,1)S(1)}, bf16[24,1152]{1,0:T(8,128)(2,1)S(1)}, u32[]{:S(2)}, u32[]{:S(2)}) collective-permute-start(bf16[24,1152]{1,0:T(8,128)(2,1)S(1)} %get-tuple-element.55), channel_id=1, source_target_pairs={{0,2},{1,3},{2,0},{3,1},{4,6},{5,7},{6,4},{7,5},{8,10},{9,11},{10,... | collective-permute-start | bytes 165896 | tf_op jit(solution)/shard_map/ppermute | solution.py:234
  105.1 3.5 %copy-start.7 = (bf16[192,1152]{1,0:T(8,128)(2,1)S(1)}, bf16[192,1152]{1,0:T(8,128)(2,1)}, u32[]{:S(2)}) copy-start(bf16[192,1152]{1,0:T(8,128)(2,1)} %shard_map.255) | copy-start | bytes 1327108

commit v19 on v18

--- a/solution.py
+++ b/solution.py
@@ -245,8 +245,11 @@
         place = (token_ids[:, None] == recv_cells[None, :]).astype(jnp.bfloat16)
         partner = jnp.dot(place, arrived, preferred_element_type=jnp.float32)
         dep = strip_depth(1)[:, None]
-        w_keep = jnp.where(dep == 0, keep[0], keep[1])
-        w_take = jnp.where(dep == 0, take[0], take[1])
+        cell = lax.broadcasted_iota(jnp.int32, (S * S, 1), 0)
+        row, col = cell // S, cell % S
+        near = (row == 0) | (row == S - 1) | (col == 0) | (col == S - 1)
+        w_keep = jnp.where(near, keep[0], keep[1])
+        w_take = jnp.where(near, take[0], take[1])
         grid_shape = (part_frames, S * S, tile_out.shape[1])
         own = tile_out.astype(jnp.float32).reshape(grid_shape)
         partner = partner.reshape(grid_shape)

time: 111 us -> 111 us (level)
    mul x1 -> x0, other arithmetic: 2.56 us -> none  [space_blend(): mixed = jnp.where(dep >= 0, w_keep * own + w_take * partner, own)]
    select_n x0 -> x2, other arithmetic: none -> 2.49 us  [the longest x1 1.25 us: space_blend(): w_keep = jnp.where(near, keep[0], keep[1])]
    unnamed x45 -> x43, local copies, waits for them, and re-layouts: 4.71 us -> 4.7 us
where the time goes in v19:
time: 111 us; the launch traced here: 110 us
  Pallas kernels  34.9 us (31%)
  local copies, waits for them, and re-layouts  27.1 us (24%)
  starting transfers between devices  19.8 us (18%)
  matrix products  12.3 us (11%)
  other arithmetic  10.8 us (10%)
  waiting for transfers between devices  4.97 us (4%)
    pallas_call x3, Pallas kernels, attend_project(): pl.pallas_call(attention_kernel, grid=(1, heads // hb), in_specs=in_specs...  34.9 us
    ppermute x12, starting transfers between devices, strips_in(): lax.ppermute(sent, 'face', [(i, (i + shift) % n) for i in range(n)])  9.55 us
    dot_general x2, matrix products, chip_part(): jnp.dot(lax.dynamic_index_in_dim(moved_chips, chip, 0, keepdims=False), w...  7.49 us
    ppermute x6, starting transfers between devices, fetch(): return lax.ppermute(x, 'face', [(src_of(i), i) for i in range(n)])  5.1 us
    unnamed x43, local copies, waits for them, and re-layouts  4.7 us
    ppermute x1, starting transfers between devices, per_device(): lower = lax.ppermute(high, 'tm', [(i, i + 1) for i in range(count - 1)])  3.91 us
    dot_general x3, matrix products, strips_out(): jnp.dot(pick, tile_out, preferred_element_type=jnp.float32)  3.36 us
    ppermute x12, waiting for transfers between devices, strips_in(): lax.ppermute(sent, 'face', [(i, (i + shift) % n) for i in range(n)])  3.22 us
  transfers between devices with their start and end apart: 20, of which 8 were waited for; matrix products, arithmetic and copies ran while one was open for 38% of the time, Pallas kernels for 16%

profile of v19, /device:TPU:0, one launch (start us, length us, event | category | flops | bytes accessed | tf_op | source)
XLA Modules:
  0.0 110.5 jit_solution(13450565556935665267)
XLA Ops:
  0.5 2.6 %collective-permute-start.1 = (bf16[288,1728]{1,0:T(8,128)(2,1)}, bf16[288,1728]{1,0:T(8,128)(2,1)}, u32[]{:S(2)}, u32[]{:S(2)}) collective-permute-start(bf16[288,1728]{1,0:T(8,128)(2,1)} %param.22), channel_id=1, source_target_pairs={{2,0},{3,1},{0,2},{1,3},{6,4},{7,5},{4,6},{5,7},{10,8},{11,9},{8,1... | collective-permute-start | bytes 2985992 | tf_op jit(solution)/shard_map/ppermute | solution.py:158
  3.0 2.4 %slice_bitcast_fusion.4 = (bf16[256,1152]{1,0:T(8,128)(2,1)S(1)}, bf16[256,1152]{1,0:T(8,128)(2,1)S(1)}, bf16[1,1,256,1152]{3,2,1,0:T(8,128)(2,1)}, bf16[1,1,256,1152]{3,2,1,0:T(8,128)(2,1)}) fusion(bf16[1,1,896,1152]{3,2,1,0:T(8,128)(2,1)} %param.20), kind=kLoop, calls=%fused_computation.104 | loop fusion | bytes 3538944 | tf_op jit(solution)/shard_map/slice | solution.py:150
  6.0 1.1 %pad_maximum_fusion.1.refs_16_ = bf16[512,1152]{1,0:T(8,128)(2,1)} fusion(bf16[256,1152]{1,0:T(8,128)(2,1)S(1)} %get-tuple-element.43, bf16[256,1152]{1,0:T(8,128)(2,1)S(1)} %get-tuple-element.42), kind=kLoop, calls=%fused_computation.29 | loop fusion | flops 2359296 | bytes 2359296 | tf_op jit(solution)/shard_map/concatenate | solution.py:149
  7.5 0.9 copy.75
  8.9 0.6 fusion.1
  9.5 0.6 add_reduce_fusion
  10.3 0.7 fusion.44
  11.3 1.3 %broadcast_select_fusion.3 = f32[64]{0:T(128)S(1)} fusion(f32[]{:T(128)} %bitcast.18, f32[]{:T(128)} %bitcast.17), kind=kLoop, calls=%fused_computation.101 | loop fusion | flops 1280 | bytes 264 | tf_op jit(solution)/shard_map/jit(_where)/select_n | solution.py:251
  13.2 1.9 %add_convert_fusion.1 = bf16[896,2,576]{0,2,1:T(8,128)(2,1)} fusion(bf16[384,2,576]{0,2,1:T(8,128)(2,1)S(1)} %bitcast.79, bf16[256,2,576]{0,2,1:T(8,128)(2,1)S(1)} %bitcast.85, bf16[256,2,576]{0,2,1:T(8,128)(2,1)S(1)} %bitcast.84, f32[2,576]{1,0:T(2,128)S(1)} %add.148, f32[2,576]{1,0:T(2,128)S(1)} %mul.143, f32[896]{0:T(1024)S(1)} %add_rsqrt_fusion, ...), kind=kLoop, calls=%fused_computation.5 | loop fusion | flops 11354112 | bytes 4145152 | tf_op jit(solution)/shard_map/convert_element_type | solution.py:30
  15.1 1.4 %broadcast.301.clone = bf16[2,288,1728]{2,1,0:T(8,128)(2,1)} broadcast(bf16[]{:T(256)} %constant.148.clone.1), dimensions={} | broadcast | bytes 1990658 | tf_op jit(solution)/shard_map/broadcast.10
  16.7 1.0 bitcast_dynamic-update-slice_fusion.3
  17.8 1.2 %broadcast_select_fusion.2 = f32[64]{0:T(128)S(1)} fusion(f32[]{:T(128)} %bitcast.32, f32[]{:T(128)} %bitcast.31), kind=kLoop, calls=%fused_computation.100 | loop fusion | flops 1280 | bytes 264 | tf_op jit(solution)/shard_map/jit(_where)/select_n | solution.py:252
  19.7 2.2 %bitcast_dynamic-update-slice_fusion.2 = bf16[2,288,1728]{2,1,0:T(8,128)(2,1)} fusion(bf16[2,288,1728]{2,1,0:T(8,128)(2,1)} %bitcast_dynamic-update-slice_fusion.3, s32[]{:T(128)S(6)} %select_n.183, bf16[288,1728]{1,0:T(8,128)(2,1)} %collective-permute-done), kind=kLoop, calls=%fused_computation.38 | loop fusion | bytes 2064388 | tf_op jit(solution)/shard_map/jit(dynamic_update_index_in_dim)/dynamic_update_slice | solution.py:165
  21.9 4.6 %fusion.14 = f32[896,1728]{0,1:T(8,128)S(1)} fusion(bf16[576,1728]{1,0:T(8,128)(2,1)} %bitcast.9, bf16[896,2,576]{0,2,1:T(8,128)(2,1)S(1)} %copy-done.5, s32[]{:T(128)S(6)} %select_n.180), kind=kOutput, calls=%fused_computation.40 | convolution fusion | flops 1783627776 | bytes 9216004 | tf_op jit(solution)/shard_map/dot_general | solution.py:169
  26.8 1.0 slice_bitcast_fusion.1
  27.9 1.3 %bitcast_dynamic-update-slice_fusion.1 = bf16[2,288,1728]{2,1,0:T(8,128)(2,1)S(1)} fusion(bf16[2,288,1728]{2,1,0:T(8,128)(2,1)S(1)} %broadcast.301, s32[]{:T(128)S(6)} %select_n.182, bf16[288,1728]{1,0:T(8,128)(2,1)} %collective-permute-done.1), kind=kLoop, calls=%fused_computation.35 | loop fusion | bytes 2027524 | tf_op jit(solution)/shard_map/jit(dynamic_update_index_in_dim)/dynamic_update_slice | solution.py:164
  29.8 1.7 %collective-permute-start.4 = (bf16[576,288]{0,1:T(8,128)(2,1)}, bf16[576,288]{0,1:T(8,128)(2,1)}, u32[]{:S(2)}, u32[]{:S(2)}) collective-permute-start(bf16[576,288]{0,1:T(8,128)(2,1)} %param.23), channel_id=1, source_target_pairs={{2,0},{3,1},{0,2},{1,3},{6,4},{7,5},{4,6},{5,7},{10,8},{11,9},{8,1... | collective-permute-start | bytes 995336 | tf_op jit(solution)/shard_map/ppermute | solution.py:104
  31.6 2.9 %fusion.12 = f32[896,1728]{0,1:T(8,128)S(1)} fusion(bf16[576,1728]{1,0:T(8,128)(2,1)S(1)} %bitcast.86, bf16[896,2,576]{0,2,1:T(8,128)(2,1)S(1)} %copy-done.5, s32[]{:T(128)S(6)} %select_n.184), kind=kOutput, calls=%fused_computation.36 | convolution fusion | flops 1783627776 | bytes 9289732 | tf_op jit(solution)/shard_map/dot_general | solution.py:169
  34.5 0.8 add_convert_fusion
  35.3 1.6 %fusion.38 = (bf16[896,1,8,72]{0,3,2,1:T(8,128)(2,1)S(1)}, bf16[896,1,8,72]{0,3,2,1:T(8,128)(2,1)}, bf16[8,72,896]{2,1,0:T(8,128)(2,1)}) fusion(bf16[896,3,8,72]{0,3,2,1:T(8,128)(2,1)S(1)} %bitcast.80), kind=kLoop, calls=%fused_computation.105 | loop fusion | bytes 6193152 | tf_op jit(solution)/shard_map/slice | solution.py:200
  36.9 1.9 %copy.76 = bf16[896,1,8,72]{3,0,2,1:T(8,128)(2,1)S(1)} copy(bf16[896,1,8,72]{0,3,2,1:T(8,128)(2,1)} %get-tuple-element.38) | data formatting | bytes 2064384
  38.8 1.1 slice.170.refs_0_.refs_4_.refs_8_.refs_12_
  39.9 1.7 %copy.77 = bf16[896,1,8,72]{3,0,2,1:T(8,128)(2,1)} copy(bf16[896,1,8,72]{0,3,2,1:T(8,128)(2,1)S(1)} %get-tuple-element.37) | data formatting | bytes 2064384
  41.7 1.0 bitcast_dynamic-update-slice_fusion.7
  42.8 1.0 bitcast_dynamic-update-slice_fusion.6
  43.9 1.0 bitcast_dynamic-update-slice_fusion.5
  45.0 1.8 %copy.63.refs_3_.refs_7_.refs_11_.refs_15_ = bf16[576,1152]{1,0:T(8,128)(2,1)} copy(bf16[576,1152]{0,1:T(8,128)(2,1)S(1)} %bitcast.83) | data formatting | bytes 2654208 | tf_op jit(solution)/shard_map/reshape | solution.py:195
  46.8 16.7 %shard_map.199 = bf16[512,1152]{1,0:T(8,128)(2,1)} custom-call(bf16[8,512,72]{2,1,0:T(8,128)(2,1)} %slice.170.refs_0_.refs_4_.refs_8_.refs_12_, bf16[8,72,896]{2,1,0:T(8,128)(2,1)} %get-tuple-element.39.refs_1_.refs_5_.refs_9_.refs_13_, bf16[8,896,72]{2,1,0:T(8,128)(2,1)} %bitcast.65, bf16[576,1152]{1,0:T(8,128)(2,1)} %copy.63.refs_3_.refs_7_.refs_11_.refs_15_, ...), custom_call_target="tpu_custom_call" | custom-call | tf_op jit(solution)/shard_map/pallas_call | solution.py:88
  63.5 1.8 %convolution_convert_fusion = bf16[256,1152]{1,0:T(8,128)(2,1)S(1)} fusion(bf16[512,1152]{1,0:T(8,128)(2,1)} %shard_map.199, s32[256]{0:T(256)S(1)} %eq.214), kind=kOutput, calls=%fused_computation.15 | convolution fusion | flops 302415872 | bytes 1770496 | tf_op jit(solution)/shard_map/dot_general | solution.py:225
  66.0 1.6 %collective-permute-start.8 = (bf16[64,1152]{1,0:T(8,128)(2,1)S(1)}, bf16[64,1152]{1,0:T(8,128)(2,1)S(1)}, u32[]{:S(2)}, u32[]{:S(2)}) collective-permute-start(bf16[64,1152]{1,0:T(8,128)(2,1)S(1)} %get-tuple-element.52), channel_id=1, source_target_pairs={{0,2},{1,3},{2,0},{3,1},{4,6},{5,7},{6,4},{7,5},{8,10},{9,11},{10,... | collective-permute-start | bytes 442376 | tf_op jit(solution)/shard_map/ppermute | solution.py:234
  68.0 1.0 fusion.39
  69.0 9.1 %shard_map.200 = bf16[192,1152]{1,0:T(8,128)(2,1)} custom-call(bf16[8,192,72]{2,1,0:T(8,128)(2,1)} %get-tuple-element.23.refs_0_.refs_4_.refs_8_.refs_12_, bf16[8,72,896]{2,1,0:T(8,128)(2,1)} %get-tuple-element.39.refs_1_.refs_5_.refs_9_.refs_13_, bf16[8,896,72]{2,1,0:T(8,128)(2,1)} %bitcast.69, bf16[576,1152]{1,0:T(8,128)(2,1)} %copy.63.refs_3_.refs_7_.refs_11_.refs_15_, ...), custom_call_target="tpu_custom_call" | custom-call | tf_op jit(solution)/shard_map/pallas_call | solution.py:88
  78.4 0.7 fusion.4
  79.2 3.9 %collective-permute-start.10 = (bf16[256,1152]{1,0:T(8,128)(2,1)S(1)}, bf16[256,1152]{1,0:T(8,128)(2,1)S(1)}, u32[]{:S(2)}, u32[]{:S(2)}) collective-permute-start(bf16[256,1152]{1,0:T(8,128)(2,1)S(1)} %get-tuple-element.33), channel_id=1, source_target_pairs={{0,4},{4,8},{8,12},{1,5},{5,9},{9,13},{2,6},{6,10},{10,14},{3,7},{... | collective-permute-start | bytes 1769480 | tf_op jit(solution)/shard_map/ppermute | solution.py:270
  83.1 1.3 %collective-permute-start.11 = (bf16[256,1152]{1,0:T(8,128)(2,1)S(1)}, bf16[256,1152]{1,0:T(8,128)(2,1)S(1)}, u32[]{:S(2)}, u32[]{:S(2)}) collective-permute-start(bf16[256,1152]{1,0:T(8,128)(2,1)S(1)} %get-tuple-element.28), channel_id=1, source_target_pairs={{4,0},{8,4},{12,8},{5,1},{9,5},{13,9},{6,2},{10,6},{14,10},{7,3},{... | collective-permute-start | bytes 1769480 | tf_op jit(solution)/shard_map/ppermute | solution.py:271
  84.7 0.6 collective-permute-start.12
  85.5 1.4 %collective-permute-start.14 = (bf16[24,1152]{1,0:T(8,128)(2,1)S(1)}, bf16[24,1152]{1,0:T(8,128)(2,1)S(1)}, u32[]{:S(2)}, u32[]{:S(2)}) collective-permute-start(bf16[24,1152]{1,0:T(8,128)(2,1)S(1)} %get-tuple-element.60), channel_id=1, source_target_pairs={{0,2},{1,3},{2,0},{3,1},{4,6},{5,7},{6,4},{7,5},{8,10},{9,11},{10,... | collective-permute-start | bytes 165896 | tf_op jit(solution)/shard_map/ppermute | solution.py:234
  87.2 1.9 %collective-permute-start.15 = (bf16[24,1152]{1,0:T(8,128)(2,1)S(1)}, bf16[24,1152]{1,0:T(8,128)(2,1)S(1)}, u32[]{:S(2)}, u32[]{:S(2)}) collective-permute-start(bf16[24,1152]{1,0:T(8,128)(2,1)S(1)} %get-tuple-element.59), channel_id=1, source_target_pairs={{0,2},{1,3},{2,0},{3,1},{4,6},{5,7},{6,4},{7,5},{8,10},{9,11},{10,... | collective-permute-start | bytes 165896 | tf_op jit(solution)/shard_map/ppermute | solution.py:234
  90.4 9.0 %shard_map.201 = bf16[192,1152]{1,0:T(8,128)(2,1)} custom-call(bf16[8,192,72]{2,1,0:T(8,128)(2,1)} %get-tuple-element.29.refs_0_.refs_4_.refs_8_.refs_12_, bf16[8,72,896]{2,1,0:T(8,128)(2,1)} %get-tuple-element.39.refs_1_.refs_5_.refs_9_.refs_13_, bf16[8,896,72]{2,1,0:T(8,128)(2,1)} %bitcast.73, bf16[576,1152]{1,0:T(8,128)(2,1)} %copy.63.refs_3_.refs_7_.refs_11_.refs_15_, ...), custom_call_target="tpu_custom_call" | custom-call | tf_op jit(solution)/shard_map/pallas_call | solution.py:88
  99.5 1.2 %collective-permute-done.11 = bf16[256,1152]{1,0:T(8,128)(2,1)S(1)} collective-permute-done((bf16[256,1152]{1,0:T(8,128)(2,1)S(1)}, bf16[256,1152]{1,0:T(8,128)(2,1)S(1)}, u32[]{:S(2)}, u32[]{:S(2)}) %collective-permute-start.11) | collective-permute-done | bytes 589856 | tf_op jit(solution)/shard_map/ppermute | solution.py:271
  100.7 1.3 %convolution_convert_fusion.1 = bf16[96,1152]{1,0:T(8,128)(2,1)S(1)} fusion(bf16[192,1152]{1,0:T(8,128)(2,1)} %shard_map.201, s32[96]{0:T(128)S(1)} %eq.218), kind=kOutput, calls=%fused_computation.17 | convolution fusion | flops 42596352 | bytes 663936 | tf_op jit(solution)/shard_map/dot_general | solution.py:225
  102.0 0.7 collective-permute-start.16
  102.7 0.6 collective-permute-start.18
  103.4 1.4 %collective-permute-start.19 = (bf16[24,1152]{1,0:T(8,128)(2,1)S(1)}, bf16[24,1152]{1,0:T(8,128)(2,1)S(1)}, u32[]{:S(2)}, u32[]{:S(2)}) collective-permute-start(bf16[24,1152]{1,0:T(8,128)(2,1)S(1)} %get-tuple-element.55), channel_id=1, source_target_pairs={{0,2},{1,3},{2,0},{3,1},{4,6},{5,7},{6,4},{7,5},{8,10},{9,11},{10,... | collective-permute-start | bytes 165896 | tf_op jit(solution)/shard_map/ppermute | solution.py:234
  105.8 0.5 collective-permute-done.17
  106.3 1.1 %collective-permute-done.18 = bf16[24,1152]{1,0:T(8,128)(2,1)S(1)} collective-permute-done((bf16[24,1152]{1,0:T(8,128)(2,1)S(1)}, bf16[24,1152]{1,0:T(8,128)(2,1)S(1)}, u32[]{:S(2)}, u32[]{:S(2)}) %collective-permute-start.18) | collective-permute-done | bytes 55328 | tf_op jit(solution)/shard_map/ppermute | solution.py:234
  107.5 1.2 %collective-permute-done.19 = bf16[24,1152]{1,0:T(8,128)(2,1)S(1)} collective-permute-done((bf16[24,1152]{1,0:T(8,128)(2,1)S(1)}, bf16[24,1152]{1,0:T(8,128)(2,1)S(1)}, u32[]{:S(2)}, u32[]{:S(2)}) %collective-permute-start.19) | collective-permute-done | bytes 55328 | tf_op jit(solution)/shard_map/ppermute | solution.py:234
  109.0 1.5 %maximum_bitcast_fusion = bf16[1,1,896,1152]{3,2,1,0:T(8,128)(2,1)} fusion(bf16[256,1152]{1,0:T(8,128)(2,1)S(1)} %fusion.11, bf16[192,1152]{1,0:T(8,128)(2,1)S(1)} %fusion.19, bf16[192,1152]{1,0:T(8,128)(2,1)S(1)} %fusion.7, bf16[256,1152]{1,0:T(8,128)(2,1)S(1)} %fusion.9), kind=kLoop, calls=%fused_computation.20 | loop fusion | flops 8257536 | bytes 4128768 | tf_op jit(solution)/shard_map/reshape | solution.py:311
  (132 shorter events, 9.7 us)
Async XLA Ops:
  0.0 7.1 %copy-start = (s32[4,4,4]{2,1,0:T(4,128)S(1)}, s32[4,4,4]{2,1,0:T(4,128)}, u32[]{:S(2)}) copy-start(s32[4,4,4]{2,1,0:T(4,128)} %param.24) | copy-start | bytes 772
  0.0 19.7 %collective-permute-start = (bf16[288,1728]{1,0:T(8,128)(2,1)}, bf16[288,1728]{1,0:T(8,128)(2,1)}, u32[]{:S(2)}, u32[]{:S(2)}) collective-permute-start(bf16[288,1728]{1,0:T(8,128)(2,1)} %param.22), channel_id=1, source_target_pairs={{1,0},{0,1},{3,2},{2,3},{5,4},{4,5},{7,6},{6,7},{9,8},{8,9},{11,10... | collective-permute-start | bytes 2985992 | tf_op jit(solution)/shard_map/ppermute | solution.py:158
  0.5 26.3 %collective-permute-start.1 = (bf16[288,1728]{1,0:T(8,128)(2,1)}, bf16[288,1728]{1,0:T(8,128)(2,1)}, u32[]{:S(2)}, u32[]{:S(2)}) collective-permute-start(bf16[288,1728]{1,0:T(8,128)(2,1)} %param.22), channel_id=1, source_target_pairs={{2,0},{3,1},{0,2},{1,3},{6,4},{7,5},{4,6},{5,7},{10,8},{11,9},{8,1... | collective-permute-start | bytes 2985992 | tf_op jit(solution)/shard_map/ppermute | solution.py:158
  5.7 1.8 %slice-start = ((bf16[1,1,896,1152]{3,2,1,0:T(8,128)(2,1)}), bf16[1,1,384,1152]{3,2,1,0:T(8,128)(2,1)S(1)}, s32[]{:S(2)}) async-start(bf16[1,1,896,1152]{3,2,1,0:T(8,128)(2,1)} %param.20), calls=%async_computation | async-start | bytes 1769472 | tf_op jit(solution)/shard_map/slice | solution.py:150
  8.4 1.1 copy-start.9
  8.4 1.7 %copy-start.16 = (s32[2]{0:T(128)S(1)}, s32[2]{0:T(128)}, u32[]{:S(2)}) copy-start(s32[2]{0:T(128)} %param.25) | copy-start | bytes 28
  8.4 1.8 %copy-start.18 = (s32[4]{0:T(128)S(1)}, s32[4]{0:T(128)}, u32[]{:S(2)}) copy-start(s32[4]{0:T(128)} %constant.153.clone) | copy-start | bytes 52
  8.4 2.5 %copy-start.13 = (s32[4,64]{1,0:T(4,128)S(1)}, s32[4,64]{1,0:T(4,128)}, u32[]{:S(2)}) copy-start(s32[4,64]{1,0:T(4,128)} %constant.154.clone) | copy-start | bytes 3076
  8.4 2.5 %copy-start.14 = (s32[4,64]{1,0:T(4,128)S(1)}, s32[4,64]{1,0:T(4,128)}, u32[]{:S(2)}) copy-start(s32[4,64]{1,0:T(4,128)} %constant.155.clone) | copy-start | bytes 3076
  8.4 2.6 %copy-start.11 = (s32[4,24]{1,0:T(4,128)S(1)}, s32[4,24]{1,0:T(4,128)}, u32[]{:S(2)}) copy-start(s32[4,24]{1,0:T(4,128)} %constant.158.clone) | copy-start | bytes 1156
  8.4 2.6 %copy-start.12 = (s32[4,24]{1,0:T(4,128)S(1)}, s32[4,24]{1,0:T(4,128)}, u32[]{:S(2)}) copy-start(s32[4,24]{1,0:T(4,128)} %constant.159.clone) | copy-start | bytes 1156
  8.5 2.7 %copy-start.15 = (s32[4,64]{1,0:T(4,128)S(1)}, s32[4,64]{1,0:T(4,128)}, u32[]{:S(2)}) copy-start(s32[4,64]{1,0:T(4,128)} %constant.164) | copy-start | bytes 3076
  8.5 4.1 %copy-start.4 = (bf16[1,1,256,1152]{3,2,1,0:T(8,128)(2,1)S(1)}, bf16[1,1,256,1152]{3,2,1,0:T(8,128)(2,1)}, u32[]{:S(2)}) copy-start(bf16[1,1,256,1152]{3,2,1,0:T(8,128)(2,1)} %get-tuple-element.45) | copy-start | bytes 1769476
  8.8 4.0 %copy-start.3 = (bf16[1,1,256,1152]{3,2,1,0:T(8,128)(2,1)S(1)}, bf16[1,1,256,1152]{3,2,1,0:T(8,128)(2,1)}, u32[]{:S(2)}) copy-start(bf16[1,1,256,1152]{3,2,1,0:T(8,128)(2,1)} %get-tuple-element.44) | copy-start | bytes 1769476
  15.1 1.6 %copy-start.8 = (bf16[288,1728]{1,0:T(8,128)(2,1)S(1)}, bf16[288,1728]{1,0:T(8,128)(2,1)}, u32[]{:S(2)}) copy-start(bf16[288,1728]{1,0:T(8,128)(2,1)} %param.22) | copy-start | bytes 2985988
  15.1 4.3 %copy-start.19 = (pred[64]{0:T(512)(128)(4,1)S(1)}, pred[64]{0:T(512)(128)(4,1)}, u32[]{:S(2)}) copy-start(pred[64]{0:T(512)(128)(4,1)} %constant.163) | copy-start | bytes 196
  15.1 4.4 %copy-start.17 = (s32[4]{0:T(128)S(1)}, s32[4]{0:T(128)}, u32[]{:S(2)}) copy-start(s32[4]{0:T(128)} %param.26) | copy-start | bytes 52
  16.7 5.2 %copy-start.5 = (bf16[896,2,576]{0,2,1:T(8,128)(2,1)S(1)}, bf16[896,2,576]{0,2,1:T(8,128)(2,1)}, u32[]{:S(2)}) copy-start(bf16[896,2,576]{0,2,1:T(8,128)(2,1)} %add_convert_fusion.1) | copy-start | bytes 6193156
  21.9 4.9 %copy-start.2 = (bf16[1,1,896,1152]{3,2,1,0:T(8,128)(2,1)S(1)}, bf16[1,1,896,1152]{3,2,1,0:T(8,128)(2,1)}, u32[]{:S(2)}) copy-start(bf16[1,1,896,1152]{3,2,1,0:T(8,128)(2,1)} %param.20) | copy-start | bytes 6193156
  26.7 2.8 %collective-permute-start.2 = (bf16[288,1728]{1,0:T(8,128)(2,1)}, bf16[288,1728]{1,0:T(8,128)(2,1)S(1)}, u32[]{:S(2)}, u32[]{:S(2)}) collective-permute-start(bf16[288,1728]{1,0:T(8,128)(2,1)} %collective-permute-done.1), channel_id=1, source_target_pairs={{1,0},{0,1},{3,2},{2,3},{5,4},{4,5},{7,6},{6,7},{9,8},{8,9},{11,10... | collective-permute-start | bytes 2985992 | tf_op jit(solution)/shard_map/ppermute | solution.py:158
  29.6 13.2 %collective-permute-start.3 = (bf16[576,288]{0,1:T(8,128)(2,1)}, bf16[576,288]{0,1:T(8,128)(2,1)}, u32[]{:S(2)}, u32[]{:S(2)}) collective-permute-start(bf16[576,288]{0,1:T(8,128)(2,1)} %param.23), channel_id=1, source_target_pairs={{1,0},{0,1},{3,2},{2,3},{5,4},{4,5},{7,6},{6,7},{9,8},{8,9},{11,10... | collective-permute-start | bytes 995336 | tf_op jit(solution)/shard_map/ppermute | solution.py:104
  29.8 12.9 %collective-permute-start.4 = (bf16[576,288]{0,1:T(8,128)(2,1)}, bf16[576,288]{0,1:T(8,128)(2,1)}, u32[]{:S(2)}, u32[]{:S(2)}) collective-permute-start(bf16[576,288]{0,1:T(8,128)(2,1)} %param.23), channel_id=1, source_target_pairs={{2,0},{3,1},{0,2},{1,3},{6,4},{7,5},{4,6},{5,7},{10,8},{11,9},{8,1... | collective-permute-start | bytes 995336 | tf_op jit(solution)/shard_map/ppermute | solution.py:104
  42.7 2.2 %collective-permute-start.5 = (bf16[576,288]{0,1:T(8,128)(2,1)}, bf16[576,288]{0,1:T(8,128)(2,1)S(1)}, u32[]{:S(2)}, u32[]{:S(2)}) collective-permute-start(bf16[576,288]{0,1:T(8,128)(2,1)} %collective-permute-done.4), channel_id=1, source_target_pairs={{1,0},{0,1},{3,2},{2,3},{5,4},{4,5},{7,6},{6,7},{9,8},{8,9},{11,10... | collective-permute-start | bytes 995336 | tf_op jit(solution)/shard_map/ppermute | solution.py:104
  65.4 12.7 %collective-permute-start.6 = (bf16[64,1152]{1,0:T(8,128)(2,1)S(1)}, bf16[64,1152]{1,0:T(8,128)(2,1)S(1)}, u32[]{:S(2)}, u32[]{:S(2)}) collective-permute-start(bf16[64,1152]{1,0:T(8,128)(2,1)S(1)} %get-tuple-element.50), channel_id=1, source_target_pairs={{0,3},{1,0},{2,1},{3,2},{4,7},{5,4},{6,5},{7,6},{8,11},{9,8},{10,9... | collective-permute-start | bytes 442376 | tf_op jit(solution)/shard_map/ppermute | solution.py:234
  65.8 12.3 %collective-permute-start.7 = (bf16[64,1152]{1,0:T(8,128)(2,1)S(1)}, bf16[64,1152]{1,0:T(8,128)(2,1)S(1)}, u32[]{:S(2)}, u32[]{:S(2)}) collective-permute-start(bf16[64,1152]{1,0:T(8,128)(2,1)S(1)} %get-tuple-element.53), channel_id=1, source_target_pairs={{0,1},{1,2},{2,3},{3,0},{4,5},{5,6},{6,7},{7,4},{8,9},{9,10},{10,1... | collective-permute-start | bytes 442376 | tf_op jit(solution)/shard_map/ppermute | solution.py:234
  66.0 12.1 %collective-permute-start.8 = (bf16[64,1152]{1,0:T(8,128)(2,1)S(1)}, bf16[64,1152]{1,0:T(8,128)(2,1)S(1)}, u32[]{:S(2)}, u32[]{:S(2)}) collective-permute-start(bf16[64,1152]{1,0:T(8,128)(2,1)S(1)} %get-tuple-element.52), channel_id=1, source_target_pairs={{0,2},{1,3},{2,0},{3,1},{4,6},{5,7},{6,4},{7,5},{8,10},{9,11},{10,... | collective-permute-start | bytes 442376 | tf_op jit(solution)/shard_map/ppermute | solution.py:234
  67.6 10.7 %collective-permute-start.9 = (bf16[64,1152]{1,0:T(8,128)(2,1)S(1)}, bf16[64,1152]{1,0:T(8,128)(2,1)S(1)}, u32[]{:S(2)}, u32[]{:S(2)}) collective-permute-start(bf16[64,1152]{1,0:T(8,128)(2,1)S(1)} %get-tuple-element.51), channel_id=1, source_target_pairs={{0,2},{1,3},{2,0},{3,1},{4,6},{5,7},{6,4},{7,5},{8,10},{9,11},{10,... | collective-permute-start | bytes 442376 | tf_op jit(solution)/shard_map/ppermute | solution.py:234
  69.0 9.4 %copy-start.1 = (bf16[512,1152]{1,0:T(8,128)(2,1)S(1)}, bf16[512,1152]{1,0:T(8,128)(2,1)}, u32[]{:S(2)}) copy-start(bf16[512,1152]{1,0:T(8,128)(2,1)} %shard_map.199) | copy-start | bytes 3538948
  79.1 5.3 %copy-start.6 = (bf16[192,1152]{1,0:T(8,128)(2,1)S(1)}, bf16[192,1152]{1,0:T(8,128)(2,1)}, u32[]{:S(2)}) copy-start(bf16[192,1152]{1,0:T(8,128)(2,1)} %shard_map.200) | copy-start | bytes 1327108
  79.1 10.0 %copy-start.10 = (s32[4,24]{1,0:T(4,128)S(1)}, s32[4,24]{1,0:T(4,128)}, u32[]{:S(2)}) copy-start(s32[4,24]{1,0:T(4,128)} %constant.165) | copy-start | bytes 1156
  79.2 20.3 %collective-permute-start.10 = (bf16[256,1152]{1,0:T(8,128)(2,1)S(1)}, bf16[256,1152]{1,0:T(8,128)(2,1)S(1)}, u32[]{:S(2)}, u32[]{:S(2)}) collective-permute-start(bf16[256,1152]{1,0:T(8,128)(2,1)S(1)} %get-tuple-element.33), channel_id=1, source_target_pairs={{0,4},{4,8},{8,12},{1,5},{5,9},{9,13},{2,6},{6,10},{10,14},{3,7},{... | collective-permute-start | bytes 1769480 | tf_op jit(solution)/shard_map/ppermute | solution.py:270
  83.1 17.6 %collective-permute-start.11 = (bf16[256,1152]{1,0:T(8,128)(2,1)S(1)}, bf16[256,1152]{1,0:T(8,128)(2,1)S(1)}, u32[]{:S(2)}, u32[]{:S(2)}) collective-permute-start(bf16[256,1152]{1,0:T(8,128)(2,1)S(1)} %get-tuple-element.28), channel_id=1, source_target_pairs={{4,0},{8,4},{12,8},{5,1},{9,5},{13,9},{6,2},{10,6},{14,10},{7,3},{... | collective-permute-start | bytes 1769480 | tf_op jit(solution)/shard_map/ppermute | solution.py:271
  84.7 2.4 %collective-permute-start.12 = (bf16[24,1152]{1,0:T(8,128)(2,1)S(1)}, bf16[24,1152]{1,0:T(8,128)(2,1)S(1)}, u32[]{:S(2)}, u32[]{:S(2)}) collective-permute-start(bf16[24,1152]{1,0:T(8,128)(2,1)S(1)} %get-tuple-element.58), channel_id=1, source_target_pairs={{0,3},{1,0},{2,1},{3,2},{4,7},{5,4},{6,5},{7,6},{8,11},{9,8},{10,9... | collective-permute-start | bytes 165896 | tf_op jit(solution)/shard_map/ppermute | solution.py:234
  85.4 14.0 %collective-permute-start.13 = (bf16[24,1152]{1,0:T(8,128)(2,1)S(1)}, bf16[24,1152]{1,0:T(8,128)(2,1)S(1)}, u32[]{:S(2)}, u32[]{:S(2)}) collective-permute-start(bf16[24,1152]{1,0:T(8,128)(2,1)S(1)} %get-tuple-element.61), channel_id=1, source_target_pairs={{0,1},{1,2},{2,3},{3,0},{4,5},{5,6},{6,7},{7,4},{8,9},{9,10},{10,1... | collective-permute-start | bytes 165896 | tf_op jit(solution)/shard_map/ppermute | solution.py:234
  85.5 13.9 %collective-permute-start.14 = (bf16[24,1152]{1,0:T(8,128)(2,1)S(1)}, bf16[24,1152]{1,0:T(8,128)(2,1)S(1)}, u32[]{:S(2)}, u32[]{:S(2)}) collective-permute-start(bf16[24,1152]{1,0:T(8,128)(2,1)S(1)} %get-tuple-element.60), channel_id=1, source_target_pairs={{0,2},{1,3},{2,0},{3,1},{4,6},{5,7},{6,4},{7,5},{8,10},{9,11},{10,... | collective-permute-start | bytes 165896 | tf_op jit(solution)/shard_map/ppermute | solution.py:234
  87.2 12.3 %collective-permute-start.15 = (bf16[24,1152]{1,0:T(8,128)(2,1)S(1)}, bf16[24,1152]{1,0:T(8,128)(2,1)S(1)}, u32[]{:S(2)}, u32[]{:S(2)}) collective-permute-start(bf16[24,1152]{1,0:T(8,128)(2,1)S(1)} %get-tuple-element.59), channel_id=1, source_target_pairs={{0,2},{1,3},{2,0},{3,1},{4,6},{5,7},{6,4},{7,5},{8,10},{9,11},{10,... | collective-permute-start | bytes 165896 | tf_op jit(solution)/shard_map/ppermute | solution.py:234
  102.0 3.8 %collective-permute-start.16 = (bf16[24,1152]{1,0:T(8,128)(2,1)S(1)}, bf16[24,1152]{1,0:T(8,128)(2,1)S(1)}, u32[]{:S(2)}, u32[]{:S(2)}) collective-permute-start(bf16[24,1152]{1,0:T(8,128)(2,1)S(1)} %get-tuple-element.54), channel_id=1, source_target_pairs={{0,3},{1,0},{2,1},{3,2},{4,7},{5,4},{6,5},{7,6},{8,11},{9,8},{10,9... | collective-permute-start | bytes 165896 | tf_op jit(solution)/shard_map/ppermute | solution.py:234
  102.7 3.6 %collective-permute-start.17 = (bf16[24,1152]{1,0:T(8,128)(2,1)S(1)}, bf16[24,1152]{1,0:T(8,128)(2,1)S(1)}, u32[]{:S(2)}, u32[]{:S(2)}) collective-permute-start(bf16[24,1152]{1,0:T(8,128)(2,1)S(1)} %get-tuple-element.57), channel_id=1, source_target_pairs={{0,1},{1,2},{2,3},{3,0},{4,5},{5,6},{6,7},{7,4},{8,9},{9,10},{10,1... | collective-permute-start | bytes 165896 | tf_op jit(solution)/shard_map/ppermute | solution.py:234
  102.7 4.7 %collective-permute-start.18 = (bf16[24,1152]{1,0:T(8,128)(2,1)S(1)}, bf16[24,1152]{1,0:T(8,128)(2,1)S(1)}, u32[]{:S(2)}, u32[]{:S(2)}) collective-permute-start(bf16[24,1152]{1,0:T(8,128)(2,1)S(1)} %get-tuple-element.56), channel_id=1, source_target_pairs={{0,2},{1,3},{2,0},{3,1},{4,6},{5,7},{6,4},{7,5},{8,10},{9,11},{10,... | collective-permute-start | bytes 165896 | tf_op jit(solution)/shard_map/ppermute | solution.py:234
  103.4 5.3 %collective-permute-start.19 = (bf16[24,1152]{1,0:T(8,128)(2,1)S(1)}, bf16[24,1152]{1,0:T(8,128)(2,1)S(1)}, u32[]{:S(2)}, u32[]{:S(2)}) collective-permute-start(bf16[24,1152]{1,0:T(8,128)(2,1)S(1)} %get-tuple-element.55), channel_id=1, source_target_pairs={{0,2},{1,3},{2,0},{3,1},{4,6},{5,7},{6,4},{7,5},{8,10},{9,11},{10,... | collective-permute-start | bytes 165896 | tf_op jit(solution)/shard_map/ppermute | solution.py:234
  105.1 3.5 %copy-start.7 = (bf16[192,1152]{1,0:T(8,128)(2,1)S(1)}, bf16[192,1152]{1,0:T(8,128)(2,1)}, u32[]{:S(2)}) copy-start(bf16[192,1152]{1,0:T(8,128)(2,1)} %shard_map.201) | copy-start | bytes 1327108

commit v20 on v19

--- a/solution.py
+++ b/solution.py
@@ -160,10 +160,9 @@
         moved_chips = moved.reshape(tokens, 2, 2 * rows).transpose(1, 0, 2)
 
         def chip_weight(same_core, other_core):
-            stack = jnp.zeros((2,) + w_qkv.shape, w_qkv.dtype)
-            stack = lax.dynamic_update_index_in_dim(stack, same_core, core, 0)
-            stack = lax.dynamic_update_index_in_dim(stack, other_core, 1 - core, 0)
-            return stack.reshape(2 * rows, w_qkv.shape[1])
+            first = jnp.where(core == 0, same_core, other_core)
+            second = jnp.where(core == 0, other_core, same_core)
+            return jnp.concatenate([first, second], axis=0)
 
         def chip_part(chip, weight):
             return jnp.dot(

time: 111 us -> 115 us (1.036)
  local copies, waits for them, and re-layouts: 27.1 us -> 29.5 us
  other arithmetic: 10.8 us -> 13.1 us
    dynamic_update_slice x4 -> x0, local copies, waits for them, and re-layouts: 4.68 us -> none  [the longest x2 2.34 us: chip_weight(): stack = lax.dynamic_update_index_in_dim(stack, same_core, core, 0)]
    select_n x0 -> x2, other arithmetic: none -> 3.28 us  [chip_weight(): first = jnp.where(core == 0, same_core, other_core)]
    slice x2 -> x1, local copies, waits for them, and re-layouts: 0.01 us -> 2.15 us  [per_device(): block_in[rim:tokens - rim]]
    slice x3, local copies, waits for them, and re-layouts: 2.94 us -> 4.83 us  [per_device(): block_in[:rim]]
    slice x2, local copies, waits for them, and re-layouts: 0.51 us -> 2.37 us  [per_device(): block_in[tokens - rim:]]
    unnamed x43 -> x47, local copies, waits for them, and re-layouts: 4.7 us -> 6.3 us
    another operation x2 -> x0, local copies, waits for them, and re-layouts: 1.57 us -> none
    slice x1, local copies, waits for them, and re-layouts: 1.01 us -> 2.21 us  [per_device(): tile_second = tile_part(second_queries, block_in[mid_a:])]
  transfers between devices with their start and end apart: 20 -> 20, of which waited for: 8 -> 5; matrix products, arithmetic and copies ran while one was open for 38% -> 41% of each run, Pallas kernels for 16% -> 16%
where the time goes in v20:
time: 115 us; the launch traced here: 114 us
  Pallas kernels  35.2 us (31%)
  local copies, waits for them, and re-layouts  29.5 us (26%)
  starting transfers between devices  18.7 us (16%)
  other arithmetic  13.1 us (11%)
  matrix products  12.5 us (11%)
  waiting for transfers between devices  4.83 us (4%)
    pallas_call x3, Pallas kernels, attend_project(): pl.pallas_call(attention_kernel, grid=(1, heads // hb), in_specs=in_specs...  35.2 us
    ppermute x12, starting transfers between devices, strips_in(): lax.ppermute(sent, 'face', [(i, (i + shift) % n) for i in range(n)])  9.17 us
    dot_general x2, matrix products, chip_part(): jnp.dot(lax.dynamic_index_in_dim(moved_chips, chip, 0, keepdims=False), w...  7.74 us
    unnamed x47, local copies, waits for them, and re-layouts  6.3 us
    slice x3, local copies, waits for them, and re-layouts, per_device(): block_in[:rim]  4.83 us
    ppermute x6, starting transfers between devices, fetch(): return lax.ppermute(x, 'face', [(src_of(i), i) for i in range(n)])  4.64 us
    ppermute x1, starting transfers between devices, per_device(): lower = lax.ppermute(high, 'tm', [(i, i + 1) for i in range(count - 1)])  3.63 us
    ppermute x12, waiting for transfers between devices, strips_in(): lax.ppermute(sent, 'face', [(i, (i + shift) % n) for i in range(n)])  3.53 us
  transfers between devices with their start and end apart: 20, of which 5 were waited for; matrix products, arithmetic and copies ran while one was open for 41% of the time, Pallas kernels for 16%

profile of v20, /device:TPU:0, one launch (start us, length us, event | category | flops | bytes accessed | tf_op | source)
XLA Modules:
  0.0 114.4 jit_solution(3839925520023802525)
XLA Ops:
  0.5 2.6 %collective-permute-start.1 = (bf16[288,1728]{1,0:T(8,128)(2,1)}, bf16[288,1728]{1,0:T(8,128)(2,1)}, u32[]{:S(2)}, u32[]{:S(2)}) collective-permute-start(bf16[288,1728]{1,0:T(8,128)(2,1)} %param.22), channel_id=1, source_target_pairs={{2,0},{3,1},{0,2},{1,3},{6,4},{7,5},{4,6},{5,7},{10,8},{11,9},{8,1... | collective-permute-start | bytes 2985992 | tf_op jit(solution)/shard_map/ppermute | solution.py:158
  3.0 2.4 %slice_bitcast_fusion.4 = (bf16[256,1152]{1,0:T(8,128)(2,1)S(1)}, bf16[256,1152]{1,0:T(8,128)(2,1)S(1)}, bf16[1,1,256,1152]{3,2,1,0:T(8,128)(2,1)}, bf16[1,1,256,1152]{3,2,1,0:T(8,128)(2,1)}) fusion(bf16[1,1,896,1152]{3,2,1,0:T(8,128)(2,1)} %param.20), kind=kLoop, calls=%fused_computation.111 | loop fusion | bytes 3538944 | tf_op jit(solution)/shard_map/slice | solution.py:150
  5.5 2.1 %slice.131 = bf16[1,1,384,1152]{3,2,1,0:T(8,128)(2,1)} slice(bf16[1,1,896,1152]{3,2,1,0:T(8,128)(2,1)} %param.20), slice={[0:1], [0:1], [256:640], [0:1152]} | slice | bytes 1769472 | tf_op jit(solution)/shard_map/slice | solution.py:150
  8.5 1.8 %copy.75 = bf16[1,1,384,1152]{2,3,1,0:T(8,128)(2,1)S(1)} copy(bf16[1,1,384,1152]{3,2,1,0:T(8,128)(2,1)} %slice.131) | data formatting | bytes 1769472
  10.7 2.1 %copy.56 = bf16[1,1,256,1152]{2,3,1,0:T(8,128)(2,1)} copy(bf16[1,1,256,1152]{3,2,1,0:T(8,128)(2,1)} %get-tuple-element.47) | data formatting | bytes 1179648 | tf_op jit(solution)/shard_map/slice | solution.py:150
  12.8 2.1 %copy.57 = bf16[1,1,256,1152]{2,3,1,0:T(8,128)(2,1)} copy(bf16[1,1,256,1152]{3,2,1,0:T(8,128)(2,1)} %get-tuple-element.46) | data formatting | bytes 1179648 | tf_op jit(solution)/shard_map/slice | solution.py:150
  16.9 1.3 %broadcast_select_fusion.7 = f32[64]{0:T(128)S(1)} fusion(f32[]{:T(128)} %bitcast.12, f32[]{:T(128)} %bitcast.11), kind=kLoop, calls=%fused_computation.106 | loop fusion | flops 1280 | bytes 264 | tf_op jit(solution)/shard_map/jit(_where)/select_n | solution.py:250
  19.5 0.9 add_convert_fusion.1
  20.7 1.8 %broadcast_select_fusion.3 = (bf16[288,1728]{1,0:T(8,128)(2,1)S(1)}, bf16[288,1728]{1,0:T(8,128)(2,1)S(1)}) fusion(bf16[288,1728]{1,0:T(8,128)(2,1)S(1)} %copy-done.8, bf16[288,1728]{1,0:T(8,128)(2,1)} %collective-permute-done, pred[]{:T(512)S(6)} %eq.206), kind=kLoop, calls=%fused_computation.49 | loop fusion | flops 995328 | bytes 3981313 | tf_op jit(solution)/shard_map/jit(_where)/select_n | solution.py:163
  22.5 4.9 %fusion.8 = f32[896,1728]{0,1:T(8,128)} fusion(bf16[288,1728]{1,0:T(8,128)(2,1)S(1)} %get-tuple-element.49, bf16[288,1728]{1,0:T(8,128)(2,1)S(1)} %get-tuple-element.48, bf16[896,2,576]{0,2,1:T(8,128)(2,1)S(1)} %add_convert_fusion.1, s32[]{:T(128)S(6)} %select_n.191), kind=kOutput, calls=%fused_computation.20 | convolution fusion | flops 1787609088 | bytes 9289732 | tf_op jit(solution)/shard_map/dot_general | solution.py:168
  27.6 1.3 %broadcast_select_fusion.6 = f32[64]{0:T(128)S(1)} fusion(f32[]{:T(128)} %bitcast.26, f32[]{:T(128)} %bitcast.25), kind=kLoop, calls=%fused_computation.105 | loop fusion | flops 1280 | bytes 264 | tf_op jit(solution)/shard_map/jit(_where)/select_n | solution.py:251
  29.3 1.1 pad_maximum_fusion.1.refs_16_
  30.4 2.2 %slice_bitcast_fusion.1 = (bf16[192,1152]{1,0:T(8,128)(2,1)}, bf16[192,1152]{1,0:T(8,128)(2,1)}) fusion(bf16[1,1,896,1152]{3,2,1,0:T(8,128)(2,1)} %param.20), kind=kLoop, calls=%fused_computation.55 | loop fusion | bytes 1769472 | tf_op jit(solution)/shard_map/slice | solution.py:276
  33.0 1.1 collective-permute-start.4
  34.0 1.5 %broadcast_select_fusion.1 = (bf16[288,1728]{1,0:T(8,128)(2,1)S(1)}, bf16[288,1728]{1,0:T(8,128)(2,1)S(1)}) fusion(bf16[288,1728]{1,0:T(8,128)(2,1)} %collective-permute-done.1, bf16[288,1728]{1,0:T(8,128)(2,1)S(1)} %collective-permute-done.2, pred[]{:T(512)S(6)} %eq.206), kind=kLoop, calls=%fused_computation.47 | loop fusion | flops 995328 | bytes 3981313 | tf_op jit(solution)/shard_map/jit(_where)/select_n | solution.py:163
  35.6 2.9 %fusion.12 = f32[896,1728]{0,1:T(8,128)S(1)} fusion(bf16[288,1728]{1,0:T(8,128)(2,1)S(1)} %get-tuple-element.43, bf16[288,1728]{1,0:T(8,128)(2,1)S(1)} %get-tuple-element.42, bf16[896,2,576]{0,2,1:T(8,128)(2,1)S(1)} %copy-done.5, s32[]{:T(128)S(6)} %select_n.196), kind=kOutput, calls=%fused_computation.24 | convolution fusion | flops 1787609088 | bytes 9289732 | tf_op jit(solution)/shard_map/dot_general | solution.py:168
  38.5 0.8 add_convert_fusion
  39.3 1.6 %fusion.45 = (bf16[896,1,8,72]{0,3,2,1:T(8,128)(2,1)S(1)}, bf16[896,1,8,72]{0,3,2,1:T(8,128)(2,1)}, bf16[8,72,896]{2,1,0:T(8,128)(2,1)}) fusion(bf16[896,3,8,72]{0,3,2,1:T(8,128)(2,1)S(1)} %bitcast.68), kind=kLoop, calls=%fused_computation.112 | loop fusion | bytes 6193152 | tf_op jit(solution)/shard_map/slice | solution.py:199
  40.8 1.9 %copy.76 = bf16[896,1,8,72]{3,0,2,1:T(8,128)(2,1)S(1)} copy(bf16[896,1,8,72]{0,3,2,1:T(8,128)(2,1)} %get-tuple-element.38) | data formatting | bytes 2064384
  42.8 1.0 slice.170.refs_0_.refs_4_.refs_8_.refs_12_
  43.8 1.7 %copy.77 = bf16[896,1,8,72]{3,0,2,1:T(8,128)(2,1)} copy(bf16[896,1,8,72]{0,3,2,1:T(8,128)(2,1)S(1)} %get-tuple-element.37) | data formatting | bytes 2064384
  45.6 1.0 bitcast_dynamic-update-slice_fusion.3
  46.7 1.0 bitcast_dynamic-update-slice_fusion.2
  47.8 1.0 bitcast_dynamic-update-slice_fusion.1
  48.9 1.8 %copy.63.refs_3_.refs_7_.refs_11_.refs_15_ = bf16[576,1152]{1,0:T(8,128)(2,1)} copy(bf16[576,1152]{0,1:T(8,128)(2,1)S(1)} %bitcast.73) | data formatting | bytes 2654208 | tf_op jit(solution)/shard_map/reshape | solution.py:194
  50.7 16.9 %shard_map.199 = bf16[512,1152]{1,0:T(8,128)(2,1)} custom-call(bf16[8,512,72]{2,1,0:T(8,128)(2,1)} %slice.170.refs_0_.refs_4_.refs_8_.refs_12_, bf16[8,72,896]{2,1,0:T(8,128)(2,1)} %get-tuple-element.39.refs_1_.refs_5_.refs_9_.refs_13_, bf16[8,896,72]{2,1,0:T(8,128)(2,1)} %bitcast.53, bf16[576,1152]{1,0:T(8,128)(2,1)} %copy.63.refs_3_.refs_7_.refs_11_.refs_15_, ...), custom_call_target="tpu_custom_call" | custom-call | tf_op jit(solution)/shard_map/pallas_call | solution.py:88
  67.5 1.8 %convolution_convert_fusion = bf16[256,1152]{1,0:T(8,128)(2,1)S(1)} fusion(bf16[512,1152]{1,0:T(8,128)(2,1)} %shard_map.199, s32[256]{0:T(256)S(1)} %eq.221), kind=kOutput, calls=%fused_computation.15 | convolution fusion | flops 302415872 | bytes 1770496 | tf_op jit(solution)/shard_map/dot_general | solution.py:224
  69.4 1.1 collective-permute-start.6
  70.5 1.1 collective-permute-start.8
  71.6 1.0 collective-permute-start.9
  72.6 1.0 fusion.46
  73.6 9.1 %shard_map.200 = bf16[192,1152]{1,0:T(8,128)(2,1)} custom-call(bf16[8,192,72]{2,1,0:T(8,128)(2,1)} %get-tuple-element.23.refs_0_.refs_4_.refs_8_.refs_12_, bf16[8,72,896]{2,1,0:T(8,128)(2,1)} %get-tuple-element.39.refs_1_.refs_5_.refs_9_.refs_13_, bf16[8,896,72]{2,1,0:T(8,128)(2,1)} %bitcast.57, bf16[576,1152]{1,0:T(8,128)(2,1)} %copy.63.refs_3_.refs_7_.refs_11_.refs_15_, ...), custom_call_target="tpu_custom_call" | custom-call | tf_op jit(solution)/shard_map/pallas_call | solution.py:88
  82.8 0.7 fusion.4
  83.6 3.6 %collective-permute-start.10 = (bf16[256,1152]{1,0:T(8,128)(2,1)S(1)}, bf16[256,1152]{1,0:T(8,128)(2,1)S(1)}, u32[]{:S(2)}, u32[]{:S(2)}) collective-permute-start(bf16[256,1152]{1,0:T(8,128)(2,1)S(1)} %get-tuple-element.33), channel_id=1, source_target_pairs={{0,4},{4,8},{8,12},{1,5},{5,9},{9,13},{2,6},{6,10},{10,14},{3,7},{... | collective-permute-start | bytes 1769480 | tf_op jit(solution)/shard_map/ppermute | solution.py:269
  87.3 1.3 %collective-permute-start.11 = (bf16[256,1152]{1,0:T(8,128)(2,1)S(1)}, bf16[256,1152]{1,0:T(8,128)(2,1)S(1)}, u32[]{:S(2)}, u32[]{:S(2)}) collective-permute-start(bf16[256,1152]{1,0:T(8,128)(2,1)S(1)} %get-tuple-element.28), channel_id=1, source_target_pairs={{4,0},{8,4},{12,8},{5,1},{9,5},{13,9},{6,2},{10,6},{14,10},{7,3},{... | collective-permute-start | bytes 1769480 | tf_op jit(solution)/shard_map/ppermute | solution.py:270
  88.9 0.9 collective-permute-start.12
  89.8 1.1 collective-permute-start.14
  90.9 0.7 collective-permute-done.12
  91.6 1.2 %collective-permute-start.15 = (bf16[24,1152]{1,0:T(8,128)(2,1)S(1)}, bf16[24,1152]{1,0:T(8,128)(2,1)S(1)}, u32[]{:S(2)}, u32[]{:S(2)}) collective-permute-start(bf16[24,1152]{1,0:T(8,128)(2,1)S(1)} %get-tuple-element.63), channel_id=1, source_target_pairs={{0,2},{1,3},{2,0},{3,1},{4,6},{5,7},{6,4},{7,5},{8,10},{9,11},{10,... | collective-permute-start | bytes 165896 | tf_op jit(solution)/shard_map/ppermute | solution.py:233
  94.1 9.3 %shard_map.201 = bf16[192,1152]{1,0:T(8,128)(2,1)} custom-call(bf16[8,192,72]{2,1,0:T(8,128)(2,1)} %get-tuple-element.29.refs_0_.refs_4_.refs_8_.refs_12_, bf16[8,72,896]{2,1,0:T(8,128)(2,1)} %get-tuple-element.39.refs_1_.refs_5_.refs_9_.refs_13_, bf16[8,896,72]{2,1,0:T(8,128)(2,1)} %bitcast.61, bf16[576,1152]{1,0:T(8,128)(2,1)} %copy.63.refs_3_.refs_7_.refs_11_.refs_15_, ...), custom_call_target="tpu_custom_call" | custom-call | tf_op jit(solution)/shard_map/pallas_call | solution.py:88
  103.4 1.3 %collective-permute-done.11 = bf16[256,1152]{1,0:T(8,128)(2,1)S(1)} collective-permute-done((bf16[256,1152]{1,0:T(8,128)(2,1)S(1)}, bf16[256,1152]{1,0:T(8,128)(2,1)S(1)}, u32[]{:S(2)}, u32[]{:S(2)}) %collective-permute-start.11) | collective-permute-done | bytes 589856 | tf_op jit(solution)/shard_map/ppermute | solution.py:270
  104.7 1.3 %convolution_convert_fusion.1 = bf16[96,1152]{1,0:T(8,128)(2,1)S(1)} fusion(bf16[192,1152]{1,0:T(8,128)(2,1)} %shard_map.201, s32[96]{0:T(128)S(1)} %eq.225), kind=kOutput, calls=%fused_computation.17 | convolution fusion | flops 42596352 | bytes 663936 | tf_op jit(solution)/shard_map/dot_general | solution.py:224
  106.0 0.7 collective-permute-start.16
  106.7 0.9 collective-permute-start.18
  107.6 1.2 %collective-permute-start.19 = (bf16[24,1152]{1,0:T(8,128)(2,1)S(1)}, bf16[24,1152]{1,0:T(8,128)(2,1)S(1)}, u32[]{:S(2)}, u32[]{:S(2)}) collective-permute-start(bf16[24,1152]{1,0:T(8,128)(2,1)S(1)} %get-tuple-element.59), channel_id=1, source_target_pairs={{0,2},{1,3},{2,0},{3,1},{4,6},{5,7},{6,4},{7,5},{8,10},{9,11},{10,... | collective-permute-start | bytes 165896 | tf_op jit(solution)/shard_map/ppermute | solution.py:233
  110.3 1.1 collective-permute-done.18
  111.4 1.2 %collective-permute-done.19 = bf16[24,1152]{1,0:T(8,128)(2,1)S(1)} collective-permute-done((bf16[24,1152]{1,0:T(8,128)(2,1)S(1)}, bf16[24,1152]{1,0:T(8,128)(2,1)S(1)}, u32[]{:S(2)}, u32[]{:S(2)}) %collective-permute-start.19) | collective-permute-done | bytes 55328 | tf_op jit(solution)/shard_map/ppermute | solution.py:233
  113.0 1.5 %maximum_bitcast_fusion = bf16[1,1,896,1152]{3,2,1,0:T(8,128)(2,1)} fusion(bf16[256,1152]{1,0:T(8,128)(2,1)S(1)} %fusion.19, bf16[192,1152]{1,0:T(8,128)(2,1)S(1)} %fusion.25, bf16[192,1152]{1,0:T(8,128)(2,1)S(1)} %fusion.7, bf16[256,1152]{1,0:T(8,128)(2,1)S(1)} %fusion.17), kind=kLoop, calls=%fused_computation.28 | loop fusion | flops 8257536 | bytes 4128768 | tf_op jit(solution)/shard_map/reshape | solution.py:310
  (132 shorter events, 10.2 us)
Async XLA Ops:
  0.0 7.6 %copy-start = (s32[4,4,4]{2,1,0:T(4,128)S(1)}, s32[4,4,4]{2,1,0:T(4,128)}, u32[]{:S(2)}) copy-start(s32[4,4,4]{2,1,0:T(4,128)} %param.24) | copy-start | bytes 772
  0.0 20.5 %collective-permute-start = (bf16[288,1728]{1,0:T(8,128)(2,1)}, bf16[288,1728]{1,0:T(8,128)(2,1)}, u32[]{:S(2)}, u32[]{:S(2)}) collective-permute-start(bf16[288,1728]{1,0:T(8,128)(2,1)} %param.22), channel_id=1, source_target_pairs={{1,0},{0,1},{3,2},{2,3},{5,4},{4,5},{7,6},{6,7},{9,8},{8,9},{11,10... | collective-permute-start | bytes 2985992 | tf_op jit(solution)/shard_map/ppermute | solution.py:158
  0.5 27.0 %collective-permute-start.1 = (bf16[288,1728]{1,0:T(8,128)(2,1)}, bf16[288,1728]{1,0:T(8,128)(2,1)}, u32[]{:S(2)}, u32[]{:S(2)}) collective-permute-start(bf16[288,1728]{1,0:T(8,128)(2,1)} %param.22), channel_id=1, source_target_pairs={{2,0},{3,1},{0,2},{1,3},{6,4},{7,5},{4,6},{5,7},{10,8},{11,9},{8,1... | collective-permute-start | bytes 2985992 | tf_op jit(solution)/shard_map/ppermute | solution.py:158
  10.3 4.7 %copy-start.9 = (f32[3,1152]{1,0:T(4,128)S(1)}, f32[3,1152]{1,0:T(4,128)}, u32[]{:S(2)}) copy-start(f32[3,1152]{1,0:T(4,128)} %param.21) | copy-start | bytes 41476
  10.3 5.4 %copy-start.18 = (s32[4]{0:T(128)S(1)}, s32[4]{0:T(128)}, u32[]{:S(2)}) copy-start(s32[4]{0:T(128)} %constant.141.clone) | copy-start | bytes 52
  10.3 5.5 %copy-start.13 = (s32[4,64]{1,0:T(4,128)S(1)}, s32[4,64]{1,0:T(4,128)}, u32[]{:S(2)}) copy-start(s32[4,64]{1,0:T(4,128)} %constant.142.clone) | copy-start | bytes 3076
  10.3 5.5 %copy-start.14 = (s32[4,64]{1,0:T(4,128)S(1)}, s32[4,64]{1,0:T(4,128)}, u32[]{:S(2)}) copy-start(s32[4,64]{1,0:T(4,128)} %constant.143.clone) | copy-start | bytes 3076
  10.3 5.6 %copy-start.15 = (s32[4,64]{1,0:T(4,128)S(1)}, s32[4,64]{1,0:T(4,128)}, u32[]{:S(2)}) copy-start(s32[4,64]{1,0:T(4,128)} %constant.152) | copy-start | bytes 3076
  10.3 5.8 %copy-start.16 = (s32[2]{0:T(128)S(1)}, s32[2]{0:T(128)}, u32[]{:S(2)}) copy-start(s32[2]{0:T(128)} %param.25) | copy-start | bytes 28
  18.2 1.1 copy-start.2
  18.2 1.2 %copy-start.3 = (bf16[1,1,256,1152]{2,3,1,0:T(8,128)(2,1)S(1)}, bf16[1,1,256,1152]{2,3,1,0:T(8,128)(2,1)}, u32[]{:S(2)}) copy-start(bf16[1,1,256,1152]{2,3,1,0:T(8,128)(2,1)} %copy.57) | copy-start | bytes 1769476
  19.5 0.9 copy-start.11
  19.5 0.9 copy-start.12
  19.5 1.2 %copy-start.8 = (bf16[288,1728]{1,0:T(8,128)(2,1)S(1)}, bf16[288,1728]{1,0:T(8,128)(2,1)}, u32[]{:S(2)}) copy-start(bf16[288,1728]{1,0:T(8,128)(2,1)} %param.22) | copy-start | bytes 2985988
  20.4 2.1 %copy-start.4 = (bf16[896,2,576]{0,2,1:T(8,128)(2,1)}, bf16[896,2,576]{0,2,1:T(8,128)(2,1)S(1)}, u32[]{:S(2)}) copy-start(bf16[896,2,576]{0,2,1:T(8,128)(2,1)S(1)} %add_convert_fusion.1) | copy-start | bytes 6193156
  22.5 6.4 %copy-start.19 = (pred[64]{0:T(512)(128)(4,1)S(1)}, pred[64]{0:T(512)(128)(4,1)}, u32[]{:S(2)}) copy-start(pred[64]{0:T(512)(128)(4,1)} %constant.151) | copy-start | bytes 196
  22.5 6.7 %copy-start.17 = (s32[4]{0:T(128)S(1)}, s32[4]{0:T(128)}, u32[]{:S(2)}) copy-start(s32[4]{0:T(128)} %param.26) | copy-start | bytes 52
  27.4 5.2 %collective-permute-start.2 = (bf16[288,1728]{1,0:T(8,128)(2,1)}, bf16[288,1728]{1,0:T(8,128)(2,1)S(1)}, u32[]{:S(2)}, u32[]{:S(2)}) collective-permute-start(bf16[288,1728]{1,0:T(8,128)(2,1)} %collective-permute-done.1), channel_id=1, source_target_pairs={{1,0},{0,1},{3,2},{2,3},{5,4},{4,5},{7,6},{6,7},{9,8},{8,9},{11,10... | collective-permute-start | bytes 2985992 | tf_op jit(solution)/shard_map/ppermute | solution.py:158
  32.6 2.9 %copy-start.5 = (bf16[896,2,576]{0,2,1:T(8,128)(2,1)S(1)}, bf16[896,2,576]{0,2,1:T(8,128)(2,1)}, u32[]{:S(2)}) copy-start(bf16[896,2,576]{0,2,1:T(8,128)(2,1)} %copy-done.4) | copy-start | bytes 6193156
  32.6 14.1 %collective-permute-start.3 = (bf16[576,288]{0,1:T(8,128)(2,1)}, bf16[576,288]{0,1:T(8,128)(2,1)}, u32[]{:S(2)}, u32[]{:S(2)}) collective-permute-start(bf16[576,288]{0,1:T(8,128)(2,1)} %param.23), channel_id=1, source_target_pairs={{1,0},{0,1},{3,2},{2,3},{5,4},{4,5},{7,6},{6,7},{9,8},{8,9},{11,10... | collective-permute-start | bytes 995336 | tf_op jit(solution)/shard_map/ppermute | solution.py:104
  33.0 13.6 %collective-permute-start.4 = (bf16[576,288]{0,1:T(8,128)(2,1)}, bf16[576,288]{0,1:T(8,128)(2,1)}, u32[]{:S(2)}, u32[]{:S(2)}) collective-permute-start(bf16[576,288]{0,1:T(8,128)(2,1)} %param.23), channel_id=1, source_target_pairs={{2,0},{3,1},{0,2},{1,3},{6,4},{7,5},{4,6},{5,7},{10,8},{11,9},{8,1... | collective-permute-start | bytes 995336 | tf_op jit(solution)/shard_map/ppermute | solution.py:104
  34.0 4.4 %slice-start = ((s8[6193152]{0:T(1024)(128)(4,1)}), s8[4194304]{0:T(1024)(128)(4,1)S(1)}, s32[]{:S(2)}) async-start(s8[6193152]{0:T(1024)(128)(4,1)} %bitcast.71), calls=%async_computation | async-start | bytes 8388608
  35.6 2.9 %slice-start.1 = ((s8[6193152]{0:T(1024)(128)(4,1)}), s8[1998848]{0:T(1024)(128)(4,1)S(1)}, s32[]{:S(2)}) async-start(s8[6193152]{0:T(1024)(128)(4,1)} %bitcast.71), calls=%async_computation.1 | async-start | bytes 3997696
  46.6 2.2 %collective-permute-start.5 = (bf16[576,288]{0,1:T(8,128)(2,1)}, bf16[576,288]{0,1:T(8,128)(2,1)S(1)}, u32[]{:S(2)}, u32[]{:S(2)}) collective-permute-start(bf16[576,288]{0,1:T(8,128)(2,1)} %collective-permute-done.4), channel_id=1, source_target_pairs={{1,0},{0,1},{3,2},{2,3},{5,4},{4,5},{7,6},{6,7},{9,8},{8,9},{11,10... | collective-permute-start | bytes 995336 | tf_op jit(solution)/shard_map/ppermute | solution.py:104
  69.4 13.3 %collective-permute-start.6 = (bf16[64,1152]{1,0:T(8,128)(2,1)S(1)}, bf16[64,1152]{1,0:T(8,128)(2,1)S(1)}, u32[]{:S(2)}, u32[]{:S(2)}) collective-permute-start(bf16[64,1152]{1,0:T(8,128)(2,1)S(1)} %get-tuple-element.54), channel_id=1, source_target_pairs={{0,3},{1,0},{2,1},{3,2},{4,7},{5,4},{6,5},{7,6},{8,11},{9,8},{10,9... | collective-permute-start | bytes 442376 | tf_op jit(solution)/shard_map/ppermute | solution.py:233
  70.5 12.2 %collective-permute-start.7 = (bf16[64,1152]{1,0:T(8,128)(2,1)S(1)}, bf16[64,1152]{1,0:T(8,128)(2,1)S(1)}, u32[]{:S(2)}, u32[]{:S(2)}) collective-permute-start(bf16[64,1152]{1,0:T(8,128)(2,1)S(1)} %get-tuple-element.57), channel_id=1, source_target_pairs={{0,1},{1,2},{2,3},{3,0},{4,5},{5,6},{6,7},{7,4},{8,9},{9,10},{10,1... | collective-permute-start | bytes 442376 | tf_op jit(solution)/shard_map/ppermute | solution.py:233
  70.5 12.2 %collective-permute-start.8 = (bf16[64,1152]{1,0:T(8,128)(2,1)S(1)}, bf16[64,1152]{1,0:T(8,128)(2,1)S(1)}, u32[]{:S(2)}, u32[]{:S(2)}) collective-permute-start(bf16[64,1152]{1,0:T(8,128)(2,1)S(1)} %get-tuple-element.56), channel_id=1, source_target_pairs={{0,2},{1,3},{2,0},{3,1},{4,6},{5,7},{6,4},{7,5},{8,10},{9,11},{10,... | collective-permute-start | bytes 442376 | tf_op jit(solution)/shard_map/ppermute | solution.py:233
  71.6 11.1 %collective-permute-start.9 = (bf16[64,1152]{1,0:T(8,128)(2,1)S(1)}, bf16[64,1152]{1,0:T(8,128)(2,1)S(1)}, u32[]{:S(2)}, u32[]{:S(2)}) collective-permute-start(bf16[64,1152]{1,0:T(8,128)(2,1)S(1)} %get-tuple-element.55), channel_id=1, source_target_pairs={{0,2},{1,3},{2,0},{3,1},{4,6},{5,7},{6,4},{7,5},{8,10},{9,11},{10,... | collective-permute-start | bytes 442376 | tf_op jit(solution)/shard_map/ppermute | solution.py:233
  73.6 9.2 %copy-start.1 = (bf16[512,1152]{1,0:T(8,128)(2,1)S(1)}, bf16[512,1152]{1,0:T(8,128)(2,1)}, u32[]{:S(2)}) copy-start(bf16[512,1152]{1,0:T(8,128)(2,1)} %shard_map.199) | copy-start | bytes 3538948
  83.5 5.1 %copy-start.6 = (bf16[192,1152]{1,0:T(8,128)(2,1)S(1)}, bf16[192,1152]{1,0:T(8,128)(2,1)}, u32[]{:S(2)}) copy-start(bf16[192,1152]{1,0:T(8,128)(2,1)} %shard_map.200) | copy-start | bytes 1327108
  83.5 9.3 %copy-start.10 = (s32[4,24]{1,0:T(4,128)S(1)}, s32[4,24]{1,0:T(4,128)}, u32[]{:S(2)}) copy-start(s32[4,24]{1,0:T(4,128)} %constant.153) | copy-start | bytes 1156
  83.6 19.8 %collective-permute-start.10 = (bf16[256,1152]{1,0:T(8,128)(2,1)S(1)}, bf16[256,1152]{1,0:T(8,128)(2,1)S(1)}, u32[]{:S(2)}, u32[]{:S(2)}) collective-permute-start(bf16[256,1152]{1,0:T(8,128)(2,1)S(1)} %get-tuple-element.33), channel_id=1, source_target_pairs={{0,4},{4,8},{8,12},{1,5},{5,9},{9,13},{2,6},{6,10},{10,14},{3,7},{... | collective-permute-start | bytes 1769480 | tf_op jit(solution)/shard_map/ppermute | solution.py:269
  87.3 17.4 %collective-permute-start.11 = (bf16[256,1152]{1,0:T(8,128)(2,1)S(1)}, bf16[256,1152]{1,0:T(8,128)(2,1)S(1)}, u32[]{:S(2)}, u32[]{:S(2)}) collective-permute-start(bf16[256,1152]{1,0:T(8,128)(2,1)S(1)} %get-tuple-element.28), channel_id=1, source_target_pairs={{4,0},{8,4},{12,8},{5,1},{9,5},{13,9},{6,2},{10,6},{14,10},{7,3},{... | collective-permute-start | bytes 1769480 | tf_op jit(solution)/shard_map/ppermute | solution.py:270
  88.9 2.8 %collective-permute-start.12 = (bf16[24,1152]{1,0:T(8,128)(2,1)S(1)}, bf16[24,1152]{1,0:T(8,128)(2,1)S(1)}, u32[]{:S(2)}, u32[]{:S(2)}) collective-permute-start(bf16[24,1152]{1,0:T(8,128)(2,1)S(1)} %get-tuple-element.62), channel_id=1, source_target_pairs={{0,3},{1,0},{2,1},{3,2},{4,7},{5,4},{6,5},{7,6},{8,11},{9,8},{10,9... | collective-permute-start | bytes 165896 | tf_op jit(solution)/shard_map/ppermute | solution.py:233
  89.8 13.5 %collective-permute-start.13 = (bf16[24,1152]{1,0:T(8,128)(2,1)S(1)}, bf16[24,1152]{1,0:T(8,128)(2,1)S(1)}, u32[]{:S(2)}, u32[]{:S(2)}) collective-permute-start(bf16[24,1152]{1,0:T(8,128)(2,1)S(1)} %get-tuple-element.65), channel_id=1, source_target_pairs={{0,1},{1,2},{2,3},{3,0},{4,5},{5,6},{6,7},{7,4},{8,9},{9,10},{10,1... | collective-permute-start | bytes 165896 | tf_op jit(solution)/shard_map/ppermute | solution.py:233
  89.8 13.6 %collective-permute-start.14 = (bf16[24,1152]{1,0:T(8,128)(2,1)S(1)}, bf16[24,1152]{1,0:T(8,128)(2,1)S(1)}, u32[]{:S(2)}, u32[]{:S(2)}) collective-permute-start(bf16[24,1152]{1,0:T(8,128)(2,1)S(1)} %get-tuple-element.64), channel_id=1, source_target_pairs={{0,2},{1,3},{2,0},{3,1},{4,6},{5,7},{6,4},{7,5},{8,10},{9,11},{10,... | collective-permute-start | bytes 165896 | tf_op jit(solution)/shard_map/ppermute | solution.py:233
  91.6 11.7 %collective-permute-start.15 = (bf16[24,1152]{1,0:T(8,128)(2,1)S(1)}, bf16[24,1152]{1,0:T(8,128)(2,1)S(1)}, u32[]{:S(2)}, u32[]{:S(2)}) collective-permute-start(bf16[24,1152]{1,0:T(8,128)(2,1)S(1)} %get-tuple-element.63), channel_id=1, source_target_pairs={{0,2},{1,3},{2,0},{3,1},{4,6},{5,7},{6,4},{7,5},{8,10},{9,11},{10,... | collective-permute-start | bytes 165896 | tf_op jit(solution)/shard_map/ppermute | solution.py:233
  106.0 3.8 %collective-permute-start.16 = (bf16[24,1152]{1,0:T(8,128)(2,1)S(1)}, bf16[24,1152]{1,0:T(8,128)(2,1)S(1)}, u32[]{:S(2)}, u32[]{:S(2)}) collective-permute-start(bf16[24,1152]{1,0:T(8,128)(2,1)S(1)} %get-tuple-element.58), channel_id=1, source_target_pairs={{0,3},{1,0},{2,1},{3,2},{4,7},{5,4},{6,5},{7,6},{8,11},{9,8},{10,9... | collective-permute-start | bytes 165896 | tf_op jit(solution)/shard_map/ppermute | solution.py:233
  106.7 3.6 %collective-permute-start.17 = (bf16[24,1152]{1,0:T(8,128)(2,1)S(1)}, bf16[24,1152]{1,0:T(8,128)(2,1)S(1)}, u32[]{:S(2)}, u32[]{:S(2)}) collective-permute-start(bf16[24,1152]{1,0:T(8,128)(2,1)S(1)} %get-tuple-element.61), channel_id=1, source_target_pairs={{0,1},{1,2},{2,3},{3,0},{4,5},{5,6},{6,7},{7,4},{8,9},{9,10},{10,1... | collective-permute-start | bytes 165896 | tf_op jit(solution)/shard_map/ppermute | solution.py:233
  106.7 4.7 %collective-permute-start.18 = (bf16[24,1152]{1,0:T(8,128)(2,1)S(1)}, bf16[24,1152]{1,0:T(8,128)(2,1)S(1)}, u32[]{:S(2)}, u32[]{:S(2)}) collective-permute-start(bf16[24,1152]{1,0:T(8,128)(2,1)S(1)} %get-tuple-element.60), channel_id=1, source_target_pairs={{0,2},{1,3},{2,0},{3,1},{4,6},{5,7},{6,4},{7,5},{8,10},{9,11},{10,... | collective-permute-start | bytes 165896 | tf_op jit(solution)/shard_map/ppermute | solution.py:233
  107.6 5.0 %collective-permute-start.19 = (bf16[24,1152]{1,0:T(8,128)(2,1)S(1)}, bf16[24,1152]{1,0:T(8,128)(2,1)S(1)}, u32[]{:S(2)}, u32[]{:S(2)}) collective-permute-start(bf16[24,1152]{1,0:T(8,128)(2,1)S(1)} %get-tuple-element.59), channel_id=1, source_target_pairs={{0,2},{1,3},{2,0},{3,1},{4,6},{5,7},{6,4},{7,5},{8,10},{9,11},{10,... | collective-permute-start | bytes 165896 | tf_op jit(solution)/shard_map/ppermute | solution.py:233
  109.1 3.5 %copy-start.7 = (bf16[192,1152]{1,0:T(8,128)(2,1)S(1)}, bf16[192,1152]{1,0:T(8,128)(2,1)}, u32[]{:S(2)}) copy-start(bf16[192,1152]{1,0:T(8,128)(2,1)} %shard_map.201) | copy-start | bytes 1327108

commit v21 on v19

--- a/solution.py
+++ b/solution.py
@@ -66,9 +66,9 @@
         )
 
 
-def attend_project(queries, keys, values, w_out_full, block_in, gate):
+def attend_project(queries, keys, values, w_out_full, block_in, gate, chunk=None):
     heads, size, tokens = keys.shape
-    chunk = queries.shape[1]
+    chunk = queries.shape[1] if chunk is None else chunk
     width = block_in.shape[1]
     hb = HEADS_PER_STEP
     in_specs = []
@@ -90,7 +90,7 @@
         grid=(1, heads // hb),
         in_specs=in_specs,
         out_specs=pl.BlockSpec((chunk, width), lambda i, h: (i, 0)),
-        out_shape=jax.ShapeDtypeStruct(block_in.shape, block_in.dtype),
+        out_shape=jax.ShapeDtypeStruct((chunk, width), block_in.dtype),
         scratch_shapes=[pltpu.VMEM((chunk, width), jnp.float32)],
         compiler_params=pltpu.CompilerParams(dimension_semantics=("arbitrary", "arbitrary")),
     )(*operands, block_in, gate.reshape(1, width))
@@ -256,7 +256,7 @@
         mixed = jnp.where(dep >= 0, w_keep * own + w_take * partner, own)
         return mixed.reshape(tile_out.shape).astype(jnp.bfloat16)
 
-    tile_rim = tile_part(queries[:, : 2 * rim], block_in[: 2 * rim])
+    tile_rim = attend_project(queries, keys, values, w_out_full, block_in, gate, 2 * rim)
     outgoing_rim = strips_out(tile_rim)
     arrived_rim = strips_in(outgoing_rim)
     first_queries, outgoing_rim = lax.optimization_barrier(

time: 111 us -> 120 us (1.081)
  local copies, waits for them, and re-layouts: 27.1 us -> 31.6 us
  other arithmetic: 10.8 us -> 13.9 us
  waiting for transfers between devices: 4.97 us -> 7.72 us
  starting transfers between devices: 19.8 us -> 18.5 us
    ppermute x6, waiting for transfers between devices: 0.51 us -> 3.66 us  [fetch(): return lax.ppermute(x, 'face', [(src_of(i), i) for i in range(n)])]
    slice x2, local copies, waits for them, and re-layouts: 0.01 us -> 3.05 us  [per_device(): block_in[rim:tokens - rim]]
    dynamic_update_slice x4, local copies, waits for them, and re-layouts: 3.17 us -> 0.19 us  [per_device(): out_stack = lax.dynamic_update_index_in_dim(out_stack, piece, index, 0)]
    slice x2 -> x1, local copies, waits for them, and re-layouts: 0.51 us -> 2.12 us  [per_device(): block_in[tokens - rim:]]
    ppermute x6, starting transfers between devices: 5.1 us -> 3.67 us  [fetch(): return lax.ppermute(x, 'face', [(src_of(i), i) for i in range(n)])]
    reduce_sum x1, other arithmetic: 0.36 us -> 1.7 us  [modulate(): center = jnp.mean(values, axis=-1, keepdims=True)]
    slice x1, local copies, waits for them, and re-layouts: 1.01 us -> 2.24 us  [per_device(): tile_second = tile_part(second_queries, block_in[mid_a:])]
    unnamed x43 -> x58, local copies, waits for them, and re-layouts: 4.7 us -> 3.5 us
  transfers between devices with their start and end apart: 20 -> 20, of which waited for: 8 -> 7; matrix products, arithmetic and copies ran while one was open for 38% -> 42% of each run, Pallas kernels for 16% -> 15%
where the time goes in v21:
time: 120 us
  Pallas kernels  35.3 us (29%)
  local copies, waits for them, and re-layouts  31.6 us (26%)
  starting transfers between devices  18.5 us (15%)
  other arithmetic  13.9 us (12%)
  matrix products  12.1 us (10%)
  waiting for transfers between devices  7.72 us (6%)
    pallas_call x3, Pallas kernels, attend_project(): pl.pallas_call(attention_kernel, grid=(1, heads // hb), in_specs=in_specs...  35.3 us
    ppermute x12, starting transfers between devices, strips_in(): lax.ppermute(sent, 'face', [(i, (i + shift) % n) for i in range(n)])  9.85 us
    dot_general x2, matrix products, chip_part(): jnp.dot(lax.dynamic_index_in_dim(moved_chips, chip, 0, keepdims=False), w...  7.34 us
    slice x2, local copies, waits for them, and re-layouts, per_device(): block_in[:rim]  3.84 us
    ppermute x6, starting transfers between devices, fetch(): return lax.ppermute(x, 'face', [(src_of(i), i) for i in range(n)])  3.67 us
    ppermute x6, waiting for transfers between devices, fetch(): return lax.ppermute(x, 'face', [(src_of(i), i) for i in range(n)])  3.66 us
    ppermute x1, starting transfers between devices, per_device(): lower = lax.ppermute(high, 'tm', [(i, i + 1) for i in range(count - 1)])  3.66 us
    unnamed x58, local copies, waits for them, and re-layouts  3.5 us
  transfers between devices with their start and end apart: 20, of which 7 were waited for; matrix products, arithmetic and copies ran while one was open for 42% of the time, Pallas kernels for 15%

profile of v21, /device:TPU:0, one launch (start us, length us, event | category | flops | bytes accessed | tf_op | source)
XLA Modules:
  0.0 119.7 jit_solution(4628947932026509826)
XLA Ops:
  0.5 2.6 %collective-permute-start.1 = (bf16[288,1728]{1,0:T(8,128)(2,1)}, bf16[288,1728]{1,0:T(8,128)(2,1)}, u32[]{:S(2)}, u32[]{:S(2)}) collective-permute-start(bf16[288,1728]{1,0:T(8,128)(2,1)} %param.22), channel_id=1, source_target_pairs={{2,0},{3,1},{0,2},{1,3},{6,4},{7,5},{4,6},{5,7},{10,8},{11,9},{8,1... | collective-permute-start | bytes 2985992 | tf_op jit(solution)/shard_map/ppermute | solution.py:158
  3.0 2.5 %slice_bitcast_fusion.4 = (bf16[256,1152]{1,0:T(8,128)(2,1)S(1)}, bf16[256,1152]{1,0:T(8,128)(2,1)}, bf16[1,1,256,1152]{3,2,1,0:T(8,128)(2,1)}, bf16[1,1,256,1152]{3,2,1,0:T(8,128)(2,1)}) fusion(bf16[1,1,896,1152]{3,2,1,0:T(8,128)(2,1)} %param.20), kind=kLoop, calls=%fused_computation.103 | loop fusion | bytes 3538944 | tf_op jit(solution)/shard_map/slice | solution.py:150
  5.6 2.2 %slice_bitcast_fusion.5 = (bf16[384,1152]{1,0:T(8,128)(2,1)}, bf16[1,1,384,1152]{3,2,1,0:T(8,128)(2,1)S(1)}) fusion(bf16[1,1,896,1152]{3,2,1,0:T(8,128)(2,1)} %param.20), kind=kLoop, calls=%fused_computation.104 | loop fusion | bytes 2654208 | tf_op jit(solution)/shard_map/slice | solution.py:150
  7.8 0.8 slice_reduce_fusion.1
  8.5 0.8 fusion.36
  9.3 1.7 %convert_reduce_fusion = (f32[896]{0:T(1024)S(1)}, bf16[896,1152]{1,0:T(8,128)(2,1)S(1)}) fusion(bf16[384,1152]{1,0:T(8,128)(2,1)} %get-tuple-element.48, bf16[256,1152]{1,0:T(8,128)(2,1)} %get-tuple-element.45, bf16[256,1152]{1,0:T(8,128)(2,1)S(1)} %get-tuple-element.44), kind=kLoop, calls=%fused_computation.2 | loop fusion | flops 8256640 | bytes 4132352 | tf_op jit(solution)/shard_map/reduce_sum | solution.py:27
  11.9 1.2 %add_reduce_fusion = (f32[1152]{0:T(1024)}, f32[1152]{0:T(1024)}, f32[1,1152]{1,0:T(1,128)}) fusion(f32[3,1152]{1,0:T(4,128)S(1)} %copy-done.9), kind=kLoop, calls=%fused_computation.75 | loop fusion | flops 1152 | bytes 27648 | tf_op jit(solution)/shard_map/add | solution.py:30
  15.4 1.8 %broadcast_select_fusion.3 = f32[64]{0:T(128)} fusion(f32[]{:T(128)} %bitcast.18, f32[]{:T(128)} %bitcast.17), kind=kLoop, calls=%fused_computation.100 | loop fusion | flops 1280 | bytes 264 | tf_op jit(solution)/shard_map/jit(_where)/select_n | solution.py:251
  17.2 1.3 %copy.54 = bf16[1,1,256,1152]{2,3,1,0:T(8,128)(2,1)S(1)} copy(bf16[1,1,256,1152]{3,2,1,0:T(8,128)(2,1)} %get-tuple-element.47) | data formatting | bytes 1179648 | tf_op jit(solution)/shard_map/slice | solution.py:150
  18.5 2.1 %copy.55 = bf16[1,1,256,1152]{2,3,1,0:T(8,128)(2,1)} copy(bf16[1,1,256,1152]{3,2,1,0:T(8,128)(2,1)} %get-tuple-element.46) | data formatting | bytes 1179648 | tf_op jit(solution)/shard_map/slice | solution.py:150
  20.6 0.8 add.148
  21.5 0.8 mul.143
  22.3 0.8 copy.56
  23.1 1.9 %add_convert_fusion.1 = bf16[896,2,576]{0,2,1:T(8,128)(2,1)} fusion(bf16[384,2,576]{0,2,1:T(8,128)(2,1)S(1)} %bitcast.85, bf16[256,2,576]{0,2,1:T(8,128)(2,1)S(1)} %bitcast.87, bf16[256,2,576]{0,2,1:T(8,128)(2,1)S(1)} %bitcast.86, f32[2,576]{1,0:T(2,128)S(1)} %add.148, f32[2,576]{1,0:T(2,128)S(1)} %mul.143, f32[896]{0:T(1024)S(1)} %add_rsqrt_fusion, ...), kind=kLoop, calls=%fused_computation.5 | loop fusion | flops 11354112 | bytes 4145152 | tf_op jit(solution)/shard_map/convert_element_type | solution.py:30
  25.1 1.4 %broadcast.301.clone = bf16[2,288,1728]{2,1,0:T(8,128)(2,1)} broadcast(bf16[]{:T(256)} %constant.148.clone.1), dimensions={} | broadcast | bytes 1990658 | tf_op jit(solution)/shard_map/broadcast.10
  26.5 1.0 bitcast_dynamic-update-slice_fusion.3
  27.5 1.3 %broadcast_select_fusion.2 = f32[64]{0:T(128)S(1)} fusion(f32[]{:T(128)} %bitcast.32, f32[]{:T(128)} %bitcast.31), kind=kLoop, calls=%fused_computation.99 | loop fusion | flops 1280 | bytes 264 | tf_op jit(solution)/shard_map/jit(_where)/select_n | solution.py:252
  29.5 2.3 %bitcast_dynamic-update-slice_fusion.2 = bf16[2,288,1728]{2,1,0:T(8,128)(2,1)} fusion(bf16[2,288,1728]{2,1,0:T(8,128)(2,1)} %bitcast_dynamic-update-slice_fusion.3, s32[]{:T(128)S(6)} %select_n.183, bf16[288,1728]{1,0:T(8,128)(2,1)} %collective-permute-done), kind=kLoop, calls=%fused_computation.37 | loop fusion | bytes 2064388 | tf_op jit(solution)/shard_map/jit(dynamic_update_index_in_dim)/dynamic_update_slice | solution.py:165
  31.8 4.5 %fusion.14 = f32[896,1728]{0,1:T(8,128)S(1)} fusion(bf16[576,1728]{1,0:T(8,128)(2,1)} %bitcast.9, bf16[896,2,576]{0,2,1:T(8,128)(2,1)S(1)} %copy-done.4, s32[]{:T(128)S(6)} %select_n.180), kind=kOutput, calls=%fused_computation.39 | convolution fusion | flops 1783627776 | bytes 9216004 | tf_op jit(solution)/shard_map/dot_general | solution.py:169
  36.4 2.2 %slice_bitcast_fusion.1 = (bf16[192,1152]{1,0:T(8,128)(2,1)}, bf16[192,1152]{1,0:T(8,128)(2,1)}) fusion(bf16[1,1,896,1152]{3,2,1,0:T(8,128)(2,1)} %param.20), kind=kLoop, calls=%fused_computation.48 | loop fusion | bytes 1769472 | tf_op jit(solution)/shard_map/slice | solution.py:277
  38.8 1.3 %bitcast_dynamic-update-slice_fusion.1 = bf16[2,288,1728]{2,1,0:T(8,128)(2,1)S(1)} fusion(bf16[2,288,1728]{2,1,0:T(8,128)(2,1)S(1)} %broadcast.301, s32[]{:T(128)S(6)} %select_n.182, bf16[288,1728]{1,0:T(8,128)(2,1)} %collective-permute-done.1), kind=kLoop, calls=%fused_computation.34 | loop fusion | bytes 2027524 | tf_op jit(solution)/shard_map/jit(dynamic_update_index_in_dim)/dynamic_update_slice | solution.py:164
  40.7 2.9 %fusion.12 = f32[896,1728]{0,1:T(8,128)S(1)} fusion(bf16[576,1728]{1,0:T(8,128)(2,1)S(1)} %bitcast.88, bf16[896,2,576]{0,2,1:T(8,128)(2,1)S(1)} %copy-done.4, s32[]{:T(128)S(6)} %select_n.184), kind=kOutput, calls=%fused_computation.35 | convolution fusion | flops 1783627776 | bytes 9289732 | tf_op jit(solution)/shard_map/dot_general | solution.py:169
  43.6 0.8 add_convert_fusion
  44.4 1.2 %fusion.38 = (bf16[896,1,8,72]{0,3,2,1:T(8,128)(2,1)S(1)}, bf16[896,1,8,72]{0,3,2,1:T(8,128)(2,1)S(1)}, bf16[8,72,896]{2,1,0:T(8,128)(2,1)}) fusion(bf16[896,3,8,72]{0,3,2,1:T(8,128)(2,1)S(1)} %bitcast.83), kind=kLoop, calls=%fused_computation.105 | loop fusion | bytes 6193152 | tf_op jit(solution)/shard_map/slice | solution.py:200
  45.6 1.7 %copy.71 = bf16[896,1,8,72]{3,0,2,1:T(8,128)(2,1)} copy(bf16[896,1,8,72]{0,3,2,1:T(8,128)(2,1)S(1)} %get-tuple-element.40) | data formatting | bytes 2064384
  47.3 1.7 %copy.72 = bf16[896,1,8,72]{3,0,2,1:T(8,128)(2,1)} copy(bf16[896,1,8,72]{0,3,2,1:T(8,128)(2,1)S(1)} %get-tuple-element.39) | data formatting | bytes 2064384
  49.2 2.1 %collective-permute-done.4 = bf16[576,288]{0,1:T(8,128)(2,1)S(1)} collective-permute-done((bf16[576,288]{0,1:T(8,128)(2,1)S(1)}, bf16[576,288]{0,1:T(8,128)(2,1)S(1)}, u32[]{:S(2)}, u32[]{:S(2)}) %collective-permute-start.4) | collective-permute-done | bytes 331808 | tf_op jit(solution)/shard_map/ppermute | solution.py:104
  51.3 1.6 %collective-permute-done.5 = bf16[576,288]{0,1:T(8,128)(2,1)S(1)} collective-permute-done((bf16[576,288]{0,1:T(8,128)(2,1)S(1)}, bf16[576,288]{0,1:T(8,128)(2,1)S(1)}, u32[]{:S(2)}, u32[]{:S(2)}) %collective-permute-start.5) | collective-permute-done | bytes 331808 | tf_op jit(solution)/shard_map/ppermute | solution.py:104
  53.0 1.9 %copy.59.refs_3_.refs_7_.refs_11_.refs_15_ = bf16[576,1152]{1,0:T(8,128)(2,1)} copy(bf16[576,1152]{0,1:T(8,128)(2,1)S(1)} %bitcast.84) | data formatting | bytes 2654208 | tf_op jit(solution)/shard_map/reshape | solution.py:195
  54.8 16.9 %shard_map.199 = bf16[512,1152]{1,0:T(8,128)(2,1)} custom-call(bf16[8,896,72]{2,1,0:T(8,128)(2,1)} %bitcast.78, bf16[8,72,896]{2,1,0:T(8,128)(2,1)} %get-tuple-element.41.refs_1_.refs_5_.refs_9_.refs_13_, bf16[8,896,72]{2,1,0:T(8,128)(2,1)} %bitcast.66, bf16[576,1152]{1,0:T(8,128)(2,1)} %copy.59.refs_3_.refs_7_.refs_11_.refs_15_, ...), custom_call_target="tpu_custom_call" | custom-call | tf_op jit(solution)/shard_map/pallas_call | solution.py:88
  71.8 1.8 %convolution_convert_fusion = bf16[256,1152]{1,0:T(8,128)(2,1)S(1)} fusion(bf16[512,1152]{1,0:T(8,128)(2,1)} %shard_map.199, s32[256]{0:T(256)S(1)} %eq.214), kind=kOutput, calls=%fused_computation.15 | convolution fusion | flops 302415872 | bytes 1770496 | tf_op jit(solution)/shard_map/dot_general | solution.py:225
  74.2 1.3 %collective-permute-start.8 = (bf16[64,1152]{1,0:T(8,128)(2,1)S(1)}, bf16[64,1152]{1,0:T(8,128)(2,1)S(1)}, u32[]{:S(2)}, u32[]{:S(2)}) collective-permute-start(bf16[64,1152]{1,0:T(8,128)(2,1)S(1)} %get-tuple-element.56), channel_id=1, source_target_pairs={{0,2},{1,3},{2,0},{3,1},{4,6},{5,7},{6,4},{7,5},{8,10},{9,11},{10,... | collective-permute-start | bytes 442376 | tf_op jit(solution)/shard_map/ppermute | solution.py:234
  75.5 0.7 collective-permute-start.9
  76.2 2.1 %fusion.39 = (bf16[8,192,72]{2,1,0:T(8,128)(2,1)}, bf16[8,192,72]{2,1,0:T(8,128)(2,1)}) fusion(bf16[8,896,72]{2,1,0:T(8,128)(2,1)} %bitcast.82), kind=kLoop, calls=%fused_computation.106 | loop fusion | bytes 884736 | tf_op jit(solution)/shard_map/slice | solution.py:263
  78.3 9.1 %shard_map.200 = bf16[192,1152]{1,0:T(8,128)(2,1)} custom-call(bf16[8,192,72]{2,1,0:T(8,128)(2,1)} %get-tuple-element.23.refs_0_.refs_4_.refs_8_.refs_12_, bf16[8,72,896]{2,1,0:T(8,128)(2,1)} %get-tuple-element.41.refs_1_.refs_5_.refs_9_.refs_13_, bf16[8,896,72]{2,1,0:T(8,128)(2,1)} %bitcast.70, bf16[576,1152]{1,0:T(8,128)(2,1)} %copy.59.refs_3_.refs_7_.refs_11_.refs_15_, ...), custom_call_target="tpu_custom_call" | custom-call | tf_op jit(solution)/shard_map/pallas_call | solution.py:88
  87.5 0.7 fusion.4
  88.4 3.7 %collective-permute-start.10 = (bf16[256,1152]{1,0:T(8,128)(2,1)S(1)}, bf16[256,1152]{1,0:T(8,128)(2,1)S(1)}, u32[]{:S(2)}, u32[]{:S(2)}) collective-permute-start(bf16[256,1152]{1,0:T(8,128)(2,1)S(1)} %get-tuple-element.33), channel_id=1, source_target_pairs={{0,4},{4,8},{8,12},{1,5},{5,9},{9,13},{2,6},{6,10},{10,14},{3,7},{... | collective-permute-start | bytes 1769480 | tf_op jit(solution)/shard_map/ppermute | solution.py:270
  92.0 1.3 %collective-permute-start.11 = (bf16[256,1152]{1,0:T(8,128)(2,1)S(1)}, bf16[256,1152]{1,0:T(8,128)(2,1)S(1)}, u32[]{:S(2)}, u32[]{:S(2)}) collective-permute-start(bf16[256,1152]{1,0:T(8,128)(2,1)S(1)} %get-tuple-element.28), channel_id=1, source_target_pairs={{4,0},{8,4},{12,8},{5,1},{9,5},{13,9},{6,2},{10,6},{14,10},{7,3},{... | collective-permute-start | bytes 1769480 | tf_op jit(solution)/shard_map/ppermute | solution.py:271
  94.4 1.5 %collective-permute-start.14 = (bf16[24,1152]{1,0:T(8,128)(2,1)S(1)}, bf16[24,1152]{1,0:T(8,128)(2,1)S(1)}, u32[]{:S(2)}, u32[]{:S(2)}) collective-permute-start(bf16[24,1152]{1,0:T(8,128)(2,1)S(1)} %get-tuple-element.64), channel_id=1, source_target_pairs={{0,2},{1,3},{2,0},{3,1},{4,6},{5,7},{6,4},{7,5},{8,10},{9,11},{10,... | collective-permute-start | bytes 165896 | tf_op jit(solution)/shard_map/ppermute | solution.py:234
  96.2 1.9 %collective-permute-start.15 = (bf16[24,1152]{1,0:T(8,128)(2,1)S(1)}, bf16[24,1152]{1,0:T(8,128)(2,1)S(1)}, u32[]{:S(2)}, u32[]{:S(2)}) collective-permute-start(bf16[24,1152]{1,0:T(8,128)(2,1)S(1)} %get-tuple-element.63), channel_id=1, source_target_pairs={{0,2},{1,3},{2,0},{3,1},{4,6},{5,7},{6,4},{7,5},{8,10},{9,11},{10,... | collective-permute-start | bytes 165896 | tf_op jit(solution)/shard_map/ppermute | solution.py:234
  99.4 9.3 %shard_map.201 = bf16[192,1152]{1,0:T(8,128)(2,1)} custom-call(bf16[8,192,72]{2,1,0:T(8,128)(2,1)} %get-tuple-element.29.refs_0_.refs_4_.refs_8_.refs_12_, bf16[8,72,896]{2,1,0:T(8,128)(2,1)} %get-tuple-element.41.refs_1_.refs_5_.refs_9_.refs_13_, bf16[8,896,72]{2,1,0:T(8,128)(2,1)} %bitcast.74, bf16[576,1152]{1,0:T(8,128)(2,1)} %copy.59.refs_3_.refs_7_.refs_11_.refs_15_, ...), custom_call_target="tpu_custom_call" | custom-call | tf_op jit(solution)/shard_map/pallas_call | solution.py:88
  108.7 1.0 collective-permute-done.11
  109.7 1.3 %convolution_convert_fusion.1 = bf16[96,1152]{1,0:T(8,128)(2,1)S(1)} fusion(bf16[192,1152]{1,0:T(8,128)(2,1)} %shard_map.201, s32[96]{0:T(128)S(1)} %eq.218), kind=kOutput, calls=%fused_computation.17 | convolution fusion | flops 42596352 | bytes 663936 | tf_op jit(solution)/shard_map/dot_general | solution.py:225
  111.0 1.0 collective-permute-start.16
  112.5 1.6 %collective-permute-start.19 = (bf16[24,1152]{1,0:T(8,128)(2,1)S(1)}, bf16[24,1152]{1,0:T(8,128)(2,1)S(1)}, u32[]{:S(2)}, u32[]{:S(2)}) collective-permute-start(bf16[24,1152]{1,0:T(8,128)(2,1)S(1)} %get-tuple-element.59), channel_id=1, source_target_pairs={{0,2},{1,3},{2,0},{3,1},{4,6},{5,7},{6,4},{7,5},{8,10},{9,11},{10,... | collective-permute-start | bytes 165896 | tf_op jit(solution)/shard_map/ppermute | solution.py:234
  115.6 1.1 collective-permute-done.18
  116.7 1.2 collective-permute-done.19
  118.3 1.5 %maximum_bitcast_fusion = bf16[1,1,896,1152]{3,2,1,0:T(8,128)(2,1)} fusion(bf16[256,1152]{1,0:T(8,128)(2,1)S(1)} %fusion.11, bf16[192,1152]{1,0:T(8,128)(2,1)S(1)} %fusion.19, bf16[192,1152]{1,0:T(8,128)(2,1)S(1)} %fusion.7, bf16[256,1152]{1,0:T(8,128)(2,1)S(1)} %fusion.9), kind=kLoop, calls=%fused_computation.20 | loop fusion | flops 8257536 | bytes 4128768 | tf_op jit(solution)/shard_map/reshape | solution.py:311
  (143 shorter events, 11.1 us)
Async XLA Ops:
  0.0 7.8 %copy-start = (s32[4,4,4]{2,1,0:T(4,128)S(1)}, s32[4,4,4]{2,1,0:T(4,128)}, u32[]{:S(2)}) copy-start(s32[4,4,4]{2,1,0:T(4,128)} %param.24) | copy-start | bytes 772
  0.0 29.5 %collective-permute-start = (bf16[288,1728]{1,0:T(8,128)(2,1)}, bf16[288,1728]{1,0:T(8,128)(2,1)}, u32[]{:S(2)}, u32[]{:S(2)}) collective-permute-start(bf16[288,1728]{1,0:T(8,128)(2,1)} %param.22), channel_id=1, source_target_pairs={{1,0},{0,1},{3,2},{2,3},{5,4},{4,5},{7,6},{6,7},{9,8},{8,9},{11,10... | collective-permute-start | bytes 2985992 | tf_op jit(solution)/shard_map/ppermute | solution.py:158
  0.5 35.8 %collective-permute-start.1 = (bf16[288,1728]{1,0:T(8,128)(2,1)}, bf16[288,1728]{1,0:T(8,128)(2,1)}, u32[]{:S(2)}, u32[]{:S(2)}) collective-permute-start(bf16[288,1728]{1,0:T(8,128)(2,1)} %param.22), channel_id=1, source_target_pairs={{2,0},{3,1},{0,2},{1,3},{6,4},{7,5},{4,6},{5,7},{10,8},{11,9},{8,1... | collective-permute-start | bytes 2985992 | tf_op jit(solution)/shard_map/ppermute | solution.py:158
  11.0 9.6 %copy-start.1 = (bf16[896,1152]{1,0:T(8,128)(2,1)}, bf16[896,1152]{1,0:T(8,128)(2,1)S(1)}, u32[]{:S(2)}) copy-start(bf16[896,1152]{1,0:T(8,128)(2,1)S(1)} %get-tuple-element.38.refs_16_) | copy-start | bytes 6193156
  11.0 0.8 copy-start.9
  11.0 2.0 %copy-start.24 = (s32[2]{0:T(128)S(1)}, s32[2]{0:T(128)}, u32[]{:S(2)}) copy-start(s32[2]{0:T(128)} %param.25) | copy-start | bytes 28
  11.0 2.1 %copy-start.22 = (s32[4]{0:T(128)S(1)}, s32[4]{0:T(128)}, u32[]{:S(2)}) copy-start(s32[4]{0:T(128)} %slice_reduce_fusion.1) | copy-start | bytes 52
  11.0 2.1 %copy-start.26 = (s32[4]{0:T(128)S(1)}, s32[4]{0:T(128)}, u32[]{:S(2)}) copy-start(s32[4]{0:T(128)} %constant.153.clone) | copy-start | bytes 52
  11.1 2.9 %copy-start.15 = (pred[4]{0:T(512)(128)(4,1)S(1)}, pred[4]{0:T(512)(128)(4,1)}, u32[]{:S(2)}) copy-start(pred[4]{0:T(512)(128)(4,1)} %fusion.36) | copy-start | bytes 16
  11.1 2.9 %copy-start.20 = (s32[4,64]{1,0:T(4,128)S(1)}, s32[4,64]{1,0:T(4,128)}, u32[]{:S(2)}) copy-start(s32[4,64]{1,0:T(4,128)} %constant.154.clone) | copy-start | bytes 3076
  11.1 2.8 %copy-start.21 = (s32[4,64]{1,0:T(4,128)S(1)}, s32[4,64]{1,0:T(4,128)}, u32[]{:S(2)}) copy-start(s32[4,64]{1,0:T(4,128)} %constant.155.clone) | copy-start | bytes 3076
  11.1 2.9 %copy-start.18 = (s32[4,24]{1,0:T(4,128)S(1)}, s32[4,24]{1,0:T(4,128)}, u32[]{:S(2)}) copy-start(s32[4,24]{1,0:T(4,128)} %constant.158.clone) | copy-start | bytes 1156
  11.1 2.9 %copy-start.19 = (s32[4,24]{1,0:T(4,128)S(1)}, s32[4,24]{1,0:T(4,128)}, u32[]{:S(2)}) copy-start(s32[4,24]{1,0:T(4,128)} %constant.159.clone) | copy-start | bytes 1156
  11.1 3.6 %copy-start.23 = (s32[4,64]{1,0:T(4,128)S(1)}, s32[4,64]{1,0:T(4,128)}, u32[]{:S(2)}) copy-start(s32[4,64]{1,0:T(4,128)} %constant.164) | copy-start | bytes 3076
  13.2 4.0 %copy-start.13 = (pred[4,4]{1,0:T(4,128)(4,1)}, pred[4,4]{1,0:T(4,128)(4,1)S(1)}, u32[]{:S(2)}) copy-start(pred[4,4]{1,0:T(4,128)(4,1)S(1)} %get-tuple-element.71) | copy-start | bytes 52
  20.6 2.5 %copy-start.3 = (bf16[1,1,256,1152]{2,3,1,0:T(8,128)(2,1)S(1)}, bf16[1,1,256,1152]{2,3,1,0:T(8,128)(2,1)}, u32[]{:S(2)}) copy-start(bf16[1,1,256,1152]{2,3,1,0:T(8,128)(2,1)} %copy.55) | copy-start | bytes 1769476
  25.0 1.5 %copy-start.7 = (bf16[288,1728]{1,0:T(8,128)(2,1)S(1)}, bf16[288,1728]{1,0:T(8,128)(2,1)}, u32[]{:S(2)}) copy-start(bf16[288,1728]{1,0:T(8,128)(2,1)} %param.22) | copy-start | bytes 2985988
  25.0 3.9 %copy-start.12 = (s32[4,64]{1,0:T(4,128)S(1)}, s32[4,64]{1,0:T(4,128)}, u32[]{:S(2)}) copy-start(s32[4,64]{1,0:T(4,128)} %get-tuple-element.79) | copy-start | bytes 3076
  25.0 3.9 %copy-start.11 = (s32[4,64]{1,0:T(4,128)S(1)}, s32[4,64]{1,0:T(4,128)}, u32[]{:S(2)}) copy-start(s32[4,64]{1,0:T(4,128)} %get-tuple-element.80) | copy-start | bytes 3076
  25.0 4.0 %copy-start.16 = (f32[64]{0:T(128)S(1)}, f32[64]{0:T(128)}, u32[]{:S(2)}) copy-start(f32[64]{0:T(128)} %broadcast_select_fusion.3) | copy-start | bytes 772
  25.0 4.2 %copy-start.27 = (pred[64]{0:T(512)(128)(4,1)S(1)}, pred[64]{0:T(512)(128)(4,1)}, u32[]{:S(2)}) copy-start(pred[64]{0:T(512)(128)(4,1)} %constant.163) | copy-start | bytes 196
  25.0 4.3 %copy-start.10 = (s32[4,24]{1,0:T(4,128)S(1)}, s32[4,24]{1,0:T(4,128)}, u32[]{:S(2)}) copy-start(s32[4,24]{1,0:T(4,128)} %select_reduce_fusion.1) | copy-start | bytes 1156
  25.0 4.3 %copy-start.25 = (s32[4]{0:T(128)S(1)}, s32[4]{0:T(128)}, u32[]{:S(2)}) copy-start(s32[4]{0:T(128)} %param.26) | copy-start | bytes 52
  26.5 5.2 %copy-start.4 = (bf16[896,2,576]{0,2,1:T(8,128)(2,1)S(1)}, bf16[896,2,576]{0,2,1:T(8,128)(2,1)}, u32[]{:S(2)}) copy-start(bf16[896,2,576]{0,2,1:T(8,128)(2,1)} %add_convert_fusion.1) | copy-start | bytes 6193156
  36.2 3.9 %collective-permute-start.2 = (bf16[288,1728]{1,0:T(8,128)(2,1)}, bf16[288,1728]{1,0:T(8,128)(2,1)S(1)}, u32[]{:S(2)}, u32[]{:S(2)}) collective-permute-start(bf16[288,1728]{1,0:T(8,128)(2,1)} %collective-permute-done.1), channel_id=1, source_target_pairs={{1,0},{0,1},{3,2},{2,3},{5,4},{4,5},{7,6},{6,7},{9,8},{8,9},{11,10... | collective-permute-start | bytes 2985992 | tf_op jit(solution)/shard_map/ppermute | solution.py:158
  38.7 1.5 %copy-start.8 = (bf16[576,288]{0,1:T(8,128)(2,1)S(1)}, bf16[576,288]{0,1:T(8,128)(2,1)}, u32[]{:S(2)}) copy-start(bf16[576,288]{0,1:T(8,128)(2,1)} %param.23) | copy-start | bytes 995332
  40.2 11.1 %collective-permute-start.3 = (bf16[576,288]{0,1:T(8,128)(2,1)S(1)}, bf16[576,288]{0,1:T(8,128)(2,1)S(1)}, u32[]{:S(2)}, u32[]{:S(2)}) collective-permute-start(bf16[576,288]{0,1:T(8,128)(2,1)S(1)} %copy-done.8), channel_id=1, source_target_pairs={{1,0},{0,1},{3,2},{2,3},{5,4},{4,5},{7,6},{6,7},{9,8},{8,9},{11,10... | collective-permute-start | bytes 995336 | tf_op jit(solution)/shard_map/ppermute | solution.py:104
  40.6 10.6 %collective-permute-start.4 = (bf16[576,288]{0,1:T(8,128)(2,1)S(1)}, bf16[576,288]{0,1:T(8,128)(2,1)S(1)}, u32[]{:S(2)}, u32[]{:S(2)}) collective-permute-start(bf16[576,288]{0,1:T(8,128)(2,1)S(1)} %copy-done.8), channel_id=1, source_target_pairs={{2,0},{3,1},{0,2},{1,3},{6,4},{7,5},{4,6},{5,7},{10,8},{11,9},{8,1... | collective-permute-start | bytes 995336 | tf_op jit(solution)/shard_map/ppermute | solution.py:104
  51.2 1.7 %collective-permute-start.5 = (bf16[576,288]{0,1:T(8,128)(2,1)S(1)}, bf16[576,288]{0,1:T(8,128)(2,1)S(1)}, u32[]{:S(2)}, u32[]{:S(2)}) collective-permute-start(bf16[576,288]{0,1:T(8,128)(2,1)S(1)} %collective-permute-done.4), channel_id=1, source_target_pairs={{1,0},{0,1},{3,2},{2,3},{5,4},{4,5},{7,6},{6,7},{9,8},{8,9},{11,10... | collective-permute-start | bytes 995336 | tf_op jit(solution)/shard_map/ppermute | solution.py:104
  73.6 13.8 %collective-permute-start.6 = (bf16[64,1152]{1,0:T(8,128)(2,1)S(1)}, bf16[64,1152]{1,0:T(8,128)(2,1)S(1)}, u32[]{:S(2)}, u32[]{:S(2)}) collective-permute-start(bf16[64,1152]{1,0:T(8,128)(2,1)S(1)} %get-tuple-element.54), channel_id=1, source_target_pairs={{0,3},{1,0},{2,1},{3,2},{4,7},{5,4},{6,5},{7,6},{8,11},{9,8},{10,9... | collective-permute-start | bytes 442376 | tf_op jit(solution)/shard_map/ppermute | solution.py:234
  73.7 13.7 %collective-permute-start.7 = (bf16[64,1152]{1,0:T(8,128)(2,1)S(1)}, bf16[64,1152]{1,0:T(8,128)(2,1)S(1)}, u32[]{:S(2)}, u32[]{:S(2)}) collective-permute-start(bf16[64,1152]{1,0:T(8,128)(2,1)S(1)} %get-tuple-element.57), channel_id=1, source_target_pairs={{0,1},{1,2},{2,3},{3,0},{4,5},{5,6},{6,7},{7,4},{8,9},{9,10},{10,1... | collective-permute-start | bytes 442376 | tf_op jit(solution)/shard_map/ppermute | solution.py:234
  74.2 13.2 %collective-permute-start.8 = (bf16[64,1152]{1,0:T(8,128)(2,1)S(1)}, bf16[64,1152]{1,0:T(8,128)(2,1)S(1)}, u32[]{:S(2)}, u32[]{:S(2)}) collective-permute-start(bf16[64,1152]{1,0:T(8,128)(2,1)S(1)} %get-tuple-element.56), channel_id=1, source_target_pairs={{0,2},{1,3},{2,0},{3,1},{4,6},{5,7},{6,4},{7,5},{8,10},{9,11},{10,... | collective-permute-start | bytes 442376 | tf_op jit(solution)/shard_map/ppermute | solution.py:234
  75.5 11.9 %collective-permute-start.9 = (bf16[64,1152]{1,0:T(8,128)(2,1)S(1)}, bf16[64,1152]{1,0:T(8,128)(2,1)S(1)}, u32[]{:S(2)}, u32[]{:S(2)}) collective-permute-start(bf16[64,1152]{1,0:T(8,128)(2,1)S(1)} %get-tuple-element.55), channel_id=1, source_target_pairs={{0,2},{1,3},{2,0},{3,1},{4,6},{5,7},{6,4},{7,5},{8,10},{9,11},{10,... | collective-permute-start | bytes 442376 | tf_op jit(solution)/shard_map/ppermute | solution.py:234
  78.3 9.2 %copy-start.2 = (bf16[512,1152]{1,0:T(8,128)(2,1)S(1)}, bf16[512,1152]{1,0:T(8,128)(2,1)}, u32[]{:S(2)}) copy-start(bf16[512,1152]{1,0:T(8,128)(2,1)} %shard_map.199) | copy-start | bytes 3538948
  88.2 5.1 %copy-start.5 = (bf16[192,1152]{1,0:T(8,128)(2,1)S(1)}, bf16[192,1152]{1,0:T(8,128)(2,1)}, u32[]{:S(2)}) copy-start(bf16[192,1152]{1,0:T(8,128)(2,1)} %shard_map.200) | copy-start | bytes 1327108
  88.3 9.9 %copy-start.14 = (pred[4,4]{1,0:T(4,128)(4,1)S(1)}, pred[4,4]{1,0:T(4,128)(4,1)}, u32[]{:S(2)}) copy-start(pred[4,4]{1,0:T(4,128)(4,1)} %copy-done.13) | copy-start | bytes 52
  88.3 9.9 %copy-start.17 = (s32[4,24]{1,0:T(4,128)S(1)}, s32[4,24]{1,0:T(4,128)}, u32[]{:S(2)}) copy-start(s32[4,24]{1,0:T(4,128)} %constant.165) | copy-start | bytes 1156
  88.4 20.3 %collective-permute-start.10 = (bf16[256,1152]{1,0:T(8,128)(2,1)S(1)}, bf16[256,1152]{1,0:T(8,128)(2,1)S(1)}, u32[]{:S(2)}, u32[]{:S(2)}) collective-permute-start(bf16[256,1152]{1,0:T(8,128)(2,1)S(1)} %get-tuple-element.33), channel_id=1, source_target_pairs={{0,4},{4,8},{8,12},{1,5},{5,9},{9,13},{2,6},{6,10},{10,14},{3,7},{... | collective-permute-start | bytes 1769480 | tf_op jit(solution)/shard_map/ppermute | solution.py:270
  92.0 17.6 %collective-permute-start.11 = (bf16[256,1152]{1,0:T(8,128)(2,1)S(1)}, bf16[256,1152]{1,0:T(8,128)(2,1)S(1)}, u32[]{:S(2)}, u32[]{:S(2)}) collective-permute-start(bf16[256,1152]{1,0:T(8,128)(2,1)S(1)} %get-tuple-element.28), channel_id=1, source_target_pairs={{4,0},{8,4},{12,8},{5,1},{9,5},{13,9},{6,2},{10,6},{14,10},{7,3},{... | collective-permute-start | bytes 1769480 | tf_op jit(solution)/shard_map/ppermute | solution.py:271
  93.7 2.5 %collective-permute-start.12 = (bf16[24,1152]{1,0:T(8,128)(2,1)S(1)}, bf16[24,1152]{1,0:T(8,128)(2,1)S(1)}, u32[]{:S(2)}, u32[]{:S(2)}) collective-permute-start(bf16[24,1152]{1,0:T(8,128)(2,1)S(1)} %get-tuple-element.62), channel_id=1, source_target_pairs={{0,3},{1,0},{2,1},{3,2},{4,7},{5,4},{6,5},{7,6},{8,11},{9,8},{10,9... | collective-permute-start | bytes 165896 | tf_op jit(solution)/shard_map/ppermute | solution.py:234
  94.4 14.3 %collective-permute-start.13 = (bf16[24,1152]{1,0:T(8,128)(2,1)S(1)}, bf16[24,1152]{1,0:T(8,128)(2,1)S(1)}, u32[]{:S(2)}, u32[]{:S(2)}) collective-permute-start(bf16[24,1152]{1,0:T(8,128)(2,1)S(1)} %get-tuple-element.65), channel_id=1, source_target_pairs={{0,1},{1,2},{2,3},{3,0},{4,5},{5,6},{6,7},{7,4},{8,9},{9,10},{10,1... | collective-permute-start | bytes 165896 | tf_op jit(solution)/shard_map/ppermute | solution.py:234
  94.4 14.3 %collective-permute-start.14 = (bf16[24,1152]{1,0:T(8,128)(2,1)S(1)}, bf16[24,1152]{1,0:T(8,128)(2,1)S(1)}, u32[]{:S(2)}, u32[]{:S(2)}) collective-permute-start(bf16[24,1152]{1,0:T(8,128)(2,1)S(1)} %get-tuple-element.64), channel_id=1, source_target_pairs={{0,2},{1,3},{2,0},{3,1},{4,6},{5,7},{6,4},{7,5},{8,10},{9,11},{10,... | collective-permute-start | bytes 165896 | tf_op jit(solution)/shard_map/ppermute | solution.py:234
  96.2 12.5 %collective-permute-start.15 = (bf16[24,1152]{1,0:T(8,128)(2,1)S(1)}, bf16[24,1152]{1,0:T(8,128)(2,1)S(1)}, u32[]{:S(2)}, u32[]{:S(2)}) collective-permute-start(bf16[24,1152]{1,0:T(8,128)(2,1)S(1)} %get-tuple-element.63), channel_id=1, source_target_pairs={{0,2},{1,3},{2,0},{3,1},{4,6},{5,7},{6,4},{7,5},{8,10},{9,11},{10,... | collective-permute-start | bytes 165896 | tf_op jit(solution)/shard_map/ppermute | solution.py:234
  111.0 4.1 %collective-permute-start.16 = (bf16[24,1152]{1,0:T(8,128)(2,1)S(1)}, bf16[24,1152]{1,0:T(8,128)(2,1)S(1)}, u32[]{:S(2)}, u32[]{:S(2)}) collective-permute-start(bf16[24,1152]{1,0:T(8,128)(2,1)S(1)} %get-tuple-element.58), channel_id=1, source_target_pairs={{0,3},{1,0},{2,1},{3,2},{4,7},{5,4},{6,5},{7,6},{8,11},{9,8},{10,9... | collective-permute-start | bytes 165896 | tf_op jit(solution)/shard_map/ppermute | solution.py:234
  112.0 3.6 %collective-permute-start.17 = (bf16[24,1152]{1,0:T(8,128)(2,1)S(1)}, bf16[24,1152]{1,0:T(8,128)(2,1)S(1)}, u32[]{:S(2)}, u32[]{:S(2)}) collective-permute-start(bf16[24,1152]{1,0:T(8,128)(2,1)S(1)} %get-tuple-element.61), channel_id=1, source_target_pairs={{0,1},{1,2},{2,3},{3,0},{4,5},{5,6},{6,7},{7,4},{8,9},{9,10},{10,1... | collective-permute-start | bytes 165896 | tf_op jit(solution)/shard_map/ppermute | solution.py:234
  112.0 4.7 %collective-permute-start.18 = (bf16[24,1152]{1,0:T(8,128)(2,1)S(1)}, bf16[24,1152]{1,0:T(8,128)(2,1)S(1)}, u32[]{:S(2)}, u32[]{:S(2)}) collective-permute-start(bf16[24,1152]{1,0:T(8,128)(2,1)S(1)} %get-tuple-element.60), channel_id=1, source_target_pairs={{0,2},{1,3},{2,0},{3,1},{4,6},{5,7},{6,4},{7,5},{8,10},{9,11},{10,... | collective-permute-start | bytes 165896 | tf_op jit(solution)/shard_map/ppermute | solution.py:234
  112.5 5.4 %collective-permute-start.19 = (bf16[24,1152]{1,0:T(8,128)(2,1)S(1)}, bf16[24,1152]{1,0:T(8,128)(2,1)S(1)}, u32[]{:S(2)}, u32[]{:S(2)}) collective-permute-start(bf16[24,1152]{1,0:T(8,128)(2,1)S(1)} %get-tuple-element.59), channel_id=1, source_target_pairs={{0,2},{1,3},{2,0},{3,1},{4,6},{5,7},{6,4},{7,5},{8,10},{9,11},{10,... | collective-permute-start | bytes 165896 | tf_op jit(solution)/shard_map/ppermute | solution.py:234
  114.4 3.5 %copy-start.6 = (bf16[192,1152]{1,0:T(8,128)(2,1)S(1)}, bf16[192,1152]{1,0:T(8,128)(2,1)}, u32[]{:S(2)}) copy-start(bf16[192,1152]{1,0:T(8,128)(2,1)} %shard_map.201) | copy-start | bytes 1327108
